TPU v7x, 32 devices: a whole 2x2x4 slice. The times are simulated.
32 devices in a mesh: slab: 4 (over x, core), chan: 2 (over y), filt: 4 (over z).
Axes of the slice: x: 2, y: 2, z: 4, core: 2. Of those that a mesh axis runs over, the one named last changes fastest.
Arguments:
- volume: bfloat16 [256, 8, 32, 128], P('chan', 'slab'), may hold values from -6 to 6
- plane_weight: bfloat16 [3, 3, 256, 256], P(None, None, 'chan', 'filt'), may hold values from -0.125 to 0.125
- depth_weight: bfloat16 [3, 256, 256], replicated, may hold values from -0.21875 to 0.21875
- grad_out: bfloat16 [256, 8, 32, 128], P('filt', 'slab', 'chan'), may hold values from -6 to 6
Outputs:
- output: bfloat16 [256, 8, 32, 128], P('filt', 'slab', 'chan')
- grad_in: bfloat16 [256, 8, 32, 128], P('chan', 'slab', 'filt')
All inputs are finite; a program needn't handle non-finite values.
Results may differ from a plain program's by a relative error of at most 0.0049.
Values may be sent and summed in bfloat16 or wider, within the bound.
No kernel may reach another device: no remote copies, remote signals or barrier semaphores. Data moves between devices by JAX's collectives and lax.ppermute only.
A program may use at most 64 MiB of HBM per device.

v0:
```python
import jax
import jax.numpy as jnp
from jax import lax
from jax.sharding import PartitionSpec as P


def with_halo(value, sides, width):
    for axis, dim in sides:
        size, length = (lax.axis_size(axis), value.shape[dim])
        up = [(i, (i + 1) % size) for i in range(size - 1)]
        down = [(j, i) for i, j in up]
        last = lax.slice_in_dim(value, length - width, length, axis=dim)
        leading = lax.slice_in_dim(value, 0, width, axis=dim)
        before = lax.ppermute(last, axis, up)
        after = lax.ppermute(leading, axis, down)
        value = jnp.concatenate([before, value, after], axis=dim)
    return value


def plane_conv(padded, weight):
    rows = padded.shape[2] - 2
    cols = padded.shape[3] - 2
    inputs = weight.shape[2]
    outputs = weight.shape[3]
    total = None
    for row_tap in range(3):
        stacked = jnp.concatenate(
            [
                padded[:, :, row_tap : row_tap + rows, col_tap : col_tap + cols]
                for col_tap in range(3)
            ],
            axis=0,
        )
        flat_weight = weight[row_tap].reshape(3 * inputs, outputs)
        term = jnp.einsum("cm,czhw->mzhw", flat_weight, stacked, preferred_element_type=jnp.float32)
        total = term if total is None else total + term
    return total


def depth_conv(padded, weight):
    depth = padded.shape[1] - 2
    stacked = jnp.stack([padded[:, tap : tap + depth] for tap in range(3)], axis=0)
    return jnp.einsum("kom,kmzhw->ozhw", weight, stacked, preferred_element_type=jnp.float32)


def pad_plane(field):
    return jnp.pad(field, ((0, 0), (0, 0), (1, 1), (1, 1)))


def pad_columns(field):
    return jnp.pad(field, ((0, 0), (0, 0), (0, 0), (1, 1)))


def local(volume, plane_weight, depth_weight, grad_out):
    filt_index = lax.axis_index("filt")
    partial_mid = plane_conv(pad_plane(volume), plane_weight)
    mid = lax.psum_scatter(partial_mid, "chan", scatter_dimension=2, tiled=True).astype(
        jnp.bfloat16
    )
    out_count = grad_out.shape[0]
    mid_count = mid.shape[0]
    forward_weight = lax.dynamic_slice_in_dim(depth_weight, filt_index * out_count, out_count, 1)
    own_columns = lax.dynamic_slice_in_dim(depth_weight, filt_index * mid_count, mid_count, 2)
    backward_weight = jnp.transpose(own_columns[::-1], (0, 2, 1))
    whole_mid = lax.all_gather(mid, "filt", axis=0, tiled=True)
    padded_mid = with_halo(whole_mid, (("slab", 1),), 1)
    output = depth_conv(padded_mid, forward_weight).astype(jnp.bfloat16)
    whole_grad = lax.all_gather(grad_out, "filt", axis=0, tiled=True)
    padded_grad = with_halo(whole_grad, (("slab", 1),), 1)
    grad_mid = depth_conv(padded_grad, backward_weight).astype(jnp.bfloat16)
    tall_grad = lax.all_gather(grad_mid, "chan", axis=2, tiled=True)
    turned = lax.all_to_all(tall_grad, "filt", split_axis=2, concat_axis=0, tiled=True)
    rimmed_grad = with_halo(turned, (("filt", 2),), 1)
    all_mid_weight = lax.all_gather(plane_weight, "filt", axis=3, tiled=True)
    flipped = jnp.transpose(all_mid_weight[::-1, ::-1], (0, 1, 3, 2))
    grad_in = plane_conv(pad_columns(rimmed_grad), flipped).astype(jnp.bfloat16)
    return (output, grad_in)


def solution(mesh):
    placed = (
        P("chan", "slab", None, None),
        P(None, None, "chan", "filt"),
        P(),
        P("filt", "slab", "chan", None),
    )
    return jax.shard_map(
        local,
        mesh=mesh,
        in_specs=placed,
        out_specs=(P("filt", "slab", "chan", None), P("chan", "slab", "filt", None)),
        check_vma=False,
    )
```

profile of v0, /device:TPU:1, one launch (start us, length us, event | category | flops | bytes accessed | tf_op | source)
XLA Modules:
  0.0 231.0 jit_solution(7157435260248938483)
XLA Ops:
  8.1 2.1 copy.65
  10.2 3.0 %copy.58 = bf16[128,2,32,128]{3,0,2,1:T(8,128)(2,1)S(1)} copy(bf16[128,2,32,128]{3,2,1,0:T(8,128)(2,1)} %param.4) | data formatting | bytes 4194304 | tf_op args[0]
  13.5 4.0 %pad_slice_fusion.2 = (bf16[128,2,32,128]{3,0,2,1:T(8,128)(2,1)S(1)}, bf16[128,2,32,128]{3,0,2,1:T(8,128)(2,1)S(1)}, bf16[128,2,32,128]{3,0,2,1:T(8,128)(2,1)S(1...) fusion(bf16[128,2,32,128]{3,0,2,1:T(8,128)(2,1)S(1)} %copy.58), kind=kLoop, calls=%fused_computation.2 | loop fusion | bytes 18874368 | tf_op jit(solution)/shard_map/slice | solution.py:29
  17.5 1.7 fusion.6
  19.2 1.7 fusion
  20.9 1.7 add_bitcast_fusion
  22.7 2.6 %copy.99 = f32[4,8,128,128]{3,1,2,0:T(8,128)} copy(f32[4,8,128,128]{3,2,1,0:T(8,128)S(1)} %bitcast.96) | data formatting | bytes 4194304
  25.4 33.7 %all-gather.6.cloned.1.call-done = bf16[256,2,16,128]{3,0,2,1:T(8,128)(2,1)} async-done(((bf16[64,2,16,128]{3,0,2,1:T(8,128)(2,1)}), bf16[256,2,16,128]{3,0,2,1:T(8,128)(2,1)}) %all-gather.6.cloned.1.call-update) | async-done | bytes 2097168 | tf_op jit(solution)/shard_map/all_gather | solution.py:68
  59.1 2.9 %fusion.95 = (bf16[256,1,16,128]{3,0,2,1:T(8,128)(2,1)}, bf16[256,1,16,128]{3,0,2,1:T(8,128)(2,1)S(1)}) fusion(bf16[256,2,16,128]{3,0,2,1:T(8,128)(2,1)} %all-gather.6.cloned.1.call-done), kind=kLoop, calls=%fused_computation.96 | loop fusion | bytes 4194304 | tf_op jit(solution)/shard_map/slice | solution.py:12
  62.0 3.6 %collective-permute-start.2 = (bf16[256,1,16,128]{3,0,2,1:T(8,128)(2,1)}, bf16[256,1,16,128]{3,0,2,1:T(8,128)(2,1)}, u32[]{:S(2)}, u32[]{:S(2)}) collective-permute-start(bf16[256,1,16,128]{3,0,2,1:T(8,128)(2,1)} %get-tuple-element.12), channel_id=1, source_target_pairs={{0,8},{8,16},{16,24},{1,9},{9,17},{17,25},{2,10},{10,18},{18,26},{... | collective-permute-start | bytes 3145736 | tf_op jit(solution)/shard_map/ppermute | solution.py:14
  65.7 1.9 collective-permute-start.3
  68.4 1.6 rev.6
  70.0 7.7 %collective-permute-done.2 = bf16[256,1,16,128]{3,0,2,1:T(8,128)(2,1)} collective-permute-done((bf16[256,1,16,128]{3,0,2,1:T(8,128)(2,1)}, bf16[256,1,16,128]{3,0,2,1:T(8,128)(2,1)}, u32[]{:S(2)}, u32[]{:S(2)}) %collective-permute-start.2) | collective-permute-done | bytes 1048608 | tf_op jit(solution)/shard_map/ppermute | solution.py:14
  77.7 4.2 %collective-permute-done.3 = bf16[256,1,16,128]{3,0,2,1:T(8,128)(2,1)} collective-permute-done((bf16[256,1,16,128]{3,0,2,1:T(8,128)(2,1)S(1)}, bf16[256,1,16,128]{3,0,2,1:T(8,128)(2,1)}, u32[]{:S(2)}, u32[]{:S(2)}) %collective-permute-start.3) | collective-permute-done | bytes 1048608 | tf_op jit(solution)/shard_map/ppermute | solution.py:15
  81.9 1.9 fusion.46
  83.8 2.1 fusion.74
  86.0 1.4 copy.95
  88.3 16.1 %all-gather.8.cloned.1.call-done = bf16[64,2,32,128]{3,0,2,1:T(8,128)(2,1)} async-done(((bf16[64,2,16,128]{3,0,2,1:T(8,128)(2,1)}), bf16[64,2,32,128]{3,0,2,1:T(8,128)(2,1)}) %all-gather.8.cloned.1.call-update) | async-done | bytes 1048592 | tf_op jit(solution)/shard_map/all_gather | solution.py:71
  104.4 2.3 copy.69
  106.7 4.3 %all-to-all-start = ((bf16[64,2,32,128]{3,0,1,2:T(8,128)(2,1)}), bf16[64,2,32,128]{3,0,1,2:T(8,128)(2,1)S(1)}, u32[]{:S(2)}, u32[]{:S(2)}) async-start(bf16[64,2,32,128]{3,0,1,2:T(8,128)(2,1)} %copy.69), calls=%async_computation | async-start | bytes 2097152 | tf_op jit(solution)/shard_map/all_to_all | solution.py:72
  111.0 62.1 %all_gather.15 = bf16[3,3,128,256]{2,3,1,0:T(8,128)(2,1)S(1)} all-gather(bf16[3,3,128,64]{2,3,1,0:T(8,128)(2,1)S(1)} %copy-done.9), channel_id=1, replica_groups=mesh['slab'=4,'chan'=2,'filt'=4] {'filt'}, dimensions={3}, use_global_device_ids=true | all-gather | bytes 737280 | tf_op jit(solution)/shard_map/all_gather | solution.py:74
  176.9 6.1 %collective-permute-start.4 = (bf16[256,2,1,128]{0,3,2,1:T(8,128)(2,1)S(1)}, bf16[256,2,1,128]{0,3,2,1:T(8,128)(2,1)S(1)}, u32[]{:S(2)}, u32[]{:S(2)}) collective-permute-start(bf16[256,2,1,128]{0,3,2,1:T(8,128)(2,1)S(1)} %get-tuple-element.32), channel_id=1, source_target_pairs={{0,1},{1,2},{2,3},{4,5},{5,6},{6,7},{8,9},{9,10},{10,11},{12,13},{... | collective-permute-start | bytes 393224 | tf_op jit(solution)/shard_map/ppermute | solution.py:14
  186.2 3.2 %fusion.97 = (bf16[256,2,8,128]{0,3,2,1:T(8,128)(2,1)}, bf16[256,2,8,128]{0,3,2,1:T(8,128)(2,1)S(1)}, bf16[256,2,8,128]{0,3,2,1:T(8,128)(2,1)}, bf16[256,2,8,128...) fusion(bf16[256,2,10,130]{0,3,2,1:T(8,128)(2,1)S(1)} %fusion.55), kind=kLoop, calls=%fused_computation.98 | loop fusion | bytes 12582912 | tf_op jit(solution)/shard_map/slice | solution.py:29
  189.4 3.3 %fusion.96 = (bf16[256,1,16,128]{3,0,2,1:T(8,128)(2,1)}, bf16[256,1,16,128]{3,0,2,1:T(8,128)(2,1)}) fusion(bf16[256,2,16,128]{3,0,2,1:T(8,128)(2,1)} %all-gather.4.cloned.1.call-done), kind=kLoop, calls=%fused_computation.97 | loop fusion | bytes 4194304 | tf_op jit(solution)/shard_map/slice | solution.py:12
  192.7 9.8 %collective-permute-start = (bf16[256,1,16,128]{3,0,2,1:T(8,128)(2,1)}, bf16[256,1,16,128]{3,0,2,1:T(8,128)(2,1)}, u32[]{:S(2)}, u32[]{:S(2)}) collective-permute-start(bf16[256,1,16,128]{3,0,2,1:T(8,128)(2,1)} %get-tuple-element.16), channel_id=1, source_target_pairs={{0,8},{8,16},{16,24},{1,9},{9,17},{17,25},{2,10},{10,18},{18,26},{... | collective-permute-start | bytes 3145736 | tf_op jit(solution)/shard_map/ppermute | solution.py:14
  202.6 2.1 collective-permute-start.1
  207.5 1.9 fusion.77
  209.5 2.2 copy.79
  211.7 2.9 %collective-permute-done = bf16[256,1,16,128]{3,0,2,1:T(8,128)(2,1)} collective-permute-done((bf16[256,1,16,128]{3,0,2,1:T(8,128)(2,1)}, bf16[256,1,16,128]{3,0,2,1:T(8,128)(2,1)}, u32[]{:S(2)}, u32[]{:S(2)}) %collective-permute-start) | collective-permute-done | bytes 1048608 | tf_op jit(solution)/shard_map/ppermute | solution.py:14
  214.6 4.4 %collective-permute-done.1 = bf16[256,1,16,128]{3,0,2,1:T(8,128)(2,1)} collective-permute-done((bf16[256,1,16,128]{3,0,2,1:T(8,128)(2,1)}, bf16[256,1,16,128]{3,0,2,1:T(8,128)(2,1)}, u32[]{:S(2)}, u32[]{:S(2)}) %collective-permute-start.1) | collective-permute-done | bytes 1048608 | tf_op jit(solution)/shard_map/ppermute | solution.py:15
  219.0 1.9 fusion.48
  220.9 1.4 fusion.71
  (69 shorter events, 13.2 us)
Async XLA Ops:
  8.0 59.6 %copy-start = (bf16[3,256,256]{2,1,0:T(8,128)(2,1)S(1)}, bf16[3,256,256]{2,1,0:T(8,128)(2,1)}, u32[]{:S(2)}) copy-start(bf16[3,256,256]{2,1,0:T(8,128)(2,1)} %param.6) | copy-start | bytes 1179652
  8.0 51.1 %all-gather.6.cloned.1.call-start = ((), (), s32[]{:S(2)}) async-start(), calls=%async_computation.3 | async-start | bytes 2621440 | tf_op jit(solution)/shard_map/all_gather | solution.py:68
  10.2 3.0 %copy-start.8 = (bf16[3,3,128,64]{2,3,1,0:T(8,128)(2,1)S(1)}, bf16[3,3,128,64]{2,3,1,0:T(8,128)(2,1)}, u32[]{:S(2)}) copy-start(bf16[3,3,128,64]{2,3,1,0:T(8,128)(2,1)} %param.5) | copy-start | bytes 442372
  10.2 75.8 %reduce-scatter.5.cloned.1.call-start = ((), (), s32[]{:S(2)}) async-start(), calls=%async_computation.5 | async-start | bytes 3145728
  25.3 79.1 %all-gather.8.cloned.1.call-start = ((), (), s32[]{:S(2)}) async-start(), calls=%async_computation.4 | async-start | bytes 1572864 | tf_op jit(solution)/shard_map/all_gather | solution.py:71
  59.1 22.8 %copy-start.1 = (bf16[256,2,16,128]{3,0,2,1:T(8,128)(2,1)S(1)}, bf16[256,2,16,128]{3,0,2,1:T(8,128)(2,1)}, u32[]{:S(2)}) copy-start(bf16[256,2,16,128]{3,0,2,1:T(8,128)(2,1)} %all-gather.6.cloned.1.call-done) | copy-start | bytes 6291460
  62.0 15.7 %collective-permute-start.2 = (bf16[256,1,16,128]{3,0,2,1:T(8,128)(2,1)}, bf16[256,1,16,128]{3,0,2,1:T(8,128)(2,1)}, u32[]{:S(2)}, u32[]{:S(2)}) collective-permute-start(bf16[256,1,16,128]{3,0,2,1:T(8,128)(2,1)} %get-tuple-element.12), channel_id=1, source_target_pairs={{0,8},{8,16},{16,24},{1,9},{9,17},{17,25},{2,10},{10,18},{18,26},{... | collective-permute-start | bytes 3145736 | tf_op jit(solution)/shard_map/ppermute | solution.py:14
  65.7 16.2 %collective-permute-start.3 = (bf16[256,1,16,128]{3,0,2,1:T(8,128)(2,1)S(1)}, bf16[256,1,16,128]{3,0,2,1:T(8,128)(2,1)}, u32[]{:S(2)}, u32[]{:S(2)}) collective-permute-start(bf16[256,1,16,128]{3,0,2,1:T(8,128)(2,1)S(1)} %get-tuple-element.13), channel_id=1, source_target_pairs={{8,0},{16,8},{24,16},{9,1},{17,9},{25,17},{10,2},{18,10},{26,18},{... | collective-permute-start | bytes 3145736 | tf_op jit(solution)/shard_map/ppermute | solution.py:15
  70.0 13.8 %copy-start.13 = (bf16[3,256,64]{2,1,0:T(8,128)(2,1)S(1)}, bf16[3,256,64]{2,1,0:T(8,128)(2,1)}, u32[]{:S(2)}) copy-start(bf16[3,256,64]{2,1,0:T(8,128)(2,1)} %rev.6) | copy-start | bytes 294916
  85.9 103.5 %all-gather.4.cloned.1.call-start = ((), (), s32[]{:S(2)}) async-start(), calls=%async_computation.2 | async-start | bytes 2621440 | tf_op jit(solution)/shard_map/all_gather | solution.py:65
  88.3 22.7 %copy-start.9 = (bf16[3,3,128,64]{2,3,1,0:T(8,128)(2,1)S(1)}, bf16[3,3,128,64]{2,3,1,0:T(8,128)(2,1)}, u32[]{:S(2)}) copy-start(bf16[3,3,128,64]{2,3,1,0:T(8,128)(2,1)} %param.5) | copy-start | bytes 442372
  106.7 67.3 %all-to-all-start = ((bf16[64,2,32,128]{3,0,1,2:T(8,128)(2,1)}), bf16[64,2,32,128]{3,0,1,2:T(8,128)(2,1)S(1)}, u32[]{:S(2)}, u32[]{:S(2)}) async-start(bf16[64,2,32,128]{3,0,1,2:T(8,128)(2,1)} %copy.69), calls=%async_computation | async-start | bytes 2097152 | tf_op jit(solution)/shard_map/all_to_all | solution.py:72
  174.7 8.2 %copy-start.3 = (bf16[3,3,256,128]{3,2,1,0:T(8,128)(2,1)S(1)}, bf16[3,3,256,128]{3,2,1,0:T(8,128)(2,1)}, u32[]{:S(2)}) copy-start(bf16[3,3,256,128]{3,2,1,0:T(8,128)(2,1)} %reverse_bitcast_fusion) | copy-start | bytes 1769476
  175.6 8.2 %collective-permute-start.5 = (bf16[256,2,1,128]{0,3,2,1:T(8,128)(2,1)S(1)}, bf16[256,2,1,128]{0,3,2,1:T(8,128)(2,1)S(1)}, u32[]{:S(2)}, u32[]{:S(2)}) collective-permute-start(bf16[256,2,1,128]{0,3,2,1:T(8,128)(2,1)S(1)} %get-tuple-element.33), channel_id=1, source_target_pairs={{1,0},{2,1},{3,2},{5,4},{6,5},{7,6},{9,8},{10,9},{11,10},{13,12},{... | collective-permute-start | bytes 393224 | tf_op jit(solution)/shard_map/ppermute | solution.py:15
  176.9 8.0 %collective-permute-start.4 = (bf16[256,2,1,128]{0,3,2,1:T(8,128)(2,1)S(1)}, bf16[256,2,1,128]{0,3,2,1:T(8,128)(2,1)S(1)}, u32[]{:S(2)}, u32[]{:S(2)}) collective-permute-start(bf16[256,2,1,128]{0,3,2,1:T(8,128)(2,1)S(1)} %get-tuple-element.32), channel_id=1, source_target_pairs={{0,1},{1,2},{2,3},{4,5},{5,6},{6,7},{8,9},{9,10},{10,11},{12,13},{... | collective-permute-start | bytes 393224 | tf_op jit(solution)/shard_map/ppermute | solution.py:14
  183.8 1.1 copy-start.16
  184.9 0.7 copy-start.14
  189.4 15.3 %copy-start.6 = (bf16[256,2,8,128]{0,3,2,1:T(8,128)(2,1)S(1)}, bf16[256,2,8,128]{0,3,2,1:T(8,128)(2,1)}, u32[]{:S(2)}) copy-start(bf16[256,2,8,128]{0,3,2,1:T(8,128)(2,1)} %get-tuple-element.28) | copy-start | bytes 3145732
  189.4 15.3 %copy-start.7 = (bf16[256,2,8,128]{0,3,2,1:T(8,128)(2,1)S(1)}, bf16[256,2,8,128]{0,3,2,1:T(8,128)(2,1)}, u32[]{:S(2)}) copy-start(bf16[256,2,8,128]{0,3,2,1:T(8,128)(2,1)} %get-tuple-element.29) | copy-start | bytes 3145732
  189.4 15.3 %copy-start.12 = (bf16[1,3,256,128]{3,2,1,0:T(8,128)(2,1)S(1)}, bf16[1,3,256,128]{3,2,1,0:T(8,128)(2,1)}, u32[]{:S(2)}) copy-start(bf16[1,3,256,128]{3,2,1,0:T(8,128)(2,1)} %get-tuple-element.36) | copy-start | bytes 589828
  192.7 21.9 %collective-permute-start = (bf16[256,1,16,128]{3,0,2,1:T(8,128)(2,1)}, bf16[256,1,16,128]{3,0,2,1:T(8,128)(2,1)}, u32[]{:S(2)}, u32[]{:S(2)}) collective-permute-start(bf16[256,1,16,128]{3,0,2,1:T(8,128)(2,1)} %get-tuple-element.16), channel_id=1, source_target_pairs={{0,8},{8,16},{16,24},{1,9},{9,17},{17,25},{2,10},{10,18},{18,26},{... | collective-permute-start | bytes 3145736 | tf_op jit(solution)/shard_map/ppermute | solution.py:14
  202.6 16.4 %collective-permute-start.1 = (bf16[256,1,16,128]{3,0,2,1:T(8,128)(2,1)}, bf16[256,1,16,128]{3,0,2,1:T(8,128)(2,1)}, u32[]{:S(2)}, u32[]{:S(2)}) collective-permute-start(bf16[256,1,16,128]{3,0,2,1:T(8,128)(2,1)} %get-tuple-element.17), channel_id=1, source_target_pairs={{8,0},{16,8},{24,16},{9,1},{17,9},{25,17},{10,2},{18,10},{26,18},{... | collective-permute-start | bytes 3145736 | tf_op jit(solution)/shard_map/ppermute | solution.py:15
  204.7 1.2 copy-start.11
  204.7 1.2 copy-start.17
  205.9 1.2 copy-start.4
  205.9 1.5 copy-start.5
  206.0 1.5 copy-start.10
  206.0 1.6 copy-start.15
  207.5 11.5 %copy-start.2 = (bf16[256,2,16,128]{3,0,2,1:T(8,128)(2,1)S(1)}, bf16[256,2,16,128]{3,0,2,1:T(8,128)(2,1)}, u32[]{:S(2)}) copy-start(bf16[256,2,16,128]{3,0,2,1:T(8,128)(2,1)} %all-gather.4.cloned.1.call-done) | copy-start | bytes 6291460
Sparse Core Ops, SparseCore 0:
  11.1 47.9 all-gather.5
Sparse Core Ops, SparseCore 1:
  25.4 33.7 reduce-scatter.4
  86.0 18.3 all-gather.7
  106.5 74.2 all-gather.3
where the time goes:
time: 232 us; the launch traced here: 231 us
  waiting for transfers between devices  70.1 us (30%)
  blocking collectives  62.1 us (27%)
  local copies, waits for them, and re-layouts  36.1 us (16%)
  starting transfers between devices  29.4 us (13%)
  between operations  16 us (7%)
  matrix products  12.8 us (6%)
  other arithmetic  4.51 us (2%)
    all_gather x1, blocking collectives, local(): all_mid_weight = lax.all_gather(plane_weight, 'filt', axis=3, tiled=True)  62.1 us
    all_gather x1, waiting for transfers between devices, local(): whole_grad = lax.all_gather(grad_out, 'filt', axis=0, tiled=True)  33.7 us
    ppermute x3, starting transfers between devices, with_halo(): before = lax.ppermute(last, axis, up)  19.6 us
    all_gather x1, waiting for transfers between devices, local(): tall_grad = lax.all_gather(grad_mid, 'chan', axis=2, tiled=True)  16.1 us
    unnamed x44, local copies, waits for them, and re-layouts  14.5 us
    ppermute x3, waiting for transfers between devices, with_halo(): before = lax.ppermute(last, axis, up)  11.7 us
    dot_general x6, matrix products, plane_conv(): jnp.einsum('cm,czhw->mzhw', flat_weight, stacked, preferred_element_type=...  9.31 us
    ppermute x3, waiting for transfers between devices, with_halo(): after = lax.ppermute(leading, axis, down)  8.59 us
  transfers between devices with their start and end apart: 11, of which 7 were waited for; matrix products, arithmetic and copies ran while one was open for 18% of the time, Pallas kernels for 0%

commit v1 on v0

v1 whole, which is shorter than its diff:
```python
import jax
import jax.numpy as jnp
from jax import lax
from jax.sharding import PartitionSpec as P

ROWS = ("chan", "filt")


def shift_pairs(n, k):
    return [(i, (i + k) % n) for i in range(n)]


def order_blocks(pieces, me, dim):
    n = len(pieces)
    if n == 1:
        return pieces[0]
    block = pieces[0].shape[dim]
    stacked = jnp.concatenate(pieces[::-1], axis=dim)
    return jnp.roll(stacked, (me + 1) * block, axis=dim)


def gather_blocks(x, axis, dim):
    n = lax.axis_size(axis)
    me = lax.axis_index(axis)
    pieces = [x] + [lax.ppermute(x, axis, shift_pairs(n, k)) for k in range(1, n)]
    return order_blocks(pieces, me, dim)


def scatter_blocks(x, axis, dim, gather_dim):
    n = lax.axis_size(axis)
    me = lax.axis_index(axis)
    size = x.shape[dim] // n
    take = lambda t: lax.dynamic_slice_in_dim(x, t * size, size, dim)
    pieces = [take(me)]
    for k in range(1, n):
        pieces.append(lax.ppermute(take((me + k) % n), axis, shift_pairs(n, k)))
    return order_blocks(pieces, me, gather_dim)


def halo(x, axis, dim, place=None):
    n = lax.axis_size(axis)
    place = place or (lambda i: i)
    up = [(place(i), place(i + 1)) for i in range(n - 1)]
    down = [(place(i + 1), place(i)) for i in range(n - 1)]
    length = x.shape[dim]
    before = lax.ppermute(lax.slice_in_dim(x, length - 1, length, axis=dim), axis, up)
    after = lax.ppermute(lax.slice_in_dim(x, 0, 1, axis=dim), axis, down)
    return jnp.concatenate([before, x, after], axis=dim)


def plane_conv(rows, weight, spec):
    return lax.conv_general_dilated(
        rows,
        weight,
        window_strides=(1, 1),
        padding=((0, 0), (1, 1)),
        dimension_numbers=("CNHW", spec, "CNHW"),
        preferred_element_type=jnp.float32,
    )


def depth_conv(padded, weight, spec):
    out = lax.conv_general_dilated(
        padded[None],
        weight[:, None, None],
        window_strides=(1, 1, 1),
        padding=((0, 0), (0, 0), (0, 0)),
        dimension_numbers=("NCDHW", spec, "NCDHW"),
        preferred_element_type=jnp.float32,
    )
    return out[0]


def forward(volume, weight, depth_weight):
    chans = lax.axis_size("chan")
    filts = lax.axis_size("filt")
    chan = lax.axis_index("chan")
    filt = lax.axis_index("filt")
    rows = volume.shape[2] // (chans * filts)
    padded = jnp.pad(volume, ((0, 0), (0, 0), (1, 1), (0, 0)))
    window = lambda group: lax.dynamic_slice_in_dim(padded, group * rows, rows + 2, 2)
    pieces = [window(chan * filts + filt)]
    for k in range(1, chans):
        target = (chan + k) % chans
        pieces.append(lax.ppermute(window(target * filts + filt), "chan", shift_pairs(chans, k)))
    all_channels = order_blocks(pieces, chan, 0)
    mid = plane_conv(all_channels, weight, "HWIO").astype(jnp.bfloat16)
    deep = halo(mid, "slab", 1)
    out = depth_conv(deep, depth_weight, "DHWOI").astype(jnp.bfloat16)
    return scatter_blocks(out, "filt", 0, 2)


def backward(grad_out, weight, depth_weight):
    chans = lax.axis_size("chan")
    filts = lax.axis_size("filt")
    chan = lax.axis_index("chan")
    filt = lax.axis_index("filt")
    rows = grad_out.shape[2] // filts
    group = filt * chans + chan
    own = group % filts
    place = lambda g: (g % chans) * filts + g // chans
    pieces = []
    for k in range(filts):
        pairs = [(c * filts + f, place(c * filts + (f + k) % filts)) for f in range(filts) for c in range(chans)]
        block = lax.dynamic_slice_in_dim(grad_out, ((filt + k) % filts) * rows, rows, 2)
        pieces.append(lax.ppermute(block, ROWS, pairs))
    all_filters = order_blocks(pieces, own, 0)
    deep = halo(all_filters, "slab", 1)
    grad_mid = depth_conv(deep, depth_weight[::-1], "DHWIO").astype(jnp.bfloat16)
    rimmed = halo(grad_mid, ROWS, 2, place)
    grad_in = plane_conv(rimmed, weight[::-1, ::-1], "HWOI").astype(jnp.bfloat16)
    return scatter_blocks(grad_in, "chan", 0, 2)


def local(volume, plane_weight, depth_weight, grad_out):
    weight = gather_blocks(gather_blocks(plane_weight, "filt", 3), "chan", 2)
    output = forward(volume, weight, depth_weight)
    grad_in = backward(grad_out, weight, depth_weight)
    return (output, grad_in)


def solution(mesh):
    placed = (
        P("chan", "slab", None, None),
        P(None, None, "chan", "filt"),
        P(),
        P("filt", "slab", "chan", None),
    )
    return jax.shard_map(
        local,
        mesh=mesh,
        in_specs=placed,
        out_specs=(P("filt", "slab", "chan", None), P("chan", "slab", "filt", None)),
        check_vma=False,
    )
```

time: 232 us -> 159 us (0.69)
  blocking collectives: 62.1 us -> 0 us
  starting transfers between devices: 29.4 us -> 79.3 us
  waiting for transfers between devices: 70.1 us -> 35.4 us
  between operations: 16 us -> 1.26 us
  local copies, waits for them, and re-layouts: 36.1 us -> 26.9 us
  matrix products: 12.8 us -> 5.04 us
  other arithmetic: 4.51 us -> 10.2 us
    all_gather x1 -> x0, blocking collectives: 62.1 us -> none  [local(): all_mid_weight = lax.all_gather(plane_weight, 'filt', axis=3, tiled=True)]
    ppermute x6 -> x19, starting transfers between devices: 24.9 us -> 79.3 us  [the longest x4 32.5 us: gather_blocks(): lax.ppermute(x, axis, shift_pairs(n, k))]
    all_gather x3 -> x0, waiting for transfers between devices: 49.8 us -> none  [the longest x1 33.7 us: local(): whole_grad = lax.all_gather(grad_out, 'filt', axis=0, tiled=True)]
    ppermute x6 -> x19, waiting for transfers between devices: 20.3 us -> 35.4 us  [the longest x4 16.1 us: scatter_blocks(): pieces.append(lax.ppermute(take((me + k) % n), axis, shift_pairs(n, k)))]
    dot_general x8 -> x0, matrix products: 12.8 us -> none  [the longest x6 9.31 us: plane_conv(): jnp.einsum('cm,czhw->mzhw', flat_weight, stacked, preferred_element_type=...]
    slice x10 -> x3, local copies, waits for them, and re-layouts: 14.4 us -> 1.93 us  [halo(): lax.slice_in_dim(x, length - 1, length, axis=dim)]
    concatenate x0 -> x4, local copies, waits for them, and re-layouts: none -> 6.43 us  [the longest x3 5.8 us: order_blocks(): return jnp.roll(stacked, (me + 1) * block, axis=dim)]
    conv_general_dilated x0 -> x4, matrix products: none -> 5.04 us  [the longest x2 2.98 us: plane_conv(): lax.conv_general_dilated(rows, weight, window_strides=(1, 1), padding=((0...]
  transfers between devices with their start and end apart: 11 -> 19, of which waited for: 7 -> 7; matrix products, arithmetic and copies ran while one was open for 18% -> 21% of each run, Pallas kernels for 0% -> 0%
where the time goes in v1:
time: 159 us; the launch traced here: 158 us
  starting transfers between devices  79.3 us (50%)
  waiting for transfers between devices  35.4 us (22%)
  local copies, waits for them, and re-layouts  26.9 us (17%)
  other arithmetic  10.2 us (6%)
  matrix products  5.04 us (3%)
    ppermute x4, starting transfers between devices, gather_blocks(): lax.ppermute(x, axis, shift_pairs(n, k))  32.5 us
    ppermute x4, starting transfers between devices, scatter_blocks(): pieces.append(lax.ppermute(take((me + k) % n), axis, shift_pairs(n, k)))  16.8 us
    ppermute x4, waiting for transfers between devices, scatter_blocks(): pieces.append(lax.ppermute(take((me + k) % n), axis, shift_pairs(n, k)))  16.1 us
    ppermute x4, starting transfers between devices, backward(): pieces.append(lax.ppermute(block, ROWS, pairs))  12.8 us
    ppermute x3, starting transfers between devices, halo(): lax.ppermute(lax.slice_in_dim(x, length - 1, length, axis=dim), axis, up)  11.7 us
    unnamed x36, local copies, waits for them, and re-layouts  9.96 us
    ppermute x3, waiting for transfers between devices, halo(): lax.ppermute(lax.slice_in_dim(x, length - 1, length, axis=dim), axis, up)  8.83 us
    ppermute x4, waiting for transfers between devices, backward(): pieces.append(lax.ppermute(block, ROWS, pairs))  6.25 us
  transfers between devices with their start and end apart: 19, of which 7 were waited for; matrix products, arithmetic and copies ran while one was open for 21% of the time, Pallas kernels for 0%

profile of v1, /device:TPU:1, one launch (start us, length us, event | category | flops | bytes accessed | tf_op | source)
XLA Modules:
  0.0 158.1 jit_solution(12626822483559392693)
XLA Ops:
  0.7 1.5 constant_dynamic-slice_fusion.3
  3.1 5.0 %collective-permute-start.10 = (bf16[64,2,4,128]{0,3,2,1:T(8,128)(2,1)}, bf16[64,2,4,128]{0,3,2,1:T(8,128)(2,1)S(1)}, u32[]{:S(2)}, u32[]{:S(2)}) collective-permute-start(bf16[64,2,4,128]{0,3,2,1:T(8,128)(2,1)} %copy.41), channel_id=1, source_target_pairs={{0,5},{4,7},{1,0},{5,2},{2,4},{6,6},{3,1},{7,3},{8,13},{12,15},{9,... | collective-permute-start | bytes 393224 | tf_op jit(solution)/shard_map/ppermute | solution.py:106
  9.1 4.2 %collective-permute-start.12 = (bf16[64,2,4,128]{0,3,2,1:T(8,128)(2,1)S(1)}, bf16[64,2,4,128]{0,3,2,1:T(8,128)(2,1)S(1)}, u32[]{:S(2)}, u32[]{:S(2)}) collective-permute-start(bf16[64,2,4,128]{0,3,2,1:T(8,128)(2,1)S(1)} %copy.43), channel_id=1, source_target_pairs={{0,4},{4,6},{1,1},{5,3},{2,5},{6,7},{3,0},{7,2},{8,12},{12,14},{9,... | collective-permute-start | bytes 393224 | tf_op jit(solution)/shard_map/ppermute | solution.py:106
  14.2 3.6 %collective-permute-start.13 = (bf16[64,2,4,128]{0,3,2,1:T(8,128)(2,1)}, bf16[64,2,4,128]{0,3,2,1:T(8,128)(2,1)}, u32[]{:S(2)}, u32[]{:S(2)}) collective-permute-start(bf16[64,2,4,128]{0,3,2,1:T(8,128)(2,1)} %copy.44), channel_id=1, source_target_pairs={{0,0},{4,2},{1,4},{5,6},{2,1},{6,3},{3,5},{7,7},{8,8},{12,10},{9,1... | collective-permute-start | bytes 393224 | tf_op jit(solution)/shard_map/ppermute | solution.py:106
  18.2 32.4 %collective-permute-start.2 = (bf16[3,3,128,64]{3,2,1,0:T(8,128)(2,1)S(1)}, bf16[3,3,128,64]{3,2,1,0:T(8,128)(2,1)}, u32[]{:S(2)}, u32[]{:S(2)}) collective-permute-start(bf16[3,3,128,64]{3,2,1,0:T(8,128)(2,1)S(1)} %copy.17), channel_id=1, source_target_pairs={{0,2},{1,3},{2,0},{3,1},{4,6},{5,7},{6,4},{7,5},{8,10},{9,11},{10,... | collective-permute-start | bytes 442376 | tf_op jit(solution)/shard_map/ppermute | solution.py:25
  50.6 6.2 %collective-permute-done.11 = bf16[64,2,4,128]{0,3,2,1:T(8,128)(2,1)S(1)} collective-permute-done((bf16[64,2,4,128]{0,3,2,1:T(8,128)(2,1)}, bf16[64,2,4,128]{0,3,2,1:T(8,128)(2,1)S(1)}, u32[]{:S(2)}, u32[]{:S(2)}) %collective-permute-start.11) | collective-permute-done | bytes 131104 | tf_op jit(solution)/shard_map/ppermute | solution.py:106
  58.2 2.8 %concatenate.50 = bf16[512,2,4,128]{0,3,2,1:T(8,128)(2,1)S(1)} concatenate(bf16[64,2,4,128]{0,3,2,1:T(8,128)(2,1)} %copy-done.3, bf16[64,2,4,128]{0,3,2,1:T(8,128)(2,1)} %copy-done.4, bf16[64,2,4,128]{0,3,2,1:T(8,128)(2,1)} %copy-done.5, bf16[64,2,4,128]{0,3,2,1:T(8,128)(2,1)} %collective-permute-done.13, bf16[64,2,4,128]{0,3,2,1:T(8,128)(2,1)} %copy-done.3, ...), dimensions={0} | concatenate | bytes 2097152 | tf_op jit(solution)/shard_map/jit(_roll_dynamic)/concatenate | solution.py:19
  62.1 3.7 %collective-permute-start.14 = (bf16[256,1,4,128]{0,3,2,1:T(8,128)(2,1)}, bf16[256,1,4,128]{0,3,2,1:T(8,128)(2,1)}, u32[]{:S(2)}, u32[]{:S(2)}) collective-permute-start(bf16[256,1,4,128]{0,3,2,1:T(8,128)(2,1)} %get-tuple-element.6), channel_id=1, source_target_pairs={{0,8},{8,16},{16,24},{1,9},{9,17},{17,25},{2,10},{10,18},{18,26},{... | collective-permute-start | bytes 786440 | tf_op jit(solution)/shard_map/ppermute | solution.py:46
  65.8 1.9 %collective-permute-start.15 = (bf16[256,1,4,128]{0,3,2,1:T(8,128)(2,1)}, bf16[256,1,4,128]{0,3,2,1:T(8,128)(2,1)}, u32[]{:S(2)}, u32[]{:S(2)}) collective-permute-start(bf16[256,1,4,128]{0,3,2,1:T(8,128)(2,1)} %get-tuple-element.7), channel_id=1, source_target_pairs={{8,0},{16,8},{24,16},{9,1},{17,9},{25,17},{10,2},{18,10},{26,18},{... | collective-permute-start | bytes 786440 | tf_op jit(solution)/shard_map/ppermute | solution.py:47
  67.8 1.5 pad_dynamic-slice_fusion
  69.3 1.8 %rev.4 = bf16[3,256,256]{2,1,0:T(8,128)(2,1)} reverse(bf16[3,256,256]{2,1,0:T(8,128)(2,1)} %param.6), dimensions={0} | reverse | bytes 786432 | tf_op jit(solution)/shard_map/rev | solution.py:109
  72.1 2.4 %collective-permute-done.2 = bf16[3,3,128,64]{3,2,1,0:T(8,128)(2,1)} collective-permute-done((bf16[3,3,128,64]{3,2,1,0:T(8,128)(2,1)S(1)}, bf16[3,3,128,64]{3,2,1,0:T(8,128)(2,1)}, u32[]{:S(2)}, u32[]{:S(2)}) %collective-permute-start.2) | collective-permute-done | bytes 147488 | tf_op jit(solution)/shard_map/ppermute | solution.py:25
  74.5 2.8 %concatenate.46 = bf16[3,3,128,512]{3,2,1,0:T(8,128)(2,1)S(1)} concatenate(bf16[3,3,128,64]{3,2,1,0:T(8,128)(2,1)} %collective-permute-done.1, bf16[3,3,128,64]{3,2,1,0:T(8,128)(2,1)} %collective-permute-done.2, bf16[3,3,128,64]{3,2,1,0:T(8,128)(2,1)} %collective-permute-done.3, bf16[3,3,128,64]{3,2,1,0:T(8,128)(2,1)S(1)} %copy.17, ...), dimensions={3} | concatenate | bytes 2359296 | tf_op jit(solution)/shard_map/jit(_roll_dynamic)/concatenate | solution.py:19
  77.7 1.2 pad_maximum_fusion.1
  80.3 4.0 %collective-permute-start.16 = (bf16[256,2,1,128]{0,3,2,1:T(8,128)(2,1)}, bf16[256,2,1,128]{0,3,2,1:T(8,128)(2,1)}, u32[]{:S(2)}, u32[]{:S(2)}) collective-permute-start(bf16[256,2,1,128]{0,3,2,1:T(8,128)(2,1)} %get-tuple-element.10), channel_id=1, source_target_pairs={{0,4},{4,1},{1,5},{5,2},{2,6},{6,3},{3,7},{8,12},{12,9},{9,13},{13... | collective-permute-start | bytes 393224 | tf_op jit(solution)/shard_map/ppermute | solution.py:46
  84.3 1.5 collective-permute-start.17
  86.2 3.4 %fusion.10 = bf16[256,6,2,128]{3,1,2,0:T(8,128)(2,1)S(1)} fusion(s32[]{:T(128)S(6)} %select_n.133, bf16[128,2,6,128]{3,2,1,0:T(8,128)(2,1)S(1)} %collective-permute-done, bf16[128,2,6,128]{3,2,1,0:T(8,128)(2,1)S(1)} %copy-done.1), kind=kLoop, calls=%fused_computation.25 | loop fusion | flops 1179648 | bytes 1572868 | tf_op jit(solution)/shard_map/jit(_roll_dynamic)/dynamic_slice | solution.py:19
  89.6 1.3 copy.45
  92.5 8.8 %collective-permute-done.16 = bf16[256,2,1,128]{0,3,2,1:T(8,128)(2,1)} collective-permute-done((bf16[256,2,1,128]{0,3,2,1:T(8,128)(2,1)}, bf16[256,2,1,128]{0,3,2,1:T(8,128)(2,1)}, u32[]{:S(2)}, u32[]{:S(2)}) %collective-permute-start.16) | collective-permute-done | bytes 131104 | tf_op jit(solution)/shard_map/ppermute | solution.py:46
  105.9 1.5 fusion.2
  108.0 4.0 %collective-permute-start.5 = (bf16[256,1,4,128]{0,2,3,1:T(4,128)(2,1)S(1)}, bf16[256,1,4,128]{0,2,3,1:T(4,128)(2,1)S(1)}, u32[]{:S(2)}, u32[]{:S(2)}) collective-permute-start(bf16[256,1,4,128]{0,2,3,1:T(4,128)(2,1)S(1)} %get-tuple-element.19), channel_id=1, source_target_pairs={{0,8},{8,16},{16,24},{1,9},{9,17},{17,25},{2,10},{10,18},{18,26},{... | collective-permute-start | bytes 786440 | tf_op jit(solution)/shard_map/ppermute | solution.py:46
  112.1 2.1 %collective-permute-start.6 = (bf16[256,1,4,128]{0,2,3,1:T(4,128)(2,1)S(1)}, bf16[256,1,4,128]{0,2,3,1:T(4,128)(2,1)S(1)}, u32[]{:S(2)}, u32[]{:S(2)}) collective-permute-start(bf16[256,1,4,128]{0,2,3,1:T(4,128)(2,1)S(1)} %get-tuple-element.20), channel_id=1, source_target_pairs={{8,0},{16,8},{24,16},{9,1},{17,9},{25,17},{10,2},{18,10},{26,18},{... | collective-permute-start | bytes 786440 | tf_op jit(solution)/shard_map/ppermute | solution.py:47
  114.2 1.5 fusion.3
  116.5 2.3 %collective-permute-start.18 = (bf16[128,2,4,128]{0,2,3,1:T(4,128)(2,1)S(1)}, bf16[128,2,4,128]{0,2,3,1:T(4,128)(2,1)S(1)}, u32[]{:S(2)}, u32[]{:S(2)}) collective-permute-start(bf16[128,2,4,128]{0,2,3,1:T(4,128)(2,1)S(1)} %get-tuple-element.9), channel_id=1, source_target_pairs={{0,4},{4,0},{1,5},{5,1},{2,6},{6,2},{3,7},{7,3},{8,12},{12,8},{9,1... | collective-permute-start | bytes 786440 | tf_op jit(solution)/shard_map/ppermute | solution.py:36
  118.7 1.4 collective-permute-done.6
  120.9 1.4 convolution_convert_fusion.1
  122.7 3.1 %collective-permute-start.7 = (bf16[64,2,4,128]{0,3,2,1:T(8,128)(2,1)S(1)}, bf16[64,2,4,128]{0,3,2,1:T(8,128)(2,1)S(1)}, u32[]{:S(2)}, u32[]{:S(2)}) collective-permute-start(bf16[64,2,4,128]{0,3,2,1:T(8,128)(2,1)S(1)} %get-tuple-element.18), channel_id=1, source_target_pairs={{0,3},{1,0},{2,1},{3,2},{4,7},{5,4},{6,5},{7,6},{8,11},{9,8},{10,9... | collective-permute-start | bytes 393224 | tf_op jit(solution)/shard_map/ppermute | solution.py:36
  125.8 10.5 %collective-permute-start.8 = (bf16[64,2,4,128]{0,3,2,1:T(8,128)(2,1)S(1)}, bf16[64,2,4,128]{0,3,2,1:T(8,128)(2,1)S(1)}, u32[]{:S(2)}, u32[]{:S(2)}) collective-permute-start(bf16[64,2,4,128]{0,3,2,1:T(8,128)(2,1)S(1)} %get-tuple-element.17), channel_id=1, source_target_pairs={{0,2},{1,3},{2,0},{3,1},{4,6},{5,7},{6,4},{7,5},{8,10},{9,11},{10,... | collective-permute-start | bytes 393224 | tf_op jit(solution)/shard_map/ppermute | solution.py:36
  137.4 1.3 copy.38
  139.6 1.2 collective-permute-done.7
  140.8 14.9 %collective-permute-done.8 = bf16[64,2,4,128]{0,3,2,1:T(8,128)(2,1)S(1)} collective-permute-done((bf16[64,2,4,128]{0,3,2,1:T(8,128)(2,1)S(1)}, bf16[64,2,4,128]{0,3,2,1:T(8,128)(2,1)S(1)}, u32[]{:S(2)}, u32[]{:S(2)}) %collective-permute-start.8) | collective-permute-done | bytes 131104 | tf_op jit(solution)/shard_map/ppermute | solution.py:36
  156.5 1.6 %copy.37 = bf16[64,2,16,128]{3,2,1,0:T(8,128)(2,1)} copy(bf16[64,2,16,128]{0,3,2,1:T(8,128)(2,1)S(1)} %constant_dynamic-slice_fusion.7) | data formatting | bytes 1048576
  (78 shorter events, 19.9 us)
Async XLA Ops:
  0.6 17.2 %copy-start.8 = (bf16[3,3,128,64]{2,3,1,0:T(8,128)(2,1)S(1)}, bf16[3,3,128,64]{2,3,1,0:T(8,128)(2,1)}, u32[]{:S(2)}) copy-start(bf16[3,3,128,64]{2,3,1,0:T(8,128)(2,1)} %param.5) | copy-start | bytes 442372
  3.1 15.1 %collective-permute-start.10 = (bf16[64,2,4,128]{0,3,2,1:T(8,128)(2,1)}, bf16[64,2,4,128]{0,3,2,1:T(8,128)(2,1)S(1)}, u32[]{:S(2)}, u32[]{:S(2)}) collective-permute-start(bf16[64,2,4,128]{0,3,2,1:T(8,128)(2,1)} %copy.41), channel_id=1, source_target_pairs={{0,5},{4,7},{1,0},{5,2},{2,4},{6,6},{3,1},{7,3},{8,13},{12,15},{9,... | collective-permute-start | bytes 393224 | tf_op jit(solution)/shard_map/ppermute | solution.py:106
  8.9 47.9 %collective-permute-start.11 = (bf16[64,2,4,128]{0,3,2,1:T(8,128)(2,1)}, bf16[64,2,4,128]{0,3,2,1:T(8,128)(2,1)S(1)}, u32[]{:S(2)}, u32[]{:S(2)}) collective-permute-start(bf16[64,2,4,128]{0,3,2,1:T(8,128)(2,1)} %copy.42), channel_id=1, source_target_pairs={{0,1},{4,3},{1,5},{5,7},{2,0},{6,2},{3,4},{7,6},{8,9},{12,11},{9,1... | collective-permute-start | bytes 393224 | tf_op jit(solution)/shard_map/ppermute | solution.py:106
  9.1 47.7 %collective-permute-start.12 = (bf16[64,2,4,128]{0,3,2,1:T(8,128)(2,1)S(1)}, bf16[64,2,4,128]{0,3,2,1:T(8,128)(2,1)S(1)}, u32[]{:S(2)}, u32[]{:S(2)}) collective-permute-start(bf16[64,2,4,128]{0,3,2,1:T(8,128)(2,1)S(1)} %copy.43), channel_id=1, source_target_pairs={{0,4},{4,6},{1,1},{5,3},{2,5},{6,7},{3,0},{7,2},{8,12},{12,14},{9,... | collective-permute-start | bytes 393224 | tf_op jit(solution)/shard_map/ppermute | solution.py:106
  14.2 44.0 %collective-permute-start.13 = (bf16[64,2,4,128]{0,3,2,1:T(8,128)(2,1)}, bf16[64,2,4,128]{0,3,2,1:T(8,128)(2,1)}, u32[]{:S(2)}, u32[]{:S(2)}) collective-permute-start(bf16[64,2,4,128]{0,3,2,1:T(8,128)(2,1)} %copy.44), channel_id=1, source_target_pairs={{0,0},{4,2},{1,4},{5,6},{2,1},{6,3},{3,5},{7,7},{8,8},{12,10},{9,1... | collective-permute-start | bytes 393224 | tf_op jit(solution)/shard_map/ppermute | solution.py:106
  18.0 54.0 %collective-permute-start.3 = (bf16[3,3,128,64]{3,2,1,0:T(8,128)(2,1)S(1)}, bf16[3,3,128,64]{3,2,1,0:T(8,128)(2,1)}, u32[]{:S(2)}, u32[]{:S(2)}) collective-permute-start(bf16[3,3,128,64]{3,2,1,0:T(8,128)(2,1)S(1)} %copy.17), channel_id=1, source_target_pairs={{0,1},{1,2},{2,3},{3,0},{4,5},{5,6},{6,7},{7,4},{8,9},{9,10},{10,1... | collective-permute-start | bytes 442376 | tf_op jit(solution)/shard_map/ppermute | solution.py:25
  18.2 49.6 %copy-start = (bf16[128,2,32,128]{3,2,1,0:T(8,128)(2,1)S(1)}, bf16[128,2,32,128]{3,2,1,0:T(8,128)(2,1)}, u32[]{:S(2)}) copy-start(bf16[128,2,32,128]{3,2,1,0:T(8,128)(2,1)} %param.4) | copy-start | bytes 6291460
  18.2 38.7 %copy-start.3 = (bf16[64,2,4,128]{0,3,2,1:T(8,128)(2,1)}, bf16[64,2,4,128]{0,3,2,1:T(8,128)(2,1)S(1)}, u32[]{:S(2)}) copy-start(bf16[64,2,4,128]{0,3,2,1:T(8,128)(2,1)S(1)} %collective-permute-done.10) | copy-start | bytes 393220
  18.2 56.3 %collective-permute-start.2 = (bf16[3,3,128,64]{3,2,1,0:T(8,128)(2,1)S(1)}, bf16[3,3,128,64]{3,2,1,0:T(8,128)(2,1)}, u32[]{:S(2)}, u32[]{:S(2)}) collective-permute-start(bf16[3,3,128,64]{3,2,1,0:T(8,128)(2,1)S(1)} %copy.17), channel_id=1, source_target_pairs={{0,2},{1,3},{2,0},{3,1},{4,6},{5,7},{6,4},{7,5},{8,10},{9,11},{10,... | collective-permute-start | bytes 442376 | tf_op jit(solution)/shard_map/ppermute | solution.py:25
  56.8 0.7 copy-start.4
  56.8 17.7 %collective-permute-start.1 = (bf16[3,3,128,64]{3,2,1,0:T(8,128)(2,1)S(1)}, bf16[3,3,128,64]{3,2,1,0:T(8,128)(2,1)}, u32[]{:S(2)}, u32[]{:S(2)}) collective-permute-start(bf16[3,3,128,64]{3,2,1,0:T(8,128)(2,1)S(1)} %copy.17), channel_id=1, source_target_pairs={{0,3},{1,0},{2,1},{3,2},{4,7},{5,4},{6,5},{7,6},{8,11},{9,8},{10,9... | collective-permute-start | bytes 442376 | tf_op jit(solution)/shard_map/ppermute | solution.py:25
  57.5 0.7 copy-start.5
  62.1 15.5 %collective-permute-start.14 = (bf16[256,1,4,128]{0,3,2,1:T(8,128)(2,1)}, bf16[256,1,4,128]{0,3,2,1:T(8,128)(2,1)}, u32[]{:S(2)}, u32[]{:S(2)}) collective-permute-start(bf16[256,1,4,128]{0,3,2,1:T(8,128)(2,1)} %get-tuple-element.6), channel_id=1, source_target_pairs={{0,8},{8,16},{16,24},{1,9},{9,17},{17,25},{2,10},{10,18},{18,26},{... | collective-permute-start | bytes 786440 | tf_op jit(solution)/shard_map/ppermute | solution.py:46
  65.8 11.8 %collective-permute-start.15 = (bf16[256,1,4,128]{0,3,2,1:T(8,128)(2,1)}, bf16[256,1,4,128]{0,3,2,1:T(8,128)(2,1)}, u32[]{:S(2)}, u32[]{:S(2)}) collective-permute-start(bf16[256,1,4,128]{0,3,2,1:T(8,128)(2,1)} %get-tuple-element.7), channel_id=1, source_target_pairs={{8,0},{16,8},{24,16},{9,1},{17,9},{25,17},{10,2},{18,10},{26,18},{... | collective-permute-start | bytes 786440 | tf_op jit(solution)/shard_map/ppermute | solution.py:47
  72.1 5.6 %copy-start.2 = (bf16[256,2,4,128]{0,3,2,1:T(8,128)(2,1)S(1)}, bf16[256,2,4,128]{0,3,2,1:T(8,128)(2,1)}, u32[]{:S(2)}) copy-start(bf16[256,2,4,128]{0,3,2,1:T(8,128)(2,1)} %constant_dynamic-slice_fusion.2) | copy-start | bytes 1572868
  72.1 14.1 %collective-permute-start = (bf16[128,2,6,128]{3,2,1,0:T(8,128)(2,1)}, bf16[128,2,6,128]{3,2,1,0:T(8,128)(2,1)S(1)}, u32[]{:S(2)}, u32[]{:S(2)}) collective-permute-start(bf16[128,2,6,128]{3,2,1,0:T(8,128)(2,1)} %get-tuple-element.5), channel_id=1, source_target_pairs={{0,4},{4,0},{1,5},{5,1},{2,6},{6,2},{3,7},{7,3},{8,12},{12,8},{9,1... | collective-permute-start | bytes 1179656 | tf_op jit(solution)/shard_map/ppermute | solution.py:85
  77.3 1.5 copy-start.7
  77.6 27.3 %collective-permute-start.4 = (bf16[3,3,128,256]{3,2,1,0:T(8,128)(2,1)S(1)}, bf16[3,3,128,256]{3,2,1,0:T(8,128)(2,1)S(1)}, u32[]{:S(2)}, u32[]{:S(2)}) collective-permute-start(bf16[3,3,128,256]{3,2,1,0:T(8,128)(2,1)S(1)} %constant_dynamic-slice_fusion.8), channel_id=1, source_target_pairs={{0,4},{4,0},{1,5},{5,1},{2,6},{6,2},{3,7},{7,3},{8,12},{12,8},{9,1... | collective-permute-start | bytes 1769480 | tf_op jit(solution)/shard_map/ppermute | solution.py:25
  78.8 7.4 %copy-start.1 = (bf16[128,2,6,128]{3,2,1,0:T(8,128)(2,1)S(1)}, bf16[128,2,6,128]{3,2,1,0:T(8,128)(2,1)}, u32[]{:S(2)}) copy-start(bf16[128,2,6,128]{3,2,1,0:T(8,128)(2,1)} %get-tuple-element.4) | copy-start | bytes 1179652
  80.3 21.0 %collective-permute-start.16 = (bf16[256,2,1,128]{0,3,2,1:T(8,128)(2,1)}, bf16[256,2,1,128]{0,3,2,1:T(8,128)(2,1)}, u32[]{:S(2)}, u32[]{:S(2)}) collective-permute-start(bf16[256,2,1,128]{0,3,2,1:T(8,128)(2,1)} %get-tuple-element.10), channel_id=1, source_target_pairs={{0,4},{4,1},{1,5},{5,2},{2,6},{6,3},{3,7},{8,12},{12,9},{9,13},{13... | collective-permute-start | bytes 393224 | tf_op jit(solution)/shard_map/ppermute | solution.py:46
  84.3 17.1 %collective-permute-start.17 = (bf16[256,2,1,128]{0,3,2,1:T(8,128)(2,1)}, bf16[256,2,1,128]{0,3,2,1:T(8,128)(2,1)}, u32[]{:S(2)}, u32[]{:S(2)}) collective-permute-start(bf16[256,2,1,128]{0,3,2,1:T(8,128)(2,1)} %get-tuple-element.11), channel_id=1, source_target_pairs={{4,0},{1,4},{5,1},{2,5},{6,2},{3,6},{7,3},{12,8},{9,12},{13,9},{10... | collective-permute-start | bytes 393224 | tf_op jit(solution)/shard_map/ppermute | solution.py:47
  103.9 1.9 %copy-start.9 = (pred[16,17]{0,1:T(8,128)(4,1)S(1)}, pred[16,17]{0,1:T(8,128)(4,1)}, u32[]{:S(2)}) copy-start(pred[16,17]{0,1:T(8,128)(4,1)} %constant.187) | copy-start | bytes 820
  108.0 10.7 %collective-permute-start.5 = (bf16[256,1,4,128]{0,2,3,1:T(4,128)(2,1)S(1)}, bf16[256,1,4,128]{0,2,3,1:T(4,128)(2,1)S(1)}, u32[]{:S(2)}, u32[]{:S(2)}) collective-permute-start(bf16[256,1,4,128]{0,2,3,1:T(4,128)(2,1)S(1)} %get-tuple-element.19), channel_id=1, source_target_pairs={{0,8},{8,16},{16,24},{1,9},{9,17},{17,25},{2,10},{10,18},{18,26},{... | collective-permute-start | bytes 786440 | tf_op jit(solution)/shard_map/ppermute | solution.py:46
  112.1 8.0 %collective-permute-start.6 = (bf16[256,1,4,128]{0,2,3,1:T(4,128)(2,1)S(1)}, bf16[256,1,4,128]{0,2,3,1:T(4,128)(2,1)S(1)}, u32[]{:S(2)}, u32[]{:S(2)}) collective-permute-start(bf16[256,1,4,128]{0,2,3,1:T(4,128)(2,1)S(1)} %get-tuple-element.20), channel_id=1, source_target_pairs={{8,0},{16,8},{24,16},{9,1},{17,9},{25,17},{10,2},{18,10},{26,18},{... | collective-permute-start | bytes 786440 | tf_op jit(solution)/shard_map/ppermute | solution.py:47
  116.0 4.8 %copy-start.6 = (bf16[3,256,256]{2,1,0:T(8,128)(2,1)S(1)}, bf16[3,256,256]{2,1,0:T(8,128)(2,1)}, u32[]{:S(2)}) copy-start(bf16[3,256,256]{2,1,0:T(8,128)(2,1)} %param.6) | copy-start | bytes 1179652
  116.5 19.9 %collective-permute-start.18 = (bf16[128,2,4,128]{0,2,3,1:T(4,128)(2,1)S(1)}, bf16[128,2,4,128]{0,2,3,1:T(4,128)(2,1)S(1)}, u32[]{:S(2)}, u32[]{:S(2)}) collective-permute-start(bf16[128,2,4,128]{0,2,3,1:T(4,128)(2,1)S(1)} %get-tuple-element.9), channel_id=1, source_target_pairs={{0,4},{4,0},{1,5},{5,1},{2,6},{6,2},{3,7},{7,3},{8,12},{12,8},{9,1... | collective-permute-start | bytes 786440 | tf_op jit(solution)/shard_map/ppermute | solution.py:36
  122.7 18.1 %collective-permute-start.7 = (bf16[64,2,4,128]{0,3,2,1:T(8,128)(2,1)S(1)}, bf16[64,2,4,128]{0,3,2,1:T(8,128)(2,1)S(1)}, u32[]{:S(2)}, u32[]{:S(2)}) collective-permute-start(bf16[64,2,4,128]{0,3,2,1:T(8,128)(2,1)S(1)} %get-tuple-element.18), channel_id=1, source_target_pairs={{0,3},{1,0},{2,1},{3,2},{4,7},{5,4},{6,5},{7,6},{8,11},{9,8},{10,9... | collective-permute-start | bytes 393224 | tf_op jit(solution)/shard_map/ppermute | solution.py:36
  125.8 29.9 %collective-permute-start.8 = (bf16[64,2,4,128]{0,3,2,1:T(8,128)(2,1)S(1)}, bf16[64,2,4,128]{0,3,2,1:T(8,128)(2,1)S(1)}, u32[]{:S(2)}, u32[]{:S(2)}) collective-permute-start(bf16[64,2,4,128]{0,3,2,1:T(8,128)(2,1)S(1)} %get-tuple-element.17), channel_id=1, source_target_pairs={{0,2},{1,3},{2,0},{3,1},{4,6},{5,7},{6,4},{7,5},{8,10},{9,11},{10,... | collective-permute-start | bytes 393224 | tf_op jit(solution)/shard_map/ppermute | solution.py:36
  138.7 17.0 %collective-permute-start.9 = (bf16[64,2,4,128]{0,3,2,1:T(8,128)(2,1)S(1)}, bf16[64,2,4,128]{0,3,2,1:T(8,128)(2,1)S(1)}, u32[]{:S(2)}, u32[]{:S(2)}) collective-permute-start(bf16[64,2,4,128]{0,3,2,1:T(8,128)(2,1)S(1)} %get-tuple-element.16), channel_id=1, source_target_pairs={{0,1},{1,2},{2,3},{3,0},{4,5},{5,6},{6,7},{7,4},{8,9},{9,10},{10,1... | collective-permute-start | bytes 393224 | tf_op jit(solution)/shard_map/ppermute | solution.py:36

commit v2 on v1

--- a/solution.py
+++ b/solution.py
@@ -71,23 +71,33 @@
     return out[0]
 
 
+def gather_weight(weight):
+    filts = lax.axis_size("filt")
+    chans = lax.axis_size("chan")
+    spread = jnp.broadcast_to(weight[None], (filts,) + weight.shape)
+    by_filt = lax.all_to_all(spread, "filt", 0, 0, tiled=True)
+    spread = jnp.broadcast_to(by_filt[None], (chans,) + by_filt.shape)
+    both = lax.all_to_all(spread, "chan", 0, 0, tiled=True)
+    c_loc, m_loc = weight.shape[2:]
+    whole = jnp.transpose(both, (2, 3, 0, 4, 1, 5))
+    return whole.reshape(3, 3, chans * c_loc, filts * m_loc)
+
+
 def forward(volume, weight, depth_weight):
     chans = lax.axis_size("chan")
     filts = lax.axis_size("filt")
-    chan = lax.axis_index("chan")
     filt = lax.axis_index("filt")
     rows = volume.shape[2] // (chans * filts)
     padded = jnp.pad(volume, ((0, 0), (0, 0), (1, 1), (0, 0)))
-    window = lambda group: lax.dynamic_slice_in_dim(padded, group * rows, rows + 2, 2)
-    pieces = [window(chan * filts + filt)]
-    for k in range(1, chans):
-        target = (chan + k) % chans
-        pieces.append(lax.ppermute(window(target * filts + filt), "chan", shift_pairs(chans, k)))
-    all_channels = order_blocks(pieces, chan, 0)
+    windows = jnp.stack(
+        [lax.dynamic_slice_in_dim(padded, (t * filts + filt) * rows, rows + 2, 2) for t in range(chans)]
+    )
+    all_channels = lax.all_to_all(windows, "chan", 0, 0, tiled=True)
+    all_channels = all_channels.reshape((-1,) + all_channels.shape[2:])
     mid = plane_conv(all_channels, weight, "HWIO").astype(jnp.bfloat16)
     deep = halo(mid, "slab", 1)
     out = depth_conv(deep, depth_weight, "DHWOI").astype(jnp.bfloat16)
-    return scatter_blocks(out, "filt", 0, 2)
+    return lax.all_to_all(out, "filt", 0, 2, tiled=True)
 
 
 def backward(grad_out, weight, depth_weight):
@@ -96,24 +106,29 @@
     chan = lax.axis_index("chan")
     filt = lax.axis_index("filt")
     rows = grad_out.shape[2] // filts
-    group = filt * chans + chan
-    own = group % filts
-    place = lambda g: (g % chans) * filts + g // chans
-    pieces = []
-    for k in range(filts):
-        pairs = [(c * filts + f, place(c * filts + (f + k) % filts)) for f in range(filts) for c in range(chans)]
-        block = lax.dynamic_slice_in_dim(grad_out, ((filt + k) % filts) * rows, rows, 2)
-        pieces.append(lax.ppermute(block, ROWS, pairs))
-    all_filters = order_blocks(pieces, own, 0)
+    rimmed = halo(grad_out, "chan", 2)
+    windows = jnp.stack([lax.slice_in_dim(rimmed, t * rows, t * rows + rows + 2, axis=2) for t in range(filts)])
+    all_filters = lax.all_to_all(windows, "filt", 0, 0, tiled=True)
+    all_filters = all_filters.reshape((-1,) + all_filters.shape[2:])
     deep = halo(all_filters, "slab", 1)
     grad_mid = depth_conv(deep, depth_weight[::-1], "DHWIO").astype(jnp.bfloat16)
-    rimmed = halo(grad_mid, ROWS, 2, place)
-    grad_in = plane_conv(rimmed, weight[::-1, ::-1], "HWOI").astype(jnp.bfloat16)
-    return scatter_blocks(grad_in, "chan", 0, 2)
+    grad_in = plane_conv(grad_mid, weight[::-1, ::-1], "HWOI").astype(jnp.bfloat16)
+    place = lambda c, f: c * filts + f
+    c_loc = grad_in.shape[0] // chans
+    pieces = []
+    for j in range(chans):
+        pairs = []
+        for c in range(chans):
+            for f in range(filts):
+                group = c * filts + f
+                pairs.append((place(c, f), place((group + j) % chans, group // chans)))
+        block = lax.dynamic_slice_in_dim(grad_in, ((chan * filts + filt + j) % chans) * c_loc, c_loc, 0)
+        pieces.append(lax.ppermute(block, ROWS, pairs))
+    return order_blocks(pieces, chan, 2)
 
 
 def local(volume, plane_weight, depth_weight, grad_out):
-    weight = gather_blocks(gather_blocks(plane_weight, "filt", 3), "chan", 2)
+    weight = gather_weight(plane_weight)
     output = forward(volume, weight, depth_weight)
     grad_in = backward(grad_out, weight, depth_weight)
     return (output, grad_in)

time: 159 us -> 149 us (0.937)
  the two profiles are of different devices: /device:TPU:1 before, /device:TPU:10 now
where the time goes in v2:
time: 149 us; the launch traced here: 148 us
  waiting for transfers between devices  54.5 us (37%)
  starting transfers between devices  42.8 us (29%)
  local copies, waits for them, and re-layouts  20 us (13%)
  blocking collectives  13.6 us (9%)
  matrix products  8.24 us (6%)
  other arithmetic  7.68 us (5%)
    ppermute x2, waiting for transfers between devices, backward(): pieces.append(lax.ppermute(block, ROWS, pairs))  28.4 us
    all_to_all x1, waiting for transfers between devices, backward(): all_filters = lax.all_to_all(windows, 'filt', 0, 0, tiled=True)  16.3 us
    all_to_all x1, blocking collectives, forward(): all_channels = lax.all_to_all(windows, 'chan', 0, 0, tiled=True)  13.6 us
    ppermute x3, starting transfers between devices, halo(): after = lax.ppermute(lax.slice_in_dim(x, 0, 1, axis=dim), axis, down)  8.76 us
    all_to_all x1, starting transfers between devices, forward(): return lax.all_to_all(out, 'filt', 0, 2, tiled=True)  7.63 us
    unnamed x22, local copies, waits for them, and re-layouts  7.16 us
    all_to_all x1, starting transfers between devices, backward(): all_filters = lax.all_to_all(windows, 'filt', 0, 0, tiled=True)  6.74 us
    ppermute x3, starting transfers between devices, halo(): lax.ppermute(lax.slice_in_dim(x, length - 1, length, axis=dim), axis, up)  6.02 us
  transfers between devices with their start and end apart: 12, of which 7 were waited for; matrix products, arithmetic and copies ran while one was open for 17% of the time, Pallas kernels for 0%

profile of v2, /device:TPU:10, one launch (start us, length us, event | category | flops | bytes accessed | tf_op | source)
XLA Modules:
  0.0 148.0 jit_solution(17619385899020912111)
XLA Ops:
  0.6 2.9 %copy.74 = bf16[128,2,32,128]{3,0,2,1:T(8,128)(2,1)S(1)} copy(bf16[128,2,32,128]{3,2,1,0:T(8,128)(2,1)} %param.4) | data formatting | bytes 4194304 | tf_op args[0]
  3.8 13.6 %all_to_all.38 = bf16[2,128,2,6,128]{4,1,3,2,0:T(8,128)(2,1)S(1)} all-to-all(bf16[2,128,2,6,128]{4,1,3,2,0:T(8,128)(2,1)S(1)} %pad_maximum_fusion.2), channel_id=1, replica_groups=mesh['slab'=4,'chan'=2,'filt'=4] {'chan'}, dimensions={0} | all-to-all | bytes 1572864 | tf_op jit(solution)/shard_map/all_to_all | solution.py:95
  18.4 5.3 %all-to-all-start.1 = ((bf16[4,3,3,128,64]{3,4,2,1,0:T(8,128)(2,1)}), bf16[4,3,3,128,64]{3,4,2,1,0:T(8,128)(2,1)S(1)}, u32[]{:S(2)}, u32[]{:S(2)}) async-start(bf16[4,3,3,128,64]{3,4,2,1,0:T(8,128)(2,1)} %broadcast_in_dim.24), calls=%async_computation.1 | async-start | bytes 1179648 | tf_op jit(solution)/shard_map/all_to_all | solution.py:78
  24.0 2.2 %collective-permute-start.2 = (bf16[64,2,1,128]{3,0,2,1:T(8,128)(2,1)S(1)}, bf16[64,2,1,128]{3,0,2,1:T(8,128)(2,1)S(1)}, u32[]{:S(2)}, u32[]{:S(2)}) collective-permute-start(bf16[64,2,1,128]{3,0,2,1:T(8,128)(2,1)S(1)} %get-tuple-element.20), channel_id=1, source_target_pairs={{0,4},{1,5},{2,6},{3,7},{8,12},{9,13},{10,14},{11,15},{16,20},{17,... | collective-permute-start | bytes 98312 | tf_op jit(solution)/shard_map/ppermute | solution.py:46
  26.2 1.3 collective-permute-start.3
  27.7 4.2 %collective-permute-done.3 = bf16[64,2,1,128]{3,0,2,1:T(8,128)(2,1)S(1)} collective-permute-done((bf16[64,2,1,128]{3,0,2,1:T(8,128)(2,1)S(1)}, bf16[64,2,1,128]{3,0,2,1:T(8,128)(2,1)S(1)}, u32[]{:S(2)}, u32[]{:S(2)}) %collective-permute-start.3) | collective-permute-done | bytes 32800 | tf_op jit(solution)/shard_map/ppermute | solution.py:47
  33.0 2.3 %all-to-all-done.1 = bf16[4,3,3,128,64]{3,4,2,1,0:T(8,128)(2,1)S(1)} async-done(((bf16[4,3,3,128,64]{3,4,2,1,0:T(8,128)(2,1)}), bf16[4,3,3,128,64]{3,4,2,1,0:T(8,128)(2,1)S(1)}, u32[]{:S(2)}, u32[]{:S(2)}) %all-to-all-start.1) | async-done | bytes 589856 | tf_op jit(solution)/shard_map/all_to_all | solution.py:78
  35.3 6.7 %all-to-all-start.4 = ((bf16[4,64,2,6,128]{4,1,3,2,0:T(8,128)(2,1)}), bf16[4,64,2,6,128]{4,1,3,2,0:T(8,128)(2,1)S(1)}, u32[]{:S(2)}, u32[]{:S(2)}) async-start(bf16[4,64,2,6,128]{4,1,3,2,0:T(8,128)(2,1)} %pad_maximum_fusion.3), calls=%async_computation.4 | async-start | bytes 1572864 | tf_op jit(solution)/shard_map/all_to_all | solution.py:111
  42.1 16.3 %all-to-all-done.4 = bf16[4,64,2,6,128]{4,1,3,2,0:T(8,128)(2,1)S(1)} async-done(((bf16[4,64,2,6,128]{4,1,3,2,0:T(8,128)(2,1)}), bf16[4,64,2,6,128]{4,1,3,2,0:T(8,128)(2,1)S(1)}, u32[]{:S(2)}, u32[]{:S(2)}) %all-to-all-start.4) | async-done | bytes 786464 | tf_op jit(solution)/shard_map/all_to_all | solution.py:111
  58.4 1.4 broadcast_in_dim.25
  59.8 3.7 %all-to-all-start.2 = ((bf16[2,4,3,3,128,64]{4,5,1,3,2,0:T(8,128)(2,1)}), bf16[2,4,3,3,128,64]{4,5,1,3,2,0:T(8,128)(2,1)S(1)}, u32[]{:S(2)}, u32[]{:S(2)}) async-start(bf16[2,4,3,3,128,64]{4,5,1,3,2,0:T(8,128)(2,1)} %broadcast_in_dim.25), calls=%async_computation.2 | async-start | bytes 2359296 | tf_op jit(solution)/shard_map/all_to_all | solution.py:80
  65.8 1.7 %fusion.10 = bf16[256,6,2,8,19]{0,2,4,3,1:T(2,128)(2,1)} fusion(bf16[256,6,2,7,2]{0,2,4,3,1:T(2,128)(2,1)S(1)} %slice.48, bf16[256,6,2,8,17]{0,2,4,3,1:T(2,128)(2,1)S(1)} %bitcast.71), kind=kLoop, calls=%fused_computation.20 | loop fusion | flops 2801664 | bytes 1855488 | tf_op jit(solution)/shard_map/conv_general_dilated | solution.py:52
  68.5 1.9 %collective-permute-start.4 = (bf16[256,1,6,128]{3,0,2,1:T(8,128)(2,1)}, bf16[256,1,6,128]{3,0,2,1:T(8,128)(2,1)S(1)}, u32[]{:S(2)}, u32[]{:S(2)}) collective-permute-start(bf16[256,1,6,128]{3,0,2,1:T(8,128)(2,1)} %get-tuple-element.12), channel_id=1, source_target_pairs={{0,8},{8,16},{16,24},{1,9},{9,17},{17,25},{2,10},{10,18},{18,26},{... | collective-permute-start | bytes 1179656 | tf_op jit(solution)/shard_map/ppermute | solution.py:46
  70.4 3.6 %collective-permute-start.5 = (bf16[256,1,6,128]{3,0,2,1:T(8,128)(2,1)}, bf16[256,1,6,128]{3,0,2,1:T(8,128)(2,1)}, u32[]{:S(2)}, u32[]{:S(2)}) collective-permute-start(bf16[256,1,6,128]{3,0,2,1:T(8,128)(2,1)} %get-tuple-element.13), channel_id=1, source_target_pairs={{8,0},{16,8},{24,16},{9,1},{17,9},{25,17},{10,2},{18,10},{26,18},{... | collective-permute-start | bytes 1179656 | tf_op jit(solution)/shard_map/ppermute | solution.py:47
  74.0 3.0 %all-to-all-done.2 = bf16[2,4,3,3,128,64]{4,5,1,3,2,0:T(8,128)(2,1)S(1)} async-done(((bf16[2,4,3,3,128,64]{4,5,1,3,2,0:T(8,128)(2,1)}), bf16[2,4,3,3,128,64]{4,5,1,3,2,0:T(8,128)(2,1)S(1)}, u32[]{:S(2)}, u32[]{:S(2)}) %all-to-all-start.2) | async-done | bytes 1179680 | tf_op jit(solution)/shard_map/all_to_all | solution.py:80
  77.1 1.2 copy.79
  79.1 3.1 %fusion.7 = bf16[4,16,17,256]{3,1,2,0:T(8,128)(2,1)S(1)} fusion(bf16[3,3,256,256]{2,3,1,0:T(8,128)(2,1)S(1)} %reshape.18, bf16[256,6,2,8,19]{0,2,4,3,1:T(2,128)(2,1)} %fusion.10, pred[16,17]{0,1:T(8,128)(4,1)S(1)} %copy-done.7), kind=kOutput, calls=%fused_computation.11 | convolution fusion | flops 1284014080 | bytes 2670864 | tf_op jit(solution)/shard_map/conv_general_dilated | solution.py:52
  83.6 1.9 %collective-permute-start = (bf16[256,1,4,128]{0,2,3,1:T(4,128)(2,1)}, bf16[256,1,4,128]{0,2,3,1:T(4,128)(2,1)}, u32[]{:S(2)}, u32[]{:S(2)}) collective-permute-start(bf16[256,1,4,128]{0,2,3,1:T(4,128)(2,1)} %get-tuple-element.22), channel_id=1, source_target_pairs={{0,8},{8,16},{16,24},{1,9},{9,17},{17,25},{2,10},{10,18},{18,26},{... | collective-permute-start | bytes 786440 | tf_op jit(solution)/shard_map/ppermute | solution.py:46
  85.5 3.8 %collective-permute-start.1 = (bf16[256,1,4,128]{0,2,3,1:T(4,128)(2,1)S(1)}, bf16[256,1,4,128]{0,2,3,1:T(4,128)(2,1)}, u32[]{:S(2)}, u32[]{:S(2)}) collective-permute-start(bf16[256,1,4,128]{0,2,3,1:T(4,128)(2,1)S(1)} %get-tuple-element.23), channel_id=1, source_target_pairs={{8,0},{16,8},{24,16},{9,1},{17,9},{25,17},{10,2},{18,10},{26,18},{... | collective-permute-start | bytes 786440 | tf_op jit(solution)/shard_map/ppermute | solution.py:47
  89.4 1.2 pad_maximum_fusion
  90.6 1.6 %copy.95 = bf16[256,4,6,128]{0,3,2,1:T(8,128)(2,1)} copy(bf16[256,4,6,128]{3,0,2,1:T(8,128)(2,1)S(1)} %pad_maximum_fusion) | data formatting | bytes 3145728 | tf_op jit(solution)/shard_map/concatenate | solution.py:48
  92.2 2.2 %fusion.4 = bf16[2,6,8,16,256]{4,2,3,1,0:T(8,128)(2,1)S(1)} fusion(bf16[256,4,6,8,16]{0,4,3,2,1:T(8,128)(2,1)} %bitcast.79, bf16[3,256,256]{2,1,0:T(8,128)(2,1)S(1)} %copy-done.5), kind=kOutput, calls=%fused_computation.8 | convolution fusion | flops 604372992 | bytes 2752512 | tf_op jit(solution)/shard_map/conv_general_dilated | solution.py:63
  97.1 1.8 %pad_maximum_fusion.1 = bf16[256,4,4,128]{0,2,3,1:T(4,128)(2,1)S(1)} fusion(bf16[256,1,4,128]{0,2,3,1:T(4,128)(2,1)} %collective-permute-done.1, bf16[256,2,4,128]{0,2,3,1:T(4,128)(2,1)S(1)} %slice_bitcast_fusion, bf16[256,1,4,128]{0,2,3,1:T(4,128)(2,1)} %collective-permute-done), kind=kLoop, calls=%fused_computation.14 | loop fusion | flops 1048576 | bytes 2097152 | tf_op jit(solution)/shard_map/concatenate | solution.py:48
  98.9 1.4 convolution_convert_fusion
  100.4 1.1 copy.85
  101.5 7.6 %all-to-all-start.3 = ((bf16[256,2,4,128]{3,2,1,0:T(4,128)(2,1)}), bf16[256,2,4,128]{3,2,1,0:T(4,128)(2,1)S(1)}, u32[]{:S(2)}, u32[]{:S(2)}) async-start(bf16[256,2,4,128]{3,2,1,0:T(4,128)(2,1)} %copy.85), calls=%async_computation.3 | async-start | bytes 1048576 | tf_op jit(solution)/shard_map/all_to_all | solution.py:100
  109.2 1.5 fusion.8
  111.4 4.5 %collective-permute-start.7 = (bf16[128,2,4,128]{0,2,3,1:T(4,128)(2,1)S(1)}, bf16[128,2,4,128]{0,2,3,1:T(4,128)(2,1)S(1)}, u32[]{:S(2)}, u32[]{:S(2)}) collective-permute-start(bf16[128,2,4,128]{0,2,3,1:T(4,128)(2,1)S(1)} %get-tuple-element.14), channel_id=1, source_target_pairs={{0,0},{1,4},{2,1},{3,5},{4,2},{5,6},{6,3},{7,7},{8,8},{9,12},{10,9... | collective-permute-start | bytes 786440 | tf_op jit(solution)/shard_map/ppermute | solution.py:126
  115.9 11.4 %collective-permute-done.6 = bf16[128,2,4,128]{0,2,3,1:T(4,128)(2,1)S(1)} collective-permute-done((bf16[128,2,4,128]{0,2,3,1:T(4,128)(2,1)S(1)}, bf16[128,2,4,128]{0,2,3,1:T(4,128)(2,1)S(1)}, u32[]{:S(2)}, u32[]{:S(2)}) %collective-permute-start.6) | collective-permute-done | bytes 262176 | tf_op jit(solution)/shard_map/ppermute | solution.py:126
  127.4 17.0 %collective-permute-done.7 = bf16[128,2,4,128]{0,2,3,1:T(4,128)(2,1)S(1)} collective-permute-done((bf16[128,2,4,128]{0,2,3,1:T(4,128)(2,1)S(1)}, bf16[128,2,4,128]{0,2,3,1:T(4,128)(2,1)S(1)}, u32[]{:S(2)}, u32[]{:S(2)}) %collective-permute-start.7) | collective-permute-done | bytes 262176 | tf_op jit(solution)/shard_map/ppermute | solution.py:126
  145.4 1.3 copy.103
  146.9 1.1 copy.102
  (54 shorter events, 12.7 us)
Async XLA Ops:
  3.7 13.7 %copy-start.6 = (bf16[3,3,128,64]{2,3,1,0:T(8,128)(2,1)S(1)}, bf16[3,3,128,64]{2,3,1,0:T(8,128)(2,1)}, u32[]{:S(2)}) copy-start(bf16[3,3,128,64]{2,3,1,0:T(8,128)(2,1)} %param.5) | copy-start | bytes 442372
  3.8 19.9 %copy-start.2 = (bf16[64,2,16,128]{3,2,1,0:T(8,128)(2,1)S(1)}, bf16[64,2,16,128]{3,2,1,0:T(8,128)(2,1)}, u32[]{:S(2)}) copy-start(bf16[64,2,16,128]{3,2,1,0:T(8,128)(2,1)} %param.7) | copy-start | bytes 1572868
  18.4 16.9 %all-to-all-start.1 = ((bf16[4,3,3,128,64]{3,4,2,1,0:T(8,128)(2,1)}), bf16[4,3,3,128,64]{3,4,2,1,0:T(8,128)(2,1)S(1)}, u32[]{:S(2)}, u32[]{:S(2)}) async-start(bf16[4,3,3,128,64]{3,4,2,1,0:T(8,128)(2,1)} %broadcast_in_dim.24), calls=%async_computation.1 | async-start | bytes 1179648 | tf_op jit(solution)/shard_map/all_to_all | solution.py:78
  24.0 3.8 %collective-permute-start.2 = (bf16[64,2,1,128]{3,0,2,1:T(8,128)(2,1)S(1)}, bf16[64,2,1,128]{3,0,2,1:T(8,128)(2,1)S(1)}, u32[]{:S(2)}, u32[]{:S(2)}) collective-permute-start(bf16[64,2,1,128]{3,0,2,1:T(8,128)(2,1)S(1)} %get-tuple-element.20), channel_id=1, source_target_pairs={{0,4},{1,5},{2,6},{3,7},{8,12},{9,13},{10,14},{11,15},{16,20},{17,... | collective-permute-start | bytes 98312 | tf_op jit(solution)/shard_map/ppermute | solution.py:46
  26.2 5.8 %collective-permute-start.3 = (bf16[64,2,1,128]{3,0,2,1:T(8,128)(2,1)S(1)}, bf16[64,2,1,128]{3,0,2,1:T(8,128)(2,1)S(1)}, u32[]{:S(2)}, u32[]{:S(2)}) collective-permute-start(bf16[64,2,1,128]{3,0,2,1:T(8,128)(2,1)S(1)} %get-tuple-element.21), channel_id=1, source_target_pairs={{4,0},{5,1},{6,2},{7,3},{12,8},{13,9},{14,10},{15,11},{20,16},{21,... | collective-permute-start | bytes 98312 | tf_op jit(solution)/shard_map/ppermute | solution.py:47
  35.3 23.1 %all-to-all-start.4 = ((bf16[4,64,2,6,128]{4,1,3,2,0:T(8,128)(2,1)}), bf16[4,64,2,6,128]{4,1,3,2,0:T(8,128)(2,1)S(1)}, u32[]{:S(2)}, u32[]{:S(2)}) async-start(bf16[4,64,2,6,128]{4,1,3,2,0:T(8,128)(2,1)} %pad_maximum_fusion.3), calls=%async_computation.4 | async-start | bytes 1572864 | tf_op jit(solution)/shard_map/all_to_all | solution.py:111
  59.8 3.8 %copy-start.3 = (bf16[3,256,256]{2,1,0:T(8,128)(2,1)S(1)}, bf16[3,256,256]{2,1,0:T(8,128)(2,1)}, u32[]{:S(2)}) copy-start(bf16[3,256,256]{2,1,0:T(8,128)(2,1)} %param.6) | copy-start | bytes 1179652
  59.8 17.3 %all-to-all-start.2 = ((bf16[2,4,3,3,128,64]{4,5,1,3,2,0:T(8,128)(2,1)}), bf16[2,4,3,3,128,64]{4,5,1,3,2,0:T(8,128)(2,1)S(1)}, u32[]{:S(2)}, u32[]{:S(2)}) async-start(bf16[2,4,3,3,128,64]{4,5,1,3,2,0:T(8,128)(2,1)} %broadcast_in_dim.25), calls=%async_computation.2 | async-start | bytes 2359296 | tf_op jit(solution)/shard_map/all_to_all | solution.py:80
  68.5 20.9 %collective-permute-start.4 = (bf16[256,1,6,128]{3,0,2,1:T(8,128)(2,1)}, bf16[256,1,6,128]{3,0,2,1:T(8,128)(2,1)S(1)}, u32[]{:S(2)}, u32[]{:S(2)}) collective-permute-start(bf16[256,1,6,128]{3,0,2,1:T(8,128)(2,1)} %get-tuple-element.12), channel_id=1, source_target_pairs={{0,8},{8,16},{16,24},{1,9},{9,17},{17,25},{2,10},{10,18},{18,26},{... | collective-permute-start | bytes 1179656 | tf_op jit(solution)/shard_map/ppermute | solution.py:46
  70.4 19.0 %collective-permute-start.5 = (bf16[256,1,6,128]{3,0,2,1:T(8,128)(2,1)}, bf16[256,1,6,128]{3,0,2,1:T(8,128)(2,1)}, u32[]{:S(2)}, u32[]{:S(2)}) collective-permute-start(bf16[256,1,6,128]{3,0,2,1:T(8,128)(2,1)} %get-tuple-element.13), channel_id=1, source_target_pairs={{8,0},{16,8},{24,16},{9,1},{17,9},{25,17},{10,2},{18,10},{26,18},{... | collective-permute-start | bytes 1179656 | tf_op jit(solution)/shard_map/ppermute | solution.py:47
  78.3 0.8 copy-start.7
  79.1 3.1 %copy-start = (bf16[3,3,256,256]{2,3,1,0:T(8,128)(2,1)}, bf16[3,3,256,256]{2,3,1,0:T(8,128)(2,1)S(1)}, u32[]{:S(2)}) copy-start(bf16[3,3,256,256]{2,3,1,0:T(8,128)(2,1)S(1)} %reshape.18) | copy-start | bytes 3538948
  83.6 13.4 %collective-permute-start = (bf16[256,1,4,128]{0,2,3,1:T(4,128)(2,1)}, bf16[256,1,4,128]{0,2,3,1:T(4,128)(2,1)}, u32[]{:S(2)}, u32[]{:S(2)}) collective-permute-start(bf16[256,1,4,128]{0,2,3,1:T(4,128)(2,1)} %get-tuple-element.22), channel_id=1, source_target_pairs={{0,8},{8,16},{16,24},{1,9},{9,17},{17,25},{2,10},{10,18},{18,26},{... | collective-permute-start | bytes 786440 | tf_op jit(solution)/shard_map/ppermute | solution.py:46
  85.5 11.5 %collective-permute-start.1 = (bf16[256,1,4,128]{0,2,3,1:T(4,128)(2,1)S(1)}, bf16[256,1,4,128]{0,2,3,1:T(4,128)(2,1)}, u32[]{:S(2)}, u32[]{:S(2)}) collective-permute-start(bf16[256,1,4,128]{0,2,3,1:T(4,128)(2,1)S(1)} %get-tuple-element.23), channel_id=1, source_target_pairs={{8,0},{16,8},{24,16},{9,1},{17,9},{25,17},{10,2},{18,10},{26,18},{... | collective-permute-start | bytes 786440 | tf_op jit(solution)/shard_map/ppermute | solution.py:47
  90.6 1.6 %copy-start.5 = (bf16[3,256,256]{2,1,0:T(8,128)(2,1)S(1)}, bf16[3,256,256]{2,1,0:T(8,128)(2,1)}, u32[]{:S(2)}) copy-start(bf16[3,256,256]{2,1,0:T(8,128)(2,1)} %rev.4) | copy-start | bytes 1179652
  96.2 2.7 %copy-start.4 = (bf16[3,256,256]{2,1,0:T(8,128)(2,1)S(1)}, bf16[3,256,256]{2,1,0:T(8,128)(2,1)}, u32[]{:S(2)}) copy-start(bf16[3,256,256]{2,1,0:T(8,128)(2,1)} %param.6) | copy-start | bytes 1179652
  100.3 8.8 %copy-start.1 = (bf16[3,3,256,256]{2,3,1,0:T(8,128)(2,1)S(1)}, bf16[3,3,256,256]{2,3,1,0:T(8,128)(2,1)}, u32[]{:S(2)}) copy-start(bf16[3,3,256,256]{2,3,1,0:T(8,128)(2,1)} %copy-done) | copy-start | bytes 3538948
  101.5 45.2 %all-to-all-start.3 = ((bf16[256,2,4,128]{3,2,1,0:T(4,128)(2,1)}), bf16[256,2,4,128]{3,2,1,0:T(4,128)(2,1)S(1)}, u32[]{:S(2)}, u32[]{:S(2)}) async-start(bf16[256,2,4,128]{3,2,1,0:T(4,128)(2,1)} %copy.85), calls=%async_computation.3 | async-start | bytes 1048576 | tf_op jit(solution)/shard_map/all_to_all | solution.py:100
  111.3 16.1 %collective-permute-start.6 = (bf16[128,2,4,128]{0,2,3,1:T(4,128)(2,1)S(1)}, bf16[128,2,4,128]{0,2,3,1:T(4,128)(2,1)S(1)}, u32[]{:S(2)}, u32[]{:S(2)}) collective-permute-start(bf16[128,2,4,128]{0,2,3,1:T(4,128)(2,1)S(1)} %get-tuple-element.15), channel_id=1, source_target_pairs={{0,4},{1,0},{2,5},{3,1},{4,6},{5,2},{6,7},{7,3},{8,12},{9,8},{10,1... | collective-permute-start | bytes 786440 | tf_op jit(solution)/shard_map/ppermute | solution.py:126
  111.4 32.9 %collective-permute-start.7 = (bf16[128,2,4,128]{0,2,3,1:T(4,128)(2,1)S(1)}, bf16[128,2,4,128]{0,2,3,1:T(4,128)(2,1)S(1)}, u32[]{:S(2)}, u32[]{:S(2)}) collective-permute-start(bf16[128,2,4,128]{0,2,3,1:T(4,128)(2,1)S(1)} %get-tuple-element.14), channel_id=1, source_target_pairs={{0,0},{1,4},{2,1},{3,5},{4,2},{5,6},{6,3},{7,7},{8,8},{9,12},{10,9... | collective-permute-start | bytes 786440 | tf_op jit(solution)/shard_map/ppermute | solution.py:126

commit v3 on v1

--- a/solution.py
+++ b/solution.py
@@ -71,23 +71,39 @@
     return out[0]
 
 
+def gather_weight(weight):
+    filts = lax.axis_size("filt")
+    chans = lax.axis_size("chan")
+    slabs = lax.axis_size("slab")
+    core = lax.axis_index("slab") % 2
+    c_loc, m_loc = weight.shape[2:]
+    half = c_loc // 2
+    mine = lax.dynamic_slice_in_dim(weight, core * half, half, 2)
+    spread = jnp.broadcast_to(mine[None], (filts,) + mine.shape)
+    by_filt = lax.all_to_all(spread, "filt", 0, 0, tiled=True)
+    spread = jnp.broadcast_to(by_filt[None], (chans,) + by_filt.shape)
+    both = lax.all_to_all(spread, "chan", 0, 0, tiled=True)
+    other = lax.ppermute(both, "slab", [(i, i ^ 1) for i in range(slabs)])
+    halves = jnp.where(core == 0, jnp.stack([both, other]), jnp.stack([other, both]))
+    whole = jnp.transpose(halves, (3, 4, 1, 0, 5, 2, 6))
+    return whole.reshape(3, 3, chans * c_loc, filts * m_loc)
+
+
 def forward(volume, weight, depth_weight):
     chans = lax.axis_size("chan")
     filts = lax.axis_size("filt")
-    chan = lax.axis_index("chan")
     filt = lax.axis_index("filt")
     rows = volume.shape[2] // (chans * filts)
     padded = jnp.pad(volume, ((0, 0), (0, 0), (1, 1), (0, 0)))
-    window = lambda group: lax.dynamic_slice_in_dim(padded, group * rows, rows + 2, 2)
-    pieces = [window(chan * filts + filt)]
-    for k in range(1, chans):
-        target = (chan + k) % chans
-        pieces.append(lax.ppermute(window(target * filts + filt), "chan", shift_pairs(chans, k)))
-    all_channels = order_blocks(pieces, chan, 0)
+    windows = jnp.stack(
+        [lax.dynamic_slice_in_dim(padded, (t * filts + filt) * rows, rows + 2, 2) for t in range(chans)]
+    )
+    all_channels = lax.all_to_all(windows, "chan", 0, 0, tiled=True)
+    all_channels = all_channels.reshape((-1,) + all_channels.shape[2:])
     mid = plane_conv(all_channels, weight, "HWIO").astype(jnp.bfloat16)
     deep = halo(mid, "slab", 1)
     out = depth_conv(deep, depth_weight, "DHWOI").astype(jnp.bfloat16)
-    return scatter_blocks(out, "filt", 0, 2)
+    return lax.all_to_all(out, "filt", 0, 2, tiled=True)
 
 
 def backward(grad_out, weight, depth_weight):
@@ -96,24 +112,22 @@
     chan = lax.axis_index("chan")
     filt = lax.axis_index("filt")
     rows = grad_out.shape[2] // filts
-    group = filt * chans + chan
-    own = group % filts
     place = lambda g: (g % chans) * filts + g // chans
     pieces = []
     for k in range(filts):
         pairs = [(c * filts + f, place(c * filts + (f + k) % filts)) for f in range(filts) for c in range(chans)]
         block = lax.dynamic_slice_in_dim(grad_out, ((filt + k) % filts) * rows, rows, 2)
         pieces.append(lax.ppermute(block, ROWS, pairs))
-    all_filters = order_blocks(pieces, own, 0)
+    all_filters = order_blocks(pieces, (filt * chans + chan) % filts, 0)
     deep = halo(all_filters, "slab", 1)
     grad_mid = depth_conv(deep, depth_weight[::-1], "DHWIO").astype(jnp.bfloat16)
     rimmed = halo(grad_mid, ROWS, 2, place)
     grad_in = plane_conv(rimmed, weight[::-1, ::-1], "HWOI").astype(jnp.bfloat16)
-    return scatter_blocks(grad_in, "chan", 0, 2)
+    return lax.all_to_all(grad_in, "chan", 0, 2, tiled=True)
 
 
 def local(volume, plane_weight, depth_weight, grad_out):
-    weight = gather_blocks(gather_blocks(plane_weight, "filt", 3), "chan", 2)
+    weight = gather_weight(plane_weight)
     output = forward(volume, weight, depth_weight)
     grad_in = backward(grad_out, weight, depth_weight)
     return (output, grad_in)

time: 159 us -> 160 us (level); the launches traced: 158 us -> 157 us
  starting transfers between devices: 79.3 us -> 62.8 us
  local copies, waits for them, and re-layouts: 26.9 us -> 35.4 us
  waiting for transfers between devices: 35.4 us -> 42.2 us
    ppermute x9 -> x1, starting transfers between devices: 49.3 us -> 1.74 us  [gather_weight(): other = lax.ppermute(both, 'slab', [(i, i ^ 1) for i in range(slabs)])]
    all_to_all x0 -> x5, starting transfers between devices: none -> 31.6 us  [the longest x1 10.7 us: backward(): return lax.all_to_all(grad_in, 'chan', 0, 2, tiled=True)]
    all_to_all x0 -> x5, waiting for transfers between devices: none -> 23.7 us  [the longest x1 12.8 us: forward(): return lax.all_to_all(out, 'filt', 0, 2, tiled=True)]
    ppermute x9 -> x1, waiting for transfers between devices: 18.9 us -> 0.01 us  [gather_weight(): other = lax.ppermute(both, 'slab', [(i, i ^ 1) for i in range(slabs)])]
    ppermute x4, waiting for transfers between devices: 6.25 us -> 18.6 us  [backward(): pieces.append(lax.ppermute(block, ROWS, pairs))]
    ppermute x3, waiting for transfers between devices: 8.83 us -> 0.01 us  [halo(): lax.ppermute(lax.slice_in_dim(x, length - 1, length, axis=dim), axis, up)]
    unnamed x36 -> x30, local copies, waits for them, and re-layouts: 9.96 us -> 17.1 us
    dynamic_slice x1 -> x0, other arithmetic: 3.41 us -> none  [order_blocks(): return jnp.roll(stacked, (me + 1) * block, axis=dim)]
  transfers between devices with their start and end apart: 19 -> 16, of which waited for: 7 -> 4; matrix products, arithmetic and copies ran while one was open for 21% -> 24% of each run, Pallas kernels for 0% -> 0%
where the time goes in v3:
time: 160 us; the launch traced here: 157 us
  starting transfers between devices  62.8 us (39%)
  waiting for transfers between devices  42.2 us (26%)
  local copies, waits for them, and re-layouts  35.4 us (22%)
  other arithmetic  9.62 us (6%)
  matrix products  6.26 us (4%)
    ppermute x4, waiting for transfers between devices, backward(): pieces.append(lax.ppermute(block, ROWS, pairs))  18.6 us
    unnamed x30, local copies, waits for them, and re-layouts  17.1 us
    ppermute x4, starting transfers between devices, backward(): pieces.append(lax.ppermute(block, ROWS, pairs))  12.8 us
    all_to_all x1, waiting for transfers between devices, forward(): return lax.all_to_all(out, 'filt', 0, 2, tiled=True)  12.8 us
    all_to_all x1, starting transfers between devices, backward(): return lax.all_to_all(grad_in, 'chan', 0, 2, tiled=True)  10.7 us
    ppermute x3, starting transfers between devices, halo(): lax.ppermute(lax.slice_in_dim(x, length - 1, length, axis=dim), axis, up)  10.3 us
    all_to_all x1, starting transfers between devices, forward(): return lax.all_to_all(out, 'filt', 0, 2, tiled=True)  8.08 us
    ppermute x3, starting transfers between devices, halo(): after = lax.ppermute(lax.slice_in_dim(x, 0, 1, axis=dim), axis, down)  6.37 us
  transfers between devices with their start and end apart: 16, of which 4 were waited for; matrix products, arithmetic and copies ran while one was open for 24% of the time, Pallas kernels for 0%

profile of v3, /device:TPU:1, one launch (start us, length us, event | category | flops | bytes accessed | tf_op | source)
XLA Modules:
  0.0 157.5 jit_solution(8529260373055933776)
XLA Ops:
  0.7 1.5 constant_dynamic-slice_fusion.3
  3.1 5.0 %collective-permute-start.3 = (bf16[64,2,4,128]{0,3,2,1:T(8,128)(2,1)}, bf16[64,2,4,128]{0,3,2,1:T(8,128)(2,1)S(1)}, u32[]{:S(2)}, u32[]{:S(2)}) collective-permute-start(bf16[64,2,4,128]{0,3,2,1:T(8,128)(2,1)} %copy.169), channel_id=1, source_target_pairs={{0,5},{4,7},{1,0},{5,2},{2,4},{6,6},{3,1},{7,3},{8,13},{12,15},{9,... | collective-permute-start | bytes 393224 | tf_op jit(solution)/shard_map/ppermute | solution.py:120
  9.8 4.2 %collective-permute-start.5 = (bf16[64,2,4,128]{0,3,2,1:T(8,128)(2,1)}, bf16[64,2,4,128]{0,3,2,1:T(8,128)(2,1)S(1)}, u32[]{:S(2)}, u32[]{:S(2)}) collective-permute-start(bf16[64,2,4,128]{0,3,2,1:T(8,128)(2,1)} %copy.171), channel_id=1, source_target_pairs={{0,4},{4,6},{1,1},{5,3},{2,5},{6,7},{3,0},{7,2},{8,12},{12,14},{9,... | collective-permute-start | bytes 393224 | tf_op jit(solution)/shard_map/ppermute | solution.py:120
  14.9 3.6 %collective-permute-start.6 = (bf16[64,2,4,128]{0,3,2,1:T(8,128)(2,1)}, bf16[64,2,4,128]{0,3,2,1:T(8,128)(2,1)}, u32[]{:S(2)}, u32[]{:S(2)}) collective-permute-start(bf16[64,2,4,128]{0,3,2,1:T(8,128)(2,1)} %copy.172), channel_id=1, source_target_pairs={{0,0},{4,2},{1,4},{5,6},{2,1},{6,3},{3,5},{7,7},{8,8},{12,10},{9,1... | collective-permute-start | bytes 393224 | tf_op jit(solution)/shard_map/ppermute | solution.py:120
  20.0 5.8 %all-to-all-start.1 = ((bf16[4,2,18432]{2,1,0:T(2,128)(2,1)}), bf16[4,2,18432]{2,1,0:T(2,128)(2,1)}, u32[]{:S(2)}, u32[]{:S(2)}) async-start(bf16[4,2,18432]{2,1,0:T(2,128)(2,1)} %reshape.64), calls=%async_computation.1 | async-start | bytes 589824 | tf_op jit(solution)/shard_map/all_to_all | solution.py:83
  25.9 2.9 %copy.137 = bf16[128,2,32,128]{3,0,2,1:T(8,128)(2,1)S(1)} copy(bf16[128,2,32,128]{3,2,1,0:T(8,128)(2,1)} %param.4) | data formatting | bytes 4194304 | tf_op args[0]
  28.9 18.5 %collective-permute-done.4 = bf16[64,2,4,128]{0,3,2,1:T(8,128)(2,1)S(1)} collective-permute-done((bf16[64,2,4,128]{0,3,2,1:T(8,128)(2,1)}, bf16[64,2,4,128]{0,3,2,1:T(8,128)(2,1)S(1)}, u32[]{:S(2)}, u32[]{:S(2)}) %collective-permute-start.4) | collective-permute-done | bytes 131104 | tf_op jit(solution)/shard_map/ppermute | solution.py:120
  48.8 2.7 %concatenate.16 = bf16[512,2,4,128]{0,3,2,1:T(8,128)(2,1)S(1)} concatenate(bf16[64,2,4,128]{0,3,2,1:T(8,128)(2,1)S(1)} %collective-permute-done.3, bf16[64,2,4,128]{0,3,2,1:T(8,128)(2,1)} %copy-done.2, bf16[64,2,4,128]{0,3,2,1:T(8,128)(2,1)} %copy-done.3, bf16[64,2,4,128]{0,3,2,1:T(8,128)(2,1)} %collective-permute-done.6, bf16[64,2,4,128]{0,3,2,1:T(8,128)(2,1)S(1)} %collective-permute-done.3, ...), dimensions={0} | concatenate | bytes 2097152 | tf_op jit(solution)/shard_map/jit(_roll_dynamic)/concatenate | solution.py:19
  52.5 2.6 %collective-permute-start.8 = (bf16[256,1,4,128]{0,3,2,1:T(8,128)(2,1)}, bf16[256,1,4,128]{0,3,2,1:T(8,128)(2,1)}, u32[]{:S(2)}, u32[]{:S(2)}) collective-permute-start(bf16[256,1,4,128]{0,3,2,1:T(8,128)(2,1)} %get-tuple-element.15), channel_id=1, source_target_pairs={{8,0},{16,8},{24,16},{9,1},{17,9},{25,17},{10,2},{18,10},{26,18},{... | collective-permute-start | bytes 786440 | tf_op jit(solution)/shard_map/ppermute | solution.py:47
  55.1 3.0 %collective-permute-start.7 = (bf16[256,1,4,128]{0,3,2,1:T(8,128)(2,1)S(1)}, bf16[256,1,4,128]{0,3,2,1:T(8,128)(2,1)}, u32[]{:S(2)}, u32[]{:S(2)}) collective-permute-start(bf16[256,1,4,128]{0,3,2,1:T(8,128)(2,1)S(1)} %get-tuple-element.14), channel_id=1, source_target_pairs={{0,8},{8,16},{16,24},{1,9},{9,17},{17,25},{2,10},{10,18},{18,26},{... | collective-permute-start | bytes 786440 | tf_op jit(solution)/shard_map/ppermute | solution.py:46
  60.1 2.1 %pad_maximum_fusion.2 = bf16[2,128,2,6,128]{4,1,3,2,0:T(8,128)(2,1)} fusion(bf16[1,128,2,6,128]{4,1,3,2,0:T(8,128)(2,1)} %get-tuple-element.13, bf16[1,128,2,6,128]{4,1,3,2,0:T(8,128)(2,1)} %get-tuple-element.12), kind=kLoop, calls=%fused_computation.23 | loop fusion | flops 393216 | bytes 1572864 | tf_op jit(solution)/shard_map/stack | solution.py:98
  63.6 3.5 %all-to-all-start = ((bf16[2,128,2,6,128]{4,1,3,2,0:T(8,128)(2,1)}), bf16[2,128,2,6,128]{4,1,3,2,0:T(8,128)(2,1)S(1)}, u32[]{:S(2)}, u32[]{:S(2)}) async-start(bf16[2,128,2,6,128]{4,1,3,2,0:T(8,128)(2,1)} %pad_maximum_fusion.2), calls=%async_computation | async-start | bytes 1572864 | tf_op jit(solution)/shard_map/all_to_all | solution.py:101
  67.9 1.4 reshape.65
  70.2 1.7 %reshape.66 = bf16[2,2,73728]{2,1,0:T(2,128)(2,1)} reshape(bf16[2,3,3,64,4,64]{5,4,3,2,1,0:T(4,128)(2,1)S(1)} %broadcast_bitcast_fusion) | data formatting | bytes 1179648
  71.9 6.1 %all-to-all-done = bf16[2,128,2,6,128]{4,1,3,2,0:T(8,128)(2,1)S(1)} async-done(((bf16[2,128,2,6,128]{4,1,3,2,0:T(8,128)(2,1)}), bf16[2,128,2,6,128]{4,1,3,2,0:T(8,128)(2,1)S(1)}, u32[]{:S(2)}, u32[]{:S(2)}) %all-to-all-start) | async-done | bytes 786464 | tf_op jit(solution)/shard_map/all_to_all | solution.py:101
  78.0 3.5 %all-to-all-start.2 = ((bf16[2,2,73728]{2,1,0:T(2,128)(2,1)}), bf16[2,2,73728]{2,1,0:T(2,128)(2,1)S(1)}, u32[]{:S(2)}, u32[]{:S(2)}) async-start(bf16[2,2,73728]{2,1,0:T(2,128)(2,1)} %reshape.66), calls=%async_computation.2 | async-start | bytes 1179648 | tf_op jit(solution)/shard_map/all_to_all | solution.py:85
  82.3 1.3 collective-permute-start.10
  83.6 4.2 %collective-permute-start.9 = (bf16[256,2,1,128]{0,3,2,1:T(8,128)(2,1)}, bf16[256,2,1,128]{0,3,2,1:T(8,128)(2,1)S(1)}, u32[]{:S(2)}, u32[]{:S(2)}) collective-permute-start(bf16[256,2,1,128]{0,3,2,1:T(8,128)(2,1)} %get-tuple-element.16), channel_id=1, source_target_pairs={{0,4},{4,1},{1,5},{5,2},{2,6},{6,3},{3,7},{8,12},{12,9},{9,13},{13... | collective-permute-start | bytes 393224 | tf_op jit(solution)/shard_map/ppermute | solution.py:46
  89.2 1.6 %fusion.7 = bf16[256,6,2,8,19]{0,2,4,3,1:T(2,128)(2,1)} fusion(bf16[256,6,2,7,2]{0,2,4,3,1:T(2,128)(2,1)S(1)} %slice.30, bf16[256,6,2,8,17]{0,2,4,3,1:T(2,128)(2,1)S(1)} %bitcast.68), kind=kLoop, calls=%fused_computation.17 | loop fusion | flops 2801664 | bytes 1855488 | tf_op jit(solution)/shard_map/conv_general_dilated | solution.py:52
  91.7 1.7 %collective-permute-start = (bf16[2,4,3,3,64,64]{5,1,4,3,2,0:T(4,128)(2,1)S(1)}, bf16[2,4,3,3,64,64]{5,1,4,3,2,0:T(4,128)(2,1)S(1)}, u32[]{:S(2)}, u32[]{:S(2)}) collective-permute-start(bf16[2,4,3,3,64,64]{5,1,4,3,2,0:T(4,128)(2,1)S(1)} %bitcast.64), channel_id=1, source_target_pairs={{0,8},{8,0},{16,24},{24,16},{1,9},{9,1},{17,25},{25,17},{2,10},{10... | collective-permute-start | bytes 1769480 | tf_op jit(solution)/shard_map/ppermute | solution.py:86
  95.0 1.6 %fusion.8 = bf16[256,6,2,8,19]{0,2,4,3,1:T(2,128)(2,1)} fusion(bf16[256,6,2,7,2]{0,2,4,3,1:T(2,128)(2,1)S(1)} %slice.36, bf16[256,6,2,8,17]{0,2,4,3,1:T(2,128)(2,1)S(1)} %bitcast.66), kind=kLoop, calls=%fused_computation.18 | loop fusion | flops 2801664 | bytes 1855488 | tf_op jit(solution)/shard_map/conv_general_dilated | solution.py:52
  97.2 2.2 %fusion = bf16[3,3,2,2,64,4,64]{6,5,4,1,0,2,3:T(4,128)(2,1)S(1)} fusion(bf16[1,2,4,3,3,64,64]{6,2,5,4,3,1,0:T(4,128)(2,1)S(1)} %bitcast.79, bf16[1,2,4,3,3,64,64]{6,2,5,4,3,1,0:T(4,128)(2,1)S(1)} %bitcast_bitcast_fusion, pred[]{:T(512)S(6)} %eq.13), kind=kLoop, calls=%fused_computation.1 | loop fusion | flops 1769472 | bytes 2359297 | tf_op jit(solution)/shard_map/transpose | solution.py:88
  100.4 2.5 %reshape.15 = bf16[3,3,256,256]{3,2,1,0:T(8,128)(2,1)} reshape(bf16[3,3,2,2,64,4,64]{6,5,4,3,2,1,0:T(4,128)(2,1)S(1)} %copy.143) | data formatting | bytes 2359296 | tf_op jit(solution)/shard_map/reshape | solution.py:89
  102.9 2.7 %fusion.3 = bf16[4,16,17,256]{3,1,2,0:T(8,128)(2,1)S(1)} fusion(bf16[3,3,256,256]{3,2,1,0:T(8,128)(2,1)} %reshape.15, bf16[256,6,2,8,19]{0,2,4,3,1:T(2,128)(2,1)S(1)} %copy-done.4, pred[16,17]{0,1:T(8,128)(4,1)S(1)} %copy-done.7), kind=kOutput, calls=%fused_computation.9 | convolution fusion | flops 1284014080 | bytes 2670864 | tf_op jit(solution)/shard_map/conv_general_dilated | solution.py:52
  106.3 2.5 %collective-permute-start.2 = (bf16[256,1,4,128]{0,2,3,1:T(4,128)(2,1)S(1)}, bf16[256,1,4,128]{0,2,3,1:T(4,128)(2,1)S(1)}, u32[]{:S(2)}, u32[]{:S(2)}) collective-permute-start(bf16[256,1,4,128]{0,2,3,1:T(4,128)(2,1)S(1)} %get-tuple-element.23), channel_id=1, source_target_pairs={{8,0},{16,8},{24,16},{9,1},{17,9},{25,17},{10,2},{18,10},{26,18},{... | collective-permute-start | bytes 786440 | tf_op jit(solution)/shard_map/ppermute | solution.py:47
  108.8 3.1 %collective-permute-start.1 = (bf16[256,1,4,128]{0,2,3,1:T(4,128)(2,1)S(1)}, bf16[256,1,4,128]{0,2,3,1:T(4,128)(2,1)S(1)}, u32[]{:S(2)}, u32[]{:S(2)}) collective-permute-start(bf16[256,1,4,128]{0,2,3,1:T(4,128)(2,1)S(1)} %get-tuple-element.22), channel_id=1, source_target_pairs={{0,8},{8,16},{16,24},{1,9},{9,17},{17,25},{2,10},{10,18},{18,26},{... | collective-permute-start | bytes 786440 | tf_op jit(solution)/shard_map/ppermute | solution.py:46
  111.9 1.5 fusion.4
  115.2 10.7 %all-to-all-start.4 = ((bf16[256,2,4,128]{3,2,1,0:T(4,128)(2,1)}), bf16[256,2,4,128]{3,2,1,0:T(4,128)(2,1)S(1)}, u32[]{:S(2)}, u32[]{:S(2)}) async-start(bf16[256,2,4,128]{3,2,1,0:T(4,128)(2,1)} %copy.162), calls=%async_computation.4 | async-start | bytes 1048576 | tf_op jit(solution)/shard_map/all_to_all | solution.py:126
  126.7 1.4 convolution_convert_fusion.1
  129.3 4.8 %all-to-all-done.4 = bf16[256,2,4,128]{3,2,1,0:T(4,128)(2,1)S(1)} async-done(((bf16[256,2,4,128]{3,2,1,0:T(4,128)(2,1)}), bf16[256,2,4,128]{3,2,1,0:T(4,128)(2,1)S(1)}, u32[]{:S(2)}, u32[]{:S(2)}) %all-to-all-start.4) | async-done | bytes 524320 | tf_op jit(solution)/shard_map/all_to_all | solution.py:126
  134.1 8.1 %all-to-all-start.3 = ((bf16[256,2,4,128]{3,2,1,0:T(4,128)(2,1)}), bf16[256,2,4,128]{3,2,1,0:T(4,128)(2,1)S(1)}, u32[]{:S(2)}, u32[]{:S(2)}) async-start(bf16[256,2,4,128]{3,2,1,0:T(4,128)(2,1)} %copy.149), calls=%async_computation.3 | async-start | bytes 1048576 | tf_op jit(solution)/shard_map/all_to_all | solution.py:106
  143.4 12.8 %all-to-all-done.3 = bf16[256,2,4,128]{3,2,1,0:T(4,128)(2,1)S(1)} async-done(((bf16[256,2,4,128]{3,2,1,0:T(4,128)(2,1)}), bf16[256,2,4,128]{3,2,1,0:T(4,128)(2,1)S(1)}, u32[]{:S(2)}, u32[]{:S(2)}) %all-to-all-start.3) | async-done | bytes 524320 | tf_op jit(solution)/shard_map/all_to_all | solution.py:106
  (73 shorter events, 25.3 us)
Async XLA Ops:
  0.6 17.9 %copy-start = (bf16[3,3,128,64]{2,3,1,0:T(8,128)(2,1)S(1)}, bf16[3,3,128,64]{2,3,1,0:T(8,128)(2,1)}, u32[]{:S(2)}) copy-start(bf16[3,3,128,64]{2,3,1,0:T(8,128)(2,1)} %param.5) | copy-start | bytes 442372
  3.1 25.8 %collective-permute-start.3 = (bf16[64,2,4,128]{0,3,2,1:T(8,128)(2,1)}, bf16[64,2,4,128]{0,3,2,1:T(8,128)(2,1)S(1)}, u32[]{:S(2)}, u32[]{:S(2)}) collective-permute-start(bf16[64,2,4,128]{0,3,2,1:T(8,128)(2,1)} %copy.169), channel_id=1, source_target_pairs={{0,5},{4,7},{1,0},{5,2},{2,4},{6,6},{3,1},{7,3},{8,13},{12,15},{9,... | collective-permute-start | bytes 393224 | tf_op jit(solution)/shard_map/ppermute | solution.py:120
  8.9 38.5 %collective-permute-start.4 = (bf16[64,2,4,128]{0,3,2,1:T(8,128)(2,1)}, bf16[64,2,4,128]{0,3,2,1:T(8,128)(2,1)S(1)}, u32[]{:S(2)}, u32[]{:S(2)}) collective-permute-start(bf16[64,2,4,128]{0,3,2,1:T(8,128)(2,1)} %copy.170), channel_id=1, source_target_pairs={{0,1},{4,3},{1,5},{5,7},{2,0},{6,2},{3,4},{7,6},{8,9},{12,11},{9,1... | collective-permute-start | bytes 393224 | tf_op jit(solution)/shard_map/ppermute | solution.py:120
  9.8 37.6 %collective-permute-start.5 = (bf16[64,2,4,128]{0,3,2,1:T(8,128)(2,1)}, bf16[64,2,4,128]{0,3,2,1:T(8,128)(2,1)S(1)}, u32[]{:S(2)}, u32[]{:S(2)}) collective-permute-start(bf16[64,2,4,128]{0,3,2,1:T(8,128)(2,1)} %copy.171), channel_id=1, source_target_pairs={{0,4},{4,6},{1,1},{5,3},{2,5},{6,7},{3,0},{7,2},{8,12},{12,14},{9,... | collective-permute-start | bytes 393224 | tf_op jit(solution)/shard_map/ppermute | solution.py:120
  14.9 33.9 %collective-permute-start.6 = (bf16[64,2,4,128]{0,3,2,1:T(8,128)(2,1)}, bf16[64,2,4,128]{0,3,2,1:T(8,128)(2,1)}, u32[]{:S(2)}, u32[]{:S(2)}) collective-permute-start(bf16[64,2,4,128]{0,3,2,1:T(8,128)(2,1)} %copy.172), channel_id=1, source_target_pairs={{0,0},{4,2},{1,4},{5,6},{2,1},{6,3},{3,5},{7,7},{8,8},{12,10},{9,1... | collective-permute-start | bytes 393224 | tf_op jit(solution)/shard_map/ppermute | solution.py:120
  20.0 43.6 %all-to-all-start.1 = ((bf16[4,2,18432]{2,1,0:T(2,128)(2,1)}), bf16[4,2,18432]{2,1,0:T(2,128)(2,1)}, u32[]{:S(2)}, u32[]{:S(2)}) async-start(bf16[4,2,18432]{2,1,0:T(2,128)(2,1)} %reshape.64), calls=%async_computation.1 | async-start | bytes 589824 | tf_op jit(solution)/shard_map/all_to_all | solution.py:83
  47.4 0.7 copy-start.2
  48.1 0.7 copy-start.3
  52.5 10.0 %collective-permute-start.8 = (bf16[256,1,4,128]{0,3,2,1:T(8,128)(2,1)}, bf16[256,1,4,128]{0,3,2,1:T(8,128)(2,1)}, u32[]{:S(2)}, u32[]{:S(2)}) collective-permute-start(bf16[256,1,4,128]{0,3,2,1:T(8,128)(2,1)} %get-tuple-element.15), channel_id=1, source_target_pairs={{8,0},{16,8},{24,16},{9,1},{17,9},{25,17},{10,2},{18,10},{26,18},{... | collective-permute-start | bytes 786440 | tf_op jit(solution)/shard_map/ppermute | solution.py:47
  55.1 7.4 %collective-permute-start.7 = (bf16[256,1,4,128]{0,3,2,1:T(8,128)(2,1)S(1)}, bf16[256,1,4,128]{0,3,2,1:T(8,128)(2,1)}, u32[]{:S(2)}, u32[]{:S(2)}) collective-permute-start(bf16[256,1,4,128]{0,3,2,1:T(8,128)(2,1)S(1)} %get-tuple-element.14), channel_id=1, source_target_pairs={{0,8},{8,16},{16,24},{1,9},{9,17},{17,25},{2,10},{10,18},{18,26},{... | collective-permute-start | bytes 786440 | tf_op jit(solution)/shard_map/ppermute | solution.py:46
  63.6 14.4 %all-to-all-start = ((bf16[2,128,2,6,128]{4,1,3,2,0:T(8,128)(2,1)}), bf16[2,128,2,6,128]{4,1,3,2,0:T(8,128)(2,1)S(1)}, u32[]{:S(2)}, u32[]{:S(2)}) async-start(bf16[2,128,2,6,128]{4,1,3,2,0:T(8,128)(2,1)} %pad_maximum_fusion.2), calls=%async_computation | async-start | bytes 1572864 | tf_op jit(solution)/shard_map/all_to_all | solution.py:101
  78.0 12.8 %all-to-all-start.2 = ((bf16[2,2,73728]{2,1,0:T(2,128)(2,1)}), bf16[2,2,73728]{2,1,0:T(2,128)(2,1)S(1)}, u32[]{:S(2)}, u32[]{:S(2)}) async-start(bf16[2,2,73728]{2,1,0:T(2,128)(2,1)} %reshape.66), calls=%async_computation.2 | async-start | bytes 1179648 | tf_op jit(solution)/shard_map/all_to_all | solution.py:85
  82.3 11.1 %collective-permute-start.10 = (bf16[256,2,1,128]{0,3,2,1:T(8,128)(2,1)}, bf16[256,2,1,128]{0,3,2,1:T(8,128)(2,1)S(1)}, u32[]{:S(2)}, u32[]{:S(2)}) collective-permute-start(bf16[256,2,1,128]{0,3,2,1:T(8,128)(2,1)} %get-tuple-element.17), channel_id=1, source_target_pairs={{4,0},{1,4},{5,1},{2,5},{6,2},{3,6},{7,3},{12,8},{9,12},{13,9},{10... | collective-permute-start | bytes 393224 | tf_op jit(solution)/shard_map/ppermute | solution.py:47
  83.6 9.8 %collective-permute-start.9 = (bf16[256,2,1,128]{0,3,2,1:T(8,128)(2,1)}, bf16[256,2,1,128]{0,3,2,1:T(8,128)(2,1)S(1)}, u32[]{:S(2)}, u32[]{:S(2)}) collective-permute-start(bf16[256,2,1,128]{0,3,2,1:T(8,128)(2,1)} %get-tuple-element.16), channel_id=1, source_target_pairs={{0,4},{4,1},{1,5},{5,2},{2,6},{6,3},{3,7},{8,12},{12,9},{9,13},{13... | collective-permute-start | bytes 393224 | tf_op jit(solution)/shard_map/ppermute | solution.py:46
  91.7 5.5 %collective-permute-start = (bf16[2,4,3,3,64,64]{5,1,4,3,2,0:T(4,128)(2,1)S(1)}, bf16[2,4,3,3,64,64]{5,1,4,3,2,0:T(4,128)(2,1)S(1)}, u32[]{:S(2)}, u32[]{:S(2)}) collective-permute-start(bf16[2,4,3,3,64,64]{5,1,4,3,2,0:T(4,128)(2,1)S(1)} %bitcast.64), channel_id=1, source_target_pairs={{0,8},{8,0},{16,24},{24,16},{1,9},{9,1},{17,25},{25,17},{2,10},{10... | collective-permute-start | bytes 1769480 | tf_op jit(solution)/shard_map/ppermute | solution.py:86
  100.4 2.5 %copy-start.4 = (bf16[256,6,2,8,19]{0,2,4,3,1:T(2,128)(2,1)S(1)}, bf16[256,6,2,8,19]{0,2,4,3,1:T(2,128)(2,1)}, u32[]{:S(2)}) copy-start(bf16[256,6,2,8,19]{0,2,4,3,1:T(2,128)(2,1)} %fusion.7) | copy-start | bytes 2801668
  100.4 2.5 %copy-start.7 = (pred[16,17]{0,1:T(8,128)(4,1)S(1)}, pred[16,17]{0,1:T(8,128)(4,1)}, u32[]{:S(2)}) copy-start(pred[16,17]{0,1:T(8,128)(4,1)} %constant.104) | copy-start | bytes 820
  105.6 6.3 %copy-start.1 = (bf16[3,3,256,256]{3,2,1,0:T(8,128)(2,1)S(1)}, bf16[3,3,256,256]{3,2,1,0:T(8,128)(2,1)}, u32[]{:S(2)}) copy-start(bf16[3,3,256,256]{3,2,1,0:T(8,128)(2,1)} %reshape.15) | copy-start | bytes 3538948
  105.6 6.3 %copy-start.5 = (bf16[256,6,2,8,19]{0,2,4,3,1:T(2,128)(2,1)S(1)}, bf16[256,6,2,8,19]{0,2,4,3,1:T(2,128)(2,1)}, u32[]{:S(2)}) copy-start(bf16[256,6,2,8,19]{0,2,4,3,1:T(2,128)(2,1)} %fusion.8) | copy-start | bytes 2801668
  106.3 19.6 %collective-permute-start.2 = (bf16[256,1,4,128]{0,2,3,1:T(4,128)(2,1)S(1)}, bf16[256,1,4,128]{0,2,3,1:T(4,128)(2,1)S(1)}, u32[]{:S(2)}, u32[]{:S(2)}) collective-permute-start(bf16[256,1,4,128]{0,2,3,1:T(4,128)(2,1)S(1)} %get-tuple-element.23), channel_id=1, source_target_pairs={{8,0},{16,8},{24,16},{9,1},{17,9},{25,17},{10,2},{18,10},{26,18},{... | collective-permute-start | bytes 786440 | tf_op jit(solution)/shard_map/ppermute | solution.py:47
  108.8 17.1 %collective-permute-start.1 = (bf16[256,1,4,128]{0,2,3,1:T(4,128)(2,1)S(1)}, bf16[256,1,4,128]{0,2,3,1:T(4,128)(2,1)S(1)}, u32[]{:S(2)}, u32[]{:S(2)}) collective-permute-start(bf16[256,1,4,128]{0,2,3,1:T(4,128)(2,1)S(1)} %get-tuple-element.22), channel_id=1, source_target_pairs={{0,8},{8,16},{16,24},{1,9},{9,17},{17,25},{2,10},{10,18},{18,26},{... | collective-permute-start | bytes 786440 | tf_op jit(solution)/shard_map/ppermute | solution.py:46
  113.9 12.8 %copy-start.6 = (bf16[3,256,256]{2,1,0:T(8,128)(2,1)S(1)}, bf16[3,256,256]{2,1,0:T(8,128)(2,1)}, u32[]{:S(2)}) copy-start(bf16[3,256,256]{2,1,0:T(8,128)(2,1)} %param.6) | copy-start | bytes 1179652
  115.2 18.9 %all-to-all-start.4 = ((bf16[256,2,4,128]{3,2,1,0:T(4,128)(2,1)}), bf16[256,2,4,128]{3,2,1,0:T(4,128)(2,1)S(1)}, u32[]{:S(2)}, u32[]{:S(2)}) async-start(bf16[256,2,4,128]{3,2,1,0:T(4,128)(2,1)} %copy.162), calls=%async_computation.4 | async-start | bytes 1048576 | tf_op jit(solution)/shard_map/all_to_all | solution.py:126
  134.1 22.1 %all-to-all-start.3 = ((bf16[256,2,4,128]{3,2,1,0:T(4,128)(2,1)}), bf16[256,2,4,128]{3,2,1,0:T(4,128)(2,1)S(1)}, u32[]{:S(2)}, u32[]{:S(2)}) async-start(bf16[256,2,4,128]{3,2,1,0:T(4,128)(2,1)} %copy.149), calls=%async_computation.3 | async-start | bytes 1048576 | tf_op jit(solution)/shard_map/all_to_all | solution.py:106

commit v4 on v2

--- a/solution.py
+++ b/solution.py
@@ -71,16 +71,37 @@
     return out[0]
 
 
-def gather_weight(weight):
+def spread_weight(weight):
     filts = lax.axis_size("filt")
+    core = lax.axis_index("slab") % 2
+    half = weight.shape[2] // 2
+    mine = lax.dynamic_slice_in_dim(weight, core * half, half, 2)
+    return jnp.broadcast_to(mine[None], (filts,) + mine.shape)
+
+
+def finish_weight(by_filt, c_loc):
     chans = lax.axis_size("chan")
-    spread = jnp.broadcast_to(weight[None], (filts,) + weight.shape)
-    by_filt = lax.all_to_all(spread, "filt", 0, 0, tiled=True)
+    slabs = lax.axis_size("slab")
+    core = lax.axis_index("slab") % 2
+    filts, m_loc = by_filt.shape[0], by_filt.shape[-1]
     spread = jnp.broadcast_to(by_filt[None], (chans,) + by_filt.shape)
     both = lax.all_to_all(spread, "chan", 0, 0, tiled=True)
-    c_loc, m_loc = weight.shape[2:]
-    whole = jnp.transpose(both, (2, 3, 0, 4, 1, 5))
+    other = lax.ppermute(both, "slab", [(i, i ^ 1) for i in range(slabs)])
+    halves = jnp.where(core == 0, jnp.stack([both, other]), jnp.stack([other, both]))
+    whole = jnp.transpose(halves, (3, 4, 1, 0, 5, 2, 6))
     return whole.reshape(3, 3, chans * c_loc, filts * m_loc)
+
+
+def send_filt(parts):
+    filts = lax.axis_size("filt")
+    flat = [p.reshape(filts, -1) for p in parts]
+    sizes = [f.shape[1] for f in flat]
+    got = lax.all_to_all(jnp.concatenate(flat, axis=1), "filt", 0, 0, tiled=True)
+    out, at = [], 0
+    for p, n in zip(parts, sizes):
+        out.append(got[:, at : at + n].reshape(p.shape))
+        at += n
+    return out
 
 
 def forward(volume, weight, depth_weight):
@@ -100,16 +121,19 @@
     return lax.all_to_all(out, "filt", 0, 2, tiled=True)
 
 
-def backward(grad_out, weight, depth_weight):
+def grad_windows(grad_out):
+    filts = lax.axis_size("filt")
+    rows = grad_out.shape[2] // filts
+    rimmed = halo(grad_out, "chan", 2)
+    return jnp.stack([lax.slice_in_dim(rimmed, t * rows, t * rows + rows + 2, axis=2) for t in range(filts)])
+
+
+def backward(windows, weight, depth_weight):
     chans = lax.axis_size("chan")
     filts = lax.axis_size("filt")
     chan = lax.axis_index("chan")
     filt = lax.axis_index("filt")
-    rows = grad_out.shape[2] // filts
-    rimmed = halo(grad_out, "chan", 2)
-    windows = jnp.stack([lax.slice_in_dim(rimmed, t * rows, t * rows + rows + 2, axis=2) for t in range(filts)])
-    all_filters = lax.all_to_all(windows, "filt", 0, 0, tiled=True)
-    all_filters = all_filters.reshape((-1,) + all_filters.shape[2:])
+    all_filters = windows.reshape((-1,) + windows.shape[2:])
     deep = halo(all_filters, "slab", 1)
     grad_mid = depth_conv(deep, depth_weight[::-1], "DHWIO").astype(jnp.bfloat16)
     grad_in = plane_conv(grad_mid, weight[::-1, ::-1], "HWOI").astype(jnp.bfloat16)
@@ -128,9 +152,10 @@
 
 
 def local(volume, plane_weight, depth_weight, grad_out):
-    weight = gather_weight(plane_weight)
+    by_filt, windows = send_filt([spread_weight(plane_weight), grad_windows(grad_out)])
+    weight = finish_weight(by_filt, plane_weight.shape[2])
     output = forward(volume, weight, depth_weight)
-    grad_in = backward(grad_out, weight, depth_weight)
+    grad_in = backward(windows, weight, depth_weight)
     return (output, grad_in)
 
 

time: 149 us -> 157 us (1.054)
  the two profiles are of different devices: /device:TPU:10 before, /device:TPU:9 now
where the time goes in v4:
time: 157 us; the launch traced here: 156 us
  waiting for transfers between devices  49.8 us (32%)
  starting transfers between devices  41.3 us (26%)
  local copies, waits for them, and re-layouts  37.7 us (24%)
  other arithmetic  18 us (11%)
  matrix products  8.18 us (5%)
    ppermute x2, waiting for transfers between devices, backward(): pieces.append(lax.ppermute(block, ROWS, pairs))  24.5 us
    all_to_all x1, waiting for transfers between devices, send_filt(): lax.all_to_all(jnp.concatenate(flat, axis=1), 'filt', 0, 0, tiled=True)  18.8 us
    unnamed x31, local copies, waits for them, and re-layouts  16.9 us
    ppermute x3, starting transfers between devices, halo(): lax.ppermute(lax.slice_in_dim(x, length - 1, length, axis=dim), axis, up)  10.7 us
    ppermute x3, waiting for transfers between devices, halo(): after = lax.ppermute(lax.slice_in_dim(x, 0, 1, axis=dim), axis, down)  6.51 us
    all_to_all x1, starting transfers between devices, forward(): return lax.all_to_all(out, 'filt', 0, 2, tiled=True)  6.44 us
    ppermute x3, starting transfers between devices, halo(): after = lax.ppermute(lax.slice_in_dim(x, 0, 1, axis=dim), axis, down)  6.24 us
    all_to_all x2, other arithmetic, send_filt(): lax.all_to_all(jnp.concatenate(flat, axis=1), 'filt', 0, 0, tiled=True)  6.19 us
  transfers between devices with their start and end apart: 13, of which 5 were waited for; matrix products, arithmetic and copies ran while one was open for 24% of the time, Pallas kernels for 0%

profile of v4, /device:TPU:9, one launch (start us, length us, event | category | flops | bytes accessed | tf_op | source)
XLA Modules:
  0.0 156.2 jit_solution(7455026868050710411)
XLA Ops:
  1.8 3.1 %collective-permute-start = (bf16[64,2,1,128]{3,2,1,0:T(2,128)(2,1)S(1)}, bf16[64,2,1,128]{3,2,1,0:T(2,128)(2,1)S(1)}, u32[]{:S(2)}, u32[]{:S(2)}) collective-permute-start(bf16[64,2,1,128]{3,2,1,0:T(2,128)(2,1)S(1)} %get-tuple-element.24), channel_id=1, source_target_pairs={{0,4},{1,5},{2,6},{3,7},{8,12},{9,13},{10,14},{11,15},{16,20},{17,... | collective-permute-start | bytes 98312 | tf_op jit(solution)/shard_map/ppermute | solution.py:46
  6.3 2.9 %copy.92 = bf16[128,2,32,128]{3,0,2,1:T(8,128)(2,1)S(1)} copy(bf16[128,2,32,128]{3,2,1,0:T(8,128)(2,1)} %param.4) | data formatting | bytes 4194304 | tf_op args[0]
  10.3 3.5 %all-to-all-start = ((bf16[2,128,2,6,128]{4,1,3,2,0:T(8,128)(2,1)}), bf16[2,128,2,6,128]{4,1,3,2,0:T(8,128)(2,1)S(1)}, u32[]{:S(2)}, u32[]{:S(2)}) async-start(bf16[2,128,2,6,128]{4,1,3,2,0:T(8,128)(2,1)} %pad_maximum_fusion.2), calls=%async_computation | async-start | bytes 1572864 | tf_op jit(solution)/shard_map/all_to_all | solution.py:116
  16.1 4.2 %maximum_bitcast_fusion = bf16[4,1,135168]{2,0,1:T(4,128)(2,1)S(1)} fusion(bf16[1,98304]{1,0:T(2,128)(2,1)} %stack.44, bf16[1,98304]{1,0:T(2,128)(2,1)S(1)} %stack.43, bf16[1,98304]{1,0:T(2,128)(2,1)S(1)} %stack.42, bf16[1,98304]{1,0:T(2,128)(2,1)S(1)} %stack.41, bf16[135168]{0:T(1024)(128)(2,1)S(1)} %pad.25.clone), kind=kLoop, calls=%fused_computation.16 | loop fusion | flops 5406720 | bytes 2138112 | tf_op jit(solution)/shard_map/all_to_all | solution.py:99
  20.8 2.0 %reduce = bf16[4,135168]{1,0:T(4,128)(2,1)S(1)} reduce(bf16[4,1,135168]{2,0,1:T(4,128)(2,1)S(1)} %maximum_bitcast_fusion, bf16[]{:T(256)} %broadcast.33), dimensions={1}, to_apply=%copy.97.reduce_sub_computation | reduce | bytes 2162690 | tf_op jit(solution)/shard_map/all_to_all | solution.py:99
  22.8 2.1 %reshape.79 = bf16[4,2,67584]{2,1,0:T(2,128)(2,1)} reshape(bf16[4,135168]{1,0:T(4,128)(2,1)S(1)} %reduce) | data formatting | bytes 2162688
  24.9 4.8 %all-to-all-start.1 = ((bf16[4,2,67584]{2,1,0:T(2,128)(2,1)}), bf16[4,2,67584]{2,1,0:T(2,128)(2,1)S(1)}, u32[]{:S(2)}, u32[]{:S(2)}) async-start(bf16[4,2,67584]{2,1,0:T(2,128)(2,1)} %reshape.79), calls=%async_computation.1 | async-start | bytes 2162688 | tf_op jit(solution)/shard_map/all_to_all | solution.py:99
  32.7 18.8 %all-to-all-done.1 = bf16[4,2,67584]{2,1,0:T(2,128)(2,1)S(1)} async-done(((bf16[4,2,67584]{2,1,0:T(2,128)(2,1)}), bf16[4,2,67584]{2,1,0:T(2,128)(2,1)S(1)}, u32[]{:S(2)}, u32[]{:S(2)}) %all-to-all-start.1) | async-done | bytes 1081376 | tf_op jit(solution)/shard_map/all_to_all | solution.py:99
  52.5 2.3 %copy.137 = bf16[4,1,135168]{2,0,1:T(4,128)(2,1)S(1)} copy(bf16[4,1,135168]{2,1,0:T(2,128)(2,1)S(1)} %reshape.80) | data formatting | bytes 2162688
  57.4 1.7 %reshape.81 = bf16[2,2,73728]{2,1,0:T(2,128)(2,1)} reshape(bf16[2,3,3,64,4,64]{5,4,3,2,1,0:T(4,128)(2,1)S(1)} %broadcast_bitcast_fusion) | data formatting | bytes 1179648
  59.1 3.6 %all-to-all-start.2 = ((bf16[2,2,73728]{2,1,0:T(2,128)(2,1)}), bf16[2,2,73728]{2,1,0:T(2,128)(2,1)S(1)}, u32[]{:S(2)}, u32[]{:S(2)}) async-start(bf16[2,2,73728]{2,1,0:T(2,128)(2,1)} %reshape.81), calls=%async_computation.2 | async-start | bytes 1179648 | tf_op jit(solution)/shard_map/all_to_all | solution.py:88
  63.6 5.6 %collective-permute-start.5 = (bf16[256,1,6,128]{3,2,1,0:T(8,128)(2,1)}, bf16[256,1,6,128]{3,2,1,0:T(8,128)(2,1)}, u32[]{:S(2)}, u32[]{:S(2)}) collective-permute-start(bf16[256,1,6,128]{3,2,1,0:T(8,128)(2,1)} %get-tuple-element.14), channel_id=1, source_target_pairs={{0,8},{8,16},{16,24},{1,9},{9,17},{17,25},{2,10},{10,18},{18,26},{... | collective-permute-start | bytes 1179656 | tf_op jit(solution)/shard_map/ppermute | solution.py:46
  69.3 2.1 %collective-permute-start.6 = (bf16[256,1,6,128]{3,2,1,0:T(8,128)(2,1)S(1)}, bf16[256,1,6,128]{3,2,1,0:T(8,128)(2,1)}, u32[]{:S(2)}, u32[]{:S(2)}) collective-permute-start(bf16[256,1,6,128]{3,2,1,0:T(8,128)(2,1)S(1)} %get-tuple-element.15), channel_id=1, source_target_pairs={{8,0},{16,8},{24,16},{9,1},{17,9},{25,17},{10,2},{18,10},{26,18},{... | collective-permute-start | bytes 1179656 | tf_op jit(solution)/shard_map/ppermute | solution.py:47
  71.5 1.7 %fusion.11 = bf16[256,6,2,8,19]{0,2,4,3,1:T(2,128)(2,1)} fusion(bf16[256,6,2,7,2]{0,2,4,3,1:T(2,128)(2,1)S(1)} %slice.56, bf16[256,6,2,8,17]{0,2,4,3,1:T(2,128)(2,1)S(1)} %bitcast.72), kind=kLoop, calls=%fused_computation.24 | loop fusion | flops 2801664 | bytes 1855488 | tf_op jit(solution)/shard_map/conv_general_dilated | solution.py:52
  73.1 1.6 %reshape.82 = bf16[2,3,3,64,4,64]{5,4,3,2,1,0:T(4,128)(2,1)} reshape(bf16[2,2,73728]{2,1,0:T(2,128)(2,1)S(1)} %all-to-all-done.2) | data formatting | bytes 1179648
  74.7 2.8 %bitcast_bitcast_fusion = bf16[1,2,4,3,3,64,64]{6,2,5,4,3,1,0:T(4,128)(2,1)} fusion(bf16[2,3,3,64,4,64]{5,4,3,2,1,0:T(4,128)(2,1)} %reshape.82), kind=kLoop, calls=%fused_computation.48 | loop fusion | bytes 1179648 | tf_op jit(solution)/shard_map/stack | solution.py:90
  77.5 2.4 %collective-permute-done.6 = bf16[256,1,6,128]{3,2,1,0:T(8,128)(2,1)} collective-permute-done((bf16[256,1,6,128]{3,2,1,0:T(8,128)(2,1)S(1)}, bf16[256,1,6,128]{3,2,1,0:T(8,128)(2,1)}, u32[]{:S(2)}, u32[]{:S(2)}) %collective-permute-start.6) | collective-permute-done | bytes 393248 | tf_op jit(solution)/shard_map/ppermute | solution.py:47
  79.9 1.7 %pad_maximum_fusion = bf16[256,4,6,128]{3,2,1,0:T(8,128)(2,1)S(1)} fusion(bf16[256,1,6,128]{3,2,1,0:T(8,128)(2,1)} %collective-permute-done.6, bf16[256,2,6,128]{3,2,1,0:T(8,128)(2,1)S(1)} %reshape_reshape.3, bf16[256,1,6,128]{3,2,1,0:T(8,128)(2,1)} %collective-permute-done.5), kind=kLoop, calls=%fused_computation.2 | loop fusion | flops 1572864 | bytes 3145728 | tf_op jit(solution)/shard_map/concatenate | solution.py:48
  81.7 2.6 %copy.108 = bf16[256,4,6,128]{0,3,2,1:T(8,128)(2,1)} copy(bf16[256,4,6,128]{3,2,1,0:T(8,128)(2,1)S(1)} %pad_maximum_fusion) | data formatting | bytes 3145728 | tf_op jit(solution)/shard_map/concatenate | solution.py:48
  84.2 2.2 %fusion.5 = bf16[2,6,8,16,256]{4,2,3,1,0:T(8,128)(2,1)S(1)} fusion(bf16[256,4,6,8,16]{0,4,3,2,1:T(8,128)(2,1)} %bitcast.82, bf16[3,256,256]{2,1,0:T(8,128)(2,1)S(1)} %copy-done.8), kind=kOutput, calls=%fused_computation.10 | convolution fusion | flops 604372992 | bytes 2752512 | tf_op jit(solution)/shard_map/conv_general_dilated | solution.py:63
  88.2 4.3 %fusion = bf16[3,3,2,2,64,4,64]{6,5,4,1,0,2,3:T(4,128)(2,1)S(1)} fusion(bf16[1,2,4,3,3,64,64]{6,2,5,4,3,1,0:T(4,128)(2,1)} %bitcast.8, bf16[1,2,4,3,3,64,64]{6,2,5,4,3,1,0:T(4,128)(2,1)S(1)} %copy-done.1, pred[]{:T(512)S(6)} %eq.11), kind=kLoop, calls=%fused_computation.1 | loop fusion | flops 1769472 | bytes 2359297 | tf_op jit(solution)/shard_map/transpose | solution.py:91
  92.5 1.5 copy.99
  94.0 2.5 %reshape.29 = bf16[3,3,256,256]{3,2,1,0:T(8,128)(2,1)} reshape(bf16[3,3,2,2,64,4,64]{6,5,4,3,2,1,0:T(4,128)(2,1)S(1)} %copy.99) | data formatting | bytes 2359296 | tf_op jit(solution)/shard_map/reshape | solution.py:92
  96.5 3.0 %fusion.8 = bf16[4,16,17,256]{3,1,2,0:T(8,128)(2,1)S(1)} fusion(bf16[3,3,256,256]{3,2,1,0:T(8,128)(2,1)} %reshape.29, bf16[256,6,2,8,19]{0,2,4,3,1:T(2,128)(2,1)} %fusion.11, pred[16,17]{0,1:T(8,128)(4,1)S(1)} %copy-done.9), kind=kOutput, calls=%fused_computation.13 | convolution fusion | flops 1284014080 | bytes 2670864 | tf_op jit(solution)/shard_map/conv_general_dilated | solution.py:52
  100.2 1.9 %collective-permute-start.3 = (bf16[256,1,4,128]{0,2,3,1:T(4,128)(2,1)S(1)}, bf16[256,1,4,128]{0,2,3,1:T(4,128)(2,1)S(1)}, u32[]{:S(2)}, u32[]{:S(2)}) collective-permute-start(bf16[256,1,4,128]{0,2,3,1:T(4,128)(2,1)S(1)} %get-tuple-element.18), channel_id=1, source_target_pairs={{0,8},{8,16},{16,24},{1,9},{9,17},{17,25},{2,10},{10,18},{18,26},{... | collective-permute-start | bytes 786440 | tf_op jit(solution)/shard_map/ppermute | solution.py:46
  102.2 2.8 %collective-permute-start.4 = (bf16[256,1,4,128]{0,2,3,1:T(4,128)(2,1)S(1)}, bf16[256,1,4,128]{0,2,3,1:T(4,128)(2,1)S(1)}, u32[]{:S(2)}, u32[]{:S(2)}) collective-permute-start(bf16[256,1,4,128]{0,2,3,1:T(4,128)(2,1)S(1)} %get-tuple-element.19), channel_id=1, source_target_pairs={{8,0},{16,8},{24,16},{9,1},{17,9},{25,17},{10,2},{18,10},{26,18},{... | collective-permute-start | bytes 786440 | tf_op jit(solution)/shard_map/ppermute | solution.py:47
  105.9 4.1 %collective-permute-done.4 = bf16[256,1,4,128]{0,2,3,1:T(4,128)(2,1)S(1)} collective-permute-done((bf16[256,1,4,128]{0,2,3,1:T(4,128)(2,1)S(1)}, bf16[256,1,4,128]{0,2,3,1:T(4,128)(2,1)S(1)}, u32[]{:S(2)}, u32[]{:S(2)}) %collective-permute-start.4) | collective-permute-done | bytes 262176 | tf_op jit(solution)/shard_map/ppermute | solution.py:47
  113.4 6.4 %all-to-all-start.3 = ((bf16[256,2,4,128]{3,2,1,0:T(4,128)(2,1)}), bf16[256,2,4,128]{3,2,1,0:T(4,128)(2,1)S(1)}, u32[]{:S(2)}, u32[]{:S(2)}) async-start(bf16[256,2,4,128]{3,2,1,0:T(4,128)(2,1)} %copy.105), calls=%async_computation.3 | async-start | bytes 1048576 | tf_op jit(solution)/shard_map/all_to_all | solution.py:121
  119.9 1.5 fusion.9
  122.2 5.9 %collective-permute-start.8 = (bf16[128,2,4,128]{0,2,3,1:T(4,128)(2,1)S(1)}, bf16[128,2,4,128]{0,2,3,1:T(4,128)(2,1)S(1)}, u32[]{:S(2)}, u32[]{:S(2)}) collective-permute-start(bf16[128,2,4,128]{0,2,3,1:T(4,128)(2,1)S(1)} %get-tuple-element.16), channel_id=1, source_target_pairs={{0,0},{1,4},{2,1},{3,5},{4,2},{5,6},{6,3},{7,7},{8,8},{9,12},{10,9... | collective-permute-start | bytes 786440 | tf_op jit(solution)/shard_map/ppermute | solution.py:150
  128.1 8.7 %collective-permute-done.7 = bf16[128,2,4,128]{0,2,3,1:T(4,128)(2,1)S(1)} collective-permute-done((bf16[128,2,4,128]{0,2,3,1:T(4,128)(2,1)S(1)}, bf16[128,2,4,128]{0,2,3,1:T(4,128)(2,1)S(1)}, u32[]{:S(2)}, u32[]{:S(2)}) %collective-permute-start.7) | collective-permute-done | bytes 262176 | tf_op jit(solution)/shard_map/ppermute | solution.py:150
  136.8 15.9 %collective-permute-done.8 = bf16[128,2,4,128]{0,2,3,1:T(4,128)(2,1)S(1)} collective-permute-done((bf16[128,2,4,128]{0,2,3,1:T(4,128)(2,1)S(1)}, bf16[128,2,4,128]{0,2,3,1:T(4,128)(2,1)S(1)}, u32[]{:S(2)}, u32[]{:S(2)}) %collective-permute-start.8) | collective-permute-done | bytes 262176 | tf_op jit(solution)/shard_map/ppermute | solution.py:150
  (77 shorter events, 24.7 us)
Async XLA Ops:
  0.6 13.3 %copy-start = (bf16[3,3,128,64]{2,3,1,0:T(8,128)(2,1)S(1)}, bf16[3,3,128,64]{2,3,1,0:T(8,128)(2,1)}, u32[]{:S(2)}) copy-start(bf16[3,3,128,64]{2,3,1,0:T(8,128)(2,1)} %param.5) | copy-start | bytes 442372
  1.8 12.5 %collective-permute-start = (bf16[64,2,1,128]{3,2,1,0:T(2,128)(2,1)S(1)}, bf16[64,2,1,128]{3,2,1,0:T(2,128)(2,1)S(1)}, u32[]{:S(2)}, u32[]{:S(2)}) collective-permute-start(bf16[64,2,1,128]{3,2,1,0:T(2,128)(2,1)S(1)} %get-tuple-element.24), channel_id=1, source_target_pairs={{0,4},{1,5},{2,6},{3,7},{8,12},{9,13},{10,14},{11,15},{16,20},{17,... | collective-permute-start | bytes 98312 | tf_op jit(solution)/shard_map/ppermute | solution.py:46
  5.0 9.4 %collective-permute-start.1 = (bf16[64,2,1,128]{3,2,1,0:T(2,128)(2,1)S(1)}, bf16[64,2,1,128]{3,2,1,0:T(2,128)(2,1)S(1)}, u32[]{:S(2)}, u32[]{:S(2)}) collective-permute-start(bf16[64,2,1,128]{3,2,1,0:T(2,128)(2,1)S(1)} %get-tuple-element.25), channel_id=1, source_target_pairs={{4,0},{5,1},{6,2},{7,3},{12,8},{13,9},{14,10},{15,11},{20,16},{21,... | collective-permute-start | bytes 98312 | tf_op jit(solution)/shard_map/ppermute | solution.py:47
  9.3 5.0 %copy-start.4 = (bf16[64,2,16,128]{3,2,1,0:T(8,128)(2,1)S(1)}, bf16[64,2,16,128]{3,2,1,0:T(8,128)(2,1)}, u32[]{:S(2)}) copy-start(bf16[64,2,16,128]{3,2,1,0:T(8,128)(2,1)} %param.7) | copy-start | bytes 1572868
  10.3 14.5 %all-to-all-start = ((bf16[2,128,2,6,128]{4,1,3,2,0:T(8,128)(2,1)}), bf16[2,128,2,6,128]{4,1,3,2,0:T(8,128)(2,1)S(1)}, u32[]{:S(2)}, u32[]{:S(2)}) async-start(bf16[2,128,2,6,128]{4,1,3,2,0:T(8,128)(2,1)} %pad_maximum_fusion.2), calls=%async_computation | async-start | bytes 1572864 | tf_op jit(solution)/shard_map/all_to_all | solution.py:116
  22.8 6.9 %copy-start.6 = (bf16[3,256,256]{2,1,0:T(8,128)(2,1)S(1)}, bf16[3,256,256]{2,1,0:T(8,128)(2,1)}, u32[]{:S(2)}) copy-start(bf16[3,256,256]{2,1,0:T(8,128)(2,1)} %param.6) | copy-start | bytes 1179652
  24.9 26.6 %all-to-all-start.1 = ((bf16[4,2,67584]{2,1,0:T(2,128)(2,1)}), bf16[4,2,67584]{2,1,0:T(2,128)(2,1)S(1)}, u32[]{:S(2)}, u32[]{:S(2)}) async-start(bf16[4,2,67584]{2,1,0:T(2,128)(2,1)} %reshape.79), calls=%async_computation.1 | async-start | bytes 2162688 | tf_op jit(solution)/shard_map/all_to_all | solution.py:99
  31.8 0.9 copy-start.2
  59.1 12.4 %copy-start.3 = (bf16[256,6,2,136]{0,2,3,1:T(2,128)(2,1)S(1)}, bf16[256,6,2,136]{0,2,3,1:T(2,128)(2,1)}, u32[]{:S(2)}) copy-start(bf16[256,6,2,136]{0,2,3,1:T(2,128)(2,1)} %copy-done.2) | copy-start | bytes 2506756
  59.1 14.1 %all-to-all-start.2 = ((bf16[2,2,73728]{2,1,0:T(2,128)(2,1)}), bf16[2,2,73728]{2,1,0:T(2,128)(2,1)S(1)}, u32[]{:S(2)}, u32[]{:S(2)}) async-start(bf16[2,2,73728]{2,1,0:T(2,128)(2,1)} %reshape.81), calls=%async_computation.2 | async-start | bytes 1179648 | tf_op jit(solution)/shard_map/all_to_all | solution.py:88
  63.6 13.9 %collective-permute-start.5 = (bf16[256,1,6,128]{3,2,1,0:T(8,128)(2,1)}, bf16[256,1,6,128]{3,2,1,0:T(8,128)(2,1)}, u32[]{:S(2)}, u32[]{:S(2)}) collective-permute-start(bf16[256,1,6,128]{3,2,1,0:T(8,128)(2,1)} %get-tuple-element.14), channel_id=1, source_target_pairs={{0,8},{8,16},{16,24},{1,9},{9,17},{17,25},{2,10},{10,18},{18,26},{... | collective-permute-start | bytes 1179656 | tf_op jit(solution)/shard_map/ppermute | solution.py:46
  69.3 10.6 %collective-permute-start.6 = (bf16[256,1,6,128]{3,2,1,0:T(8,128)(2,1)S(1)}, bf16[256,1,6,128]{3,2,1,0:T(8,128)(2,1)}, u32[]{:S(2)}, u32[]{:S(2)}) collective-permute-start(bf16[256,1,6,128]{3,2,1,0:T(8,128)(2,1)S(1)} %get-tuple-element.15), channel_id=1, source_target_pairs={{8,0},{16,8},{24,16},{9,1},{17,9},{25,17},{10,2},{18,10},{26,18},{... | collective-permute-start | bytes 1179656 | tf_op jit(solution)/shard_map/ppermute | solution.py:47
  74.7 13.4 %collective-permute-start.2 = (bf16[2,4,3,3,64,64]{5,1,4,3,2,0:T(4,128)(2,1)}, bf16[2,4,3,3,64,64]{5,1,4,3,2,0:T(4,128)(2,1)}, u32[]{:S(2)}, u32[]{:S(2)}) collective-permute-start(bf16[2,4,3,3,64,64]{5,1,4,3,2,0:T(4,128)(2,1)} %bitcast.62), channel_id=1, source_target_pairs={{0,8},{8,0},{16,24},{24,16},{1,9},{9,1},{17,25},{25,17},{2,10},{10... | collective-permute-start | bytes 1769480 | tf_op jit(solution)/shard_map/ppermute | solution.py:89
  81.7 2.6 %copy-start.8 = (bf16[3,256,256]{2,1,0:T(8,128)(2,1)S(1)}, bf16[3,256,256]{2,1,0:T(8,128)(2,1)}, u32[]{:S(2)}) copy-start(bf16[3,256,256]{2,1,0:T(8,128)(2,1)} %rev.4) | copy-start | bytes 1179652
  86.6 1.5 copy-start.1
  94.0 2.5 %copy-start.9 = (pred[16,17]{0,1:T(8,128)(4,1)S(1)}, pred[16,17]{0,1:T(8,128)(4,1)}, u32[]{:S(2)}) copy-start(pred[16,17]{0,1:T(8,128)(4,1)} %constant.89) | copy-start | bytes 820
  100.2 5.6 %collective-permute-start.3 = (bf16[256,1,4,128]{0,2,3,1:T(4,128)(2,1)S(1)}, bf16[256,1,4,128]{0,2,3,1:T(4,128)(2,1)S(1)}, u32[]{:S(2)}, u32[]{:S(2)}) collective-permute-start(bf16[256,1,4,128]{0,2,3,1:T(4,128)(2,1)S(1)} %get-tuple-element.18), channel_id=1, source_target_pairs={{0,8},{8,16},{16,24},{1,9},{9,17},{17,25},{2,10},{10,18},{18,26},{... | collective-permute-start | bytes 786440 | tf_op jit(solution)/shard_map/ppermute | solution.py:46
  102.2 8.6 %copy-start.7 = (bf16[3,256,256]{2,1,0:T(8,128)(2,1)S(1)}, bf16[3,256,256]{2,1,0:T(8,128)(2,1)}, u32[]{:S(2)}) copy-start(bf16[3,256,256]{2,1,0:T(8,128)(2,1)} %param.6) | copy-start | bytes 1179652
  102.2 7.8 %collective-permute-start.4 = (bf16[256,1,4,128]{0,2,3,1:T(4,128)(2,1)S(1)}, bf16[256,1,4,128]{0,2,3,1:T(4,128)(2,1)S(1)}, u32[]{:S(2)}, u32[]{:S(2)}) collective-permute-start(bf16[256,1,4,128]{0,2,3,1:T(4,128)(2,1)S(1)} %get-tuple-element.19), channel_id=1, source_target_pairs={{8,0},{16,8},{24,16},{9,1},{17,9},{25,17},{10,2},{18,10},{26,18},{... | collective-permute-start | bytes 786440 | tf_op jit(solution)/shard_map/ppermute | solution.py:47
  112.2 7.6 %copy-start.5 = (bf16[3,3,256,256]{3,2,1,0:T(8,128)(2,1)S(1)}, bf16[3,3,256,256]{3,2,1,0:T(8,128)(2,1)}, u32[]{:S(2)}) copy-start(bf16[3,3,256,256]{3,2,1,0:T(8,128)(2,1)} %reshape.29) | copy-start | bytes 3538948
  113.4 41.6 %all-to-all-start.3 = ((bf16[256,2,4,128]{3,2,1,0:T(4,128)(2,1)}), bf16[256,2,4,128]{3,2,1,0:T(4,128)(2,1)S(1)}, u32[]{:S(2)}, u32[]{:S(2)}) async-start(bf16[256,2,4,128]{3,2,1,0:T(4,128)(2,1)} %copy.105), calls=%async_computation.3 | async-start | bytes 1048576 | tf_op jit(solution)/shard_map/all_to_all | solution.py:121
  122.1 14.7 %collective-permute-start.7 = (bf16[128,2,4,128]{0,2,3,1:T(4,128)(2,1)S(1)}, bf16[128,2,4,128]{0,2,3,1:T(4,128)(2,1)S(1)}, u32[]{:S(2)}, u32[]{:S(2)}) collective-permute-start(bf16[128,2,4,128]{0,2,3,1:T(4,128)(2,1)S(1)} %get-tuple-element.17), channel_id=1, source_target_pairs={{0,4},{1,0},{2,5},{3,1},{4,6},{5,2},{6,7},{7,3},{8,12},{9,8},{10,1... | collective-permute-start | bytes 786440 | tf_op jit(solution)/shard_map/ppermute | solution.py:150
  122.2 30.5 %collective-permute-start.8 = (bf16[128,2,4,128]{0,2,3,1:T(4,128)(2,1)S(1)}, bf16[128,2,4,128]{0,2,3,1:T(4,128)(2,1)S(1)}, u32[]{:S(2)}, u32[]{:S(2)}) collective-permute-start(bf16[128,2,4,128]{0,2,3,1:T(4,128)(2,1)S(1)} %get-tuple-element.16), channel_id=1, source_target_pairs={{0,0},{1,4},{2,1},{3,5},{4,2},{5,6},{6,3},{7,7},{8,8},{9,12},{10,9... | collective-permute-start | bytes 786440 | tf_op jit(solution)/shard_map/ppermute | solution.py:150

commit v5 on v2

--- a/solution.py
+++ b/solution.py
@@ -76,8 +76,7 @@
     chans = lax.axis_size("chan")
     spread = jnp.broadcast_to(weight[None], (filts,) + weight.shape)
     by_filt = lax.all_to_all(spread, "filt", 0, 0, tiled=True)
-    spread = jnp.broadcast_to(by_filt[None], (chans,) + by_filt.shape)
-    both = lax.all_to_all(spread, "chan", 0, 0, tiled=True)
+    both = gather_blocks(by_filt[None], "chan", 0)
     c_loc, m_loc = weight.shape[2:]
     whole = jnp.transpose(both, (2, 3, 0, 4, 1, 5))
     return whole.reshape(3, 3, chans * c_loc, filts * m_loc)
@@ -89,11 +88,13 @@
     filt = lax.axis_index("filt")
     rows = volume.shape[2] // (chans * filts)
     padded = jnp.pad(volume, ((0, 0), (0, 0), (1, 1), (0, 0)))
-    windows = jnp.stack(
-        [lax.dynamic_slice_in_dim(padded, (t * filts + filt) * rows, rows + 2, 2) for t in range(chans)]
-    )
-    all_channels = lax.all_to_all(windows, "chan", 0, 0, tiled=True)
-    all_channels = all_channels.reshape((-1,) + all_channels.shape[2:])
+    chan = lax.axis_index("chan")
+    window = lambda group: lax.dynamic_slice_in_dim(padded, group * rows, rows + 2, 2)
+    pieces = [window(chan * filts + filt)]
+    for k in range(1, chans):
+        target = (chan + k) % chans
+        pieces.append(lax.ppermute(window(target * filts + filt), "chan", shift_pairs(chans, k)))
+    all_channels = order_blocks(pieces, chan, 0)
     mid = plane_conv(all_channels, weight, "HWIO").astype(jnp.bfloat16)
     deep = halo(mid, "slab", 1)
     out = depth_conv(deep, depth_weight, "DHWOI").astype(jnp.bfloat16)

time: 149 us -> 129 us (0.87)
  the two profiles are of different devices: /device:TPU:10 before, /device:TPU:9 now
where the time goes in v5:
time: 129 us; the launch traced here: 128 us
  waiting for transfers between devices  43.9 us (34%)
  starting transfers between devices  42.8 us (33%)
  local copies, waits for them, and re-layouts  18.5 us (14%)
  other arithmetic  13.6 us (11%)
  matrix products  8.24 us (6%)
    ppermute x2, waiting for transfers between devices, backward(): pieces.append(lax.ppermute(block, ROWS, pairs))  28.1 us
    ppermute x3, starting transfers between devices, halo(): lax.ppermute(lax.slice_in_dim(x, length - 1, length, axis=dim), axis, up)  14.7 us
    ppermute x1, waiting for transfers between devices, forward(): lax.ppermute(window(target * filts + filt), 'chan', shift_pairs(chans, k))  9.54 us
    all_to_all x1, starting transfers between devices, backward(): all_filters = lax.all_to_all(windows, 'filt', 0, 0, tiled=True)  6.87 us
    ppermute x3, starting transfers between devices, halo(): after = lax.ppermute(lax.slice_in_dim(x, 0, 1, axis=dim), axis, down)  5.32 us
    ppermute x2, starting transfers between devices, backward(): pieces.append(lax.ppermute(block, ROWS, pairs))  5.29 us
    unnamed x21, local copies, waits for them, and re-layouts  4.86 us
    all_to_all x1, starting transfers between devices, gather_weight(): by_filt = lax.all_to_all(spread, 'filt', 0, 0, tiled=True)  4.76 us
  transfers between devices with their start and end apart: 13, of which 5 were waited for; matrix products, arithmetic and copies ran while one was open for 26% of the time, Pallas kernels for 0%

profile of v5, /device:TPU:9, one launch (start us, length us, event | category | flops | bytes accessed | tf_op | source)
XLA Modules:
  0.0 128.2 jit_solution(3961047174417584045)
XLA Ops:
  0.6 1.9 %broadcast_in_dim.21 = bf16[4,3,3,128,64]{3,4,2,1,0:T(8,128)(2,1)} broadcast(bf16[3,3,128,64]{2,3,1,0:T(8,128)(2,1)} %param.5), dimensions={1,2,3,4} | broadcast | bytes 737280 | tf_op jit(solution)/shard_map/broadcast_in_dim | solution.py:77
  2.6 4.8 %all-to-all-start = ((bf16[4,3,3,128,64]{3,4,2,1,0:T(8,128)(2,1)}), bf16[4,3,3,128,64]{3,4,2,1,0:T(8,128)(2,1)S(1)}, u32[]{:S(2)}, u32[]{:S(2)}) async-start(bf16[4,3,3,128,64]{3,4,2,1,0:T(8,128)(2,1)} %broadcast_in_dim.21), calls=%async_computation | async-start | bytes 1179648 | tf_op jit(solution)/shard_map/all_to_all | solution.py:78
  7.5 3.1 %collective-permute-start.4 = (bf16[64,2,1,128]{3,0,2,1:T(8,128)(2,1)S(1)}, bf16[64,2,1,128]{3,0,2,1:T(8,128)(2,1)S(1)}, u32[]{:S(2)}, u32[]{:S(2)}) collective-permute-start(bf16[64,2,1,128]{3,0,2,1:T(8,128)(2,1)S(1)} %get-tuple-element.18), channel_id=1, source_target_pairs={{0,4},{1,5},{2,6},{3,7},{8,12},{9,13},{10,14},{11,15},{16,20},{17,... | collective-permute-start | bytes 98312 | tf_op jit(solution)/shard_map/ppermute | solution.py:46
  10.7 1.3 %collective-permute-start.5 = (bf16[64,2,1,128]{3,0,2,1:T(8,128)(2,1)S(1)}, bf16[64,2,1,128]{3,0,2,1:T(8,128)(2,1)S(1)}, u32[]{:S(2)}, u32[]{:S(2)}) collective-permute-start(bf16[64,2,1,128]{3,0,2,1:T(8,128)(2,1)S(1)} %get-tuple-element.19), channel_id=1, source_target_pairs={{4,0},{5,1},{6,2},{7,3},{12,8},{13,9},{14,10},{15,11},{20,16},{21,... | collective-permute-start | bytes 98312 | tf_op jit(solution)/shard_map/ppermute | solution.py:47
  12.0 3.6 %collective-permute-done.5 = bf16[64,2,1,128]{3,0,2,1:T(8,128)(2,1)S(1)} collective-permute-done((bf16[64,2,1,128]{3,0,2,1:T(8,128)(2,1)S(1)}, bf16[64,2,1,128]{3,0,2,1:T(8,128)(2,1)S(1)}, u32[]{:S(2)}, u32[]{:S(2)}) %collective-permute-start.5) | collective-permute-done | bytes 32800 | tf_op jit(solution)/shard_map/ppermute | solution.py:47
  16.7 2.6 %all-to-all-done = bf16[4,3,3,128,64]{3,4,2,1,0:T(8,128)(2,1)S(1)} async-done(((bf16[4,3,3,128,64]{3,4,2,1,0:T(8,128)(2,1)}), bf16[4,3,3,128,64]{3,4,2,1,0:T(8,128)(2,1)S(1)}, u32[]{:S(2)}, u32[]{:S(2)}) %all-to-all-start) | async-done | bytes 589856 | tf_op jit(solution)/shard_map/all_to_all | solution.py:78
  19.3 6.9 %all-to-all-start.2 = ((bf16[4,64,2,6,128]{4,1,3,2,0:T(8,128)(2,1)}), bf16[4,64,2,6,128]{4,1,3,2,0:T(8,128)(2,1)S(1)}, u32[]{:S(2)}, u32[]{:S(2)}) async-start(bf16[4,64,2,6,128]{4,1,3,2,0:T(8,128)(2,1)} %pad_maximum_fusion.2), calls=%async_computation.2 | async-start | bytes 1572864 | tf_op jit(solution)/shard_map/all_to_all | solution.py:112
  26.2 2.2 %pad_dynamic-slice_fusion = (bf16[128,2,6,128]{3,2,1,0:T(8,128)(2,1)S(1)}, bf16[128,2,6,128]{3,2,1,0:T(8,128)(2,1)S(1)}) fusion(s32[]{:T(128)S(6)} %select_n.59, bf16[128,2,32,128]{3,2,1,0:T(8,128)(2,1)} %param.4, s32[]{:T(128)S(6)} %select_n.58), kind=kLoop, calls=%fused_computation | loop fusion | bytes 2883592 | tf_op jit(solution)/shard_map/dynamic_slice | solution.py:92
  28.4 1.3 %collective-permute-start = (bf16[128,2,6,128]{3,2,1,0:T(8,128)(2,1)S(1)}, bf16[128,2,6,128]{3,2,1,0:T(8,128)(2,1)}, u32[]{:S(2)}, u32[]{:S(2)}) collective-permute-start(bf16[128,2,6,128]{3,2,1,0:T(8,128)(2,1)S(1)} %get-tuple-element.9), channel_id=1, source_target_pairs={{0,4},{4,0},{1,5},{5,1},{2,6},{6,2},{3,7},{7,3},{8,12},{12,8},{9,1... | collective-permute-start | bytes 1179656 | tf_op jit(solution)/shard_map/ppermute | solution.py:96
  30.7 9.5 %collective-permute-done = bf16[128,2,6,128]{3,2,1,0:T(8,128)(2,1)} collective-permute-done((bf16[128,2,6,128]{3,2,1,0:T(8,128)(2,1)S(1)}, bf16[128,2,6,128]{3,2,1,0:T(8,128)(2,1)}, u32[]{:S(2)}, u32[]{:S(2)}) %collective-permute-start) | collective-permute-done | bytes 393248 | tf_op jit(solution)/shard_map/ppermute | solution.py:96
  40.3 3.2 %fusion.16 = bf16[256,6,2,128]{3,1,2,0:T(8,128)(2,1)S(1)} fusion(s32[]{:T(128)S(6)} %select_n.61, bf16[128,2,6,128]{3,2,1,0:T(8,128)(2,1)} %collective-permute-done, bf16[128,2,6,128]{3,2,1,0:T(8,128)(2,1)S(1)} %get-tuple-element.8), kind=kLoop, calls=%fused_computation.29 | loop fusion | flops 1179648 | bytes 1572868 | tf_op jit(solution)/shard_map/jit(_roll_dynamic)/dynamic_slice | solution.py:19
  43.5 1.3 %copy.81 = bf16[256,6,2,128]{0,2,3,1:T(2,128)(2,1)S(1)} copy(bf16[256,6,2,128]{3,1,2,0:T(8,128)(2,1)S(1)} %fusion.16) | data formatting | bytes 1572864
  45.6 1.6 %fusion.18 = bf16[256,6,2,8,19]{0,2,4,3,1:T(2,128)(2,1)} fusion(bf16[256,6,2,7,2]{0,2,4,3,1:T(2,128)(2,1)S(1)} %slice.48, bf16[256,6,2,8,17]{0,2,4,3,1:T(2,128)(2,1)S(1)} %bitcast.67), kind=kLoop, calls=%fused_computation.36 | loop fusion | flops 2801664 | bytes 1855488 | tf_op jit(solution)/shard_map/conv_general_dilated | solution.py:52
  48.2 7.9 %collective-permute-start.6 = (bf16[256,1,6,128]{3,0,2,1:T(8,128)(2,1)}, bf16[256,1,6,128]{3,0,2,1:T(8,128)(2,1)}, u32[]{:S(2)}, u32[]{:S(2)}) collective-permute-start(bf16[256,1,6,128]{3,0,2,1:T(8,128)(2,1)} %get-tuple-element.10), channel_id=1, source_target_pairs={{0,8},{8,16},{16,24},{1,9},{9,17},{17,25},{2,10},{10,18},{18,26},{... | collective-permute-start | bytes 1179656 | tf_op jit(solution)/shard_map/ppermute | solution.py:46
  56.1 1.9 %collective-permute-start.7 = (bf16[256,1,6,128]{3,0,2,1:T(8,128)(2,1)}, bf16[256,1,6,128]{3,0,2,1:T(8,128)(2,1)}, u32[]{:S(2)}, u32[]{:S(2)}) collective-permute-start(bf16[256,1,6,128]{3,0,2,1:T(8,128)(2,1)} %get-tuple-element.11), channel_id=1, source_target_pairs={{8,0},{16,8},{24,16},{9,1},{17,9},{25,17},{10,2},{18,10},{26,18},{... | collective-permute-start | bytes 1179656 | tf_op jit(solution)/shard_map/ppermute | solution.py:47
  58.0 1.9 %fusion.12 = bf16[3,3,2,128,4,64]{3,5,1,0,4,2:T(8,128)(2,1)S(1)} fusion(s32[]{:T(128)S(6)} %select_n.62, bf16[1,4,3,3,128,64]{4,5,3,2,1,0:T(8,128)(2,1)} %collective-permute-done.1, bf16[1,4,3,3,128,64]{4,5,3,2,1,0:T(8,128)(2,1)S(1)} %bitcast.70), kind=kLoop, calls=%fused_computation.25 | loop fusion | flops 1769472 | bytes 2359300 | tf_op jit(solution)/shard_map/transpose | solution.py:81
  59.9 1.2 copy.54
  62.0 3.1 %fusion.7 = bf16[4,16,17,256]{3,1,2,0:T(8,128)(2,1)S(1)} fusion(bf16[3,3,256,256]{2,3,1,0:T(8,128)(2,1)S(1)} %reshape.13, bf16[256,6,2,8,19]{0,2,4,3,1:T(2,128)(2,1)} %fusion.18, pred[16,17]{0,1:T(8,128)(4,1)S(1)} %copy-done.7), kind=kOutput, calls=%fused_computation.19 | convolution fusion | flops 1284014080 | bytes 2670864 | tf_op jit(solution)/shard_map/conv_general_dilated | solution.py:52
  65.8 3.6 %collective-permute-start.2 = (bf16[256,1,4,128]{0,2,3,1:T(4,128)(2,1)S(1)}, bf16[256,1,4,128]{0,2,3,1:T(4,128)(2,1)}, u32[]{:S(2)}, u32[]{:S(2)}) collective-permute-start(bf16[256,1,4,128]{0,2,3,1:T(4,128)(2,1)S(1)} %get-tuple-element.20), channel_id=1, source_target_pairs={{0,8},{8,16},{16,24},{1,9},{9,17},{17,25},{2,10},{10,18},{18,26},{... | collective-permute-start | bytes 786440 | tf_op jit(solution)/shard_map/ppermute | solution.py:46
  69.5 2.1 %collective-permute-start.3 = (bf16[256,1,4,128]{0,2,3,1:T(4,128)(2,1)S(1)}, bf16[256,1,4,128]{0,2,3,1:T(4,128)(2,1)}, u32[]{:S(2)}, u32[]{:S(2)}) collective-permute-start(bf16[256,1,4,128]{0,2,3,1:T(4,128)(2,1)S(1)} %get-tuple-element.21), channel_id=1, source_target_pairs={{8,0},{16,8},{24,16},{9,1},{17,9},{25,17},{10,2},{18,10},{26,18},{... | collective-permute-start | bytes 786440 | tf_op jit(solution)/shard_map/ppermute | solution.py:47
  71.6 1.3 %pad_maximum_fusion = bf16[256,4,6,128]{3,0,2,1:T(8,128)(2,1)S(1)} fusion(bf16[256,1,6,128]{3,0,2,1:T(8,128)(2,1)} %collective-permute-done.7, bf16[256,2,6,128]{3,0,2,1:T(8,128)(2,1)S(1)} %bitcast.63, bf16[256,1,6,128]{3,0,2,1:T(8,128)(2,1)} %collective-permute-done.6), kind=kLoop, calls=%fused_computation.13 | loop fusion | flops 1572864 | bytes 3145728 | tf_op jit(solution)/shard_map/concatenate | solution.py:48
  72.9 1.6 %copy.70 = bf16[256,4,6,128]{0,3,2,1:T(8,128)(2,1)} copy(bf16[256,4,6,128]{3,0,2,1:T(8,128)(2,1)S(1)} %pad_maximum_fusion) | data formatting | bytes 3145728 | tf_op jit(solution)/shard_map/concatenate | solution.py:48
  74.5 2.2 %fusion.4 = bf16[2,6,8,16,256]{4,2,3,1,0:T(8,128)(2,1)S(1)} fusion(bf16[256,4,6,8,16]{0,4,3,2,1:T(8,128)(2,1)} %bitcast.76, bf16[3,256,256]{2,1,0:T(8,128)(2,1)S(1)} %copy-done.6), kind=kOutput, calls=%fused_computation.16 | convolution fusion | flops 604372992 | bytes 2752512 | tf_op jit(solution)/shard_map/conv_general_dilated | solution.py:63
  78.5 1.6 %fusion.19 = bf16[256,6,2,8,19]{0,2,4,3,1:T(2,128)(2,1)} fusion(bf16[256,6,2,7,2]{0,2,4,3,1:T(2,128)(2,1)S(1)} %slice.58, bf16[256,6,2,8,17]{0,2,4,3,1:T(2,128)(2,1)S(1)} %bitcast.65), kind=kLoop, calls=%fused_computation.37 | loop fusion | flops 2801664 | bytes 1855488 | tf_op jit(solution)/shard_map/conv_general_dilated | solution.py:52
  80.1 1.8 %pad_maximum_fusion.1 = bf16[256,4,4,128]{0,2,3,1:T(4,128)(2,1)S(1)} fusion(bf16[256,1,4,128]{0,2,3,1:T(4,128)(2,1)} %collective-permute-done.3, bf16[256,2,4,128]{0,2,3,1:T(4,128)(2,1)S(1)} %slice_bitcast_fusion, bf16[256,1,4,128]{0,2,3,1:T(4,128)(2,1)} %collective-permute-done.2), kind=kLoop, calls=%fused_computation.30 | loop fusion | flops 1048576 | bytes 2097152 | tf_op jit(solution)/shard_map/concatenate | solution.py:48
  82.0 1.4 %convolution_convert_fusion = bf16[2,4,8,16,256]{4,2,3,1,0:T(8,128)(2,1)S(1)} fusion(bf16[256,4,4,8,16]{0,2,4,3,1:T(4,128)(2,1)S(1)} %bitcast.77, bf16[3,256,256]{2,1,0:T(8,128)(2,1)S(1)} %copy-done.5), kind=kOutput, calls=%fused_computation.21 | convolution fusion | flops 402915328 | bytes 1966080 | tf_op jit(solution)/shard_map/conv_general_dilated | solution.py:63
  84.6 4.4 %all-to-all-start.1 = ((bf16[256,2,4,128]{3,2,1,0:T(4,128)(2,1)}), bf16[256,2,4,128]{3,2,1,0:T(4,128)(2,1)S(1)}, u32[]{:S(2)}, u32[]{:S(2)}) async-start(bf16[256,2,4,128]{3,2,1,0:T(4,128)(2,1)} %copy.60), calls=%async_computation.1 | async-start | bytes 1048576 | tf_op jit(solution)/shard_map/all_to_all | solution.py:101
  89.0 1.5 %fusion.8 = bf16[4,16,17,256]{3,1,2,0:T(8,128)(2,1)S(1)} fusion(bf16[3,3,256,256]{2,3,1,0:T(8,128)(2,1)S(1)} %copy-done.1, bf16[256,6,2,8,19]{0,2,4,3,1:T(2,128)(2,1)S(1)} %copy-done.2, pred[16,17]{0,1:T(8,128)(4,1)S(1)} %copy-done.7), kind=kOutput, calls=%fused_computation.20 | convolution fusion | flops 1284014080 | bytes 2670864 | tf_op jit(solution)/shard_map/conv_general_dilated | solution.py:52
  91.2 5.2 %collective-permute-start.9 = (bf16[128,2,4,128]{0,2,3,1:T(4,128)(2,1)S(1)}, bf16[128,2,4,128]{0,2,3,1:T(4,128)(2,1)S(1)}, u32[]{:S(2)}, u32[]{:S(2)}) collective-permute-start(bf16[128,2,4,128]{0,2,3,1:T(4,128)(2,1)S(1)} %get-tuple-element.12), channel_id=1, source_target_pairs={{0,0},{1,4},{2,1},{3,5},{4,2},{5,6},{6,3},{7,7},{8,8},{9,12},{10,9... | collective-permute-start | bytes 786440 | tf_op jit(solution)/shard_map/ppermute | solution.py:127
  96.5 9.9 %collective-permute-done.8 = bf16[128,2,4,128]{0,2,3,1:T(4,128)(2,1)S(1)} collective-permute-done((bf16[128,2,4,128]{0,2,3,1:T(4,128)(2,1)S(1)}, bf16[128,2,4,128]{0,2,3,1:T(4,128)(2,1)S(1)}, u32[]{:S(2)}, u32[]{:S(2)}) %collective-permute-start.8) | collective-permute-done | bytes 262176 | tf_op jit(solution)/shard_map/ppermute | solution.py:127
  106.3 18.3 %collective-permute-done.9 = bf16[128,2,4,128]{0,2,3,1:T(4,128)(2,1)S(1)} collective-permute-done((bf16[128,2,4,128]{0,2,3,1:T(4,128)(2,1)S(1)}, bf16[128,2,4,128]{0,2,3,1:T(4,128)(2,1)S(1)}, u32[]{:S(2)}, u32[]{:S(2)}) %collective-permute-start.9) | collective-permute-done | bytes 262176 | tf_op jit(solution)/shard_map/ppermute | solution.py:127
  125.6 1.3 %copy.78 = bf16[128,2,8,128]{3,2,1,0:T(8,128)(2,1)} copy(bf16[128,2,8,128]{0,2,3,1:T(8,128)(2,1)S(1)} %fusion.26) | data formatting | bytes 1048576
  (52 shorter events, 11.3 us)
Async XLA Ops:
  0.6 6.7 %copy-start.3 = (bf16[64,2,16,128]{3,2,1,0:T(8,128)(2,1)S(1)}, bf16[64,2,16,128]{3,2,1,0:T(8,128)(2,1)}, u32[]{:S(2)}) copy-start(bf16[64,2,16,128]{3,2,1,0:T(8,128)(2,1)} %param.7) | copy-start | bytes 1572868
  2.6 16.8 %all-to-all-start = ((bf16[4,3,3,128,64]{3,4,2,1,0:T(8,128)(2,1)}), bf16[4,3,3,128,64]{3,4,2,1,0:T(8,128)(2,1)S(1)}, u32[]{:S(2)}, u32[]{:S(2)}) async-start(bf16[4,3,3,128,64]{3,4,2,1,0:T(8,128)(2,1)} %broadcast_in_dim.21), calls=%async_computation | async-start | bytes 1179648 | tf_op jit(solution)/shard_map/all_to_all | solution.py:78
  7.5 4.5 %collective-permute-start.4 = (bf16[64,2,1,128]{3,0,2,1:T(8,128)(2,1)S(1)}, bf16[64,2,1,128]{3,0,2,1:T(8,128)(2,1)S(1)}, u32[]{:S(2)}, u32[]{:S(2)}) collective-permute-start(bf16[64,2,1,128]{3,0,2,1:T(8,128)(2,1)S(1)} %get-tuple-element.18), channel_id=1, source_target_pairs={{0,4},{1,5},{2,6},{3,7},{8,12},{9,13},{10,14},{11,15},{16,20},{17,... | collective-permute-start | bytes 98312 | tf_op jit(solution)/shard_map/ppermute | solution.py:46
  10.7 5.0 %collective-permute-start.5 = (bf16[64,2,1,128]{3,0,2,1:T(8,128)(2,1)S(1)}, bf16[64,2,1,128]{3,0,2,1:T(8,128)(2,1)S(1)}, u32[]{:S(2)}, u32[]{:S(2)}) collective-permute-start(bf16[64,2,1,128]{3,0,2,1:T(8,128)(2,1)S(1)} %get-tuple-element.19), channel_id=1, source_target_pairs={{4,0},{5,1},{6,2},{7,3},{12,8},{13,9},{14,10},{15,11},{20,16},{21,... | collective-permute-start | bytes 98312 | tf_op jit(solution)/shard_map/ppermute | solution.py:47
  19.3 27.9 %all-to-all-start.2 = ((bf16[4,64,2,6,128]{4,1,3,2,0:T(8,128)(2,1)}), bf16[4,64,2,6,128]{4,1,3,2,0:T(8,128)(2,1)S(1)}, u32[]{:S(2)}, u32[]{:S(2)}) async-start(bf16[4,64,2,6,128]{4,1,3,2,0:T(8,128)(2,1)} %pad_maximum_fusion.2), calls=%async_computation.2 | async-start | bytes 1572864 | tf_op jit(solution)/shard_map/all_to_all | solution.py:112
  26.2 3.6 %copy-start.4 = (bf16[3,256,256]{2,1,0:T(8,128)(2,1)S(1)}, bf16[3,256,256]{2,1,0:T(8,128)(2,1)}, u32[]{:S(2)}) copy-start(bf16[3,256,256]{2,1,0:T(8,128)(2,1)} %param.6) | copy-start | bytes 1179652
  28.4 11.9 %collective-permute-start = (bf16[128,2,6,128]{3,2,1,0:T(8,128)(2,1)S(1)}, bf16[128,2,6,128]{3,2,1,0:T(8,128)(2,1)}, u32[]{:S(2)}, u32[]{:S(2)}) collective-permute-start(bf16[128,2,6,128]{3,2,1,0:T(8,128)(2,1)S(1)} %get-tuple-element.9), channel_id=1, source_target_pairs={{0,4},{4,0},{1,5},{5,1},{2,6},{6,2},{3,7},{7,3},{8,12},{12,8},{9,1... | collective-permute-start | bytes 1179656 | tf_op jit(solution)/shard_map/ppermute | solution.py:96
  30.5 27.5 %collective-permute-start.1 = (bf16[1,4,3,3,128,64]{4,5,3,2,1,0:T(8,128)(2,1)S(1)}, bf16[1,4,3,3,128,64]{4,5,3,2,1,0:T(8,128)(2,1)}, u32[]{:S(2)}, u32[]{:S(2)}) collective-permute-start(bf16[1,4,3,3,128,64]{4,5,3,2,1,0:T(8,128)(2,1)S(1)} %bitcast.69), channel_id=1, source_target_pairs={{0,4},{4,0},{1,5},{5,1},{2,6},{6,2},{3,7},{7,3},{8,12},{12,8},{9,1... | collective-permute-start | bytes 1769480 | tf_op jit(solution)/shard_map/ppermute | solution.py:25
  48.2 23.4 %collective-permute-start.6 = (bf16[256,1,6,128]{3,0,2,1:T(8,128)(2,1)}, bf16[256,1,6,128]{3,0,2,1:T(8,128)(2,1)}, u32[]{:S(2)}, u32[]{:S(2)}) collective-permute-start(bf16[256,1,6,128]{3,0,2,1:T(8,128)(2,1)} %get-tuple-element.10), channel_id=1, source_target_pairs={{0,8},{8,16},{16,24},{1,9},{9,17},{17,25},{2,10},{10,18},{18,26},{... | collective-permute-start | bytes 1179656 | tf_op jit(solution)/shard_map/ppermute | solution.py:46
  56.1 15.5 %collective-permute-start.7 = (bf16[256,1,6,128]{3,0,2,1:T(8,128)(2,1)}, bf16[256,1,6,128]{3,0,2,1:T(8,128)(2,1)}, u32[]{:S(2)}, u32[]{:S(2)}) collective-permute-start(bf16[256,1,6,128]{3,0,2,1:T(8,128)(2,1)} %get-tuple-element.11), channel_id=1, source_target_pairs={{8,0},{16,8},{24,16},{9,1},{17,9},{25,17},{10,2},{18,10},{26,18},{... | collective-permute-start | bytes 1179656 | tf_op jit(solution)/shard_map/ppermute | solution.py:47
  61.2 0.8 copy-start.7
  62.0 3.1 %copy-start = (bf16[3,3,256,256]{2,3,1,0:T(8,128)(2,1)}, bf16[3,3,256,256]{2,3,1,0:T(8,128)(2,1)S(1)}, u32[]{:S(2)}) copy-start(bf16[3,3,256,256]{2,3,1,0:T(8,128)(2,1)S(1)} %reshape.13) | copy-start | bytes 3538948
  65.8 14.3 %collective-permute-start.2 = (bf16[256,1,4,128]{0,2,3,1:T(4,128)(2,1)S(1)}, bf16[256,1,4,128]{0,2,3,1:T(4,128)(2,1)}, u32[]{:S(2)}, u32[]{:S(2)}) collective-permute-start(bf16[256,1,4,128]{0,2,3,1:T(4,128)(2,1)S(1)} %get-tuple-element.20), channel_id=1, source_target_pairs={{0,8},{8,16},{16,24},{1,9},{9,17},{17,25},{2,10},{10,18},{18,26},{... | collective-permute-start | bytes 786440 | tf_op jit(solution)/shard_map/ppermute | solution.py:46
  69.5 10.6 %collective-permute-start.3 = (bf16[256,1,4,128]{0,2,3,1:T(4,128)(2,1)S(1)}, bf16[256,1,4,128]{0,2,3,1:T(4,128)(2,1)}, u32[]{:S(2)}, u32[]{:S(2)}) collective-permute-start(bf16[256,1,4,128]{0,2,3,1:T(4,128)(2,1)S(1)} %get-tuple-element.21), channel_id=1, source_target_pairs={{8,0},{16,8},{24,16},{9,1},{17,9},{25,17},{10,2},{18,10},{26,18},{... | collective-permute-start | bytes 786440 | tf_op jit(solution)/shard_map/ppermute | solution.py:47
  72.9 1.6 %copy-start.6 = (bf16[3,256,256]{2,1,0:T(8,128)(2,1)S(1)}, bf16[3,256,256]{2,1,0:T(8,128)(2,1)}, u32[]{:S(2)}) copy-start(bf16[3,256,256]{2,1,0:T(8,128)(2,1)} %rev.4) | copy-start | bytes 1179652
  78.4 3.5 %copy-start.5 = (bf16[3,256,256]{2,1,0:T(8,128)(2,1)S(1)}, bf16[3,256,256]{2,1,0:T(8,128)(2,1)}, u32[]{:S(2)}) copy-start(bf16[3,256,256]{2,1,0:T(8,128)(2,1)} %param.6) | copy-start | bytes 1179652
  83.4 5.6 %copy-start.1 = (bf16[3,3,256,256]{2,3,1,0:T(8,128)(2,1)S(1)}, bf16[3,3,256,256]{2,3,1,0:T(8,128)(2,1)}, u32[]{:S(2)}) copy-start(bf16[3,3,256,256]{2,3,1,0:T(8,128)(2,1)} %copy-done) | copy-start | bytes 3538948
  83.4 5.6 %copy-start.2 = (bf16[256,6,2,8,19]{0,2,4,3,1:T(2,128)(2,1)S(1)}, bf16[256,6,2,8,19]{0,2,4,3,1:T(2,128)(2,1)}, u32[]{:S(2)}) copy-start(bf16[256,6,2,8,19]{0,2,4,3,1:T(2,128)(2,1)} %fusion.19) | copy-start | bytes 2801668
  84.6 42.4 %all-to-all-start.1 = ((bf16[256,2,4,128]{3,2,1,0:T(4,128)(2,1)}), bf16[256,2,4,128]{3,2,1,0:T(4,128)(2,1)S(1)}, u32[]{:S(2)}, u32[]{:S(2)}) async-start(bf16[256,2,4,128]{3,2,1,0:T(4,128)(2,1)} %copy.60), calls=%async_computation.1 | async-start | bytes 1048576 | tf_op jit(solution)/shard_map/all_to_all | solution.py:101
  91.1 15.2 %collective-permute-start.8 = (bf16[128,2,4,128]{0,2,3,1:T(4,128)(2,1)S(1)}, bf16[128,2,4,128]{0,2,3,1:T(4,128)(2,1)S(1)}, u32[]{:S(2)}, u32[]{:S(2)}) collective-permute-start(bf16[128,2,4,128]{0,2,3,1:T(4,128)(2,1)S(1)} %get-tuple-element.13), channel_id=1, source_target_pairs={{0,4},{1,0},{2,5},{3,1},{4,6},{5,2},{6,7},{7,3},{8,12},{9,8},{10,1... | collective-permute-start | bytes 786440 | tf_op jit(solution)/shard_map/ppermute | solution.py:127
  91.2 33.4 %collective-permute-start.9 = (bf16[128,2,4,128]{0,2,3,1:T(4,128)(2,1)S(1)}, bf16[128,2,4,128]{0,2,3,1:T(4,128)(2,1)S(1)}, u32[]{:S(2)}, u32[]{:S(2)}) collective-permute-start(bf16[128,2,4,128]{0,2,3,1:T(4,128)(2,1)S(1)} %get-tuple-element.12), channel_id=1, source_target_pairs={{0,0},{1,4},{2,1},{3,5},{4,2},{5,6},{6,3},{7,7},{8,8},{9,12},{10,9... | collective-permute-start | bytes 786440 | tf_op jit(solution)/shard_map/ppermute | solution.py:127

commit v6 on v5

--- a/solution.py
+++ b/solution.py
@@ -74,11 +74,17 @@
 def gather_weight(weight):
     filts = lax.axis_size("filt")
     chans = lax.axis_size("chan")
-    spread = jnp.broadcast_to(weight[None], (filts,) + weight.shape)
+    slabs = lax.axis_size("slab")
+    core = lax.axis_index("slab") % 2
+    c_loc, m_loc = weight.shape[2:]
+    half = c_loc // 2
+    mine = lax.dynamic_slice_in_dim(weight, core * half, half, 2)
+    spread = jnp.broadcast_to(mine[None], (filts,) + mine.shape)
     by_filt = lax.all_to_all(spread, "filt", 0, 0, tiled=True)
     both = gather_blocks(by_filt[None], "chan", 0)
-    c_loc, m_loc = weight.shape[2:]
-    whole = jnp.transpose(both, (2, 3, 0, 4, 1, 5))
+    other = lax.ppermute(both, "slab", [(i, i ^ 1) for i in range(slabs)])
+    halves = jnp.roll(jnp.stack([both, other]), core, axis=0)
+    whole = jnp.transpose(halves, (3, 4, 1, 0, 5, 2, 6))
     return whole.reshape(3, 3, chans * c_loc, filts * m_loc)
 
 

time: 129 us -> 130 us (level)
  the two profiles are of different devices: /device:TPU:9 before, /device:TPU:18 now
where the time goes in v6:
time: 130 us; the launch traced here: 129 us
  starting transfers between devices  38.7 us (30%)
  waiting for transfers between devices  38.3 us (29%)
  local copies, waits for them, and re-layouts  24.3 us (19%)
  other arithmetic  18.2 us (14%)
  matrix products  8.18 us (6%)
    ppermute x2, waiting for transfers between devices, backward(): pieces.append(lax.ppermute(block, ROWS, pairs))  21.9 us
    ppermute x1, waiting for transfers between devices, gather_blocks(): lax.ppermute(x, axis, shift_pairs(n, k))  16.4 us
    unnamed x25, local copies, waits for them, and re-layouts  9.33 us
    ppermute x3, starting transfers between devices, halo(): after = lax.ppermute(lax.slice_in_dim(x, 0, 1, axis=dim), axis, down)  8.1 us
    ppermute x3, starting transfers between devices, halo(): lax.ppermute(lax.slice_in_dim(x, length - 1, length, axis=dim), axis, up)  7.73 us
    all_to_all x1, starting transfers between devices, gather_weight(): by_filt = lax.all_to_all(spread, 'filt', 0, 0, tiled=True)  5.2 us
    all_to_all x1, starting transfers between devices, backward(): all_filters = lax.all_to_all(windows, 'filt', 0, 0, tiled=True)  5.09 us
    all_to_all x1, starting transfers between devices, forward(): return lax.all_to_all(out, 'filt', 0, 2, tiled=True)  5.09 us
  transfers between devices with their start and end apart: 14, of which 3 were waited for; matrix products, arithmetic and copies ran while one was open for 36% of the time, Pallas kernels for 0%

profile of v6, /device:TPU:18, one launch (start us, length us, event | category | flops | bytes accessed | tf_op | source)
XLA Modules:
  0.0 128.9 jit_solution(9603950949318648926)
XLA Ops:
  3.1 5.2 %all-to-all-start = ((bf16[4,2,18432]{2,1,0:T(2,128)(2,1)}), bf16[4,2,18432]{2,1,0:T(2,128)(2,1)}, u32[]{:S(2)}, u32[]{:S(2)}) async-start(bf16[4,2,18432]{2,1,0:T(2,128)(2,1)} %reshape.63), calls=%async_computation | async-start | bytes 589824 | tf_op jit(solution)/shard_map/all_to_all | solution.py:83
  8.3 1.2 copy.65
  9.6 3.4 %collective-permute-start.5 = (bf16[64,2,1,128]{3,0,2,1:T(8,128)(2,1)S(1)}, bf16[64,2,1,128]{3,0,2,1:T(8,128)(2,1)S(1)}, u32[]{:S(2)}, u32[]{:S(2)}) collective-permute-start(bf16[64,2,1,128]{3,0,2,1:T(8,128)(2,1)S(1)} %get-tuple-element.18), channel_id=1, source_target_pairs={{0,4},{1,5},{2,6},{3,7},{8,12},{9,13},{10,14},{11,15},{16,20},{17,... | collective-permute-start | bytes 98312 | tf_op jit(solution)/shard_map/ppermute | solution.py:46
  13.0 1.3 %collective-permute-start.6 = (bf16[64,2,1,128]{3,0,2,1:T(8,128)(2,1)S(1)}, bf16[64,2,1,128]{3,0,2,1:T(8,128)(2,1)S(1)}, u32[]{:S(2)}, u32[]{:S(2)}) collective-permute-start(bf16[64,2,1,128]{3,0,2,1:T(8,128)(2,1)S(1)} %get-tuple-element.19), channel_id=1, source_target_pairs={{4,0},{5,1},{6,2},{7,3},{12,8},{13,9},{14,10},{15,11},{20,16},{21,... | collective-permute-start | bytes 98312 | tf_op jit(solution)/shard_map/ppermute | solution.py:47
  14.3 1.5 %pad_dynamic-slice_fusion.4 = (bf16[128,2,6,128]{3,2,1,0:T(8,128)(2,1)}, bf16[128,2,6,128]{3,2,1,0:T(8,128)(2,1)}) fusion(s32[]{:T(128)S(6)} %select_n.76, bf16[128,2,32,128]{3,2,1,0:T(8,128)(2,1)S(1)} %copy-done.3, s32[]{:T(128)S(6)} %select_n.75), kind=kLoop, calls=%fused_computation.4 | loop fusion | bytes 2883592 | tf_op jit(solution)/shard_map/dynamic_slice | solution.py:98
  15.9 2.6 %collective-permute-start = (bf16[128,2,6,128]{3,2,1,0:T(8,128)(2,1)}, bf16[128,2,6,128]{3,2,1,0:T(8,128)(2,1)}, u32[]{:S(2)}, u32[]{:S(2)}) collective-permute-start(bf16[128,2,6,128]{3,2,1,0:T(8,128)(2,1)} %get-tuple-element.9), channel_id=1, source_target_pairs={{0,4},{4,0},{1,5},{5,1},{2,6},{6,2},{3,7},{7,3},{8,12},{12,8},{9,1... | collective-permute-start | bytes 1179656 | tf_op jit(solution)/shard_map/ppermute | solution.py:102
  18.5 1.4 %reshape.64 = bf16[4,3,3,64,64]{4,3,2,1,0:T(8,128)(2,1)S(1)} reshape(bf16[4,2,18432]{2,1,0:T(2,128)(2,1)} %all-to-all-done) | data formatting | bytes 589824
  21.1 5.1 %all-to-all-start.2 = ((bf16[4,64,2,6,128]{4,1,3,2,0:T(8,128)(2,1)}), bf16[4,64,2,6,128]{4,1,3,2,0:T(8,128)(2,1)S(1)}, u32[]{:S(2)}, u32[]{:S(2)}) async-start(bf16[4,64,2,6,128]{4,1,3,2,0:T(8,128)(2,1)} %pad_maximum_fusion.2), calls=%async_computation.2 | async-start | bytes 1572864 | tf_op jit(solution)/shard_map/all_to_all | solution.py:118
  26.2 16.4 %collective-permute-done.1 = bf16[1,4,3,3,64,64]{5,4,3,2,1,0:T(8,128)(2,1)S(1)} collective-permute-done((bf16[1,4,3,3,64,64]{5,4,3,2,1,0:T(8,128)(2,1)S(1)}, bf16[1,4,3,3,64,64]{5,4,3,2,1,0:T(8,128)(2,1)S(1)}, u32[]{:S(2)}, u32[]{:S(2)}) %collective-permute-start.1) | collective-permute-done | bytes 294944 | tf_op jit(solution)/shard_map/ppermute | solution.py:25
  42.5 2.2 %fusion.15 = bf16[2,4,3,3,64,64]{5,4,3,2,1,0:T(8,128)(2,1)} fusion(s32[]{:T(128)S(6)} %select_n.81, bf16[1,4,3,3,64,64]{5,4,3,2,1,0:T(8,128)(2,1)S(1)} %collective-permute-done.1, bf16[1,4,3,3,64,64]{5,4,3,2,1,0:T(8,128)(2,1)S(1)} %bitcast.66), kind=kLoop, calls=%fused_computation.32 | loop fusion | flops 884736 | bytes 1179652 | tf_op jit(solution)/shard_map/jit(_roll_dynamic)/concatenate | solution.py:19
  44.8 3.3 %fusion.19 = bf16[256,6,2,128]{3,1,2,0:T(8,128)(2,1)S(1)} fusion(s32[]{:T(128)S(6)} %select_n.78, bf16[128,2,6,128]{3,2,1,0:T(8,128)(2,1)} %collective-permute-done, bf16[128,2,6,128]{3,2,1,0:T(8,128)(2,1)S(1)} %copy-done.4), kind=kLoop, calls=%fused_computation.36 | loop fusion | flops 1179648 | bytes 1572868 | tf_op jit(solution)/shard_map/jit(_roll_dynamic)/dynamic_slice | solution.py:19
  48.0 1.3 %copy.83 = bf16[256,6,2,128]{0,2,3,1:T(2,128)(2,1)S(1)} copy(bf16[256,6,2,128]{3,1,2,0:T(8,128)(2,1)S(1)} %fusion.19) | data formatting | bytes 1572864
  50.1 1.7 %fusion.21 = bf16[256,6,2,8,19]{0,2,4,3,1:T(2,128)(2,1)} fusion(bf16[256,6,2,7,2]{0,2,4,3,1:T(2,128)(2,1)S(1)} %slice.48, bf16[256,6,2,8,17]{0,2,4,3,1:T(2,128)(2,1)S(1)} %bitcast.71), kind=kLoop, calls=%fused_computation.43 | loop fusion | flops 2801664 | bytes 1855488 | tf_op jit(solution)/shard_map/conv_general_dilated | solution.py:52
  53.0 3.9 %fusion.3 = bf16[3,3,2,2,64,4,64]{6,4,1,0,5,2,3:T(8,128)(2,1)S(1)} fusion(s32[]{:T(128)S(6)} %select_n.83, bf16[1,2,4,3,3,64,64]{6,5,4,3,2,1,0:T(8,128)(2,1)S(1)} %fusion.39, bf16[1,2,4,3,3,64,64]{6,5,4,3,2,1,0:T(8,128)(2,1)} %bitcast.5), kind=kLoop, calls=%fused_computation.9 | loop fusion | flops 1769472 | bytes 2359300 | tf_op jit(solution)/shard_map/transpose | solution.py:87
  56.9 2.2 %copy.56 = bf16[3,3,2,2,64,4,64]{6,5,4,3,2,1,0:T(4,128)(2,1)S(1)} copy(bf16[3,3,2,2,64,4,64]{6,4,1,0,5,2,3:T(8,128)(2,1)S(1)} %fusion.3) | data formatting | bytes 2359296 | tf_op jit(solution)/shard_map/transpose | solution.py:87
  59.1 2.7 %reshape.13 = bf16[3,3,256,256]{3,2,1,0:T(8,128)(2,1)} reshape(bf16[3,3,2,2,64,4,64]{6,5,4,3,2,1,0:T(4,128)(2,1)S(1)} %copy.56) | data formatting | bytes 2359296 | tf_op jit(solution)/shard_map/reshape | solution.py:88
  61.8 3.0 %fusion.11 = bf16[4,16,17,256]{3,1,2,0:T(8,128)(2,1)S(1)} fusion(bf16[3,3,256,256]{3,2,1,0:T(8,128)(2,1)} %reshape.13, bf16[256,6,2,8,19]{0,2,4,3,1:T(2,128)(2,1)} %fusion.21, pred[16,17]{0,1:T(8,128)(4,1)S(1)} %copy-done.8), kind=kOutput, calls=%fused_computation.27 | convolution fusion | flops 1284014080 | bytes 2670864 | tf_op jit(solution)/shard_map/conv_general_dilated | solution.py:52
  66.3 2.4 %collective-permute-start.3 = (bf16[256,1,4,128]{0,2,3,1:T(4,128)(2,1)}, bf16[256,1,4,128]{0,2,3,1:T(4,128)(2,1)}, u32[]{:S(2)}, u32[]{:S(2)}) collective-permute-start(bf16[256,1,4,128]{0,2,3,1:T(4,128)(2,1)} %get-tuple-element.20), channel_id=1, source_target_pairs={{0,8},{8,16},{16,24},{1,9},{9,17},{17,25},{2,10},{10,18},{18,26},{... | collective-permute-start | bytes 786440 | tf_op jit(solution)/shard_map/ppermute | solution.py:46
  68.7 3.2 %collective-permute-start.4 = (bf16[256,1,4,128]{0,2,3,1:T(4,128)(2,1)S(1)}, bf16[256,1,4,128]{0,2,3,1:T(4,128)(2,1)}, u32[]{:S(2)}, u32[]{:S(2)}) collective-permute-start(bf16[256,1,4,128]{0,2,3,1:T(4,128)(2,1)S(1)} %get-tuple-element.21), channel_id=1, source_target_pairs={{8,0},{16,8},{24,16},{9,1},{17,9},{25,17},{10,2},{18,10},{26,18},{... | collective-permute-start | bytes 786440 | tf_op jit(solution)/shard_map/ppermute | solution.py:47
  73.5 1.9 %collective-permute-start.7 = (bf16[256,1,6,128]{3,0,2,1:T(8,128)(2,1)}, bf16[256,1,6,128]{3,0,2,1:T(8,128)(2,1)S(1)}, u32[]{:S(2)}, u32[]{:S(2)}) collective-permute-start(bf16[256,1,6,128]{3,0,2,1:T(8,128)(2,1)} %get-tuple-element.10), channel_id=1, source_target_pairs={{0,8},{8,16},{16,24},{1,9},{9,17},{17,25},{2,10},{10,18},{18,26},{... | collective-permute-start | bytes 1179656 | tf_op jit(solution)/shard_map/ppermute | solution.py:46
  75.4 3.6 %collective-permute-start.8 = (bf16[256,1,6,128]{3,0,2,1:T(8,128)(2,1)S(1)}, bf16[256,1,6,128]{3,0,2,1:T(8,128)(2,1)}, u32[]{:S(2)}, u32[]{:S(2)}) collective-permute-start(bf16[256,1,6,128]{3,0,2,1:T(8,128)(2,1)S(1)} %get-tuple-element.11), channel_id=1, source_target_pairs={{8,0},{16,8},{24,16},{9,1},{17,9},{25,17},{10,2},{18,10},{26,18},{... | collective-permute-start | bytes 1179656 | tf_op jit(solution)/shard_map/ppermute | solution.py:47
  79.1 1.8 %pad_maximum_fusion.1 = bf16[256,4,4,128]{0,2,3,1:T(4,128)(2,1)S(1)} fusion(bf16[256,1,4,128]{0,2,3,1:T(4,128)(2,1)} %collective-permute-done.4, bf16[256,2,4,128]{0,2,3,1:T(4,128)(2,1)S(1)} %slice_bitcast_fusion, bf16[256,1,4,128]{0,2,3,1:T(4,128)(2,1)} %collective-permute-done.3), kind=kLoop, calls=%fused_computation.37 | loop fusion | flops 1048576 | bytes 2097152 | tf_op jit(solution)/shard_map/concatenate | solution.py:48
  80.9 1.4 %convolution_convert_fusion = bf16[2,4,8,16,256]{4,2,3,1,0:T(8,128)(2,1)S(1)} fusion(bf16[256,4,4,8,16]{0,2,4,3,1:T(4,128)(2,1)S(1)} %bitcast.79, bf16[3,256,256]{2,1,0:T(8,128)(2,1)S(1)} %copy-done.6), kind=kOutput, calls=%fused_computation.29 | convolution fusion | flops 402915328 | bytes 1966080 | tf_op jit(solution)/shard_map/conv_general_dilated | solution.py:63
  83.5 5.1 %all-to-all-start.1 = ((bf16[256,2,4,128]{3,2,1,0:T(4,128)(2,1)}), bf16[256,2,4,128]{3,2,1,0:T(4,128)(2,1)S(1)}, u32[]{:S(2)}, u32[]{:S(2)}) async-start(bf16[256,2,4,128]{3,2,1,0:T(4,128)(2,1)} %copy.62), calls=%async_computation.1 | async-start | bytes 1048576 | tf_op jit(solution)/shard_map/all_to_all | solution.py:107
  89.8 1.6 %copy.72 = bf16[256,4,6,128]{0,3,2,1:T(8,128)(2,1)} copy(bf16[256,4,6,128]{3,0,2,1:T(8,128)(2,1)S(1)} %pad_maximum_fusion) | data formatting | bytes 3145728 | tf_op jit(solution)/shard_map/concatenate | solution.py:48
  91.5 2.2 %fusion.8 = bf16[2,6,8,16,256]{4,2,3,1,0:T(8,128)(2,1)S(1)} fusion(bf16[256,4,6,8,16]{0,4,3,2,1:T(8,128)(2,1)} %bitcast.78, bf16[3,256,256]{2,1,0:T(8,128)(2,1)S(1)} %copy-done.7), kind=kOutput, calls=%fused_computation.24 | convolution fusion | flops 604372992 | bytes 2752512 | tf_op jit(solution)/shard_map/conv_general_dilated | solution.py:63
  96.3 1.5 %fusion.12 = bf16[4,16,17,256]{3,1,2,0:T(8,128)(2,1)S(1)} fusion(bf16[3,3,256,256]{3,2,1,0:T(8,128)(2,1)S(1)} %copy-done.5, bf16[256,6,2,8,19]{0,2,4,3,1:T(2,128)(2,1)S(1)} %fusion.22, pred[16,17]{0,1:T(8,128)(4,1)S(1)} %copy-done.8), kind=kOutput, calls=%fused_computation.28 | convolution fusion | flops 1284014080 | bytes 2670864 | tf_op jit(solution)/shard_map/conv_general_dilated | solution.py:52
  98.5 2.5 %collective-permute-start.10 = (bf16[128,2,4,128]{0,2,3,1:T(4,128)(2,1)S(1)}, bf16[128,2,4,128]{0,2,3,1:T(4,128)(2,1)S(1)}, u32[]{:S(2)}, u32[]{:S(2)}) collective-permute-start(bf16[128,2,4,128]{0,2,3,1:T(4,128)(2,1)S(1)} %get-tuple-element.12), channel_id=1, source_target_pairs={{0,0},{1,4},{2,1},{3,5},{4,2},{5,6},{6,3},{7,7},{8,8},{9,12},{10,9... | collective-permute-start | bytes 786440 | tf_op jit(solution)/shard_map/ppermute | solution.py:133
  101.0 2.3 %collective-permute-start.9 = (bf16[128,2,4,128]{0,2,3,1:T(4,128)(2,1)S(1)}, bf16[128,2,4,128]{0,2,3,1:T(4,128)(2,1)S(1)}, u32[]{:S(2)}, u32[]{:S(2)}) collective-permute-start(bf16[128,2,4,128]{0,2,3,1:T(4,128)(2,1)S(1)} %get-tuple-element.13), channel_id=1, source_target_pairs={{0,4},{1,0},{2,5},{3,1},{4,6},{5,2},{6,7},{7,3},{8,12},{9,8},{10,1... | collective-permute-start | bytes 786440 | tf_op jit(solution)/shard_map/ppermute | solution.py:133
  103.3 15.4 %collective-permute-done.10 = bf16[128,2,4,128]{0,2,3,1:T(4,128)(2,1)S(1)} collective-permute-done((bf16[128,2,4,128]{0,2,3,1:T(4,128)(2,1)S(1)}, bf16[128,2,4,128]{0,2,3,1:T(4,128)(2,1)S(1)}, u32[]{:S(2)}, u32[]{:S(2)}) %collective-permute-start.10) | collective-permute-done | bytes 262176 | tf_op jit(solution)/shard_map/ppermute | solution.py:133
  118.7 6.5 %collective-permute-done.9 = bf16[128,2,4,128]{0,2,3,1:T(4,128)(2,1)S(1)} collective-permute-done((bf16[128,2,4,128]{0,2,3,1:T(4,128)(2,1)S(1)}, bf16[128,2,4,128]{0,2,3,1:T(4,128)(2,1)S(1)}, u32[]{:S(2)}, u32[]{:S(2)}) %collective-permute-start.9) | collective-permute-done | bytes 262176 | tf_op jit(solution)/shard_map/ppermute | solution.py:133
  126.3 1.3 %copy.80 = bf16[128,2,8,128]{3,2,1,0:T(8,128)(2,1)} copy(bf16[128,2,8,128]{0,2,3,1:T(8,128)(2,1)S(1)} %fusion.29) | data formatting | bytes 1048576
  (62 shorter events, 16.4 us)
Async XLA Ops:
  0.6 0.9 copy-start
  1.8 12.5 %copy-start.3 = (bf16[128,2,32,128]{3,2,1,0:T(8,128)(2,1)S(1)}, bf16[128,2,32,128]{3,2,1,0:T(8,128)(2,1)}, u32[]{:S(2)}) copy-start(bf16[128,2,32,128]{3,2,1,0:T(8,128)(2,1)} %param.4) | copy-start | bytes 6291460
  3.1 15.4 %all-to-all-start = ((bf16[4,2,18432]{2,1,0:T(2,128)(2,1)}), bf16[4,2,18432]{2,1,0:T(2,128)(2,1)}, u32[]{:S(2)}, u32[]{:S(2)}) async-start(bf16[4,2,18432]{2,1,0:T(2,128)(2,1)} %reshape.63), calls=%async_computation | async-start | bytes 589824 | tf_op jit(solution)/shard_map/all_to_all | solution.py:83
  9.6 10.4 %collective-permute-start.5 = (bf16[64,2,1,128]{3,0,2,1:T(8,128)(2,1)S(1)}, bf16[64,2,1,128]{3,0,2,1:T(8,128)(2,1)S(1)}, u32[]{:S(2)}, u32[]{:S(2)}) collective-permute-start(bf16[64,2,1,128]{3,0,2,1:T(8,128)(2,1)S(1)} %get-tuple-element.18), channel_id=1, source_target_pairs={{0,4},{1,5},{2,6},{3,7},{8,12},{9,13},{10,14},{11,15},{16,20},{17,... | collective-permute-start | bytes 98312 | tf_op jit(solution)/shard_map/ppermute | solution.py:46
  13.0 7.0 %collective-permute-start.6 = (bf16[64,2,1,128]{3,0,2,1:T(8,128)(2,1)S(1)}, bf16[64,2,1,128]{3,0,2,1:T(8,128)(2,1)S(1)}, u32[]{:S(2)}, u32[]{:S(2)}) collective-permute-start(bf16[64,2,1,128]{3,0,2,1:T(8,128)(2,1)S(1)} %get-tuple-element.19), channel_id=1, source_target_pairs={{4,0},{5,1},{6,2},{7,3},{12,8},{13,9},{14,10},{15,11},{20,16},{21,... | collective-permute-start | bytes 98312 | tf_op jit(solution)/shard_map/ppermute | solution.py:47
  15.9 28.9 %collective-permute-start = (bf16[128,2,6,128]{3,2,1,0:T(8,128)(2,1)}, bf16[128,2,6,128]{3,2,1,0:T(8,128)(2,1)}, u32[]{:S(2)}, u32[]{:S(2)}) collective-permute-start(bf16[128,2,6,128]{3,2,1,0:T(8,128)(2,1)} %get-tuple-element.9), channel_id=1, source_target_pairs={{0,4},{4,0},{1,5},{5,1},{2,6},{6,2},{3,7},{7,3},{8,12},{12,8},{9,1... | collective-permute-start | bytes 1179656 | tf_op jit(solution)/shard_map/ppermute | solution.py:102
  19.9 22.6 %collective-permute-start.1 = (bf16[1,4,3,3,64,64]{5,4,3,2,1,0:T(8,128)(2,1)S(1)}, bf16[1,4,3,3,64,64]{5,4,3,2,1,0:T(8,128)(2,1)S(1)}, u32[]{:S(2)}, u32[]{:S(2)}) collective-permute-start(bf16[1,4,3,3,64,64]{5,4,3,2,1,0:T(8,128)(2,1)S(1)} %bitcast.65), channel_id=1, source_target_pairs={{0,4},{4,0},{1,5},{5,1},{2,6},{6,2},{3,7},{7,3},{8,12},{12,8},{9,1... | collective-permute-start | bytes 884744 | tf_op jit(solution)/shard_map/ppermute | solution.py:25
  21.1 51.6 %all-to-all-start.2 = ((bf16[4,64,2,6,128]{4,1,3,2,0:T(8,128)(2,1)}), bf16[4,64,2,6,128]{4,1,3,2,0:T(8,128)(2,1)S(1)}, u32[]{:S(2)}, u32[]{:S(2)}) async-start(bf16[4,64,2,6,128]{4,1,3,2,0:T(8,128)(2,1)} %pad_maximum_fusion.2), calls=%async_computation.2 | async-start | bytes 1572864 | tf_op jit(solution)/shard_map/all_to_all | solution.py:118
  26.2 18.6 %copy-start.4 = (bf16[128,2,6,128]{3,2,1,0:T(8,128)(2,1)S(1)}, bf16[128,2,6,128]{3,2,1,0:T(8,128)(2,1)}, u32[]{:S(2)}) copy-start(bf16[128,2,6,128]{3,2,1,0:T(8,128)(2,1)} %get-tuple-element.8) | copy-start | bytes 1179652
  42.5 2.3 %copy-start.1 = (bf16[1,4,3,3,64,64]{5,4,3,2,1,0:T(8,128)(2,1)}, bf16[1,4,3,3,64,64]{5,4,3,2,1,0:T(8,128)(2,1)S(1)}, u32[]{:S(2)}) copy-start(bf16[1,4,3,3,64,64]{5,4,3,2,1,0:T(8,128)(2,1)S(1)} %collective-permute-done.1) | copy-start | bytes 884740
  44.8 8.2 %collective-permute-start.2 = (bf16[2,4,3,3,64,64]{5,4,3,2,1,0:T(8,128)(2,1)}, bf16[2,4,3,3,64,64]{5,4,3,2,1,0:T(8,128)(2,1)}, u32[]{:S(2)}, u32[]{:S(2)}) collective-permute-start(bf16[2,4,3,3,64,64]{5,4,3,2,1,0:T(8,128)(2,1)} %fusion.15), channel_id=1, source_target_pairs={{0,8},{8,0},{16,24},{24,16},{1,9},{9,1},{17,25},{25,17},{2,10},{10... | collective-permute-start | bytes 1769480 | tf_op jit(solution)/shard_map/ppermute | solution.py:85
  49.4 2.4 %copy-start.2 = (bf16[1,4,3,3,64,64]{5,4,3,2,1,0:T(8,128)(2,1)S(1)}, bf16[1,4,3,3,64,64]{5,4,3,2,1,0:T(8,128)(2,1)}, u32[]{:S(2)}) copy-start(bf16[1,4,3,3,64,64]{5,4,3,2,1,0:T(8,128)(2,1)} %copy-done.1) | copy-start | bytes 884740
  59.1 2.7 %copy-start.8 = (pred[16,17]{0,1:T(8,128)(4,1)S(1)}, pred[16,17]{0,1:T(8,128)(4,1)}, u32[]{:S(2)}) copy-start(pred[16,17]{0,1:T(8,128)(4,1)} %constant.134) | copy-start | bytes 820
  64.9 7.0 %copy-start.6 = (bf16[3,256,256]{2,1,0:T(8,128)(2,1)S(1)}, bf16[3,256,256]{2,1,0:T(8,128)(2,1)}, u32[]{:S(2)}) copy-start(bf16[3,256,256]{2,1,0:T(8,128)(2,1)} %param.6) | copy-start | bytes 1179652
  66.3 12.8 %collective-permute-start.3 = (bf16[256,1,4,128]{0,2,3,1:T(4,128)(2,1)}, bf16[256,1,4,128]{0,2,3,1:T(4,128)(2,1)}, u32[]{:S(2)}, u32[]{:S(2)}) collective-permute-start(bf16[256,1,4,128]{0,2,3,1:T(4,128)(2,1)} %get-tuple-element.20), channel_id=1, source_target_pairs={{0,8},{8,16},{16,24},{1,9},{9,17},{17,25},{2,10},{10,18},{18,26},{... | collective-permute-start | bytes 786440 | tf_op jit(solution)/shard_map/ppermute | solution.py:46
  68.7 10.4 %collective-permute-start.4 = (bf16[256,1,4,128]{0,2,3,1:T(4,128)(2,1)S(1)}, bf16[256,1,4,128]{0,2,3,1:T(4,128)(2,1)}, u32[]{:S(2)}, u32[]{:S(2)}) collective-permute-start(bf16[256,1,4,128]{0,2,3,1:T(4,128)(2,1)S(1)} %get-tuple-element.21), channel_id=1, source_target_pairs={{8,0},{16,8},{24,16},{9,1},{17,9},{25,17},{10,2},{18,10},{26,18},{... | collective-permute-start | bytes 786440 | tf_op jit(solution)/shard_map/ppermute | solution.py:47
  73.5 15.1 %collective-permute-start.7 = (bf16[256,1,6,128]{3,0,2,1:T(8,128)(2,1)}, bf16[256,1,6,128]{3,0,2,1:T(8,128)(2,1)S(1)}, u32[]{:S(2)}, u32[]{:S(2)}) collective-permute-start(bf16[256,1,6,128]{3,0,2,1:T(8,128)(2,1)} %get-tuple-element.10), channel_id=1, source_target_pairs={{0,8},{8,16},{16,24},{1,9},{9,17},{17,25},{2,10},{10,18},{18,26},{... | collective-permute-start | bytes 1179656 | tf_op jit(solution)/shard_map/ppermute | solution.py:46
  75.4 13.2 %collective-permute-start.8 = (bf16[256,1,6,128]{3,0,2,1:T(8,128)(2,1)S(1)}, bf16[256,1,6,128]{3,0,2,1:T(8,128)(2,1)}, u32[]{:S(2)}, u32[]{:S(2)}) collective-permute-start(bf16[256,1,6,128]{3,0,2,1:T(8,128)(2,1)S(1)} %get-tuple-element.11), channel_id=1, source_target_pairs={{8,0},{16,8},{24,16},{9,1},{17,9},{25,17},{10,2},{18,10},{26,18},{... | collective-permute-start | bytes 1179656 | tf_op jit(solution)/shard_map/ppermute | solution.py:47
  83.5 44.1 %all-to-all-start.1 = ((bf16[256,2,4,128]{3,2,1,0:T(4,128)(2,1)}), bf16[256,2,4,128]{3,2,1,0:T(4,128)(2,1)S(1)}, u32[]{:S(2)}, u32[]{:S(2)}) async-start(bf16[256,2,4,128]{3,2,1,0:T(4,128)(2,1)} %copy.62), calls=%async_computation.1 | async-start | bytes 1048576 | tf_op jit(solution)/shard_map/all_to_all | solution.py:107
  89.8 1.6 %copy-start.7 = (bf16[3,256,256]{2,1,0:T(8,128)(2,1)S(1)}, bf16[3,256,256]{2,1,0:T(8,128)(2,1)}, u32[]{:S(2)}) copy-start(bf16[3,256,256]{2,1,0:T(8,128)(2,1)} %rev.4) | copy-start | bytes 1179652
  94.7 1.6 %copy-start.5 = (bf16[3,3,256,256]{3,2,1,0:T(8,128)(2,1)S(1)}, bf16[3,3,256,256]{3,2,1,0:T(8,128)(2,1)}, u32[]{:S(2)}) copy-start(bf16[3,3,256,256]{3,2,1,0:T(8,128)(2,1)} %reshape.13) | copy-start | bytes 3538948
  98.5 20.3 %collective-permute-start.10 = (bf16[128,2,4,128]{0,2,3,1:T(4,128)(2,1)S(1)}, bf16[128,2,4,128]{0,2,3,1:T(4,128)(2,1)S(1)}, u32[]{:S(2)}, u32[]{:S(2)}) collective-permute-start(bf16[128,2,4,128]{0,2,3,1:T(4,128)(2,1)S(1)} %get-tuple-element.12), channel_id=1, source_target_pairs={{0,0},{1,4},{2,1},{3,5},{4,2},{5,6},{6,3},{7,7},{8,8},{9,12},{10,9... | collective-permute-start | bytes 786440 | tf_op jit(solution)/shard_map/ppermute | solution.py:133
  101.0 24.3 %collective-permute-start.9 = (bf16[128,2,4,128]{0,2,3,1:T(4,128)(2,1)S(1)}, bf16[128,2,4,128]{0,2,3,1:T(4,128)(2,1)S(1)}, u32[]{:S(2)}, u32[]{:S(2)}) collective-permute-start(bf16[128,2,4,128]{0,2,3,1:T(4,128)(2,1)S(1)} %get-tuple-element.13), channel_id=1, source_target_pairs={{0,4},{1,0},{2,5},{3,1},{4,6},{5,2},{6,7},{7,3},{8,12},{9,8},{10,1... | collective-permute-start | bytes 786440 | tf_op jit(solution)/shard_map/ppermute | solution.py:133

commit v7 on v5

--- a/solution.py
+++ b/solution.py
@@ -82,23 +82,33 @@
     return whole.reshape(3, 3, chans * c_loc, filts * m_loc)
 
 
+def sub_block(chan, filt, filts):
+    return jnp.where(chan % 2 == 0, filt, filts - 1 - filt)
+
+
+def sub_block_of(c, f, filts):
+    return f if c % 2 == 0 else filts - 1 - f
+
+
 def forward(volume, weight, depth_weight):
     chans = lax.axis_size("chan")
     filts = lax.axis_size("filt")
+    chan = lax.axis_index("chan")
     filt = lax.axis_index("filt")
     rows = volume.shape[2] // (chans * filts)
     padded = jnp.pad(volume, ((0, 0), (0, 0), (1, 1), (0, 0)))
-    chan = lax.axis_index("chan")
-    window = lambda group: lax.dynamic_slice_in_dim(padded, group * rows, rows + 2, 2)
-    pieces = [window(chan * filts + filt)]
+    window = lambda c: lax.dynamic_slice_in_dim(padded, (c * filts + sub_block(c, filt, filts)) * rows, rows + 2, 2)
+    pieces = [window(chan)]
     for k in range(1, chans):
-        target = (chan + k) % chans
-        pieces.append(lax.ppermute(window(target * filts + filt), "chan", shift_pairs(chans, k)))
+        pieces.append(lax.ppermute(window((chan + k) % chans), "chan", shift_pairs(chans, k)))
     all_channels = order_blocks(pieces, chan, 0)
     mid = plane_conv(all_channels, weight, "HWIO").astype(jnp.bfloat16)
     deep = halo(mid, "slab", 1)
     out = depth_conv(deep, depth_weight, "DHWOI").astype(jnp.bfloat16)
-    return lax.all_to_all(out, "filt", 0, 2, tiled=True)
+    got = lax.all_to_all(out, "filt", 0, 2, tiled=True)
+    split = got.reshape(got.shape[:2] + (filts, rows) + got.shape[3:])
+    flipped = jnp.where(chan % 2 == 0, split, split[:, :, ::-1])
+    return flipped.reshape(got.shape)
 
 
 def backward(grad_out, weight, depth_weight):
@@ -107,23 +117,26 @@
     chan = lax.axis_index("chan")
     filt = lax.axis_index("filt")
     rows = grad_out.shape[2] // filts
-    rimmed = halo(grad_out, "chan", 2)
-    windows = jnp.stack([lax.slice_in_dim(rimmed, t * rows, t * rows + rows + 2, axis=2) for t in range(filts)])
-    all_filters = lax.all_to_all(windows, "filt", 0, 0, tiled=True)
+    blocks = jnp.stack(
+        [lax.dynamic_slice_in_dim(grad_out, sub_block(chan, t, filts) * rows, rows, 2) for t in range(filts)]
+    )
+    all_filters = lax.all_to_all(blocks, "filt", 0, 0, tiled=True)
     all_filters = all_filters.reshape((-1,) + all_filters.shape[2:])
     deep = halo(all_filters, "slab", 1)
     grad_mid = depth_conv(deep, depth_weight[::-1], "DHWIO").astype(jnp.bfloat16)
-    grad_in = plane_conv(grad_mid, weight[::-1, ::-1], "HWOI").astype(jnp.bfloat16)
-    place = lambda c, f: c * filts + f
+    place = lambda g: (g // filts) * filts + sub_block_of(g // filts, g % filts, filts)
+    rimmed = halo(grad_mid, ROWS, 2, place)
+    grad_in = plane_conv(rimmed, weight[::-1, ::-1], "HWOI").astype(jnp.bfloat16)
+    group = chan * filts + sub_block(chan, filt, filts)
     c_loc = grad_in.shape[0] // chans
     pieces = []
     for j in range(chans):
         pairs = []
         for c in range(chans):
             for f in range(filts):
-                group = c * filts + f
-                pairs.append((place(c, f), place((group + j) % chans, group // chans)))
-        block = lax.dynamic_slice_in_dim(grad_in, ((chan * filts + filt + j) % chans) * c_loc, c_loc, 0)
+                g = c * filts + sub_block_of(c, f, filts)
+                pairs.append((c * filts + f, ((g + j) % chans) * filts + g // chans))
+        block = lax.dynamic_slice_in_dim(grad_in, ((group + j) % chans) * c_loc, c_loc, 0)
         pieces.append(lax.ppermute(block, ROWS, pairs))
     return order_blocks(pieces, chan, 2)
 

time: 129 us -> 128 us (level)
  the two profiles are of different devices: /device:TPU:9 before, /device:TPU:13 now
where the time goes in v7:
time: 128 us; the launch traced here: 127 us
  starting transfers between devices  39.6 us (31%)
  waiting for transfers between devices  34 us (27%)
  local copies, waits for them, and re-layouts  16.7 us (13%)
  blocking collectives  16.7 us (13%)
  other arithmetic  12.2 us (10%)
  matrix products  7.17 us (6%)
    ppermute x2, waiting for transfers between devices, backward(): pieces.append(lax.ppermute(block, ROWS, pairs))  26 us
    all_to_all x1, blocking collectives, backward(): all_filters = lax.all_to_all(blocks, 'filt', 0, 0, tiled=True)  16.7 us
    ppermute x3, starting transfers between devices, halo(): lax.ppermute(lax.slice_in_dim(x, length - 1, length, axis=dim), axis, up)  14.6 us
    all_to_all x1, starting transfers between devices, forward(): got = lax.all_to_all(out, 'filt', 0, 2, tiled=True)  7.28 us
    ppermute x3, starting transfers between devices, halo(): after = lax.ppermute(lax.slice_in_dim(x, 0, 1, axis=dim), axis, down)  7.13 us
    all_to_all x1, starting transfers between devices, gather_weight(): by_filt = lax.all_to_all(spread, 'filt', 0, 0, tiled=True)  5.8 us
    ppermute x3, waiting for transfers between devices, halo(): after = lax.ppermute(lax.slice_in_dim(x, 0, 1, axis=dim), axis, down)  5.41 us
    unnamed x16, local copies, waits for them, and re-layouts  4.64 us
  transfers between devices with their start and end apart: 12, of which 5 were waited for; matrix products, arithmetic and copies ran while one was open for 17% of the time, Pallas kernels for 0%

profile of v7, /device:TPU:13, one launch (start us, length us, event | category | flops | bytes accessed | tf_op | source)
XLA Modules:
  0.0 127.5 jit_solution(3910157208516061672)
XLA Ops:
  0.7 1.5 %constant_dynamic-slice_fusion.3 = (bf16[64,2,4,128]{3,2,1,0:T(4,128)(2,1)S(1)}, bf16[64,2,4,128]{3,2,1,0:T(4,128)(2,1)S(1)}, bf16[64,2,4,128]{3,2,1,0:T(4,128)(2,1)S(1)}, bf16[64,2,4,128]{3,2,1,0:T(4,128)(2,1)S(1)}) fusion(bf16[64,2,16,128]{3,2,1,0:T(8,128)(2,1)} %param.7, s32[]{:T(128)S(6)} %select_n.130, s32[]{:T(128)S(6)} %select_n.134, ...), kind=kLoop, calls=%fused_computation.59 | loop fusion | bytes 1048592 | tf_op jit(solution)/shard_map/dynamic_slice | solution.py:121
  2.4 16.7 %all_to_all.25 = bf16[4,64,2,4,128]{4,1,3,2,0:T(8,128)(2,1)S(1)} all-to-all(bf16[4,64,2,4,128]{4,1,3,2,0:T(8,128)(2,1)S(1)} %pad_maximum_fusion.2), channel_id=1, replica_groups=mesh['slab'=4,'chan'=2,'filt'=4] {'filt'}, dimensions={0} | all-to-all | bytes 1048576 | tf_op jit(solution)/shard_map/all_to_all | solution.py:123
  20.0 5.8 %all-to-all-start = ((bf16[4,3,3,128,64]{3,4,2,1,0:T(8,128)(2,1)}), bf16[4,3,3,128,64]{3,4,2,1,0:T(8,128)(2,1)}, u32[]{:S(2)}, u32[]{:S(2)}) async-start(bf16[4,3,3,128,64]{3,4,2,1,0:T(8,128)(2,1)} %broadcast_in_dim.21), calls=%async_computation | async-start | bytes 1179648 | tf_op jit(solution)/shard_map/all_to_all | solution.py:78
  25.8 1.3 %pad_dynamic-slice_fusion = (bf16[128,2,6,128]{3,2,1,0:T(8,128)(2,1)S(1)}, bf16[128,2,6,128]{3,2,1,0:T(8,128)(2,1)}) fusion(s32[]{:T(128)S(6)} %select_n.124, bf16[128,2,32,128]{3,2,1,0:T(8,128)(2,1)S(1)} %copy-done, s32[]{:T(128)S(6)} %select_n.122), kind=kLoop, calls=%fused_computation | loop fusion | bytes 2883592 | tf_op jit(solution)/shard_map/dynamic_slice | solution.py:100
  28.1 5.4 %collective-permute-start.4 = (bf16[256,1,4,128]{3,0,2,1:T(8,128)(2,1)}, bf16[256,1,4,128]{3,0,2,1:T(8,128)(2,1)}, u32[]{:S(2)}, u32[]{:S(2)}) collective-permute-start(bf16[256,1,4,128]{3,0,2,1:T(8,128)(2,1)} %get-tuple-element.14), channel_id=1, source_target_pairs={{0,8},{8,16},{16,24},{1,9},{9,17},{17,25},{2,10},{10,18},{18,26},{... | collective-permute-start | bytes 786440 | tf_op jit(solution)/shard_map/ppermute | solution.py:46
  33.5 1.9 %collective-permute-start.5 = (bf16[256,1,4,128]{3,0,2,1:T(8,128)(2,1)S(1)}, bf16[256,1,4,128]{3,0,2,1:T(8,128)(2,1)}, u32[]{:S(2)}, u32[]{:S(2)}) collective-permute-start(bf16[256,1,4,128]{3,0,2,1:T(8,128)(2,1)S(1)} %get-tuple-element.15), channel_id=1, source_target_pairs={{8,0},{16,8},{24,16},{9,1},{17,9},{25,17},{10,2},{18,10},{26,18},{... | collective-permute-start | bytes 786440 | tf_op jit(solution)/shard_map/ppermute | solution.py:47
  36.3 2.5 %collective-permute-done = bf16[128,2,6,128]{3,2,1,0:T(8,128)(2,1)S(1)} collective-permute-done((bf16[128,2,6,128]{3,2,1,0:T(8,128)(2,1)}, bf16[128,2,6,128]{3,2,1,0:T(8,128)(2,1)S(1)}, u32[]{:S(2)}, u32[]{:S(2)}) %collective-permute-start) | collective-permute-done | bytes 393248 | tf_op jit(solution)/shard_map/ppermute | solution.py:103
  38.8 3.4 %fusion.11 = bf16[256,6,2,128]{3,1,2,0:T(8,128)(2,1)S(1)} fusion(s32[]{:T(128)S(6)} %select_n.126, bf16[128,2,6,128]{3,2,1,0:T(8,128)(2,1)S(1)} %collective-permute-done, bf16[128,2,6,128]{3,2,1,0:T(8,128)(2,1)S(1)} %get-tuple-element.8), kind=kLoop, calls=%fused_computation.26 | loop fusion | flops 1179648 | bytes 1572868 | tf_op jit(solution)/shard_map/jit(_roll_dynamic)/dynamic_slice | solution.py:19
  42.2 1.3 %copy.81 = bf16[256,6,2,128]{0,2,3,1:T(2,128)(2,1)S(1)} copy(bf16[256,6,2,128]{3,1,2,0:T(8,128)(2,1)S(1)} %fusion.11) | data formatting | bytes 1572864
  44.5 1.2 pad_maximum_fusion.1
  46.2 1.6 %convolution_convert_fusion = bf16[2,4,8,16,256]{4,2,3,1,0:T(8,128)(2,1)S(1)} fusion(bf16[256,4,4,8,16]{0,4,3,2,1:T(8,128)(2,1)S(1)} %bitcast.76, bf16[3,256,256]{2,1,0:T(8,128)(2,1)} %rev.8), kind=kOutput, calls=%fused_computation.17 | convolution fusion | flops 402915328 | bytes 1966080 | tf_op jit(solution)/shard_map/conv_general_dilated | solution.py:63
  48.0 2.3 %collective-permute-start.6 = (bf16[256,2,1,128]{0,3,2,1:T(8,128)(2,1)S(1)}, bf16[256,2,1,128]{0,3,2,1:T(8,128)(2,1)S(1)}, u32[]{:S(2)}, u32[]{:S(2)}) collective-permute-start(bf16[256,2,1,128]{0,3,2,1:T(8,128)(2,1)S(1)} %get-tuple-element.12), channel_id=1, source_target_pairs={{0,1},{1,2},{2,3},{3,7},{7,6},{6,5},{5,4},{8,9},{9,10},{10,11},{11... | collective-permute-start | bytes 393224 | tf_op jit(solution)/shard_map/ppermute | solution.py:46
  50.3 3.2 %collective-permute-start.7 = (bf16[256,2,1,128]{0,3,2,1:T(8,128)(2,1)S(1)}, bf16[256,2,1,128]{0,3,2,1:T(8,128)(2,1)S(1)}, u32[]{:S(2)}, u32[]{:S(2)}) collective-permute-start(bf16[256,2,1,128]{0,3,2,1:T(8,128)(2,1)S(1)} %get-tuple-element.13), channel_id=1, source_target_pairs={{1,0},{2,1},{3,2},{7,3},{6,7},{5,6},{4,5},{9,8},{10,9},{11,10},{15... | collective-permute-start | bytes 393224 | tf_op jit(solution)/shard_map/ppermute | solution.py:47
  53.4 1.6 %fusion.14 = bf16[256,6,2,8,19]{0,2,4,3,1:T(2,128)(2,1)} fusion(bf16[256,6,2,7,2]{0,2,4,3,1:T(2,128)(2,1)S(1)} %slice.30, bf16[256,6,2,8,17]{0,2,4,3,1:T(2,128)(2,1)S(1)} %bitcast.65), kind=kLoop, calls=%fused_computation.35 | loop fusion | flops 2801664 | bytes 1855488 | tf_op jit(solution)/shard_map/conv_general_dilated | solution.py:52
  55.1 1.3 %collective-permute-done.7 = bf16[256,2,1,128]{0,3,2,1:T(8,128)(2,1)S(1)} collective-permute-done((bf16[256,2,1,128]{0,3,2,1:T(8,128)(2,1)S(1)}, bf16[256,2,1,128]{0,3,2,1:T(8,128)(2,1)S(1)}, u32[]{:S(2)}, u32[]{:S(2)}) %collective-permute-start.7) | collective-permute-done | bytes 131104 | tf_op jit(solution)/shard_map/ppermute | solution.py:47
  58.0 2.3 %fusion.7 = bf16[3,3,2,128,4,64]{3,5,1,0,4,2:T(8,128)(2,1)S(1)} fusion(s32[]{:T(128)S(6)} %select_n.127, bf16[1,4,3,3,128,64]{4,5,3,2,1,0:T(8,128)(2,1)} %collective-permute-done.1, bf16[1,4,3,3,128,64]{4,5,3,2,1,0:T(8,128)(2,1)} %bitcast.3), kind=kLoop, calls=%fused_computation.22 | loop fusion | flops 1769472 | bytes 2359300 | tf_op jit(solution)/shard_map/transpose | solution.py:81
  60.3 1.2 copy.52
  62.3 2.7 %fusion.2 = bf16[4,16,17,256]{3,1,2,0:T(8,128)(2,1)S(1)} fusion(bf16[3,3,256,256]{2,3,1,0:T(8,128)(2,1)S(1)} %reshape.18, bf16[256,6,2,8,19]{0,2,4,3,1:T(2,128)(2,1)} %fusion.14, pred[16,17]{0,1:T(8,128)(4,1)S(1)} %copy-done.5), kind=kOutput, calls=%fused_computation.15 | convolution fusion | flops 1284014080 | bytes 2670864 | tf_op jit(solution)/shard_map/conv_general_dilated | solution.py:52
  65.7 6.9 %collective-permute-start.2 = (bf16[256,1,4,128]{0,2,3,1:T(4,128)(2,1)S(1)}, bf16[256,1,4,128]{0,2,3,1:T(4,128)(2,1)S(1)}, u32[]{:S(2)}, u32[]{:S(2)}) collective-permute-start(bf16[256,1,4,128]{0,2,3,1:T(4,128)(2,1)S(1)} %get-tuple-element.20), channel_id=1, source_target_pairs={{0,8},{8,16},{16,24},{1,9},{9,17},{17,25},{2,10},{10,18},{18,26},{... | collective-permute-start | bytes 786440 | tf_op jit(solution)/shard_map/ppermute | solution.py:46
  72.7 2.1 %collective-permute-start.3 = (bf16[256,1,4,128]{0,2,3,1:T(4,128)(2,1)S(1)}, bf16[256,1,4,128]{0,2,3,1:T(4,128)(2,1)S(1)}, u32[]{:S(2)}, u32[]{:S(2)}) collective-permute-start(bf16[256,1,4,128]{0,2,3,1:T(4,128)(2,1)S(1)} %get-tuple-element.21), channel_id=1, source_target_pairs={{8,0},{16,8},{24,16},{9,1},{17,9},{25,17},{10,2},{18,10},{26,18},{... | collective-permute-start | bytes 786440 | tf_op jit(solution)/shard_map/ppermute | solution.py:47
  74.7 1.7 %fusion.15 = bf16[256,6,2,8,19]{0,2,4,3,1:T(2,128)(2,1)} fusion(bf16[256,6,2,7,2]{0,2,4,3,1:T(2,128)(2,1)S(1)} %slice.38, bf16[256,6,2,8,17]{0,2,4,3,1:T(2,128)(2,1)S(1)} %bitcast.67), kind=kLoop, calls=%fused_computation.36 | loop fusion | flops 2801664 | bytes 1855488 | tf_op jit(solution)/shard_map/conv_general_dilated | solution.py:52
  76.4 4.1 %collective-permute-done.3 = bf16[256,1,4,128]{0,2,3,1:T(4,128)(2,1)S(1)} collective-permute-done((bf16[256,1,4,128]{0,2,3,1:T(4,128)(2,1)S(1)}, bf16[256,1,4,128]{0,2,3,1:T(4,128)(2,1)S(1)}, u32[]{:S(2)}, u32[]{:S(2)}) %collective-permute-start.3) | collective-permute-done | bytes 262176 | tf_op jit(solution)/shard_map/ppermute | solution.py:47
  81.3 1.4 %convolution_convert_fusion.1 = bf16[2,4,8,16,256]{4,2,3,1,0:T(8,128)(2,1)S(1)} fusion(bf16[256,4,4,8,16]{0,2,4,3,1:T(4,128)(2,1)S(1)} %bitcast.75, bf16[3,256,256]{2,1,0:T(8,128)(2,1)S(1)} %copy-done.3), kind=kOutput, calls=%fused_computation.18 | convolution fusion | flops 402915328 | bytes 1966080 | tf_op jit(solution)/shard_map/conv_general_dilated | solution.py:63
  82.8 1.1 copy.58
  83.9 7.3 %all-to-all-start.1 = ((bf16[256,2,4,128]{3,2,1,0:T(4,128)(2,1)}), bf16[256,2,4,128]{3,2,1,0:T(4,128)(2,1)S(1)}, u32[]{:S(2)}, u32[]{:S(2)}) async-start(bf16[256,2,4,128]{3,2,1,0:T(4,128)(2,1)} %copy.58), calls=%async_computation.1 | async-start | bytes 1048576 | tf_op jit(solution)/shard_map/all_to_all | solution.py:108
  91.2 1.5 %fusion.3 = bf16[4,16,17,256]{3,1,2,0:T(8,128)(2,1)S(1)} fusion(bf16[3,3,256,256]{2,3,1,0:T(8,128)(2,1)S(1)} %reshape.18, bf16[256,6,2,8,19]{0,2,4,3,1:T(2,128)(2,1)S(1)} %copy-done.1, pred[16,17]{0,1:T(8,128)(4,1)S(1)} %copy-done.5), kind=kOutput, calls=%fused_computation.16 | convolution fusion | flops 1284014080 | bytes 2670864 | tf_op jit(solution)/shard_map/conv_general_dilated | solution.py:52
  93.4 3.9 %collective-permute-start.9 = (bf16[128,2,4,128]{0,2,3,1:T(4,128)(2,1)S(1)}, bf16[128,2,4,128]{0,2,3,1:T(4,128)(2,1)S(1)}, u32[]{:S(2)}, u32[]{:S(2)}) collective-permute-start(bf16[128,2,4,128]{0,2,3,1:T(4,128)(2,1)S(1)} %get-tuple-element.10), channel_id=1, source_target_pairs={{0,0},{1,4},{2,1},{3,5},{4,7},{5,3},{6,6},{7,2},{8,8},{9,12},{10,9... | collective-permute-start | bytes 786440 | tf_op jit(solution)/shard_map/ppermute | solution.py:140
  97.6 19.9 %collective-permute-done.9 = bf16[128,2,4,128]{0,2,3,1:T(4,128)(2,1)S(1)} collective-permute-done((bf16[128,2,4,128]{0,2,3,1:T(4,128)(2,1)S(1)}, bf16[128,2,4,128]{0,2,3,1:T(4,128)(2,1)S(1)}, u32[]{:S(2)}, u32[]{:S(2)}) %collective-permute-start.9) | collective-permute-done | bytes 262176 | tf_op jit(solution)/shard_map/ppermute | solution.py:140
  117.5 6.1 %collective-permute-done.8 = bf16[128,2,4,128]{0,2,3,1:T(4,128)(2,1)S(1)} collective-permute-done((bf16[128,2,4,128]{0,2,3,1:T(4,128)(2,1)S(1)}, bf16[128,2,4,128]{0,2,3,1:T(4,128)(2,1)S(1)}, u32[]{:S(2)}, u32[]{:S(2)}) %collective-permute-start.8) | collective-permute-done | bytes 262176 | tf_op jit(solution)/shard_map/ppermute | solution.py:140
  123.7 1.0 fusion.22
  124.7 1.3 %copy.74 = bf16[128,2,8,128]{3,2,1,0:T(8,128)(2,1)} copy(bf16[128,2,8,128]{0,2,3,1:T(8,128)(2,1)S(1)} %fusion.22) | data formatting | bytes 1048576
  126.3 1.1 copy.73
  (50 shorter events, 9.8 us)
Async XLA Ops:
  0.7 18.4 %copy-start.4 = (bf16[3,3,128,64]{2,3,1,0:T(8,128)(2,1)S(1)}, bf16[3,3,128,64]{2,3,1,0:T(8,128)(2,1)}, u32[]{:S(2)}) copy-start(bf16[3,3,128,64]{2,3,1,0:T(8,128)(2,1)} %param.5) | copy-start | bytes 442372
  2.3 23.5 %copy-start = (bf16[128,2,32,128]{3,2,1,0:T(8,128)(2,1)S(1)}, bf16[128,2,32,128]{3,2,1,0:T(8,128)(2,1)}, u32[]{:S(2)}) copy-start(bf16[128,2,32,128]{3,2,1,0:T(8,128)(2,1)} %param.4) | copy-start | bytes 6291460
  20.0 24.2 %all-to-all-start = ((bf16[4,3,3,128,64]{3,4,2,1,0:T(8,128)(2,1)}), bf16[4,3,3,128,64]{3,4,2,1,0:T(8,128)(2,1)}, u32[]{:S(2)}, u32[]{:S(2)}) async-start(bf16[4,3,3,128,64]{3,4,2,1,0:T(8,128)(2,1)} %broadcast_in_dim.21), calls=%async_computation | async-start | bytes 1179648 | tf_op jit(solution)/shard_map/all_to_all | solution.py:78
  27.1 8.4 %copy-start.2 = (bf16[3,256,256]{2,1,0:T(8,128)(2,1)S(1)}, bf16[3,256,256]{2,1,0:T(8,128)(2,1)}, u32[]{:S(2)}) copy-start(bf16[3,256,256]{2,1,0:T(8,128)(2,1)} %param.6) | copy-start | bytes 1179652
  27.1 11.6 %collective-permute-start = (bf16[128,2,6,128]{3,2,1,0:T(8,128)(2,1)}, bf16[128,2,6,128]{3,2,1,0:T(8,128)(2,1)S(1)}, u32[]{:S(2)}, u32[]{:S(2)}) collective-permute-start(bf16[128,2,6,128]{3,2,1,0:T(8,128)(2,1)} %get-tuple-element.9), channel_id=1, source_target_pairs={{0,4},{4,0},{1,5},{5,1},{2,6},{6,2},{3,7},{7,3},{8,12},{12,8},{9,1... | collective-permute-start | bytes 1179656 | tf_op jit(solution)/shard_map/ppermute | solution.py:103
  28.1 16.4 %collective-permute-start.4 = (bf16[256,1,4,128]{3,0,2,1:T(8,128)(2,1)}, bf16[256,1,4,128]{3,0,2,1:T(8,128)(2,1)}, u32[]{:S(2)}, u32[]{:S(2)}) collective-permute-start(bf16[256,1,4,128]{3,0,2,1:T(8,128)(2,1)} %get-tuple-element.14), channel_id=1, source_target_pairs={{0,8},{8,16},{16,24},{1,9},{9,17},{17,25},{2,10},{10,18},{18,26},{... | collective-permute-start | bytes 786440 | tf_op jit(solution)/shard_map/ppermute | solution.py:46
  33.5 11.0 %collective-permute-start.5 = (bf16[256,1,4,128]{3,0,2,1:T(8,128)(2,1)S(1)}, bf16[256,1,4,128]{3,0,2,1:T(8,128)(2,1)}, u32[]{:S(2)}, u32[]{:S(2)}) collective-permute-start(bf16[256,1,4,128]{3,0,2,1:T(8,128)(2,1)S(1)} %get-tuple-element.15), channel_id=1, source_target_pairs={{8,0},{16,8},{24,16},{9,1},{17,9},{25,17},{10,2},{18,10},{26,18},{... | collective-permute-start | bytes 786440 | tf_op jit(solution)/shard_map/ppermute | solution.py:47
  44.2 13.8 %collective-permute-start.1 = (bf16[1,4,3,3,128,64]{4,5,3,2,1,0:T(8,128)(2,1)}, bf16[1,4,3,3,128,64]{4,5,3,2,1,0:T(8,128)(2,1)}, u32[]{:S(2)}, u32[]{:S(2)}) collective-permute-start(bf16[1,4,3,3,128,64]{4,5,3,2,1,0:T(8,128)(2,1)} %bitcast.3), channel_id=1, source_target_pairs={{0,4},{4,0},{1,5},{5,1},{2,6},{6,2},{3,7},{7,3},{8,12},{12,8},{9,1... | collective-permute-start | bytes 1769480 | tf_op jit(solution)/shard_map/ppermute | solution.py:25
  48.0 7.1 %collective-permute-start.6 = (bf16[256,2,1,128]{0,3,2,1:T(8,128)(2,1)S(1)}, bf16[256,2,1,128]{0,3,2,1:T(8,128)(2,1)S(1)}, u32[]{:S(2)}, u32[]{:S(2)}) collective-permute-start(bf16[256,2,1,128]{0,3,2,1:T(8,128)(2,1)S(1)} %get-tuple-element.12), channel_id=1, source_target_pairs={{0,1},{1,2},{2,3},{3,7},{7,6},{6,5},{5,4},{8,9},{9,10},{10,11},{11... | collective-permute-start | bytes 393224 | tf_op jit(solution)/shard_map/ppermute | solution.py:46
  50.3 6.1 %collective-permute-start.7 = (bf16[256,2,1,128]{0,3,2,1:T(8,128)(2,1)S(1)}, bf16[256,2,1,128]{0,3,2,1:T(8,128)(2,1)S(1)}, u32[]{:S(2)}, u32[]{:S(2)}) collective-permute-start(bf16[256,2,1,128]{0,3,2,1:T(8,128)(2,1)S(1)} %get-tuple-element.13), channel_id=1, source_target_pairs={{1,0},{2,1},{3,2},{7,3},{6,7},{5,6},{4,5},{9,8},{10,9},{11,10},{15... | collective-permute-start | bytes 393224 | tf_op jit(solution)/shard_map/ppermute | solution.py:47
  60.3 2.0 %copy-start.5 = (pred[16,17]{0,1:T(8,128)(4,1)S(1)}, pred[16,17]{0,1:T(8,128)(4,1)}, u32[]{:S(2)}) copy-start(pred[16,17]{0,1:T(8,128)(4,1)} %constant.136) | copy-start | bytes 820
  65.7 10.7 %collective-permute-start.2 = (bf16[256,1,4,128]{0,2,3,1:T(4,128)(2,1)S(1)}, bf16[256,1,4,128]{0,2,3,1:T(4,128)(2,1)S(1)}, u32[]{:S(2)}, u32[]{:S(2)}) collective-permute-start(bf16[256,1,4,128]{0,2,3,1:T(4,128)(2,1)S(1)} %get-tuple-element.20), channel_id=1, source_target_pairs={{0,8},{8,16},{16,24},{1,9},{9,17},{17,25},{2,10},{10,18},{18,26},{... | collective-permute-start | bytes 786440 | tf_op jit(solution)/shard_map/ppermute | solution.py:46
  72.6 8.6 %copy-start.3 = (bf16[3,256,256]{2,1,0:T(8,128)(2,1)S(1)}, bf16[3,256,256]{2,1,0:T(8,128)(2,1)}, u32[]{:S(2)}) copy-start(bf16[3,256,256]{2,1,0:T(8,128)(2,1)} %param.6) | copy-start | bytes 1179652
  72.7 7.8 %collective-permute-start.3 = (bf16[256,1,4,128]{0,2,3,1:T(4,128)(2,1)S(1)}, bf16[256,1,4,128]{0,2,3,1:T(4,128)(2,1)S(1)}, u32[]{:S(2)}, u32[]{:S(2)}) collective-permute-start(bf16[256,1,4,128]{0,2,3,1:T(4,128)(2,1)S(1)} %get-tuple-element.21), channel_id=1, source_target_pairs={{8,0},{16,8},{24,16},{9,1},{17,9},{25,17},{10,2},{18,10},{26,18},{... | collective-permute-start | bytes 786440 | tf_op jit(solution)/shard_map/ppermute | solution.py:47
  82.7 8.5 %copy-start.1 = (bf16[256,6,2,8,19]{0,2,4,3,1:T(2,128)(2,1)S(1)}, bf16[256,6,2,8,19]{0,2,4,3,1:T(2,128)(2,1)}, u32[]{:S(2)}) copy-start(bf16[256,6,2,8,19]{0,2,4,3,1:T(2,128)(2,1)} %fusion.15) | copy-start | bytes 2801668
  83.9 42.1 %all-to-all-start.1 = ((bf16[256,2,4,128]{3,2,1,0:T(4,128)(2,1)}), bf16[256,2,4,128]{3,2,1,0:T(4,128)(2,1)S(1)}, u32[]{:S(2)}, u32[]{:S(2)}) async-start(bf16[256,2,4,128]{3,2,1,0:T(4,128)(2,1)} %copy.58), calls=%async_computation.1 | async-start | bytes 1048576 | tf_op jit(solution)/shard_map/all_to_all | solution.py:108
  93.4 24.2 %collective-permute-start.9 = (bf16[128,2,4,128]{0,2,3,1:T(4,128)(2,1)S(1)}, bf16[128,2,4,128]{0,2,3,1:T(4,128)(2,1)S(1)}, u32[]{:S(2)}, u32[]{:S(2)}) collective-permute-start(bf16[128,2,4,128]{0,2,3,1:T(4,128)(2,1)S(1)} %get-tuple-element.10), channel_id=1, source_target_pairs={{0,0},{1,4},{2,1},{3,5},{4,7},{5,3},{6,6},{7,2},{8,8},{9,12},{10,9... | collective-permute-start | bytes 786440 | tf_op jit(solution)/shard_map/ppermute | solution.py:140
  97.3 26.4 %collective-permute-start.8 = (bf16[128,2,4,128]{0,2,3,1:T(4,128)(2,1)S(1)}, bf16[128,2,4,128]{0,2,3,1:T(4,128)(2,1)S(1)}, u32[]{:S(2)}, u32[]{:S(2)}) collective-permute-start(bf16[128,2,4,128]{0,2,3,1:T(4,128)(2,1)S(1)} %get-tuple-element.11), channel_id=1, source_target_pairs={{0,4},{1,0},{2,5},{3,1},{4,3},{5,7},{6,2},{7,6},{8,12},{9,8},{10,1... | collective-permute-start | bytes 786440 | tf_op jit(solution)/shard_map/ppermute | solution.py:140

commit v8 on v7

--- a/solution.py
+++ b/solution.py
@@ -117,28 +117,23 @@
     chan = lax.axis_index("chan")
     filt = lax.axis_index("filt")
     rows = grad_out.shape[2] // filts
-    blocks = jnp.stack(
-        [lax.dynamic_slice_in_dim(grad_out, sub_block(chan, t, filts) * rows, rows, 2) for t in range(filts)]
-    )
-    all_filters = lax.all_to_all(blocks, "filt", 0, 0, tiled=True)
-    all_filters = all_filters.reshape((-1,) + all_filters.shape[2:])
+    turn = lambda f, r: r if f % 2 == 0 else chans - 1 - r
+    place = lambda g: turn(g // chans, g % chans) * filts + g // chans
+    group = filt * chans + jnp.where(filt % 2 == 0, chan, chans - 1 - chan)
+    pieces = []
+    for k in range(filts):
+        pairs = [(c * filts + f, place(c * filts + (f + k) % filts)) for f in range(filts) for c in range(chans)]
+        block = lax.dynamic_slice_in_dim(grad_out, ((filt + k) % filts) * rows, rows, 2)
+        pieces.append(lax.ppermute(block, ROWS, pairs))
+    all_filters = order_blocks(pieces, group % filts, 0)
     deep = halo(all_filters, "slab", 1)
     grad_mid = depth_conv(deep, depth_weight[::-1], "DHWIO").astype(jnp.bfloat16)
-    place = lambda g: (g // filts) * filts + sub_block_of(g // filts, g % filts, filts)
     rimmed = halo(grad_mid, ROWS, 2, place)
     grad_in = plane_conv(rimmed, weight[::-1, ::-1], "HWOI").astype(jnp.bfloat16)
-    group = chan * filts + sub_block(chan, filt, filts)
-    c_loc = grad_in.shape[0] // chans
-    pieces = []
-    for j in range(chans):
-        pairs = []
-        for c in range(chans):
-            for f in range(filts):
-                g = c * filts + sub_block_of(c, f, filts)
-                pairs.append((c * filts + f, ((g + j) % chans) * filts + g // chans))
-        block = lax.dynamic_slice_in_dim(grad_in, ((group + j) % chans) * c_loc, c_loc, 0)
-        pieces.append(lax.ppermute(block, ROWS, pairs))
-    return order_blocks(pieces, chan, 2)
+    got = lax.all_to_all(grad_in, "chan", 0, 2, tiled=True)
+    split = got.reshape(got.shape[:2] + (chans, rows) + got.shape[3:])
+    flipped = jnp.where(filt % 2 == 0, split, split[:, :, ::-1])
+    return flipped.reshape(got.shape)
 
 
 def local(volume, plane_weight, depth_weight, grad_out):

time: 128 us -> 148 us (1.16)
  the two profiles are of different devices: /device:TPU:13 before, /device:TPU:1 now
where the time goes in v8:
time: 148 us
  waiting for transfers between devices  55.2 us (37%)
  starting transfers between devices  53.9 us (36%)
  local copies, waits for them, and re-layouts  21.5 us (15%)
  other arithmetic  10.8 us (7%)
  matrix products  5.03 us (3%)
    ppermute x4, waiting for transfers between devices, backward(): pieces.append(lax.ppermute(block, ROWS, pairs))  29 us
    all_to_all x1, waiting for transfers between devices, forward(): got = lax.all_to_all(out, 'filt', 0, 2, tiled=True)  13.4 us
    ppermute x3, starting transfers between devices, halo(): lax.ppermute(lax.slice_in_dim(x, length - 1, length, axis=dim), axis, up)  12 us
    ppermute x1, starting transfers between devices, gather_blocks(): lax.ppermute(x, axis, shift_pairs(n, k))  9.97 us
    ppermute x4, starting transfers between devices, backward(): pieces.append(lax.ppermute(block, ROWS, pairs))  9.89 us
    all_to_all x1, starting transfers between devices, forward(): got = lax.all_to_all(out, 'filt', 0, 2, tiled=True)  7.34 us
    all_to_all x1, starting transfers between devices, gather_weight(): by_filt = lax.all_to_all(spread, 'filt', 0, 0, tiled=True)  5.86 us
    unnamed x22, local copies, waits for them, and re-layouts  5.41 us
  transfers between devices with their start and end apart: 15, of which 6 were waited for; matrix products, arithmetic and copies ran while one was open for 20% of the time, Pallas kernels for 0%

profile of v8, /device:TPU:1, one launch (start us, length us, event | category | flops | bytes accessed | tf_op | source)
XLA Modules:
  0.0 147.6 jit_solution(169903441353267988)
XLA Ops:
  0.7 1.5 %constant_dynamic-slice_fusion.3 = (bf16[64,2,4,128]{3,2,1,0:T(4,128)(2,1)S(1)}, bf16[64,2,4,128]{3,2,1,0:T(4,128)(2,1)S(1)}, bf16[64,2,4,128]{3,2,1,0:T(4,128)(2,1)S(1)}, bf16[64,2,4,128]{3,2,1,0:T(4,128)(2,1)S(1)}) fusion(bf16[64,2,16,128]{3,2,1,0:T(8,128)(2,1)} %param.7, s32[]{:T(128)S(6)} %select_n.137, s32[]{:T(128)S(6)} %select_n.135, ...), kind=kLoop, calls=%fused_computation.47 | loop fusion | bytes 1048592 | tf_op jit(solution)/shard_map/dynamic_slice | solution.py:126
  2.4 4.0 %collective-permute-start.4 = (bf16[64,2,4,128]{0,3,2,1:T(8,128)(2,1)S(1)}, bf16[64,2,4,128]{0,3,2,1:T(8,128)(2,1)S(1)}, u32[]{:S(2)}, u32[]{:S(2)}) collective-permute-start(bf16[64,2,4,128]{0,3,2,1:T(8,128)(2,1)S(1)} %copy.108), channel_id=1, source_target_pairs={{0,1},{4,3},{1,0},{5,2},{2,4},{6,6},{3,5},{7,7},{8,9},{12,11},{9,8... | collective-permute-start | bytes 393224 | tf_op jit(solution)/shard_map/ppermute | solution.py:127
  6.7 4.1 %collective-permute-start.5 = (bf16[64,2,4,128]{0,3,2,1:T(8,128)(2,1)S(1)}, bf16[64,2,4,128]{0,3,2,1:T(8,128)(2,1)S(1)}, u32[]{:S(2)}, u32[]{:S(2)}) collective-permute-start(bf16[64,2,4,128]{0,3,2,1:T(8,128)(2,1)S(1)} %copy.109), channel_id=1, source_target_pairs={{0,5},{4,7},{1,1},{5,3},{2,0},{6,2},{3,4},{7,6},{8,13},{12,15},{9,... | collective-permute-start | bytes 393224 | tf_op jit(solution)/shard_map/ppermute | solution.py:127
  13.9 5.9 %all-to-all-start = ((bf16[4,3,3,128,64]{3,4,2,1,0:T(8,128)(2,1)}), bf16[4,3,3,128,64]{3,4,2,1,0:T(8,128)(2,1)S(1)}, u32[]{:S(2)}, u32[]{:S(2)}) async-start(bf16[4,3,3,128,64]{3,4,2,1,0:T(8,128)(2,1)} %broadcast_in_dim.21), calls=%async_computation | async-start | bytes 1179648 | tf_op jit(solution)/shard_map/all_to_all | solution.py:78
  19.8 29.0 %collective-permute-done.5 = bf16[64,2,4,128]{0,3,2,1:T(8,128)(2,1)S(1)} collective-permute-done((bf16[64,2,4,128]{0,3,2,1:T(8,128)(2,1)S(1)}, bf16[64,2,4,128]{0,3,2,1:T(8,128)(2,1)S(1)}, u32[]{:S(2)}, u32[]{:S(2)}) %collective-permute-start.5) | collective-permute-done | bytes 131104 | tf_op jit(solution)/shard_map/ppermute | solution.py:127
  50.7 5.6 %collective-permute-start.8 = (bf16[256,1,4,128]{0,3,2,1:T(8,128)(2,1)}, bf16[256,1,4,128]{0,3,2,1:T(8,128)(2,1)}, u32[]{:S(2)}, u32[]{:S(2)}) collective-permute-start(bf16[256,1,4,128]{0,3,2,1:T(8,128)(2,1)} %get-tuple-element.10), channel_id=1, source_target_pairs={{0,8},{8,16},{16,24},{1,9},{9,17},{17,25},{2,10},{10,18},{18,26},{... | collective-permute-start | bytes 786440 | tf_op jit(solution)/shard_map/ppermute | solution.py:46
  56.2 1.9 %collective-permute-start.9 = (bf16[256,1,4,128]{0,3,2,1:T(8,128)(2,1)S(1)}, bf16[256,1,4,128]{0,3,2,1:T(8,128)(2,1)}, u32[]{:S(2)}, u32[]{:S(2)}) collective-permute-start(bf16[256,1,4,128]{0,3,2,1:T(8,128)(2,1)S(1)} %get-tuple-element.11), channel_id=1, source_target_pairs={{8,0},{16,8},{24,16},{9,1},{17,9},{25,17},{10,2},{18,10},{26,18},{... | collective-permute-start | bytes 786440 | tf_op jit(solution)/shard_map/ppermute | solution.py:47
  58.2 2.7 %pad_dynamic-slice_fusion = (bf16[128,2,6,128]{3,2,1,0:T(8,128)(2,1)S(1)}, bf16[128,2,6,128]{3,2,1,0:T(8,128)(2,1)}) fusion(s32[]{:T(128)S(6)} %select_n.123, bf16[128,2,32,128]{3,2,1,0:T(8,128)(2,1)} %param.4, s32[]{:T(128)S(6)} %select_n.121), kind=kLoop, calls=%fused_computation | loop fusion | bytes 2883592 | tf_op jit(solution)/shard_map/dynamic_slice | solution.py:100
  61.9 2.4 %collective-permute-done.9 = bf16[256,1,4,128]{0,3,2,1:T(8,128)(2,1)} collective-permute-done((bf16[256,1,4,128]{0,3,2,1:T(8,128)(2,1)S(1)}, bf16[256,1,4,128]{0,3,2,1:T(8,128)(2,1)}, u32[]{:S(2)}, u32[]{:S(2)}) %collective-permute-start.9) | collective-permute-done | bytes 262176 | tf_op jit(solution)/shard_map/ppermute | solution.py:47
  64.2 1.1 pad_maximum_fusion.1
  66.9 1.9 %collective-permute-start.10 = (bf16[256,2,1,128]{0,3,2,1:T(8,128)(2,1)}, bf16[256,2,1,128]{0,3,2,1:T(8,128)(2,1)}, u32[]{:S(2)}, u32[]{:S(2)}) collective-permute-start(bf16[256,2,1,128]{0,3,2,1:T(8,128)(2,1)} %get-tuple-element.12), channel_id=1, source_target_pairs={{0,4},{4,5},{5,1},{1,2},{2,6},{6,7},{7,3},{8,12},{12,13},{13,9},{9... | collective-permute-start | bytes 393224 | tf_op jit(solution)/shard_map/ppermute | solution.py:46
  68.8 1.3 collective-permute-start.11
  70.1 3.4 %collective-permute-done = bf16[128,2,6,128]{3,2,1,0:T(8,128)(2,1)S(1)} collective-permute-done((bf16[128,2,6,128]{3,2,1,0:T(8,128)(2,1)}, bf16[128,2,6,128]{3,2,1,0:T(8,128)(2,1)S(1)}, u32[]{:S(2)}, u32[]{:S(2)}) %collective-permute-start) | collective-permute-done | bytes 393248 | tf_op jit(solution)/shard_map/ppermute | solution.py:103
  73.5 3.4 %fusion.11 = bf16[256,6,2,128]{3,1,2,0:T(8,128)(2,1)S(1)} fusion(s32[]{:T(128)S(6)} %select_n.125, bf16[128,2,6,128]{3,2,1,0:T(8,128)(2,1)S(1)} %collective-permute-done, bf16[128,2,6,128]{3,2,1,0:T(8,128)(2,1)S(1)} %get-tuple-element.8), kind=kLoop, calls=%fused_computation.26 | loop fusion | flops 1179648 | bytes 1572868 | tf_op jit(solution)/shard_map/jit(_roll_dynamic)/dynamic_slice | solution.py:19
  76.9 1.5 %copy.112 = bf16[256,6,2,128]{0,2,3,1:T(2,128)(2,1)S(1)} copy(bf16[256,6,2,128]{3,1,2,0:T(8,128)(2,1)S(1)} %fusion.11) | data formatting | bytes 1572864
  79.1 10.0 %collective-permute-start.1 = (bf16[1,4,3,3,128,64]{4,5,3,2,1,0:T(8,128)(2,1)S(1)}, bf16[1,4,3,3,128,64]{4,5,3,2,1,0:T(8,128)(2,1)S(1)}, u32[]{:S(2)}, u32[]{:S(2)}) collective-permute-start(bf16[1,4,3,3,128,64]{4,5,3,2,1,0:T(8,128)(2,1)S(1)} %bitcast.61), channel_id=1, source_target_pairs={{0,4},{4,0},{1,5},{5,1},{2,6},{6,2},{3,7},{7,3},{8,12},{12,8},{9,1... | collective-permute-start | bytes 1769480 | tf_op jit(solution)/shard_map/ppermute | solution.py:25
  89.1 1.6 %fusion.14 = bf16[256,6,2,8,19]{0,2,4,3,1:T(2,128)(2,1)} fusion(bf16[256,6,2,7,2]{0,2,4,3,1:T(2,128)(2,1)S(1)} %slice.30, bf16[256,6,2,8,17]{0,2,4,3,1:T(2,128)(2,1)S(1)} %bitcast.56), kind=kLoop, calls=%fused_computation.31 | loop fusion | flops 2801664 | bytes 1855488 | tf_op jit(solution)/shard_map/conv_general_dilated | solution.py:52
  93.3 1.7 %fusion.15 = bf16[256,6,2,8,19]{0,2,4,3,1:T(2,128)(2,1)} fusion(bf16[256,6,2,7,2]{0,2,4,3,1:T(2,128)(2,1)S(1)} %slice.36, bf16[256,6,2,8,17]{0,2,4,3,1:T(2,128)(2,1)S(1)} %bitcast.58), kind=kLoop, calls=%fused_computation.32 | loop fusion | flops 2801664 | bytes 1855488 | tf_op jit(solution)/shard_map/conv_general_dilated | solution.py:52
  95.0 4.5 %collective-permute-done.1 = bf16[1,4,3,3,128,64]{4,5,3,2,1,0:T(8,128)(2,1)S(1)} collective-permute-done((bf16[1,4,3,3,128,64]{4,5,3,2,1,0:T(8,128)(2,1)S(1)}, bf16[1,4,3,3,128,64]{4,5,3,2,1,0:T(8,128)(2,1)S(1)}, u32[]{:S(2)}, u32[]{:S(2)}) %collective-permute-start.1) | collective-permute-done | bytes 589856 | tf_op jit(solution)/shard_map/ppermute | solution.py:25
  100.4 1.2 copy.82
  102.4 1.5 %fusion.2 = bf16[4,16,17,256]{3,1,2,0:T(8,128)(2,1)S(1)} fusion(bf16[3,3,256,256]{2,3,1,0:T(8,128)(2,1)S(1)} %reshape.20, bf16[256,6,2,8,19]{0,2,4,3,1:T(2,128)(2,1)S(1)} %copy-done, pred[16,17]{0,1:T(8,128)(4,1)S(1)} %copy-done.6), kind=kOutput, calls=%fused_computation.15 | convolution fusion | flops 1284014080 | bytes 2670864 | tf_op jit(solution)/shard_map/conv_general_dilated | solution.py:52
  104.6 4.5 %collective-permute-start.2 = (bf16[256,1,4,128]{0,2,3,1:T(4,128)(2,1)S(1)}, bf16[256,1,4,128]{0,2,3,1:T(4,128)(2,1)S(1)}, u32[]{:S(2)}, u32[]{:S(2)}) collective-permute-start(bf16[256,1,4,128]{0,2,3,1:T(4,128)(2,1)S(1)} %get-tuple-element.18), channel_id=1, source_target_pairs={{0,8},{8,16},{16,24},{1,9},{9,17},{17,25},{2,10},{10,18},{18,26},{... | collective-permute-start | bytes 786440 | tf_op jit(solution)/shard_map/ppermute | solution.py:46
  109.1 1.9 %collective-permute-start.3 = (bf16[256,1,4,128]{0,2,3,1:T(4,128)(2,1)S(1)}, bf16[256,1,4,128]{0,2,3,1:T(4,128)(2,1)S(1)}, u32[]{:S(2)}, u32[]{:S(2)}) collective-permute-start(bf16[256,1,4,128]{0,2,3,1:T(4,128)(2,1)S(1)} %get-tuple-element.19), channel_id=1, source_target_pairs={{8,0},{16,8},{24,16},{9,1},{17,9},{25,17},{10,2},{18,10},{26,18},{... | collective-permute-start | bytes 786440 | tf_op jit(solution)/shard_map/ppermute | solution.py:47
  111.1 1.5 fusion.3
  113.0 1.3 copy.101
  114.3 3.7 %all-to-all-start.2 = ((bf16[256,2,4,128]{3,2,1,0:T(4,128)(2,1)}), bf16[256,2,4,128]{3,2,1,0:T(4,128)(2,1)S(1)}, u32[]{:S(2)}, u32[]{:S(2)}) async-start(bf16[256,2,4,128]{3,2,1,0:T(4,128)(2,1)} %copy.101), calls=%async_computation.2 | async-start | bytes 1048576 | tf_op jit(solution)/shard_map/all_to_all | solution.py:133
  118.9 1.4 convolution_convert_fusion.1
  121.5 2.5 %all-to-all-done.2 = bf16[256,2,4,128]{3,2,1,0:T(4,128)(2,1)S(1)} async-done(((bf16[256,2,4,128]{3,2,1,0:T(4,128)(2,1)}), bf16[256,2,4,128]{3,2,1,0:T(4,128)(2,1)S(1)}, u32[]{:S(2)}, u32[]{:S(2)}) %all-to-all-start.2) | async-done | bytes 524320 | tf_op jit(solution)/shard_map/all_to_all | solution.py:133
  124.0 7.3 %all-to-all-start.1 = ((bf16[256,2,4,128]{3,2,1,0:T(4,128)(2,1)}), bf16[256,2,4,128]{3,2,1,0:T(4,128)(2,1)S(1)}, u32[]{:S(2)}, u32[]{:S(2)}) async-start(bf16[256,2,4,128]{3,2,1,0:T(4,128)(2,1)} %copy.88), calls=%async_computation.1 | async-start | bytes 1048576 | tf_op jit(solution)/shard_map/all_to_all | solution.py:108
  131.6 1.1 copy.105
  132.8 13.4 %all-to-all-done.1 = bf16[256,2,4,128]{3,2,1,0:T(4,128)(2,1)S(1)} async-done(((bf16[256,2,4,128]{3,2,1,0:T(4,128)(2,1)}), bf16[256,2,4,128]{3,2,1,0:T(4,128)(2,1)S(1)}, u32[]{:S(2)}, u32[]{:S(2)}) %all-to-all-start.1) | async-done | bytes 524320 | tf_op jit(solution)/shard_map/all_to_all | solution.py:108
  146.4 1.1 copy.104
  (60 shorter events, 16.4 us)
Async XLA Ops:
  0.6 12.3 %copy-start.5 = (bf16[3,3,128,64]{2,3,1,0:T(8,128)(2,1)S(1)}, bf16[3,3,128,64]{2,3,1,0:T(8,128)(2,1)}, u32[]{:S(2)}) copy-start(bf16[3,3,128,64]{2,3,1,0:T(8,128)(2,1)} %param.5) | copy-start | bytes 442372
  2.4 17.4 %collective-permute-start.4 = (bf16[64,2,4,128]{0,3,2,1:T(8,128)(2,1)S(1)}, bf16[64,2,4,128]{0,3,2,1:T(8,128)(2,1)S(1)}, u32[]{:S(2)}, u32[]{:S(2)}) collective-permute-start(bf16[64,2,4,128]{0,3,2,1:T(8,128)(2,1)S(1)} %copy.108), channel_id=1, source_target_pairs={{0,1},{4,3},{1,0},{5,2},{2,4},{6,6},{3,5},{7,7},{8,9},{12,11},{9,8... | collective-permute-start | bytes 393224 | tf_op jit(solution)/shard_map/ppermute | solution.py:127
  6.7 42.1 %collective-permute-start.5 = (bf16[64,2,4,128]{0,3,2,1:T(8,128)(2,1)S(1)}, bf16[64,2,4,128]{0,3,2,1:T(8,128)(2,1)S(1)}, u32[]{:S(2)}, u32[]{:S(2)}) collective-permute-start(bf16[64,2,4,128]{0,3,2,1:T(8,128)(2,1)S(1)} %copy.109), channel_id=1, source_target_pairs={{0,5},{4,7},{1,1},{5,3},{2,0},{6,2},{3,4},{7,6},{8,13},{12,15},{9,... | collective-permute-start | bytes 393224 | tf_op jit(solution)/shard_map/ppermute | solution.py:127
  11.0 37.8 %collective-permute-start.6 = (bf16[64,2,4,128]{0,3,2,1:T(8,128)(2,1)S(1)}, bf16[64,2,4,128]{0,3,2,1:T(8,128)(2,1)S(1)}, u32[]{:S(2)}, u32[]{:S(2)}) collective-permute-start(bf16[64,2,4,128]{0,3,2,1:T(8,128)(2,1)S(1)} %copy.110), channel_id=1, source_target_pairs={{0,4},{4,6},{1,5},{5,7},{2,1},{6,3},{3,0},{7,2},{8,12},{12,14},{9,... | collective-permute-start | bytes 393224 | tf_op jit(solution)/shard_map/ppermute | solution.py:127
  12.3 36.5 %collective-permute-start.7 = (bf16[64,2,4,128]{0,3,2,1:T(8,128)(2,1)S(1)}, bf16[64,2,4,128]{0,3,2,1:T(8,128)(2,1)S(1)}, u32[]{:S(2)}, u32[]{:S(2)}) collective-permute-start(bf16[64,2,4,128]{0,3,2,1:T(8,128)(2,1)S(1)} %copy.111), channel_id=1, source_target_pairs={{0,0},{4,2},{1,4},{5,6},{2,5},{6,7},{3,1},{7,3},{8,8},{12,10},{9,1... | collective-permute-start | bytes 393224 | tf_op jit(solution)/shard_map/ppermute | solution.py:127
  13.9 65.2 %all-to-all-start = ((bf16[4,3,3,128,64]{3,4,2,1,0:T(8,128)(2,1)}), bf16[4,3,3,128,64]{3,4,2,1,0:T(8,128)(2,1)S(1)}, u32[]{:S(2)}, u32[]{:S(2)}) async-start(bf16[4,3,3,128,64]{3,4,2,1,0:T(8,128)(2,1)} %broadcast_in_dim.21), calls=%async_computation | async-start | bytes 1179648 | tf_op jit(solution)/shard_map/all_to_all | solution.py:78
  49.7 11.1 %copy-start.2 = (bf16[3,256,256]{2,1,0:T(8,128)(2,1)S(1)}, bf16[3,256,256]{2,1,0:T(8,128)(2,1)}, u32[]{:S(2)}) copy-start(bf16[3,256,256]{2,1,0:T(8,128)(2,1)} %param.6) | copy-start | bytes 1179652
  50.7 11.2 %collective-permute-start.8 = (bf16[256,1,4,128]{0,3,2,1:T(8,128)(2,1)}, bf16[256,1,4,128]{0,3,2,1:T(8,128)(2,1)}, u32[]{:S(2)}, u32[]{:S(2)}) collective-permute-start(bf16[256,1,4,128]{0,3,2,1:T(8,128)(2,1)} %get-tuple-element.10), channel_id=1, source_target_pairs={{0,8},{8,16},{16,24},{1,9},{9,17},{17,25},{2,10},{10,18},{18,26},{... | collective-permute-start | bytes 786440 | tf_op jit(solution)/shard_map/ppermute | solution.py:46
  56.2 8.0 %collective-permute-start.9 = (bf16[256,1,4,128]{0,3,2,1:T(8,128)(2,1)S(1)}, bf16[256,1,4,128]{0,3,2,1:T(8,128)(2,1)}, u32[]{:S(2)}, u32[]{:S(2)}) collective-permute-start(bf16[256,1,4,128]{0,3,2,1:T(8,128)(2,1)S(1)} %get-tuple-element.11), channel_id=1, source_target_pairs={{8,0},{16,8},{24,16},{9,1},{17,9},{25,17},{10,2},{18,10},{26,18},{... | collective-permute-start | bytes 786440 | tf_op jit(solution)/shard_map/ppermute | solution.py:47
  60.8 12.7 %collective-permute-start = (bf16[128,2,6,128]{3,2,1,0:T(8,128)(2,1)}, bf16[128,2,6,128]{3,2,1,0:T(8,128)(2,1)S(1)}, u32[]{:S(2)}, u32[]{:S(2)}) collective-permute-start(bf16[128,2,6,128]{3,2,1,0:T(8,128)(2,1)} %get-tuple-element.9), channel_id=1, source_target_pairs={{0,4},{4,0},{1,5},{5,1},{2,6},{6,2},{3,7},{7,3},{8,12},{12,8},{9,1... | collective-permute-start | bytes 1179656 | tf_op jit(solution)/shard_map/ppermute | solution.py:103
  61.6 3.8 %copy-start.4 = (bf16[3,256,256]{2,1,0:T(8,128)(2,1)S(1)}, bf16[3,256,256]{2,1,0:T(8,128)(2,1)}, u32[]{:S(2)}) copy-start(bf16[3,256,256]{2,1,0:T(8,128)(2,1)} %rev.11) | copy-start | bytes 1179652
  66.9 23.9 %collective-permute-start.10 = (bf16[256,2,1,128]{0,3,2,1:T(8,128)(2,1)}, bf16[256,2,1,128]{0,3,2,1:T(8,128)(2,1)}, u32[]{:S(2)}, u32[]{:S(2)}) collective-permute-start(bf16[256,2,1,128]{0,3,2,1:T(8,128)(2,1)} %get-tuple-element.12), channel_id=1, source_target_pairs={{0,4},{4,5},{5,1},{1,2},{2,6},{6,7},{7,3},{8,12},{12,13},{13,9},{9... | collective-permute-start | bytes 393224 | tf_op jit(solution)/shard_map/ppermute | solution.py:46
  68.8 22.0 %collective-permute-start.11 = (bf16[256,2,1,128]{0,3,2,1:T(8,128)(2,1)}, bf16[256,2,1,128]{0,3,2,1:T(8,128)(2,1)}, u32[]{:S(2)}, u32[]{:S(2)}) collective-permute-start(bf16[256,2,1,128]{0,3,2,1:T(8,128)(2,1)} %get-tuple-element.13), channel_id=1, source_target_pairs={{4,0},{5,4},{1,5},{2,1},{6,2},{7,6},{3,7},{12,8},{13,12},{9,13},{1... | collective-permute-start | bytes 393224 | tf_op jit(solution)/shard_map/ppermute | solution.py:47
  79.1 20.4 %collective-permute-start.1 = (bf16[1,4,3,3,128,64]{4,5,3,2,1,0:T(8,128)(2,1)S(1)}, bf16[1,4,3,3,128,64]{4,5,3,2,1,0:T(8,128)(2,1)S(1)}, u32[]{:S(2)}, u32[]{:S(2)}) collective-permute-start(bf16[1,4,3,3,128,64]{4,5,3,2,1,0:T(8,128)(2,1)S(1)} %bitcast.61), channel_id=1, source_target_pairs={{0,4},{4,0},{1,5},{5,1},{2,6},{6,2},{3,7},{7,3},{8,12},{12,8},{9,1... | collective-permute-start | bytes 1769480 | tf_op jit(solution)/shard_map/ppermute | solution.py:25
  100.4 2.0 %copy-start = (bf16[256,6,2,8,19]{0,2,4,3,1:T(2,128)(2,1)S(1)}, bf16[256,6,2,8,19]{0,2,4,3,1:T(2,128)(2,1)}, u32[]{:S(2)}) copy-start(bf16[256,6,2,8,19]{0,2,4,3,1:T(2,128)(2,1)} %fusion.14) | copy-start | bytes 2801668
  100.4 2.0 %copy-start.6 = (pred[16,17]{0,1:T(8,128)(4,1)S(1)}, pred[16,17]{0,1:T(8,128)(4,1)}, u32[]{:S(2)}) copy-start(pred[16,17]{0,1:T(8,128)(4,1)} %constant.142) | copy-start | bytes 820
  103.9 7.1 %copy-start.1 = (bf16[256,6,2,8,19]{0,2,4,3,1:T(2,128)(2,1)S(1)}, bf16[256,6,2,8,19]{0,2,4,3,1:T(2,128)(2,1)}, u32[]{:S(2)}) copy-start(bf16[256,6,2,8,19]{0,2,4,3,1:T(2,128)(2,1)} %fusion.15) | copy-start | bytes 2801668
  104.6 13.4 %collective-permute-start.2 = (bf16[256,1,4,128]{0,2,3,1:T(4,128)(2,1)S(1)}, bf16[256,1,4,128]{0,2,3,1:T(4,128)(2,1)S(1)}, u32[]{:S(2)}, u32[]{:S(2)}) collective-permute-start(bf16[256,1,4,128]{0,2,3,1:T(4,128)(2,1)S(1)} %get-tuple-element.18), channel_id=1, source_target_pairs={{0,8},{8,16},{16,24},{1,9},{9,17},{17,25},{2,10},{10,18},{18,26},{... | collective-permute-start | bytes 786440 | tf_op jit(solution)/shard_map/ppermute | solution.py:46
  109.1 8.9 %collective-permute-start.3 = (bf16[256,1,4,128]{0,2,3,1:T(4,128)(2,1)S(1)}, bf16[256,1,4,128]{0,2,3,1:T(4,128)(2,1)S(1)}, u32[]{:S(2)}, u32[]{:S(2)}) collective-permute-start(bf16[256,1,4,128]{0,2,3,1:T(4,128)(2,1)S(1)} %get-tuple-element.19), channel_id=1, source_target_pairs={{8,0},{16,8},{24,16},{9,1},{17,9},{25,17},{10,2},{18,10},{26,18},{... | collective-permute-start | bytes 786440 | tf_op jit(solution)/shard_map/ppermute | solution.py:47
  113.0 5.8 %copy-start.3 = (bf16[3,256,256]{2,1,0:T(8,128)(2,1)S(1)}, bf16[3,256,256]{2,1,0:T(8,128)(2,1)}, u32[]{:S(2)}) copy-start(bf16[3,256,256]{2,1,0:T(8,128)(2,1)} %param.6) | copy-start | bytes 1179652
  114.3 9.7 %all-to-all-start.2 = ((bf16[256,2,4,128]{3,2,1,0:T(4,128)(2,1)}), bf16[256,2,4,128]{3,2,1,0:T(4,128)(2,1)S(1)}, u32[]{:S(2)}, u32[]{:S(2)}) async-start(bf16[256,2,4,128]{3,2,1,0:T(4,128)(2,1)} %copy.101), calls=%async_computation.2 | async-start | bytes 1048576 | tf_op jit(solution)/shard_map/all_to_all | solution.py:133
  124.0 22.1 %all-to-all-start.1 = ((bf16[256,2,4,128]{3,2,1,0:T(4,128)(2,1)}), bf16[256,2,4,128]{3,2,1,0:T(4,128)(2,1)S(1)}, u32[]{:S(2)}, u32[]{:S(2)}) async-start(bf16[256,2,4,128]{3,2,1,0:T(4,128)(2,1)} %copy.88), calls=%async_computation.1 | async-start | bytes 1048576 | tf_op jit(solution)/shard_map/all_to_all | solution.py:108

commit v9 on v8

--- a/solution.py
+++ b/solution.py
@@ -119,13 +119,25 @@
     rows = grad_out.shape[2] // filts
     turn = lambda f, r: r if f % 2 == 0 else chans - 1 - r
     place = lambda g: turn(g // chans, g % chans) * filts + g // chans
-    group = filt * chans + jnp.where(filt % 2 == 0, chan, chans - 1 - chan)
-    pieces = []
-    for k in range(filts):
-        pairs = [(c * filts + f, place(c * filts + (f + k) % filts)) for f in range(filts) for c in range(chans)]
-        block = lax.dynamic_slice_in_dim(grad_out, ((filt + k) % filts) * rows, rows, 2)
-        pieces.append(lax.ppermute(block, ROWS, pairs))
-    all_filters = order_blocks(pieces, group % filts, 0)
+    group_of = lambda c, f: f * chans + turn(f, c)
+    need = [[[f for f in range(filts) if group_of(t, f) // filts == r] for r in range(chans)] for t in range(chans)]
+    per = max(len(need[t][r]) for t in range(chans) for r in range(chans))
+    pick = lambda t, r: [group_of(t, f) % filts for f in need[t][r]] + [0] * (per - len(need[t][r]))
+    received = []
+    for k in range(chans):
+        table = jnp.array([pick((r + k) % chans, r) for r in range(chans)], jnp.int32)[chan]
+        send = jnp.stack([lax.dynamic_slice_in_dim(grad_out, table[q] * rows, rows, 2) for q in range(per)])
+        received.append(send if k == 0 else lax.ppermute(send, "chan", shift_pairs(chans, k)))
+    received = jnp.concatenate(received)
+    slot = [[0] * filts for _ in range(chans)]
+    for t in range(chans):
+        for k in range(chans):
+            r = (t - k) % chans
+            for q, f in enumerate(need[t][r]):
+                slot[t][f] = k * per + q
+    blocks = jnp.take(received, jnp.array(slot, jnp.int32)[chan], axis=0)
+    all_filters = lax.all_to_all(blocks, "filt", 0, 0, tiled=True)
+    all_filters = all_filters.reshape((-1,) + all_filters.shape[2:])
     deep = halo(all_filters, "slab", 1)
     grad_mid = depth_conv(deep, depth_weight[::-1], "DHWIO").astype(jnp.bfloat16)
     rimmed = halo(grad_mid, ROWS, 2, place)

time: 148 us -> 128 us (0.86); the launches traced: 148 us -> 126 us
  waiting for transfers between devices: 55.2 us -> 31.2 us
  blocking collectives: 0 us -> 18 us
  starting transfers between devices: 53.9 us -> 37.4 us
  between operations: 1.14 us -> 3.73 us
  local copies, waits for them, and re-layouts: 21.5 us -> 19.6 us
    ppermute x4 -> x1, waiting for transfers between devices: 29 us -> 5.93 us  [backward(): lax.ppermute(send, 'chan', shift_pairs(chans, k))]
    all_to_all x0 -> x1, blocking collectives: none -> 18 us  [backward(): all_filters = lax.all_to_all(blocks, 'filt', 0, 0, tiled=True)]
    ppermute x1, starting transfers between devices: 9.97 us -> 1.3 us  [gather_blocks(): lax.ppermute(x, axis, shift_pairs(n, k))]
    ppermute x4 -> x1, starting transfers between devices: 9.89 us -> 2.13 us  [backward(): lax.ppermute(send, 'chan', shift_pairs(chans, k))]
    ppermute x3, starting transfers between devices: 5.12 us -> 10.8 us  [halo(): after = lax.ppermute(lax.slice_in_dim(x, 0, 1, axis=dim), axis, down)]
    ppermute x1, waiting for transfers between devices: 4.52 us -> 0.01 us  [gather_blocks(): lax.ppermute(x, axis, shift_pairs(n, k))]
    all_to_all x1, starting transfers between devices: 7.34 us -> 4.12 us  [forward(): got = lax.all_to_all(out, 'filt', 0, 2, tiled=True)]
    ppermute x3, waiting for transfers between devices: 2.36 us -> 5.2 us  [halo(): after = lax.ppermute(lax.slice_in_dim(x, 0, 1, axis=dim), axis, down)]
  transfers between devices with their start and end apart: 15 -> 12, of which waited for: 6 -> 5; matrix products, arithmetic and copies ran while one was open for 20% -> 18% of each run, Pallas kernels for 0% -> 0%
where the time goes in v9:
time: 128 us; the launch traced here: 126 us
  starting transfers between devices  37.4 us (29%)
  waiting for transfers between devices  31.2 us (24%)
  local copies, waits for them, and re-layouts  19.6 us (15%)
  blocking collectives  18 us (14%)
  other arithmetic  10.7 us (8%)
  matrix products  4.99 us (4%)
  between operations  3.73 us (3%)
    all_to_all x1, blocking collectives, backward(): all_filters = lax.all_to_all(blocks, 'filt', 0, 0, tiled=True)  18 us
    all_to_all x1, waiting for transfers between devices, forward(): got = lax.all_to_all(out, 'filt', 0, 2, tiled=True)  12.6 us
    ppermute x3, starting transfers between devices, halo(): after = lax.ppermute(lax.slice_in_dim(x, 0, 1, axis=dim), axis, down)  10.8 us
    ppermute x3, starting transfers between devices, halo(): lax.ppermute(lax.slice_in_dim(x, length - 1, length, axis=dim), axis, up)  10.2 us
    ppermute x1, waiting for transfers between devices, backward(): lax.ppermute(send, 'chan', shift_pairs(chans, k))  5.93 us
    ppermute x3, waiting for transfers between devices, halo(): after = lax.ppermute(lax.slice_in_dim(x, 0, 1, axis=dim), axis, down)  5.2 us
    all_to_all x1, waiting for transfers between devices, backward(): got = lax.all_to_all(grad_in, 'chan', 0, 2, tiled=True)  4.83 us
    unnamed x20, local copies, waits for them, and re-layouts  4.45 us
  transfers between devices with their start and end apart: 12, of which 5 were waited for; matrix products, arithmetic and copies ran while one was open for 18% of the time, Pallas kernels for 0%

profile of v9, /device:TPU:1, one launch (start us, length us, event | category | flops | bytes accessed | tf_op | source)
XLA Modules:
  0.0 125.6 jit_solution(2866569833968492222)
XLA Ops:
  5.0 1.5 %constant_dynamic-slice_fusion.4 = (bf16[64,2,4,128]{3,2,1,0:T(4,128)(2,1)S(1)}, bf16[64,2,4,128]{3,2,1,0:T(4,128)(2,1)S(1)}, bf16[64,2,4,128]{3,2,1,0:T(4,128)(2,1)S(1)}, bf16[64,2,4,128]{3,2,1,0:T(4,128)(2,1)S(1)}) fusion(bf16[64,2,16,128]{3,2,1,0:T(8,128)(2,1)} %param.10, s32[]{:T(128)S(6)} %select_n.122, s32[]{:T(128)S(6)} %select_n.123, ...), kind=kLoop, calls=%fused_computation.56 | loop fusion | bytes 1048592 | tf_op jit(solution)/shard_map/dynamic_slice | solution.py:129
  6.6 2.1 %collective-permute-start.4 = (bf16[2,64,2,4,128]{4,1,3,2,0:T(8,128)(2,1)S(1)}, bf16[2,64,2,4,128]{4,1,3,2,0:T(8,128)(2,1)S(1)}, u32[]{:S(2)}, u32[]{:S(2)}) collective-permute-start(bf16[2,64,2,4,128]{4,1,3,2,0:T(8,128)(2,1)S(1)} %pad_maximum_fusion.3), channel_id=1, source_target_pairs={{0,4},{4,0},{1,5},{5,1},{2,6},{6,2},{3,7},{7,3},{8,12},{12,8},{9,1... | collective-permute-start | bytes 786440 | tf_op jit(solution)/shard_map/ppermute | solution.py:130
  8.9 5.9 %collective-permute-done.4 = bf16[2,64,2,4,128]{4,1,3,2,0:T(8,128)(2,1)S(1)} collective-permute-done((bf16[2,64,2,4,128]{4,1,3,2,0:T(8,128)(2,1)S(1)}, bf16[2,64,2,4,128]{4,1,3,2,0:T(8,128)(2,1)S(1)}, u32[]{:S(2)}, u32[]{:S(2)}) %collective-permute-start.4) | collective-permute-done | bytes 262176 | tf_op jit(solution)/shard_map/ppermute | solution.py:130
  15.6 18.0 %all_to_all.40 = bf16[4,64,2,4,128]{4,1,3,2,0:T(8,128)(2,1)S(1)} all-to-all(bf16[4,64,2,4,128]{4,1,3,2,0:T(8,128)(2,1)S(1)} %broadcast_select_fusion), channel_id=1, replica_groups=mesh['slab'=4,'chan'=2,'filt'=4] {'filt'}, dimensions={0} | all-to-all | bytes 1048576 | tf_op jit(solution)/shard_map/all_to_all | solution.py:139
  34.6 4.1 %all-to-all-start = ((bf16[4,3,3,128,64]{3,4,2,1,0:T(8,128)(2,1)}), bf16[4,3,3,128,64]{3,4,2,1,0:T(8,128)(2,1)}, u32[]{:S(2)}, u32[]{:S(2)}) async-start(bf16[4,3,3,128,64]{3,4,2,1,0:T(8,128)(2,1)} %broadcast_in_dim.31), calls=%async_computation | async-start | bytes 1179648 | tf_op jit(solution)/shard_map/all_to_all | solution.py:78
  38.8 1.3 %pad_dynamic-slice_fusion = (bf16[128,2,6,128]{3,2,1,0:T(8,128)(2,1)S(1)}, bf16[128,2,6,128]{3,2,1,0:T(8,128)(2,1)}) fusion(s32[]{:T(128)S(6)} %select_n.113, bf16[128,2,32,128]{3,2,1,0:T(8,128)(2,1)S(1)} %copy-done, s32[]{:T(128)S(6)} %select_n.111), kind=kLoop, calls=%fused_computation.1 | loop fusion | bytes 2883592 | tf_op jit(solution)/shard_map/dynamic_slice | solution.py:100
  40.2 1.2 collective-permute-start
  41.5 4.1 %collective-permute-start.6 = (bf16[256,1,4,128]{3,0,2,1:T(8,128)(2,1)S(1)}, bf16[256,1,4,128]{3,0,2,1:T(8,128)(2,1)}, u32[]{:S(2)}, u32[]{:S(2)}) collective-permute-start(bf16[256,1,4,128]{3,0,2,1:T(8,128)(2,1)S(1)} %get-tuple-element.13), channel_id=1, source_target_pairs={{8,0},{16,8},{24,16},{9,1},{17,9},{25,17},{10,2},{18,10},{26,18},{... | collective-permute-start | bytes 786440 | tf_op jit(solution)/shard_map/ppermute | solution.py:47
  45.6 3.0 %collective-permute-start.5 = (bf16[256,1,4,128]{3,0,2,1:T(8,128)(2,1)S(1)}, bf16[256,1,4,128]{3,0,2,1:T(8,128)(2,1)}, u32[]{:S(2)}, u32[]{:S(2)}) collective-permute-start(bf16[256,1,4,128]{3,0,2,1:T(8,128)(2,1)S(1)} %get-tuple-element.12), channel_id=1, source_target_pairs={{0,8},{8,16},{16,24},{1,9},{9,17},{17,25},{2,10},{10,18},{18,26},{... | collective-permute-start | bytes 786440 | tf_op jit(solution)/shard_map/ppermute | solution.py:46
  49.4 2.6 %collective-permute-done = bf16[128,2,6,128]{3,2,1,0:T(8,128)(2,1)S(1)} collective-permute-done((bf16[128,2,6,128]{3,2,1,0:T(8,128)(2,1)}, bf16[128,2,6,128]{3,2,1,0:T(8,128)(2,1)S(1)}, u32[]{:S(2)}, u32[]{:S(2)}) %collective-permute-start) | collective-permute-done | bytes 393248 | tf_op jit(solution)/shard_map/ppermute | solution.py:103
  52.0 3.4 %fusion.11 = bf16[256,6,2,128]{3,1,2,0:T(8,128)(2,1)S(1)} fusion(s32[]{:T(128)S(6)} %select_n.115, bf16[128,2,6,128]{3,2,1,0:T(8,128)(2,1)S(1)} %collective-permute-done, bf16[128,2,6,128]{3,2,1,0:T(8,128)(2,1)S(1)} %get-tuple-element.8), kind=kLoop, calls=%fused_computation.27 | loop fusion | flops 1179648 | bytes 1572868 | tf_op jit(solution)/shard_map/jit(_roll_dynamic)/dynamic_slice | solution.py:19
  55.4 1.3 %copy.113 = bf16[256,6,2,128]{0,2,3,1:T(2,128)(2,1)S(1)} copy(bf16[256,6,2,128]{3,1,2,0:T(8,128)(2,1)S(1)} %fusion.11) | data formatting | bytes 1572864
  57.5 1.3 %collective-permute-start.1 = (bf16[1,4,3,3,128,64]{4,5,3,2,1,0:T(8,128)(2,1)}, bf16[1,4,3,3,128,64]{4,5,3,2,1,0:T(8,128)(2,1)}, u32[]{:S(2)}, u32[]{:S(2)}) collective-permute-start(bf16[1,4,3,3,128,64]{4,5,3,2,1,0:T(8,128)(2,1)} %bitcast.3), channel_id=1, source_target_pairs={{0,4},{4,0},{1,5},{5,1},{2,6},{6,2},{3,7},{7,3},{8,12},{12,8},{9,1... | collective-permute-start | bytes 1769480 | tf_op jit(solution)/shard_map/ppermute | solution.py:25
  58.8 1.2 pad_maximum_fusion.1
  61.2 1.3 %collective-permute-start.8 = (bf16[256,2,1,128]{0,3,2,1:T(8,128)(2,1)S(1)}, bf16[256,2,1,128]{0,3,2,1:T(8,128)(2,1)S(1)}, u32[]{:S(2)}, u32[]{:S(2)}) collective-permute-start(bf16[256,2,1,128]{0,3,2,1:T(8,128)(2,1)S(1)} %get-tuple-element.11), channel_id=1, source_target_pairs={{4,0},{5,4},{1,5},{2,1},{6,2},{7,6},{3,7},{12,8},{13,12},{9,13},{1... | collective-permute-start | bytes 393224 | tf_op jit(solution)/shard_map/ppermute | solution.py:47
  62.5 4.2 %collective-permute-start.7 = (bf16[256,2,1,128]{0,3,2,1:T(8,128)(2,1)S(1)}, bf16[256,2,1,128]{0,3,2,1:T(8,128)(2,1)S(1)}, u32[]{:S(2)}, u32[]{:S(2)}) collective-permute-start(bf16[256,2,1,128]{0,3,2,1:T(8,128)(2,1)S(1)} %get-tuple-element.10), channel_id=1, source_target_pairs={{0,4},{4,5},{5,1},{1,2},{2,6},{6,7},{7,3},{8,12},{12,13},{13,9},{9... | collective-permute-start | bytes 393224 | tf_op jit(solution)/shard_map/ppermute | solution.py:46
  67.6 5.2 %collective-permute-done.8 = bf16[256,2,1,128]{0,3,2,1:T(8,128)(2,1)S(1)} collective-permute-done((bf16[256,2,1,128]{0,3,2,1:T(8,128)(2,1)S(1)}, bf16[256,2,1,128]{0,3,2,1:T(8,128)(2,1)S(1)}, u32[]{:S(2)}, u32[]{:S(2)}) %collective-permute-start.8) | collective-permute-done | bytes 131104 | tf_op jit(solution)/shard_map/ppermute | solution.py:47
  74.4 1.7 %fusion.15 = bf16[256,6,2,8,19]{0,2,4,3,1:T(2,128)(2,1)} fusion(bf16[256,6,2,7,2]{0,2,4,3,1:T(2,128)(2,1)S(1)} %slice.60, bf16[256,6,2,8,17]{0,2,4,3,1:T(2,128)(2,1)S(1)} %bitcast.83), kind=kLoop, calls=%fused_computation.33 | loop fusion | flops 2801664 | bytes 1855488 | tf_op jit(solution)/shard_map/conv_general_dilated | solution.py:52
  76.1 2.2 %fusion.7 = bf16[3,3,2,128,4,64]{3,5,1,0,4,2:T(8,128)(2,1)S(1)} fusion(s32[]{:T(128)S(6)} %select_n.116, bf16[1,4,3,3,128,64]{4,5,3,2,1,0:T(8,128)(2,1)} %collective-permute-done.1, bf16[1,4,3,3,128,64]{4,5,3,2,1,0:T(8,128)(2,1)} %bitcast.3), kind=kLoop, calls=%fused_computation.23 | loop fusion | flops 1769472 | bytes 2359300 | tf_op jit(solution)/shard_map/transpose | solution.py:81
  78.3 1.2 copy.85
  80.3 1.5 %fusion.2 = bf16[4,16,17,256]{3,1,2,0:T(8,128)(2,1)S(1)} fusion(bf16[3,3,256,256]{2,3,1,0:T(8,128)(2,1)S(1)} %reshape.73, bf16[256,6,2,8,19]{0,2,4,3,1:T(2,128)(2,1)S(1)} %fusion.14, pred[16,17]{0,1:T(8,128)(4,1)S(1)} %copy-done.7), kind=kOutput, calls=%fused_computation.16 | convolution fusion | flops 1284014080 | bytes 2670864 | tf_op jit(solution)/shard_map/conv_general_dilated | solution.py:52
  82.5 5.4 %collective-permute-start.3 = (bf16[256,1,4,128]{0,2,3,1:T(4,128)(2,1)S(1)}, bf16[256,1,4,128]{0,2,3,1:T(4,128)(2,1)S(1)}, u32[]{:S(2)}, u32[]{:S(2)}) collective-permute-start(bf16[256,1,4,128]{0,2,3,1:T(4,128)(2,1)S(1)} %get-tuple-element.19), channel_id=1, source_target_pairs={{8,0},{16,8},{24,16},{9,1},{17,9},{25,17},{10,2},{18,10},{26,18},{... | collective-permute-start | bytes 786440 | tf_op jit(solution)/shard_map/ppermute | solution.py:47
  88.0 3.0 %collective-permute-start.2 = (bf16[256,1,4,128]{0,2,3,1:T(4,128)(2,1)S(1)}, bf16[256,1,4,128]{0,2,3,1:T(4,128)(2,1)S(1)}, u32[]{:S(2)}, u32[]{:S(2)}) collective-permute-start(bf16[256,1,4,128]{0,2,3,1:T(4,128)(2,1)S(1)} %get-tuple-element.18), channel_id=1, source_target_pairs={{0,8},{8,16},{16,24},{1,9},{9,17},{17,25},{2,10},{10,18},{18,26},{... | collective-permute-start | bytes 786440 | tf_op jit(solution)/shard_map/ppermute | solution.py:46
  91.0 1.5 %fusion.3 = bf16[4,16,17,256]{3,1,2,0:T(8,128)(2,1)S(1)} fusion(bf16[3,3,256,256]{2,3,1,0:T(8,128)(2,1)S(1)} %reshape.73, bf16[256,6,2,8,19]{0,2,4,3,1:T(2,128)(2,1)S(1)} %copy-done.1, pred[16,17]{0,1:T(8,128)(4,1)S(1)} %copy-done.7), kind=kOutput, calls=%fused_computation.17 | convolution fusion | flops 1284014080 | bytes 2670864 | tf_op jit(solution)/shard_map/conv_general_dilated | solution.py:52
  93.0 1.3 %copy.106 = bf16[256,2,4,128]{3,2,1,0:T(4,128)(2,1)} copy(bf16[256,2,4,128]{0,2,3,1:T(4,128)(2,1)S(1)} %slice_bitcast_fusion) | data formatting | bytes 1048576 | tf_op jit(solution)/shard_map/convert_element_type | solution.py:144
  94.3 3.5 %all-to-all-start.3 = ((bf16[256,2,4,128]{3,2,1,0:T(4,128)(2,1)}), bf16[256,2,4,128]{3,2,1,0:T(4,128)(2,1)S(1)}, u32[]{:S(2)}, u32[]{:S(2)}) async-start(bf16[256,2,4,128]{3,2,1,0:T(4,128)(2,1)} %copy.106), calls=%async_computation.3 | async-start | bytes 1048576 | tf_op jit(solution)/shard_map/all_to_all | solution.py:145
  98.6 1.4 %convolution_convert_fusion.1 = bf16[2,4,8,16,256]{4,2,3,1,0:T(8,128)(2,1)S(1)} fusion(bf16[256,4,4,8,16]{0,2,4,3,1:T(4,128)(2,1)S(1)} %bitcast.93, bf16[3,256,256]{2,1,0:T(8,128)(2,1)S(1)} %copy-done.3), kind=kOutput, calls=%fused_computation.19 | convolution fusion | flops 402915328 | bytes 1966080 | tf_op jit(solution)/shard_map/conv_general_dilated | solution.py:63
  101.2 4.8 %all-to-all-done.3 = bf16[256,2,4,128]{3,2,1,0:T(4,128)(2,1)S(1)} async-done(((bf16[256,2,4,128]{3,2,1,0:T(4,128)(2,1)}), bf16[256,2,4,128]{3,2,1,0:T(4,128)(2,1)S(1)}, u32[]{:S(2)}, u32[]{:S(2)}) %all-to-all-start.3) | async-done | bytes 524320 | tf_op jit(solution)/shard_map/all_to_all | solution.py:145
  106.0 4.1 %all-to-all-start.1 = ((bf16[256,2,4,128]{3,2,1,0:T(4,128)(2,1)}), bf16[256,2,4,128]{3,2,1,0:T(4,128)(2,1)S(1)}, u32[]{:S(2)}, u32[]{:S(2)}) async-start(bf16[256,2,4,128]{3,2,1,0:T(4,128)(2,1)} %copy.91), calls=%async_computation.1 | async-start | bytes 1048576 | tf_op jit(solution)/shard_map/all_to_all | solution.py:108
  110.4 1.1 copy.110
  111.6 12.6 %all-to-all-done.1 = bf16[256,2,4,128]{3,2,1,0:T(4,128)(2,1)S(1)} async-done(((bf16[256,2,4,128]{3,2,1,0:T(4,128)(2,1)}), bf16[256,2,4,128]{3,2,1,0:T(4,128)(2,1)S(1)}, u32[]{:S(2)}, u32[]{:S(2)}) %all-to-all-start.1) | async-done | bytes 524320 | tf_op jit(solution)/shard_map/all_to_all | solution.py:108
  124.5 1.1 copy.109
  (67 shorter events, 13.5 us)
Async XLA Ops:
  0.6 8.1 %copy-start.6 = (s32[2,4]{1,0:T(2,128)S(1)}, s32[2,4]{1,0:T(2,128)}, u32[]{:S(2)}) copy-start(s32[2,4]{1,0:T(2,128)} %constant.109.clone) | copy-start | bytes 100
  6.6 8.2 %collective-permute-start.4 = (bf16[2,64,2,4,128]{4,1,3,2,0:T(8,128)(2,1)S(1)}, bf16[2,64,2,4,128]{4,1,3,2,0:T(8,128)(2,1)S(1)}, u32[]{:S(2)}, u32[]{:S(2)}) collective-permute-start(bf16[2,64,2,4,128]{4,1,3,2,0:T(8,128)(2,1)S(1)} %pad_maximum_fusion.3), channel_id=1, source_target_pairs={{0,4},{4,0},{1,5},{5,1},{2,6},{6,2},{3,7},{7,3},{8,12},{12,8},{9,1... | collective-permute-start | bytes 786440 | tf_op jit(solution)/shard_map/ppermute | solution.py:130
  14.8 18.8 %copy-start.5 = (bf16[3,3,128,64]{2,3,1,0:T(8,128)(2,1)S(1)}, bf16[3,3,128,64]{2,3,1,0:T(8,128)(2,1)}, u32[]{:S(2)}) copy-start(bf16[3,3,128,64]{2,3,1,0:T(8,128)(2,1)} %param.8) | copy-start | bytes 442372
  15.5 23.3 %copy-start = (bf16[128,2,32,128]{3,2,1,0:T(8,128)(2,1)S(1)}, bf16[128,2,32,128]{3,2,1,0:T(8,128)(2,1)}, u32[]{:S(2)}) copy-start(bf16[128,2,32,128]{3,2,1,0:T(8,128)(2,1)} %param.7) | copy-start | bytes 6291460
  34.6 22.9 %all-to-all-start = ((bf16[4,3,3,128,64]{3,4,2,1,0:T(8,128)(2,1)}), bf16[4,3,3,128,64]{3,4,2,1,0:T(8,128)(2,1)}, u32[]{:S(2)}, u32[]{:S(2)}) async-start(bf16[4,3,3,128,64]{3,4,2,1,0:T(8,128)(2,1)} %broadcast_in_dim.31), calls=%async_computation | async-start | bytes 1179648 | tf_op jit(solution)/shard_map/all_to_all | solution.py:78
  38.8 9.8 %copy-start.2 = (bf16[3,256,256]{2,1,0:T(8,128)(2,1)S(1)}, bf16[3,256,256]{2,1,0:T(8,128)(2,1)}, u32[]{:S(2)}) copy-start(bf16[3,256,256]{2,1,0:T(8,128)(2,1)} %param.9) | copy-start | bytes 1179652
  40.2 11.8 %collective-permute-start = (bf16[128,2,6,128]{3,2,1,0:T(8,128)(2,1)}, bf16[128,2,6,128]{3,2,1,0:T(8,128)(2,1)S(1)}, u32[]{:S(2)}, u32[]{:S(2)}) collective-permute-start(bf16[128,2,6,128]{3,2,1,0:T(8,128)(2,1)} %get-tuple-element.9), channel_id=1, source_target_pairs={{0,4},{4,0},{1,5},{5,1},{2,6},{6,2},{3,7},{7,3},{8,12},{12,8},{9,1... | collective-permute-start | bytes 1179656 | tf_op jit(solution)/shard_map/ppermute | solution.py:103
  41.5 17.3 %collective-permute-start.6 = (bf16[256,1,4,128]{3,0,2,1:T(8,128)(2,1)S(1)}, bf16[256,1,4,128]{3,0,2,1:T(8,128)(2,1)}, u32[]{:S(2)}, u32[]{:S(2)}) collective-permute-start(bf16[256,1,4,128]{3,0,2,1:T(8,128)(2,1)S(1)} %get-tuple-element.13), channel_id=1, source_target_pairs={{8,0},{16,8},{24,16},{9,1},{17,9},{25,17},{10,2},{18,10},{26,18},{... | collective-permute-start | bytes 786440 | tf_op jit(solution)/shard_map/ppermute | solution.py:47
  45.6 13.2 %collective-permute-start.5 = (bf16[256,1,4,128]{3,0,2,1:T(8,128)(2,1)S(1)}, bf16[256,1,4,128]{3,0,2,1:T(8,128)(2,1)}, u32[]{:S(2)}, u32[]{:S(2)}) collective-permute-start(bf16[256,1,4,128]{3,0,2,1:T(8,128)(2,1)S(1)} %get-tuple-element.12), channel_id=1, source_target_pairs={{0,8},{8,16},{16,24},{1,9},{9,17},{17,25},{2,10},{10,18},{18,26},{... | collective-permute-start | bytes 786440 | tf_op jit(solution)/shard_map/ppermute | solution.py:46
  57.5 3.0 %copy-start.4 = (bf16[3,256,256]{2,1,0:T(8,128)(2,1)S(1)}, bf16[3,256,256]{2,1,0:T(8,128)(2,1)}, u32[]{:S(2)}) copy-start(bf16[3,256,256]{2,1,0:T(8,128)(2,1)} %rev.11) | copy-start | bytes 1179652
  57.5 18.6 %collective-permute-start.1 = (bf16[1,4,3,3,128,64]{4,5,3,2,1,0:T(8,128)(2,1)}, bf16[1,4,3,3,128,64]{4,5,3,2,1,0:T(8,128)(2,1)}, u32[]{:S(2)}, u32[]{:S(2)}) collective-permute-start(bf16[1,4,3,3,128,64]{4,5,3,2,1,0:T(8,128)(2,1)} %bitcast.3), channel_id=1, source_target_pairs={{0,4},{4,0},{1,5},{5,1},{2,6},{6,2},{3,7},{7,3},{8,12},{12,8},{9,1... | collective-permute-start | bytes 1769480 | tf_op jit(solution)/shard_map/ppermute | solution.py:25
  61.2 11.5 %collective-permute-start.8 = (bf16[256,2,1,128]{0,3,2,1:T(8,128)(2,1)S(1)}, bf16[256,2,1,128]{0,3,2,1:T(8,128)(2,1)S(1)}, u32[]{:S(2)}, u32[]{:S(2)}) collective-permute-start(bf16[256,2,1,128]{0,3,2,1:T(8,128)(2,1)S(1)} %get-tuple-element.11), channel_id=1, source_target_pairs={{4,0},{5,4},{1,5},{2,1},{6,2},{7,6},{3,7},{12,8},{13,12},{9,13},{1... | collective-permute-start | bytes 393224 | tf_op jit(solution)/shard_map/ppermute | solution.py:47
  62.5 10.3 %collective-permute-start.7 = (bf16[256,2,1,128]{0,3,2,1:T(8,128)(2,1)S(1)}, bf16[256,2,1,128]{0,3,2,1:T(8,128)(2,1)S(1)}, u32[]{:S(2)}, u32[]{:S(2)}) collective-permute-start(bf16[256,2,1,128]{0,3,2,1:T(8,128)(2,1)S(1)} %get-tuple-element.10), channel_id=1, source_target_pairs={{0,4},{4,5},{5,1},{1,2},{2,6},{6,7},{7,3},{8,12},{12,13},{13,9},{9... | collective-permute-start | bytes 393224 | tf_op jit(solution)/shard_map/ppermute | solution.py:46
  78.3 2.0 %copy-start.7 = (pred[16,17]{0,1:T(8,128)(4,1)S(1)}, pred[16,17]{0,1:T(8,128)(4,1)}, u32[]{:S(2)}) copy-start(pred[16,17]{0,1:T(8,128)(4,1)} %constant.129) | copy-start | bytes 820
  81.8 9.2 %copy-start.1 = (bf16[256,6,2,8,19]{0,2,4,3,1:T(2,128)(2,1)S(1)}, bf16[256,6,2,8,19]{0,2,4,3,1:T(2,128)(2,1)}, u32[]{:S(2)}) copy-start(bf16[256,6,2,8,19]{0,2,4,3,1:T(2,128)(2,1)} %fusion.15) | copy-start | bytes 2801668
  82.5 15.2 %collective-permute-start.3 = (bf16[256,1,4,128]{0,2,3,1:T(4,128)(2,1)S(1)}, bf16[256,1,4,128]{0,2,3,1:T(4,128)(2,1)S(1)}, u32[]{:S(2)}, u32[]{:S(2)}) collective-permute-start(bf16[256,1,4,128]{0,2,3,1:T(4,128)(2,1)S(1)} %get-tuple-element.19), channel_id=1, source_target_pairs={{8,0},{16,8},{24,16},{9,1},{17,9},{25,17},{10,2},{18,10},{26,18},{... | collective-permute-start | bytes 786440 | tf_op jit(solution)/shard_map/ppermute | solution.py:47
  88.0 9.8 %collective-permute-start.2 = (bf16[256,1,4,128]{0,2,3,1:T(4,128)(2,1)S(1)}, bf16[256,1,4,128]{0,2,3,1:T(4,128)(2,1)S(1)}, u32[]{:S(2)}, u32[]{:S(2)}) collective-permute-start(bf16[256,1,4,128]{0,2,3,1:T(4,128)(2,1)S(1)} %get-tuple-element.18), channel_id=1, source_target_pairs={{0,8},{8,16},{16,24},{1,9},{9,17},{17,25},{2,10},{10,18},{18,26},{... | collective-permute-start | bytes 786440 | tf_op jit(solution)/shard_map/ppermute | solution.py:46
  93.0 5.6 %copy-start.3 = (bf16[3,256,256]{2,1,0:T(8,128)(2,1)S(1)}, bf16[3,256,256]{2,1,0:T(8,128)(2,1)}, u32[]{:S(2)}) copy-start(bf16[3,256,256]{2,1,0:T(8,128)(2,1)} %param.9) | copy-start | bytes 1179652
  94.3 11.8 %all-to-all-start.3 = ((bf16[256,2,4,128]{3,2,1,0:T(4,128)(2,1)}), bf16[256,2,4,128]{3,2,1,0:T(4,128)(2,1)S(1)}, u32[]{:S(2)}, u32[]{:S(2)}) async-start(bf16[256,2,4,128]{3,2,1,0:T(4,128)(2,1)} %copy.106), calls=%async_computation.3 | async-start | bytes 1048576 | tf_op jit(solution)/shard_map/all_to_all | solution.py:145
  106.0 18.2 %all-to-all-start.1 = ((bf16[256,2,4,128]{3,2,1,0:T(4,128)(2,1)}), bf16[256,2,4,128]{3,2,1,0:T(4,128)(2,1)S(1)}, u32[]{:S(2)}, u32[]{:S(2)}) async-start(bf16[256,2,4,128]{3,2,1,0:T(4,128)(2,1)} %copy.91), calls=%async_computation.1 | async-start | bytes 1048576 | tf_op jit(solution)/shard_map/all_to_all | solution.py:108

commit v10 on v9

--- a/solution.py
+++ b/solution.py
@@ -71,14 +71,38 @@
     return out[0]
 
 
+def relay_gather(x, axis):
+    n = lax.axis_size(axis)
+    me = lax.axis_index(axis)
+    right = [(i, i + 1) for i in range(n - 1)]
+    left = [(i + 1, i) for i in range(n - 1)]
+    from_left, from_right = [x], [x]
+    for _ in range(n - 1):
+        from_left.append(lax.ppermute(from_left[-1], axis, right))
+        from_right.append(lax.ppermute(from_right[-1], axis, left))
+    blocks = []
+    for position in range(n):
+        block = jnp.zeros_like(x)
+        for k in range(n):
+            block = jnp.where(me - position == k, from_left[k], block)
+            block = jnp.where(position - me == k, from_right[k], block)
+        blocks.append(block)
+    return jnp.stack(blocks)
+
+
 def gather_weight(weight):
     filts = lax.axis_size("filt")
     chans = lax.axis_size("chan")
-    spread = jnp.broadcast_to(weight[None], (filts,) + weight.shape)
-    by_filt = lax.all_to_all(spread, "filt", 0, 0, tiled=True)
+    slabs = lax.axis_size("slab")
+    core = lax.axis_index("slab") % 2
+    c_loc, m_loc = weight.shape[2:]
+    half = c_loc // 2
+    mine = lax.dynamic_slice_in_dim(weight, core * half, half, 2)
+    by_filt = relay_gather(mine, "filt")
     both = gather_blocks(by_filt[None], "chan", 0)
-    c_loc, m_loc = weight.shape[2:]
-    whole = jnp.transpose(both, (2, 3, 0, 4, 1, 5))
+    other = lax.ppermute(both, "slab", [(i, i ^ 1) for i in range(slabs)])
+    halves = jnp.roll(jnp.stack([both, other]), core, axis=0)
+    whole = jnp.transpose(halves, (3, 4, 1, 0, 5, 2, 6))
     return whole.reshape(3, 3, chans * c_loc, filts * m_loc)
 
 

time: 128 us -> 138 us (1.078)
  blocking collectives: 18 us -> 0 us
  starting transfers between devices: 37.4 us -> 54.6 us
  other arithmetic: 10.7 us -> 20 us
  waiting for transfers between devices: 31.2 us -> 22.7 us
  local copies, waits for them, and re-layouts: 19.6 us -> 27.8 us
    ppermute x0 -> x7, starting transfers between devices: none -> 21.4 us  [the longest x3 12.9 us: relay_gather(): from_left.append(lax.ppermute(from_left[-1], axis, right))]
    all_to_all x1 -> x0, blocking collectives: 18 us -> none  [backward(): all_filters = lax.all_to_all(blocks, 'filt', 0, 0, tiled=True)]
    ppermute x1, waiting for transfers between devices: 5.93 us -> 0.01 us  [backward(): lax.ppermute(send, 'chan', shift_pairs(chans, k))]
    ppermute x3, starting transfers between devices: 10.8 us -> 5.15 us  [halo(): after = lax.ppermute(lax.slice_in_dim(x, 0, 1, axis=dim), axis, down)]
    ppermute x3, waiting for transfers between devices: 5.2 us -> 0.12 us  [halo(): after = lax.ppermute(lax.slice_in_dim(x, 0, 1, axis=dim), axis, down)]
    another operation x0 -> x5, other arithmetic: none -> 3.36 us  [the longest x1 2.29 us: gather_weight(): halves = jnp.roll(jnp.stack([both, other]), core, axis=0)]
    reshape x1, local copies, waits for them, and re-layouts: 0.79 us -> 3.82 us  [gather_weight(): return whole.reshape(3, 3, chans * c_loc, filts * m_loc)]
    ppermute x0 -> x7, waiting for transfers between devices: none -> 2.92 us  [the longest x3 1.81 us: relay_gather(): from_right.append(lax.ppermute(from_right[-1], axis, left))]
  transfers between devices with their start and end apart: 12 -> 19, of which waited for: 5 -> 7; matrix products, arithmetic and copies ran while one was open for 18% -> 34% of each run, Pallas kernels for 0% -> 0%
where the time goes in v10:
time: 138 us; the launch traced here: 135 us
  starting transfers between devices  54.6 us (40%)
  local copies, waits for them, and re-layouts  27.8 us (20%)
  waiting for transfers between devices  22.7 us (16%)
  other arithmetic  20 us (14%)
  matrix products  6.18 us (4%)
  between operations  3.98 us (3%)
    ppermute x3, starting transfers between devices, relay_gather(): from_left.append(lax.ppermute(from_left[-1], axis, right))  12.9 us
    all_to_all x1, waiting for transfers between devices, forward(): got = lax.all_to_all(out, 'filt', 0, 2, tiled=True)  12.6 us
    ppermute x3, starting transfers between devices, halo(): lax.ppermute(lax.slice_in_dim(x, length - 1, length, axis=dim), axis, up)  11.6 us
    all_to_all x1, waiting for transfers between devices, backward(): got = lax.all_to_all(grad_in, 'chan', 0, 2, tiled=True)  5.92 us
    all_to_all x1, starting transfers between devices, backward(): all_filters = lax.all_to_all(blocks, 'filt', 0, 0, tiled=True)  5.46 us
    ppermute x3, starting transfers between devices, halo(): after = lax.ppermute(lax.slice_in_dim(x, 0, 1, axis=dim), axis, down)  5.15 us
    ppermute x1, starting transfers between devices, gather_weight(): other = lax.ppermute(both, 'slab', [(i, i ^ 1) for i in range(slabs)])  4.6 us
    unnamed x30, local copies, waits for them, and re-layouts  4.47 us
  transfers between devices with their start and end apart: 19, of which 7 were waited for; matrix products, arithmetic and copies ran while one was open for 34% of the time, Pallas kernels for 0%

profile of v10, /device:TPU:1, one launch (start us, length us, event | category | flops | bytes accessed | tf_op | source)
XLA Modules:
  0.0 135.2 jit_solution(10357899052255114050)
XLA Ops:
  1.8 1.3 collective-permute-start.1
  3.1 4.7 %collective-permute-start.4 = (bf16[3,3,64,64]{2,3,1,0:T(8,128)(2,1)S(1)}, bf16[3,3,64,64]{2,3,1,0:T(8,128)(2,1)S(1)}, u32[]{:S(2)}, u32[]{:S(2)}) collective-permute-start(bf16[3,3,64,64]{2,3,1,0:T(8,128)(2,1)S(1)} %constant_dynamic-slice_fusion.7), channel_id=1, source_target_pairs={{0,1},{1,2},{2,3},{4,5},{5,6},{6,7},{8,9},{9,10},{10,11},{12,13},{... | collective-permute-start | bytes 221192 | tf_op jit(solution)/shard_map/ppermute | solution.py:81
  7.8 2.7 %pad_dynamic-slice_fusion.4 = (bf16[128,2,6,128]{3,2,1,0:T(8,128)(2,1)S(1)}, bf16[128,2,6,128]{3,2,1,0:T(8,128)(2,1)}) fusion(s32[]{:T(128)S(6)} %select_n.324, bf16[128,2,32,128]{3,2,1,0:T(8,128)(2,1)} %param.7, s32[]{:T(128)S(6)} %select_n.322), kind=kLoop, calls=%fused_computation.5 | loop fusion | bytes 2883592 | tf_op jit(solution)/shard_map/dynamic_slice | solution.py:124
  10.5 1.4 %collective-permute-start = (bf16[128,2,6,128]{3,2,1,0:T(8,128)(2,1)}, bf16[128,2,6,128]{3,2,1,0:T(8,128)(2,1)S(1)}, u32[]{:S(2)}, u32[]{:S(2)}) collective-permute-start(bf16[128,2,6,128]{3,2,1,0:T(8,128)(2,1)} %get-tuple-element.9), channel_id=1, source_target_pairs={{0,4},{4,0},{1,5},{5,1},{2,6},{6,2},{3,7},{7,3},{8,12},{12,8},{9,1... | collective-permute-start | bytes 1179656 | tf_op jit(solution)/shard_map/ppermute | solution.py:127
  16.4 1.3 collective-permute-start.2
  17.7 4.3 %collective-permute-start.5 = (bf16[3,3,64,64]{2,3,1,0:T(8,128)(2,1)S(1)}, bf16[3,3,64,64]{2,3,1,0:T(8,128)(2,1)S(1)}, u32[]{:S(2)}, u32[]{:S(2)}) collective-permute-start(bf16[3,3,64,64]{2,3,1,0:T(8,128)(2,1)S(1)} %collective-permute-done.4), channel_id=1, source_target_pairs={{0,1},{1,2},{2,3},{4,5},{5,6},{6,7},{8,9},{9,10},{10,11},{12,13},{... | collective-permute-start | bytes 221192 | tf_op jit(solution)/shard_map/ppermute | solution.py:81
  24.2 4.0 %collective-permute-start.6 = (bf16[3,3,64,64]{2,3,1,0:T(8,128)(2,1)S(1)}, bf16[3,3,64,64]{2,3,1,0:T(8,128)(2,1)S(1)}, u32[]{:S(2)}, u32[]{:S(2)}) collective-permute-start(bf16[3,3,64,64]{2,3,1,0:T(8,128)(2,1)S(1)} %collective-permute-done.5), channel_id=1, source_target_pairs={{0,1},{1,2},{2,3},{4,5},{5,6},{6,7},{8,9},{9,10},{10,11},{12,13},{... | collective-permute-start | bytes 221192 | tf_op jit(solution)/shard_map/ppermute | solution.py:81
  31.5 1.3 collective-permute-start.7
  35.4 5.5 %all-to-all-start.1 = ((bf16[4,64,2,4,128]{4,1,3,2,0:T(8,128)(2,1)}), bf16[4,64,2,4,128]{4,1,3,2,0:T(8,128)(2,1)}, u32[]{:S(2)}, u32[]{:S(2)}) async-start(bf16[4,64,2,4,128]{4,1,3,2,0:T(8,128)(2,1)} %broadcast_select_fusion), calls=%async_computation.1 | async-start | bytes 1048576 | tf_op jit(solution)/shard_map/all_to_all | solution.py:163
  41.7 3.4 %fusion.14 = bf16[256,6,2,128]{3,1,2,0:T(8,128)(2,1)S(1)} fusion(s32[]{:T(128)S(6)} %select_n.326, bf16[128,2,6,128]{3,2,1,0:T(8,128)(2,1)S(1)} %collective-permute-done, bf16[128,2,6,128]{3,2,1,0:T(8,128)(2,1)S(1)} %get-tuple-element.8), kind=kLoop, calls=%fused_computation.34 | loop fusion | flops 1179648 | bytes 1572868 | tf_op jit(solution)/shard_map/jit(_roll_dynamic)/dynamic_slice | solution.py:19
  45.1 1.3 copy.114
  48.4 4.6 %collective-permute-start.8 = (bf16[2,4,3,3,64,64]{4,5,3,2,1,0:T(8,128)(2,1)S(1)}, bf16[2,4,3,3,64,64]{4,5,3,2,1,0:T(8,128)(2,1)}, u32[]{:S(2)}, u32[]{:S(2)}) collective-permute-start(bf16[2,4,3,3,64,64]{4,5,3,2,1,0:T(8,128)(2,1)S(1)} %fusion.10), channel_id=1, source_target_pairs={{0,8},{8,0},{16,24},{24,16},{1,9},{9,1},{17,25},{25,17},{2,10},{10... | collective-permute-start | bytes 1769480 | tf_op jit(solution)/shard_map/ppermute | solution.py:103
  53.0 1.6 %fusion.17 = bf16[256,6,2,8,19]{0,2,4,3,1:T(2,128)(2,1)} fusion(bf16[256,6,2,7,2]{0,2,4,3,1:T(2,128)(2,1)S(1)} %slice.52, bf16[256,6,2,8,17]{0,2,4,3,1:T(2,128)(2,1)S(1)} %bitcast.91), kind=kLoop, calls=%fused_computation.39 | loop fusion | flops 2801664 | bytes 1855488 | tf_op jit(solution)/shard_map/conv_general_dilated | solution.py:52
  54.6 2.3 %fusion.61 = bf16[1,2,4,3,3,64,64]{5,6,4,3,2,1,0:T(8,128)(2,1)S(1)} fusion(s32[]{:T(128)S(6)} %select_n.393, bf16[1,4,3,3,64,64]{4,5,3,2,1,0:T(8,128)(2,1)S(1)} %maximum_bitcast_fusion.1, bf16[1,4,3,3,64,64]{4,5,3,2,1,0:T(8,128)(2,1)} %copy-done.3), kind=kLoop, calls=%fused_computation.110 | loop fusion | flops 884736 | bytes 1179652 | tf_op jit(solution)/shard_map/stack | solution.py:104
  58.9 1.9 %collective-permute-start.13 = (bf16[256,1,4,128]{3,0,2,1:T(8,128)(2,1)}, bf16[256,1,4,128]{3,0,2,1:T(8,128)(2,1)}, u32[]{:S(2)}, u32[]{:S(2)}) collective-permute-start(bf16[256,1,4,128]{3,0,2,1:T(8,128)(2,1)} %get-tuple-element.13), channel_id=1, source_target_pairs={{8,0},{16,8},{24,16},{9,1},{17,9},{25,17},{10,2},{18,10},{26,18},{... | collective-permute-start | bytes 786440 | tf_op jit(solution)/shard_map/ppermute | solution.py:47
  60.9 3.8 %collective-permute-start.12 = (bf16[256,1,4,128]{3,0,2,1:T(8,128)(2,1)}, bf16[256,1,4,128]{3,0,2,1:T(8,128)(2,1)}, u32[]{:S(2)}, u32[]{:S(2)}) collective-permute-start(bf16[256,1,4,128]{3,0,2,1:T(8,128)(2,1)} %get-tuple-element.12), channel_id=1, source_target_pairs={{0,8},{8,16},{16,24},{1,9},{9,17},{17,25},{2,10},{10,18},{18,26},{... | collective-permute-start | bytes 786440 | tf_op jit(solution)/shard_map/ppermute | solution.py:46
  64.7 4.0 %fusion.3 = bf16[3,3,2,2,64,4,64]{4,6,1,0,5,2,3:T(8,128)(2,1)S(1)} fusion(s32[]{:T(128)S(6)} %select_n.395, bf16[1,2,4,3,3,64,64]{5,6,4,3,2,1,0:T(8,128)(2,1)S(1)} %fusion.61, bf16[1,2,4,3,3,64,64]{5,6,4,3,2,1,0:T(8,128)(2,1)} %bitcast.9), kind=kLoop, calls=%fused_computation.10 | loop fusion | flops 1769472 | bytes 2359300 | tf_op jit(solution)/shard_map/transpose | solution.py:105
  68.7 3.3 %copy.86 = bf16[3,3,2,2,64,4,64]{6,5,4,3,2,1,0:T(4,128)(2,1)} copy(bf16[3,3,2,2,64,4,64]{4,6,1,0,5,2,3:T(8,128)(2,1)S(1)} %fusion.3) | data formatting | bytes 2359296 | tf_op jit(solution)/shard_map/transpose | solution.py:105
  72.0 3.8 %reshape.72 = bf16[3,3,256,256]{3,2,1,0:T(8,128)(2,1)S(1)} reshape(bf16[3,3,2,2,64,4,64]{6,5,4,3,2,1,0:T(4,128)(2,1)} %copy.86) | data formatting | bytes 2359296 | tf_op jit(solution)/shard_map/reshape | solution.py:106
  75.9 1.5 %fusion.6 = bf16[4,16,17,256]{3,1,2,0:T(8,128)(2,1)S(1)} fusion(bf16[3,3,256,256]{3,2,1,0:T(8,128)(2,1)S(1)} %reshape.72, bf16[256,6,2,8,19]{0,2,4,3,1:T(2,128)(2,1)S(1)} %copy-done.4, pred[16,17]{0,1:T(8,128)(4,1)S(1)} %copy-done.12), kind=kOutput, calls=%fused_computation.24 | convolution fusion | flops 1284014080 | bytes 2670864 | tf_op jit(solution)/shard_map/conv_general_dilated | solution.py:52
  78.7 1.9 %collective-permute-start.10 = (bf16[256,1,4,128]{0,2,3,1:T(4,128)(2,1)}, bf16[256,1,4,128]{0,2,3,1:T(4,128)(2,1)}, u32[]{:S(2)}, u32[]{:S(2)}) collective-permute-start(bf16[256,1,4,128]{0,2,3,1:T(4,128)(2,1)} %get-tuple-element.19), channel_id=1, source_target_pairs={{8,0},{16,8},{24,16},{9,1},{17,9},{25,17},{10,2},{18,10},{26,18},{... | collective-permute-start | bytes 786440 | tf_op jit(solution)/shard_map/ppermute | solution.py:47
  80.7 3.8 %collective-permute-start.9 = (bf16[256,1,4,128]{0,2,3,1:T(4,128)(2,1)S(1)}, bf16[256,1,4,128]{0,2,3,1:T(4,128)(2,1)}, u32[]{:S(2)}, u32[]{:S(2)}) collective-permute-start(bf16[256,1,4,128]{0,2,3,1:T(4,128)(2,1)S(1)} %get-tuple-element.18), channel_id=1, source_target_pairs={{0,8},{8,16},{16,24},{1,9},{9,17},{17,25},{2,10},{10,18},{18,26},{... | collective-permute-start | bytes 786440 | tf_op jit(solution)/shard_map/ppermute | solution.py:46
  85.6 1.4 %copy.100 = bf16[256,4,4,128]{0,3,2,1:T(8,128)(2,1)} copy(bf16[256,4,4,128]{3,0,2,1:T(8,128)(2,1)S(1)} %pad_maximum_fusion.1) | data formatting | bytes 2097152 | tf_op jit(solution)/shard_map/concatenate | solution.py:48
  87.0 1.8 %convolution_convert_fusion = bf16[2,4,8,16,256]{4,2,3,1,0:T(8,128)(2,1)S(1)} fusion(bf16[256,4,4,8,16]{0,4,3,2,1:T(8,128)(2,1)} %bitcast.104, bf16[3,256,256]{2,1,0:T(8,128)(2,1)S(1)} %copy-done.8), kind=kOutput, calls=%fused_computation.26 | convolution fusion | flops 402915328 | bytes 1966080 | tf_op jit(solution)/shard_map/conv_general_dilated | solution.py:63
  90.3 4.0 %collective-permute-start.14 = (bf16[256,2,1,128]{0,3,2,1:T(8,128)(2,1)S(1)}, bf16[256,2,1,128]{0,3,2,1:T(8,128)(2,1)S(1)}, u32[]{:S(2)}, u32[]{:S(2)}) collective-permute-start(bf16[256,2,1,128]{0,3,2,1:T(8,128)(2,1)S(1)} %get-tuple-element.10), channel_id=1, source_target_pairs={{0,4},{4,5},{5,1},{1,2},{2,6},{6,7},{7,3},{8,12},{12,13},{13,9},{9... | collective-permute-start | bytes 393224 | tf_op jit(solution)/shard_map/ppermute | solution.py:46
  94.3 1.8 %pad_maximum_fusion = bf16[256,4,4,128]{0,2,3,1:T(4,128)(2,1)S(1)} fusion(bf16[256,1,4,128]{0,2,3,1:T(4,128)(2,1)} %collective-permute-done.10, bf16[256,2,4,128]{0,2,3,1:T(4,128)(2,1)S(1)} %slice_bitcast_fusion.1, bf16[256,1,4,128]{0,2,3,1:T(4,128)(2,1)} %collective-permute-done.9), kind=kLoop, calls=%fused_computation.35 | loop fusion | flops 1048576 | bytes 2097152 | tf_op jit(solution)/shard_map/concatenate | solution.py:48
  99.8 1.5 %fusion.7 = bf16[4,16,17,256]{3,1,2,0:T(8,128)(2,1)S(1)} fusion(bf16[3,3,256,256]{3,2,1,0:T(8,128)(2,1)S(1)} %reshape.72, bf16[256,6,2,8,19]{0,2,4,3,1:T(2,128)(2,1)S(1)} %fusion.18, pred[16,17]{0,1:T(8,128)(4,1)S(1)} %copy-done.12), kind=kOutput, calls=%fused_computation.25 | convolution fusion | flops 1284014080 | bytes 2670864 | tf_op jit(solution)/shard_map/conv_general_dilated | solution.py:52
  103.1 3.8 %all-to-all-start.2 = ((bf16[256,2,4,128]{3,2,1,0:T(4,128)(2,1)}), bf16[256,2,4,128]{3,2,1,0:T(4,128)(2,1)S(1)}, u32[]{:S(2)}, u32[]{:S(2)}) async-start(bf16[256,2,4,128]{3,2,1,0:T(4,128)(2,1)} %copy.107), calls=%async_computation.2 | async-start | bytes 1048576 | tf_op jit(solution)/shard_map/all_to_all | solution.py:169
  106.9 1.4 %convolution_convert_fusion.1 = bf16[2,4,8,16,256]{4,2,3,1,0:T(8,128)(2,1)S(1)} fusion(bf16[256,4,4,8,16]{0,2,4,3,1:T(4,128)(2,1)S(1)} %bitcast.103, bf16[3,256,256]{2,1,0:T(8,128)(2,1)S(1)} %copy-done.7), kind=kOutput, calls=%fused_computation.27 | convolution fusion | flops 402915328 | bytes 1966080 | tf_op jit(solution)/shard_map/conv_general_dilated | solution.py:63
  109.5 5.9 %all-to-all-done.2 = bf16[256,2,4,128]{3,2,1,0:T(4,128)(2,1)S(1)} async-done(((bf16[256,2,4,128]{3,2,1,0:T(4,128)(2,1)}), bf16[256,2,4,128]{3,2,1,0:T(4,128)(2,1)S(1)}, u32[]{:S(2)}, u32[]{:S(2)}) %all-to-all-start.2) | async-done | bytes 524320 | tf_op jit(solution)/shard_map/all_to_all | solution.py:169
  115.4 4.4 %all-to-all-start = ((bf16[256,2,4,128]{3,2,1,0:T(4,128)(2,1)}), bf16[256,2,4,128]{3,2,1,0:T(4,128)(2,1)S(1)}, u32[]{:S(2)}, u32[]{:S(2)}) async-start(bf16[256,2,4,128]{3,2,1,0:T(4,128)(2,1)} %copy.92), calls=%async_computation | async-start | bytes 1048576 | tf_op jit(solution)/shard_map/all_to_all | solution.py:132
  121.2 12.6 %all-to-all-done = bf16[256,2,4,128]{3,2,1,0:T(4,128)(2,1)S(1)} async-done(((bf16[256,2,4,128]{3,2,1,0:T(4,128)(2,1)}), bf16[256,2,4,128]{3,2,1,0:T(4,128)(2,1)S(1)}, u32[]{:S(2)}, u32[]{:S(2)}) %all-to-all-start) | async-done | bytes 524320 | tf_op jit(solution)/shard_map/all_to_all | solution.py:132
  (97 shorter events, 29.0 us)
Async XLA Ops:
  0.6 11.3 %copy-start.9 = (s32[2,2]{1,0:T(2,128)S(1)}, s32[2,2]{1,0:T(2,128)}, u32[]{:S(2)}) copy-start(s32[2,2]{1,0:T(2,128)} %constant.137.clone) | copy-start | bytes 52
  0.6 11.2 %copy-start.10 = (s32[2,2]{1,0:T(2,128)S(1)}, s32[2,2]{1,0:T(2,128)}, u32[]{:S(2)}) copy-start(s32[2,2]{1,0:T(2,128)} %constant.136.clone) | copy-start | bytes 52
  0.7 15.1 %copy-start.5 = (bf16[64,2,16,128]{3,2,1,0:T(8,128)(2,1)S(1)}, bf16[64,2,16,128]{3,2,1,0:T(8,128)(2,1)}, u32[]{:S(2)}) copy-start(bf16[64,2,16,128]{3,2,1,0:T(8,128)(2,1)} %param.10) | copy-start | bytes 1572868
  1.8 14.6 %collective-permute-start.1 = (bf16[3,3,64,64]{2,3,1,0:T(8,128)(2,1)S(1)}, bf16[3,3,64,64]{2,3,1,0:T(8,128)(2,1)S(1)}, u32[]{:S(2)}, u32[]{:S(2)}) collective-permute-start(bf16[3,3,64,64]{2,3,1,0:T(8,128)(2,1)S(1)} %constant_dynamic-slice_fusion.7), channel_id=1, source_target_pairs={{1,0},{2,1},{3,2},{5,4},{6,5},{7,6},{9,8},{10,9},{11,10},{13,12},{... | collective-permute-start | bytes 221192 | tf_op jit(solution)/shard_map/ppermute | solution.py:82
  3.1 14.6 %collective-permute-start.4 = (bf16[3,3,64,64]{2,3,1,0:T(8,128)(2,1)S(1)}, bf16[3,3,64,64]{2,3,1,0:T(8,128)(2,1)S(1)}, u32[]{:S(2)}, u32[]{:S(2)}) collective-permute-start(bf16[3,3,64,64]{2,3,1,0:T(8,128)(2,1)S(1)} %constant_dynamic-slice_fusion.7), channel_id=1, source_target_pairs={{0,1},{1,2},{2,3},{4,5},{5,6},{6,7},{8,9},{9,10},{10,11},{12,13},{... | collective-permute-start | bytes 221192 | tf_op jit(solution)/shard_map/ppermute | solution.py:81
  10.5 5.9 %copy-start.11 = (s32[2,4]{1,0:T(2,128)S(1)}, s32[2,4]{1,0:T(2,128)}, u32[]{:S(2)}) copy-start(s32[2,4]{1,0:T(2,128)} %constant.138.clone) | copy-start | bytes 100
  10.5 19.8 %copy-start.2 = (bf16[3,3,128,64]{2,3,1,0:T(8,128)(2,1)S(1)}, bf16[3,3,128,64]{2,3,1,0:T(8,128)(2,1)}, u32[]{:S(2)}) copy-start(bf16[3,3,128,64]{2,3,1,0:T(8,128)(2,1)} %param.8) | copy-start | bytes 442372
  10.5 31.2 %collective-permute-start = (bf16[128,2,6,128]{3,2,1,0:T(8,128)(2,1)}, bf16[128,2,6,128]{3,2,1,0:T(8,128)(2,1)S(1)}, u32[]{:S(2)}, u32[]{:S(2)}) collective-permute-start(bf16[128,2,6,128]{3,2,1,0:T(8,128)(2,1)} %get-tuple-element.9), channel_id=1, source_target_pairs={{0,4},{4,0},{1,5},{5,1},{2,6},{6,2},{3,7},{7,3},{8,12},{12,8},{9,1... | collective-permute-start | bytes 1179656 | tf_op jit(solution)/shard_map/ppermute | solution.py:127
  16.2 16.7 %collective-permute-start.11 = (bf16[2,64,2,4,128]{4,1,3,2,0:T(8,128)(2,1)S(1)}, bf16[2,64,2,4,128]{4,1,3,2,0:T(8,128)(2,1)}, u32[]{:S(2)}, u32[]{:S(2)}) collective-permute-start(bf16[2,64,2,4,128]{4,1,3,2,0:T(8,128)(2,1)S(1)} %pad_maximum_fusion.3), channel_id=1, source_target_pairs={{0,4},{4,0},{1,5},{5,1},{2,6},{6,2},{3,7},{7,3},{8,12},{12,8},{9,1... | collective-permute-start | bytes 786440 | tf_op jit(solution)/shard_map/ppermute | solution.py:154
  16.4 6.4 %collective-permute-start.2 = (bf16[3,3,64,64]{2,3,1,0:T(8,128)(2,1)S(1)}, bf16[3,3,64,64]{2,3,1,0:T(8,128)(2,1)S(1)}, u32[]{:S(2)}, u32[]{:S(2)}) collective-permute-start(bf16[3,3,64,64]{2,3,1,0:T(8,128)(2,1)S(1)} %collective-permute-done.1), channel_id=1, source_target_pairs={{1,0},{2,1},{3,2},{5,4},{6,5},{7,6},{9,8},{10,9},{11,10},{13,12},{... | collective-permute-start | bytes 221192 | tf_op jit(solution)/shard_map/ppermute | solution.py:82
  17.7 6.4 %collective-permute-start.5 = (bf16[3,3,64,64]{2,3,1,0:T(8,128)(2,1)S(1)}, bf16[3,3,64,64]{2,3,1,0:T(8,128)(2,1)S(1)}, u32[]{:S(2)}, u32[]{:S(2)}) collective-permute-start(bf16[3,3,64,64]{2,3,1,0:T(8,128)(2,1)S(1)} %collective-permute-done.4), channel_id=1, source_target_pairs={{0,1},{1,2},{2,3},{4,5},{5,6},{6,7},{8,9},{9,10},{10,11},{12,13},{... | collective-permute-start | bytes 221192 | tf_op jit(solution)/shard_map/ppermute | solution.py:81
  22.9 6.3 %collective-permute-start.3 = (bf16[3,3,64,64]{2,3,1,0:T(8,128)(2,1)S(1)}, bf16[3,3,64,64]{2,3,1,0:T(8,128)(2,1)S(1)}, u32[]{:S(2)}, u32[]{:S(2)}) collective-permute-start(bf16[3,3,64,64]{2,3,1,0:T(8,128)(2,1)S(1)} %collective-permute-done.2), channel_id=1, source_target_pairs={{1,0},{2,1},{3,2},{5,4},{6,5},{7,6},{9,8},{10,9},{11,10},{13,12},{... | collective-permute-start | bytes 221192 | tf_op jit(solution)/shard_map/ppermute | solution.py:82
  24.2 6.1 %collective-permute-start.6 = (bf16[3,3,64,64]{2,3,1,0:T(8,128)(2,1)S(1)}, bf16[3,3,64,64]{2,3,1,0:T(8,128)(2,1)S(1)}, u32[]{:S(2)}, u32[]{:S(2)}) collective-permute-start(bf16[3,3,64,64]{2,3,1,0:T(8,128)(2,1)S(1)} %collective-permute-done.5), channel_id=1, source_target_pairs={{0,1},{1,2},{2,3},{4,5},{5,6},{6,7},{8,9},{9,10},{10,11},{12,13},{... | collective-permute-start | bytes 221192 | tf_op jit(solution)/shard_map/ppermute | solution.py:81
  31.5 15.6 %collective-permute-start.7 = (bf16[1,4,3,3,64,64]{4,5,3,2,1,0:T(8,128)(2,1)S(1)}, bf16[1,4,3,3,64,64]{4,5,3,2,1,0:T(8,128)(2,1)S(1)}, u32[]{:S(2)}, u32[]{:S(2)}) collective-permute-start(bf16[1,4,3,3,64,64]{4,5,3,2,1,0:T(8,128)(2,1)S(1)} %maximum_bitcast_fusion.1), channel_id=1, source_target_pairs={{0,4},{4,0},{1,5},{5,1},{2,6},{6,2},{3,7},{7,3},{8,12},{12,8},{9,1... | collective-permute-start | bytes 884744 | tf_op jit(solution)/shard_map/ppermute | solution.py:25
  34.5 6.4 %copy-start.6 = (bf16[3,256,256]{2,1,0:T(8,128)(2,1)S(1)}, bf16[3,256,256]{2,1,0:T(8,128)(2,1)}, u32[]{:S(2)}) copy-start(bf16[3,256,256]{2,1,0:T(8,128)(2,1)} %param.9) | copy-start | bytes 1179652
  35.4 21.5 %all-to-all-start.1 = ((bf16[4,64,2,4,128]{4,1,3,2,0:T(8,128)(2,1)}), bf16[4,64,2,4,128]{4,1,3,2,0:T(8,128)(2,1)}, u32[]{:S(2)}, u32[]{:S(2)}) async-start(bf16[4,64,2,4,128]{4,1,3,2,0:T(8,128)(2,1)} %broadcast_select_fusion), calls=%async_computation.1 | async-start | bytes 1048576 | tf_op jit(solution)/shard_map/all_to_all | solution.py:163
  47.1 5.9 %copy-start.3 = (bf16[1,4,3,3,64,64]{4,5,3,2,1,0:T(8,128)(2,1)}, bf16[1,4,3,3,64,64]{4,5,3,2,1,0:T(8,128)(2,1)S(1)}, u32[]{:S(2)}) copy-start(bf16[1,4,3,3,64,64]{4,5,3,2,1,0:T(8,128)(2,1)S(1)} %collective-permute-done.7) | copy-start | bytes 884740
  48.4 16.3 %collective-permute-start.8 = (bf16[2,4,3,3,64,64]{4,5,3,2,1,0:T(8,128)(2,1)S(1)}, bf16[2,4,3,3,64,64]{4,5,3,2,1,0:T(8,128)(2,1)}, u32[]{:S(2)}, u32[]{:S(2)}) collective-permute-start(bf16[2,4,3,3,64,64]{4,5,3,2,1,0:T(8,128)(2,1)S(1)} %fusion.10), channel_id=1, source_target_pairs={{0,8},{8,0},{16,24},{24,16},{1,9},{9,1},{17,25},{25,17},{2,10},{10... | collective-permute-start | bytes 1769480 | tf_op jit(solution)/shard_map/ppermute | solution.py:103
  58.0 6.7 %copy-start = (bf16[4,64,2,4,128]{4,1,0,3,2:T(8,128)(2,1)}, bf16[4,64,2,4,128]{4,1,0,3,2:T(8,128)(2,1)S(1)}, u32[]{:S(2)}) copy-start(bf16[4,64,2,4,128]{4,1,0,3,2:T(8,128)(2,1)S(1)} %copy.99) | copy-start | bytes 1572868
  58.9 25.5 %collective-permute-start.13 = (bf16[256,1,4,128]{3,0,2,1:T(8,128)(2,1)}, bf16[256,1,4,128]{3,0,2,1:T(8,128)(2,1)}, u32[]{:S(2)}, u32[]{:S(2)}) collective-permute-start(bf16[256,1,4,128]{3,0,2,1:T(8,128)(2,1)} %get-tuple-element.13), channel_id=1, source_target_pairs={{8,0},{16,8},{24,16},{9,1},{17,9},{25,17},{10,2},{18,10},{26,18},{... | collective-permute-start | bytes 786440 | tf_op jit(solution)/shard_map/ppermute | solution.py:47
  60.9 23.6 %collective-permute-start.12 = (bf16[256,1,4,128]{3,0,2,1:T(8,128)(2,1)}, bf16[256,1,4,128]{3,0,2,1:T(8,128)(2,1)}, u32[]{:S(2)}, u32[]{:S(2)}) collective-permute-start(bf16[256,1,4,128]{3,0,2,1:T(8,128)(2,1)} %get-tuple-element.12), channel_id=1, source_target_pairs={{0,8},{8,16},{16,24},{1,9},{9,17},{17,25},{2,10},{10,18},{18,26},{... | collective-permute-start | bytes 786440 | tf_op jit(solution)/shard_map/ppermute | solution.py:46
  72.0 3.8 %copy-start.4 = (bf16[256,6,2,8,19]{0,2,4,3,1:T(2,128)(2,1)S(1)}, bf16[256,6,2,8,19]{0,2,4,3,1:T(2,128)(2,1)}, u32[]{:S(2)}) copy-start(bf16[256,6,2,8,19]{0,2,4,3,1:T(2,128)(2,1)} %fusion.17) | copy-start | bytes 2801668
  72.0 3.8 %copy-start.12 = (pred[16,17]{0,1:T(8,128)(4,1)S(1)}, pred[16,17]{0,1:T(8,128)(4,1)}, u32[]{:S(2)}) copy-start(pred[16,17]{0,1:T(8,128)(4,1)} %constant.158) | copy-start | bytes 820
  77.4 7.1 %copy-start.1 = (bf16[4,64,2,4,128]{4,1,0,3,2:T(8,128)(2,1)S(1)}, bf16[4,64,2,4,128]{4,1,0,3,2:T(8,128)(2,1)}, u32[]{:S(2)}) copy-start(bf16[4,64,2,4,128]{4,1,0,3,2:T(8,128)(2,1)} %copy-done) | copy-start | bytes 1572868
  78.7 15.5 %collective-permute-start.10 = (bf16[256,1,4,128]{0,2,3,1:T(4,128)(2,1)}, bf16[256,1,4,128]{0,2,3,1:T(4,128)(2,1)}, u32[]{:S(2)}, u32[]{:S(2)}) collective-permute-start(bf16[256,1,4,128]{0,2,3,1:T(4,128)(2,1)} %get-tuple-element.19), channel_id=1, source_target_pairs={{8,0},{16,8},{24,16},{9,1},{17,9},{25,17},{10,2},{18,10},{26,18},{... | collective-permute-start | bytes 786440 | tf_op jit(solution)/shard_map/ppermute | solution.py:47
  80.7 6.3 %copy-start.8 = (bf16[3,256,256]{2,1,0:T(8,128)(2,1)S(1)}, bf16[3,256,256]{2,1,0:T(8,128)(2,1)}, u32[]{:S(2)}) copy-start(bf16[3,256,256]{2,1,0:T(8,128)(2,1)} %rev.11) | copy-start | bytes 1179652
  80.7 13.6 %collective-permute-start.9 = (bf16[256,1,4,128]{0,2,3,1:T(4,128)(2,1)S(1)}, bf16[256,1,4,128]{0,2,3,1:T(4,128)(2,1)}, u32[]{:S(2)}, u32[]{:S(2)}) collective-permute-start(bf16[256,1,4,128]{0,2,3,1:T(4,128)(2,1)S(1)} %get-tuple-element.18), channel_id=1, source_target_pairs={{0,8},{8,16},{16,24},{1,9},{9,17},{17,25},{2,10},{10,18},{18,26},{... | collective-permute-start | bytes 786440 | tf_op jit(solution)/shard_map/ppermute | solution.py:46
  89.0 7.3 %collective-permute-start.15 = (bf16[256,2,1,128]{0,3,2,1:T(8,128)(2,1)S(1)}, bf16[256,2,1,128]{0,3,2,1:T(8,128)(2,1)S(1)}, u32[]{:S(2)}, u32[]{:S(2)}) collective-permute-start(bf16[256,2,1,128]{0,3,2,1:T(8,128)(2,1)S(1)} %get-tuple-element.11), channel_id=1, source_target_pairs={{4,0},{5,4},{1,5},{2,1},{6,2},{7,6},{3,7},{12,8},{13,12},{9,13},{1... | collective-permute-start | bytes 393224 | tf_op jit(solution)/shard_map/ppermute | solution.py:47
  90.3 7.1 %collective-permute-start.14 = (bf16[256,2,1,128]{0,3,2,1:T(8,128)(2,1)S(1)}, bf16[256,2,1,128]{0,3,2,1:T(8,128)(2,1)S(1)}, u32[]{:S(2)}, u32[]{:S(2)}) collective-permute-start(bf16[256,2,1,128]{0,3,2,1:T(8,128)(2,1)S(1)} %get-tuple-element.10), channel_id=1, source_target_pairs={{0,4},{4,5},{5,1},{1,2},{2,6},{6,7},{7,3},{8,12},{12,13},{13,9},{9... | collective-permute-start | bytes 393224 | tf_op jit(solution)/shard_map/ppermute | solution.py:46
  101.3 5.5 %copy-start.7 = (bf16[3,256,256]{2,1,0:T(8,128)(2,1)S(1)}, bf16[3,256,256]{2,1,0:T(8,128)(2,1)}, u32[]{:S(2)}) copy-start(bf16[3,256,256]{2,1,0:T(8,128)(2,1)} %param.9) | copy-start | bytes 1179652
  103.1 12.3 %all-to-all-start.2 = ((bf16[256,2,4,128]{3,2,1,0:T(4,128)(2,1)}), bf16[256,2,4,128]{3,2,1,0:T(4,128)(2,1)S(1)}, u32[]{:S(2)}, u32[]{:S(2)}) async-start(bf16[256,2,4,128]{3,2,1,0:T(4,128)(2,1)} %copy.107), calls=%async_computation.2 | async-start | bytes 1048576 | tf_op jit(solution)/shard_map/all_to_all | solution.py:169
  115.4 18.4 %all-to-all-start = ((bf16[256,2,4,128]{3,2,1,0:T(4,128)(2,1)}), bf16[256,2,4,128]{3,2,1,0:T(4,128)(2,1)S(1)}, u32[]{:S(2)}, u32[]{:S(2)}) async-start(bf16[256,2,4,128]{3,2,1,0:T(4,128)(2,1)} %copy.92), calls=%async_computation | async-start | bytes 1048576 | tf_op jit(solution)/shard_map/all_to_all | solution.py:132

commit v11 on v9

--- a/solution.py
+++ b/solution.py
@@ -102,8 +102,14 @@
     for k in range(1, chans):
         pieces.append(lax.ppermute(window((chan + k) % chans), "chan", shift_pairs(chans, k)))
     all_channels = order_blocks(pieces, chan, 0)
-    mid = plane_conv(all_channels, weight, "HWIO").astype(jnp.bfloat16)
-    deep = halo(mid, "slab", 1)
+    return plane_conv(all_channels, weight, "HWIO").astype(jnp.bfloat16)
+
+
+def forward_out(deep, depth_weight):
+    chans = lax.axis_size("chan")
+    filts = lax.axis_size("filt")
+    chan = lax.axis_index("chan")
+    rows = deep.shape[2]
     out = depth_conv(deep, depth_weight, "DHWOI").astype(jnp.bfloat16)
     got = lax.all_to_all(out, "filt", 0, 2, tiled=True)
     split = got.reshape(got.shape[:2] + (filts, rows) + got.shape[3:])
@@ -137,12 +143,20 @@
                 slot[t][f] = k * per + q
     blocks = jnp.take(received, jnp.array(slot, jnp.int32)[chan], axis=0)
     all_filters = lax.all_to_all(blocks, "filt", 0, 0, tiled=True)
-    all_filters = all_filters.reshape((-1,) + all_filters.shape[2:])
-    deep = halo(all_filters, "slab", 1)
+    return all_filters.reshape((-1,) + all_filters.shape[2:])
+
+
+def backward_in(deep, weight, depth_weight):
+    chans = lax.axis_size("chan")
+    filts = lax.axis_size("filt")
+    filt = lax.axis_index("filt")
+    rows = deep.shape[2]
+    turn = lambda f, r: r if f % 2 == 0 else chans - 1 - r
+    place = lambda g: turn(g // chans, g % chans) * filts + g // chans
     grad_mid = depth_conv(deep, depth_weight[::-1], "DHWIO").astype(jnp.bfloat16)
     rimmed = halo(grad_mid, ROWS, 2, place)
     grad_in = plane_conv(rimmed, weight[::-1, ::-1], "HWOI").astype(jnp.bfloat16)
-    got = lax.all_to_all(grad_in, "chan", 0, 2, tiled=True)
+    got = scatter_blocks(grad_in, "chan", 0, 2)
     split = got.reshape(got.shape[:2] + (chans, rows) + got.shape[3:])
     flipped = jnp.where(filt % 2 == 0, split, split[:, :, ::-1])
     return flipped.reshape(got.shape)
@@ -150,8 +164,11 @@
 
 def local(volume, plane_weight, depth_weight, grad_out):
     weight = gather_weight(plane_weight)
-    output = forward(volume, weight, depth_weight)
-    grad_in = backward(grad_out, weight, depth_weight)
+    mid = forward(volume, weight, depth_weight)
+    all_filters = backward(grad_out, weight, depth_weight)
+    deep = halo(jnp.concatenate([mid, all_filters]), "slab", 1)
+    output = forward_out(deep[: mid.shape[0]], depth_weight)
+    grad_in = backward_in(deep[mid.shape[0] :], weight, depth_weight)
     return (output, grad_in)
 
 

time: 128 us -> 98.4 us (0.77); the launches traced: 126 us -> 97.8 us
  blocking collectives: 18 us -> 0 us
  starting transfers between devices: 37.4 us -> 28 us
  waiting for transfers between devices: 31.2 us -> 27.4 us
  other arithmetic: 10.7 us -> 12.7 us
  matrix products: 4.99 us -> 6.95 us
    all_to_all x1 -> x0, blocking collectives: 18 us -> none  [backward(): all_filters = lax.all_to_all(blocks, 'filt', 0, 0, tiled=True)]
    all_to_all x2, waiting for transfers between devices: 17.5 us -> 6.55 us  [the longest x1 6.54 us: backward(): all_filters = lax.all_to_all(blocks, 'filt', 0, 0, tiled=True)]
    ppermute x3 -> x2, starting transfers between devices: 10.8 us -> 3.39 us  [halo(): after = lax.ppermute(lax.slice_in_dim(x, 0, 1, axis=dim), axis, down)]
    ppermute x0 -> x1, waiting for transfers between devices: none -> 4.99 us  [scatter_blocks(): pieces.append(lax.ppermute(take((me + k) % n), axis, shift_pairs(n, k)))]
    ppermute x3 -> x2, starting transfers between devices: 10.2 us -> 6.73 us  [halo(): lax.ppermute(lax.slice_in_dim(x, length - 1, length, axis=dim), axis, up)]
    all_to_all x1, waiting for transfers between devices: 0.01 us -> 2.86 us  [gather_weight(): by_filt = lax.all_to_all(spread, 'filt', 0, 0, tiled=True)]
    ppermute x1, waiting for transfers between devices: 2.6 us -> 0.01 us  [forward(): lax.ppermute(window((chan + k) % chans), 'chan', shift_pairs(chans, k))]
    ppermute x3 -> x2, waiting for transfers between devices: 0.01 us -> 2.22 us  [halo(): lax.ppermute(lax.slice_in_dim(x, length - 1, length, axis=dim), axis, up)]
  transfers between devices with their start and end apart: 12 -> 11, of which waited for: 5 -> 6; matrix products, arithmetic and copies ran while one was open for 18% -> 24% of each run, Pallas kernels for 0% -> 0%
where the time goes in v11:
time: 98.4 us; the launch traced here: 97.8 us
  starting transfers between devices  28 us (28%)
  waiting for transfers between devices  27.4 us (28%)
  local copies, waits for them, and re-layouts  19 us (19%)
  other arithmetic  12.7 us (13%)
  matrix products  6.95 us (7%)
  between operations  3.8 us (4%)
    ppermute x2, starting transfers between devices, halo(): lax.ppermute(lax.slice_in_dim(x, length - 1, length, axis=dim), axis, up)  6.73 us
    all_to_all x1, waiting for transfers between devices, backward(): all_filters = lax.all_to_all(blocks, 'filt', 0, 0, tiled=True)  6.54 us
    all_to_all x1, starting transfers between devices, forward_out(): got = lax.all_to_all(out, 'filt', 0, 2, tiled=True)  6.29 us
    ppermute x1, waiting for transfers between devices, backward(): lax.ppermute(send, 'chan', shift_pairs(chans, k))  6.23 us
    all_to_all x1, starting transfers between devices, gather_weight(): by_filt = lax.all_to_all(spread, 'filt', 0, 0, tiled=True)  5.11 us
    ppermute x1, waiting for transfers between devices, scatter_blocks(): pieces.append(lax.ppermute(take((me + k) % n), axis, shift_pairs(n, k)))  4.99 us
    unnamed x20, local copies, waits for them, and re-layouts  4.7 us
    ppermute x2, waiting for transfers between devices, halo(): after = lax.ppermute(lax.slice_in_dim(x, 0, 1, axis=dim), axis, down)  4.5 us
  transfers between devices with their start and end apart: 11, of which 6 were waited for; matrix products, arithmetic and copies ran while one was open for 24% of the time, Pallas kernels for 0%

profile of v11, /device:TPU:1, one launch (start us, length us, event | category | flops | bytes accessed | tf_op | source)
XLA Modules:
  0.0 97.8 jit_solution(17017920342042798925)
XLA Ops:
  0.7 1.9 %pad_dynamic-slice_fusion = (bf16[128,2,6,128]{3,2,1,0:T(8,128)(2,1)S(1)}, bf16[128,2,6,128]{3,2,1,0:T(8,128)(2,1)S(1)}) fusion(s32[]{:T(128)S(6)} %select_n.131, bf16[128,2,32,128]{3,2,1,0:T(8,128)(2,1)} %param.7, s32[]{:T(128)S(6)} %select_n.129), kind=kLoop, calls=%fused_computation.1 | loop fusion | bytes 2883592 | tf_op jit(solution)/shard_map/dynamic_slice | solution.py:100
  2.7 2.1 %collective-permute-start = (bf16[128,2,6,128]{3,2,1,0:T(8,128)(2,1)S(1)}, bf16[128,2,6,128]{3,2,1,0:T(8,128)(2,1)S(1)}, u32[]{:S(2)}, u32[]{:S(2)}) collective-permute-start(bf16[128,2,6,128]{3,2,1,0:T(8,128)(2,1)S(1)} %get-tuple-element.9), channel_id=1, source_target_pairs={{0,4},{4,0},{1,5},{5,1},{2,6},{6,2},{3,7},{7,3},{8,12},{12,8},{9,1... | collective-permute-start | bytes 1179656 | tf_op jit(solution)/shard_map/ppermute | solution.py:103
  4.8 1.0 broadcast_in_dim.31
  5.8 5.1 %all-to-all-start = ((bf16[4,3,3,128,64]{3,4,2,1,0:T(8,128)(2,1)}), bf16[4,3,3,128,64]{3,4,2,1,0:T(8,128)(2,1)S(1)}, u32[]{:S(2)}, u32[]{:S(2)}) async-start(bf16[4,3,3,128,64]{3,4,2,1,0:T(8,128)(2,1)} %broadcast_in_dim.31), calls=%async_computation | async-start | bytes 1179648 | tf_op jit(solution)/shard_map/all_to_all | solution.py:78
  15.6 6.2 %collective-permute-done.2 = bf16[2,64,2,4,128]{4,1,3,2,0:T(8,128)(2,1)S(1)} collective-permute-done((bf16[2,64,2,4,128]{4,1,3,2,0:T(8,128)(2,1)S(1)}, bf16[2,64,2,4,128]{4,1,3,2,0:T(8,128)(2,1)S(1)}, u32[]{:S(2)}, u32[]{:S(2)}) %collective-permute-start.2) | collective-permute-done | bytes 262176 | tf_op jit(solution)/shard_map/ppermute | solution.py:136
  22.5 0.9 broadcast_select_fusion
  23.4 2.9 %all-to-all-done = bf16[4,3,3,128,64]{3,4,2,1,0:T(8,128)(2,1)S(1)} async-done(((bf16[4,3,3,128,64]{3,4,2,1,0:T(8,128)(2,1)}), bf16[4,3,3,128,64]{3,4,2,1,0:T(8,128)(2,1)S(1)}, u32[]{:S(2)}, u32[]{:S(2)}) %all-to-all-start) | async-done | bytes 589856 | tf_op jit(solution)/shard_map/all_to_all | solution.py:78
  26.3 3.5 %all-to-all-start.1 = ((bf16[4,64,2,4,128]{4,1,3,2,0:T(8,128)(2,1)}), bf16[4,64,2,4,128]{4,1,3,2,0:T(8,128)(2,1)S(1)}, u32[]{:S(2)}, u32[]{:S(2)}) async-start(bf16[4,64,2,4,128]{4,1,3,2,0:T(8,128)(2,1)} %broadcast_select_fusion), calls=%async_computation.1 | async-start | bytes 1048576 | tf_op jit(solution)/shard_map/all_to_all | solution.py:145
  30.1 3.4 %fusion.11 = bf16[256,6,2,128]{3,1,2,0:T(8,128)(2,1)S(1)} fusion(s32[]{:T(128)S(6)} %select_n.133, bf16[128,2,6,128]{3,2,1,0:T(8,128)(2,1)S(1)} %collective-permute-done, bf16[128,2,6,128]{3,2,1,0:T(8,128)(2,1)S(1)} %get-tuple-element.8), kind=kLoop, calls=%fused_computation.28 | loop fusion | flops 1179648 | bytes 1572868 | tf_op jit(solution)/shard_map/jit(_roll_dynamic)/dynamic_slice | solution.py:19
  33.5 1.3 %copy.86 = bf16[256,6,2,128]{0,2,3,1:T(2,128)(2,1)S(1)} copy(bf16[256,6,2,128]{3,1,2,0:T(8,128)(2,1)S(1)} %fusion.11) | data formatting | bytes 1572864
  35.5 1.7 %fusion.14 = bf16[256,6,2,8,19]{0,2,4,3,1:T(2,128)(2,1)} fusion(bf16[256,6,2,7,2]{0,2,4,3,1:T(2,128)(2,1)S(1)} %slice.52, bf16[256,6,2,8,17]{0,2,4,3,1:T(2,128)(2,1)S(1)} %bitcast.81), kind=kLoop, calls=%fused_computation.37 | loop fusion | flops 2801664 | bytes 1855488 | tf_op jit(solution)/shard_map/conv_general_dilated | solution.py:52
  37.2 6.5 %all-to-all-done.1 = bf16[4,64,2,4,128]{4,1,3,2,0:T(8,128)(2,1)S(1)} async-done(((bf16[4,64,2,4,128]{4,1,3,2,0:T(8,128)(2,1)}), bf16[4,64,2,4,128]{4,1,3,2,0:T(8,128)(2,1)S(1)}, u32[]{:S(2)}, u32[]{:S(2)}) %all-to-all-start.1) | async-done | bytes 524320 | tf_op jit(solution)/shard_map/all_to_all | solution.py:145
  44.1 1.9 %fusion.7 = bf16[3,3,2,128,4,64]{3,5,1,0,4,2:T(8,128)(2,1)S(1)} fusion(s32[]{:T(128)S(6)} %select_n.134, bf16[1,4,3,3,128,64]{4,5,3,2,1,0:T(8,128)(2,1)} %collective-permute-done.1, bf16[1,4,3,3,128,64]{4,5,3,2,1,0:T(8,128)(2,1)S(1)} %bitcast.85), kind=kLoop, calls=%fused_computation.24 | loop fusion | flops 1769472 | bytes 2359300 | tf_op jit(solution)/shard_map/transpose | solution.py:81
  46.0 1.2 %copy.57 = bf16[3,3,2,128,4,64]{3,2,5,4,1,0:T(2,128)(2,1)S(1)} copy(bf16[3,3,2,128,4,64]{3,5,1,0,4,2:T(8,128)(2,1)S(1)} %fusion.7) | data formatting | bytes 2359296 | tf_op jit(solution)/shard_map/transpose | solution.py:81
  48.0 2.7 %fusion.2 = bf16[4,16,17,256]{3,1,2,0:T(8,128)(2,1)S(1)} fusion(bf16[3,3,256,256]{2,3,1,0:T(8,128)(2,1)S(1)} %reshape.74, bf16[256,6,2,8,19]{0,2,4,3,1:T(2,128)(2,1)} %fusion.14, pred[16,17]{0,1:T(8,128)(4,1)S(1)} %copy-done.7), kind=kOutput, calls=%fused_computation.17 | convolution fusion | flops 1284014080 | bytes 2670864 | tf_op jit(solution)/shard_map/conv_general_dilated | solution.py:52
  51.7 4.6 %collective-permute-start.3 = (bf16[512,1,4,128]{0,2,3,1:T(4,128)(2,1)S(1)}, bf16[512,1,4,128]{0,2,3,1:T(4,128)(2,1)}, u32[]{:S(2)}, u32[]{:S(2)}) collective-permute-start(bf16[512,1,4,128]{0,2,3,1:T(4,128)(2,1)S(1)} %get-tuple-element.10), channel_id=1, source_target_pairs={{0,8},{8,16},{16,24},{1,9},{9,17},{17,25},{2,10},{10,18},{18,26},{... | collective-permute-start | bytes 1572872 | tf_op jit(solution)/shard_map/ppermute | solution.py:46
  56.3 2.1 %collective-permute-start.4 = (bf16[512,1,4,128]{0,2,3,1:T(4,128)(2,1)S(1)}, bf16[512,1,4,128]{0,2,3,1:T(4,128)(2,1)}, u32[]{:S(2)}, u32[]{:S(2)}) collective-permute-start(bf16[512,1,4,128]{0,2,3,1:T(4,128)(2,1)S(1)} %get-tuple-element.11), channel_id=1, source_target_pairs={{8,0},{16,8},{24,16},{9,1},{17,9},{25,17},{10,2},{18,10},{26,18},{... | collective-permute-start | bytes 1572872 | tf_op jit(solution)/shard_map/ppermute | solution.py:47
  58.4 1.8 %rev.11 = bf16[3,256,256]{2,1,0:T(8,128)(2,1)} reverse(bf16[3,256,256]{2,1,0:T(8,128)(2,1)} %param.9), dimensions={0} | reverse | bytes 786432 | tf_op jit(solution)/shard_map/rev | solution.py:156
  60.2 2.2 %collective-permute-done.3 = bf16[512,1,4,128]{0,2,3,1:T(4,128)(2,1)} collective-permute-done((bf16[512,1,4,128]{0,2,3,1:T(4,128)(2,1)S(1)}, bf16[512,1,4,128]{0,2,3,1:T(4,128)(2,1)}, u32[]{:S(2)}, u32[]{:S(2)}) %collective-permute-start.3) | collective-permute-done | bytes 524320 | tf_op jit(solution)/shard_map/ppermute | solution.py:46
  62.4 4.5 %collective-permute-done.4 = bf16[512,1,4,128]{0,2,3,1:T(4,128)(2,1)} collective-permute-done((bf16[512,1,4,128]{0,2,3,1:T(4,128)(2,1)S(1)}, bf16[512,1,4,128]{0,2,3,1:T(4,128)(2,1)}, u32[]{:S(2)}, u32[]{:S(2)}) %collective-permute-start.4) | collective-permute-done | bytes 524320 | tf_op jit(solution)/shard_map/ppermute | solution.py:47
  66.9 2.0 %pad_maximum_fusion = bf16[512,4,4,128]{0,2,3,1:T(4,128)(2,1)S(1)} fusion(bf16[512,1,4,128]{0,2,3,1:T(4,128)(2,1)} %collective-permute-done.4, bf16[256,2,4,128]{0,2,3,1:T(4,128)(2,1)S(1)} %copy.64, bf16[256,2,4,128]{0,2,3,1:T(4,128)(2,1)S(1)} %slice_bitcast_fusion, bf16[512,1,4,128]{0,2,3,1:T(4,128)(2,1)} %collective-permute-done.3), kind=kLoop, calls=%fused_computation.11 | loop fusion | flops 8388608 | bytes 4194304 | tf_op jit(solution)/shard_map/concatenate | solution.py:48
  69.9 1.4 %convolution_convert_fusion = bf16[2,4,8,16,256]{4,2,3,1,0:T(8,128)(2,1)S(1)} fusion(bf16[256,4,4,8,16]{0,2,4,3,1:T(4,128)(2,1)S(1)} %bitcast.95, bf16[3,256,256]{2,1,0:T(8,128)(2,1)S(1)} %copy-done.2), kind=kOutput, calls=%fused_computation.19 | convolution fusion | flops 402915328 | bytes 1966080 | tf_op jit(solution)/shard_map/conv_general_dilated | solution.py:63
  71.4 2.1 %collective-permute-start.5 = (bf16[256,2,1,128]{0,3,2,1:T(8,128)(2,1)S(1)}, bf16[256,2,1,128]{0,3,2,1:T(8,128)(2,1)S(1)}, u32[]{:S(2)}, u32[]{:S(2)}) collective-permute-start(bf16[256,2,1,128]{0,3,2,1:T(8,128)(2,1)S(1)} %get-tuple-element.14), channel_id=1, source_target_pairs={{0,4},{4,5},{5,1},{1,2},{2,6},{6,7},{7,3},{8,12},{12,13},{13,9},{9... | collective-permute-start | bytes 393224 | tf_op jit(solution)/shard_map/ppermute | solution.py:46
  73.6 1.3 %collective-permute-start.6 = (bf16[256,2,1,128]{0,3,2,1:T(8,128)(2,1)S(1)}, bf16[256,2,1,128]{0,3,2,1:T(8,128)(2,1)S(1)}, u32[]{:S(2)}, u32[]{:S(2)}) collective-permute-start(bf16[256,2,1,128]{0,3,2,1:T(8,128)(2,1)S(1)} %get-tuple-element.15), channel_id=1, source_target_pairs={{4,0},{5,4},{1,5},{2,1},{6,2},{7,6},{3,7},{12,8},{13,12},{9,13},{1... | collective-permute-start | bytes 393224 | tf_op jit(solution)/shard_map/ppermute | solution.py:47
  74.9 1.4 %convolution_convert_fusion.1 = bf16[2,4,8,16,256]{4,2,3,1,0:T(8,128)(2,1)S(1)} fusion(bf16[256,4,4,8,16]{0,2,4,3,1:T(4,128)(2,1)S(1)} %bitcast.94, bf16[3,256,256]{2,1,0:T(8,128)(2,1)S(1)} %copy-done.1), kind=kOutput, calls=%fused_computation.20 | convolution fusion | flops 402915328 | bytes 1966080 | tf_op jit(solution)/shard_map/conv_general_dilated | solution.py:63
  76.4 1.1 %copy.69 = bf16[256,2,4,128]{3,2,1,0:T(4,128)(2,1)} copy(bf16[256,2,4,128]{0,3,2,1:T(8,128)(2,1)S(1)} %bitcast.92) | data formatting | bytes 1048576 | tf_op jit(solution)/shard_map/convert_element_type | solution.py:113
  77.5 6.3 %all-to-all-start.2 = ((bf16[256,2,4,128]{3,2,1,0:T(4,128)(2,1)}), bf16[256,2,4,128]{3,2,1,0:T(4,128)(2,1)S(1)}, u32[]{:S(2)}, u32[]{:S(2)}) async-start(bf16[256,2,4,128]{3,2,1,0:T(4,128)(2,1)} %copy.69), calls=%async_computation.2 | async-start | bytes 1048576 | tf_op jit(solution)/shard_map/all_to_all | solution.py:114
  86.3 1.5 %fusion.3 = bf16[4,16,17,256]{3,1,2,0:T(8,128)(2,1)S(1)} fusion(bf16[3,3,256,256]{2,3,1,0:T(8,128)(2,1)S(1)} %reshape.74, bf16[256,6,2,8,19]{0,2,4,3,1:T(2,128)(2,1)S(1)} %fusion.15, pred[16,17]{0,1:T(8,128)(4,1)S(1)} %copy-done.7), kind=kOutput, calls=%fused_computation.18 | convolution fusion | flops 1284014080 | bytes 2670864 | tf_op jit(solution)/shard_map/conv_general_dilated | solution.py:52
  88.7 5.0 %collective-permute-done.7 = bf16[128,2,4,128]{0,2,3,1:T(4,128)(2,1)S(1)} collective-permute-done((bf16[128,2,4,128]{0,2,3,1:T(4,128)(2,1)S(1)}, bf16[128,2,4,128]{0,2,3,1:T(4,128)(2,1)S(1)}, u32[]{:S(2)}, u32[]{:S(2)}) %collective-permute-start.7) | collective-permute-done | bytes 262176 | tf_op jit(solution)/shard_map/ppermute | solution.py:36
  93.7 1.0 %fusion.22 = bf16[128,2,8,128]{0,2,3,1:T(8,128)(2,1)S(1)} fusion(s32[]{:T(128)S(6)} %select_n.149, bf16[128,2,4,128]{0,2,3,1:T(4,128)(2,1)S(1)} %collective-permute-done.7, bf16[128,2,4,128]{0,2,3,1:T(4,128)(2,1)S(1)} %get-tuple-element.12), kind=kLoop, calls=%fused_computation.48 | loop fusion | flops 2097152 | bytes 1048580 | tf_op jit(solution)/shard_map/jit(_roll_dynamic)/concatenate | solution.py:19
  95.3 1.1 %copy.81 = bf16[128,2,8,128]{3,2,1,0:T(8,128)(2,1)} copy(bf16[128,2,8,128]{3,0,2,1:T(8,128)(2,1)S(1)} %bitcast.89) | data formatting | bytes 1048576
  96.7 1.1 %copy.80 = bf16[64,2,16,128]{3,2,1,0:T(8,128)(2,1)} copy(bf16[64,2,16,128]{3,0,2,1:T(8,128)(2,1)S(1)} %bitcast.93) | data formatting | bytes 1048576
  (63 shorter events, 11.1 us)
Async XLA Ops:
  0.6 4.2 %copy-start.3 = (bf16[3,3,128,64]{2,3,1,0:T(8,128)(2,1)S(1)}, bf16[3,3,128,64]{2,3,1,0:T(8,128)(2,1)}, u32[]{:S(2)}) copy-start(bf16[3,3,128,64]{2,3,1,0:T(8,128)(2,1)} %param.8) | copy-start | bytes 442372
  0.7 10.2 %copy-start.4 = (s32[2,2]{1,0:T(2,128)S(1)}, s32[2,2]{1,0:T(2,128)}, u32[]{:S(2)}) copy-start(s32[2,2]{1,0:T(2,128)} %constant.129.clone) | copy-start | bytes 52
  0.7 10.2 %copy-start.5 = (s32[2,2]{1,0:T(2,128)S(1)}, s32[2,2]{1,0:T(2,128)}, u32[]{:S(2)}) copy-start(s32[2,2]{1,0:T(2,128)} %constant.130.clone) | copy-start | bytes 52
  0.7 14.1 %copy-start = (bf16[64,2,16,128]{3,2,1,0:T(8,128)(2,1)S(1)}, bf16[64,2,16,128]{3,2,1,0:T(8,128)(2,1)}, u32[]{:S(2)}) copy-start(bf16[64,2,16,128]{3,2,1,0:T(8,128)(2,1)} %param.10) | copy-start | bytes 1572868
  2.7 12.8 %copy-start.6 = (s32[2,4]{1,0:T(2,128)S(1)}, s32[2,4]{1,0:T(2,128)}, u32[]{:S(2)}) copy-start(s32[2,4]{1,0:T(2,128)} %constant.131.clone) | copy-start | bytes 100
  2.7 27.4 %collective-permute-start = (bf16[128,2,6,128]{3,2,1,0:T(8,128)(2,1)S(1)}, bf16[128,2,6,128]{3,2,1,0:T(8,128)(2,1)S(1)}, u32[]{:S(2)}, u32[]{:S(2)}) collective-permute-start(bf16[128,2,6,128]{3,2,1,0:T(8,128)(2,1)S(1)} %get-tuple-element.9), channel_id=1, source_target_pairs={{0,4},{4,0},{1,5},{5,1},{2,6},{6,2},{3,7},{7,3},{8,12},{12,8},{9,1... | collective-permute-start | bytes 1179656 | tf_op jit(solution)/shard_map/ppermute | solution.py:103
  5.8 20.5 %all-to-all-start = ((bf16[4,3,3,128,64]{3,4,2,1,0:T(8,128)(2,1)}), bf16[4,3,3,128,64]{3,4,2,1,0:T(8,128)(2,1)S(1)}, u32[]{:S(2)}, u32[]{:S(2)}) async-start(bf16[4,3,3,128,64]{3,4,2,1,0:T(8,128)(2,1)} %broadcast_in_dim.31), calls=%async_computation | async-start | bytes 1179648 | tf_op jit(solution)/shard_map/all_to_all | solution.py:78
  15.2 6.6 %collective-permute-start.2 = (bf16[2,64,2,4,128]{4,1,3,2,0:T(8,128)(2,1)S(1)}, bf16[2,64,2,4,128]{4,1,3,2,0:T(8,128)(2,1)S(1)}, u32[]{:S(2)}, u32[]{:S(2)}) collective-permute-start(bf16[2,64,2,4,128]{4,1,3,2,0:T(8,128)(2,1)S(1)} %pad_maximum_fusion.3), channel_id=1, source_target_pairs={{0,4},{4,0},{1,5},{5,1},{2,6},{6,2},{3,7},{7,3},{8,12},{12,8},{9,1... | collective-permute-start | bytes 786440 | tf_op jit(solution)/shard_map/ppermute | solution.py:136
  26.3 17.4 %all-to-all-start.1 = ((bf16[4,64,2,4,128]{4,1,3,2,0:T(8,128)(2,1)}), bf16[4,64,2,4,128]{4,1,3,2,0:T(8,128)(2,1)S(1)}, u32[]{:S(2)}, u32[]{:S(2)}) async-start(bf16[4,64,2,4,128]{4,1,3,2,0:T(8,128)(2,1)} %broadcast_select_fusion), calls=%async_computation.1 | async-start | bytes 1048576 | tf_op jit(solution)/shard_map/all_to_all | solution.py:145
  29.8 14.3 %collective-permute-start.1 = (bf16[1,4,3,3,128,64]{4,5,3,2,1,0:T(8,128)(2,1)S(1)}, bf16[1,4,3,3,128,64]{4,5,3,2,1,0:T(8,128)(2,1)}, u32[]{:S(2)}, u32[]{:S(2)}) collective-permute-start(bf16[1,4,3,3,128,64]{4,5,3,2,1,0:T(8,128)(2,1)S(1)} %bitcast.84), channel_id=1, source_target_pairs={{0,4},{4,0},{1,5},{5,1},{2,6},{6,2},{3,7},{7,3},{8,12},{12,8},{9,1... | collective-permute-start | bytes 1769480 | tf_op jit(solution)/shard_map/ppermute | solution.py:25
  46.0 2.0 %copy-start.7 = (pred[16,17]{0,1:T(8,128)(4,1)S(1)}, pred[16,17]{0,1:T(8,128)(4,1)}, u32[]{:S(2)}) copy-start(pred[16,17]{0,1:T(8,128)(4,1)} %constant.151) | copy-start | bytes 820
  51.7 10.7 %collective-permute-start.3 = (bf16[512,1,4,128]{0,2,3,1:T(4,128)(2,1)S(1)}, bf16[512,1,4,128]{0,2,3,1:T(4,128)(2,1)}, u32[]{:S(2)}, u32[]{:S(2)}) collective-permute-start(bf16[512,1,4,128]{0,2,3,1:T(4,128)(2,1)S(1)} %get-tuple-element.10), channel_id=1, source_target_pairs={{0,8},{8,16},{16,24},{1,9},{9,17},{17,25},{2,10},{10,18},{18,26},{... | collective-permute-start | bytes 1572872 | tf_op jit(solution)/shard_map/ppermute | solution.py:46
  56.3 10.6 %collective-permute-start.4 = (bf16[512,1,4,128]{0,2,3,1:T(4,128)(2,1)S(1)}, bf16[512,1,4,128]{0,2,3,1:T(4,128)(2,1)}, u32[]{:S(2)}, u32[]{:S(2)}) collective-permute-start(bf16[512,1,4,128]{0,2,3,1:T(4,128)(2,1)S(1)} %get-tuple-element.11), channel_id=1, source_target_pairs={{8,0},{16,8},{24,16},{9,1},{17,9},{25,17},{10,2},{18,10},{26,18},{... | collective-permute-start | bytes 1572872 | tf_op jit(solution)/shard_map/ppermute | solution.py:47
  68.9 1.0 %copy-start.2 = (bf16[3,256,256]{2,1,0:T(8,128)(2,1)S(1)}, bf16[3,256,256]{2,1,0:T(8,128)(2,1)}, u32[]{:S(2)}) copy-start(bf16[3,256,256]{2,1,0:T(8,128)(2,1)} %rev.11) | copy-start | bytes 1179652
  69.9 5.0 %copy-start.1 = (bf16[3,256,256]{2,1,0:T(8,128)(2,1)S(1)}, bf16[3,256,256]{2,1,0:T(8,128)(2,1)}, u32[]{:S(2)}) copy-start(bf16[3,256,256]{2,1,0:T(8,128)(2,1)} %param.9) | copy-start | bytes 1179652
  71.4 12.3 %collective-permute-start.5 = (bf16[256,2,1,128]{0,3,2,1:T(8,128)(2,1)S(1)}, bf16[256,2,1,128]{0,3,2,1:T(8,128)(2,1)S(1)}, u32[]{:S(2)}, u32[]{:S(2)}) collective-permute-start(bf16[256,2,1,128]{0,3,2,1:T(8,128)(2,1)S(1)} %get-tuple-element.14), channel_id=1, source_target_pairs={{0,4},{4,5},{5,1},{1,2},{2,6},{6,7},{7,3},{8,12},{12,13},{13,9},{9... | collective-permute-start | bytes 393224 | tf_op jit(solution)/shard_map/ppermute | solution.py:46
  73.6 10.2 %collective-permute-start.6 = (bf16[256,2,1,128]{0,3,2,1:T(8,128)(2,1)S(1)}, bf16[256,2,1,128]{0,3,2,1:T(8,128)(2,1)S(1)}, u32[]{:S(2)}, u32[]{:S(2)}) collective-permute-start(bf16[256,2,1,128]{0,3,2,1:T(8,128)(2,1)S(1)} %get-tuple-element.15), channel_id=1, source_target_pairs={{4,0},{5,4},{1,5},{2,1},{6,2},{7,6},{3,7},{12,8},{13,12},{9,13},{1... | collective-permute-start | bytes 393224 | tf_op jit(solution)/shard_map/ppermute | solution.py:47
  77.5 18.9 %all-to-all-start.2 = ((bf16[256,2,4,128]{3,2,1,0:T(4,128)(2,1)}), bf16[256,2,4,128]{3,2,1,0:T(4,128)(2,1)S(1)}, u32[]{:S(2)}, u32[]{:S(2)}) async-start(bf16[256,2,4,128]{3,2,1,0:T(4,128)(2,1)} %copy.69), calls=%async_computation.2 | async-start | bytes 1048576 | tf_op jit(solution)/shard_map/all_to_all | solution.py:114
  88.4 5.3 %collective-permute-start.7 = (bf16[128,2,4,128]{0,2,3,1:T(4,128)(2,1)S(1)}, bf16[128,2,4,128]{0,2,3,1:T(4,128)(2,1)S(1)}, u32[]{:S(2)}, u32[]{:S(2)}) collective-permute-start(bf16[128,2,4,128]{0,2,3,1:T(4,128)(2,1)S(1)} %get-tuple-element.13), channel_id=1, source_target_pairs={{0,4},{4,0},{1,5},{5,1},{2,6},{6,2},{3,7},{7,3},{8,12},{12,8},{9,1... | collective-permute-start | bytes 786440 | tf_op jit(solution)/shard_map/ppermute | solution.py:36

commit v12 on v11

--- a/solution.py
+++ b/solution.py
@@ -90,7 +90,7 @@
     return f if c % 2 == 0 else filts - 1 - f
 
 
-def forward(volume, weight, depth_weight):
+def volume_sends(volume):
     chans = lax.axis_size("chan")
     filts = lax.axis_size("filt")
     chan = lax.axis_index("chan")
@@ -98,10 +98,11 @@
     rows = volume.shape[2] // (chans * filts)
     padded = jnp.pad(volume, ((0, 0), (0, 0), (1, 1), (0, 0)))
     window = lambda c: lax.dynamic_slice_in_dim(padded, (c * filts + sub_block(c, filt, filts)) * rows, rows + 2, 2)
-    pieces = [window(chan)]
-    for k in range(1, chans):
-        pieces.append(lax.ppermute(window((chan + k) % chans), "chan", shift_pairs(chans, k)))
-    all_channels = order_blocks(pieces, chan, 0)
+    return [window((chan + k) % chans) for k in range(chans)]
+
+
+def forward(pieces, weight):
+    all_channels = order_blocks(pieces, lax.axis_index("chan"), 0)
     return plane_conv(all_channels, weight, "HWIO").astype(jnp.bfloat16)
 
 
@@ -117,7 +118,7 @@
     return flipped.reshape(got.shape)
 
 
-def backward(grad_out, weight, depth_weight):
+def grad_sends(grad_out):
     chans = lax.axis_size("chan")
     filts = lax.axis_size("filt")
     chan = lax.axis_index("chan")
@@ -129,11 +130,21 @@
     need = [[[f for f in range(filts) if group_of(t, f) // filts == r] for r in range(chans)] for t in range(chans)]
     per = max(len(need[t][r]) for t in range(chans) for r in range(chans))
     pick = lambda t, r: [group_of(t, f) % filts for f in need[t][r]] + [0] * (per - len(need[t][r]))
-    received = []
+    sends = []
     for k in range(chans):
         table = jnp.array([pick((r + k) % chans, r) for r in range(chans)], jnp.int32)[chan]
-        send = jnp.stack([lax.dynamic_slice_in_dim(grad_out, table[q] * rows, rows, 2) for q in range(per)])
-        received.append(send if k == 0 else lax.ppermute(send, "chan", shift_pairs(chans, k)))
+        sends.append(jnp.stack([lax.dynamic_slice_in_dim(grad_out, table[q] * rows, rows, 2) for q in range(per)]))
+    return sends
+
+
+def grad_blocks(received):
+    chans = lax.axis_size("chan")
+    filts = lax.axis_size("filt")
+    chan = lax.axis_index("chan")
+    turn = lambda f, r: r if f % 2 == 0 else chans - 1 - r
+    group_of = lambda c, f: f * chans + turn(f, c)
+    need = [[[f for f in range(filts) if group_of(t, f) // filts == r] for r in range(chans)] for t in range(chans)]
+    per = received[0].shape[0]
     received = jnp.concatenate(received)
     slot = [[0] * filts for _ in range(chans)]
     for t in range(chans):
@@ -164,8 +175,22 @@
 
 def local(volume, plane_weight, depth_weight, grad_out):
     weight = gather_weight(plane_weight)
-    mid = forward(volume, weight, depth_weight)
-    all_filters = backward(grad_out, weight, depth_weight)
+    chans = lax.axis_size("chan")
+    vol_sends, grad_send = volume_sends(volume), grad_sends(grad_out)
+    vol_got, grad_got = [vol_sends[0]], [grad_send[0]]
+    for k in range(1, chans):
+        a, b = vol_sends[k], grad_send[k]
+        lead, depth, width = a.shape[0], a.shape[1], a.shape[3]
+        if b.size % (lead * depth * width) == 0:
+            both = jnp.concatenate([a, b.reshape(lead, depth, -1, width)], axis=2)
+            both = lax.ppermute(both, "chan", shift_pairs(chans, k))
+            vol_got.append(both[:, :, : a.shape[2]])
+            grad_got.append(both[:, :, a.shape[2] :].reshape(b.shape))
+        else:
+            vol_got.append(lax.ppermute(a, "chan", shift_pairs(chans, k)))
+            grad_got.append(lax.ppermute(b, "chan", shift_pairs(chans, k)))
+    mid = forward(vol_got, weight)
+    all_filters = grad_blocks(grad_got)
     deep = halo(jnp.concatenate([mid, all_filters]), "slab", 1)
     output = forward_out(deep[: mid.shape[0]], depth_weight)
     grad_in = backward_in(deep[mid.shape[0] :], weight, depth_weight)

time: 98.4 us -> 104 us (1.057)
  waiting for transfers between devices: 27.4 us -> 34.4 us
  other arithmetic: 12.7 us -> 10.1 us
  local copies, waits for them, and re-layouts: 19 us -> 20.2 us
    all_to_all x1, waiting for transfers between devices: 6.54 us -> 9.42 us  [grad_blocks(): all_filters = lax.all_to_all(blocks, 'filt', 0, 0, tiled=True)]
    dynamic_slice x1, other arithmetic: 3.41 us -> 0.73 us  [order_blocks(): return jnp.roll(stacked, (me + 1) * block, axis=dim)]
    ppermute x2 -> x1, waiting for transfers between devices: 6.23 us -> 8.76 us  [local(): both = lax.ppermute(both, 'chan', shift_pairs(chans, k))]
    unnamed x20 -> x19, local copies, waits for them, and re-layouts: 4.7 us -> 7.09 us
    all_to_all x1, waiting for transfers between devices: 2.86 us -> 4.88 us  [gather_weight(): by_filt = lax.all_to_all(spread, 'filt', 0, 0, tiled=True)]
    dynamic_slice x7 -> x5, local copies, waits for them, and re-layouts: 2.31 us -> 1.14 us  [the longest x1 0.71 us: grad_sends(): jnp.array([pick((r + k) % chans, r) for r in range(chans)], jnp.int32)[chan]]
    ppermute x2 -> x1, starting transfers between devices: 2.43 us -> 2.13 us  [local(): both = lax.ppermute(both, 'chan', shift_pairs(chans, k))]
  transfers between devices with their start and end apart: 11 -> 10, of which waited for: 6 -> 6; matrix products, arithmetic and copies ran while one was open for 24% -> 18% of each run, Pallas kernels for 0% -> 0%
where the time goes in v12:
time: 104 us
  waiting for transfers between devices  34.4 us (33%)
  starting transfers between devices  28 us (27%)
  local copies, waits for them, and re-layouts  20.2 us (19%)
  other arithmetic  10.1 us (10%)
  matrix products  6.95 us (7%)
  between operations  3.83 us (4%)
    all_to_all x1, waiting for transfers between devices, grad_blocks(): all_filters = lax.all_to_all(blocks, 'filt', 0, 0, tiled=True)  9.42 us
    ppermute x1, waiting for transfers between devices, local(): both = lax.ppermute(both, 'chan', shift_pairs(chans, k))  8.76 us
    ppermute x2, starting transfers between devices, halo(): lax.ppermute(lax.slice_in_dim(x, length - 1, length, axis=dim), axis, up)  7.16 us
    unnamed x19, local copies, waits for them, and re-layouts  7.09 us
    all_to_all x1, starting transfers between devices, forward_out(): got = lax.all_to_all(out, 'filt', 0, 2, tiled=True)  5.87 us
    all_to_all x1, waiting for transfers between devices, gather_weight(): by_filt = lax.all_to_all(spread, 'filt', 0, 0, tiled=True)  4.88 us
    all_to_all x1, starting transfers between devices, gather_weight(): by_filt = lax.all_to_all(spread, 'filt', 0, 0, tiled=True)  4.59 us
    ppermute x1, waiting for transfers between devices, scatter_blocks(): pieces.append(lax.ppermute(take((me + k) % n), axis, shift_pairs(n, k)))  4.58 us
  transfers between devices with their start and end apart: 10, of which 6 were waited for; matrix products, arithmetic and copies ran while one was open for 18% of the time, Pallas kernels for 0%

profile of v12, /device:TPU:1, one launch (start us, length us, event | category | flops | bytes accessed | tf_op | source)
XLA Modules:
  0.0 103.5 jit_solution(16718008024856111526)
XLA Ops:
  5.2 3.0 %copy.136 = bf16[128,2,32,128]{3,0,2,1:T(8,128)(2,1)S(1)} copy(bf16[128,2,32,128]{3,2,1,0:T(8,128)(2,1)} %param.7) | data formatting | bytes 4194304 | tf_op args[0]
  8.9 2.1 %collective-permute-start = (bf16[128,2,10,128]{3,0,2,1:T(8,128)(2,1)S(1)}, bf16[128,2,10,128]{3,0,2,1:T(8,128)(2,1)S(1)}, u32[]{:S(2)}, u32[]{:S(2)}) collective-permute-start(bf16[128,2,10,128]{3,0,2,1:T(8,128)(2,1)S(1)} %pad_maximum_fusion.1), channel_id=1, source_target_pairs={{0,4},{4,0},{1,5},{5,1},{2,6},{6,2},{3,7},{7,3},{8,12},{12,8},{9,1... | collective-permute-start | bytes 1966088 | tf_op jit(solution)/shard_map/ppermute | solution.py:186
  11.0 1.0 broadcast_in_dim.31
  12.0 4.6 %all-to-all-start = ((bf16[4,3,3,128,64]{3,4,2,1,0:T(8,128)(2,1)}), bf16[4,3,3,128,64]{3,4,2,1,0:T(8,128)(2,1)S(1)}, u32[]{:S(2)}, u32[]{:S(2)}) async-start(bf16[4,3,3,128,64]{3,4,2,1,0:T(8,128)(2,1)} %broadcast_in_dim.31), calls=%async_computation | async-start | bytes 1179648 | tf_op jit(solution)/shard_map/all_to_all | solution.py:78
  16.7 8.8 %collective-permute-done = bf16[128,2,10,128]{3,0,2,1:T(8,128)(2,1)S(1)} collective-permute-done((bf16[128,2,10,128]{3,0,2,1:T(8,128)(2,1)S(1)}, bf16[128,2,10,128]{3,0,2,1:T(8,128)(2,1)S(1)}, u32[]{:S(2)}, u32[]{:S(2)}) %collective-permute-start) | collective-permute-done | bytes 655392 | tf_op jit(solution)/shard_map/ppermute | solution.py:186
  26.2 0.9 broadcast_select_fusion
  27.1 4.9 %all-to-all-done = bf16[4,3,3,128,64]{3,4,2,1,0:T(8,128)(2,1)S(1)} async-done(((bf16[4,3,3,128,64]{3,4,2,1,0:T(8,128)(2,1)}), bf16[4,3,3,128,64]{3,4,2,1,0:T(8,128)(2,1)S(1)}, u32[]{:S(2)}, u32[]{:S(2)}) %all-to-all-start) | async-done | bytes 589856 | tf_op jit(solution)/shard_map/all_to_all | solution.py:78
  32.0 3.5 %all-to-all-start.1 = ((bf16[4,64,2,4,128]{4,1,3,2,0:T(8,128)(2,1)}), bf16[4,64,2,4,128]{4,1,3,2,0:T(8,128)(2,1)S(1)}, u32[]{:S(2)}, u32[]{:S(2)}) async-start(bf16[4,64,2,4,128]{4,1,3,2,0:T(8,128)(2,1)} %broadcast_select_fusion), calls=%async_computation.1 | async-start | bytes 1048576 | tf_op jit(solution)/shard_map/all_to_all | solution.py:156
  38.3 1.7 %fusion.10 = bf16[256,6,2,8,19]{0,2,4,3,1:T(2,128)(2,1)} fusion(bf16[256,6,2,7,2]{0,2,4,3,1:T(2,128)(2,1)S(1)} %slice.61, bf16[256,6,2,8,17]{0,2,4,3,1:T(2,128)(2,1)S(1)} %bitcast.83), kind=kLoop, calls=%fused_computation.33 | loop fusion | flops 2801664 | bytes 1855488 | tf_op jit(solution)/shard_map/conv_general_dilated | solution.py:52
  40.0 9.4 %all-to-all-done.1 = bf16[4,64,2,4,128]{4,1,3,2,0:T(8,128)(2,1)S(1)} async-done(((bf16[4,64,2,4,128]{4,1,3,2,0:T(8,128)(2,1)}), bf16[4,64,2,4,128]{4,1,3,2,0:T(8,128)(2,1)S(1)}, u32[]{:S(2)}, u32[]{:S(2)}) %all-to-all-start.1) | async-done | bytes 524320 | tf_op jit(solution)/shard_map/all_to_all | solution.py:156
  49.8 1.9 %fusion.7 = bf16[3,3,2,128,4,64]{3,5,1,0,4,2:T(8,128)(2,1)S(1)} fusion(s32[]{:T(128)S(6)} %select_n.142, bf16[1,4,3,3,128,64]{4,5,3,2,1,0:T(8,128)(2,1)} %collective-permute-done.1, bf16[1,4,3,3,128,64]{4,5,3,2,1,0:T(8,128)(2,1)S(1)} %bitcast.87), kind=kLoop, calls=%fused_computation.24 | loop fusion | flops 1769472 | bytes 2359300 | tf_op jit(solution)/shard_map/transpose | solution.py:81
  51.7 1.2 %copy.142 = bf16[3,3,2,128,4,64]{3,2,5,4,1,0:T(2,128)(2,1)S(1)} copy(bf16[3,3,2,128,4,64]{3,5,1,0,4,2:T(8,128)(2,1)S(1)} %fusion.7) | data formatting | bytes 2359296 | tf_op jit(solution)/shard_map/transpose | solution.py:81
  53.7 2.7 %fusion.2 = bf16[4,16,17,256]{3,1,2,0:T(8,128)(2,1)S(1)} fusion(bf16[3,3,256,256]{2,3,1,0:T(8,128)(2,1)S(1)} %reshape.81, bf16[256,6,2,8,19]{0,2,4,3,1:T(2,128)(2,1)} %fusion.10, pred[16,17]{0,1:T(8,128)(4,1)S(1)} %copy-done.5), kind=kOutput, calls=%fused_computation.17 | convolution fusion | flops 1284014080 | bytes 2670864 | tf_op jit(solution)/shard_map/conv_general_dilated | solution.py:52
  57.3 4.6 %collective-permute-start.2 = (bf16[512,1,4,128]{0,2,3,1:T(4,128)(2,1)S(1)}, bf16[512,1,4,128]{0,2,3,1:T(4,128)(2,1)}, u32[]{:S(2)}, u32[]{:S(2)}) collective-permute-start(bf16[512,1,4,128]{0,2,3,1:T(4,128)(2,1)S(1)} %get-tuple-element.16), channel_id=1, source_target_pairs={{0,8},{8,16},{16,24},{1,9},{9,17},{17,25},{2,10},{10,18},{18,26},{... | collective-permute-start | bytes 1572872 | tf_op jit(solution)/shard_map/ppermute | solution.py:46
  61.9 2.1 %collective-permute-start.3 = (bf16[512,1,4,128]{0,2,3,1:T(4,128)(2,1)S(1)}, bf16[512,1,4,128]{0,2,3,1:T(4,128)(2,1)}, u32[]{:S(2)}, u32[]{:S(2)}) collective-permute-start(bf16[512,1,4,128]{0,2,3,1:T(4,128)(2,1)S(1)} %get-tuple-element.17), channel_id=1, source_target_pairs={{8,0},{16,8},{24,16},{9,1},{17,9},{25,17},{10,2},{18,10},{26,18},{... | collective-permute-start | bytes 1572872 | tf_op jit(solution)/shard_map/ppermute | solution.py:47
  64.1 1.8 %rev.11 = bf16[3,256,256]{2,1,0:T(8,128)(2,1)} reverse(bf16[3,256,256]{2,1,0:T(8,128)(2,1)} %param.9), dimensions={0} | reverse | bytes 786432 | tf_op jit(solution)/shard_map/rev | solution.py:167
  65.8 2.2 %collective-permute-done.2 = bf16[512,1,4,128]{0,2,3,1:T(4,128)(2,1)} collective-permute-done((bf16[512,1,4,128]{0,2,3,1:T(4,128)(2,1)S(1)}, bf16[512,1,4,128]{0,2,3,1:T(4,128)(2,1)}, u32[]{:S(2)}, u32[]{:S(2)}) %collective-permute-start.2) | collective-permute-done | bytes 524320 | tf_op jit(solution)/shard_map/ppermute | solution.py:46
  68.1 4.5 %collective-permute-done.3 = bf16[512,1,4,128]{0,2,3,1:T(4,128)(2,1)} collective-permute-done((bf16[512,1,4,128]{0,2,3,1:T(4,128)(2,1)S(1)}, bf16[512,1,4,128]{0,2,3,1:T(4,128)(2,1)}, u32[]{:S(2)}, u32[]{:S(2)}) %collective-permute-start.3) | collective-permute-done | bytes 524320 | tf_op jit(solution)/shard_map/ppermute | solution.py:47
  72.6 2.0 %pad_maximum_fusion = bf16[512,4,4,128]{0,2,3,1:T(4,128)(2,1)S(1)} fusion(bf16[512,1,4,128]{0,2,3,1:T(4,128)(2,1)} %collective-permute-done.3, bf16[256,2,4,128]{0,2,3,1:T(4,128)(2,1)S(1)} %copy.148, bf16[256,2,4,128]{0,2,3,1:T(4,128)(2,1)S(1)} %slice_bitcast_fusion, bf16[512,1,4,128]{0,2,3,1:T(4,128)(2,1)} %collective-permute-done.2), kind=kLoop, calls=%fused_computation.5 | loop fusion | flops 8388608 | bytes 4194304 | tf_op jit(solution)/shard_map/concatenate | solution.py:48
  75.6 1.4 %convolution_convert_fusion = bf16[2,4,8,16,256]{4,2,3,1,0:T(8,128)(2,1)S(1)} fusion(bf16[256,4,4,8,16]{0,2,4,3,1:T(4,128)(2,1)S(1)} %bitcast.99, bf16[3,256,256]{2,1,0:T(8,128)(2,1)S(1)} %copy-done.2), kind=kOutput, calls=%fused_computation.19 | convolution fusion | flops 402915328 | bytes 1966080 | tf_op jit(solution)/shard_map/conv_general_dilated | solution.py:63
  77.1 2.6 %collective-permute-start.4 = (bf16[256,2,1,128]{0,3,2,1:T(8,128)(2,1)S(1)}, bf16[256,2,1,128]{0,3,2,1:T(8,128)(2,1)S(1)}, u32[]{:S(2)}, u32[]{:S(2)}) collective-permute-start(bf16[256,2,1,128]{0,3,2,1:T(8,128)(2,1)S(1)} %get-tuple-element.20), channel_id=1, source_target_pairs={{0,4},{4,5},{5,1},{1,2},{2,6},{6,7},{7,3},{8,12},{12,13},{13,9},{9... | collective-permute-start | bytes 393224 | tf_op jit(solution)/shard_map/ppermute | solution.py:46
  79.7 1.3 %collective-permute-start.5 = (bf16[256,2,1,128]{0,3,2,1:T(8,128)(2,1)S(1)}, bf16[256,2,1,128]{0,3,2,1:T(8,128)(2,1)S(1)}, u32[]{:S(2)}, u32[]{:S(2)}) collective-permute-start(bf16[256,2,1,128]{0,3,2,1:T(8,128)(2,1)S(1)} %get-tuple-element.21), channel_id=1, source_target_pairs={{4,0},{5,4},{1,5},{2,1},{6,2},{7,6},{3,7},{12,8},{13,12},{9,13},{1... | collective-permute-start | bytes 393224 | tf_op jit(solution)/shard_map/ppermute | solution.py:47
  81.0 1.4 %convolution_convert_fusion.1 = bf16[2,4,8,16,256]{4,2,3,1,0:T(8,128)(2,1)S(1)} fusion(bf16[256,4,4,8,16]{0,2,4,3,1:T(4,128)(2,1)S(1)} %bitcast.98, bf16[3,256,256]{2,1,0:T(8,128)(2,1)S(1)} %copy-done.1), kind=kOutput, calls=%fused_computation.20 | convolution fusion | flops 402915328 | bytes 1966080 | tf_op jit(solution)/shard_map/conv_general_dilated | solution.py:63
  82.5 1.1 %copy.153 = bf16[256,2,4,128]{3,2,1,0:T(4,128)(2,1)} copy(bf16[256,2,4,128]{0,3,2,1:T(8,128)(2,1)S(1)} %bitcast.94) | data formatting | bytes 1048576 | tf_op jit(solution)/shard_map/convert_element_type | solution.py:114
  83.6 5.9 %all-to-all-start.2 = ((bf16[256,2,4,128]{3,2,1,0:T(4,128)(2,1)}), bf16[256,2,4,128]{3,2,1,0:T(4,128)(2,1)S(1)}, u32[]{:S(2)}, u32[]{:S(2)}) async-start(bf16[256,2,4,128]{3,2,1,0:T(4,128)(2,1)} %copy.153), calls=%async_computation.2 | async-start | bytes 1048576 | tf_op jit(solution)/shard_map/all_to_all | solution.py:115
  89.6 0.8 copy.173
  91.1 0.9 fusion.11
  91.9 1.5 %fusion.3 = bf16[4,16,17,256]{3,1,2,0:T(8,128)(2,1)S(1)} fusion(bf16[3,3,256,256]{2,3,1,0:T(8,128)(2,1)S(1)} %reshape.81, bf16[256,6,2,8,19]{0,2,4,3,1:T(2,128)(2,1)S(1)} %fusion.11, pred[16,17]{0,1:T(8,128)(4,1)S(1)} %copy-done.5), kind=kOutput, calls=%fused_computation.18 | convolution fusion | flops 1284014080 | bytes 2670864 | tf_op jit(solution)/shard_map/conv_general_dilated | solution.py:52
  94.8 4.6 %collective-permute-done.6 = bf16[128,2,4,128]{0,2,3,1:T(4,128)(2,1)S(1)} collective-permute-done((bf16[128,2,4,128]{0,2,3,1:T(4,128)(2,1)S(1)}, bf16[128,2,4,128]{0,2,3,1:T(4,128)(2,1)S(1)}, u32[]{:S(2)}, u32[]{:S(2)}) %collective-permute-start.6) | collective-permute-done | bytes 262176 | tf_op jit(solution)/shard_map/ppermute | solution.py:36
  99.4 1.0 fusion.22
  101.0 1.1 %copy.165 = bf16[128,2,8,128]{3,2,1,0:T(8,128)(2,1)} copy(bf16[128,2,8,128]{3,0,2,1:T(8,128)(2,1)S(1)} %bitcast.91) | data formatting | bytes 1048576
  102.4 1.1 %copy.164 = bf16[64,2,16,128]{3,2,1,0:T(8,128)(2,1)} copy(bf16[64,2,16,128]{3,0,2,1:T(8,128)(2,1)S(1)} %bitcast.95) | data formatting | bytes 1048576
  (62 shorter events, 12.3 us)
Async XLA Ops:
  5.2 3.0 %copy-start = (bf16[64,2,16,128]{3,2,1,0:T(8,128)(2,1)S(1)}, bf16[64,2,16,128]{3,2,1,0:T(8,128)(2,1)}, u32[]{:S(2)}) copy-start(bf16[64,2,16,128]{3,2,1,0:T(8,128)(2,1)} %param.10) | copy-start | bytes 1572868
  8.7 2.3 %copy-start.3 = (bf16[3,3,128,64]{2,3,1,0:T(8,128)(2,1)S(1)}, bf16[3,3,128,64]{2,3,1,0:T(8,128)(2,1)}, u32[]{:S(2)}) copy-start(bf16[3,3,128,64]{2,3,1,0:T(8,128)(2,1)} %param.8) | copy-start | bytes 442372
  8.8 7.8 %copy-start.4 = (s32[2,4]{1,0:T(2,128)S(1)}, s32[2,4]{1,0:T(2,128)}, u32[]{:S(2)}) copy-start(s32[2,4]{1,0:T(2,128)} %constant.135.clone) | copy-start | bytes 100
  8.9 16.6 %collective-permute-start = (bf16[128,2,10,128]{3,0,2,1:T(8,128)(2,1)S(1)}, bf16[128,2,10,128]{3,0,2,1:T(8,128)(2,1)S(1)}, u32[]{:S(2)}, u32[]{:S(2)}) collective-permute-start(bf16[128,2,10,128]{3,0,2,1:T(8,128)(2,1)S(1)} %pad_maximum_fusion.1), channel_id=1, source_target_pairs={{0,4},{4,0},{1,5},{5,1},{2,6},{6,2},{3,7},{7,3},{8,12},{12,8},{9,1... | collective-permute-start | bytes 1966088 | tf_op jit(solution)/shard_map/ppermute | solution.py:186
  12.0 20.0 %all-to-all-start = ((bf16[4,3,3,128,64]{3,4,2,1,0:T(8,128)(2,1)}), bf16[4,3,3,128,64]{3,4,2,1,0:T(8,128)(2,1)S(1)}, u32[]{:S(2)}, u32[]{:S(2)}) async-start(bf16[4,3,3,128,64]{3,4,2,1,0:T(8,128)(2,1)} %broadcast_in_dim.31), calls=%async_computation | async-start | bytes 1179648 | tf_op jit(solution)/shard_map/all_to_all | solution.py:78
  32.0 17.4 %all-to-all-start.1 = ((bf16[4,64,2,4,128]{4,1,3,2,0:T(8,128)(2,1)}), bf16[4,64,2,4,128]{4,1,3,2,0:T(8,128)(2,1)S(1)}, u32[]{:S(2)}, u32[]{:S(2)}) async-start(bf16[4,64,2,4,128]{4,1,3,2,0:T(8,128)(2,1)} %broadcast_select_fusion), calls=%async_computation.1 | async-start | bytes 1048576 | tf_op jit(solution)/shard_map/all_to_all | solution.py:156
  35.4 14.3 %collective-permute-start.1 = (bf16[1,4,3,3,128,64]{4,5,3,2,1,0:T(8,128)(2,1)S(1)}, bf16[1,4,3,3,128,64]{4,5,3,2,1,0:T(8,128)(2,1)}, u32[]{:S(2)}, u32[]{:S(2)}) collective-permute-start(bf16[1,4,3,3,128,64]{4,5,3,2,1,0:T(8,128)(2,1)S(1)} %bitcast.86), channel_id=1, source_target_pairs={{0,4},{4,0},{1,5},{5,1},{2,6},{6,2},{3,7},{7,3},{8,12},{12,8},{9,1... | collective-permute-start | bytes 1769480 | tf_op jit(solution)/shard_map/ppermute | solution.py:25
  51.7 2.0 %copy-start.5 = (pred[16,17]{0,1:T(8,128)(4,1)S(1)}, pred[16,17]{0,1:T(8,128)(4,1)}, u32[]{:S(2)}) copy-start(pred[16,17]{0,1:T(8,128)(4,1)} %constant.155) | copy-start | bytes 820
  57.3 10.7 %collective-permute-start.2 = (bf16[512,1,4,128]{0,2,3,1:T(4,128)(2,1)S(1)}, bf16[512,1,4,128]{0,2,3,1:T(4,128)(2,1)}, u32[]{:S(2)}, u32[]{:S(2)}) collective-permute-start(bf16[512,1,4,128]{0,2,3,1:T(4,128)(2,1)S(1)} %get-tuple-element.16), channel_id=1, source_target_pairs={{0,8},{8,16},{16,24},{1,9},{9,17},{17,25},{2,10},{10,18},{18,26},{... | collective-permute-start | bytes 1572872 | tf_op jit(solution)/shard_map/ppermute | solution.py:46
  61.9 10.6 %collective-permute-start.3 = (bf16[512,1,4,128]{0,2,3,1:T(4,128)(2,1)S(1)}, bf16[512,1,4,128]{0,2,3,1:T(4,128)(2,1)}, u32[]{:S(2)}, u32[]{:S(2)}) collective-permute-start(bf16[512,1,4,128]{0,2,3,1:T(4,128)(2,1)S(1)} %get-tuple-element.17), channel_id=1, source_target_pairs={{8,0},{16,8},{24,16},{9,1},{17,9},{25,17},{10,2},{18,10},{26,18},{... | collective-permute-start | bytes 1572872 | tf_op jit(solution)/shard_map/ppermute | solution.py:47
  74.6 1.0 copy-start.2
  75.6 5.4 %copy-start.1 = (bf16[3,256,256]{2,1,0:T(8,128)(2,1)S(1)}, bf16[3,256,256]{2,1,0:T(8,128)(2,1)}, u32[]{:S(2)}) copy-start(bf16[3,256,256]{2,1,0:T(8,128)(2,1)} %param.9) | copy-start | bytes 1179652
  77.1 12.4 %collective-permute-start.4 = (bf16[256,2,1,128]{0,3,2,1:T(8,128)(2,1)S(1)}, bf16[256,2,1,128]{0,3,2,1:T(8,128)(2,1)S(1)}, u32[]{:S(2)}, u32[]{:S(2)}) collective-permute-start(bf16[256,2,1,128]{0,3,2,1:T(8,128)(2,1)S(1)} %get-tuple-element.20), channel_id=1, source_target_pairs={{0,4},{4,5},{5,1},{1,2},{2,6},{6,7},{7,3},{8,12},{12,13},{13,9},{9... | collective-permute-start | bytes 393224 | tf_op jit(solution)/shard_map/ppermute | solution.py:46
  79.7 9.8 %collective-permute-start.5 = (bf16[256,2,1,128]{0,3,2,1:T(8,128)(2,1)S(1)}, bf16[256,2,1,128]{0,3,2,1:T(8,128)(2,1)S(1)}, u32[]{:S(2)}, u32[]{:S(2)}) collective-permute-start(bf16[256,2,1,128]{0,3,2,1:T(8,128)(2,1)S(1)} %get-tuple-element.21), channel_id=1, source_target_pairs={{4,0},{5,4},{1,5},{2,1},{6,2},{7,6},{3,7},{12,8},{13,12},{9,13},{1... | collective-permute-start | bytes 393224 | tf_op jit(solution)/shard_map/ppermute | solution.py:47
  83.6 18.5 %all-to-all-start.2 = ((bf16[256,2,4,128]{3,2,1,0:T(4,128)(2,1)}), bf16[256,2,4,128]{3,2,1,0:T(4,128)(2,1)S(1)}, u32[]{:S(2)}, u32[]{:S(2)}) async-start(bf16[256,2,4,128]{3,2,1,0:T(4,128)(2,1)} %copy.153), calls=%async_computation.2 | async-start | bytes 1048576 | tf_op jit(solution)/shard_map/all_to_all | solution.py:115
  94.1 5.3 %collective-permute-start.6 = (bf16[128,2,4,128]{0,2,3,1:T(4,128)(2,1)S(1)}, bf16[128,2,4,128]{0,2,3,1:T(4,128)(2,1)S(1)}, u32[]{:S(2)}, u32[]{:S(2)}) collective-permute-start(bf16[128,2,4,128]{0,2,3,1:T(4,128)(2,1)S(1)} %get-tuple-element.19), channel_id=1, source_target_pairs={{0,4},{4,0},{1,5},{5,1},{2,6},{6,2},{3,7},{7,3},{8,12},{12,8},{9,1... | collective-permute-start | bytes 786440 | tf_op jit(solution)/shard_map/ppermute | solution.py:36

commit v13 on v11

--- a/solution.py
+++ b/solution.py
@@ -97,7 +97,7 @@
     filt = lax.axis_index("filt")
     rows = volume.shape[2] // (chans * filts)
     padded = jnp.pad(volume, ((0, 0), (0, 0), (1, 1), (0, 0)))
-    window = lambda c: lax.dynamic_slice_in_dim(padded, (c * filts + sub_block(c, filt, filts)) * rows, rows + 2, 2)
+    window = lambda c: lax.dynamic_slice_in_dim(padded, (c * filts + filt) * rows, rows + 2, 2)
     pieces = [window(chan)]
     for k in range(1, chans):
         pieces.append(lax.ppermute(window((chan + k) % chans), "chan", shift_pairs(chans, k)))
@@ -111,10 +111,7 @@
     chan = lax.axis_index("chan")
     rows = deep.shape[2]
     out = depth_conv(deep, depth_weight, "DHWOI").astype(jnp.bfloat16)
-    got = lax.all_to_all(out, "filt", 0, 2, tiled=True)
-    split = got.reshape(got.shape[:2] + (filts, rows) + got.shape[3:])
-    flipped = jnp.where(chan % 2 == 0, split, split[:, :, ::-1])
-    return flipped.reshape(got.shape)
+    return lax.all_to_all(out, "filt", 0, 2, tiled=True)
 
 
 def backward(grad_out, weight, depth_weight):
@@ -156,10 +153,16 @@
     grad_mid = depth_conv(deep, depth_weight[::-1], "DHWIO").astype(jnp.bfloat16)
     rimmed = halo(grad_mid, ROWS, 2, place)
     grad_in = plane_conv(rimmed, weight[::-1, ::-1], "HWOI").astype(jnp.bfloat16)
-    got = scatter_blocks(grad_in, "chan", 0, 2)
-    split = got.reshape(got.shape[:2] + (chans, rows) + got.shape[3:])
-    flipped = jnp.where(filt % 2 == 0, split, split[:, :, ::-1])
-    return flipped.reshape(got.shape)
+    chan = lax.axis_index("chan")
+    c_loc = grad_in.shape[0] // chans
+    even = filt % 2 == 0
+    pieces = [lax.dynamic_slice_in_dim(grad_in, chan * c_loc, c_loc, 0)]
+    for k in range(1, chans):
+        target = jnp.where(even, (chan + k) % chans, (chan - k) % chans)
+        pairs = [(c * filts + f, (((c + k) if f % 2 == 0 else (c - k)) % chans) * filts + f)
+                 for c in range(chans) for f in range(filts)]
+        pieces.append(lax.ppermute(lax.dynamic_slice_in_dim(grad_in, target * c_loc, c_loc, 0), ROWS, pairs))
+    return order_blocks(pieces, jnp.where(even, chan, chans - 1 - chan), 2)
 
 
 def local(volume, plane_weight, depth_weight, grad_out):

time: 98.4 us -> 97.6 us (level)
  no operation moved by 1% of the time
where the time goes in v13:
time: 97.6 us; the launch traced here: 97 us
  waiting for transfers between devices  27.4 us (28%)
  starting transfers between devices  27.3 us (28%)
  local copies, waits for them, and re-layouts  19.2 us (20%)
  other arithmetic  12.4 us (13%)
  matrix products  6.95 us (7%)
  between operations  3.78 us (4%)
    ppermute x2, starting transfers between devices, halo(): lax.ppermute(lax.slice_in_dim(x, length - 1, length, axis=dim), axis, up)  6.7 us
    all_to_all x1, waiting for transfers between devices, backward(): all_filters = lax.all_to_all(blocks, 'filt', 0, 0, tiled=True)  6.58 us
    all_to_all x1, starting transfers between devices, forward_out(): return lax.all_to_all(out, 'filt', 0, 2, tiled=True)  6.32 us
    ppermute x1, waiting for transfers between devices, backward(): lax.ppermute(send, 'chan', shift_pairs(chans, k))  6.27 us
    ppermute x1, waiting for transfers between devices, backward_in(): lax.ppermute(lax.dynamic_slice_in_dim(grad_in, target * c_loc, c_loc, 0),...  4.99 us
    unnamed x20, local copies, waits for them, and re-layouts  4.91 us
    ppermute x2, waiting for transfers between devices, halo(): after = lax.ppermute(lax.slice_in_dim(x, 0, 1, axis=dim), axis, down)  4.5 us
    all_to_all x1, starting transfers between devices, gather_weight(): by_filt = lax.all_to_all(spread, 'filt', 0, 0, tiled=True)  4.48 us
  transfers between devices with their start and end apart: 11, of which 6 were waited for; matrix products, arithmetic and copies ran while one was open for 24% of the time, Pallas kernels for 0%

profile of v13, /device:TPU:1, one launch (start us, length us, event | category | flops | bytes accessed | tf_op | source)
XLA Modules:
  0.0 97.0 jit_solution(17733253368688572047)
XLA Ops:
  0.7 2.3 %pad_dynamic-slice_fusion = (bf16[128,2,6,128]{3,2,1,0:T(8,128)(2,1)S(1)}, bf16[128,2,6,128]{3,2,1,0:T(8,128)(2,1)S(1)}) fusion(s32[]{:T(128)S(6)} %select_n.104, bf16[128,2,32,128]{3,2,1,0:T(8,128)(2,1)} %param.7, s32[]{:T(128)S(6)} %select_n.103), kind=kLoop, calls=%fused_computation.1 | loop fusion | bytes 2883592 | tf_op jit(solution)/shard_map/dynamic_slice | solution.py:100
  3.0 2.1 %collective-permute-start = (bf16[128,2,6,128]{3,2,1,0:T(8,128)(2,1)S(1)}, bf16[128,2,6,128]{3,2,1,0:T(8,128)(2,1)S(1)}, u32[]{:S(2)}, u32[]{:S(2)}) collective-permute-start(bf16[128,2,6,128]{3,2,1,0:T(8,128)(2,1)S(1)} %get-tuple-element.11), channel_id=1, source_target_pairs={{0,4},{4,0},{1,5},{5,1},{2,6},{6,2},{3,7},{7,3},{8,12},{12,8},{9,1... | collective-permute-start | bytes 1179656 | tf_op jit(solution)/shard_map/ppermute | solution.py:103
  5.1 1.0 broadcast_in_dim.31
  6.1 4.5 %all-to-all-start = ((bf16[4,3,3,128,64]{3,4,2,1,0:T(8,128)(2,1)}), bf16[4,3,3,128,64]{3,4,2,1,0:T(8,128)(2,1)S(1)}, u32[]{:S(2)}, u32[]{:S(2)}) async-start(bf16[4,3,3,128,64]{3,4,2,1,0:T(8,128)(2,1)} %broadcast_in_dim.31), calls=%async_computation | async-start | bytes 1179648 | tf_op jit(solution)/shard_map/all_to_all | solution.py:78
  15.2 6.3 %collective-permute-done.2 = bf16[2,64,2,4,128]{4,1,3,2,0:T(8,128)(2,1)S(1)} collective-permute-done((bf16[2,64,2,4,128]{4,1,3,2,0:T(8,128)(2,1)S(1)}, bf16[2,64,2,4,128]{4,1,3,2,0:T(8,128)(2,1)S(1)}, u32[]{:S(2)}, u32[]{:S(2)}) %collective-permute-start.2) | collective-permute-done | bytes 262176 | tf_op jit(solution)/shard_map/ppermute | solution.py:133
  22.2 0.9 broadcast_select_fusion
  23.1 2.9 %all-to-all-done = bf16[4,3,3,128,64]{3,4,2,1,0:T(8,128)(2,1)S(1)} async-done(((bf16[4,3,3,128,64]{3,4,2,1,0:T(8,128)(2,1)}), bf16[4,3,3,128,64]{3,4,2,1,0:T(8,128)(2,1)S(1)}, u32[]{:S(2)}, u32[]{:S(2)}) %all-to-all-start) | async-done | bytes 589856 | tf_op jit(solution)/shard_map/all_to_all | solution.py:78
  25.9 3.5 %all-to-all-start.1 = ((bf16[4,64,2,4,128]{4,1,3,2,0:T(8,128)(2,1)}), bf16[4,64,2,4,128]{4,1,3,2,0:T(8,128)(2,1)S(1)}, u32[]{:S(2)}, u32[]{:S(2)}) async-start(bf16[4,64,2,4,128]{4,1,3,2,0:T(8,128)(2,1)} %broadcast_select_fusion), calls=%async_computation.1 | async-start | bytes 1048576 | tf_op jit(solution)/shard_map/all_to_all | solution.py:142
  29.7 3.4 %fusion.11 = bf16[256,6,2,128]{3,1,2,0:T(8,128)(2,1)S(1)} fusion(s32[]{:T(128)S(6)} %select_n.106, bf16[128,2,6,128]{3,2,1,0:T(8,128)(2,1)S(1)} %collective-permute-done, bf16[128,2,6,128]{3,2,1,0:T(8,128)(2,1)S(1)} %get-tuple-element.10), kind=kLoop, calls=%fused_computation.28 | loop fusion | flops 1179648 | bytes 1572868 | tf_op jit(solution)/shard_map/jit(_roll_dynamic)/dynamic_slice | solution.py:19
  33.1 1.3 %copy.85 = bf16[256,6,2,128]{0,2,3,1:T(2,128)(2,1)S(1)} copy(bf16[256,6,2,128]{3,1,2,0:T(8,128)(2,1)S(1)} %fusion.11) | data formatting | bytes 1572864
  35.1 1.7 %fusion.14 = bf16[256,6,2,8,19]{0,2,4,3,1:T(2,128)(2,1)} fusion(bf16[256,6,2,7,2]{0,2,4,3,1:T(2,128)(2,1)S(1)} %slice.52, bf16[256,6,2,8,17]{0,2,4,3,1:T(2,128)(2,1)S(1)} %bitcast.79), kind=kLoop, calls=%fused_computation.37 | loop fusion | flops 2801664 | bytes 1855488 | tf_op jit(solution)/shard_map/conv_general_dilated | solution.py:52
  36.8 6.6 %all-to-all-done.1 = bf16[4,64,2,4,128]{4,1,3,2,0:T(8,128)(2,1)S(1)} async-done(((bf16[4,64,2,4,128]{4,1,3,2,0:T(8,128)(2,1)}), bf16[4,64,2,4,128]{4,1,3,2,0:T(8,128)(2,1)S(1)}, u32[]{:S(2)}, u32[]{:S(2)}) %all-to-all-start.1) | async-done | bytes 524320 | tf_op jit(solution)/shard_map/all_to_all | solution.py:142
  43.7 1.9 %fusion.7 = bf16[3,3,2,128,4,64]{3,5,1,0,4,2:T(8,128)(2,1)S(1)} fusion(s32[]{:T(128)S(6)} %select_n.107, bf16[1,4,3,3,128,64]{4,5,3,2,1,0:T(8,128)(2,1)} %collective-permute-done.1, bf16[1,4,3,3,128,64]{4,5,3,2,1,0:T(8,128)(2,1)S(1)} %bitcast.83), kind=kLoop, calls=%fused_computation.24 | loop fusion | flops 1769472 | bytes 2359300 | tf_op jit(solution)/shard_map/transpose | solution.py:81
  45.6 1.2 %copy.57 = bf16[3,3,2,128,4,64]{3,2,5,4,1,0:T(2,128)(2,1)S(1)} copy(bf16[3,3,2,128,4,64]{3,5,1,0,4,2:T(8,128)(2,1)S(1)} %fusion.7) | data formatting | bytes 2359296 | tf_op jit(solution)/shard_map/transpose | solution.py:81
  47.7 2.7 %fusion.2 = bf16[4,16,17,256]{3,1,2,0:T(8,128)(2,1)S(1)} fusion(bf16[3,3,256,256]{2,3,1,0:T(8,128)(2,1)S(1)} %reshape.63, bf16[256,6,2,8,19]{0,2,4,3,1:T(2,128)(2,1)} %fusion.14, pred[16,17]{0,1:T(8,128)(4,1)S(1)} %copy-done.7), kind=kOutput, calls=%fused_computation.17 | convolution fusion | flops 1284014080 | bytes 2670864 | tf_op jit(solution)/shard_map/conv_general_dilated | solution.py:52
  51.3 4.6 %collective-permute-start.3 = (bf16[512,1,4,128]{0,2,3,1:T(4,128)(2,1)S(1)}, bf16[512,1,4,128]{0,2,3,1:T(4,128)(2,1)}, u32[]{:S(2)}, u32[]{:S(2)}) collective-permute-start(bf16[512,1,4,128]{0,2,3,1:T(4,128)(2,1)S(1)} %get-tuple-element.12), channel_id=1, source_target_pairs={{0,8},{8,16},{16,24},{1,9},{9,17},{17,25},{2,10},{10,18},{18,26},{... | collective-permute-start | bytes 1572872 | tf_op jit(solution)/shard_map/ppermute | solution.py:46
  55.9 2.1 %collective-permute-start.4 = (bf16[512,1,4,128]{0,2,3,1:T(4,128)(2,1)S(1)}, bf16[512,1,4,128]{0,2,3,1:T(4,128)(2,1)}, u32[]{:S(2)}, u32[]{:S(2)}) collective-permute-start(bf16[512,1,4,128]{0,2,3,1:T(4,128)(2,1)S(1)} %get-tuple-element.13), channel_id=1, source_target_pairs={{8,0},{16,8},{24,16},{9,1},{17,9},{25,17},{10,2},{18,10},{26,18},{... | collective-permute-start | bytes 1572872 | tf_op jit(solution)/shard_map/ppermute | solution.py:47
  58.1 1.8 %rev.4 = bf16[3,256,256]{2,1,0:T(8,128)(2,1)} reverse(bf16[3,256,256]{2,1,0:T(8,128)(2,1)} %param.9), dimensions={0} | reverse | bytes 786432 | tf_op jit(solution)/shard_map/rev | solution.py:153
  59.8 2.2 %collective-permute-done.3 = bf16[512,1,4,128]{0,2,3,1:T(4,128)(2,1)} collective-permute-done((bf16[512,1,4,128]{0,2,3,1:T(4,128)(2,1)S(1)}, bf16[512,1,4,128]{0,2,3,1:T(4,128)(2,1)}, u32[]{:S(2)}, u32[]{:S(2)}) %collective-permute-start.3) | collective-permute-done | bytes 524320 | tf_op jit(solution)/shard_map/ppermute | solution.py:46
  62.0 4.5 %collective-permute-done.4 = bf16[512,1,4,128]{0,2,3,1:T(4,128)(2,1)} collective-permute-done((bf16[512,1,4,128]{0,2,3,1:T(4,128)(2,1)S(1)}, bf16[512,1,4,128]{0,2,3,1:T(4,128)(2,1)}, u32[]{:S(2)}, u32[]{:S(2)}) %collective-permute-start.4) | collective-permute-done | bytes 524320 | tf_op jit(solution)/shard_map/ppermute | solution.py:47
  66.5 2.0 %pad_maximum_fusion = bf16[512,4,4,128]{0,2,3,1:T(4,128)(2,1)S(1)} fusion(bf16[512,1,4,128]{0,2,3,1:T(4,128)(2,1)} %collective-permute-done.4, bf16[256,2,4,128]{0,2,3,1:T(4,128)(2,1)S(1)} %copy.64, bf16[256,2,4,128]{0,2,3,1:T(4,128)(2,1)S(1)} %slice_bitcast_fusion, bf16[512,1,4,128]{0,2,3,1:T(4,128)(2,1)} %collective-permute-done.3), kind=kLoop, calls=%fused_computation.11 | loop fusion | flops 8388608 | bytes 4194304 | tf_op jit(solution)/shard_map/concatenate | solution.py:48
  69.5 1.4 %convolution_convert_fusion = bf16[2,4,8,16,256]{4,2,3,1,0:T(8,128)(2,1)S(1)} fusion(bf16[256,4,4,8,16]{0,2,4,3,1:T(4,128)(2,1)S(1)} %bitcast.91, bf16[3,256,256]{2,1,0:T(8,128)(2,1)S(1)} %copy-done.2), kind=kOutput, calls=%fused_computation.19 | convolution fusion | flops 402915328 | bytes 1966080 | tf_op jit(solution)/shard_map/conv_general_dilated | solution.py:63
  71.1 2.1 %collective-permute-start.5 = (bf16[256,2,1,128]{0,3,2,1:T(8,128)(2,1)S(1)}, bf16[256,2,1,128]{0,3,2,1:T(8,128)(2,1)S(1)}, u32[]{:S(2)}, u32[]{:S(2)}) collective-permute-start(bf16[256,2,1,128]{0,3,2,1:T(8,128)(2,1)S(1)} %get-tuple-element.16), channel_id=1, source_target_pairs={{0,4},{4,5},{5,1},{1,2},{2,6},{6,7},{7,3},{8,12},{12,13},{13,9},{9... | collective-permute-start | bytes 393224 | tf_op jit(solution)/shard_map/ppermute | solution.py:46
  73.2 1.3 %collective-permute-start.6 = (bf16[256,2,1,128]{0,3,2,1:T(8,128)(2,1)S(1)}, bf16[256,2,1,128]{0,3,2,1:T(8,128)(2,1)S(1)}, u32[]{:S(2)}, u32[]{:S(2)}) collective-permute-start(bf16[256,2,1,128]{0,3,2,1:T(8,128)(2,1)S(1)} %get-tuple-element.17), channel_id=1, source_target_pairs={{4,0},{5,4},{1,5},{2,1},{6,2},{7,6},{3,7},{12,8},{13,12},{9,13},{1... | collective-permute-start | bytes 393224 | tf_op jit(solution)/shard_map/ppermute | solution.py:47
  74.5 1.4 %convolution_convert_fusion.1 = bf16[2,4,8,16,256]{4,2,3,1,0:T(8,128)(2,1)S(1)} fusion(bf16[256,4,4,8,16]{0,2,4,3,1:T(4,128)(2,1)S(1)} %bitcast.90, bf16[3,256,256]{2,1,0:T(8,128)(2,1)S(1)} %copy-done.1), kind=kOutput, calls=%fused_computation.20 | convolution fusion | flops 402915328 | bytes 1966080 | tf_op jit(solution)/shard_map/conv_general_dilated | solution.py:63
  76.0 1.1 %copy.69 = bf16[256,2,4,128]{3,2,1,0:T(4,128)(2,1)} copy(bf16[256,2,4,128]{0,3,2,1:T(8,128)(2,1)S(1)} %bitcast.87) | data formatting | bytes 1048576 | tf_op jit(solution)/shard_map/convert_element_type | solution.py:113
  77.1 6.3 %all-to-all-start.2 = ((bf16[256,2,4,128]{3,2,1,0:T(4,128)(2,1)}), bf16[256,2,4,128]{3,2,1,0:T(4,128)(2,1)S(1)}, u32[]{:S(2)}, u32[]{:S(2)}) async-start(bf16[256,2,4,128]{3,2,1,0:T(4,128)(2,1)} %copy.69), calls=%async_computation.2 | async-start | bytes 1048576 | tf_op jit(solution)/shard_map/all_to_all | solution.py:114
  85.9 1.5 %fusion.3 = bf16[4,16,17,256]{3,1,2,0:T(8,128)(2,1)S(1)} fusion(bf16[3,3,256,256]{2,3,1,0:T(8,128)(2,1)S(1)} %reshape.63, bf16[256,6,2,8,19]{0,2,4,3,1:T(2,128)(2,1)S(1)} %fusion.15, pred[16,17]{0,1:T(8,128)(4,1)S(1)} %copy-done.7), kind=kOutput, calls=%fused_computation.18 | convolution fusion | flops 1284014080 | bytes 2670864 | tf_op jit(solution)/shard_map/conv_general_dilated | solution.py:52
  88.4 5.0 %collective-permute-done.7 = bf16[128,2,4,128]{0,2,3,1:T(4,128)(2,1)S(1)} collective-permute-done((bf16[128,2,4,128]{0,2,3,1:T(4,128)(2,1)S(1)}, bf16[128,2,4,128]{0,2,3,1:T(4,128)(2,1)S(1)}, u32[]{:S(2)}, u32[]{:S(2)}) %collective-permute-start.7) | collective-permute-done | bytes 262176 | tf_op jit(solution)/shard_map/ppermute | solution.py:164
  93.4 1.0 %fusion.22 = bf16[128,2,8,128]{0,2,3,1:T(8,128)(2,1)S(1)} fusion(s32[]{:T(128)S(6)} %select_n.123, bf16[128,2,4,128]{0,2,3,1:T(4,128)(2,1)S(1)} %collective-permute-done.7, bf16[128,2,4,128]{0,2,3,1:T(4,128)(2,1)S(1)} %get-tuple-element.14), kind=kLoop, calls=%fused_computation.46 | loop fusion | flops 2097152 | bytes 1048580 | tf_op jit(solution)/shard_map/jit(_roll_dynamic)/concatenate | solution.py:19
  94.4 1.3 %copy.80 = bf16[128,2,8,128]{3,2,1,0:T(8,128)(2,1)} copy(bf16[128,2,8,128]{0,2,3,1:T(8,128)(2,1)S(1)} %fusion.22) | data formatting | bytes 1048576
  95.8 1.1 %copy.79 = bf16[64,2,16,128]{3,2,1,0:T(8,128)(2,1)} copy(bf16[64,2,16,128]{3,0,2,1:T(8,128)(2,1)S(1)} %bitcast.89) | data formatting | bytes 1048576
  (60 shorter events, 10.4 us)
Async XLA Ops:
  0.6 4.5 %copy-start.3 = (bf16[3,3,128,64]{2,3,1,0:T(8,128)(2,1)S(1)}, bf16[3,3,128,64]{2,3,1,0:T(8,128)(2,1)}, u32[]{:S(2)}) copy-start(bf16[3,3,128,64]{2,3,1,0:T(8,128)(2,1)} %param.8) | copy-start | bytes 442372
  0.7 9.9 %copy-start.4 = (s32[2,2]{1,0:T(2,128)S(1)}, s32[2,2]{1,0:T(2,128)}, u32[]{:S(2)}) copy-start(s32[2,2]{1,0:T(2,128)} %constant.124.clone) | copy-start | bytes 52
  0.7 9.9 %copy-start.5 = (s32[2,2]{1,0:T(2,128)S(1)}, s32[2,2]{1,0:T(2,128)}, u32[]{:S(2)}) copy-start(s32[2,2]{1,0:T(2,128)} %constant.125.clone) | copy-start | bytes 52
  0.7 13.7 %copy-start = (bf16[64,2,16,128]{3,2,1,0:T(8,128)(2,1)S(1)}, bf16[64,2,16,128]{3,2,1,0:T(8,128)(2,1)}, u32[]{:S(2)}) copy-start(bf16[64,2,16,128]{3,2,1,0:T(8,128)(2,1)} %param.10) | copy-start | bytes 1572868
  3.0 12.1 %copy-start.6 = (s32[2,4]{1,0:T(2,128)S(1)}, s32[2,4]{1,0:T(2,128)}, u32[]{:S(2)}) copy-start(s32[2,4]{1,0:T(2,128)} %constant.126.clone) | copy-start | bytes 100
  3.0 26.7 %collective-permute-start = (bf16[128,2,6,128]{3,2,1,0:T(8,128)(2,1)S(1)}, bf16[128,2,6,128]{3,2,1,0:T(8,128)(2,1)S(1)}, u32[]{:S(2)}, u32[]{:S(2)}) collective-permute-start(bf16[128,2,6,128]{3,2,1,0:T(8,128)(2,1)S(1)} %get-tuple-element.11), channel_id=1, source_target_pairs={{0,4},{4,0},{1,5},{5,1},{2,6},{6,2},{3,7},{7,3},{8,12},{12,8},{9,1... | collective-permute-start | bytes 1179656 | tf_op jit(solution)/shard_map/ppermute | solution.py:103
  6.1 19.9 %all-to-all-start = ((bf16[4,3,3,128,64]{3,4,2,1,0:T(8,128)(2,1)}), bf16[4,3,3,128,64]{3,4,2,1,0:T(8,128)(2,1)S(1)}, u32[]{:S(2)}, u32[]{:S(2)}) async-start(bf16[4,3,3,128,64]{3,4,2,1,0:T(8,128)(2,1)} %broadcast_in_dim.31), calls=%async_computation | async-start | bytes 1179648 | tf_op jit(solution)/shard_map/all_to_all | solution.py:78
  14.8 6.6 %collective-permute-start.2 = (bf16[2,64,2,4,128]{4,1,3,2,0:T(8,128)(2,1)S(1)}, bf16[2,64,2,4,128]{4,1,3,2,0:T(8,128)(2,1)S(1)}, u32[]{:S(2)}, u32[]{:S(2)}) collective-permute-start(bf16[2,64,2,4,128]{4,1,3,2,0:T(8,128)(2,1)S(1)} %pad_maximum_fusion.3), channel_id=1, source_target_pairs={{0,4},{4,0},{1,5},{5,1},{2,6},{6,2},{3,7},{7,3},{8,12},{12,8},{9,1... | collective-permute-start | bytes 786440 | tf_op jit(solution)/shard_map/ppermute | solution.py:133
  25.9 17.4 %all-to-all-start.1 = ((bf16[4,64,2,4,128]{4,1,3,2,0:T(8,128)(2,1)}), bf16[4,64,2,4,128]{4,1,3,2,0:T(8,128)(2,1)S(1)}, u32[]{:S(2)}, u32[]{:S(2)}) async-start(bf16[4,64,2,4,128]{4,1,3,2,0:T(8,128)(2,1)} %broadcast_select_fusion), calls=%async_computation.1 | async-start | bytes 1048576 | tf_op jit(solution)/shard_map/all_to_all | solution.py:142
  29.4 14.3 %collective-permute-start.1 = (bf16[1,4,3,3,128,64]{4,5,3,2,1,0:T(8,128)(2,1)S(1)}, bf16[1,4,3,3,128,64]{4,5,3,2,1,0:T(8,128)(2,1)}, u32[]{:S(2)}, u32[]{:S(2)}) collective-permute-start(bf16[1,4,3,3,128,64]{4,5,3,2,1,0:T(8,128)(2,1)S(1)} %bitcast.82), channel_id=1, source_target_pairs={{0,4},{4,0},{1,5},{5,1},{2,6},{6,2},{3,7},{7,3},{8,12},{12,8},{9,1... | collective-permute-start | bytes 1769480 | tf_op jit(solution)/shard_map/ppermute | solution.py:25
  45.6 2.0 %copy-start.7 = (pred[16,17]{0,1:T(8,128)(4,1)S(1)}, pred[16,17]{0,1:T(8,128)(4,1)}, u32[]{:S(2)}) copy-start(pred[16,17]{0,1:T(8,128)(4,1)} %constant.146) | copy-start | bytes 820
  51.3 10.7 %collective-permute-start.3 = (bf16[512,1,4,128]{0,2,3,1:T(4,128)(2,1)S(1)}, bf16[512,1,4,128]{0,2,3,1:T(4,128)(2,1)}, u32[]{:S(2)}, u32[]{:S(2)}) collective-permute-start(bf16[512,1,4,128]{0,2,3,1:T(4,128)(2,1)S(1)} %get-tuple-element.12), channel_id=1, source_target_pairs={{0,8},{8,16},{16,24},{1,9},{9,17},{17,25},{2,10},{10,18},{18,26},{... | collective-permute-start | bytes 1572872 | tf_op jit(solution)/shard_map/ppermute | solution.py:46
  55.9 10.6 %collective-permute-start.4 = (bf16[512,1,4,128]{0,2,3,1:T(4,128)(2,1)S(1)}, bf16[512,1,4,128]{0,2,3,1:T(4,128)(2,1)}, u32[]{:S(2)}, u32[]{:S(2)}) collective-permute-start(bf16[512,1,4,128]{0,2,3,1:T(4,128)(2,1)S(1)} %get-tuple-element.13), channel_id=1, source_target_pairs={{8,0},{16,8},{24,16},{9,1},{17,9},{25,17},{10,2},{18,10},{26,18},{... | collective-permute-start | bytes 1572872 | tf_op jit(solution)/shard_map/ppermute | solution.py:47
  68.5 1.0 %copy-start.2 = (bf16[3,256,256]{2,1,0:T(8,128)(2,1)S(1)}, bf16[3,256,256]{2,1,0:T(8,128)(2,1)}, u32[]{:S(2)}) copy-start(bf16[3,256,256]{2,1,0:T(8,128)(2,1)} %rev.4) | copy-start | bytes 1179652
  69.5 4.9 %copy-start.1 = (bf16[3,256,256]{2,1,0:T(8,128)(2,1)S(1)}, bf16[3,256,256]{2,1,0:T(8,128)(2,1)}, u32[]{:S(2)}) copy-start(bf16[3,256,256]{2,1,0:T(8,128)(2,1)} %param.9) | copy-start | bytes 1179652
  71.1 12.3 %collective-permute-start.5 = (bf16[256,2,1,128]{0,3,2,1:T(8,128)(2,1)S(1)}, bf16[256,2,1,128]{0,3,2,1:T(8,128)(2,1)S(1)}, u32[]{:S(2)}, u32[]{:S(2)}) collective-permute-start(bf16[256,2,1,128]{0,3,2,1:T(8,128)(2,1)S(1)} %get-tuple-element.16), channel_id=1, source_target_pairs={{0,4},{4,5},{5,1},{1,2},{2,6},{6,7},{7,3},{8,12},{12,13},{13,9},{9... | collective-permute-start | bytes 393224 | tf_op jit(solution)/shard_map/ppermute | solution.py:46
  73.2 10.2 %collective-permute-start.6 = (bf16[256,2,1,128]{0,3,2,1:T(8,128)(2,1)S(1)}, bf16[256,2,1,128]{0,3,2,1:T(8,128)(2,1)S(1)}, u32[]{:S(2)}, u32[]{:S(2)}) collective-permute-start(bf16[256,2,1,128]{0,3,2,1:T(8,128)(2,1)S(1)} %get-tuple-element.17), channel_id=1, source_target_pairs={{4,0},{5,4},{1,5},{2,1},{6,2},{7,6},{3,7},{12,8},{13,12},{9,13},{1... | collective-permute-start | bytes 393224 | tf_op jit(solution)/shard_map/ppermute | solution.py:47
  77.1 18.7 %all-to-all-start.2 = ((bf16[256,2,4,128]{3,2,1,0:T(4,128)(2,1)}), bf16[256,2,4,128]{3,2,1,0:T(4,128)(2,1)S(1)}, u32[]{:S(2)}, u32[]{:S(2)}) async-start(bf16[256,2,4,128]{3,2,1,0:T(4,128)(2,1)} %copy.69), calls=%async_computation.2 | async-start | bytes 1048576 | tf_op jit(solution)/shard_map/all_to_all | solution.py:114
  88.1 5.3 %collective-permute-start.7 = (bf16[128,2,4,128]{0,2,3,1:T(4,128)(2,1)S(1)}, bf16[128,2,4,128]{0,2,3,1:T(4,128)(2,1)S(1)}, u32[]{:S(2)}, u32[]{:S(2)}) collective-permute-start(bf16[128,2,4,128]{0,2,3,1:T(4,128)(2,1)S(1)} %get-tuple-element.15), channel_id=1, source_target_pairs={{0,4},{1,5},{2,6},{3,7},{4,0},{5,1},{6,2},{7,3},{8,12},{9,13},{10,... | collective-permute-start | bytes 786440 | tf_op jit(solution)/shard_map/ppermute | solution.py:164

commit v14 on v13

--- a/solution.py
+++ b/solution.py
@@ -110,7 +110,10 @@
     filts = lax.axis_size("filt")
     chan = lax.axis_index("chan")
     rows = deep.shape[2]
-    out = depth_conv(deep, depth_weight, "DHWOI").astype(jnp.bfloat16)
+    return depth_conv(deep, depth_weight, "DHWOI").astype(jnp.bfloat16)
+
+
+def send_out(out):
     return lax.all_to_all(out, "filt", 0, 2, tiled=True)
 
 
@@ -152,7 +155,13 @@
     place = lambda g: turn(g // chans, g % chans) * filts + g // chans
     grad_mid = depth_conv(deep, depth_weight[::-1], "DHWIO").astype(jnp.bfloat16)
     rimmed = halo(grad_mid, ROWS, 2, place)
-    grad_in = plane_conv(rimmed, weight[::-1, ::-1], "HWOI").astype(jnp.bfloat16)
+    return plane_conv(rimmed, weight[::-1, ::-1], "HWOI").astype(jnp.bfloat16)
+
+
+def send_grad_in(grad_in):
+    chans = lax.axis_size("chan")
+    filts = lax.axis_size("filt")
+    filt = lax.axis_index("filt")
     chan = lax.axis_index("chan")
     c_loc = grad_in.shape[0] // chans
     even = filt % 2 == 0
@@ -172,7 +181,8 @@
     deep = halo(jnp.concatenate([mid, all_filters]), "slab", 1)
     output = forward_out(deep[: mid.shape[0]], depth_weight)
     grad_in = backward_in(deep[mid.shape[0] :], weight, depth_weight)
-    return (output, grad_in)
+    output, grad_in = lax.optimization_barrier((output, grad_in))
+    return (send_out(output), send_grad_in(grad_in))
 
 
 def solution(mesh):

time: 97.6 us -> 100 us (1.025)
  waiting for transfers between devices: 27.4 us -> 30.9 us
    ppermute x2, waiting for transfers between devices: 4.5 us -> 7.37 us  [halo(): after = lax.ppermute(lax.slice_in_dim(x, 0, 1, axis=dim), axis, down)]
    all_to_all x1, starting transfers between devices: 6.32 us -> 3.83 us  [send_out(): return lax.all_to_all(out, 'filt', 0, 2, tiled=True)]
    ppermute x1, starting transfers between devices: 0.3 us -> 1.94 us  [send_grad_in(): lax.ppermute(lax.dynamic_slice_in_dim(grad_in, target * c_loc, c_loc, 0),...]
    all_to_all x1, waiting for transfers between devices: 0.01 us -> 1.5 us  [send_out(): return lax.all_to_all(out, 'filt', 0, 2, tiled=True)]
    optimization_barrier x0 -> x1, local copies, waits for them, and re-layouts: none -> 1.08 us  [local(): output, grad_in = lax.optimization_barrier((output, grad_in))]
    convert_element_type x4 -> x3, local copies, waits for them, and re-layouts: 1.65 us -> 0.58 us  [the longest x2 0.47 us: backward_in(): return plane_conv(rimmed, weight[::-1, ::-1], 'HWOI').astype(jnp.bfloat16)]
  transfers between devices with their start and end apart: 11 -> 11, of which waited for: 6 -> 8; matrix products, arithmetic and copies ran while one was open for 24% -> 18% of each run, Pallas kernels for 0% -> 0%
where the time goes in v14:
time: 100 us; the launch traced here: 99.5 us
  waiting for transfers between devices  30.9 us (31%)
  starting transfers between devices  26.4 us (26%)
  local copies, waits for them, and re-layouts  19.2 us (19%)
  other arithmetic  12.4 us (12%)
  matrix products  6.95 us (7%)
  between operations  3.73 us (4%)
    ppermute x2, waiting for transfers between devices, halo(): after = lax.ppermute(lax.slice_in_dim(x, 0, 1, axis=dim), axis, down)  7.37 us
    ppermute x2, starting transfers between devices, halo(): lax.ppermute(lax.slice_in_dim(x, length - 1, length, axis=dim), axis, up)  6.7 us
    all_to_all x1, waiting for transfers between devices, backward(): all_filters = lax.all_to_all(blocks, 'filt', 0, 0, tiled=True)  6.58 us
    ppermute x1, waiting for transfers between devices, backward(): lax.ppermute(send, 'chan', shift_pairs(chans, k))  6.27 us
    unnamed x20, local copies, waits for them, and re-layouts  4.91 us
    all_to_all x1, starting transfers between devices, gather_weight(): by_filt = lax.all_to_all(spread, 'filt', 0, 0, tiled=True)  4.48 us
    conv_general_dilated x2, matrix products, plane_conv(): lax.conv_general_dilated(rows, weight, window_strides=(1, 1), padding=((0...  4.16 us
    ppermute x1, waiting for transfers between devices, send_grad_in(): lax.ppermute(lax.dynamic_slice_in_dim(grad_in, target * c_loc, c_loc, 0),...  4.06 us
  transfers between devices with their start and end apart: 11, of which 8 were waited for; matrix products, arithmetic and copies ran while one was open for 18% of the time, Pallas kernels for 0%

profile of v14, /device:TPU:1, one launch (start us, length us, event | category | flops | bytes accessed | tf_op | source)
XLA Modules:
  0.0 99.5 jit_solution(12951413792281194212)
XLA Ops:
  0.7 2.3 %pad_dynamic-slice_fusion = (bf16[128,2,6,128]{3,2,1,0:T(8,128)(2,1)S(1)}, bf16[128,2,6,128]{3,2,1,0:T(8,128)(2,1)S(1)}) fusion(s32[]{:T(128)S(6)} %select_n.104, bf16[128,2,32,128]{3,2,1,0:T(8,128)(2,1)} %param.7, s32[]{:T(128)S(6)} %select_n.103), kind=kLoop, calls=%fused_computation.1 | loop fusion | bytes 2883592 | tf_op jit(solution)/shard_map/dynamic_slice | solution.py:100
  3.0 2.1 %collective-permute-start = (bf16[128,2,6,128]{3,2,1,0:T(8,128)(2,1)S(1)}, bf16[128,2,6,128]{3,2,1,0:T(8,128)(2,1)S(1)}, u32[]{:S(2)}, u32[]{:S(2)}) collective-permute-start(bf16[128,2,6,128]{3,2,1,0:T(8,128)(2,1)S(1)} %get-tuple-element.15), channel_id=1, source_target_pairs={{0,4},{4,0},{1,5},{5,1},{2,6},{6,2},{3,7},{7,3},{8,12},{12,8},{9,1... | collective-permute-start | bytes 1179656 | tf_op jit(solution)/shard_map/ppermute | solution.py:103
  6.1 4.5 %all-to-all-start = ((bf16[4,3,3,128,64]{3,4,2,1,0:T(8,128)(2,1)}), bf16[4,3,3,128,64]{3,4,2,1,0:T(8,128)(2,1)S(1)}, u32[]{:S(2)}, u32[]{:S(2)}) async-start(bf16[4,3,3,128,64]{3,4,2,1,0:T(8,128)(2,1)} %broadcast_in_dim.31), calls=%async_computation | async-start | bytes 1179648 | tf_op jit(solution)/shard_map/all_to_all | solution.py:78
  15.2 6.3 %collective-permute-done.2 = bf16[2,64,2,4,128]{4,1,3,2,0:T(8,128)(2,1)S(1)} collective-permute-done((bf16[2,64,2,4,128]{4,1,3,2,0:T(8,128)(2,1)S(1)}, bf16[2,64,2,4,128]{4,1,3,2,0:T(8,128)(2,1)S(1)}, u32[]{:S(2)}, u32[]{:S(2)}) %collective-permute-start.2) | collective-permute-done | bytes 262176 | tf_op jit(solution)/shard_map/ppermute | solution.py:136
  23.1 2.9 %all-to-all-done = bf16[4,3,3,128,64]{3,4,2,1,0:T(8,128)(2,1)S(1)} async-done(((bf16[4,3,3,128,64]{3,4,2,1,0:T(8,128)(2,1)}), bf16[4,3,3,128,64]{3,4,2,1,0:T(8,128)(2,1)S(1)}, u32[]{:S(2)}, u32[]{:S(2)}) %all-to-all-start) | async-done | bytes 589856 | tf_op jit(solution)/shard_map/all_to_all | solution.py:78
  25.9 3.5 %all-to-all-start.1 = ((bf16[4,64,2,4,128]{4,1,3,2,0:T(8,128)(2,1)}), bf16[4,64,2,4,128]{4,1,3,2,0:T(8,128)(2,1)S(1)}, u32[]{:S(2)}, u32[]{:S(2)}) async-start(bf16[4,64,2,4,128]{4,1,3,2,0:T(8,128)(2,1)} %broadcast_select_fusion), calls=%async_computation.1 | async-start | bytes 1048576 | tf_op jit(solution)/shard_map/all_to_all | solution.py:145
  29.7 3.4 %fusion.11 = bf16[256,6,2,128]{3,1,2,0:T(8,128)(2,1)S(1)} fusion(s32[]{:T(128)S(6)} %select_n.106, bf16[128,2,6,128]{3,2,1,0:T(8,128)(2,1)S(1)} %collective-permute-done, bf16[128,2,6,128]{3,2,1,0:T(8,128)(2,1)S(1)} %get-tuple-element.14), kind=kLoop, calls=%fused_computation.28 | loop fusion | flops 1179648 | bytes 1572868 | tf_op jit(solution)/shard_map/jit(_roll_dynamic)/dynamic_slice | solution.py:19
  33.1 1.3 %copy.85 = bf16[256,6,2,128]{0,2,3,1:T(2,128)(2,1)S(1)} copy(bf16[256,6,2,128]{3,1,2,0:T(8,128)(2,1)S(1)} %fusion.11) | data formatting | bytes 1572864
  35.1 1.7 %fusion.14 = bf16[256,6,2,8,19]{0,2,4,3,1:T(2,128)(2,1)} fusion(bf16[256,6,2,7,2]{0,2,4,3,1:T(2,128)(2,1)S(1)} %slice.52, bf16[256,6,2,8,17]{0,2,4,3,1:T(2,128)(2,1)S(1)} %bitcast.77), kind=kLoop, calls=%fused_computation.37 | loop fusion | flops 2801664 | bytes 1855488 | tf_op jit(solution)/shard_map/conv_general_dilated | solution.py:52
  36.8 6.6 %all-to-all-done.1 = bf16[4,64,2,4,128]{4,1,3,2,0:T(8,128)(2,1)S(1)} async-done(((bf16[4,64,2,4,128]{4,1,3,2,0:T(8,128)(2,1)}), bf16[4,64,2,4,128]{4,1,3,2,0:T(8,128)(2,1)S(1)}, u32[]{:S(2)}, u32[]{:S(2)}) %all-to-all-start.1) | async-done | bytes 524320 | tf_op jit(solution)/shard_map/all_to_all | solution.py:145
  43.7 1.9 %fusion.7 = bf16[3,3,2,128,4,64]{3,5,1,0,4,2:T(8,128)(2,1)S(1)} fusion(s32[]{:T(128)S(6)} %select_n.107, bf16[1,4,3,3,128,64]{4,5,3,2,1,0:T(8,128)(2,1)} %collective-permute-done.1, bf16[1,4,3,3,128,64]{4,5,3,2,1,0:T(8,128)(2,1)S(1)} %bitcast.81), kind=kLoop, calls=%fused_computation.24 | loop fusion | flops 1769472 | bytes 2359300 | tf_op jit(solution)/shard_map/transpose | solution.py:81
  45.6 1.2 %copy.57 = bf16[3,3,2,128,4,64]{3,2,5,4,1,0:T(2,128)(2,1)S(1)} copy(bf16[3,3,2,128,4,64]{3,5,1,0,4,2:T(8,128)(2,1)S(1)} %fusion.7) | data formatting | bytes 2359296 | tf_op jit(solution)/shard_map/transpose | solution.py:81
  47.7 2.7 %fusion.2 = bf16[4,16,17,256]{3,1,2,0:T(8,128)(2,1)S(1)} fusion(bf16[3,3,256,256]{2,3,1,0:T(8,128)(2,1)S(1)} %reshape.63, bf16[256,6,2,8,19]{0,2,4,3,1:T(2,128)(2,1)} %fusion.14, pred[16,17]{0,1:T(8,128)(4,1)S(1)} %copy-done.7), kind=kOutput, calls=%fused_computation.17 | convolution fusion | flops 1284014080 | bytes 2670864 | tf_op jit(solution)/shard_map/conv_general_dilated | solution.py:52
  51.3 4.6 %collective-permute-start.3 = (bf16[512,1,4,128]{0,2,3,1:T(4,128)(2,1)S(1)}, bf16[512,1,4,128]{0,2,3,1:T(4,128)(2,1)}, u32[]{:S(2)}, u32[]{:S(2)}) collective-permute-start(bf16[512,1,4,128]{0,2,3,1:T(4,128)(2,1)S(1)} %get-tuple-element.16), channel_id=1, source_target_pairs={{0,8},{8,16},{16,24},{1,9},{9,17},{17,25},{2,10},{10,18},{18,26},{... | collective-permute-start | bytes 1572872 | tf_op jit(solution)/shard_map/ppermute | solution.py:46
  55.9 2.1 %collective-permute-start.4 = (bf16[512,1,4,128]{0,2,3,1:T(4,128)(2,1)S(1)}, bf16[512,1,4,128]{0,2,3,1:T(4,128)(2,1)}, u32[]{:S(2)}, u32[]{:S(2)}) collective-permute-start(bf16[512,1,4,128]{0,2,3,1:T(4,128)(2,1)S(1)} %get-tuple-element.17), channel_id=1, source_target_pairs={{8,0},{16,8},{24,16},{9,1},{17,9},{25,17},{10,2},{18,10},{26,18},{... | collective-permute-start | bytes 1572872 | tf_op jit(solution)/shard_map/ppermute | solution.py:47
  58.0 1.8 %rev.4 = bf16[3,256,256]{2,1,0:T(8,128)(2,1)} reverse(bf16[3,256,256]{2,1,0:T(8,128)(2,1)} %param.9), dimensions={0} | reverse | bytes 786432 | tf_op jit(solution)/shard_map/rev | solution.py:156
  59.8 2.2 %collective-permute-done.3 = bf16[512,1,4,128]{0,2,3,1:T(4,128)(2,1)} collective-permute-done((bf16[512,1,4,128]{0,2,3,1:T(4,128)(2,1)S(1)}, bf16[512,1,4,128]{0,2,3,1:T(4,128)(2,1)}, u32[]{:S(2)}, u32[]{:S(2)}) %collective-permute-start.3) | collective-permute-done | bytes 524320 | tf_op jit(solution)/shard_map/ppermute | solution.py:46
  62.0 4.5 %collective-permute-done.4 = bf16[512,1,4,128]{0,2,3,1:T(4,128)(2,1)} collective-permute-done((bf16[512,1,4,128]{0,2,3,1:T(4,128)(2,1)S(1)}, bf16[512,1,4,128]{0,2,3,1:T(4,128)(2,1)}, u32[]{:S(2)}, u32[]{:S(2)}) %collective-permute-start.4) | collective-permute-done | bytes 524320 | tf_op jit(solution)/shard_map/ppermute | solution.py:47
  66.5 2.0 %pad_maximum_fusion = bf16[512,4,4,128]{0,2,3,1:T(4,128)(2,1)S(1)} fusion(bf16[512,1,4,128]{0,2,3,1:T(4,128)(2,1)} %collective-permute-done.4, bf16[256,2,4,128]{0,2,3,1:T(4,128)(2,1)S(1)} %copy.64, bf16[256,2,4,128]{0,2,3,1:T(4,128)(2,1)S(1)} %slice_bitcast_fusion.1, bf16[512,1,4,128]{0,2,3,1:T(4,128)(2,1)} %collective-permute-done.3), kind=kLoop, calls=%fused_computation.11 | loop fusion | flops 8388608 | bytes 4194304 | tf_op jit(solution)/shard_map/concatenate | solution.py:48
  69.5 1.4 %convolution_convert_fusion = bf16[2,4,8,16,256]{4,2,3,1,0:T(8,128)(2,1)S(1)} fusion(bf16[256,4,4,8,16]{0,2,4,3,1:T(4,128)(2,1)S(1)} %bitcast.89, bf16[3,256,256]{2,1,0:T(8,128)(2,1)S(1)} %copy-done.2), kind=kOutput, calls=%fused_computation.19 | convolution fusion | flops 402915328 | bytes 1966080 | tf_op jit(solution)/shard_map/conv_general_dilated | solution.py:63
  71.1 2.1 %collective-permute-start.5 = (bf16[256,2,1,128]{0,3,2,1:T(8,128)(2,1)S(1)}, bf16[256,2,1,128]{0,3,2,1:T(8,128)(2,1)S(1)}, u32[]{:S(2)}, u32[]{:S(2)}) collective-permute-start(bf16[256,2,1,128]{0,3,2,1:T(8,128)(2,1)S(1)} %get-tuple-element.20), channel_id=1, source_target_pairs={{0,4},{4,5},{5,1},{1,2},{2,6},{6,7},{7,3},{8,12},{12,13},{13,9},{9... | collective-permute-start | bytes 393224 | tf_op jit(solution)/shard_map/ppermute | solution.py:46
  73.2 1.3 %collective-permute-start.6 = (bf16[256,2,1,128]{0,3,2,1:T(8,128)(2,1)S(1)}, bf16[256,2,1,128]{0,3,2,1:T(8,128)(2,1)S(1)}, u32[]{:S(2)}, u32[]{:S(2)}) collective-permute-start(bf16[256,2,1,128]{0,3,2,1:T(8,128)(2,1)S(1)} %get-tuple-element.21), channel_id=1, source_target_pairs={{4,0},{5,4},{1,5},{2,1},{6,2},{7,6},{3,7},{12,8},{13,12},{9,13},{1... | collective-permute-start | bytes 393224 | tf_op jit(solution)/shard_map/ppermute | solution.py:47
  74.5 1.4 %convolution_convert_fusion.1 = bf16[2,4,8,16,256]{4,2,3,1,0:T(8,128)(2,1)S(1)} fusion(bf16[256,4,4,8,16]{0,2,4,3,1:T(4,128)(2,1)S(1)} %bitcast.88, bf16[3,256,256]{2,1,0:T(8,128)(2,1)S(1)} %copy-done.1), kind=kOutput, calls=%fused_computation.20 | convolution fusion | flops 402915328 | bytes 1966080 | tf_op jit(solution)/shard_map/conv_general_dilated | solution.py:63
  76.0 2.9 %collective-permute-done.6 = bf16[256,2,1,128]{0,3,2,1:T(8,128)(2,1)S(1)} collective-permute-done((bf16[256,2,1,128]{0,3,2,1:T(8,128)(2,1)S(1)}, bf16[256,2,1,128]{0,3,2,1:T(8,128)(2,1)S(1)}, u32[]{:S(2)}, u32[]{:S(2)}) %collective-permute-start.6) | collective-permute-done | bytes 131104 | tf_op jit(solution)/shard_map/ppermute | solution.py:47
  81.4 1.5 %fusion.3 = bf16[4,16,17,256]{3,1,2,0:T(8,128)(2,1)S(1)} fusion(bf16[3,3,256,256]{2,3,1,0:T(8,128)(2,1)S(1)} %reshape.63, bf16[256,6,2,8,19]{0,2,4,3,1:T(2,128)(2,1)S(1)} %fusion.15, pred[16,17]{0,1:T(8,128)(4,1)S(1)} %copy-done.7), kind=kOutput, calls=%fused_computation.18 | convolution fusion | flops 1284014080 | bytes 2670864 | tf_op jit(solution)/shard_map/conv_general_dilated | solution.py:52
  83.3 1.1 %copy.76 = bf16[256,2,4,128]{3,2,1,0:T(4,128)(2,1)} copy(bf16[256,2,4,128]{0,3,2,1:T(8,128)(2,1)S(1)} %bitcast.84) | data formatting | bytes 1048576 | tf_op jit(solution)/shard_map/optimization_barrier | solution.py:184
  84.4 3.8 %all-to-all-start.2 = ((bf16[256,2,4,128]{3,2,1,0:T(4,128)(2,1)}), bf16[256,2,4,128]{3,2,1,0:T(4,128)(2,1)S(1)}, u32[]{:S(2)}, u32[]{:S(2)}) async-start(bf16[256,2,4,128]{3,2,1,0:T(4,128)(2,1)} %copy.76), calls=%async_computation.2 | async-start | bytes 1048576 | tf_op jit(solution)/shard_map/all_to_all | solution.py:117
  88.4 1.9 %collective-permute-start.7 = (bf16[128,2,4,128]{0,2,3,1:T(4,128)(2,1)S(1)}, bf16[128,2,4,128]{0,2,3,1:T(4,128)(2,1)S(1)}, u32[]{:S(2)}, u32[]{:S(2)}) collective-permute-start(bf16[128,2,4,128]{0,2,3,1:T(4,128)(2,1)S(1)} %get-tuple-element.19), channel_id=1, source_target_pairs={{0,4},{1,5},{2,6},{3,7},{4,0},{5,1},{6,2},{7,3},{8,12},{9,13},{10,... | collective-permute-start | bytes 786440 | tf_op jit(solution)/shard_map/ppermute | solution.py:173
  90.4 4.1 %collective-permute-done.7 = bf16[128,2,4,128]{0,2,3,1:T(4,128)(2,1)S(1)} collective-permute-done((bf16[128,2,4,128]{0,2,3,1:T(4,128)(2,1)S(1)}, bf16[128,2,4,128]{0,2,3,1:T(4,128)(2,1)S(1)}, u32[]{:S(2)}, u32[]{:S(2)}) %collective-permute-start.7) | collective-permute-done | bytes 262176 | tf_op jit(solution)/shard_map/ppermute | solution.py:173
  95.4 1.3 %copy.80 = bf16[128,2,8,128]{3,2,1,0:T(8,128)(2,1)} copy(bf16[128,2,8,128]{0,2,3,1:T(8,128)(2,1)S(1)} %fusion.22) | data formatting | bytes 1048576
  96.8 1.5 %all-to-all-done.2 = bf16[256,2,4,128]{3,2,1,0:T(4,128)(2,1)S(1)} async-done(((bf16[256,2,4,128]{3,2,1,0:T(4,128)(2,1)}), bf16[256,2,4,128]{3,2,1,0:T(4,128)(2,1)S(1)}, u32[]{:S(2)}, u32[]{:S(2)}) %all-to-all-start.2) | async-done | bytes 524320 | tf_op jit(solution)/shard_map/all_to_all | solution.py:117
  98.4 1.1 %copy.79 = bf16[64,2,16,128]{3,2,1,0:T(8,128)(2,1)} copy(bf16[64,2,16,128]{3,0,2,1:T(8,128)(2,1)S(1)} %bitcast.87) | data formatting | bytes 1048576
  (60 shorter events, 13.0 us)
Async XLA Ops:
  0.6 4.5 %copy-start.3 = (bf16[3,3,128,64]{2,3,1,0:T(8,128)(2,1)S(1)}, bf16[3,3,128,64]{2,3,1,0:T(8,128)(2,1)}, u32[]{:S(2)}) copy-start(bf16[3,3,128,64]{2,3,1,0:T(8,128)(2,1)} %param.8) | copy-start | bytes 442372
  0.7 9.9 %copy-start.4 = (s32[2,2]{1,0:T(2,128)S(1)}, s32[2,2]{1,0:T(2,128)}, u32[]{:S(2)}) copy-start(s32[2,2]{1,0:T(2,128)} %constant.124.clone) | copy-start | bytes 52
  0.7 9.9 %copy-start.5 = (s32[2,2]{1,0:T(2,128)S(1)}, s32[2,2]{1,0:T(2,128)}, u32[]{:S(2)}) copy-start(s32[2,2]{1,0:T(2,128)} %constant.125.clone) | copy-start | bytes 52
  0.7 13.7 %copy-start = (bf16[64,2,16,128]{3,2,1,0:T(8,128)(2,1)S(1)}, bf16[64,2,16,128]{3,2,1,0:T(8,128)(2,1)}, u32[]{:S(2)}) copy-start(bf16[64,2,16,128]{3,2,1,0:T(8,128)(2,1)} %param.10) | copy-start | bytes 1572868
  3.0 12.1 %copy-start.6 = (s32[2,4]{1,0:T(2,128)S(1)}, s32[2,4]{1,0:T(2,128)}, u32[]{:S(2)}) copy-start(s32[2,4]{1,0:T(2,128)} %constant.126.clone) | copy-start | bytes 100
  3.0 26.7 %collective-permute-start = (bf16[128,2,6,128]{3,2,1,0:T(8,128)(2,1)S(1)}, bf16[128,2,6,128]{3,2,1,0:T(8,128)(2,1)S(1)}, u32[]{:S(2)}, u32[]{:S(2)}) collective-permute-start(bf16[128,2,6,128]{3,2,1,0:T(8,128)(2,1)S(1)} %get-tuple-element.15), channel_id=1, source_target_pairs={{0,4},{4,0},{1,5},{5,1},{2,6},{6,2},{3,7},{7,3},{8,12},{12,8},{9,1... | collective-permute-start | bytes 1179656 | tf_op jit(solution)/shard_map/ppermute | solution.py:103
  6.1 19.9 %all-to-all-start = ((bf16[4,3,3,128,64]{3,4,2,1,0:T(8,128)(2,1)}), bf16[4,3,3,128,64]{3,4,2,1,0:T(8,128)(2,1)S(1)}, u32[]{:S(2)}, u32[]{:S(2)}) async-start(bf16[4,3,3,128,64]{3,4,2,1,0:T(8,128)(2,1)} %broadcast_in_dim.31), calls=%async_computation | async-start | bytes 1179648 | tf_op jit(solution)/shard_map/all_to_all | solution.py:78
  14.8 6.6 %collective-permute-start.2 = (bf16[2,64,2,4,128]{4,1,3,2,0:T(8,128)(2,1)S(1)}, bf16[2,64,2,4,128]{4,1,3,2,0:T(8,128)(2,1)S(1)}, u32[]{:S(2)}, u32[]{:S(2)}) collective-permute-start(bf16[2,64,2,4,128]{4,1,3,2,0:T(8,128)(2,1)S(1)} %pad_maximum_fusion.3), channel_id=1, source_target_pairs={{0,4},{4,0},{1,5},{5,1},{2,6},{6,2},{3,7},{7,3},{8,12},{12,8},{9,1... | collective-permute-start | bytes 786440 | tf_op jit(solution)/shard_map/ppermute | solution.py:136
  25.9 17.4 %all-to-all-start.1 = ((bf16[4,64,2,4,128]{4,1,3,2,0:T(8,128)(2,1)}), bf16[4,64,2,4,128]{4,1,3,2,0:T(8,128)(2,1)S(1)}, u32[]{:S(2)}, u32[]{:S(2)}) async-start(bf16[4,64,2,4,128]{4,1,3,2,0:T(8,128)(2,1)} %broadcast_select_fusion), calls=%async_computation.1 | async-start | bytes 1048576 | tf_op jit(solution)/shard_map/all_to_all | solution.py:145
  29.4 14.3 %collective-permute-start.1 = (bf16[1,4,3,3,128,64]{4,5,3,2,1,0:T(8,128)(2,1)S(1)}, bf16[1,4,3,3,128,64]{4,5,3,2,1,0:T(8,128)(2,1)}, u32[]{:S(2)}, u32[]{:S(2)}) collective-permute-start(bf16[1,4,3,3,128,64]{4,5,3,2,1,0:T(8,128)(2,1)S(1)} %bitcast.80), channel_id=1, source_target_pairs={{0,4},{4,0},{1,5},{5,1},{2,6},{6,2},{3,7},{7,3},{8,12},{12,8},{9,1... | collective-permute-start | bytes 1769480 | tf_op jit(solution)/shard_map/ppermute | solution.py:25
  45.6 2.0 %copy-start.7 = (pred[16,17]{0,1:T(8,128)(4,1)S(1)}, pred[16,17]{0,1:T(8,128)(4,1)}, u32[]{:S(2)}) copy-start(pred[16,17]{0,1:T(8,128)(4,1)} %constant.146) | copy-start | bytes 820
  51.3 10.7 %collective-permute-start.3 = (bf16[512,1,4,128]{0,2,3,1:T(4,128)(2,1)S(1)}, bf16[512,1,4,128]{0,2,3,1:T(4,128)(2,1)}, u32[]{:S(2)}, u32[]{:S(2)}) collective-permute-start(bf16[512,1,4,128]{0,2,3,1:T(4,128)(2,1)S(1)} %get-tuple-element.16), channel_id=1, source_target_pairs={{0,8},{8,16},{16,24},{1,9},{9,17},{17,25},{2,10},{10,18},{18,26},{... | collective-permute-start | bytes 1572872 | tf_op jit(solution)/shard_map/ppermute | solution.py:46
  55.9 10.6 %collective-permute-start.4 = (bf16[512,1,4,128]{0,2,3,1:T(4,128)(2,1)S(1)}, bf16[512,1,4,128]{0,2,3,1:T(4,128)(2,1)}, u32[]{:S(2)}, u32[]{:S(2)}) collective-permute-start(bf16[512,1,4,128]{0,2,3,1:T(4,128)(2,1)S(1)} %get-tuple-element.17), channel_id=1, source_target_pairs={{8,0},{16,8},{24,16},{9,1},{17,9},{25,17},{10,2},{18,10},{26,18},{... | collective-permute-start | bytes 1572872 | tf_op jit(solution)/shard_map/ppermute | solution.py:47
  68.5 1.0 %copy-start.2 = (bf16[3,256,256]{2,1,0:T(8,128)(2,1)S(1)}, bf16[3,256,256]{2,1,0:T(8,128)(2,1)}, u32[]{:S(2)}) copy-start(bf16[3,256,256]{2,1,0:T(8,128)(2,1)} %rev.4) | copy-start | bytes 1179652
  69.5 4.9 %copy-start.1 = (bf16[3,256,256]{2,1,0:T(8,128)(2,1)S(1)}, bf16[3,256,256]{2,1,0:T(8,128)(2,1)}, u32[]{:S(2)}) copy-start(bf16[3,256,256]{2,1,0:T(8,128)(2,1)} %param.9) | copy-start | bytes 1179652
  71.1 4.9 %collective-permute-start.5 = (bf16[256,2,1,128]{0,3,2,1:T(8,128)(2,1)S(1)}, bf16[256,2,1,128]{0,3,2,1:T(8,128)(2,1)S(1)}, u32[]{:S(2)}, u32[]{:S(2)}) collective-permute-start(bf16[256,2,1,128]{0,3,2,1:T(8,128)(2,1)S(1)} %get-tuple-element.20), channel_id=1, source_target_pairs={{0,4},{4,5},{5,1},{1,2},{2,6},{6,7},{7,3},{8,12},{12,13},{13,9},{9... | collective-permute-start | bytes 393224 | tf_op jit(solution)/shard_map/ppermute | solution.py:46
  73.2 5.7 %collective-permute-start.6 = (bf16[256,2,1,128]{0,3,2,1:T(8,128)(2,1)S(1)}, bf16[256,2,1,128]{0,3,2,1:T(8,128)(2,1)S(1)}, u32[]{:S(2)}, u32[]{:S(2)}) collective-permute-start(bf16[256,2,1,128]{0,3,2,1:T(8,128)(2,1)S(1)} %get-tuple-element.21), channel_id=1, source_target_pairs={{4,0},{5,4},{1,5},{2,1},{6,2},{7,6},{3,7},{12,8},{13,12},{9,13},{1... | collective-permute-start | bytes 393224 | tf_op jit(solution)/shard_map/ppermute | solution.py:47
  84.4 13.9 %all-to-all-start.2 = ((bf16[256,2,4,128]{3,2,1,0:T(4,128)(2,1)}), bf16[256,2,4,128]{3,2,1,0:T(4,128)(2,1)S(1)}, u32[]{:S(2)}, u32[]{:S(2)}) async-start(bf16[256,2,4,128]{3,2,1,0:T(4,128)(2,1)} %copy.76), calls=%async_computation.2 | async-start | bytes 1048576 | tf_op jit(solution)/shard_map/all_to_all | solution.py:117
  88.4 6.0 %collective-permute-start.7 = (bf16[128,2,4,128]{0,2,3,1:T(4,128)(2,1)S(1)}, bf16[128,2,4,128]{0,2,3,1:T(4,128)(2,1)S(1)}, u32[]{:S(2)}, u32[]{:S(2)}) collective-permute-start(bf16[128,2,4,128]{0,2,3,1:T(4,128)(2,1)S(1)} %get-tuple-element.19), channel_id=1, source_target_pairs={{0,4},{1,5},{2,6},{3,7},{4,0},{5,1},{6,2},{7,3},{8,12},{9,13},{10,... | collective-permute-start | bytes 786440 | tf_op jit(solution)/shard_map/ppermute | solution.py:173

commit v15 on v13

--- a/solution.py
+++ b/solution.py
@@ -73,13 +73,9 @@
 
 def gather_weight(weight):
     filts = lax.axis_size("filt")
-    chans = lax.axis_size("chan")
     spread = jnp.broadcast_to(weight[None], (filts,) + weight.shape)
-    by_filt = lax.all_to_all(spread, "filt", 0, 0, tiled=True)
-    both = gather_blocks(by_filt[None], "chan", 0)
-    c_loc, m_loc = weight.shape[2:]
-    whole = jnp.transpose(both, (2, 3, 0, 4, 1, 5))
-    return whole.reshape(3, 3, chans * c_loc, filts * m_loc)
+    by_filt = lax.all_to_all(spread, "filt", 0, 4, tiled=True)[0]
+    return gather_blocks(by_filt, "chan", 2)
 
 
 def sub_block(chan, filt, filts):

time: 97.6 us -> 94.8 us (0.971)
  local copies, waits for them, and re-layouts: 19.2 us -> 17.3 us
  matrix products: 6.95 us -> 5.77 us
  other arithmetic: 12.4 us -> 11.4 us
    concatenate x1 -> x2, other arithmetic: 1.03 us -> 2.95 us  [order_blocks(): return jnp.roll(stacked, (me + 1) * block, axis=dim)]
    transpose x1 -> x0, other arithmetic: 1.9 us -> none  [gather_weight(): whole = jnp.transpose(both, (2, 3, 0, 4, 1, 5))]
    transpose x1 -> x0, local copies, waits for them, and re-layouts: 1.22 us -> none  [gather_weight(): whole = jnp.transpose(both, (2, 3, 0, 4, 1, 5))]
    conv_general_dilated x2, matrix products: 4.16 us -> 2.98 us  [plane_conv(): lax.conv_general_dilated(rows, weight, window_strides=(1, 1), padding=((0...]
    concatenate x2, other arithmetic: 2.1 us -> 1.06 us  [halo(): return jnp.concatenate([before, x, after], axis=dim)]
    rev x1, local copies, waits for them, and re-layouts: 1.77 us -> 0.77 us  [backward_in(): depth_weight[::-1]]
    ppermute x2, waiting for transfers between devices: 2.19 us -> 3.18 us  [halo(): lax.ppermute(lax.slice_in_dim(x, length - 1, length, axis=dim), axis, up)]
    unnamed x20 -> x26, local copies, waits for them, and re-layouts: 4.91 us -> 4.92 us
where the time goes in v15:
time: 94.8 us; the launch traced here: 93.8 us
  starting transfers between devices  28 us (30%)
  waiting for transfers between devices  27.6 us (29%)
  local copies, waits for them, and re-layouts  17.3 us (18%)
  other arithmetic  11.4 us (12%)
  matrix products  5.77 us (6%)
  between operations  3.72 us (4%)
    ppermute x2, starting transfers between devices, halo(): lax.ppermute(lax.slice_in_dim(x, length - 1, length, axis=dim), axis, up)  7.21 us
    ppermute x1, waiting for transfers between devices, backward(): lax.ppermute(send, 'chan', shift_pairs(chans, k))  6.8 us
    all_to_all x1, starting transfers between devices, forward_out(): return lax.all_to_all(out, 'filt', 0, 2, tiled=True)  6.16 us
    all_to_all x1, waiting for transfers between devices, backward(): all_filters = lax.all_to_all(blocks, 'filt', 0, 0, tiled=True)  6.04 us
    unnamed x26, local copies, waits for them, and re-layouts  4.92 us
    ppermute x1, waiting for transfers between devices, backward_in(): lax.ppermute(lax.dynamic_slice_in_dim(grad_in, target * c_loc, c_loc, 0),...  4.77 us
    all_to_all x1, starting transfers between devices, gather_weight(): by_filt = lax.all_to_all(spread, 'filt', 0, 4, tiled=True)[0]  4.48 us
    ppermute x2, waiting for transfers between devices, halo(): after = lax.ppermute(lax.slice_in_dim(x, 0, 1, axis=dim), axis, down)  4.4 us
  transfers between devices with their start and end apart: 11, of which 6 were waited for; matrix products, arithmetic and copies ran while one was open for 24% of the time, Pallas kernels for 0%

profile of v15, /device:TPU:1, one launch (start us, length us, event | category | flops | bytes accessed | tf_op | source)
XLA Modules:
  0.0 93.8 jit_solution(10200246551659482815)
XLA Ops:
  0.7 3.1 %pad_dynamic-slice_fusion = (bf16[128,2,6,128]{3,2,1,0:T(8,128)(2,1)S(1)}, bf16[128,2,6,128]{3,2,1,0:T(8,128)(2,1)}) fusion(s32[]{:T(128)S(6)} %select_n.102, bf16[128,2,32,128]{3,2,1,0:T(8,128)(2,1)} %param.7, s32[]{:T(128)S(6)} %select_n.101), kind=kLoop, calls=%fused_computation.1 | loop fusion | bytes 2883592 | tf_op jit(solution)/shard_map/dynamic_slice | solution.py:96
  3.8 2.0 %collective-permute-start = (bf16[128,2,6,128]{3,2,1,0:T(8,128)(2,1)}, bf16[128,2,6,128]{3,2,1,0:T(8,128)(2,1)S(1)}, u32[]{:S(2)}, u32[]{:S(2)}) collective-permute-start(bf16[128,2,6,128]{3,2,1,0:T(8,128)(2,1)} %get-tuple-element.11), channel_id=1, source_target_pairs={{0,4},{4,0},{1,5},{5,1},{2,6},{6,2},{3,7},{7,3},{8,12},{12,8},{9,1... | collective-permute-start | bytes 1179656 | tf_op jit(solution)/shard_map/ppermute | solution.py:99
  5.8 1.0 %broadcast_in_dim.28 = bf16[4,3,3,128,64]{3,4,2,1,0:T(8,128)(2,1)} broadcast(bf16[3,3,128,64]{2,3,1,0:T(8,128)(2,1)S(1)} %copy-done.6), dimensions={1,2,3,4} | broadcast | bytes 737280 | tf_op jit(solution)/shard_map/broadcast_in_dim | solution.py:76
  6.8 4.5 %all-to-all-start = ((bf16[4,3,3,128,64]{3,4,2,1,0:T(8,128)(2,1)}), bf16[4,3,3,128,64]{3,4,2,1,0:T(8,128)(2,1)S(1)}, u32[]{:S(2)}, u32[]{:S(2)}) async-start(bf16[4,3,3,128,64]{3,4,2,1,0:T(8,128)(2,1)} %broadcast_in_dim.28), calls=%async_computation | async-start | bytes 1179648 | tf_op jit(solution)/shard_map/all_to_all | solution.py:77
  15.8 6.8 %collective-permute-done.2 = bf16[2,64,2,4,128]{4,1,3,2,0:T(8,128)(2,1)S(1)} collective-permute-done((bf16[2,64,2,4,128]{4,1,3,2,0:T(8,128)(2,1)S(1)}, bf16[2,64,2,4,128]{4,1,3,2,0:T(8,128)(2,1)S(1)}, u32[]{:S(2)}, u32[]{:S(2)}) %collective-permute-start.2) | collective-permute-done | bytes 262176 | tf_op jit(solution)/shard_map/ppermute | solution.py:129
  23.3 0.9 broadcast_select_fusion
  24.2 2.4 %all-to-all-done = bf16[4,3,3,128,64]{3,4,2,1,0:T(8,128)(2,1)S(1)} async-done(((bf16[4,3,3,128,64]{3,4,2,1,0:T(8,128)(2,1)}), bf16[4,3,3,128,64]{3,4,2,1,0:T(8,128)(2,1)S(1)}, u32[]{:S(2)}, u32[]{:S(2)}) %all-to-all-start) | async-done | bytes 589856 | tf_op jit(solution)/shard_map/all_to_all | solution.py:77
  26.6 3.5 %all-to-all-start.1 = ((bf16[4,64,2,4,128]{4,1,3,2,0:T(8,128)(2,1)}), bf16[4,64,2,4,128]{4,1,3,2,0:T(8,128)(2,1)S(1)}, u32[]{:S(2)}, u32[]{:S(2)}) async-start(bf16[4,64,2,4,128]{4,1,3,2,0:T(8,128)(2,1)} %broadcast_select_fusion), calls=%async_computation.1 | async-start | bytes 1048576 | tf_op jit(solution)/shard_map/all_to_all | solution.py:138
  30.9 3.4 %fusion.10 = bf16[256,6,2,128]{3,1,2,0:T(8,128)(2,1)S(1)} fusion(s32[]{:T(128)S(6)} %select_n.104, bf16[128,2,6,128]{3,2,1,0:T(8,128)(2,1)S(1)} %collective-permute-done, bf16[128,2,6,128]{3,2,1,0:T(8,128)(2,1)S(1)} %get-tuple-element.10), kind=kLoop, calls=%fused_computation.27 | loop fusion | flops 1179648 | bytes 1572868 | tf_op jit(solution)/shard_map/jit(_roll_dynamic)/dynamic_slice | solution.py:19
  34.3 1.3 %copy.93 = bf16[256,6,2,128]{0,2,3,1:T(2,128)(2,1)S(1)} copy(bf16[256,6,2,128]{3,1,2,0:T(8,128)(2,1)S(1)} %fusion.10) | data formatting | bytes 1572864
  36.4 1.7 %fusion.13 = bf16[256,6,2,8,19]{0,2,4,3,1:T(2,128)(2,1)} fusion(bf16[256,6,2,7,2]{0,2,4,3,1:T(2,128)(2,1)S(1)} %slice.52, bf16[256,6,2,8,17]{0,2,4,3,1:T(2,128)(2,1)S(1)} %bitcast.79), kind=kLoop, calls=%fused_computation.36 | loop fusion | flops 2801664 | bytes 1855488 | tf_op jit(solution)/shard_map/conv_general_dilated | solution.py:52
  38.0 6.0 %all-to-all-done.1 = bf16[4,64,2,4,128]{4,1,3,2,0:T(8,128)(2,1)S(1)} async-done(((bf16[4,64,2,4,128]{4,1,3,2,0:T(8,128)(2,1)}), bf16[4,64,2,4,128]{4,1,3,2,0:T(8,128)(2,1)S(1)}, u32[]{:S(2)}, u32[]{:S(2)}) %all-to-all-start.1) | async-done | bytes 524320 | tf_op jit(solution)/shard_map/all_to_all | solution.py:138
  44.4 1.9 %fusion.6 = bf16[3,3,256,256]{3,2,1,0:T(8,128)(2,1)S(1)} fusion(s32[]{:T(128)S(6)} %select_n.104, bf16[3,3,128,256]{3,2,1,0:T(8,128)(2,1)} %collective-permute-done.1, bf16[3,3,128,256]{3,2,1,0:T(8,128)(2,1)S(1)} %copy.63), kind=kLoop, calls=%fused_computation.23 | loop fusion | flops 4718592 | bytes 2359300 | tf_op jit(solution)/shard_map/jit(_roll_dynamic)/concatenate | solution.py:19
  46.4 1.5 %fusion.2 = bf16[4,16,17,256]{3,1,2,0:T(8,128)(2,1)S(1)} fusion(bf16[3,3,256,256]{3,2,1,0:T(8,128)(2,1)S(1)} %fusion.6, bf16[256,6,2,8,19]{0,2,4,3,1:T(2,128)(2,1)S(1)} %copy-done.2, pred[16,17]{0,1:T(8,128)(4,1)S(1)} %copy-done.10), kind=kOutput, calls=%fused_computation.17 | convolution fusion | flops 1284014080 | bytes 2670864 | tf_op jit(solution)/shard_map/conv_general_dilated | solution.py:52
  48.8 4.9 %collective-permute-start.3 = (bf16[512,1,4,128]{0,2,3,1:T(4,128)(2,1)S(1)}, bf16[512,1,4,128]{0,2,3,1:T(4,128)(2,1)S(1)}, u32[]{:S(2)}, u32[]{:S(2)}) collective-permute-start(bf16[512,1,4,128]{0,2,3,1:T(4,128)(2,1)S(1)} %get-tuple-element.12), channel_id=1, source_target_pairs={{0,8},{8,16},{16,24},{1,9},{9,17},{17,25},{2,10},{10,18},{18,26},{... | collective-permute-start | bytes 1572872 | tf_op jit(solution)/shard_map/ppermute | solution.py:46
  53.7 2.1 %collective-permute-start.4 = (bf16[512,1,4,128]{0,2,3,1:T(4,128)(2,1)S(1)}, bf16[512,1,4,128]{0,2,3,1:T(4,128)(2,1)S(1)}, u32[]{:S(2)}, u32[]{:S(2)}) collective-permute-start(bf16[512,1,4,128]{0,2,3,1:T(4,128)(2,1)S(1)} %get-tuple-element.13), channel_id=1, source_target_pairs={{8,0},{16,8},{24,16},{9,1},{17,9},{25,17},{10,2},{18,10},{26,18},{... | collective-permute-start | bytes 1572872 | tf_op jit(solution)/shard_map/ppermute | solution.py:47
  56.6 3.2 %collective-permute-done.3 = bf16[512,1,4,128]{0,2,3,1:T(4,128)(2,1)S(1)} collective-permute-done((bf16[512,1,4,128]{0,2,3,1:T(4,128)(2,1)S(1)}, bf16[512,1,4,128]{0,2,3,1:T(4,128)(2,1)S(1)}, u32[]{:S(2)}, u32[]{:S(2)}) %collective-permute-start.3) | collective-permute-done | bytes 524320 | tf_op jit(solution)/shard_map/ppermute | solution.py:46
  59.8 4.4 %collective-permute-done.4 = bf16[512,1,4,128]{0,2,3,1:T(4,128)(2,1)S(1)} collective-permute-done((bf16[512,1,4,128]{0,2,3,1:T(4,128)(2,1)S(1)}, bf16[512,1,4,128]{0,2,3,1:T(4,128)(2,1)S(1)}, u32[]{:S(2)}, u32[]{:S(2)}) %collective-permute-start.4) | collective-permute-done | bytes 524320 | tf_op jit(solution)/shard_map/ppermute | solution.py:47
  64.2 1.0 %pad_maximum_fusion = bf16[512,4,4,128]{0,2,3,1:T(4,128)(2,1)S(1)} fusion(bf16[512,1,4,128]{0,2,3,1:T(4,128)(2,1)S(1)} %collective-permute-done.4, bf16[256,2,4,128]{0,2,3,1:T(4,128)(2,1)S(1)} %copy.72, bf16[256,2,4,128]{0,2,3,1:T(4,128)(2,1)S(1)} %slice_bitcast_fusion, bf16[512,1,4,128]{0,2,3,1:T(4,128)(2,1)S(1)} %collective-permute-done.3), kind=kLoop, calls=%fused_computation.11 | loop fusion | flops 8388608 | bytes 4194304 | tf_op jit(solution)/shard_map/concatenate | solution.py:48
  66.2 1.4 %convolution_convert_fusion = bf16[2,4,8,16,256]{4,2,3,1,0:T(8,128)(2,1)S(1)} fusion(bf16[256,4,4,8,16]{0,2,4,3,1:T(4,128)(2,1)S(1)} %bitcast.90, bf16[3,256,256]{2,1,0:T(8,128)(2,1)S(1)} %copy-done.5), kind=kOutput, calls=%fused_computation.19 | convolution fusion | flops 402915328 | bytes 1966080 | tf_op jit(solution)/shard_map/conv_general_dilated | solution.py:63
  67.7 2.3 %collective-permute-start.5 = (bf16[256,2,1,128]{0,3,2,1:T(8,128)(2,1)S(1)}, bf16[256,2,1,128]{0,3,2,1:T(8,128)(2,1)S(1)}, u32[]{:S(2)}, u32[]{:S(2)}) collective-permute-start(bf16[256,2,1,128]{0,3,2,1:T(8,128)(2,1)S(1)} %get-tuple-element.16), channel_id=1, source_target_pairs={{0,4},{4,5},{5,1},{1,2},{2,6},{6,7},{7,3},{8,12},{12,13},{13,9},{9... | collective-permute-start | bytes 393224 | tf_op jit(solution)/shard_map/ppermute | solution.py:46
  70.1 1.3 %collective-permute-start.6 = (bf16[256,2,1,128]{0,3,2,1:T(8,128)(2,1)S(1)}, bf16[256,2,1,128]{0,3,2,1:T(8,128)(2,1)S(1)}, u32[]{:S(2)}, u32[]{:S(2)}) collective-permute-start(bf16[256,2,1,128]{0,3,2,1:T(8,128)(2,1)S(1)} %get-tuple-element.17), channel_id=1, source_target_pairs={{4,0},{5,4},{1,5},{2,1},{6,2},{7,6},{3,7},{12,8},{13,12},{9,13},{1... | collective-permute-start | bytes 393224 | tf_op jit(solution)/shard_map/ppermute | solution.py:47
  71.4 1.4 %convolution_convert_fusion.1 = bf16[2,4,8,16,256]{4,2,3,1,0:T(8,128)(2,1)S(1)} fusion(bf16[256,4,4,8,16]{0,2,4,3,1:T(4,128)(2,1)S(1)} %bitcast.89, bf16[3,256,256]{2,1,0:T(8,128)(2,1)S(1)} %copy-done.4), kind=kOutput, calls=%fused_computation.20 | convolution fusion | flops 402915328 | bytes 1966080 | tf_op jit(solution)/shard_map/conv_general_dilated | solution.py:63
  72.9 1.1 %copy.77 = bf16[256,2,4,128]{3,2,1,0:T(4,128)(2,1)} copy(bf16[256,2,4,128]{0,3,2,1:T(8,128)(2,1)S(1)} %bitcast.86) | data formatting | bytes 1048576 | tf_op jit(solution)/shard_map/convert_element_type | solution.py:109
  74.0 6.2 %all-to-all-start.2 = ((bf16[256,2,4,128]{3,2,1,0:T(4,128)(2,1)}), bf16[256,2,4,128]{3,2,1,0:T(4,128)(2,1)S(1)}, u32[]{:S(2)}, u32[]{:S(2)}) async-start(bf16[256,2,4,128]{3,2,1,0:T(4,128)(2,1)} %copy.77), calls=%async_computation.2 | async-start | bytes 1048576 | tf_op jit(solution)/shard_map/all_to_all | solution.py:110
  80.2 0.8 copy.94
  81.8 0.9 fusion.14
  82.6 1.5 %fusion.3 = bf16[4,16,17,256]{3,1,2,0:T(8,128)(2,1)S(1)} fusion(bf16[3,3,256,256]{3,2,1,0:T(8,128)(2,1)S(1)} %copy-done.1, bf16[256,6,2,8,19]{0,2,4,3,1:T(2,128)(2,1)S(1)} %fusion.14, pred[16,17]{0,1:T(8,128)(4,1)S(1)} %copy-done.10), kind=kOutput, calls=%fused_computation.18 | convolution fusion | flops 1284014080 | bytes 2670864 | tf_op jit(solution)/shard_map/conv_general_dilated | solution.py:52
  85.4 4.8 %collective-permute-done.7 = bf16[128,2,4,128]{0,2,3,1:T(4,128)(2,1)S(1)} collective-permute-done((bf16[128,2,4,128]{0,2,3,1:T(4,128)(2,1)S(1)}, bf16[128,2,4,128]{0,2,3,1:T(4,128)(2,1)S(1)}, u32[]{:S(2)}, u32[]{:S(2)}) %collective-permute-start.7) | collective-permute-done | bytes 262176 | tf_op jit(solution)/shard_map/ppermute | solution.py:160
  90.1 1.0 %fusion.21 = bf16[128,2,8,128]{0,2,3,1:T(8,128)(2,1)S(1)} fusion(s32[]{:T(128)S(6)} %select_n.120, bf16[128,2,4,128]{0,2,3,1:T(4,128)(2,1)S(1)} %collective-permute-done.7, bf16[128,2,4,128]{0,2,3,1:T(4,128)(2,1)S(1)} %get-tuple-element.14), kind=kLoop, calls=%fused_computation.45 | loop fusion | flops 2097152 | bytes 1048580 | tf_op jit(solution)/shard_map/jit(_roll_dynamic)/concatenate | solution.py:19
  91.2 1.3 %copy.88 = bf16[128,2,8,128]{3,2,1,0:T(8,128)(2,1)} copy(bf16[128,2,8,128]{0,2,3,1:T(8,128)(2,1)S(1)} %fusion.21) | data formatting | bytes 1048576
  92.6 1.1 %copy.87 = bf16[64,2,16,128]{3,2,1,0:T(8,128)(2,1)} copy(bf16[64,2,16,128]{3,0,2,1:T(8,128)(2,1)S(1)} %bitcast.88) | data formatting | bytes 1048576
  (66 shorter events, 9.5 us)
Async XLA Ops:
  0.6 5.2 %copy-start.6 = (bf16[3,3,128,64]{2,3,1,0:T(8,128)(2,1)S(1)}, bf16[3,3,128,64]{2,3,1,0:T(8,128)(2,1)}, u32[]{:S(2)}) copy-start(bf16[3,3,128,64]{2,3,1,0:T(8,128)(2,1)} %param.8) | copy-start | bytes 442372
  0.7 10.6 %copy-start.7 = (s32[2,2]{1,0:T(2,128)S(1)}, s32[2,2]{1,0:T(2,128)}, u32[]{:S(2)}) copy-start(s32[2,2]{1,0:T(2,128)} %constant.122.clone) | copy-start | bytes 52
  0.7 10.6 %copy-start.8 = (s32[2,2]{1,0:T(2,128)S(1)}, s32[2,2]{1,0:T(2,128)}, u32[]{:S(2)}) copy-start(s32[2,2]{1,0:T(2,128)} %constant.123.clone) | copy-start | bytes 52
  0.7 14.4 %copy-start.3 = (bf16[64,2,16,128]{3,2,1,0:T(8,128)(2,1)S(1)}, bf16[64,2,16,128]{3,2,1,0:T(8,128)(2,1)}, u32[]{:S(2)}) copy-start(bf16[64,2,16,128]{3,2,1,0:T(8,128)(2,1)} %param.10) | copy-start | bytes 1572868
  3.8 12.0 %copy-start.9 = (s32[2,4]{1,0:T(2,128)S(1)}, s32[2,4]{1,0:T(2,128)}, u32[]{:S(2)}) copy-start(s32[2,4]{1,0:T(2,128)} %constant.124.clone) | copy-start | bytes 100
  3.8 27.1 %collective-permute-start = (bf16[128,2,6,128]{3,2,1,0:T(8,128)(2,1)}, bf16[128,2,6,128]{3,2,1,0:T(8,128)(2,1)S(1)}, u32[]{:S(2)}, u32[]{:S(2)}) collective-permute-start(bf16[128,2,6,128]{3,2,1,0:T(8,128)(2,1)} %get-tuple-element.11), channel_id=1, source_target_pairs={{0,4},{4,0},{1,5},{5,1},{2,6},{6,2},{3,7},{7,3},{8,12},{12,8},{9,1... | collective-permute-start | bytes 1179656 | tf_op jit(solution)/shard_map/ppermute | solution.py:99
  6.8 19.9 %all-to-all-start = ((bf16[4,3,3,128,64]{3,4,2,1,0:T(8,128)(2,1)}), bf16[4,3,3,128,64]{3,4,2,1,0:T(8,128)(2,1)S(1)}, u32[]{:S(2)}, u32[]{:S(2)}) async-start(bf16[4,3,3,128,64]{3,4,2,1,0:T(8,128)(2,1)} %broadcast_in_dim.28), calls=%async_computation | async-start | bytes 1179648 | tf_op jit(solution)/shard_map/all_to_all | solution.py:77
  15.5 7.2 %collective-permute-start.2 = (bf16[2,64,2,4,128]{4,1,3,2,0:T(8,128)(2,1)S(1)}, bf16[2,64,2,4,128]{4,1,3,2,0:T(8,128)(2,1)S(1)}, u32[]{:S(2)}, u32[]{:S(2)}) collective-permute-start(bf16[2,64,2,4,128]{4,1,3,2,0:T(8,128)(2,1)S(1)} %pad_maximum_fusion.3), channel_id=1, source_target_pairs={{0,4},{4,0},{1,5},{5,1},{2,6},{6,2},{3,7},{7,3},{8,12},{12,8},{9,1... | collective-permute-start | bytes 786440 | tf_op jit(solution)/shard_map/ppermute | solution.py:129
  26.6 17.4 %all-to-all-start.1 = ((bf16[4,64,2,4,128]{4,1,3,2,0:T(8,128)(2,1)}), bf16[4,64,2,4,128]{4,1,3,2,0:T(8,128)(2,1)S(1)}, u32[]{:S(2)}, u32[]{:S(2)}) async-start(bf16[4,64,2,4,128]{4,1,3,2,0:T(8,128)(2,1)} %broadcast_select_fusion), calls=%async_computation.1 | async-start | bytes 1048576 | tf_op jit(solution)/shard_map/all_to_all | solution.py:138
  30.4 14.0 %collective-permute-start.1 = (bf16[3,3,128,256]{3,2,1,0:T(8,128)(2,1)S(1)}, bf16[3,3,128,256]{3,2,1,0:T(8,128)(2,1)}, u32[]{:S(2)}, u32[]{:S(2)}) collective-permute-start(bf16[3,3,128,256]{3,2,1,0:T(8,128)(2,1)S(1)} %copy.63), channel_id=1, source_target_pairs={{0,4},{4,0},{1,5},{5,1},{2,6},{6,2},{3,7},{7,3},{8,12},{12,8},{9,1... | collective-permute-start | bytes 1769480 | tf_op jit(solution)/shard_map/ppermute | solution.py:25
  38.0 8.3 %copy-start.10 = (pred[16,17]{0,1:T(8,128)(4,1)S(1)}, pred[16,17]{0,1:T(8,128)(4,1)}, u32[]{:S(2)}) copy-start(pred[16,17]{0,1:T(8,128)(4,1)} %constant.144) | copy-start | bytes 820
  44.1 2.3 %copy-start.2 = (bf16[256,6,2,8,19]{0,2,4,3,1:T(2,128)(2,1)S(1)}, bf16[256,6,2,8,19]{0,2,4,3,1:T(2,128)(2,1)}, u32[]{:S(2)}) copy-start(bf16[256,6,2,8,19]{0,2,4,3,1:T(2,128)(2,1)} %fusion.13) | copy-start | bytes 2801668
  46.4 1.5 %copy-start = (bf16[3,3,256,256]{3,2,1,0:T(8,128)(2,1)}, bf16[3,3,256,256]{3,2,1,0:T(8,128)(2,1)S(1)}, u32[]{:S(2)}) copy-start(bf16[3,3,256,256]{3,2,1,0:T(8,128)(2,1)S(1)} %fusion.6) | copy-start | bytes 3538948
  47.9 8.0 %copy-start.4 = (bf16[3,256,256]{2,1,0:T(8,128)(2,1)S(1)}, bf16[3,256,256]{2,1,0:T(8,128)(2,1)}, u32[]{:S(2)}) copy-start(bf16[3,256,256]{2,1,0:T(8,128)(2,1)} %param.9) | copy-start | bytes 1179652
  48.8 11.0 %collective-permute-start.3 = (bf16[512,1,4,128]{0,2,3,1:T(4,128)(2,1)S(1)}, bf16[512,1,4,128]{0,2,3,1:T(4,128)(2,1)S(1)}, u32[]{:S(2)}, u32[]{:S(2)}) collective-permute-start(bf16[512,1,4,128]{0,2,3,1:T(4,128)(2,1)S(1)} %get-tuple-element.12), channel_id=1, source_target_pairs={{0,8},{8,16},{16,24},{1,9},{9,17},{17,25},{2,10},{10,18},{18,26},{... | collective-permute-start | bytes 1572872 | tf_op jit(solution)/shard_map/ppermute | solution.py:46
  53.7 10.5 %collective-permute-start.4 = (bf16[512,1,4,128]{0,2,3,1:T(4,128)(2,1)S(1)}, bf16[512,1,4,128]{0,2,3,1:T(4,128)(2,1)S(1)}, u32[]{:S(2)}, u32[]{:S(2)}) collective-permute-start(bf16[512,1,4,128]{0,2,3,1:T(4,128)(2,1)S(1)} %get-tuple-element.13), channel_id=1, source_target_pairs={{8,0},{16,8},{24,16},{9,1},{17,9},{25,17},{10,2},{18,10},{26,18},{... | collective-permute-start | bytes 1572872 | tf_op jit(solution)/shard_map/ppermute | solution.py:47
  65.2 1.0 %copy-start.5 = (bf16[3,256,256]{2,1,0:T(8,128)(2,1)S(1)}, bf16[3,256,256]{2,1,0:T(8,128)(2,1)}, u32[]{:S(2)}) copy-start(bf16[3,256,256]{2,1,0:T(8,128)(2,1)} %rev.4) | copy-start | bytes 1179652
  67.7 12.4 %collective-permute-start.5 = (bf16[256,2,1,128]{0,3,2,1:T(8,128)(2,1)S(1)}, bf16[256,2,1,128]{0,3,2,1:T(8,128)(2,1)S(1)}, u32[]{:S(2)}, u32[]{:S(2)}) collective-permute-start(bf16[256,2,1,128]{0,3,2,1:T(8,128)(2,1)S(1)} %get-tuple-element.16), channel_id=1, source_target_pairs={{0,4},{4,5},{5,1},{1,2},{2,6},{6,7},{7,3},{8,12},{12,13},{13,9},{9... | collective-permute-start | bytes 393224 | tf_op jit(solution)/shard_map/ppermute | solution.py:46
  70.1 10.1 %collective-permute-start.6 = (bf16[256,2,1,128]{0,3,2,1:T(8,128)(2,1)S(1)}, bf16[256,2,1,128]{0,3,2,1:T(8,128)(2,1)S(1)}, u32[]{:S(2)}, u32[]{:S(2)}) collective-permute-start(bf16[256,2,1,128]{0,3,2,1:T(8,128)(2,1)S(1)} %get-tuple-element.17), channel_id=1, source_target_pairs={{4,0},{5,4},{1,5},{2,1},{6,2},{7,6},{3,7},{12,8},{13,12},{9,13},{1... | collective-permute-start | bytes 393224 | tf_op jit(solution)/shard_map/ppermute | solution.py:47
  74.0 18.6 %all-to-all-start.2 = ((bf16[256,2,4,128]{3,2,1,0:T(4,128)(2,1)}), bf16[256,2,4,128]{3,2,1,0:T(4,128)(2,1)S(1)}, u32[]{:S(2)}, u32[]{:S(2)}) async-start(bf16[256,2,4,128]{3,2,1,0:T(4,128)(2,1)} %copy.77), calls=%async_computation.2 | async-start | bytes 1048576 | tf_op jit(solution)/shard_map/all_to_all | solution.py:110
  81.0 1.6 %copy-start.1 = (bf16[3,3,256,256]{3,2,1,0:T(8,128)(2,1)S(1)}, bf16[3,3,256,256]{3,2,1,0:T(8,128)(2,1)}, u32[]{:S(2)}) copy-start(bf16[3,3,256,256]{3,2,1,0:T(8,128)(2,1)} %copy-done) | copy-start | bytes 3538948
  84.8 5.3 %collective-permute-start.7 = (bf16[128,2,4,128]{0,2,3,1:T(4,128)(2,1)S(1)}, bf16[128,2,4,128]{0,2,3,1:T(4,128)(2,1)S(1)}, u32[]{:S(2)}, u32[]{:S(2)}) collective-permute-start(bf16[128,2,4,128]{0,2,3,1:T(4,128)(2,1)S(1)} %get-tuple-element.15), channel_id=1, source_target_pairs={{0,4},{1,5},{2,6},{3,7},{4,0},{5,1},{6,2},{7,3},{8,12},{9,13},{10,... | collective-permute-start | bytes 786440 | tf_op jit(solution)/shard_map/ppermute | solution.py:160

commit v16 on v15

--- a/solution.py
+++ b/solution.py
@@ -75,7 +75,9 @@
     filts = lax.axis_size("filt")
     spread = jnp.broadcast_to(weight[None], (filts,) + weight.shape)
     by_filt = lax.all_to_all(spread, "filt", 0, 4, tiled=True)[0]
-    return gather_blocks(by_filt, "chan", 2)
+    chans = lax.axis_size("chan")
+    pieces = [by_filt] + [lax.ppermute(by_filt, "chan", shift_pairs(chans, k)) for k in range(1, chans)]
+    return jnp.concatenate(pieces, axis=2)
 
 
 def sub_block(chan, filt, filts):
@@ -97,7 +99,7 @@
     pieces = [window(chan)]
     for k in range(1, chans):
         pieces.append(lax.ppermute(window((chan + k) % chans), "chan", shift_pairs(chans, k)))
-    all_channels = order_blocks(pieces, chan, 0)
+    all_channels = jnp.concatenate(pieces, axis=0)
     return plane_conv(all_channels, weight, "HWIO").astype(jnp.bfloat16)
 
 
@@ -152,12 +154,13 @@
     chan = lax.axis_index("chan")
     c_loc = grad_in.shape[0] // chans
     even = filt % 2 == 0
-    pieces = [lax.dynamic_slice_in_dim(grad_in, chan * c_loc, c_loc, 0)]
+    pieces = [grad_in[:c_loc]]
     for k in range(1, chans):
         target = jnp.where(even, (chan + k) % chans, (chan - k) % chans)
         pairs = [(c * filts + f, (((c + k) if f % 2 == 0 else (c - k)) % chans) * filts + f)
                  for c in range(chans) for f in range(filts)]
-        pieces.append(lax.ppermute(lax.dynamic_slice_in_dim(grad_in, target * c_loc, c_loc, 0), ROWS, pairs))
+        at = (chan - target) % chans
+        pieces.append(lax.ppermute(lax.dynamic_slice_in_dim(grad_in, at * c_loc, c_loc, 0), ROWS, pairs))
     return order_blocks(pieces, jnp.where(even, chan, chans - 1 - chan), 2)
 
 

time: 94.8 us -> 95.6 us (level)
  other arithmetic: 11.4 us -> 6.52 us
  waiting for transfers between devices: 27.6 us -> 30.7 us
  matrix products: 5.77 us -> 8.26 us
    dynamic_slice x1 -> x0, other arithmetic: 3.41 us -> none  [order_blocks(): return jnp.roll(stacked, (me + 1) * block, axis=dim)]
    conv_general_dilated x2, matrix products: 2.98 us -> 5.47 us  [plane_conv(): lax.conv_general_dilated(rows, weight, window_strides=(1, 1), padding=((0...]
    all_to_all x1, waiting for transfers between devices: 6.04 us -> 8.45 us  [backward(): all_filters = lax.all_to_all(blocks, 'filt', 0, 0, tiled=True)]
    concatenate x2 -> x1, other arithmetic: 2.95 us -> 1.03 us  [order_blocks(): return jnp.roll(stacked, (me + 1) * block, axis=dim)]
    concatenate x0 -> x1, other arithmetic: none -> 1.25 us  [forward(): all_channels = jnp.concatenate(pieces, axis=0)]
    unnamed x26 -> x20, local copies, waits for them, and re-layouts: 4.92 us -> 4.91 us
  transfers between devices with their start and end apart: 11 -> 11, of which waited for: 6 -> 7; matrix products, arithmetic and copies ran while one was open for 24% -> 23% of each run, Pallas kernels for 0% -> 0%
where the time goes in v16:
time: 95.6 us; the launch traced here: 94.6 us
  waiting for transfers between devices  30.7 us (32%)
  starting transfers between devices  28.1 us (29%)
  local copies, waits for them, and re-layouts  17.4 us (18%)
  matrix products  8.26 us (9%)
  other arithmetic  6.52 us (7%)
  between operations  3.68 us (4%)
    all_to_all x1, waiting for transfers between devices, backward(): all_filters = lax.all_to_all(blocks, 'filt', 0, 0, tiled=True)  8.45 us
    ppermute x2, starting transfers between devices, halo(): lax.ppermute(lax.slice_in_dim(x, length - 1, length, axis=dim), axis, up)  7.49 us
    ppermute x1, waiting for transfers between devices, backward(): lax.ppermute(send, 'chan', shift_pairs(chans, k))  6.54 us
    all_to_all x1, starting transfers between devices, forward_out(): return lax.all_to_all(out, 'filt', 0, 2, tiled=True)  6.38 us
    conv_general_dilated x2, matrix products, plane_conv(): lax.conv_general_dilated(rows, weight, window_strides=(1, 1), padding=((0...  5.47 us
    unnamed x20, local copies, waits for them, and re-layouts  4.91 us
    ppermute x1, waiting for transfers between devices, backward_in(): lax.ppermute(lax.dynamic_slice_in_dim(grad_in, at * c_loc, c_loc, 0), ROW...  4.72 us
    all_to_all x1, starting transfers between devices, gather_weight(): by_filt = lax.all_to_all(spread, 'filt', 0, 4, tiled=True)[0]  4.48 us
  transfers between devices with their start and end apart: 11, of which 7 were waited for; matrix products, arithmetic and copies ran while one was open for 23% of the time, Pallas kernels for 0%

profile of v16, /device:TPU:1, one launch (start us, length us, event | category | flops | bytes accessed | tf_op | source)
XLA Modules:
  0.0 94.6 jit_solution(1377155133175913160)
XLA Ops:
  0.7 2.3 %pad_dynamic-slice_fusion.1 = (bf16[128,2,6,128]{3,2,1,0:T(8,128)(2,1)S(1)}, bf16[128,2,6,128]{3,2,1,0:T(8,128)(2,1)S(1)}) fusion(s32[]{:T(128)S(6)} %select_n.85, bf16[128,2,32,128]{3,2,1,0:T(8,128)(2,1)} %param.7, s32[]{:T(128)S(6)} %select_n.87), kind=kLoop, calls=%fused_computation.2 | loop fusion | bytes 2883592 | tf_op jit(solution)/shard_map/dynamic_slice | solution.py:98
  3.0 2.1 %collective-permute-start = (bf16[128,2,6,128]{3,2,1,0:T(8,128)(2,1)S(1)}, bf16[128,2,6,128]{3,2,1,0:T(8,128)(2,1)}, u32[]{:S(2)}, u32[]{:S(2)}) collective-permute-start(bf16[128,2,6,128]{3,2,1,0:T(8,128)(2,1)S(1)} %get-tuple-element.11), channel_id=1, source_target_pairs={{0,4},{4,0},{1,5},{5,1},{2,6},{6,2},{3,7},{7,3},{8,12},{12,8},{9,1... | collective-permute-start | bytes 1179656 | tf_op jit(solution)/shard_map/ppermute | solution.py:101
  5.1 1.0 %broadcast_in_dim.28 = bf16[4,3,3,128,64]{3,4,2,1,0:T(8,128)(2,1)} broadcast(bf16[3,3,128,64]{2,3,1,0:T(8,128)(2,1)S(1)} %copy-done.3), dimensions={1,2,3,4} | broadcast | bytes 737280 | tf_op jit(solution)/shard_map/broadcast_in_dim | solution.py:76
  6.1 4.5 %all-to-all-start = ((bf16[4,3,3,128,64]{3,4,2,1,0:T(8,128)(2,1)}), bf16[4,3,3,128,64]{3,4,2,1,0:T(8,128)(2,1)S(1)}, u32[]{:S(2)}, u32[]{:S(2)}) async-start(bf16[4,3,3,128,64]{3,4,2,1,0:T(8,128)(2,1)} %broadcast_in_dim.28), calls=%async_computation | async-start | bytes 1179648 | tf_op jit(solution)/shard_map/all_to_all | solution.py:77
  15.0 6.5 %collective-permute-done.2 = bf16[2,64,2,4,128]{4,1,3,2,0:T(8,128)(2,1)S(1)} collective-permute-done((bf16[2,64,2,4,128]{4,1,3,2,0:T(8,128)(2,1)S(1)}, bf16[2,64,2,4,128]{4,1,3,2,0:T(8,128)(2,1)S(1)}, u32[]{:S(2)}, u32[]{:S(2)}) %collective-permute-start.2) | collective-permute-done | bytes 262176 | tf_op jit(solution)/shard_map/ppermute | solution.py:131
  22.3 0.9 broadcast_select_fusion
  23.2 2.7 %all-to-all-done = bf16[4,3,3,128,64]{3,4,2,1,0:T(8,128)(2,1)S(1)} async-done(((bf16[4,3,3,128,64]{3,4,2,1,0:T(8,128)(2,1)}), bf16[4,3,3,128,64]{3,4,2,1,0:T(8,128)(2,1)S(1)}, u32[]{:S(2)}, u32[]{:S(2)}) %all-to-all-start) | async-done | bytes 589856 | tf_op jit(solution)/shard_map/all_to_all | solution.py:77
  25.9 3.5 %all-to-all-start.1 = ((bf16[4,64,2,4,128]{4,1,3,2,0:T(8,128)(2,1)}), bf16[4,64,2,4,128]{4,1,3,2,0:T(8,128)(2,1)S(1)}, u32[]{:S(2)}, u32[]{:S(2)}) async-start(bf16[4,64,2,4,128]{4,1,3,2,0:T(8,128)(2,1)} %broadcast_select_fusion), calls=%async_computation.1 | async-start | bytes 1048576 | tf_op jit(solution)/shard_map/all_to_all | solution.py:140
  29.5 1.1 %copy.64 = bf16[3,3,128,256]{3,2,1,0:T(8,128)(2,1)} copy(bf16[3,3,128,256]{2,3,1,0:T(8,128)(2,1)S(1)} %bitcast.81) | data formatting | bytes 1179648 | tf_op jit(solution)/shard_map/squeeze | solution.py:77
  30.7 1.2 %maximum_bitcast_fusion = bf16[256,6,2,128]{3,1,2,0:T(8,128)(2,1)S(1)} fusion(bf16[128,2,6,128]{3,2,1,0:T(8,128)(2,1)} %collective-permute-done, bf16[128,2,6,128]{3,2,1,0:T(8,128)(2,1)S(1)} %get-tuple-element.10), kind=kLoop, calls=%fused_computation.14 | loop fusion | flops 393216 | bytes 1572864 | tf_op jit(solution)/shard_map/concatenate | solution.py:102
  32.0 1.3 %copy.93 = bf16[256,6,2,128]{0,2,3,1:T(2,128)(2,1)S(1)} copy(bf16[256,6,2,128]{3,1,2,0:T(8,128)(2,1)S(1)} %maximum_bitcast_fusion) | data formatting | bytes 1572864
  34.0 0.9 fusion.6
  34.9 8.5 %all-to-all-done.1 = bf16[4,64,2,4,128]{4,1,3,2,0:T(8,128)(2,1)S(1)} async-done(((bf16[4,64,2,4,128]{4,1,3,2,0:T(8,128)(2,1)}), bf16[4,64,2,4,128]{4,1,3,2,0:T(8,128)(2,1)S(1)}, u32[]{:S(2)}, u32[]{:S(2)}) %all-to-all-start.1) | async-done | bytes 524320 | tf_op jit(solution)/shard_map/all_to_all | solution.py:140
  44.2 2.7 %fusion.2 = bf16[4,16,17,256]{3,1,2,0:T(8,128)(2,1)S(1)} fusion(bf16[256,6,2,8,19]{0,2,4,3,1:T(2,128)(2,1)S(1)} %fusion.6, bf16[3,3,128,256]{3,2,1,0:T(8,128)(2,1)} %collective-permute-done.1, bf16[3,3,128,256]{3,2,1,0:T(8,128)(2,1)} %copy.64, pred[16,17]{0,1:T(8,128)(4,1)S(1)} %copy-done.7), kind=kOutput, calls=%fused_computation.9 | convolution fusion | flops 1286373376 | bytes 2670864 | tf_op jit(solution)/shard_map/conv_general_dilated | solution.py:52
  47.9 5.4 %collective-permute-start.3 = (bf16[512,1,4,128]{0,2,3,1:T(4,128)(2,1)S(1)}, bf16[512,1,4,128]{0,2,3,1:T(4,128)(2,1)S(1)}, u32[]{:S(2)}, u32[]{:S(2)}) collective-permute-start(bf16[512,1,4,128]{0,2,3,1:T(4,128)(2,1)S(1)} %get-tuple-element.12), channel_id=1, source_target_pairs={{0,8},{8,16},{16,24},{1,9},{9,17},{17,25},{2,10},{10,18},{18,26},{... | collective-permute-start | bytes 1572872 | tf_op jit(solution)/shard_map/ppermute | solution.py:46
  53.3 1.9 %collective-permute-start.4 = (bf16[512,1,4,128]{0,2,3,1:T(4,128)(2,1)S(1)}, bf16[512,1,4,128]{0,2,3,1:T(4,128)(2,1)S(1)}, u32[]{:S(2)}, u32[]{:S(2)}) collective-permute-start(bf16[512,1,4,128]{0,2,3,1:T(4,128)(2,1)S(1)} %get-tuple-element.13), channel_id=1, source_target_pairs={{8,0},{16,8},{24,16},{9,1},{17,9},{25,17},{10,2},{18,10},{26,18},{... | collective-permute-start | bytes 1572872 | tf_op jit(solution)/shard_map/ppermute | solution.py:47
  56.0 3.3 %collective-permute-done.3 = bf16[512,1,4,128]{0,2,3,1:T(4,128)(2,1)S(1)} collective-permute-done((bf16[512,1,4,128]{0,2,3,1:T(4,128)(2,1)S(1)}, bf16[512,1,4,128]{0,2,3,1:T(4,128)(2,1)S(1)}, u32[]{:S(2)}, u32[]{:S(2)}) %collective-permute-start.3) | collective-permute-done | bytes 524320 | tf_op jit(solution)/shard_map/ppermute | solution.py:46
  59.4 4.4 %collective-permute-done.4 = bf16[512,1,4,128]{0,2,3,1:T(4,128)(2,1)S(1)} collective-permute-done((bf16[512,1,4,128]{0,2,3,1:T(4,128)(2,1)S(1)}, bf16[512,1,4,128]{0,2,3,1:T(4,128)(2,1)S(1)}, u32[]{:S(2)}, u32[]{:S(2)}) %collective-permute-start.4) | collective-permute-done | bytes 524320 | tf_op jit(solution)/shard_map/ppermute | solution.py:47
  63.8 1.0 %pad_maximum_fusion = bf16[512,4,4,128]{0,2,3,1:T(4,128)(2,1)S(1)} fusion(bf16[512,1,4,128]{0,2,3,1:T(4,128)(2,1)S(1)} %collective-permute-done.4, bf16[256,2,4,128]{0,2,3,1:T(4,128)(2,1)S(1)} %copy.71, bf16[256,2,4,128]{0,2,3,1:T(4,128)(2,1)S(1)} %slice_bitcast_fusion, bf16[512,1,4,128]{0,2,3,1:T(4,128)(2,1)S(1)} %collective-permute-done.3), kind=kLoop, calls=%fused_computation.3 | loop fusion | flops 8388608 | bytes 4194304 | tf_op jit(solution)/shard_map/concatenate | solution.py:48
  65.8 1.4 %convolution_convert_fusion = bf16[2,4,8,16,256]{4,2,3,1,0:T(8,128)(2,1)S(1)} fusion(bf16[256,4,4,8,16]{0,2,4,3,1:T(4,128)(2,1)S(1)} %bitcast.90, bf16[3,256,256]{2,1,0:T(8,128)(2,1)S(1)} %copy-done.2), kind=kOutput, calls=%fused_computation.11 | convolution fusion | flops 402915328 | bytes 1966080 | tf_op jit(solution)/shard_map/conv_general_dilated | solution.py:63
  67.3 2.1 %collective-permute-start.5 = (bf16[256,2,1,128]{0,3,2,1:T(8,128)(2,1)S(1)}, bf16[256,2,1,128]{0,3,2,1:T(8,128)(2,1)S(1)}, u32[]{:S(2)}, u32[]{:S(2)}) collective-permute-start(bf16[256,2,1,128]{0,3,2,1:T(8,128)(2,1)S(1)} %get-tuple-element.14), channel_id=1, source_target_pairs={{0,4},{4,5},{5,1},{1,2},{2,6},{6,7},{7,3},{8,12},{12,13},{13,9},{9... | collective-permute-start | bytes 393224 | tf_op jit(solution)/shard_map/ppermute | solution.py:46
  69.4 1.5 %collective-permute-start.6 = (bf16[256,2,1,128]{0,3,2,1:T(8,128)(2,1)S(1)}, bf16[256,2,1,128]{0,3,2,1:T(8,128)(2,1)S(1)}, u32[]{:S(2)}, u32[]{:S(2)}) collective-permute-start(bf16[256,2,1,128]{0,3,2,1:T(8,128)(2,1)S(1)} %get-tuple-element.15), channel_id=1, source_target_pairs={{4,0},{5,4},{1,5},{2,1},{6,2},{7,6},{3,7},{12,8},{13,12},{9,13},{1... | collective-permute-start | bytes 393224 | tf_op jit(solution)/shard_map/ppermute | solution.py:47
  70.9 1.4 %convolution_convert_fusion.1 = bf16[2,4,8,16,256]{4,2,3,1,0:T(8,128)(2,1)S(1)} fusion(bf16[256,4,4,8,16]{0,2,4,3,1:T(4,128)(2,1)S(1)} %bitcast.89, bf16[3,256,256]{2,1,0:T(8,128)(2,1)S(1)} %copy-done.1), kind=kOutput, calls=%fused_computation.12 | convolution fusion | flops 402915328 | bytes 1966080 | tf_op jit(solution)/shard_map/conv_general_dilated | solution.py:63
  72.4 1.1 %copy.76 = bf16[256,2,4,128]{3,2,1,0:T(4,128)(2,1)} copy(bf16[256,2,4,128]{0,3,2,1:T(8,128)(2,1)S(1)} %bitcast.85) | data formatting | bytes 1048576 | tf_op jit(solution)/shard_map/convert_element_type | solution.py:111
  73.5 6.4 %all-to-all-start.2 = ((bf16[256,2,4,128]{3,2,1,0:T(4,128)(2,1)}), bf16[256,2,4,128]{3,2,1,0:T(4,128)(2,1)S(1)}, u32[]{:S(2)}, u32[]{:S(2)}) async-start(bf16[256,2,4,128]{3,2,1,0:T(4,128)(2,1)} %copy.76), calls=%async_computation.2 | async-start | bytes 1048576 | tf_op jit(solution)/shard_map/all_to_all | solution.py:112
  80.0 0.8 copy.94
  81.5 0.9 fusion.7
  82.4 2.8 %fusion.3 = bf16[4,16,17,256]{3,1,2,0:T(8,128)(2,1)S(1)} fusion(bf16[256,6,2,8,19]{0,2,4,3,1:T(2,128)(2,1)S(1)} %fusion.7, bf16[3,3,128,256]{3,2,1,0:T(8,128)(2,1)} %collective-permute-done.1, bf16[3,3,128,256]{3,2,1,0:T(8,128)(2,1)} %copy.64, pred[16,17]{0,1:T(8,128)(4,1)S(1)} %copy-done.7), kind=kOutput, calls=%fused_computation.10 | convolution fusion | flops 1286373376 | bytes 2670864 | tf_op jit(solution)/shard_map/conv_general_dilated | solution.py:52
  86.3 4.7 %collective-permute-done.7 = bf16[128,2,4,128]{0,2,3,1:T(4,128)(2,1)S(1)} collective-permute-done((bf16[128,2,4,128]{0,2,3,1:T(4,128)(2,1)S(1)}, bf16[128,2,4,128]{0,2,3,1:T(4,128)(2,1)S(1)}, u32[]{:S(2)}, u32[]{:S(2)}) %collective-permute-start.7) | collective-permute-done | bytes 262176 | tf_op jit(solution)/shard_map/ppermute | solution.py:163
  91.0 1.0 %fusion.14 = bf16[128,2,8,128]{0,2,3,1:T(8,128)(2,1)S(1)} fusion(s32[]{:T(128)S(6)} %select_n.103, bf16[128,2,4,128]{0,2,3,1:T(4,128)(2,1)S(1)} %collective-permute-done.7, bf16[128,2,4,128]{0,2,3,1:T(4,128)(2,1)S(1)} %slice_bitcast_fusion.1), kind=kLoop, calls=%fused_computation.32 | loop fusion | flops 2097152 | bytes 1048580 | tf_op jit(solution)/shard_map/jit(_roll_dynamic)/concatenate | solution.py:19
  92.0 1.3 %copy.88 = bf16[128,2,8,128]{3,2,1,0:T(8,128)(2,1)} copy(bf16[128,2,8,128]{0,2,3,1:T(8,128)(2,1)S(1)} %fusion.14) | data formatting | bytes 1048576
  93.5 1.1 %copy.87 = bf16[64,2,16,128]{3,2,1,0:T(8,128)(2,1)} copy(bf16[64,2,16,128]{3,0,2,1:T(8,128)(2,1)S(1)} %bitcast.87) | data formatting | bytes 1048576
  (62 shorter events, 9.3 us)
Async XLA Ops:
  0.6 4.5 %copy-start.3 = (bf16[3,3,128,64]{2,3,1,0:T(8,128)(2,1)S(1)}, bf16[3,3,128,64]{2,3,1,0:T(8,128)(2,1)}, u32[]{:S(2)}) copy-start(bf16[3,3,128,64]{2,3,1,0:T(8,128)(2,1)} %param.8) | copy-start | bytes 442372
  0.7 9.9 %copy-start.4 = (s32[2,2]{1,0:T(2,128)S(1)}, s32[2,2]{1,0:T(2,128)}, u32[]{:S(2)}) copy-start(s32[2,2]{1,0:T(2,128)} %constant.98.clone) | copy-start | bytes 52
  0.7 9.9 %copy-start.5 = (s32[2,2]{1,0:T(2,128)S(1)}, s32[2,2]{1,0:T(2,128)}, u32[]{:S(2)}) copy-start(s32[2,2]{1,0:T(2,128)} %constant.99.clone) | copy-start | bytes 52
  0.7 13.6 %copy-start = (bf16[64,2,16,128]{3,2,1,0:T(8,128)(2,1)S(1)}, bf16[64,2,16,128]{3,2,1,0:T(8,128)(2,1)}, u32[]{:S(2)}) copy-start(bf16[64,2,16,128]{3,2,1,0:T(8,128)(2,1)} %param.10) | copy-start | bytes 1572868
  3.0 12.0 %copy-start.6 = (s32[2,4]{1,0:T(2,128)S(1)}, s32[2,4]{1,0:T(2,128)}, u32[]{:S(2)}) copy-start(s32[2,4]{1,0:T(2,128)} %constant.100.clone) | copy-start | bytes 100
  3.0 27.7 %collective-permute-start = (bf16[128,2,6,128]{3,2,1,0:T(8,128)(2,1)S(1)}, bf16[128,2,6,128]{3,2,1,0:T(8,128)(2,1)}, u32[]{:S(2)}, u32[]{:S(2)}) collective-permute-start(bf16[128,2,6,128]{3,2,1,0:T(8,128)(2,1)S(1)} %get-tuple-element.11), channel_id=1, source_target_pairs={{0,4},{4,0},{1,5},{5,1},{2,6},{6,2},{3,7},{7,3},{8,12},{12,8},{9,1... | collective-permute-start | bytes 1179656 | tf_op jit(solution)/shard_map/ppermute | solution.py:101
  6.1 19.9 %all-to-all-start = ((bf16[4,3,3,128,64]{3,4,2,1,0:T(8,128)(2,1)}), bf16[4,3,3,128,64]{3,4,2,1,0:T(8,128)(2,1)S(1)}, u32[]{:S(2)}, u32[]{:S(2)}) async-start(bf16[4,3,3,128,64]{3,4,2,1,0:T(8,128)(2,1)} %broadcast_in_dim.28), calls=%async_computation | async-start | bytes 1179648 | tf_op jit(solution)/shard_map/all_to_all | solution.py:77
  14.7 6.9 %collective-permute-start.2 = (bf16[2,64,2,4,128]{4,1,3,2,0:T(8,128)(2,1)S(1)}, bf16[2,64,2,4,128]{4,1,3,2,0:T(8,128)(2,1)S(1)}, u32[]{:S(2)}, u32[]{:S(2)}) collective-permute-start(bf16[2,64,2,4,128]{4,1,3,2,0:T(8,128)(2,1)S(1)} %pad_maximum_fusion.6), channel_id=1, source_target_pairs={{0,4},{4,0},{1,5},{5,1},{2,6},{6,2},{3,7},{7,3},{8,12},{12,8},{9,1... | collective-permute-start | bytes 786440 | tf_op jit(solution)/shard_map/ppermute | solution.py:131
  25.9 17.4 %all-to-all-start.1 = ((bf16[4,64,2,4,128]{4,1,3,2,0:T(8,128)(2,1)}), bf16[4,64,2,4,128]{4,1,3,2,0:T(8,128)(2,1)S(1)}, u32[]{:S(2)}, u32[]{:S(2)}) async-start(bf16[4,64,2,4,128]{4,1,3,2,0:T(8,128)(2,1)} %broadcast_select_fusion), calls=%async_computation.1 | async-start | bytes 1048576 | tf_op jit(solution)/shard_map/all_to_all | solution.py:140
  30.5 13.7 %collective-permute-start.1 = (bf16[3,3,128,256]{3,2,1,0:T(8,128)(2,1)}, bf16[3,3,128,256]{3,2,1,0:T(8,128)(2,1)}, u32[]{:S(2)}, u32[]{:S(2)}) collective-permute-start(bf16[3,3,128,256]{3,2,1,0:T(8,128)(2,1)} %copy.64), channel_id=1, source_target_pairs={{0,4},{4,0},{1,5},{5,1},{2,6},{6,2},{3,7},{7,3},{8,12},{12,8},{9,1... | collective-permute-start | bytes 1769480 | tf_op jit(solution)/shard_map/ppermute | solution.py:79
  34.0 10.3 %copy-start.7 = (pred[16,17]{0,1:T(8,128)(4,1)S(1)}, pred[16,17]{0,1:T(8,128)(4,1)}, u32[]{:S(2)}) copy-start(pred[16,17]{0,1:T(8,128)(4,1)} %constant.120) | copy-start | bytes 820
  46.9 8.3 %copy-start.1 = (bf16[3,256,256]{2,1,0:T(8,128)(2,1)S(1)}, bf16[3,256,256]{2,1,0:T(8,128)(2,1)}, u32[]{:S(2)}) copy-start(bf16[3,256,256]{2,1,0:T(8,128)(2,1)} %param.9) | copy-start | bytes 1179652
  47.9 11.5 %collective-permute-start.3 = (bf16[512,1,4,128]{0,2,3,1:T(4,128)(2,1)S(1)}, bf16[512,1,4,128]{0,2,3,1:T(4,128)(2,1)S(1)}, u32[]{:S(2)}, u32[]{:S(2)}) collective-permute-start(bf16[512,1,4,128]{0,2,3,1:T(4,128)(2,1)S(1)} %get-tuple-element.12), channel_id=1, source_target_pairs={{0,8},{8,16},{16,24},{1,9},{9,17},{17,25},{2,10},{10,18},{18,26},{... | collective-permute-start | bytes 1572872 | tf_op jit(solution)/shard_map/ppermute | solution.py:46
  53.3 10.5 %collective-permute-start.4 = (bf16[512,1,4,128]{0,2,3,1:T(4,128)(2,1)S(1)}, bf16[512,1,4,128]{0,2,3,1:T(4,128)(2,1)S(1)}, u32[]{:S(2)}, u32[]{:S(2)}) collective-permute-start(bf16[512,1,4,128]{0,2,3,1:T(4,128)(2,1)S(1)} %get-tuple-element.13), channel_id=1, source_target_pairs={{8,0},{16,8},{24,16},{9,1},{17,9},{25,17},{10,2},{18,10},{26,18},{... | collective-permute-start | bytes 1572872 | tf_op jit(solution)/shard_map/ppermute | solution.py:47
  64.8 1.0 %copy-start.2 = (bf16[3,256,256]{2,1,0:T(8,128)(2,1)S(1)}, bf16[3,256,256]{2,1,0:T(8,128)(2,1)}, u32[]{:S(2)}) copy-start(bf16[3,256,256]{2,1,0:T(8,128)(2,1)} %rev.4) | copy-start | bytes 1179652
  67.3 12.6 %collective-permute-start.5 = (bf16[256,2,1,128]{0,3,2,1:T(8,128)(2,1)S(1)}, bf16[256,2,1,128]{0,3,2,1:T(8,128)(2,1)S(1)}, u32[]{:S(2)}, u32[]{:S(2)}) collective-permute-start(bf16[256,2,1,128]{0,3,2,1:T(8,128)(2,1)S(1)} %get-tuple-element.14), channel_id=1, source_target_pairs={{0,4},{4,5},{5,1},{1,2},{2,6},{6,7},{7,3},{8,12},{12,13},{13,9},{9... | collective-permute-start | bytes 393224 | tf_op jit(solution)/shard_map/ppermute | solution.py:46
  69.4 10.5 %collective-permute-start.6 = (bf16[256,2,1,128]{0,3,2,1:T(8,128)(2,1)S(1)}, bf16[256,2,1,128]{0,3,2,1:T(8,128)(2,1)S(1)}, u32[]{:S(2)}, u32[]{:S(2)}) collective-permute-start(bf16[256,2,1,128]{0,3,2,1:T(8,128)(2,1)S(1)} %get-tuple-element.15), channel_id=1, source_target_pairs={{4,0},{5,4},{1,5},{2,1},{6,2},{7,6},{3,7},{12,8},{13,12},{9,13},{1... | collective-permute-start | bytes 393224 | tf_op jit(solution)/shard_map/ppermute | solution.py:47
  73.5 19.9 %all-to-all-start.2 = ((bf16[256,2,4,128]{3,2,1,0:T(4,128)(2,1)}), bf16[256,2,4,128]{3,2,1,0:T(4,128)(2,1)S(1)}, u32[]{:S(2)}, u32[]{:S(2)}) async-start(bf16[256,2,4,128]{3,2,1,0:T(4,128)(2,1)} %copy.76), calls=%async_computation.2 | async-start | bytes 1048576 | tf_op jit(solution)/shard_map/all_to_all | solution.py:112
  85.7 5.3 %collective-permute-start.7 = (bf16[128,2,4,128]{0,2,3,1:T(4,128)(2,1)S(1)}, bf16[128,2,4,128]{0,2,3,1:T(4,128)(2,1)S(1)}, u32[]{:S(2)}, u32[]{:S(2)}) collective-permute-start(bf16[128,2,4,128]{0,2,3,1:T(4,128)(2,1)S(1)} %dynamic-slice_bitcast_fusion), channel_id=1, source_target_pairs={{0,4},{1,5},{2,6},{3,7},{4,0},{5,1},{6,2},{7,3},{8,12},{9,13},{10,... | collective-permute-start | bytes 786440 | tf_op jit(solution)/shard_map/ppermute | solution.py:163

commit v17 on v15

--- a/solution.py
+++ b/solution.py
@@ -110,7 +110,7 @@
     return lax.all_to_all(out, "filt", 0, 2, tiled=True)
 
 
-def backward(grad_out, weight, depth_weight):
+def grad_rows(grad_out):
     chans = lax.axis_size("chan")
     filts = lax.axis_size("filt")
     chan = lax.axis_index("chan")
@@ -127,6 +127,17 @@
         table = jnp.array([pick((r + k) % chans, r) for r in range(chans)], jnp.int32)[chan]
         send = jnp.stack([lax.dynamic_slice_in_dim(grad_out, table[q] * rows, rows, 2) for q in range(per)])
         received.append(send if k == 0 else lax.ppermute(send, "chan", shift_pairs(chans, k)))
+    return received
+
+
+def grad_blocks(received):
+    chans = lax.axis_size("chan")
+    filts = lax.axis_size("filt")
+    chan = lax.axis_index("chan")
+    turn = lambda f, r: r if f % 2 == 0 else chans - 1 - r
+    group_of = lambda c, f: f * chans + turn(f, c)
+    need = [[[f for f in range(filts) if group_of(t, f) // filts == r] for r in range(chans)] for t in range(chans)]
+    per = received[0].shape[0]
     received = jnp.concatenate(received)
     slot = [[0] * filts for _ in range(chans)]
     for t in range(chans):
@@ -163,8 +174,10 @@
 
 def local(volume, plane_weight, depth_weight, grad_out):
     weight = gather_weight(plane_weight)
+    received = grad_rows(grad_out)
+    volume, received = lax.optimization_barrier((volume, received))
     mid = forward(volume, weight, depth_weight)
-    all_filters = backward(grad_out, weight, depth_weight)
+    all_filters = grad_blocks(received)
     deep = halo(jnp.concatenate([mid, all_filters]), "slab", 1)
     output = forward_out(deep[: mid.shape[0]], depth_weight)
     grad_in = backward_in(deep[mid.shape[0] :], weight, depth_weight)

time: 94.8 us -> 98.9 us (1.043)
  waiting for transfers between devices: 27.6 us -> 30 us
  local copies, waits for them, and re-layouts: 17.3 us -> 18.5 us
    all_to_all x1, waiting for transfers between devices: 2.39 us -> 9.76 us  [gather_weight(): by_filt = lax.all_to_all(spread, 'filt', 0, 4, tiled=True)[0]]
    ppermute x1, waiting for transfers between devices: 6.8 us -> 0.42 us  [grad_rows(): lax.ppermute(send, 'chan', shift_pairs(chans, k))]
    dynamic_slice x6, local copies, waits for them, and re-layouts: 0.37 us -> 2.34 us  [the longest x5 1.59 us: grad_rows(): lax.dynamic_slice_in_dim(grad_out, table[q] * rows, rows, 2)]
    ppermute x1, starting transfers between devices: 0.26 us -> 2.13 us  [grad_rows(): lax.ppermute(send, 'chan', shift_pairs(chans, k))]
    dynamic_slice x1, local copies, waits for them, and re-layouts: 3.07 us -> 1.34 us  [forward(): lax.dynamic_slice_in_dim(padded, (c * filts + filt) * rows, rows + 2, 2)]
    all_to_all x1, waiting for transfers between devices: 6.04 us -> 7.28 us  [grad_blocks(): all_filters = lax.all_to_all(blocks, 'filt', 0, 0, tiled=True)]
    all_to_all x1, local copies, waits for them, and re-layouts: 0.03 us -> 1.08 us  [grad_blocks(): all_filters = lax.all_to_all(blocks, 'filt', 0, 0, tiled=True)]
    unnamed x26 -> x20, local copies, waits for them, and re-layouts: 4.92 us -> 4.91 us
where the time goes in v17:
time: 98.9 us; the launch traced here: 97.7 us
  waiting for transfers between devices  30 us (30%)
  starting transfers between devices  28.2 us (29%)
  local copies, waits for them, and re-layouts  18.5 us (19%)
  other arithmetic  11.4 us (12%)
  matrix products  5.77 us (6%)
  between operations  3.78 us (4%)
    all_to_all x1, waiting for transfers between devices, gather_weight(): by_filt = lax.all_to_all(spread, 'filt', 0, 4, tiled=True)[0]  9.76 us
    all_to_all x1, waiting for transfers between devices, grad_blocks(): all_filters = lax.all_to_all(blocks, 'filt', 0, 0, tiled=True)  7.28 us
    ppermute x2, starting transfers between devices, halo(): lax.ppermute(lax.slice_in_dim(x, length - 1, length, axis=dim), axis, up)  6.61 us
    all_to_all x1, starting transfers between devices, forward_out(): return lax.all_to_all(out, 'filt', 0, 2, tiled=True)  5.62 us
    ppermute x1, waiting for transfers between devices, backward_in(): lax.ppermute(lax.dynamic_slice_in_dim(grad_in, target * c_loc, c_loc, 0),...  5 us
    unnamed x20, local copies, waits for them, and re-layouts  4.91 us
    all_to_all x1, starting transfers between devices, gather_weight(): by_filt = lax.all_to_all(spread, 'filt', 0, 4, tiled=True)[0]  4.59 us
    ppermute x2, waiting for transfers between devices, halo(): after = lax.ppermute(lax.slice_in_dim(x, 0, 1, axis=dim), axis, down)  4.4 us
  transfers between devices with their start and end apart: 11, of which 6 were waited for; matrix products, arithmetic and copies ran while one was open for 24% of the time, Pallas kernels for 0%

profile of v17, /device:TPU:1, one launch (start us, length us, event | category | flops | bytes accessed | tf_op | source)
XLA Modules:
  0.0 97.7 jit_solution(7554489493387916991)
XLA Ops:
  5.2 1.5 %constant_dynamic-slice_fusion.2 = (bf16[64,2,4,128]{3,2,1,0:T(4,128)(2,1)S(1)}, bf16[64,2,4,128]{3,2,1,0:T(4,128)(2,1)S(1)}, bf16[64,2,4,128]{3,2,1,0:T(4,128)(2,1)S(1)}, bf16[64,2,4,128]{3,2,1,0:T(4,128)(2,1)S(1)}) fusion(bf16[64,2,16,128]{3,2,1,0:T(8,128)(2,1)} %param.10, s32[]{:T(128)S(6)} %select_n.103, s32[]{:T(128)S(6)} %select_n.102, ...), kind=kLoop, calls=%fused_computation.63 | loop fusion | bytes 1048592 | tf_op jit(solution)/shard_map/dynamic_slice | solution.py:128
  6.8 2.1 %collective-permute-start = (bf16[2,64,2,4,128]{4,1,3,2,0:T(8,128)(2,1)S(1)}, bf16[2,64,2,4,128]{4,1,3,2,0:T(8,128)(2,1)}, u32[]{:S(2)}, u32[]{:S(2)}) collective-permute-start(bf16[2,64,2,4,128]{4,1,3,2,0:T(8,128)(2,1)S(1)} %pad_maximum_fusion.4), channel_id=1, source_target_pairs={{0,4},{4,0},{1,5},{5,1},{2,6},{6,2},{3,7},{7,3},{8,12},{12,8},{9,1... | collective-permute-start | bytes 786440 | tf_op jit(solution)/shard_map/ppermute | solution.py:129
  9.0 1.0 broadcast_in_dim.28
  9.9 4.6 %all-to-all-start = ((bf16[4,3,3,128,64]{3,4,2,1,0:T(8,128)(2,1)}), bf16[4,3,3,128,64]{3,4,2,1,0:T(8,128)(2,1)S(1)}, u32[]{:S(2)}, u32[]{:S(2)}) async-start(bf16[4,3,3,128,64]{3,4,2,1,0:T(8,128)(2,1)} %broadcast_in_dim.28), calls=%async_computation | async-start | bytes 1179648 | tf_op jit(solution)/shard_map/all_to_all | solution.py:77
  15.1 1.3 %pad_dynamic-slice_fusion = (bf16[128,2,6,128]{3,2,1,0:T(8,128)(2,1)S(1)}, bf16[128,2,6,128]{3,2,1,0:T(8,128)(2,1)}) fusion(s32[]{:T(128)S(6)} %select_n.107, bf16[128,2,32,128]{3,2,1,0:T(8,128)(2,1)S(1)} %copy-done, s32[]{:T(128)S(6)} %select_n.106), kind=kLoop, calls=%fused_computation.1 | loop fusion | bytes 2883592 | tf_op jit(solution)/shard_map/dynamic_slice | solution.py:96
  16.4 1.1 %collective-permute-start.1 = (bf16[128,2,6,128]{3,2,1,0:T(8,128)(2,1)}, bf16[128,2,6,128]{3,2,1,0:T(8,128)(2,1)}, u32[]{:S(2)}, u32[]{:S(2)}) collective-permute-start(bf16[128,2,6,128]{3,2,1,0:T(8,128)(2,1)} %get-tuple-element.17), channel_id=1, source_target_pairs={{0,4},{4,0},{1,5},{5,1},{2,6},{6,2},{3,7},{7,3},{8,12},{12,8},{9,1... | collective-permute-start | bytes 1179656 | tf_op jit(solution)/shard_map/ppermute | solution.py:99
  17.6 1.0 %pad_maximum_fusion.2 = bf16[4,64,2,4,128]{4,1,3,2,0:T(8,128)(2,1)S(1)} fusion(bf16[2,64,2,4,128]{4,1,3,2,0:T(8,128)(2,1)} %collective-permute-done, bf16[2,64,2,4,128]{4,1,3,2,0:T(8,128)(2,1)S(1)} %pad_maximum_fusion.3), kind=kLoop, calls=%fused_computation.49 | loop fusion | flops 262144 | bytes 1048576 | tf_op jit(solution)/shard_map/concatenate | solution.py:141
  19.2 0.9 broadcast_select_fusion
  20.1 9.8 %all-to-all-done = bf16[4,3,3,128,64]{3,4,2,1,0:T(8,128)(2,1)S(1)} async-done(((bf16[4,3,3,128,64]{3,4,2,1,0:T(8,128)(2,1)}), bf16[4,3,3,128,64]{3,4,2,1,0:T(8,128)(2,1)S(1)}, u32[]{:S(2)}, u32[]{:S(2)}) %all-to-all-start) | async-done | bytes 589856 | tf_op jit(solution)/shard_map/all_to_all | solution.py:77
  29.9 4.1 %all-to-all-start.1 = ((bf16[4,64,2,4,128]{4,1,3,2,0:T(8,128)(2,1)}), bf16[4,64,2,4,128]{4,1,3,2,0:T(8,128)(2,1)}, u32[]{:S(2)}, u32[]{:S(2)}) async-start(bf16[4,64,2,4,128]{4,1,3,2,0:T(8,128)(2,1)} %broadcast_select_fusion), calls=%async_computation.1 | async-start | bytes 1048576 | tf_op jit(solution)/shard_map/all_to_all | solution.py:149
  34.6 3.2 %fusion.10 = bf16[256,6,2,128]{3,1,2,0:T(8,128)(2,1)S(1)} fusion(s32[]{:T(128)S(6)} %select_n.109, bf16[128,2,6,128]{3,2,1,0:T(8,128)(2,1)} %collective-permute-done.1, bf16[128,2,6,128]{3,2,1,0:T(8,128)(2,1)S(1)} %get-tuple-element.16), kind=kLoop, calls=%fused_computation.27 | loop fusion | flops 1179648 | bytes 1572868 | tf_op jit(solution)/shard_map/jit(_roll_dynamic)/dynamic_slice | solution.py:19
  37.9 1.3 %copy.93 = bf16[256,6,2,128]{0,2,3,1:T(2,128)(2,1)S(1)} copy(bf16[256,6,2,128]{3,1,2,0:T(8,128)(2,1)S(1)} %fusion.10) | data formatting | bytes 1572864
  40.8 7.3 %all-to-all-done.1 = bf16[4,64,2,4,128]{4,1,3,2,0:T(8,128)(2,1)} async-done(((bf16[4,64,2,4,128]{4,1,3,2,0:T(8,128)(2,1)}), bf16[4,64,2,4,128]{4,1,3,2,0:T(8,128)(2,1)}, u32[]{:S(2)}, u32[]{:S(2)}) %all-to-all-start.1) | async-done | bytes 524320 | tf_op jit(solution)/shard_map/all_to_all | solution.py:149
  48.1 1.1 %copy.71 = bf16[4,64,2,4,128]{4,1,0,3,2:T(8,128)(2,1)S(1)} copy(bf16[4,64,2,4,128]{4,1,3,2,0:T(8,128)(2,1)} %all-to-all-done.1) | data formatting | bytes 1048576 | tf_op jit(solution)/shard_map/all_to_all | solution.py:149
  49.5 1.9 %fusion.6 = bf16[3,3,256,256]{3,2,1,0:T(8,128)(2,1)S(1)} fusion(s32[]{:T(128)S(6)} %select_n.109, bf16[3,3,128,256]{3,2,1,0:T(8,128)(2,1)} %collective-permute-done.2, bf16[3,3,128,256]{3,2,1,0:T(8,128)(2,1)S(1)} %copy.67), kind=kLoop, calls=%fused_computation.23 | loop fusion | flops 4718592 | bytes 2359300 | tf_op jit(solution)/shard_map/jit(_roll_dynamic)/concatenate | solution.py:19
  51.4 1.5 %fusion.2 = bf16[4,16,17,256]{3,1,2,0:T(8,128)(2,1)S(1)} fusion(bf16[3,3,256,256]{3,2,1,0:T(8,128)(2,1)S(1)} %fusion.6, bf16[256,6,2,8,19]{0,2,4,3,1:T(2,128)(2,1)S(1)} %fusion.13, pred[16,17]{0,1:T(8,128)(4,1)S(1)} %copy-done.7), kind=kOutput, calls=%fused_computation.17 | convolution fusion | flops 1284014080 | bytes 2670864 | tf_op jit(solution)/shard_map/conv_general_dilated | solution.py:52
  53.9 4.5 %collective-permute-start.3 = (bf16[512,1,4,128]{0,2,3,1:T(4,128)(2,1)S(1)}, bf16[512,1,4,128]{0,2,3,1:T(4,128)(2,1)S(1)}, u32[]{:S(2)}, u32[]{:S(2)}) collective-permute-start(bf16[512,1,4,128]{0,2,3,1:T(4,128)(2,1)S(1)} %get-tuple-element.18), channel_id=1, source_target_pairs={{0,8},{8,16},{16,24},{1,9},{9,17},{17,25},{2,10},{10,18},{18,26},{... | collective-permute-start | bytes 1572872 | tf_op jit(solution)/shard_map/ppermute | solution.py:46
  58.4 2.1 %collective-permute-start.4 = (bf16[512,1,4,128]{0,2,3,1:T(4,128)(2,1)S(1)}, bf16[512,1,4,128]{0,2,3,1:T(4,128)(2,1)S(1)}, u32[]{:S(2)}, u32[]{:S(2)}) collective-permute-start(bf16[512,1,4,128]{0,2,3,1:T(4,128)(2,1)S(1)} %get-tuple-element.19), channel_id=1, source_target_pairs={{8,0},{16,8},{24,16},{9,1},{17,9},{25,17},{10,2},{18,10},{26,18},{... | collective-permute-start | bytes 1572872 | tf_op jit(solution)/shard_map/ppermute | solution.py:47
  61.3 3.2 %collective-permute-done.3 = bf16[512,1,4,128]{0,2,3,1:T(4,128)(2,1)S(1)} collective-permute-done((bf16[512,1,4,128]{0,2,3,1:T(4,128)(2,1)S(1)}, bf16[512,1,4,128]{0,2,3,1:T(4,128)(2,1)S(1)}, u32[]{:S(2)}, u32[]{:S(2)}) %collective-permute-start.3) | collective-permute-done | bytes 524320 | tf_op jit(solution)/shard_map/ppermute | solution.py:46
  64.5 4.4 %collective-permute-done.4 = bf16[512,1,4,128]{0,2,3,1:T(4,128)(2,1)S(1)} collective-permute-done((bf16[512,1,4,128]{0,2,3,1:T(4,128)(2,1)S(1)}, bf16[512,1,4,128]{0,2,3,1:T(4,128)(2,1)S(1)}, u32[]{:S(2)}, u32[]{:S(2)}) %collective-permute-start.4) | collective-permute-done | bytes 524320 | tf_op jit(solution)/shard_map/ppermute | solution.py:47
  68.9 1.0 pad_maximum_fusion
  70.8 1.4 %convolution_convert_fusion = bf16[2,4,8,16,256]{4,2,3,1,0:T(8,128)(2,1)S(1)} fusion(bf16[256,4,4,8,16]{0,2,4,3,1:T(4,128)(2,1)S(1)} %bitcast.90, bf16[3,256,256]{2,1,0:T(8,128)(2,1)S(1)} %copy-done.4), kind=kOutput, calls=%fused_computation.19 | convolution fusion | flops 402915328 | bytes 1966080 | tf_op jit(solution)/shard_map/conv_general_dilated | solution.py:63
  72.4 2.1 %collective-permute-start.5 = (bf16[256,2,1,128]{0,3,2,1:T(8,128)(2,1)S(1)}, bf16[256,2,1,128]{0,3,2,1:T(8,128)(2,1)S(1)}, u32[]{:S(2)}, u32[]{:S(2)}) collective-permute-start(bf16[256,2,1,128]{0,3,2,1:T(8,128)(2,1)S(1)} %get-tuple-element.22), channel_id=1, source_target_pairs={{0,4},{4,5},{5,1},{1,2},{2,6},{6,7},{7,3},{8,12},{12,13},{13,9},{9... | collective-permute-start | bytes 393224 | tf_op jit(solution)/shard_map/ppermute | solution.py:46
  74.5 1.3 %collective-permute-start.6 = (bf16[256,2,1,128]{0,3,2,1:T(8,128)(2,1)S(1)}, bf16[256,2,1,128]{0,3,2,1:T(8,128)(2,1)S(1)}, u32[]{:S(2)}, u32[]{:S(2)}) collective-permute-start(bf16[256,2,1,128]{0,3,2,1:T(8,128)(2,1)S(1)} %get-tuple-element.23), channel_id=1, source_target_pairs={{4,0},{5,4},{1,5},{2,1},{6,2},{7,6},{3,7},{12,8},{13,12},{9,13},{1... | collective-permute-start | bytes 393224 | tf_op jit(solution)/shard_map/ppermute | solution.py:47
  75.8 1.4 %convolution_convert_fusion.1 = bf16[2,4,8,16,256]{4,2,3,1,0:T(8,128)(2,1)S(1)} fusion(bf16[256,4,4,8,16]{0,2,4,3,1:T(4,128)(2,1)S(1)} %bitcast.89, bf16[3,256,256]{2,1,0:T(8,128)(2,1)S(1)} %copy-done.3), kind=kOutput, calls=%fused_computation.20 | convolution fusion | flops 402915328 | bytes 1966080 | tf_op jit(solution)/shard_map/conv_general_dilated | solution.py:63
  77.3 1.1 %copy.77 = bf16[256,2,4,128]{3,2,1,0:T(4,128)(2,1)} copy(bf16[256,2,4,128]{0,3,2,1:T(8,128)(2,1)S(1)} %bitcast.86) | data formatting | bytes 1048576 | tf_op jit(solution)/shard_map/convert_element_type | solution.py:109
  78.4 5.6 %all-to-all-start.2 = ((bf16[256,2,4,128]{3,2,1,0:T(4,128)(2,1)}), bf16[256,2,4,128]{3,2,1,0:T(4,128)(2,1)S(1)}, u32[]{:S(2)}, u32[]{:S(2)}) async-start(bf16[256,2,4,128]{3,2,1,0:T(4,128)(2,1)} %copy.77), calls=%async_computation.2 | async-start | bytes 1048576 | tf_op jit(solution)/shard_map/all_to_all | solution.py:110
  86.6 1.5 %fusion.3 = bf16[4,16,17,256]{3,1,2,0:T(8,128)(2,1)S(1)} fusion(bf16[3,3,256,256]{3,2,1,0:T(8,128)(2,1)S(1)} %copy-done.2, bf16[256,6,2,8,19]{0,2,4,3,1:T(2,128)(2,1)S(1)} %fusion.14, pred[16,17]{0,1:T(8,128)(4,1)S(1)} %copy-done.7), kind=kOutput, calls=%fused_computation.18 | convolution fusion | flops 1284014080 | bytes 2670864 | tf_op jit(solution)/shard_map/conv_general_dilated | solution.py:52
  89.0 5.0 %collective-permute-done.7 = bf16[128,2,4,128]{0,2,3,1:T(4,128)(2,1)S(1)} collective-permute-done((bf16[128,2,4,128]{0,2,3,1:T(4,128)(2,1)S(1)}, bf16[128,2,4,128]{0,2,3,1:T(4,128)(2,1)S(1)}, u32[]{:S(2)}, u32[]{:S(2)}) %collective-permute-start.7) | collective-permute-done | bytes 262176 | tf_op jit(solution)/shard_map/ppermute | solution.py:171
  94.0 1.0 %fusion.21 = bf16[128,2,8,128]{0,2,3,1:T(8,128)(2,1)S(1)} fusion(s32[]{:T(128)S(6)} %select_n.120, bf16[128,2,4,128]{0,2,3,1:T(4,128)(2,1)S(1)} %collective-permute-done.7, bf16[128,2,4,128]{0,2,3,1:T(4,128)(2,1)S(1)} %get-tuple-element.20), kind=kLoop, calls=%fused_computation.45 | loop fusion | flops 2097152 | bytes 1048580 | tf_op jit(solution)/shard_map/jit(_roll_dynamic)/concatenate | solution.py:19
  95.1 1.3 %copy.88 = bf16[128,2,8,128]{3,2,1,0:T(8,128)(2,1)} copy(bf16[128,2,8,128]{0,2,3,1:T(8,128)(2,1)S(1)} %fusion.21) | data formatting | bytes 1048576
  96.5 1.1 %copy.87 = bf16[64,2,16,128]{3,2,1,0:T(8,128)(2,1)} copy(bf16[64,2,16,128]{3,0,2,1:T(8,128)(2,1)S(1)} %bitcast.88) | data formatting | bytes 1048576
  (61 shorter events, 12.1 us)
Async XLA Ops:
  0.6 13.9 %copy-start.6 = (s32[2,4]{1,0:T(2,128)S(1)}, s32[2,4]{1,0:T(2,128)}, u32[]{:S(2)}) copy-start(s32[2,4]{1,0:T(2,128)} %constant.124.clone) | copy-start | bytes 100
  0.6 8.3 %copy-start.5 = (bf16[3,3,128,64]{2,3,1,0:T(8,128)(2,1)S(1)}, bf16[3,3,128,64]{2,3,1,0:T(8,128)(2,1)}, u32[]{:S(2)}) copy-start(bf16[3,3,128,64]{2,3,1,0:T(8,128)(2,1)} %param.8) | copy-start | bytes 442372
  6.7 8.4 %copy-start = (bf16[128,2,32,128]{3,2,1,0:T(8,128)(2,1)S(1)}, bf16[128,2,32,128]{3,2,1,0:T(8,128)(2,1)}, u32[]{:S(2)}) copy-start(bf16[128,2,32,128]{3,2,1,0:T(8,128)(2,1)} %param.7) | copy-start | bytes 6291460
  6.8 8.3 %collective-permute-start = (bf16[2,64,2,4,128]{4,1,3,2,0:T(8,128)(2,1)S(1)}, bf16[2,64,2,4,128]{4,1,3,2,0:T(8,128)(2,1)}, u32[]{:S(2)}, u32[]{:S(2)}) collective-permute-start(bf16[2,64,2,4,128]{4,1,3,2,0:T(8,128)(2,1)S(1)} %pad_maximum_fusion.4), channel_id=1, source_target_pairs={{0,4},{4,0},{1,5},{5,1},{2,6},{6,2},{3,7},{7,3},{8,12},{12,8},{9,1... | collective-permute-start | bytes 786440 | tf_op jit(solution)/shard_map/ppermute | solution.py:129
  9.9 20.0 %all-to-all-start = ((bf16[4,3,3,128,64]{3,4,2,1,0:T(8,128)(2,1)}), bf16[4,3,3,128,64]{3,4,2,1,0:T(8,128)(2,1)S(1)}, u32[]{:S(2)}, u32[]{:S(2)}) async-start(bf16[4,3,3,128,64]{3,4,2,1,0:T(8,128)(2,1)} %broadcast_in_dim.28), calls=%async_computation | async-start | bytes 1179648 | tf_op jit(solution)/shard_map/all_to_all | solution.py:77
  16.4 18.2 %collective-permute-start.1 = (bf16[128,2,6,128]{3,2,1,0:T(8,128)(2,1)}, bf16[128,2,6,128]{3,2,1,0:T(8,128)(2,1)}, u32[]{:S(2)}, u32[]{:S(2)}) collective-permute-start(bf16[128,2,6,128]{3,2,1,0:T(8,128)(2,1)} %get-tuple-element.17), channel_id=1, source_target_pairs={{0,4},{4,0},{1,5},{5,1},{2,6},{6,2},{3,7},{7,3},{8,12},{12,8},{9,1... | collective-permute-start | bytes 1179656 | tf_op jit(solution)/shard_map/ppermute | solution.py:99
  29.9 18.2 %all-to-all-start.1 = ((bf16[4,64,2,4,128]{4,1,3,2,0:T(8,128)(2,1)}), bf16[4,64,2,4,128]{4,1,3,2,0:T(8,128)(2,1)}, u32[]{:S(2)}, u32[]{:S(2)}) async-start(bf16[4,64,2,4,128]{4,1,3,2,0:T(8,128)(2,1)} %broadcast_select_fusion), calls=%async_computation.1 | async-start | bytes 1048576 | tf_op jit(solution)/shard_map/all_to_all | solution.py:149
  34.3 15.1 %collective-permute-start.2 = (bf16[3,3,128,256]{3,2,1,0:T(8,128)(2,1)S(1)}, bf16[3,3,128,256]{3,2,1,0:T(8,128)(2,1)}, u32[]{:S(2)}, u32[]{:S(2)}) collective-permute-start(bf16[3,3,128,256]{3,2,1,0:T(8,128)(2,1)S(1)} %copy.67), channel_id=1, source_target_pairs={{0,4},{4,0},{1,5},{5,1},{2,6},{6,2},{3,7},{7,3},{8,12},{12,8},{9,1... | collective-permute-start | bytes 1769480 | tf_op jit(solution)/shard_map/ppermute | solution.py:25
  40.8 10.6 %copy-start.7 = (pred[16,17]{0,1:T(8,128)(4,1)S(1)}, pred[16,17]{0,1:T(8,128)(4,1)}, u32[]{:S(2)}) copy-start(pred[16,17]{0,1:T(8,128)(4,1)} %constant.144) | copy-start | bytes 820
  51.4 1.5 %copy-start.1 = (bf16[3,3,256,256]{3,2,1,0:T(8,128)(2,1)}, bf16[3,3,256,256]{3,2,1,0:T(8,128)(2,1)S(1)}, u32[]{:S(2)}) copy-start(bf16[3,3,256,256]{3,2,1,0:T(8,128)(2,1)S(1)} %fusion.6) | copy-start | bytes 3538948
  52.9 7.6 %copy-start.3 = (bf16[3,256,256]{2,1,0:T(8,128)(2,1)S(1)}, bf16[3,256,256]{2,1,0:T(8,128)(2,1)}, u32[]{:S(2)}) copy-start(bf16[3,256,256]{2,1,0:T(8,128)(2,1)} %param.9) | copy-start | bytes 1179652
  53.9 10.6 %collective-permute-start.3 = (bf16[512,1,4,128]{0,2,3,1:T(4,128)(2,1)S(1)}, bf16[512,1,4,128]{0,2,3,1:T(4,128)(2,1)S(1)}, u32[]{:S(2)}, u32[]{:S(2)}) collective-permute-start(bf16[512,1,4,128]{0,2,3,1:T(4,128)(2,1)S(1)} %get-tuple-element.18), channel_id=1, source_target_pairs={{0,8},{8,16},{16,24},{1,9},{9,17},{17,25},{2,10},{10,18},{18,26},{... | collective-permute-start | bytes 1572872 | tf_op jit(solution)/shard_map/ppermute | solution.py:46
  58.4 10.5 %collective-permute-start.4 = (bf16[512,1,4,128]{0,2,3,1:T(4,128)(2,1)S(1)}, bf16[512,1,4,128]{0,2,3,1:T(4,128)(2,1)S(1)}, u32[]{:S(2)}, u32[]{:S(2)}) collective-permute-start(bf16[512,1,4,128]{0,2,3,1:T(4,128)(2,1)S(1)} %get-tuple-element.19), channel_id=1, source_target_pairs={{8,0},{16,8},{24,16},{9,1},{17,9},{25,17},{10,2},{18,10},{26,18},{... | collective-permute-start | bytes 1572872 | tf_op jit(solution)/shard_map/ppermute | solution.py:47
  69.8 1.0 %copy-start.4 = (bf16[3,256,256]{2,1,0:T(8,128)(2,1)S(1)}, bf16[3,256,256]{2,1,0:T(8,128)(2,1)}, u32[]{:S(2)}) copy-start(bf16[3,256,256]{2,1,0:T(8,128)(2,1)} %rev.4) | copy-start | bytes 1179652
  72.4 11.7 %collective-permute-start.5 = (bf16[256,2,1,128]{0,3,2,1:T(8,128)(2,1)S(1)}, bf16[256,2,1,128]{0,3,2,1:T(8,128)(2,1)S(1)}, u32[]{:S(2)}, u32[]{:S(2)}) collective-permute-start(bf16[256,2,1,128]{0,3,2,1:T(8,128)(2,1)S(1)} %get-tuple-element.22), channel_id=1, source_target_pairs={{0,4},{4,5},{5,1},{1,2},{2,6},{6,7},{7,3},{8,12},{12,13},{13,9},{9... | collective-permute-start | bytes 393224 | tf_op jit(solution)/shard_map/ppermute | solution.py:46
  74.5 9.5 %collective-permute-start.6 = (bf16[256,2,1,128]{0,3,2,1:T(8,128)(2,1)S(1)}, bf16[256,2,1,128]{0,3,2,1:T(8,128)(2,1)S(1)}, u32[]{:S(2)}, u32[]{:S(2)}) collective-permute-start(bf16[256,2,1,128]{0,3,2,1:T(8,128)(2,1)S(1)} %get-tuple-element.23), channel_id=1, source_target_pairs={{4,0},{5,4},{1,5},{2,1},{6,2},{7,6},{3,7},{12,8},{13,12},{9,13},{1... | collective-permute-start | bytes 393224 | tf_op jit(solution)/shard_map/ppermute | solution.py:47
  78.4 18.0 %all-to-all-start.2 = ((bf16[256,2,4,128]{3,2,1,0:T(4,128)(2,1)}), bf16[256,2,4,128]{3,2,1,0:T(4,128)(2,1)S(1)}, u32[]{:S(2)}, u32[]{:S(2)}) async-start(bf16[256,2,4,128]{3,2,1,0:T(4,128)(2,1)} %copy.77), calls=%async_computation.2 | async-start | bytes 1048576 | tf_op jit(solution)/shard_map/all_to_all | solution.py:110
  85.0 1.6 %copy-start.2 = (bf16[3,3,256,256]{3,2,1,0:T(8,128)(2,1)S(1)}, bf16[3,3,256,256]{3,2,1,0:T(8,128)(2,1)}, u32[]{:S(2)}) copy-start(bf16[3,3,256,256]{3,2,1,0:T(8,128)(2,1)} %copy-done.1) | copy-start | bytes 3538948
  88.8 5.3 %collective-permute-start.7 = (bf16[128,2,4,128]{0,2,3,1:T(4,128)(2,1)S(1)}, bf16[128,2,4,128]{0,2,3,1:T(4,128)(2,1)S(1)}, u32[]{:S(2)}, u32[]{:S(2)}) collective-permute-start(bf16[128,2,4,128]{0,2,3,1:T(4,128)(2,1)S(1)} %get-tuple-element.21), channel_id=1, source_target_pairs={{0,4},{1,5},{2,6},{3,7},{4,0},{5,1},{6,2},{7,3},{8,12},{9,13},{10,... | collective-permute-start | bytes 786440 | tf_op jit(solution)/shard_map/ppermute | solution.py:171

commit v18 on v15

--- a/solution.py
+++ b/solution.py
@@ -73,9 +73,20 @@
 
 def gather_weight(weight):
     filts = lax.axis_size("filt")
-    spread = jnp.broadcast_to(weight[None], (filts,) + weight.shape)
-    by_filt = lax.all_to_all(spread, "filt", 0, 4, tiled=True)[0]
-    return gather_blocks(by_filt, "chan", 2)
+    chans = lax.axis_size("chan")
+    slabs = lax.axis_size("slab")
+    core = lax.axis_index("slab") % 2
+    c_loc = weight.shape[2]
+    half = c_loc // 2
+    mine = lax.dynamic_slice_in_dim(weight, core * half, half, 2)
+    spread = jnp.broadcast_to(mine[None], (filts,) + mine.shape)
+    by_filt = gather_blocks(lax.all_to_all(spread, "filt", 0, 4, tiled=True)[0], "chan", 2)
+    other = lax.ppermute(by_filt, "slab", [(i, i ^ 1) for i in range(slabs)])
+    first = jnp.where(core == 0, by_filt, other)
+    second = jnp.where(core == 0, other, by_filt)
+    split = lambda w: w.reshape(3, 3, chans, 1, half, w.shape[-1])
+    whole = jnp.concatenate([split(first), split(second)], axis=3)
+    return whole.reshape(3, 3, chans * c_loc, whole.shape[-1])
 
 
 def sub_block(chan, filt, filts):

time: 94.8 us -> 94.2 us (level)
  waiting for transfers between devices: 27.6 us -> 20.9 us
  starting transfers between devices: 28 us -> 31.2 us
  local copies, waits for them, and re-layouts: 17.3 us -> 19.8 us
    all_to_all x1, waiting for transfers between devices: 6.04 us -> 3.37 us  [backward(): all_filters = lax.all_to_all(blocks, 'filt', 0, 0, tiled=True)]
    ppermute x0 -> x1, starting transfers between devices: none -> 2.58 us  [gather_weight(): other = lax.ppermute(by_filt, 'slab', [(i, i ^ 1) for i in range(slabs)])]
    all_to_all x1, waiting for transfers between devices: 2.39 us -> 0.01 us  [gather_weight(): lax.all_to_all(spread, 'filt', 0, 4, tiled=True)[0]]
    all_to_all x1, starting transfers between devices: 6.16 us -> 4.52 us  [forward_out(): return lax.all_to_all(out, 'filt', 0, 2, tiled=True)]
    ppermute x1, starting transfers between devices: 0.48 us -> 2.09 us  [gather_blocks(): lax.ppermute(x, axis, shift_pairs(n, k))]
    unnamed x26, local copies, waits for them, and re-layouts: 4.92 us -> 6.47 us
    concatenate x2, other arithmetic: 2.95 us -> 1.53 us  [order_blocks(): return jnp.roll(stacked, (me + 1) * block, axis=dim)]
    select_n x0 -> x1, other arithmetic: none -> 1.22 us  [gather_weight(): first = jnp.where(core == 0, by_filt, other)]
  transfers between devices with their start and end apart: 11 -> 12, of which waited for: 6 -> 6; matrix products, arithmetic and copies ran while one was open for 24% -> 27% of each run, Pallas kernels for 0% -> 0%
where the time goes in v18:
time: 94.2 us; the launch traced here: 93.5 us
  starting transfers between devices  31.2 us (33%)
  waiting for transfers between devices  20.9 us (22%)
  local copies, waits for them, and re-layouts  19.8 us (21%)
  other arithmetic  12.2 us (13%)
  matrix products  5.75 us (6%)
  between operations  3.71 us (4%)
    ppermute x2, starting transfers between devices, halo(): lax.ppermute(lax.slice_in_dim(x, length - 1, length, axis=dim), axis, up)  6.58 us
    unnamed x26, local copies, waits for them, and re-layouts  6.47 us
    ppermute x1, waiting for transfers between devices, backward(): lax.ppermute(send, 'chan', shift_pairs(chans, k))  6.26 us
    all_to_all x1, starting transfers between devices, forward_out(): return lax.all_to_all(out, 'filt', 0, 2, tiled=True)  4.52 us
    ppermute x2, waiting for transfers between devices, halo(): after = lax.ppermute(lax.slice_in_dim(x, 0, 1, axis=dim), axis, down)  4.5 us
    all_to_all x1, starting transfers between devices, gather_weight(): lax.all_to_all(spread, 'filt', 0, 4, tiled=True)[0]  4.45 us
    ppermute x1, waiting for transfers between devices, backward_in(): lax.ppermute(lax.dynamic_slice_in_dim(grad_in, target * c_loc, c_loc, 0),...  4.17 us
    all_to_all x1, starting transfers between devices, backward(): all_filters = lax.all_to_all(blocks, 'filt', 0, 0, tiled=True)  4.15 us
  transfers between devices with their start and end apart: 12, of which 6 were waited for; matrix products, arithmetic and copies ran while one was open for 27% of the time, Pallas kernels for 0%

profile of v18, /device:TPU:1, one launch (start us, length us, event | category | flops | bytes accessed | tf_op | source)
XLA Modules:
  0.0 93.5 jit_solution(15734077683484393653)
XLA Ops:
  0.7 3.0 %pad_dynamic-slice_fusion = (bf16[128,2,6,128]{3,2,1,0:T(8,128)(2,1)S(1)}, bf16[128,2,6,128]{3,2,1,0:T(8,128)(2,1)}) fusion(s32[]{:T(128)S(6)} %select_n.125, bf16[128,2,32,128]{3,2,1,0:T(8,128)(2,1)} %param.7, s32[]{:T(128)S(6)} %select_n.124), kind=kLoop, calls=%fused_computation.1 | loop fusion | bytes 2883592 | tf_op jit(solution)/shard_map/dynamic_slice | solution.py:107
  3.7 2.1 %collective-permute-start = (bf16[128,2,6,128]{3,2,1,0:T(8,128)(2,1)}, bf16[128,2,6,128]{3,2,1,0:T(8,128)(2,1)}, u32[]{:S(2)}, u32[]{:S(2)}) collective-permute-start(bf16[128,2,6,128]{3,2,1,0:T(8,128)(2,1)} %get-tuple-element.13), channel_id=1, source_target_pairs={{0,4},{4,0},{1,5},{5,1},{2,6},{6,2},{3,7},{7,3},{8,12},{12,8},{9,1... | collective-permute-start | bytes 1179656 | tf_op jit(solution)/shard_map/ppermute | solution.py:110
  6.2 1.2 %reshape.130 = bf16[4,2,18432]{2,1,0:T(2,128)(2,1)} reshape(bf16[4,3,3,64,64]{4,3,2,1,0:T(8,128)(2,1)S(1)} %broadcast_in_dim.28) | data formatting | bytes 589824
  7.4 4.5 %all-to-all-start = ((bf16[4,2,18432]{2,1,0:T(2,128)(2,1)}), bf16[4,2,18432]{2,1,0:T(2,128)(2,1)S(1)}, u32[]{:S(2)}, u32[]{:S(2)}) async-start(bf16[4,2,18432]{2,1,0:T(2,128)(2,1)} %reshape.130), calls=%async_computation | async-start | bytes 589824 | tf_op jit(solution)/shard_map/all_to_all | solution.py:83
  16.4 6.3 %collective-permute-done.3 = bf16[2,64,2,4,128]{4,1,3,2,0:T(8,128)(2,1)S(1)} collective-permute-done((bf16[2,64,2,4,128]{4,1,3,2,0:T(8,128)(2,1)S(1)}, bf16[2,64,2,4,128]{4,1,3,2,0:T(8,128)(2,1)S(1)}, u32[]{:S(2)}, u32[]{:S(2)}) %collective-permute-start.3) | collective-permute-done | bytes 262176 | tf_op jit(solution)/shard_map/ppermute | solution.py:140
  24.6 2.1 %collective-permute-start.1 = (bf16[3,3,64,256]{3,2,1,0:T(8,128)(2,1)S(1)}, bf16[3,3,64,256]{3,2,1,0:T(8,128)(2,1)S(1)}, u32[]{:S(2)}, u32[]{:S(2)}) collective-permute-start(bf16[3,3,64,256]{3,2,1,0:T(8,128)(2,1)S(1)} %squeeze.6), channel_id=1, source_target_pairs={{0,4},{4,0},{1,5},{5,1},{2,6},{6,2},{3,7},{7,3},{8,12},{12,8},{9,1... | collective-permute-start | bytes 884744 | tf_op jit(solution)/shard_map/ppermute | solution.py:25
  27.6 4.2 %all-to-all-start.1 = ((bf16[4,64,2,4,128]{4,1,3,2,0:T(8,128)(2,1)}), bf16[4,64,2,4,128]{4,1,3,2,0:T(8,128)(2,1)S(1)}, u32[]{:S(2)}, u32[]{:S(2)}) async-start(bf16[4,64,2,4,128]{4,1,3,2,0:T(8,128)(2,1)} %broadcast_select_fusion.2), calls=%async_computation.1 | async-start | bytes 1048576 | tf_op jit(solution)/shard_map/all_to_all | solution.py:149
  32.7 2.6 %collective-permute-start.2 = (bf16[3,3,128,256]{3,2,1,0:T(8,128)(2,1)S(1)}, bf16[3,3,128,256]{3,2,1,0:T(8,128)(2,1)}, u32[]{:S(2)}, u32[]{:S(2)}) collective-permute-start(bf16[3,3,128,256]{3,2,1,0:T(8,128)(2,1)S(1)} %fusion.18), channel_id=1, source_target_pairs={{0,8},{8,0},{16,24},{24,16},{1,9},{9,1},{17,25},{25,17},{2,10},{10... | collective-permute-start | bytes 1769480 | tf_op jit(solution)/shard_map/ppermute | solution.py:84
  35.2 3.2 %fusion.7 = bf16[256,6,2,128]{3,1,2,0:T(8,128)(2,1)S(1)} fusion(s32[]{:T(128)S(6)} %select_n.127, bf16[128,2,6,128]{3,2,1,0:T(8,128)(2,1)} %collective-permute-done, bf16[128,2,6,128]{3,2,1,0:T(8,128)(2,1)S(1)} %get-tuple-element.12), kind=kLoop, calls=%fused_computation.25 | loop fusion | flops 1179648 | bytes 1572868 | tf_op jit(solution)/shard_map/jit(_roll_dynamic)/dynamic_slice | solution.py:19
  38.5 1.3 %copy.115 = bf16[256,6,2,128]{0,2,3,1:T(2,128)(2,1)S(1)} copy(bf16[256,6,2,128]{3,1,2,0:T(8,128)(2,1)S(1)} %fusion.7) | data formatting | bytes 1572864
  40.5 1.7 %fusion.10 = bf16[256,6,2,8,19]{0,2,4,3,1:T(2,128)(2,1)} fusion(bf16[256,6,2,7,2]{0,2,4,3,1:T(2,128)(2,1)S(1)} %slice.52, bf16[256,6,2,8,17]{0,2,4,3,1:T(2,128)(2,1)S(1)} %bitcast.84), kind=kLoop, calls=%fused_computation.34 | loop fusion | flops 2801664 | bytes 1855488 | tf_op jit(solution)/shard_map/conv_general_dilated | solution.py:52
  42.2 3.4 %all-to-all-done.1 = bf16[4,64,2,4,128]{4,1,3,2,0:T(8,128)(2,1)S(1)} async-done(((bf16[4,64,2,4,128]{4,1,3,2,0:T(8,128)(2,1)}), bf16[4,64,2,4,128]{4,1,3,2,0:T(8,128)(2,1)S(1)}, u32[]{:S(2)}, u32[]{:S(2)}) %all-to-all-start.1) | async-done | bytes 524320 | tf_op jit(solution)/shard_map/all_to_all | solution.py:149
  45.9 1.2 %broadcast_select_fusion.1 = (bf16[3,3,128,256]{3,2,1,0:T(8,128)(2,1)S(1)}, bf16[3,3,128,256]{3,2,1,0:T(8,128)(2,1)S(1)}) fusion(bf16[3,3,128,256]{3,2,1,0:T(8,128)(2,1)S(1)} %fusion.18, bf16[3,3,128,256]{3,2,1,0:T(8,128)(2,1)} %collective-permute-done.2, pred[]{:T(512)S(6)} %eq.20), kind=kLoop, calls=%fused_computation.45 | loop fusion | flops 589824 | bytes 2359297 | tf_op jit(solution)/shard_map/jit(_where)/select_n | solution.py:85
  47.3 1.5 %fusion.2 = bf16[4,16,17,256]{3,1,2,0:T(8,128)(2,1)S(1)} fusion(bf16[3,3,256,256]{3,2,1,0:T(8,128)(2,1)S(1)} %bitcast.96, bf16[256,6,2,8,19]{0,2,4,3,1:T(2,128)(2,1)S(1)} %copy-done.1, pred[16,17]{0,1:T(8,128)(4,1)S(1)} %copy-done.8), kind=kOutput, calls=%fused_computation.13 | convolution fusion | flops 1284014080 | bytes 2670864 | tf_op jit(solution)/shard_map/conv_general_dilated | solution.py:52
  49.7 4.7 %collective-permute-start.4 = (bf16[512,1,4,128]{0,2,3,1:T(4,128)(2,1)S(1)}, bf16[512,1,4,128]{0,2,3,1:T(4,128)(2,1)}, u32[]{:S(2)}, u32[]{:S(2)}) collective-permute-start(bf16[512,1,4,128]{0,2,3,1:T(4,128)(2,1)S(1)} %get-tuple-element.16), channel_id=1, source_target_pairs={{0,8},{8,16},{16,24},{1,9},{9,17},{17,25},{2,10},{10,18},{18,26},{... | collective-permute-start | bytes 1572872 | tf_op jit(solution)/shard_map/ppermute | solution.py:46
  54.4 2.1 %collective-permute-start.5 = (bf16[512,1,4,128]{0,2,3,1:T(4,128)(2,1)S(1)}, bf16[512,1,4,128]{0,2,3,1:T(4,128)(2,1)}, u32[]{:S(2)}, u32[]{:S(2)}) collective-permute-start(bf16[512,1,4,128]{0,2,3,1:T(4,128)(2,1)S(1)} %get-tuple-element.17), channel_id=1, source_target_pairs={{8,0},{16,8},{24,16},{9,1},{17,9},{25,17},{10,2},{18,10},{26,18},{... | collective-permute-start | bytes 1572872 | tf_op jit(solution)/shard_map/ppermute | solution.py:47
  56.5 1.8 %rev.4 = bf16[3,256,256]{2,1,0:T(8,128)(2,1)} reverse(bf16[3,256,256]{2,1,0:T(8,128)(2,1)} %param.9), dimensions={0} | reverse | bytes 786432 | tf_op jit(solution)/shard_map/rev | solution.py:160
  58.3 2.2 %collective-permute-done.4 = bf16[512,1,4,128]{0,2,3,1:T(4,128)(2,1)} collective-permute-done((bf16[512,1,4,128]{0,2,3,1:T(4,128)(2,1)S(1)}, bf16[512,1,4,128]{0,2,3,1:T(4,128)(2,1)}, u32[]{:S(2)}, u32[]{:S(2)}) %collective-permute-start.4) | collective-permute-done | bytes 524320 | tf_op jit(solution)/shard_map/ppermute | solution.py:46
  60.5 4.5 %collective-permute-done.5 = bf16[512,1,4,128]{0,2,3,1:T(4,128)(2,1)} collective-permute-done((bf16[512,1,4,128]{0,2,3,1:T(4,128)(2,1)S(1)}, bf16[512,1,4,128]{0,2,3,1:T(4,128)(2,1)}, u32[]{:S(2)}, u32[]{:S(2)}) %collective-permute-start.5) | collective-permute-done | bytes 524320 | tf_op jit(solution)/shard_map/ppermute | solution.py:47
  65.0 2.0 %pad_maximum_fusion = bf16[512,4,4,128]{0,2,3,1:T(4,128)(2,1)S(1)} fusion(bf16[512,1,4,128]{0,2,3,1:T(4,128)(2,1)} %collective-permute-done.5, bf16[256,2,4,128]{0,2,3,1:T(4,128)(2,1)S(1)} %copy.94, bf16[256,2,4,128]{0,2,3,1:T(4,128)(2,1)S(1)} %slice_bitcast_fusion, bf16[512,1,4,128]{0,2,3,1:T(4,128)(2,1)} %collective-permute-done.4), kind=kLoop, calls=%fused_computation.7 | loop fusion | flops 8388608 | bytes 4194304 | tf_op jit(solution)/shard_map/concatenate | solution.py:48
  68.0 1.4 %convolution_convert_fusion = bf16[2,4,8,16,256]{4,2,3,1,0:T(8,128)(2,1)S(1)} fusion(bf16[256,4,4,8,16]{0,2,4,3,1:T(4,128)(2,1)S(1)} %bitcast.99, bf16[3,256,256]{2,1,0:T(8,128)(2,1)S(1)} %copy-done.4), kind=kOutput, calls=%fused_computation.15 | convolution fusion | flops 402915328 | bytes 1966080 | tf_op jit(solution)/shard_map/conv_general_dilated | solution.py:63
  69.5 1.9 %collective-permute-start.6 = (bf16[256,2,1,128]{0,3,2,1:T(8,128)(2,1)S(1)}, bf16[256,2,1,128]{0,3,2,1:T(8,128)(2,1)S(1)}, u32[]{:S(2)}, u32[]{:S(2)}) collective-permute-start(bf16[256,2,1,128]{0,3,2,1:T(8,128)(2,1)S(1)} %get-tuple-element.20), channel_id=1, source_target_pairs={{0,4},{4,5},{5,1},{1,2},{2,6},{6,7},{7,3},{8,12},{12,13},{13,9},{9... | collective-permute-start | bytes 393224 | tf_op jit(solution)/shard_map/ppermute | solution.py:46
  71.5 1.3 %collective-permute-start.7 = (bf16[256,2,1,128]{0,3,2,1:T(8,128)(2,1)S(1)}, bf16[256,2,1,128]{0,3,2,1:T(8,128)(2,1)S(1)}, u32[]{:S(2)}, u32[]{:S(2)}) collective-permute-start(bf16[256,2,1,128]{0,3,2,1:T(8,128)(2,1)S(1)} %get-tuple-element.21), channel_id=1, source_target_pairs={{4,0},{5,4},{1,5},{2,1},{6,2},{7,6},{3,7},{12,8},{13,12},{9,13},{1... | collective-permute-start | bytes 393224 | tf_op jit(solution)/shard_map/ppermute | solution.py:47
  72.8 1.4 %convolution_convert_fusion.1 = bf16[2,4,8,16,256]{4,2,3,1,0:T(8,128)(2,1)S(1)} fusion(bf16[256,4,4,8,16]{0,2,4,3,1:T(4,128)(2,1)S(1)} %bitcast.98, bf16[3,256,256]{2,1,0:T(8,128)(2,1)S(1)} %copy-done.3), kind=kOutput, calls=%fused_computation.16 | convolution fusion | flops 402915328 | bytes 1966080 | tf_op jit(solution)/shard_map/conv_general_dilated | solution.py:63
  74.3 1.1 %copy.99 = bf16[256,2,4,128]{3,2,1,0:T(4,128)(2,1)} copy(bf16[256,2,4,128]{0,3,2,1:T(8,128)(2,1)S(1)} %bitcast.93) | data formatting | bytes 1048576 | tf_op jit(solution)/shard_map/convert_element_type | solution.py:120
  75.4 4.5 %all-to-all-start.2 = ((bf16[256,2,4,128]{3,2,1,0:T(4,128)(2,1)}), bf16[256,2,4,128]{3,2,1,0:T(4,128)(2,1)S(1)}, u32[]{:S(2)}, u32[]{:S(2)}) async-start(bf16[256,2,4,128]{3,2,1,0:T(4,128)(2,1)} %copy.99), calls=%async_computation.2 | async-start | bytes 1048576 | tf_op jit(solution)/shard_map/all_to_all | solution.py:121
  82.4 1.5 %fusion.3 = bf16[4,16,17,256]{3,1,2,0:T(8,128)(2,1)S(1)} fusion(bf16[3,3,256,256]{3,2,1,0:T(8,128)(2,1)S(1)} %bitcast.97, bf16[256,6,2,8,19]{0,2,4,3,1:T(2,128)(2,1)S(1)} %fusion.11, pred[16,17]{0,1:T(8,128)(4,1)S(1)} %copy-done.9), kind=kOutput, calls=%fused_computation.14 | convolution fusion | flops 1284014080 | bytes 2670864 | tf_op jit(solution)/shard_map/conv_general_dilated | solution.py:52
  84.6 1.1 %collective-permute-start.8 = (bf16[128,2,4,128]{0,2,3,1:T(4,128)(2,1)S(1)}, bf16[128,2,4,128]{0,2,3,1:T(4,128)(2,1)S(1)}, u32[]{:S(2)}, u32[]{:S(2)}) collective-permute-start(bf16[128,2,4,128]{0,2,3,1:T(4,128)(2,1)S(1)} %get-tuple-element.19), channel_id=1, source_target_pairs={{0,4},{1,5},{2,6},{3,7},{4,0},{5,1},{6,2},{7,3},{8,12},{9,13},{10,... | collective-permute-start | bytes 786440 | tf_op jit(solution)/shard_map/ppermute | solution.py:171
  85.7 4.2 %collective-permute-done.8 = bf16[128,2,4,128]{0,2,3,1:T(4,128)(2,1)S(1)} collective-permute-done((bf16[128,2,4,128]{0,2,3,1:T(4,128)(2,1)S(1)}, bf16[128,2,4,128]{0,2,3,1:T(4,128)(2,1)S(1)}, u32[]{:S(2)}, u32[]{:S(2)}) %collective-permute-start.8) | collective-permute-done | bytes 262176 | tf_op jit(solution)/shard_map/ppermute | solution.py:171
  89.9 1.0 %fusion.21 = bf16[128,2,8,128]{0,2,3,1:T(8,128)(2,1)S(1)} fusion(s32[]{:T(128)S(6)} %select_n.150, bf16[128,2,4,128]{0,2,3,1:T(4,128)(2,1)S(1)} %collective-permute-done.8, bf16[128,2,4,128]{0,2,3,1:T(4,128)(2,1)S(1)} %get-tuple-element.18), kind=kLoop, calls=%fused_computation.48 | loop fusion | flops 2097152 | bytes 1048580 | tf_op jit(solution)/shard_map/jit(_roll_dynamic)/concatenate | solution.py:19
  90.9 1.3 %copy.110 = bf16[128,2,8,128]{3,2,1,0:T(8,128)(2,1)} copy(bf16[128,2,8,128]{0,2,3,1:T(8,128)(2,1)S(1)} %fusion.21) | data formatting | bytes 1048576
  92.4 1.1 %copy.109 = bf16[64,2,16,128]{3,2,1,0:T(8,128)(2,1)} copy(bf16[64,2,16,128]{3,0,2,1:T(8,128)(2,1)S(1)} %bitcast.95) | data formatting | bytes 1048576
  (72 shorter events, 12.6 us)
Async XLA Ops:
  0.6 5.2 %copy-start = (bf16[3,3,128,64]{2,3,1,0:T(8,128)(2,1)S(1)}, bf16[3,3,128,64]{2,3,1,0:T(8,128)(2,1)}, u32[]{:S(2)}) copy-start(bf16[3,3,128,64]{2,3,1,0:T(8,128)(2,1)} %param.8) | copy-start | bytes 442372
  3.7 8.1 %copy-start.5 = (s32[2,2]{1,0:T(2,128)S(1)}, s32[2,2]{1,0:T(2,128)}, u32[]{:S(2)}) copy-start(s32[2,2]{1,0:T(2,128)} %constant.139.clone) | copy-start | bytes 52
  3.7 8.1 %copy-start.6 = (s32[2,2]{1,0:T(2,128)S(1)}, s32[2,2]{1,0:T(2,128)}, u32[]{:S(2)}) copy-start(s32[2,2]{1,0:T(2,128)} %constant.140.clone) | copy-start | bytes 52
  3.7 11.9 %copy-start.2 = (bf16[64,2,16,128]{3,2,1,0:T(8,128)(2,1)S(1)}, bf16[64,2,16,128]{3,2,1,0:T(8,128)(2,1)}, u32[]{:S(2)}) copy-start(bf16[64,2,16,128]{3,2,1,0:T(8,128)(2,1)} %param.10) | copy-start | bytes 1572868
  3.7 31.5 %collective-permute-start = (bf16[128,2,6,128]{3,2,1,0:T(8,128)(2,1)}, bf16[128,2,6,128]{3,2,1,0:T(8,128)(2,1)}, u32[]{:S(2)}, u32[]{:S(2)}) collective-permute-start(bf16[128,2,6,128]{3,2,1,0:T(8,128)(2,1)} %get-tuple-element.13), channel_id=1, source_target_pairs={{0,4},{4,0},{1,5},{5,1},{2,6},{6,2},{3,7},{7,3},{8,12},{12,8},{9,1... | collective-permute-start | bytes 1179656 | tf_op jit(solution)/shard_map/ppermute | solution.py:110
  6.2 10.1 %copy-start.7 = (s32[2,4]{1,0:T(2,128)S(1)}, s32[2,4]{1,0:T(2,128)}, u32[]{:S(2)}) copy-start(s32[2,4]{1,0:T(2,128)} %constant.141.clone) | copy-start | bytes 100
  7.4 16.0 %all-to-all-start = ((bf16[4,2,18432]{2,1,0:T(2,128)(2,1)}), bf16[4,2,18432]{2,1,0:T(2,128)(2,1)S(1)}, u32[]{:S(2)}, u32[]{:S(2)}) async-start(bf16[4,2,18432]{2,1,0:T(2,128)(2,1)} %reshape.130), calls=%async_computation | async-start | bytes 589824 | tf_op jit(solution)/shard_map/all_to_all | solution.py:83
  16.0 6.6 %collective-permute-start.3 = (bf16[2,64,2,4,128]{4,1,3,2,0:T(8,128)(2,1)S(1)}, bf16[2,64,2,4,128]{4,1,3,2,0:T(8,128)(2,1)S(1)}, u32[]{:S(2)}, u32[]{:S(2)}) collective-permute-start(bf16[2,64,2,4,128]{4,1,3,2,0:T(8,128)(2,1)S(1)} %pad_maximum_fusion.4), channel_id=1, source_target_pairs={{0,4},{4,0},{1,5},{5,1},{2,6},{6,2},{3,7},{7,3},{8,12},{12,8},{9,1... | collective-permute-start | bytes 786440 | tf_op jit(solution)/shard_map/ppermute | solution.py:140
  24.6 7.5 %collective-permute-start.1 = (bf16[3,3,64,256]{3,2,1,0:T(8,128)(2,1)S(1)}, bf16[3,3,64,256]{3,2,1,0:T(8,128)(2,1)S(1)}, u32[]{:S(2)}, u32[]{:S(2)}) collective-permute-start(bf16[3,3,64,256]{3,2,1,0:T(8,128)(2,1)S(1)} %squeeze.6), channel_id=1, source_target_pairs={{0,4},{4,0},{1,5},{5,1},{2,6},{6,2},{3,7},{7,3},{8,12},{12,8},{9,1... | collective-permute-start | bytes 884744 | tf_op jit(solution)/shard_map/ppermute | solution.py:25
  27.6 17.9 %all-to-all-start.1 = ((bf16[4,64,2,4,128]{4,1,3,2,0:T(8,128)(2,1)}), bf16[4,64,2,4,128]{4,1,3,2,0:T(8,128)(2,1)S(1)}, u32[]{:S(2)}, u32[]{:S(2)}) async-start(bf16[4,64,2,4,128]{4,1,3,2,0:T(8,128)(2,1)} %broadcast_select_fusion.2), calls=%async_computation.1 | async-start | bytes 1048576 | tf_op jit(solution)/shard_map/all_to_all | solution.py:149
  32.7 13.3 %collective-permute-start.2 = (bf16[3,3,128,256]{3,2,1,0:T(8,128)(2,1)S(1)}, bf16[3,3,128,256]{3,2,1,0:T(8,128)(2,1)}, u32[]{:S(2)}, u32[]{:S(2)}) collective-permute-start(bf16[3,3,128,256]{3,2,1,0:T(8,128)(2,1)S(1)} %fusion.18), channel_id=1, source_target_pairs={{0,8},{8,0},{16,24},{24,16},{1,9},{9,1},{17,25},{25,17},{2,10},{10... | collective-permute-start | bytes 1769480 | tf_op jit(solution)/shard_map/ppermute | solution.py:84
  45.9 1.4 %copy-start.1 = (bf16[256,6,2,8,19]{0,2,4,3,1:T(2,128)(2,1)S(1)}, bf16[256,6,2,8,19]{0,2,4,3,1:T(2,128)(2,1)}, u32[]{:S(2)}) copy-start(bf16[256,6,2,8,19]{0,2,4,3,1:T(2,128)(2,1)} %fusion.10) | copy-start | bytes 2801668
  45.9 1.4 %copy-start.8 = (pred[16,17]{0,1:T(8,128)(4,1)S(1)}, pred[16,17]{0,1:T(8,128)(4,1)}, u32[]{:S(2)}) copy-start(pred[16,17]{0,1:T(8,128)(4,1)} %constant.161) | copy-start | bytes 820
  49.7 10.8 %collective-permute-start.4 = (bf16[512,1,4,128]{0,2,3,1:T(4,128)(2,1)S(1)}, bf16[512,1,4,128]{0,2,3,1:T(4,128)(2,1)}, u32[]{:S(2)}, u32[]{:S(2)}) collective-permute-start(bf16[512,1,4,128]{0,2,3,1:T(4,128)(2,1)S(1)} %get-tuple-element.16), channel_id=1, source_target_pairs={{0,8},{8,16},{16,24},{1,9},{9,17},{17,25},{2,10},{10,18},{18,26},{... | collective-permute-start | bytes 1572872 | tf_op jit(solution)/shard_map/ppermute | solution.py:46
  54.4 10.6 %collective-permute-start.5 = (bf16[512,1,4,128]{0,2,3,1:T(4,128)(2,1)S(1)}, bf16[512,1,4,128]{0,2,3,1:T(4,128)(2,1)}, u32[]{:S(2)}, u32[]{:S(2)}) collective-permute-start(bf16[512,1,4,128]{0,2,3,1:T(4,128)(2,1)S(1)} %get-tuple-element.17), channel_id=1, source_target_pairs={{8,0},{16,8},{24,16},{9,1},{17,9},{25,17},{10,2},{18,10},{26,18},{... | collective-permute-start | bytes 1572872 | tf_op jit(solution)/shard_map/ppermute | solution.py:47
  67.0 1.0 %copy-start.4 = (bf16[3,256,256]{2,1,0:T(8,128)(2,1)S(1)}, bf16[3,256,256]{2,1,0:T(8,128)(2,1)}, u32[]{:S(2)}) copy-start(bf16[3,256,256]{2,1,0:T(8,128)(2,1)} %rev.4) | copy-start | bytes 1179652
  68.0 4.8 %copy-start.3 = (bf16[3,256,256]{2,1,0:T(8,128)(2,1)S(1)}, bf16[3,256,256]{2,1,0:T(8,128)(2,1)}, u32[]{:S(2)}) copy-start(bf16[3,256,256]{2,1,0:T(8,128)(2,1)} %param.9) | copy-start | bytes 1179652
  69.5 10.3 %collective-permute-start.6 = (bf16[256,2,1,128]{0,3,2,1:T(8,128)(2,1)S(1)}, bf16[256,2,1,128]{0,3,2,1:T(8,128)(2,1)S(1)}, u32[]{:S(2)}, u32[]{:S(2)}) collective-permute-start(bf16[256,2,1,128]{0,3,2,1:T(8,128)(2,1)S(1)} %get-tuple-element.20), channel_id=1, source_target_pairs={{0,4},{4,5},{5,1},{1,2},{2,6},{6,7},{7,3},{8,12},{12,13},{13,9},{9... | collective-permute-start | bytes 393224 | tf_op jit(solution)/shard_map/ppermute | solution.py:46
  71.5 8.4 %collective-permute-start.7 = (bf16[256,2,1,128]{0,3,2,1:T(8,128)(2,1)S(1)}, bf16[256,2,1,128]{0,3,2,1:T(8,128)(2,1)S(1)}, u32[]{:S(2)}, u32[]{:S(2)}) collective-permute-start(bf16[256,2,1,128]{0,3,2,1:T(8,128)(2,1)S(1)} %get-tuple-element.21), channel_id=1, source_target_pairs={{4,0},{5,4},{1,5},{2,1},{6,2},{7,6},{3,7},{12,8},{13,12},{9,13},{1... | collective-permute-start | bytes 393224 | tf_op jit(solution)/shard_map/ppermute | solution.py:47
  75.4 16.9 %all-to-all-start.2 = ((bf16[256,2,4,128]{3,2,1,0:T(4,128)(2,1)}), bf16[256,2,4,128]{3,2,1,0:T(4,128)(2,1)S(1)}, u32[]{:S(2)}, u32[]{:S(2)}) async-start(bf16[256,2,4,128]{3,2,1,0:T(4,128)(2,1)} %copy.99), calls=%async_computation.2 | async-start | bytes 1048576 | tf_op jit(solution)/shard_map/all_to_all | solution.py:121
  80.8 1.6 %copy-start.9 = (pred[16,17]{0,1:T(8,128)(4,1)S(1)}, pred[16,17]{0,1:T(8,128)(4,1)}, u32[]{:S(2)}) copy-start(pred[16,17]{0,1:T(8,128)(4,1)} %constant.161) | copy-start | bytes 820
  84.6 5.3 %collective-permute-start.8 = (bf16[128,2,4,128]{0,2,3,1:T(4,128)(2,1)S(1)}, bf16[128,2,4,128]{0,2,3,1:T(4,128)(2,1)S(1)}, u32[]{:S(2)}, u32[]{:S(2)}) collective-permute-start(bf16[128,2,4,128]{0,2,3,1:T(4,128)(2,1)S(1)} %get-tuple-element.19), channel_id=1, source_target_pairs={{0,4},{1,5},{2,6},{3,7},{4,0},{5,1},{6,2},{7,3},{8,12},{9,13},{10,... | collective-permute-start | bytes 786440 | tf_op jit(solution)/shard_map/ppermute | solution.py:171

commit v19 on v18

--- a/solution.py
+++ b/solution.py
@@ -121,7 +121,7 @@
     return lax.all_to_all(out, "filt", 0, 2, tiled=True)
 
 
-def backward(grad_out, weight, depth_weight):
+def grad_rows(grad_out):
     chans = lax.axis_size("chan")
     filts = lax.axis_size("filt")
     chan = lax.axis_index("chan")
@@ -138,6 +138,17 @@
         table = jnp.array([pick((r + k) % chans, r) for r in range(chans)], jnp.int32)[chan]
         send = jnp.stack([lax.dynamic_slice_in_dim(grad_out, table[q] * rows, rows, 2) for q in range(per)])
         received.append(send if k == 0 else lax.ppermute(send, "chan", shift_pairs(chans, k)))
+    return received
+
+
+def grad_blocks(received):
+    chans = lax.axis_size("chan")
+    filts = lax.axis_size("filt")
+    chan = lax.axis_index("chan")
+    turn = lambda f, r: r if f % 2 == 0 else chans - 1 - r
+    group_of = lambda c, f: f * chans + turn(f, c)
+    need = [[[f for f in range(filts) if group_of(t, f) // filts == r] for r in range(chans)] for t in range(chans)]
+    per = received[0].shape[0]
     received = jnp.concatenate(received)
     slot = [[0] * filts for _ in range(chans)]
     for t in range(chans):
@@ -173,9 +184,12 @@
 
 
 def local(volume, plane_weight, depth_weight, grad_out):
+    received = grad_rows(grad_out)
+    volume, received = lax.optimization_barrier((volume, received))
+    all_filters = grad_blocks(received)
+    plane_weight, all_filters = lax.optimization_barrier((plane_weight, all_filters))
     weight = gather_weight(plane_weight)
     mid = forward(volume, weight, depth_weight)
-    all_filters = backward(grad_out, weight, depth_weight)
     deep = halo(jnp.concatenate([mid, all_filters]), "slab", 1)
     output = forward_out(deep[: mid.shape[0]], depth_weight)
     grad_in = backward_in(deep[mid.shape[0] :], weight, depth_weight)

time: 94.2 us -> 122 us (1.30)
  waiting for transfers between devices: 20.9 us -> 36.2 us
  blocking collectives: 0 us -> 9.8 us
  starting transfers between devices: 31.2 us -> 34.7 us
  other arithmetic: 12.2 us -> 9.1 us
  local copies, waits for them, and re-layouts: 19.8 us -> 21.9 us
    all_to_all x2 -> x1, waiting for transfers between devices: 3.38 us -> 14 us  [grad_blocks(): all_filters = lax.all_to_all(blocks, 'filt', 0, 0, tiled=True)]
    all_to_all x0 -> x1, blocking collectives: none -> 9.8 us  [gather_weight(): lax.all_to_all(spread, 'filt', 0, 4, tiled=True)[0]]
    ppermute x1, starting transfers between devices: 2.58 us -> 7.46 us  [gather_weight(): other = lax.ppermute(by_filt, 'slab', [(i, i ^ 1) for i in range(slabs)])]
    all_to_all x2 -> x1, starting transfers between devices: 8.6 us -> 4.49 us  [grad_blocks(): all_filters = lax.all_to_all(blocks, 'filt', 0, 0, tiled=True)]
    ppermute x1, waiting for transfers between devices: 0.01 us -> 3.92 us  [forward(): lax.ppermute(window((chan + k) % chans), 'chan', shift_pairs(chans, k))]
    ppermute x2, starting transfers between devices: 6.58 us -> 9.34 us  [halo(): lax.ppermute(lax.slice_in_dim(x, length - 1, length, axis=dim), axis, up)]
    dynamic_slice x6, local copies, waits for them, and re-layouts: 0.37 us -> 2.33 us  [the longest x5 1.59 us: grad_rows(): lax.dynamic_slice_in_dim(grad_out, table[q] * rows, rows, 2)]
    ppermute x1, starting transfers between devices: 0.26 us -> 2.13 us  [grad_rows(): lax.ppermute(send, 'chan', shift_pairs(chans, k))]
  transfers between devices with their start and end apart: 12 -> 11, of which waited for: 6 -> 7; matrix products, arithmetic and copies ran while one was open for 27% -> 17% of each run, Pallas kernels for 0% -> 0%
where the time goes in v19:
time: 122 us; the launch traced here: 121 us
  waiting for transfers between devices  36.2 us (30%)
  starting transfers between devices  34.7 us (28%)
  local copies, waits for them, and re-layouts  21.9 us (18%)
  blocking collectives  9.8 us (8%)
  other arithmetic  9.1 us (7%)
  matrix products  5.19 us (4%)
  between operations  3.72 us (3%)
    all_to_all x1, waiting for transfers between devices, grad_blocks(): all_filters = lax.all_to_all(blocks, 'filt', 0, 0, tiled=True)  14 us
    all_to_all x1, blocking collectives, gather_weight(): lax.all_to_all(spread, 'filt', 0, 4, tiled=True)[0]  9.8 us
    ppermute x2, starting transfers between devices, halo(): lax.ppermute(lax.slice_in_dim(x, length - 1, length, axis=dim), axis, up)  9.34 us
    ppermute x1, starting transfers between devices, gather_weight(): other = lax.ppermute(by_filt, 'slab', [(i, i ^ 1) for i in range(slabs)])  7.46 us
    unnamed x23, local copies, waits for them, and re-layouts  6.66 us
    ppermute x1, waiting for transfers between devices, grad_rows(): lax.ppermute(send, 'chan', shift_pairs(chans, k))  5.89 us
    all_to_all x1, starting transfers between devices, forward_out(): return lax.all_to_all(out, 'filt', 0, 2, tiled=True)  4.98 us
    all_to_all x1, starting transfers between devices, grad_blocks(): all_filters = lax.all_to_all(blocks, 'filt', 0, 0, tiled=True)  4.49 us
  transfers between devices with their start and end apart: 11, of which 7 were waited for; matrix products, arithmetic and copies ran while one was open for 17% of the time, Pallas kernels for 0%

profile of v19, /device:TPU:1, one launch (start us, length us, event | category | flops | bytes accessed | tf_op | source)
XLA Modules:
  0.0 120.6 jit_solution(12874492968557948572)
XLA Ops:
  5.1 1.5 %constant_dynamic-slice_fusion.3 = (bf16[64,2,4,128]{3,2,1,0:T(4,128)(2,1)S(1)}, bf16[64,2,4,128]{3,2,1,0:T(4,128)(2,1)S(1)}, bf16[64,2,4,128]{3,2,1,0:T(4,128)(2,1)S(1)}, bf16[64,2,4,128]{3,2,1,0:T(4,128)(2,1)S(1)}) fusion(bf16[64,2,16,128]{3,2,1,0:T(8,128)(2,1)} %param.10, s32[]{:T(128)S(6)} %select_n.126, s32[]{:T(128)S(6)} %select_n.125, ...), kind=kLoop, calls=%fused_computation.66 | loop fusion | bytes 1048592 | tf_op jit(solution)/shard_map/dynamic_slice | solution.py:139
  6.7 2.1 %collective-permute-start = (bf16[2,64,2,4,128]{4,1,3,2,0:T(8,128)(2,1)S(1)}, bf16[2,64,2,4,128]{4,1,3,2,0:T(8,128)(2,1)S(1)}, u32[]{:S(2)}, u32[]{:S(2)}) collective-permute-start(bf16[2,64,2,4,128]{4,1,3,2,0:T(8,128)(2,1)S(1)} %pad_maximum_fusion.5), channel_id=1, source_target_pairs={{0,4},{4,0},{1,5},{5,1},{2,6},{6,2},{3,7},{7,3},{8,12},{12,8},{9,1... | collective-permute-start | bytes 786440 | tf_op jit(solution)/shard_map/ppermute | solution.py:140
  9.0 5.9 %collective-permute-done = bf16[2,64,2,4,128]{4,1,3,2,0:T(8,128)(2,1)S(1)} collective-permute-done((bf16[2,64,2,4,128]{4,1,3,2,0:T(8,128)(2,1)S(1)}, bf16[2,64,2,4,128]{4,1,3,2,0:T(8,128)(2,1)S(1)}, u32[]{:S(2)}, u32[]{:S(2)}) %collective-permute-start) | collective-permute-done | bytes 262176 | tf_op jit(solution)/shard_map/ppermute | solution.py:140
  15.6 0.9 broadcast_select_fusion.2
  16.5 4.5 %all-to-all-start = ((bf16[4,64,2,4,128]{4,1,3,2,0:T(8,128)(2,1)}), bf16[4,64,2,4,128]{4,1,3,2,0:T(8,128)(2,1)S(1)}, u32[]{:S(2)}, u32[]{:S(2)}) async-start(bf16[4,64,2,4,128]{4,1,3,2,0:T(8,128)(2,1)} %broadcast_select_fusion.2), calls=%async_computation | async-start | bytes 1048576 | tf_op jit(solution)/shard_map/all_to_all | solution.py:160
  21.0 14.0 %all-to-all-done = bf16[4,64,2,4,128]{4,1,3,2,0:T(8,128)(2,1)S(1)} async-done(((bf16[4,64,2,4,128]{4,1,3,2,0:T(8,128)(2,1)}), bf16[4,64,2,4,128]{4,1,3,2,0:T(8,128)(2,1)S(1)}, u32[]{:S(2)}, u32[]{:S(2)}) %all-to-all-start) | async-done | bytes 524320 | tf_op jit(solution)/shard_map/all_to_all | solution.py:160
  35.9 9.8 %all_to_all.38 = bf16[4,2,18432]{2,1,0:T(2,128)(2,1)S(1)} all-to-all(bf16[4,2,18432]{2,1,0:T(2,128)(2,1)S(1)} %reshape.130), channel_id=1, replica_groups=mesh['slab'=4,'chan'=2,'filt'=4] {'filt'}, dimensions={0} | all-to-all | bytes 589824 | tf_op jit(solution)/shard_map/all_to_all | solution.py:83
  46.9 1.3 %collective-permute-start.2 = (bf16[3,3,64,256]{3,2,1,0:T(8,128)(2,1)S(1)}, bf16[3,3,64,256]{3,2,1,0:T(8,128)(2,1)S(1)}, u32[]{:S(2)}, u32[]{:S(2)}) collective-permute-start(bf16[3,3,64,256]{3,2,1,0:T(8,128)(2,1)S(1)} %squeeze.8), channel_id=1, source_target_pairs={{0,4},{4,0},{1,5},{5,1},{2,6},{6,2},{3,7},{7,3},{8,12},{12,8},{9,1... | collective-permute-start | bytes 884744 | tf_op jit(solution)/shard_map/ppermute | solution.py:25
  48.2 2.2 %pad_dynamic-slice_fusion = (bf16[128,2,6,128]{3,2,1,0:T(8,128)(2,1)S(1)}, bf16[128,2,6,128]{3,2,1,0:T(8,128)(2,1)S(1)}) fusion(s32[]{:T(128)S(6)} %select_n.130, bf16[128,2,32,128]{3,2,1,0:T(8,128)(2,1)} %param.7, s32[]{:T(128)S(6)} %select_n.129), kind=kLoop, calls=%fused_computation.1 | loop fusion | bytes 2883592 | tf_op jit(solution)/shard_map/dynamic_slice | solution.py:107
  50.7 1.8 %collective-permute-done.2 = bf16[3,3,64,256]{3,2,1,0:T(8,128)(2,1)S(1)} collective-permute-done((bf16[3,3,64,256]{3,2,1,0:T(8,128)(2,1)S(1)}, bf16[3,3,64,256]{3,2,1,0:T(8,128)(2,1)S(1)}, u32[]{:S(2)}, u32[]{:S(2)}) %collective-permute-start.2) | collective-permute-done | bytes 294944 | tf_op jit(solution)/shard_map/ppermute | solution.py:25
  53.1 7.5 %collective-permute-start.3 = (bf16[3,3,128,256]{3,2,1,0:T(8,128)(2,1)S(1)}, bf16[3,3,128,256]{3,2,1,0:T(8,128)(2,1)}, u32[]{:S(2)}, u32[]{:S(2)}) collective-permute-start(bf16[3,3,128,256]{3,2,1,0:T(8,128)(2,1)S(1)} %fusion.18), channel_id=1, source_target_pairs={{0,8},{8,0},{16,24},{24,16},{1,9},{9,1},{17,25},{25,17},{2,10},{10... | collective-permute-start | bytes 1769480 | tf_op jit(solution)/shard_map/ppermute | solution.py:84
  60.5 3.9 %collective-permute-done.1 = bf16[128,2,6,128]{3,2,1,0:T(8,128)(2,1)S(1)} collective-permute-done((bf16[128,2,6,128]{3,2,1,0:T(8,128)(2,1)S(1)}, bf16[128,2,6,128]{3,2,1,0:T(8,128)(2,1)S(1)}, u32[]{:S(2)}, u32[]{:S(2)}) %collective-permute-start.1) | collective-permute-done | bytes 393248 | tf_op jit(solution)/shard_map/ppermute | solution.py:110
  65.2 3.2 %fusion.7 = bf16[256,6,2,128]{3,1,2,0:T(8,128)(2,1)S(1)} fusion(s32[]{:T(128)S(6)} %select_n.132, bf16[128,2,6,128]{3,2,1,0:T(8,128)(2,1)} %copy-done.3, bf16[128,2,6,128]{3,2,1,0:T(8,128)(2,1)S(1)} %get-tuple-element.22), kind=kLoop, calls=%fused_computation.25 | loop fusion | flops 1179648 | bytes 1572868 | tf_op jit(solution)/shard_map/jit(_roll_dynamic)/dynamic_slice | solution.py:19
  68.5 1.3 %copy.112 = bf16[256,6,2,128]{0,2,3,1:T(2,128)(2,1)S(1)} copy(bf16[256,6,2,128]{3,1,2,0:T(8,128)(2,1)S(1)} %fusion.7) | data formatting | bytes 1572864
  71.4 1.1 broadcast_select_fusion.1
  72.7 1.5 %fusion.2 = bf16[4,16,17,256]{3,1,2,0:T(8,128)(2,1)S(1)} fusion(bf16[3,3,256,256]{3,2,1,0:T(8,128)(2,1)S(1)} %bitcast.98, bf16[256,6,2,8,19]{0,2,4,3,1:T(2,128)(2,1)S(1)} %fusion.10, pred[16,17]{0,1:T(8,128)(4,1)S(1)} %copy-done.6), kind=kOutput, calls=%fused_computation.13 | convolution fusion | flops 1284014080 | bytes 2670864 | tf_op jit(solution)/shard_map/conv_general_dilated | solution.py:52
  75.1 6.6 %collective-permute-start.4 = (bf16[512,1,4,128]{3,0,2,1:T(8,128)(2,1)S(1)}, bf16[512,1,4,128]{3,0,2,1:T(8,128)(2,1)S(1)}, u32[]{:S(2)}, u32[]{:S(2)}) collective-permute-start(bf16[512,1,4,128]{3,0,2,1:T(8,128)(2,1)S(1)} %get-tuple-element.26), channel_id=1, source_target_pairs={{0,8},{8,16},{16,24},{1,9},{9,17},{17,25},{2,10},{10,18},{18,26},{... | collective-permute-start | bytes 1572872 | tf_op jit(solution)/shard_map/ppermute | solution.py:46
  81.7 2.1 %collective-permute-start.5 = (bf16[512,1,4,128]{3,0,2,1:T(8,128)(2,1)S(1)}, bf16[512,1,4,128]{3,0,2,1:T(8,128)(2,1)S(1)}, u32[]{:S(2)}, u32[]{:S(2)}) collective-permute-start(bf16[512,1,4,128]{3,0,2,1:T(8,128)(2,1)S(1)} %get-tuple-element.27), channel_id=1, source_target_pairs={{8,0},{16,8},{24,16},{9,1},{17,9},{25,17},{10,2},{18,10},{26,18},{... | collective-permute-start | bytes 1572872 | tf_op jit(solution)/shard_map/ppermute | solution.py:47
  83.9 1.8 %rev.4 = bf16[3,256,256]{2,1,0:T(8,128)(2,1)} reverse(bf16[3,256,256]{2,1,0:T(8,128)(2,1)} %param.9), dimensions={0} | reverse | bytes 786432 | tf_op jit(solution)/shard_map/rev | solution.py:171
  85.6 2.2 %collective-permute-done.4 = bf16[512,1,4,128]{3,0,2,1:T(8,128)(2,1)S(1)} collective-permute-done((bf16[512,1,4,128]{3,0,2,1:T(8,128)(2,1)S(1)}, bf16[512,1,4,128]{3,0,2,1:T(8,128)(2,1)S(1)}, u32[]{:S(2)}, u32[]{:S(2)}) %collective-permute-start.4) | collective-permute-done | bytes 524320 | tf_op jit(solution)/shard_map/ppermute | solution.py:46
  87.8 4.4 %collective-permute-done.5 = bf16[512,1,4,128]{3,0,2,1:T(8,128)(2,1)S(1)} collective-permute-done((bf16[512,1,4,128]{3,0,2,1:T(8,128)(2,1)S(1)}, bf16[512,1,4,128]{3,0,2,1:T(8,128)(2,1)S(1)}, u32[]{:S(2)}, u32[]{:S(2)}) %collective-permute-start.5) | collective-permute-done | bytes 524320 | tf_op jit(solution)/shard_map/ppermute | solution.py:47
  93.1 1.6 %convolution_convert_fusion = bf16[2,4,8,16,256]{4,2,3,1,0:T(8,128)(2,1)S(1)} fusion(bf16[256,4,4,8,16]{0,4,3,2,1:T(8,128)(2,1)S(1)} %bitcast.100, bf16[3,256,256]{2,1,0:T(8,128)(2,1)} %rev.4), kind=kOutput, calls=%fused_computation.15 | convolution fusion | flops 402915328 | bytes 1966080 | tf_op jit(solution)/shard_map/conv_general_dilated | solution.py:63
  95.5 2.8 %collective-permute-start.6 = (bf16[256,2,1,128]{0,3,2,1:T(8,128)(2,1)}, bf16[256,2,1,128]{0,3,2,1:T(8,128)(2,1)S(1)}, u32[]{:S(2)}, u32[]{:S(2)}) collective-permute-start(bf16[256,2,1,128]{0,3,2,1:T(8,128)(2,1)} %get-tuple-element.30), channel_id=1, source_target_pairs={{0,4},{4,5},{5,1},{1,2},{2,6},{6,7},{7,3},{8,12},{12,13},{13,9},{9... | collective-permute-start | bytes 393224 | tf_op jit(solution)/shard_map/ppermute | solution.py:46
  98.3 1.3 %collective-permute-start.7 = (bf16[256,2,1,128]{0,3,2,1:T(8,128)(2,1)}, bf16[256,2,1,128]{0,3,2,1:T(8,128)(2,1)S(1)}, u32[]{:S(2)}, u32[]{:S(2)}) collective-permute-start(bf16[256,2,1,128]{0,3,2,1:T(8,128)(2,1)} %get-tuple-element.31), channel_id=1, source_target_pairs={{4,0},{5,4},{1,5},{2,1},{6,2},{7,6},{3,7},{12,8},{13,12},{9,13},{1... | collective-permute-start | bytes 393224 | tf_op jit(solution)/shard_map/ppermute | solution.py:47
  100.9 1.1 copy.99
  101.9 5.0 %all-to-all-start.2 = ((bf16[256,2,4,128]{3,2,1,0:T(4,128)(2,1)}), bf16[256,2,4,128]{3,2,1,0:T(4,128)(2,1)S(1)}, u32[]{:S(2)}, u32[]{:S(2)}) async-start(bf16[256,2,4,128]{3,2,1,0:T(4,128)(2,1)} %copy.99), calls=%async_computation.2 | async-start | bytes 1048576 | tf_op jit(solution)/shard_map/all_to_all | solution.py:121
  109.5 1.5 %fusion.3 = bf16[4,16,17,256]{3,1,2,0:T(8,128)(2,1)S(1)} fusion(bf16[3,3,256,256]{3,2,1,0:T(8,128)(2,1)S(1)} %bitcast.99, bf16[256,6,2,8,19]{0,2,4,3,1:T(2,128)(2,1)S(1)} %fusion.11, pred[16,17]{0,1:T(8,128)(4,1)S(1)} %copy-done.7), kind=kOutput, calls=%fused_computation.14 | convolution fusion | flops 1284014080 | bytes 2670864 | tf_op jit(solution)/shard_map/conv_general_dilated | solution.py:52
  111.7 1.3 %collective-permute-start.8 = (bf16[128,2,4,128]{0,2,3,1:T(4,128)(2,1)S(1)}, bf16[128,2,4,128]{0,2,3,1:T(4,128)(2,1)S(1)}, u32[]{:S(2)}, u32[]{:S(2)}) collective-permute-start(bf16[128,2,4,128]{0,2,3,1:T(4,128)(2,1)S(1)} %get-tuple-element.29), channel_id=1, source_target_pairs={{0,4},{1,5},{2,6},{3,7},{4,0},{5,1},{6,2},{7,3},{8,12},{9,13},{10,... | collective-permute-start | bytes 786440 | tf_op jit(solution)/shard_map/ppermute | solution.py:182
  113.0 4.0 %collective-permute-done.8 = bf16[128,2,4,128]{0,2,3,1:T(4,128)(2,1)S(1)} collective-permute-done((bf16[128,2,4,128]{0,2,3,1:T(4,128)(2,1)S(1)}, bf16[128,2,4,128]{0,2,3,1:T(4,128)(2,1)S(1)}, u32[]{:S(2)}, u32[]{:S(2)}) %collective-permute-start.8) | collective-permute-done | bytes 262176 | tf_op jit(solution)/shard_map/ppermute | solution.py:182
  117.0 1.0 fusion.21
  118.0 1.3 %copy.110 = bf16[128,2,8,128]{3,2,1,0:T(8,128)(2,1)} copy(bf16[128,2,8,128]{0,2,3,1:T(8,128)(2,1)S(1)} %fusion.21) | data formatting | bytes 1048576
  119.4 1.1 copy.109
  (70 shorter events, 15.2 us)
Async XLA Ops:
  0.6 34.4 %copy-start = (bf16[3,3,128,64]{2,3,1,0:T(8,128)(2,1)S(1)}, bf16[3,3,128,64]{2,3,1,0:T(8,128)(2,1)}, u32[]{:S(2)}) copy-start(bf16[3,3,128,64]{2,3,1,0:T(8,128)(2,1)} %param.8) | copy-start | bytes 442372
  0.6 8.2 %copy-start.5 = (s32[2,4]{1,0:T(2,128)S(1)}, s32[2,4]{1,0:T(2,128)}, u32[]{:S(2)}) copy-start(s32[2,4]{1,0:T(2,128)} %constant.141.clone) | copy-start | bytes 100
  6.7 8.2 %collective-permute-start = (bf16[2,64,2,4,128]{4,1,3,2,0:T(8,128)(2,1)S(1)}, bf16[2,64,2,4,128]{4,1,3,2,0:T(8,128)(2,1)S(1)}, u32[]{:S(2)}, u32[]{:S(2)}) collective-permute-start(bf16[2,64,2,4,128]{4,1,3,2,0:T(8,128)(2,1)S(1)} %pad_maximum_fusion.5), channel_id=1, source_target_pairs={{0,4},{4,0},{1,5},{5,1},{2,6},{6,2},{3,7},{7,3},{8,12},{12,8},{9,1... | collective-permute-start | bytes 786440 | tf_op jit(solution)/shard_map/ppermute | solution.py:140
  16.5 18.5 %all-to-all-start = ((bf16[4,64,2,4,128]{4,1,3,2,0:T(8,128)(2,1)}), bf16[4,64,2,4,128]{4,1,3,2,0:T(8,128)(2,1)S(1)}, u32[]{:S(2)}, u32[]{:S(2)}) async-start(bf16[4,64,2,4,128]{4,1,3,2,0:T(8,128)(2,1)} %broadcast_select_fusion.2), calls=%async_computation | async-start | bytes 1048576 | tf_op jit(solution)/shard_map/all_to_all | solution.py:160
  46.9 5.6 %collective-permute-start.2 = (bf16[3,3,64,256]{3,2,1,0:T(8,128)(2,1)S(1)}, bf16[3,3,64,256]{3,2,1,0:T(8,128)(2,1)S(1)}, u32[]{:S(2)}, u32[]{:S(2)}) collective-permute-start(bf16[3,3,64,256]{3,2,1,0:T(8,128)(2,1)S(1)} %squeeze.8), channel_id=1, source_target_pairs={{0,4},{4,0},{1,5},{5,1},{2,6},{6,2},{3,7},{7,3},{8,12},{12,8},{9,1... | collective-permute-start | bytes 884744 | tf_op jit(solution)/shard_map/ppermute | solution.py:25
  50.5 14.0 %collective-permute-start.1 = (bf16[128,2,6,128]{3,2,1,0:T(8,128)(2,1)S(1)}, bf16[128,2,6,128]{3,2,1,0:T(8,128)(2,1)S(1)}, u32[]{:S(2)}, u32[]{:S(2)}) collective-permute-start(bf16[128,2,6,128]{3,2,1,0:T(8,128)(2,1)S(1)} %get-tuple-element.23), channel_id=1, source_target_pairs={{0,4},{4,0},{1,5},{5,1},{2,6},{6,2},{3,7},{7,3},{8,12},{12,8},{9,1... | collective-permute-start | bytes 1179656 | tf_op jit(solution)/shard_map/ppermute | solution.py:110
  53.1 18.3 %collective-permute-start.3 = (bf16[3,3,128,256]{3,2,1,0:T(8,128)(2,1)S(1)}, bf16[3,3,128,256]{3,2,1,0:T(8,128)(2,1)}, u32[]{:S(2)}, u32[]{:S(2)}) collective-permute-start(bf16[3,3,128,256]{3,2,1,0:T(8,128)(2,1)S(1)} %fusion.18), channel_id=1, source_target_pairs={{0,8},{8,0},{16,24},{24,16},{1,9},{9,1},{17,25},{25,17},{2,10},{10... | collective-permute-start | bytes 1769480 | tf_op jit(solution)/shard_map/ppermute | solution.py:84
  64.4 0.8 copy-start.3
  71.4 1.3 %copy-start.6 = (pred[16,17]{0,1:T(8,128)(4,1)S(1)}, pred[16,17]{0,1:T(8,128)(4,1)}, u32[]{:S(2)}) copy-start(pred[16,17]{0,1:T(8,128)(4,1)} %constant.161) | copy-start | bytes 820
  72.7 1.5 %copy-start.1 = (bf16[3,3,2,2,64,256]{5,4,3,2,1,0:T(8,128)(2,1)}, bf16[3,3,2,2,64,256]{5,4,3,2,1,0:T(8,128)(2,1)S(1)}, u32[]{:S(2)}) copy-start(bf16[3,3,2,2,64,256]{5,4,3,2,1,0:T(8,128)(2,1)S(1)} %pad_maximum_fusion.1) | copy-start | bytes 3538948
  75.1 12.7 %collective-permute-start.4 = (bf16[512,1,4,128]{3,0,2,1:T(8,128)(2,1)S(1)}, bf16[512,1,4,128]{3,0,2,1:T(8,128)(2,1)S(1)}, u32[]{:S(2)}, u32[]{:S(2)}) collective-permute-start(bf16[512,1,4,128]{3,0,2,1:T(8,128)(2,1)S(1)} %get-tuple-element.26), channel_id=1, source_target_pairs={{0,8},{8,16},{16,24},{1,9},{9,17},{17,25},{2,10},{10,18},{18,26},{... | collective-permute-start | bytes 1572872 | tf_op jit(solution)/shard_map/ppermute | solution.py:46
  81.7 10.5 %collective-permute-start.5 = (bf16[512,1,4,128]{3,0,2,1:T(8,128)(2,1)S(1)}, bf16[512,1,4,128]{3,0,2,1:T(8,128)(2,1)S(1)}, u32[]{:S(2)}, u32[]{:S(2)}) collective-permute-start(bf16[512,1,4,128]{3,0,2,1:T(8,128)(2,1)S(1)} %get-tuple-element.27), channel_id=1, source_target_pairs={{8,0},{16,8},{24,16},{9,1},{17,9},{25,17},{10,2},{18,10},{26,18},{... | collective-permute-start | bytes 1572872 | tf_op jit(solution)/shard_map/ppermute | solution.py:47
  94.7 5.4 %copy-start.4 = (bf16[3,256,256]{2,1,0:T(8,128)(2,1)S(1)}, bf16[3,256,256]{2,1,0:T(8,128)(2,1)}, u32[]{:S(2)}) copy-start(bf16[3,256,256]{2,1,0:T(8,128)(2,1)} %param.9) | copy-start | bytes 1179652
  95.5 11.4 %collective-permute-start.6 = (bf16[256,2,1,128]{0,3,2,1:T(8,128)(2,1)}, bf16[256,2,1,128]{0,3,2,1:T(8,128)(2,1)S(1)}, u32[]{:S(2)}, u32[]{:S(2)}) collective-permute-start(bf16[256,2,1,128]{0,3,2,1:T(8,128)(2,1)} %get-tuple-element.30), channel_id=1, source_target_pairs={{0,4},{4,5},{5,1},{1,2},{2,6},{6,7},{7,3},{8,12},{12,13},{13,9},{9... | collective-permute-start | bytes 393224 | tf_op jit(solution)/shard_map/ppermute | solution.py:46
  98.3 8.7 %collective-permute-start.7 = (bf16[256,2,1,128]{0,3,2,1:T(8,128)(2,1)}, bf16[256,2,1,128]{0,3,2,1:T(8,128)(2,1)S(1)}, u32[]{:S(2)}, u32[]{:S(2)}) collective-permute-start(bf16[256,2,1,128]{0,3,2,1:T(8,128)(2,1)} %get-tuple-element.31), channel_id=1, source_target_pairs={{4,0},{5,4},{1,5},{2,1},{6,2},{7,6},{3,7},{12,8},{13,12},{9,13},{1... | collective-permute-start | bytes 393224 | tf_op jit(solution)/shard_map/ppermute | solution.py:47
  101.9 17.4 %all-to-all-start.2 = ((bf16[256,2,4,128]{3,2,1,0:T(4,128)(2,1)}), bf16[256,2,4,128]{3,2,1,0:T(4,128)(2,1)S(1)}, u32[]{:S(2)}, u32[]{:S(2)}) async-start(bf16[256,2,4,128]{3,2,1,0:T(4,128)(2,1)} %copy.99), calls=%async_computation.2 | async-start | bytes 1048576 | tf_op jit(solution)/shard_map/all_to_all | solution.py:121
  107.8 1.6 %copy-start.2 = (bf16[3,3,2,2,64,256]{5,4,3,2,1,0:T(8,128)(2,1)S(1)}, bf16[3,3,2,2,64,256]{5,4,3,2,1,0:T(8,128)(2,1)}, u32[]{:S(2)}) copy-start(bf16[3,3,2,2,64,256]{5,4,3,2,1,0:T(8,128)(2,1)} %copy-done.1) | copy-start | bytes 3538948
  107.9 1.6 %copy-start.7 = (pred[16,17]{0,1:T(8,128)(4,1)S(1)}, pred[16,17]{0,1:T(8,128)(4,1)}, u32[]{:S(2)}) copy-start(pred[16,17]{0,1:T(8,128)(4,1)} %constant.161) | copy-start | bytes 820
  111.7 5.3 %collective-permute-start.8 = (bf16[128,2,4,128]{0,2,3,1:T(4,128)(2,1)S(1)}, bf16[128,2,4,128]{0,2,3,1:T(4,128)(2,1)S(1)}, u32[]{:S(2)}, u32[]{:S(2)}) collective-permute-start(bf16[128,2,4,128]{0,2,3,1:T(4,128)(2,1)S(1)} %get-tuple-element.29), channel_id=1, source_target_pairs={{0,4},{1,5},{2,6},{3,7},{4,0},{5,1},{6,2},{7,3},{8,12},{9,13},{10,... | collective-permute-start | bytes 786440 | tf_op jit(solution)/shard_map/ppermute | solution.py:182

commit v20 on v18

--- a/solution.py
+++ b/solution.py
@@ -176,9 +176,8 @@
     weight = gather_weight(plane_weight)
     mid = forward(volume, weight, depth_weight)
     all_filters = backward(grad_out, weight, depth_weight)
-    deep = halo(jnp.concatenate([mid, all_filters]), "slab", 1)
-    output = forward_out(deep[: mid.shape[0]], depth_weight)
-    grad_in = backward_in(deep[mid.shape[0] :], weight, depth_weight)
+    output = forward_out(halo(mid, "slab", 1), depth_weight)
+    grad_in = backward_in(halo(all_filters, "slab", 1), weight, depth_weight)
     return (output, grad_in)
 
 

time: 94.2 us -> 104 us (1.10)
  waiting for transfers between devices: 20.9 us -> 27.1 us
  starting transfers between devices: 31.2 us -> 37 us
  other arithmetic: 12.2 us -> 9.7 us
    ppermute x1, waiting for transfers between devices: 0.01 us -> 8.19 us  [forward(): lax.ppermute(window((chan + k) % chans), 'chan', shift_pairs(chans, k))]
    ppermute x2 -> x3, starting transfers between devices: 6.58 us -> 10.8 us  [halo(): lax.ppermute(lax.slice_in_dim(x, length - 1, length, axis=dim), axis, up)]
    all_to_all x1, waiting for transfers between devices: 3.37 us -> 0.01 us  [backward(): all_filters = lax.all_to_all(blocks, 'filt', 0, 0, tiled=True)]
    ppermute x1, starting transfers between devices: 2.58 us -> 0.07 us  [gather_weight(): other = lax.ppermute(by_filt, 'slab', [(i, i ^ 1) for i in range(slabs)])]
    ppermute x2 -> x3, starting transfers between devices: 3.39 us -> 5.7 us  [halo(): after = lax.ppermute(lax.slice_in_dim(x, 0, 1, axis=dim), axis, down)]
    ppermute x2 -> x3, waiting for transfers between devices: 2.19 us -> 0.01 us  [halo(): lax.ppermute(lax.slice_in_dim(x, length - 1, length, axis=dim), axis, up)]
    all_to_all x1, starting transfers between devices: 4.52 us -> 6.66 us  [forward_out(): return lax.all_to_all(out, 'filt', 0, 2, tiled=True)]
    unnamed x26 -> x28, local copies, waits for them, and re-layouts: 6.47 us -> 8.39 us
  transfers between devices with their start and end apart: 12 -> 14, of which waited for: 6 -> 6; matrix products, arithmetic and copies ran while one was open for 27% -> 26% of each run, Pallas kernels for 0% -> 0%
where the time goes in v20:
time: 104 us; the launch traced here: 103 us
  starting transfers between devices  37 us (36%)
  waiting for transfers between devices  27.1 us (26%)
  local copies, waits for them, and re-layouts  19.6 us (19%)
  other arithmetic  9.7 us (9%)
  matrix products  5.98 us (6%)
  between operations  3.71 us (4%)
    ppermute x3, starting transfers between devices, halo(): lax.ppermute(lax.slice_in_dim(x, length - 1, length, axis=dim), axis, up)  10.8 us
    unnamed x28, local copies, waits for them, and re-layouts  8.39 us
    ppermute x1, waiting for transfers between devices, forward(): lax.ppermute(window((chan + k) % chans), 'chan', shift_pairs(chans, k))  8.19 us
    all_to_all x1, starting transfers between devices, forward_out(): return lax.all_to_all(out, 'filt', 0, 2, tiled=True)  6.66 us
    ppermute x3, waiting for transfers between devices, halo(): after = lax.ppermute(lax.slice_in_dim(x, 0, 1, axis=dim), axis, down)  6.34 us
    ppermute x3, starting transfers between devices, halo(): after = lax.ppermute(lax.slice_in_dim(x, 0, 1, axis=dim), axis, down)  5.7 us
    ppermute x1, waiting for transfers between devices, backward(): lax.ppermute(send, 'chan', shift_pairs(chans, k))  5.51 us
    all_to_all x1, starting transfers between devices, gather_weight(): lax.all_to_all(spread, 'filt', 0, 4, tiled=True)[0]  5.42 us
  transfers between devices with their start and end apart: 14, of which 6 were waited for; matrix products, arithmetic and copies ran while one was open for 26% of the time, Pallas kernels for 0%

profile of v20, /device:TPU:1, one launch (start us, length us, event | category | flops | bytes accessed | tf_op | source)
XLA Modules:
  0.0 103.2 jit_solution(10349486137600041442)
XLA Ops:
  2.0 1.2 %reshape.130 = bf16[4,2,18432]{2,1,0:T(2,128)(2,1)} reshape(bf16[4,3,3,64,64]{4,3,2,1,0:T(8,128)(2,1)S(1)} %broadcast_in_dim.28) | data formatting | bytes 589824
  3.1 5.4 %all-to-all-start = ((bf16[4,2,18432]{2,1,0:T(2,128)(2,1)}), bf16[4,2,18432]{2,1,0:T(2,128)(2,1)S(1)}, u32[]{:S(2)}, u32[]{:S(2)}) async-start(bf16[4,2,18432]{2,1,0:T(2,128)(2,1)} %reshape.130), calls=%async_computation | async-start | bytes 589824 | tf_op jit(solution)/shard_map/all_to_all | solution.py:83
  12.7 1.3 %collective-permute-start.5 = (bf16[2,64,2,4,128]{4,1,3,2,0:T(8,128)(2,1)S(1)}, bf16[2,64,2,4,128]{4,1,3,2,0:T(8,128)(2,1)S(1)}, u32[]{:S(2)}, u32[]{:S(2)}) collective-permute-start(bf16[2,64,2,4,128]{4,1,3,2,0:T(8,128)(2,1)S(1)} %pad_maximum_fusion.4), channel_id=1, source_target_pairs={{0,4},{4,0},{1,5},{5,1},{2,6},{6,2},{3,7},{7,3},{8,12},{12,8},{9,1... | collective-permute-start | bytes 786440 | tf_op jit(solution)/shard_map/ppermute | solution.py:140
  14.1 5.5 %collective-permute-done.5 = bf16[2,64,2,4,128]{4,1,3,2,0:T(8,128)(2,1)S(1)} collective-permute-done((bf16[2,64,2,4,128]{4,1,3,2,0:T(8,128)(2,1)S(1)}, bf16[2,64,2,4,128]{4,1,3,2,0:T(8,128)(2,1)S(1)}, u32[]{:S(2)}, u32[]{:S(2)}) %collective-permute-start.5) | collective-permute-done | bytes 262176 | tf_op jit(solution)/shard_map/ppermute | solution.py:140
  21.3 4.2 %all-to-all-start.2 = ((bf16[4,64,2,4,128]{4,1,3,2,0:T(8,128)(2,1)}), bf16[4,64,2,4,128]{4,1,3,2,0:T(8,128)(2,1)S(1)}, u32[]{:S(2)}, u32[]{:S(2)}) async-start(bf16[4,64,2,4,128]{4,1,3,2,0:T(8,128)(2,1)} %broadcast_select_fusion.2), calls=%async_computation.2 | async-start | bytes 1048576 | tf_op jit(solution)/shard_map/all_to_all | solution.py:149
  25.5 1.3 %pad_dynamic-slice_fusion = (bf16[128,2,6,128]{3,2,1,0:T(8,128)(2,1)S(1)}, bf16[128,2,6,128]{3,2,1,0:T(8,128)(2,1)}) fusion(s32[]{:T(128)S(6)} %select_n.125, bf16[128,2,32,128]{3,2,1,0:T(8,128)(2,1)S(1)} %copy-done.1, s32[]{:T(128)S(6)} %select_n.124), kind=kLoop, calls=%fused_computation.1 | loop fusion | bytes 2883592 | tf_op jit(solution)/shard_map/dynamic_slice | solution.py:107
  26.9 1.2 %collective-permute-start = (bf16[128,2,6,128]{3,2,1,0:T(8,128)(2,1)}, bf16[128,2,6,128]{3,2,1,0:T(8,128)(2,1)S(1)}, u32[]{:S(2)}, u32[]{:S(2)}) collective-permute-start(bf16[128,2,6,128]{3,2,1,0:T(8,128)(2,1)} %get-tuple-element.11), channel_id=1, source_target_pairs={{0,4},{4,0},{1,5},{5,1},{2,6},{6,2},{3,7},{7,3},{8,12},{12,8},{9,1... | collective-permute-start | bytes 1179656 | tf_op jit(solution)/shard_map/ppermute | solution.py:110
  28.1 1.8 %rev.4 = bf16[3,256,256]{2,1,0:T(8,128)(2,1)} reverse(bf16[3,256,256]{2,1,0:T(8,128)(2,1)} %param.9), dimensions={0} | reverse | bytes 786432 | tf_op jit(solution)/shard_map/rev | solution.py:160
  29.9 8.2 %collective-permute-done = bf16[128,2,6,128]{3,2,1,0:T(8,128)(2,1)S(1)} collective-permute-done((bf16[128,2,6,128]{3,2,1,0:T(8,128)(2,1)}, bf16[128,2,6,128]{3,2,1,0:T(8,128)(2,1)S(1)}, u32[]{:S(2)}, u32[]{:S(2)}) %collective-permute-start) | collective-permute-done | bytes 393248 | tf_op jit(solution)/shard_map/ppermute | solution.py:110
  38.1 3.4 %fusion.7 = bf16[256,6,2,128]{3,1,2,0:T(8,128)(2,1)S(1)} fusion(s32[]{:T(128)S(6)} %select_n.127, bf16[128,2,6,128]{3,2,1,0:T(8,128)(2,1)S(1)} %collective-permute-done, bf16[128,2,6,128]{3,2,1,0:T(8,128)(2,1)S(1)} %get-tuple-element.10), kind=kLoop, calls=%fused_computation.24 | loop fusion | flops 1179648 | bytes 1572868 | tf_op jit(solution)/shard_map/jit(_roll_dynamic)/dynamic_slice | solution.py:19
  41.5 1.3 %copy.109 = bf16[256,6,2,128]{0,2,3,1:T(2,128)(2,1)S(1)} copy(bf16[256,6,2,128]{3,1,2,0:T(8,128)(2,1)S(1)} %fusion.7) | data formatting | bytes 1572864
  45.0 1.3 %collective-permute-start.1 = (bf16[3,3,64,256]{3,2,1,0:T(8,128)(2,1)S(1)}, bf16[3,3,64,256]{3,2,1,0:T(8,128)(2,1)S(1)}, u32[]{:S(2)}, u32[]{:S(2)}) collective-permute-start(bf16[3,3,64,256]{3,2,1,0:T(8,128)(2,1)S(1)} %squeeze.6), channel_id=1, source_target_pairs={{0,4},{4,0},{1,5},{5,1},{2,6},{6,2},{3,7},{7,3},{8,12},{12,8},{9,1... | collective-permute-start | bytes 884744 | tf_op jit(solution)/shard_map/ppermute | solution.py:25
  46.4 6.6 %collective-permute-start.6 = (bf16[256,1,4,128]{3,0,2,1:T(8,128)(2,1)S(1)}, bf16[256,1,4,128]{3,0,2,1:T(8,128)(2,1)S(1)}, u32[]{:S(2)}, u32[]{:S(2)}) collective-permute-start(bf16[256,1,4,128]{3,0,2,1:T(8,128)(2,1)S(1)} %get-tuple-element.18), channel_id=1, source_target_pairs={{0,8},{8,16},{16,24},{1,9},{9,17},{17,25},{2,10},{10,18},{18,26},{... | collective-permute-start | bytes 786440 | tf_op jit(solution)/shard_map/ppermute | solution.py:46
  53.0 1.9 %collective-permute-start.7 = (bf16[256,1,4,128]{3,0,2,1:T(8,128)(2,1)S(1)}, bf16[256,1,4,128]{3,0,2,1:T(8,128)(2,1)S(1)}, u32[]{:S(2)}, u32[]{:S(2)}) collective-permute-start(bf16[256,1,4,128]{3,0,2,1:T(8,128)(2,1)S(1)} %get-tuple-element.19), channel_id=1, source_target_pairs={{8,0},{16,8},{24,16},{9,1},{17,9},{25,17},{10,2},{18,10},{26,18},{... | collective-permute-start | bytes 786440 | tf_op jit(solution)/shard_map/ppermute | solution.py:47
  55.0 1.7 %fusion.10 = bf16[256,6,2,8,19]{0,2,4,3,1:T(2,128)(2,1)} fusion(bf16[256,6,2,7,2]{0,2,4,3,1:T(2,128)(2,1)S(1)} %slice.52, bf16[256,6,2,8,17]{0,2,4,3,1:T(2,128)(2,1)S(1)} %bitcast.84), kind=kLoop, calls=%fused_computation.33 | loop fusion | flops 2801664 | bytes 1855488 | tf_op jit(solution)/shard_map/conv_general_dilated | solution.py:52
  57.2 3.5 %collective-permute-done.7 = bf16[256,1,4,128]{3,0,2,1:T(8,128)(2,1)S(1)} collective-permute-done((bf16[256,1,4,128]{3,0,2,1:T(8,128)(2,1)S(1)}, bf16[256,1,4,128]{3,0,2,1:T(8,128)(2,1)S(1)}, u32[]{:S(2)}, u32[]{:S(2)}) %collective-permute-start.7) | collective-permute-done | bytes 262176 | tf_op jit(solution)/shard_map/ppermute | solution.py:47
  61.4 1.6 %convolution_convert_fusion = bf16[2,4,8,16,256]{4,2,3,1,0:T(8,128)(2,1)S(1)} fusion(bf16[256,4,4,8,16]{0,4,3,2,1:T(8,128)(2,1)S(1)} %bitcast.100, bf16[3,256,256]{2,1,0:T(8,128)(2,1)} %rev.4), kind=kOutput, calls=%fused_computation.14 | convolution fusion | flops 402915328 | bytes 1966080 | tf_op jit(solution)/shard_map/conv_general_dilated | solution.py:63
  63.1 2.1 %collective-permute-start.8 = (bf16[256,2,1,128]{0,3,2,1:T(8,128)(2,1)S(1)}, bf16[256,2,1,128]{0,3,2,1:T(8,128)(2,1)S(1)}, u32[]{:S(2)}, u32[]{:S(2)}) collective-permute-start(bf16[256,2,1,128]{0,3,2,1:T(8,128)(2,1)S(1)} %get-tuple-element.16), channel_id=1, source_target_pairs={{0,4},{4,5},{5,1},{1,2},{2,6},{6,7},{7,3},{8,12},{12,13},{13,9},{9... | collective-permute-start | bytes 393224 | tf_op jit(solution)/shard_map/ppermute | solution.py:46
  65.3 1.5 %collective-permute-start.9 = (bf16[256,2,1,128]{0,3,2,1:T(8,128)(2,1)S(1)}, bf16[256,2,1,128]{0,3,2,1:T(8,128)(2,1)S(1)}, u32[]{:S(2)}, u32[]{:S(2)}) collective-permute-start(bf16[256,2,1,128]{0,3,2,1:T(8,128)(2,1)S(1)} %get-tuple-element.17), channel_id=1, source_target_pairs={{4,0},{5,4},{1,5},{2,1},{6,2},{7,6},{3,7},{12,8},{13,12},{9,13},{1... | collective-permute-start | bytes 393224 | tf_op jit(solution)/shard_map/ppermute | solution.py:47
  67.0 1.0 %copy-done.4 = bf16[256,6,2,8,19]{0,2,4,3,1:T(2,128)(2,1)S(1)} copy-done((bf16[256,6,2,8,19]{0,2,4,3,1:T(2,128)(2,1)S(1)}, bf16[256,6,2,8,19]{0,2,4,3,1:T(2,128)(2,1)}, u32[]{:S(2)}) %copy-start.4) | copy-done | bytes 933912
  68.1 1.5 %fusion.2 = bf16[4,16,17,256]{3,1,2,0:T(8,128)(2,1)S(1)} fusion(bf16[3,3,256,256]{3,2,1,0:T(8,128)(2,1)S(1)} %bitcast.97, bf16[256,6,2,8,19]{0,2,4,3,1:T(2,128)(2,1)S(1)} %copy-done.4, pred[16,17]{0,1:T(8,128)(4,1)S(1)} %copy-done.10), kind=kOutput, calls=%fused_computation.12 | convolution fusion | flops 1284014080 | bytes 2670864 | tf_op jit(solution)/shard_map/conv_general_dilated | solution.py:52
  70.2 2.0 %collective-permute-start.3 = (bf16[256,1,4,128]{0,2,3,1:T(4,128)(2,1)S(1)}, bf16[256,1,4,128]{0,2,3,1:T(4,128)(2,1)S(1)}, u32[]{:S(2)}, u32[]{:S(2)}) collective-permute-start(bf16[256,1,4,128]{0,2,3,1:T(4,128)(2,1)S(1)} %get-tuple-element.24), channel_id=1, source_target_pairs={{0,8},{8,16},{16,24},{1,9},{9,17},{17,25},{2,10},{10,18},{18,26},{... | collective-permute-start | bytes 786440 | tf_op jit(solution)/shard_map/ppermute | solution.py:46
  72.2 2.3 %collective-permute-start.4 = (bf16[256,1,4,128]{0,2,3,1:T(4,128)(2,1)S(1)}, bf16[256,1,4,128]{0,2,3,1:T(4,128)(2,1)S(1)}, u32[]{:S(2)}, u32[]{:S(2)}) collective-permute-start(bf16[256,1,4,128]{0,2,3,1:T(4,128)(2,1)S(1)} %get-tuple-element.25), channel_id=1, source_target_pairs={{8,0},{16,8},{24,16},{9,1},{17,9},{25,17},{10,2},{18,10},{26,18},{... | collective-permute-start | bytes 786440 | tf_op jit(solution)/shard_map/ppermute | solution.py:47
  77.1 2.8 %collective-permute-done.4 = bf16[256,1,4,128]{0,2,3,1:T(4,128)(2,1)S(1)} collective-permute-done((bf16[256,1,4,128]{0,2,3,1:T(4,128)(2,1)S(1)}, bf16[256,1,4,128]{0,2,3,1:T(4,128)(2,1)S(1)}, u32[]{:S(2)}, u32[]{:S(2)}) %collective-permute-start.4) | collective-permute-done | bytes 262176 | tf_op jit(solution)/shard_map/ppermute | solution.py:47
  80.7 1.4 %convolution_convert_fusion.1 = bf16[2,4,8,16,256]{4,2,3,1,0:T(8,128)(2,1)S(1)} fusion(bf16[256,4,4,8,16]{0,2,4,3,1:T(4,128)(2,1)S(1)} %bitcast.99, bf16[3,256,256]{2,1,0:T(8,128)(2,1)S(1)} %copy-done.6), kind=kOutput, calls=%fused_computation.15 | convolution fusion | flops 402915328 | bytes 1966080 | tf_op jit(solution)/shard_map/conv_general_dilated | solution.py:63
  82.3 1.1 %copy.90 = bf16[256,2,4,128]{3,2,1,0:T(4,128)(2,1)} copy(bf16[256,2,4,128]{0,3,2,1:T(8,128)(2,1)S(1)} %bitcast.94) | data formatting | bytes 1048576 | tf_op jit(solution)/shard_map/convert_element_type | solution.py:120
  83.4 6.7 %all-to-all-start.1 = ((bf16[256,2,4,128]{3,2,1,0:T(4,128)(2,1)}), bf16[256,2,4,128]{3,2,1,0:T(4,128)(2,1)S(1)}, u32[]{:S(2)}, u32[]{:S(2)}) async-start(bf16[256,2,4,128]{3,2,1,0:T(4,128)(2,1)} %copy.90), calls=%async_computation.1 | async-start | bytes 1048576 | tf_op jit(solution)/shard_map/all_to_all | solution.py:121
  90.0 1.5 %fusion.3 = bf16[4,16,17,256]{3,1,2,0:T(8,128)(2,1)S(1)} fusion(bf16[3,3,256,256]{3,2,1,0:T(8,128)(2,1)S(1)} %bitcast.98, bf16[256,6,2,8,19]{0,2,4,3,1:T(2,128)(2,1)S(1)} %fusion.11, pred[16,17]{0,1:T(8,128)(4,1)S(1)} %copy-done.10), kind=kOutput, calls=%fused_computation.13 | convolution fusion | flops 1284014080 | bytes 2670864 | tf_op jit(solution)/shard_map/conv_general_dilated | solution.py:52
  92.5 5.3 %collective-permute-done.10 = bf16[128,2,4,128]{0,2,3,1:T(4,128)(2,1)S(1)} collective-permute-done((bf16[128,2,4,128]{0,2,3,1:T(4,128)(2,1)S(1)}, bf16[128,2,4,128]{0,2,3,1:T(4,128)(2,1)S(1)}, u32[]{:S(2)}, u32[]{:S(2)}) %collective-permute-start.10) | collective-permute-done | bytes 262176 | tf_op jit(solution)/shard_map/ppermute | solution.py:171
  98.8 1.3 %copy.106 = bf16[128,2,8,128]{3,2,1,0:T(8,128)(2,1)} copy(bf16[128,2,8,128]{0,2,3,1:T(8,128)(2,1)S(1)} %fusion.21) | data formatting | bytes 1048576
  100.2 1.8 %all-to-all-done.1 = bf16[256,2,4,128]{3,2,1,0:T(4,128)(2,1)S(1)} async-done(((bf16[256,2,4,128]{3,2,1,0:T(4,128)(2,1)}), bf16[256,2,4,128]{3,2,1,0:T(4,128)(2,1)S(1)}, u32[]{:S(2)}, u32[]{:S(2)}) %all-to-all-start.1) | async-done | bytes 524320 | tf_op jit(solution)/shard_map/all_to_all | solution.py:121
  102.1 1.1 %copy.105 = bf16[64,2,16,128]{3,2,1,0:T(8,128)(2,1)} copy(bf16[64,2,16,128]{3,0,2,1:T(8,128)(2,1)S(1)} %bitcast.96) | data formatting | bytes 1048576
  (79 shorter events, 14.5 us)
Async XLA Ops:
  0.6 0.9 copy-start
  1.8 6.8 %copy-start.7 = (s32[2,2]{1,0:T(2,128)S(1)}, s32[2,2]{1,0:T(2,128)}, u32[]{:S(2)}) copy-start(s32[2,2]{1,0:T(2,128)} %constant.140.clone) | copy-start | bytes 52
  1.8 6.8 %copy-start.8 = (s32[2,2]{1,0:T(2,128)S(1)}, s32[2,2]{1,0:T(2,128)}, u32[]{:S(2)}) copy-start(s32[2,2]{1,0:T(2,128)} %constant.139.clone) | copy-start | bytes 52
  1.8 10.5 %copy-start.5 = (bf16[64,2,16,128]{3,2,1,0:T(8,128)(2,1)S(1)}, bf16[64,2,16,128]{3,2,1,0:T(8,128)(2,1)}, u32[]{:S(2)}) copy-start(bf16[64,2,16,128]{3,2,1,0:T(8,128)(2,1)} %param.10) | copy-start | bytes 1572868
  3.1 18.1 %all-to-all-start = ((bf16[4,2,18432]{2,1,0:T(2,128)(2,1)}), bf16[4,2,18432]{2,1,0:T(2,128)(2,1)S(1)}, u32[]{:S(2)}, u32[]{:S(2)}) async-start(bf16[4,2,18432]{2,1,0:T(2,128)(2,1)} %reshape.130), calls=%async_computation | async-start | bytes 589824 | tf_op jit(solution)/shard_map/all_to_all | solution.py:83
  8.6 5.5 %copy-start.9 = (s32[2,4]{1,0:T(2,128)S(1)}, s32[2,4]{1,0:T(2,128)}, u32[]{:S(2)}) copy-start(s32[2,4]{1,0:T(2,128)} %constant.141.clone) | copy-start | bytes 100
  12.7 6.9 %collective-permute-start.5 = (bf16[2,64,2,4,128]{4,1,3,2,0:T(8,128)(2,1)S(1)}, bf16[2,64,2,4,128]{4,1,3,2,0:T(8,128)(2,1)S(1)}, u32[]{:S(2)}, u32[]{:S(2)}) collective-permute-start(bf16[2,64,2,4,128]{4,1,3,2,0:T(8,128)(2,1)S(1)} %pad_maximum_fusion.4), channel_id=1, source_target_pairs={{0,4},{4,0},{1,5},{5,1},{2,6},{6,2},{3,7},{7,3},{8,12},{12,8},{9,1... | collective-permute-start | bytes 786440 | tf_op jit(solution)/shard_map/ppermute | solution.py:140
  20.4 5.2 %copy-start.1 = (bf16[128,2,32,128]{3,2,1,0:T(8,128)(2,1)S(1)}, bf16[128,2,32,128]{3,2,1,0:T(8,128)(2,1)}, u32[]{:S(2)}) copy-start(bf16[128,2,32,128]{3,2,1,0:T(8,128)(2,1)} %param.7) | copy-start | bytes 6291460
  21.3 4.2 %copy-start.2 = (bf16[4,2,18432]{2,1,0:T(2,128)(2,1)}, bf16[4,2,18432]{2,1,0:T(2,128)(2,1)S(1)}, u32[]{:S(2)}) copy-start(bf16[4,2,18432]{2,1,0:T(2,128)(2,1)S(1)} %all-to-all-done) | copy-start | bytes 884740
  21.3 25.0 %all-to-all-start.2 = ((bf16[4,64,2,4,128]{4,1,3,2,0:T(8,128)(2,1)}), bf16[4,64,2,4,128]{4,1,3,2,0:T(8,128)(2,1)S(1)}, u32[]{:S(2)}, u32[]{:S(2)}) async-start(bf16[4,64,2,4,128]{4,1,3,2,0:T(8,128)(2,1)} %broadcast_select_fusion.2), calls=%async_computation.2 | async-start | bytes 1048576 | tf_op jit(solution)/shard_map/all_to_all | solution.py:149
  26.9 11.2 %collective-permute-start = (bf16[128,2,6,128]{3,2,1,0:T(8,128)(2,1)}, bf16[128,2,6,128]{3,2,1,0:T(8,128)(2,1)S(1)}, u32[]{:S(2)}, u32[]{:S(2)}) collective-permute-start(bf16[128,2,6,128]{3,2,1,0:T(8,128)(2,1)} %get-tuple-element.11), channel_id=1, source_target_pairs={{0,4},{4,0},{1,5},{5,1},{2,6},{6,2},{3,7},{7,3},{8,12},{12,8},{9,1... | collective-permute-start | bytes 1179656 | tf_op jit(solution)/shard_map/ppermute | solution.py:110
  42.8 1.0 copy-start.3
  45.0 11.6 %collective-permute-start.1 = (bf16[3,3,64,256]{3,2,1,0:T(8,128)(2,1)S(1)}, bf16[3,3,64,256]{3,2,1,0:T(8,128)(2,1)S(1)}, u32[]{:S(2)}, u32[]{:S(2)}) collective-permute-start(bf16[3,3,64,256]{3,2,1,0:T(8,128)(2,1)S(1)} %squeeze.6), channel_id=1, source_target_pairs={{0,4},{4,0},{1,5},{5,1},{2,6},{6,2},{3,7},{7,3},{8,12},{12,8},{9,1... | collective-permute-start | bytes 884744 | tf_op jit(solution)/shard_map/ppermute | solution.py:25
  46.4 10.8 %collective-permute-start.6 = (bf16[256,1,4,128]{3,0,2,1:T(8,128)(2,1)S(1)}, bf16[256,1,4,128]{3,0,2,1:T(8,128)(2,1)S(1)}, u32[]{:S(2)}, u32[]{:S(2)}) collective-permute-start(bf16[256,1,4,128]{3,0,2,1:T(8,128)(2,1)S(1)} %get-tuple-element.18), channel_id=1, source_target_pairs={{0,8},{8,16},{16,24},{1,9},{9,17},{17,25},{2,10},{10,18},{18,26},{... | collective-permute-start | bytes 786440 | tf_op jit(solution)/shard_map/ppermute | solution.py:46
  53.0 7.7 %collective-permute-start.7 = (bf16[256,1,4,128]{3,0,2,1:T(8,128)(2,1)S(1)}, bf16[256,1,4,128]{3,0,2,1:T(8,128)(2,1)S(1)}, u32[]{:S(2)}, u32[]{:S(2)}) collective-permute-start(bf16[256,1,4,128]{3,0,2,1:T(8,128)(2,1)S(1)} %get-tuple-element.19), channel_id=1, source_target_pairs={{8,0},{16,8},{24,16},{9,1},{17,9},{25,17},{10,2},{18,10},{26,18},{... | collective-permute-start | bytes 786440 | tf_op jit(solution)/shard_map/ppermute | solution.py:47
  57.1 9.6 %collective-permute-start.2 = (bf16[3,3,128,256]{3,2,1,0:T(8,128)(2,1)S(1)}, bf16[3,3,128,256]{3,2,1,0:T(8,128)(2,1)S(1)}, u32[]{:S(2)}, u32[]{:S(2)}) collective-permute-start(bf16[3,3,128,256]{3,2,1,0:T(8,128)(2,1)S(1)} %fusion.18), channel_id=1, source_target_pairs={{0,8},{8,0},{16,24},{24,16},{1,9},{9,1},{17,25},{25,17},{2,10},{10... | collective-permute-start | bytes 1769480 | tf_op jit(solution)/shard_map/ppermute | solution.py:84
  63.1 11.4 %collective-permute-start.8 = (bf16[256,2,1,128]{0,3,2,1:T(8,128)(2,1)S(1)}, bf16[256,2,1,128]{0,3,2,1:T(8,128)(2,1)S(1)}, u32[]{:S(2)}, u32[]{:S(2)}) collective-permute-start(bf16[256,2,1,128]{0,3,2,1:T(8,128)(2,1)S(1)} %get-tuple-element.16), channel_id=1, source_target_pairs={{0,4},{4,5},{5,1},{1,2},{2,6},{6,7},{7,3},{8,12},{12,13},{13,9},{9... | collective-permute-start | bytes 393224 | tf_op jit(solution)/shard_map/ppermute | solution.py:46
  65.3 9.3 %collective-permute-start.9 = (bf16[256,2,1,128]{0,3,2,1:T(8,128)(2,1)S(1)}, bf16[256,2,1,128]{0,3,2,1:T(8,128)(2,1)S(1)}, u32[]{:S(2)}, u32[]{:S(2)}) collective-permute-start(bf16[256,2,1,128]{0,3,2,1:T(8,128)(2,1)S(1)} %get-tuple-element.17), channel_id=1, source_target_pairs={{4,0},{5,4},{1,5},{2,1},{6,2},{7,6},{3,7},{12,8},{13,12},{9,13},{1... | collective-permute-start | bytes 393224 | tf_op jit(solution)/shard_map/ppermute | solution.py:47
  66.9 1.2 %copy-start.4 = (bf16[256,6,2,8,19]{0,2,4,3,1:T(2,128)(2,1)S(1)}, bf16[256,6,2,8,19]{0,2,4,3,1:T(2,128)(2,1)}, u32[]{:S(2)}) copy-start(bf16[256,6,2,8,19]{0,2,4,3,1:T(2,128)(2,1)} %fusion.10) | copy-start | bytes 2801668
  66.9 1.2 %copy-start.10 = (pred[16,17]{0,1:T(8,128)(4,1)S(1)}, pred[16,17]{0,1:T(8,128)(4,1)}, u32[]{:S(2)}) copy-start(pred[16,17]{0,1:T(8,128)(4,1)} %constant.161) | copy-start | bytes 820
  70.2 6.9 %collective-permute-start.3 = (bf16[256,1,4,128]{0,2,3,1:T(4,128)(2,1)S(1)}, bf16[256,1,4,128]{0,2,3,1:T(4,128)(2,1)S(1)}, u32[]{:S(2)}, u32[]{:S(2)}) collective-permute-start(bf16[256,1,4,128]{0,2,3,1:T(4,128)(2,1)S(1)} %get-tuple-element.24), channel_id=1, source_target_pairs={{0,8},{8,16},{16,24},{1,9},{9,17},{17,25},{2,10},{10,18},{18,26},{... | collective-permute-start | bytes 786440 | tf_op jit(solution)/shard_map/ppermute | solution.py:46
  72.2 7.7 %collective-permute-start.4 = (bf16[256,1,4,128]{0,2,3,1:T(4,128)(2,1)S(1)}, bf16[256,1,4,128]{0,2,3,1:T(4,128)(2,1)S(1)}, u32[]{:S(2)}, u32[]{:S(2)}) collective-permute-start(bf16[256,1,4,128]{0,2,3,1:T(4,128)(2,1)S(1)} %get-tuple-element.25), channel_id=1, source_target_pairs={{8,0},{16,8},{24,16},{9,1},{17,9},{25,17},{10,2},{18,10},{26,18},{... | collective-permute-start | bytes 786440 | tf_op jit(solution)/shard_map/ppermute | solution.py:47
  77.1 3.7 %copy-start.6 = (bf16[3,256,256]{2,1,0:T(8,128)(2,1)S(1)}, bf16[3,256,256]{2,1,0:T(8,128)(2,1)}, u32[]{:S(2)}) copy-start(bf16[3,256,256]{2,1,0:T(8,128)(2,1)} %param.9) | copy-start | bytes 1179652
  83.4 18.6 %all-to-all-start.1 = ((bf16[256,2,4,128]{3,2,1,0:T(4,128)(2,1)}), bf16[256,2,4,128]{3,2,1,0:T(4,128)(2,1)S(1)}, u32[]{:S(2)}, u32[]{:S(2)}) async-start(bf16[256,2,4,128]{3,2,1,0:T(4,128)(2,1)} %copy.90), calls=%async_computation.1 | async-start | bytes 1048576 | tf_op jit(solution)/shard_map/all_to_all | solution.py:121
  92.2 5.6 %collective-permute-start.10 = (bf16[128,2,4,128]{0,2,3,1:T(4,128)(2,1)S(1)}, bf16[128,2,4,128]{0,2,3,1:T(4,128)(2,1)S(1)}, u32[]{:S(2)}, u32[]{:S(2)}) collective-permute-start(bf16[128,2,4,128]{0,2,3,1:T(4,128)(2,1)S(1)} %get-tuple-element.15), channel_id=1, source_target_pairs={{0,4},{1,5},{2,6},{3,7},{4,0},{5,1},{6,2},{7,3},{8,12},{9,13},{10,... | collective-permute-start | bytes 786440 | tf_op jit(solution)/shard_map/ppermute | solution.py:171

commit v21 on v18

--- a/solution.py
+++ b/solution.py
@@ -80,13 +80,11 @@
     half = c_loc // 2
     mine = lax.dynamic_slice_in_dim(weight, core * half, half, 2)
     spread = jnp.broadcast_to(mine[None], (filts,) + mine.shape)
-    by_filt = gather_blocks(lax.all_to_all(spread, "filt", 0, 4, tiled=True)[0], "chan", 2)
+    by_filt = lax.all_to_all(spread, "filt", 0, 4, tiled=True)[0]
     other = lax.ppermute(by_filt, "slab", [(i, i ^ 1) for i in range(slabs)])
     first = jnp.where(core == 0, by_filt, other)
     second = jnp.where(core == 0, other, by_filt)
-    split = lambda w: w.reshape(3, 3, chans, 1, half, w.shape[-1])
-    whole = jnp.concatenate([split(first), split(second)], axis=3)
-    return whole.reshape(3, 3, chans * c_loc, whole.shape[-1])
+    return jnp.concatenate([first, second], axis=2)
 
 
 def sub_block(chan, filt, filts):
@@ -97,7 +95,7 @@
     return f if c % 2 == 0 else filts - 1 - f
 
 
-def forward(volume, weight, depth_weight):
+def forward(volume, local_weight):
     chans = lax.axis_size("chan")
     filts = lax.axis_size("filt")
     chan = lax.axis_index("chan")
@@ -105,11 +103,21 @@
     rows = volume.shape[2] // (chans * filts)
     padded = jnp.pad(volume, ((0, 0), (0, 0), (1, 1), (0, 0)))
     window = lambda c: lax.dynamic_slice_in_dim(padded, (c * filts + filt) * rows, rows + 2, 2)
-    pieces = [window(chan)]
+    pieces, kernels = [window(chan)], [local_weight]
     for k in range(1, chans):
-        pieces.append(lax.ppermute(window((chan + k) % chans), "chan", shift_pairs(chans, k)))
+        a = window((chan + k) % chans)
+        tile = a[0].size
+        if local_weight.size % tile == 0:
+            both = jnp.concatenate([a, local_weight.reshape((-1,) + a.shape[1:])], axis=0)
+            both = lax.ppermute(both, "chan", shift_pairs(chans, k))
+            pieces.append(both[: a.shape[0]])
+            kernels.append(both[a.shape[0] :].reshape(local_weight.shape))
+        else:
+            pieces.append(lax.ppermute(a, "chan", shift_pairs(chans, k)))
+            kernels.append(lax.ppermute(local_weight, "chan", shift_pairs(chans, k)))
+    weight = order_blocks(kernels, chan, 2)
     all_channels = order_blocks(pieces, chan, 0)
-    return plane_conv(all_channels, weight, "HWIO").astype(jnp.bfloat16)
+    return plane_conv(all_channels, weight, "HWIO").astype(jnp.bfloat16), weight
 
 
 def forward_out(deep, depth_weight):
@@ -174,7 +182,7 @@
 
 def local(volume, plane_weight, depth_weight, grad_out):
     weight = gather_weight(plane_weight)
-    mid = forward(volume, weight, depth_weight)
+    mid, weight = forward(volume, weight)
     all_filters = backward(grad_out, weight, depth_weight)
     deep = halo(jnp.concatenate([mid, all_filters]), "slab", 1)
     output = forward_out(deep[: mid.shape[0]], depth_weight)

time: 94.2 us -> 110 us (1.17)
  waiting for transfers between devices: 20.9 us -> 28 us
  local copies, waits for them, and re-layouts: 19.8 us -> 26.3 us
  other arithmetic: 12.2 us -> 15.1 us
    all_to_all x1, waiting for transfers between devices: 3.37 us -> 14.1 us  [backward(): all_filters = lax.all_to_all(blocks, 'filt', 0, 0, tiled=True)]
    ppermute x1, waiting for transfers between devices: 6.26 us -> 0.01 us  [backward(): lax.ppermute(send, 'chan', shift_pairs(chans, k))]
    unnamed x26 -> x42, local copies, waits for them, and re-layouts: 6.47 us -> 9.44 us
    ppermute x2 -> x1, waiting for transfers between devices: 0.39 us -> 3.31 us  [forward(): both = lax.ppermute(both, 'chan', shift_pairs(chans, k))]
    ppermute x2 -> x1, starting transfers between devices: 4.15 us -> 1.24 us  [forward(): both = lax.ppermute(both, 'chan', shift_pairs(chans, k))]
    dynamic_slice x5, local copies, waits for them, and re-layouts: 0.37 us -> 2.54 us  [backward(): lax.dynamic_slice_in_dim(grad_out, table[q] * rows, rows, 2)]
    dynamic_slice x1, local copies, waits for them, and re-layouts: 3.04 us -> 1.34 us  [forward(): lax.dynamic_slice_in_dim(padded, (c * filts + filt) * rows, rows + 2, 2)]
    and x1, other arithmetic: 0.02 us -> 1.28 us  [backward(): blocks = jnp.take(received, jnp.array(slot, jnp.int32)[chan], axis=0)]
  transfers between devices with their start and end apart: 12 -> 11, of which waited for: 6 -> 5; matrix products, arithmetic and copies ran while one was open for 27% -> 23% of each run, Pallas kernels for 0% -> 0%
where the time goes in v21:
time: 110 us; the launch traced here: 109 us
  starting transfers between devices  30.1 us (27%)
  waiting for transfers between devices  28 us (25%)
  local copies, waits for them, and re-layouts  26.3 us (24%)
  other arithmetic  15.1 us (14%)
  matrix products  5.78 us (5%)
  between operations  3.77 us (3%)
    all_to_all x1, waiting for transfers between devices, backward(): all_filters = lax.all_to_all(blocks, 'filt', 0, 0, tiled=True)  14.1 us
    unnamed x42, local copies, waits for them, and re-layouts  9.44 us
    ppermute x2, starting transfers between devices, halo(): lax.ppermute(lax.slice_in_dim(x, length - 1, length, axis=dim), axis, up)  6.94 us
    all_to_all x1, starting transfers between devices, gather_weight(): by_filt = lax.all_to_all(spread, 'filt', 0, 4, tiled=True)[0]  5.42 us
    ppermute x2, waiting for transfers between devices, halo(): after = lax.ppermute(lax.slice_in_dim(x, 0, 1, axis=dim), axis, down)  4.4 us
    all_to_all x1, starting transfers between devices, forward_out(): return lax.all_to_all(out, 'filt', 0, 2, tiled=True)  4.31 us
    ppermute x1, waiting for transfers between devices, backward_in(): lax.ppermute(lax.dynamic_slice_in_dim(grad_in, target * c_loc, c_loc, 0),...  3.96 us
    all_to_all x1, starting transfers between devices, backward(): all_filters = lax.all_to_all(blocks, 'filt', 0, 0, tiled=True)  3.65 us
  transfers between devices with their start and end apart: 11, of which 5 were waited for; matrix products, arithmetic and copies ran while one was open for 23% of the time, Pallas kernels for 0%

profile of v21, /device:TPU:1, one launch (start us, length us, event | category | flops | bytes accessed | tf_op | source)
XLA Modules:
  0.0 109.0 jit_solution(3858935451668689595)
XLA Ops:
  2.0 1.2 %reshape.126 = bf16[4,2,18432]{2,1,0:T(2,128)(2,1)} reshape(bf16[4,3,3,64,64]{4,3,2,1,0:T(8,128)(2,1)S(1)} %broadcast_in_dim.28) | data formatting | bytes 589824
  3.1 5.4 %all-to-all-start = ((bf16[4,2,18432]{2,1,0:T(2,128)(2,1)}), bf16[4,2,18432]{2,1,0:T(2,128)(2,1)S(1)}, u32[]{:S(2)}, u32[]{:S(2)}) async-start(bf16[4,2,18432]{2,1,0:T(2,128)(2,1)} %reshape.126), calls=%async_computation | async-start | bytes 589824 | tf_op jit(solution)/shard_map/all_to_all | solution.py:83
  14.0 1.2 %collective-permute-start.2 = (bf16[2,64,2,4,128]{4,1,3,2,0:T(8,128)(2,1)}, bf16[2,64,2,4,128]{4,1,3,2,0:T(8,128)(2,1)}, u32[]{:S(2)}, u32[]{:S(2)}) collective-permute-start(bf16[2,64,2,4,128]{4,1,3,2,0:T(8,128)(2,1)} %pad_maximum_fusion.5), channel_id=1, source_target_pairs={{0,4},{4,0},{1,5},{5,1},{2,6},{6,2},{3,7},{7,3},{8,12},{12,8},{9,1... | collective-permute-start | bytes 786440 | tf_op jit(solution)/shard_map/ppermute | solution.py:148
  17.4 1.1 %squeeze.6 = bf16[3,3,64,256]{3,2,1,0:T(8,128)(2,1)} reshape(bf16[1,3,3,64,4,64]{5,4,3,2,1,0:T(4,128)(2,1)S(1)} %copy.57) | data formatting | bytes 589824 | tf_op jit(solution)/shard_map/squeeze | solution.py:83
  18.5 2.5 %collective-permute-start = (bf16[3,3,64,256]{3,2,1,0:T(8,128)(2,1)}, bf16[3,3,64,256]{3,2,1,0:T(8,128)(2,1)}, u32[]{:S(2)}, u32[]{:S(2)}) collective-permute-start(bf16[3,3,64,256]{3,2,1,0:T(8,128)(2,1)} %squeeze.6), channel_id=1, source_target_pairs={{0,8},{8,0},{16,24},{24,16},{1,9},{9,1},{17,25},{25,17},{2,10},{10... | collective-permute-start | bytes 884744 | tf_op jit(solution)/shard_map/ppermute | solution.py:84
  21.1 1.3 %compare_and_fusion = pred[4]{0:T(512)(128)(4,1)} fusion(s32[2,4]{1,0:T(2,128)} %constant.133.clone, s32[]{:T(128)S(6)} %select_n.129), kind=kLoop, calls=%fused_computation.78 | loop fusion | flops 24 | bytes 24 | tf_op jit(solution)/shard_map/jit(_take)/and | solution.py:156
  23.9 1.3 %pad_dynamic-slice_fusion = (bf16[128,2,6,128]{3,2,1,0:T(8,128)(2,1)}, bf16[128,2,6,128]{3,2,1,0:T(8,128)(2,1)S(1)}) fusion(s32[]{:T(128)S(6)} %select_n.126, bf16[128,2,32,128]{3,2,1,0:T(8,128)(2,1)S(1)} %copy-done.2, s32[]{:T(128)S(6)} %select_n.120), kind=kLoop, calls=%fused_computation.1 | loop fusion | bytes 2883592 | tf_op jit(solution)/shard_map/dynamic_slice | solution.py:105
  27.1 1.1 %broadcast_select_fusion.2 = (bf16[3,3,64,256]{3,2,1,0:T(8,128)(2,1)S(1)}, bf16[3,3,64,256]{3,2,1,0:T(8,128)(2,1)S(1)}) fusion(bf16[3,3,64,256]{3,2,1,0:T(8,128)(2,1)} %squeeze.6, bf16[3,3,64,256]{3,2,1,0:T(8,128)(2,1)} %collective-permute-done, pred[]{:T(512)S(6)} %eq.20), kind=kLoop, calls=%fused_computation.51 | loop fusion | flops 294912 | bytes 1179649 | tf_op jit(solution)/shard_map/jit(_where)/select_n | solution.py:85
  28.8 1.2 %copy.58 = bf16[320,2,6,128]{3,0,2,1:T(8,128)(2,1)} copy(bf16[320,2,6,128]{3,2,1,0:T(8,128)(2,1)S(1)} %pad_maximum_fusion.1) | data formatting | bytes 1966080 | tf_op jit(solution)/shard_map/concatenate | solution.py:111
  30.0 1.2 %collective-permute-start.1 = (bf16[320,2,6,128]{3,0,2,1:T(8,128)(2,1)}, bf16[320,2,6,128]{3,0,2,1:T(8,128)(2,1)S(1)}, u32[]{:S(2)}, u32[]{:S(2)}) collective-permute-start(bf16[320,2,6,128]{3,0,2,1:T(8,128)(2,1)} %copy.58), channel_id=1, source_target_pairs={{0,4},{4,0},{1,5},{5,1},{2,6},{6,2},{3,7},{7,3},{8,12},{12,8},{9,1... | collective-permute-start | bytes 2949128 | tf_op jit(solution)/shard_map/ppermute | solution.py:112
  32.2 3.7 %all-to-all-start.1 = ((bf16[4,64,2,4,128]{4,1,3,2,0:T(8,128)(2,1)}), bf16[4,64,2,4,128]{4,1,3,2,0:T(8,128)(2,1)S(1)}, u32[]{:S(2)}, u32[]{:S(2)}) async-start(bf16[4,64,2,4,128]{4,1,3,2,0:T(8,128)(2,1)} %broadcast_select_fusion), calls=%async_computation.1 | async-start | bytes 1048576 | tf_op jit(solution)/shard_map/all_to_all | solution.py:157
  35.9 14.1 %all-to-all-done.1 = bf16[4,64,2,4,128]{4,1,3,2,0:T(8,128)(2,1)S(1)} async-done(((bf16[4,64,2,4,128]{4,1,3,2,0:T(8,128)(2,1)}), bf16[4,64,2,4,128]{4,1,3,2,0:T(8,128)(2,1)S(1)}, u32[]{:S(2)}, u32[]{:S(2)}) %all-to-all-start.1) | async-done | bytes 524320 | tf_op jit(solution)/shard_map/all_to_all | solution.py:157
  50.3 3.3 %collective-permute-done.1 = bf16[320,2,6,128]{3,0,2,1:T(8,128)(2,1)S(1)} collective-permute-done((bf16[320,2,6,128]{3,0,2,1:T(8,128)(2,1)}, bf16[320,2,6,128]{3,0,2,1:T(8,128)(2,1)S(1)}, u32[]{:S(2)}, u32[]{:S(2)}) %collective-permute-start.1) | collective-permute-done | bytes 983072 | tf_op jit(solution)/shard_map/ppermute | solution.py:112
  54.6 3.4 %fusion.7 = bf16[256,6,2,128]{3,1,2,0:T(8,128)(2,1)S(1)} fusion(s32[]{:T(128)S(6)} %select_n.128, bf16[128,2,6,128]{3,2,1,0:T(8,128)(2,1)S(1)} %copy.90, bf16[128,2,6,128]{3,2,1,0:T(8,128)(2,1)S(1)} %copy-done.3), kind=kLoop, calls=%fused_computation.21 | loop fusion | flops 1179648 | bytes 1572868 | tf_op jit(solution)/shard_map/jit(_roll_dynamic)/dynamic_slice | solution.py:19
  58.0 1.3 %copy.91 = bf16[256,6,2,128]{0,2,3,1:T(2,128)(2,1)S(1)} copy(bf16[256,6,2,128]{3,1,2,0:T(8,128)(2,1)S(1)} %fusion.7) | data formatting | bytes 1572864
  60.1 1.6 %fusion.12 = bf16[256,6,2,8,19]{0,2,4,3,1:T(2,128)(2,1)} fusion(bf16[256,6,2,7,2]{0,2,4,3,1:T(2,128)(2,1)S(1)} %slice.61, bf16[256,6,2,8,17]{0,2,4,3,1:T(2,128)(2,1)S(1)} %bitcast.77), kind=kLoop, calls=%fused_computation.32 | loop fusion | flops 2801664 | bytes 1855488 | tf_op jit(solution)/shard_map/conv_general_dilated | solution.py:52
  63.6 1.5 %fusion.2 = bf16[4,16,17,256]{3,1,2,0:T(8,128)(2,1)S(1)} fusion(bf16[3,3,512,256]{3,2,1,0:T(8,128)(2,1)S(1)} %constant_dynamic-update-slice_fusion, s32[]{:T(128)S(6)} %select_n.128, bf16[256,6,2,8,19]{0,2,4,3,1:T(2,128)(2,1)S(1)} %copy-done.4, pred[16,17]{0,1:T(8,128)(4,1)S(1)} %copy-done.14), kind=kOutput, calls=%fused_computation.13 | convolution fusion | flops 1284014080 | bytes 2673668 | tf_op jit(solution)/shard_map/conv_general_dilated | solution.py:52
  66.1 3.8 %collective-permute-start.3 = (bf16[512,1,4,128]{0,2,3,1:T(4,128)(2,1)S(1)}, bf16[512,1,4,128]{0,2,3,1:T(4,128)(2,1)S(1)}, u32[]{:S(2)}, u32[]{:S(2)}) collective-permute-start(bf16[512,1,4,128]{0,2,3,1:T(4,128)(2,1)S(1)} %get-tuple-element.12), channel_id=1, source_target_pairs={{0,8},{8,16},{16,24},{1,9},{9,17},{17,25},{2,10},{10,18},{18,26},{... | collective-permute-start | bytes 1572872 | tf_op jit(solution)/shard_map/ppermute | solution.py:46
  69.9 2.1 %collective-permute-start.4 = (bf16[512,1,4,128]{0,2,3,1:T(4,128)(2,1)S(1)}, bf16[512,1,4,128]{0,2,3,1:T(4,128)(2,1)S(1)}, u32[]{:S(2)}, u32[]{:S(2)}) collective-permute-start(bf16[512,1,4,128]{0,2,3,1:T(4,128)(2,1)S(1)} %get-tuple-element.13), channel_id=1, source_target_pairs={{8,0},{16,8},{24,16},{9,1},{17,9},{25,17},{10,2},{18,10},{26,18},{... | collective-permute-start | bytes 1572872 | tf_op jit(solution)/shard_map/ppermute | solution.py:47
  72.1 1.8 %rev.4 = bf16[3,256,256]{2,1,0:T(8,128)(2,1)} reverse(bf16[3,256,256]{2,1,0:T(8,128)(2,1)} %param.9), dimensions={0} | reverse | bytes 786432 | tf_op jit(solution)/shard_map/rev | solution.py:168
  73.8 2.1 %collective-permute-done.3 = bf16[512,1,4,128]{0,2,3,1:T(4,128)(2,1)S(1)} collective-permute-done((bf16[512,1,4,128]{0,2,3,1:T(4,128)(2,1)S(1)}, bf16[512,1,4,128]{0,2,3,1:T(4,128)(2,1)S(1)}, u32[]{:S(2)}, u32[]{:S(2)}) %collective-permute-start.3) | collective-permute-done | bytes 524320 | tf_op jit(solution)/shard_map/ppermute | solution.py:46
  76.0 4.4 %collective-permute-done.4 = bf16[512,1,4,128]{0,2,3,1:T(4,128)(2,1)S(1)} collective-permute-done((bf16[512,1,4,128]{0,2,3,1:T(4,128)(2,1)S(1)}, bf16[512,1,4,128]{0,2,3,1:T(4,128)(2,1)S(1)}, u32[]{:S(2)}, u32[]{:S(2)}) %collective-permute-start.4) | collective-permute-done | bytes 524320 | tf_op jit(solution)/shard_map/ppermute | solution.py:47
  82.4 1.4 %convolution_convert_fusion = bf16[2,4,8,16,256]{4,2,3,1,0:T(8,128)(2,1)S(1)} fusion(bf16[256,4,4,8,16]{0,2,4,3,1:T(4,128)(2,1)S(1)} %bitcast.88, bf16[3,256,256]{2,1,0:T(8,128)(2,1)S(1)} %copy-done.8), kind=kOutput, calls=%fused_computation.16 | convolution fusion | flops 402915328 | bytes 1966080 | tf_op jit(solution)/shard_map/conv_general_dilated | solution.py:63
  83.9 3.2 %collective-permute-start.5 = (bf16[256,2,1,128]{0,3,2,1:T(8,128)(2,1)S(1)}, bf16[256,2,1,128]{0,3,2,1:T(8,128)(2,1)S(1)}, u32[]{:S(2)}, u32[]{:S(2)}) collective-permute-start(bf16[256,2,1,128]{0,3,2,1:T(8,128)(2,1)S(1)} %get-tuple-element.18), channel_id=1, source_target_pairs={{0,4},{4,5},{5,1},{1,2},{2,6},{6,7},{7,3},{8,12},{12,13},{13,9},{9... | collective-permute-start | bytes 393224 | tf_op jit(solution)/shard_map/ppermute | solution.py:46
  87.0 1.3 %collective-permute-start.6 = (bf16[256,2,1,128]{0,3,2,1:T(8,128)(2,1)S(1)}, bf16[256,2,1,128]{0,3,2,1:T(8,128)(2,1)S(1)}, u32[]{:S(2)}, u32[]{:S(2)}) collective-permute-start(bf16[256,2,1,128]{0,3,2,1:T(8,128)(2,1)S(1)} %get-tuple-element.19), channel_id=1, source_target_pairs={{4,0},{5,4},{1,5},{2,1},{6,2},{7,6},{3,7},{12,8},{13,12},{9,13},{1... | collective-permute-start | bytes 393224 | tf_op jit(solution)/shard_map/ppermute | solution.py:47
  88.3 1.4 %convolution_convert_fusion.1 = bf16[2,4,8,16,256]{4,2,3,1,0:T(8,128)(2,1)S(1)} fusion(bf16[256,4,4,8,16]{0,2,4,3,1:T(4,128)(2,1)S(1)} %bitcast.87, bf16[3,256,256]{2,1,0:T(8,128)(2,1)S(1)} %copy-done.7), kind=kOutput, calls=%fused_computation.17 | convolution fusion | flops 402915328 | bytes 1966080 | tf_op jit(solution)/shard_map/conv_general_dilated | solution.py:63
  90.9 4.3 %all-to-all-start.2 = ((bf16[256,2,4,128]{3,2,1,0:T(4,128)(2,1)}), bf16[256,2,4,128]{3,2,1,0:T(4,128)(2,1)S(1)}, u32[]{:S(2)}, u32[]{:S(2)}) async-start(bf16[256,2,4,128]{3,2,1,0:T(4,128)(2,1)} %copy.74), calls=%async_computation.2 | async-start | bytes 1048576 | tf_op jit(solution)/shard_map/all_to_all | solution.py:129
  97.9 1.5 %fusion.3 = bf16[4,16,17,256]{3,1,2,0:T(8,128)(2,1)S(1)} fusion(bf16[3,3,512,256]{3,2,1,0:T(8,128)(2,1)S(1)} %copy-done.10, s32[]{:T(128)S(6)} %select_n.128, bf16[256,6,2,8,19]{0,2,4,3,1:T(2,128)(2,1)S(1)} %fusion.13, pred[16,17]{0,1:T(8,128)(4,1)S(1)} %copy-done.14), kind=kOutput, calls=%fused_computation.14 | convolution fusion | flops 1284014080 | bytes 2673668 | tf_op jit(solution)/shard_map/conv_general_dilated | solution.py:52
  100.1 1.3 %collective-permute-start.7 = (bf16[128,2,4,128]{0,2,3,1:T(4,128)(2,1)S(1)}, bf16[128,2,4,128]{0,2,3,1:T(4,128)(2,1)S(1)}, u32[]{:S(2)}, u32[]{:S(2)}) collective-permute-start(bf16[128,2,4,128]{0,2,3,1:T(4,128)(2,1)S(1)} %get-tuple-element.17), channel_id=1, source_target_pairs={{0,4},{1,5},{2,6},{3,7},{4,0},{5,1},{6,2},{7,3},{8,12},{9,13},{10,... | collective-permute-start | bytes 786440 | tf_op jit(solution)/shard_map/ppermute | solution.py:179
  101.4 4.0 %collective-permute-done.7 = bf16[128,2,4,128]{0,2,3,1:T(4,128)(2,1)S(1)} collective-permute-done((bf16[128,2,4,128]{0,2,3,1:T(4,128)(2,1)S(1)}, bf16[128,2,4,128]{0,2,3,1:T(4,128)(2,1)S(1)}, u32[]{:S(2)}, u32[]{:S(2)}) %collective-permute-start.7) | collective-permute-done | bytes 262176 | tf_op jit(solution)/shard_map/ppermute | solution.py:179
  106.4 1.3 %copy.85 = bf16[128,2,8,128]{3,2,1,0:T(8,128)(2,1)} copy(bf16[128,2,8,128]{0,2,3,1:T(8,128)(2,1)S(1)} %fusion.20) | data formatting | bytes 1048576
  107.8 1.1 %copy.84 = bf16[64,2,16,128]{3,2,1,0:T(8,128)(2,1)} copy(bf16[64,2,16,128]{3,0,2,1:T(8,128)(2,1)S(1)} %bitcast.86) | data formatting | bytes 1048576
  (94 shorter events, 23.6 us)
Async XLA Ops:
  0.6 0.9 copy-start
  0.6 7.9 %copy-start.12 = (s32[2,2]{1,0:T(2,128)S(1)}, s32[2,2]{1,0:T(2,128)}, u32[]{:S(2)}) copy-start(s32[2,2]{1,0:T(2,128)} %constant.131.clone) | copy-start | bytes 52
  0.7 7.9 %copy-start.13 = (s32[2,2]{1,0:T(2,128)S(1)}, s32[2,2]{1,0:T(2,128)}, u32[]{:S(2)}) copy-start(s32[2,2]{1,0:T(2,128)} %constant.132.clone) | copy-start | bytes 52
  0.7 11.6 %copy-start.5 = (bf16[64,2,16,128]{3,2,1,0:T(8,128)(2,1)S(1)}, bf16[64,2,16,128]{3,2,1,0:T(8,128)(2,1)}, u32[]{:S(2)}) copy-start(bf16[64,2,16,128]{3,2,1,0:T(8,128)(2,1)} %param.10) | copy-start | bytes 1572868
  3.1 13.5 %all-to-all-start = ((bf16[4,2,18432]{2,1,0:T(2,128)(2,1)}), bf16[4,2,18432]{2,1,0:T(2,128)(2,1)S(1)}, u32[]{:S(2)}, u32[]{:S(2)}) async-start(bf16[4,2,18432]{2,1,0:T(2,128)(2,1)} %reshape.126), calls=%async_computation | async-start | bytes 589824 | tf_op jit(solution)/shard_map/all_to_all | solution.py:83
  13.3 10.7 %copy-start.2 = (bf16[128,2,32,128]{3,2,1,0:T(8,128)(2,1)S(1)}, bf16[128,2,32,128]{3,2,1,0:T(8,128)(2,1)}, u32[]{:S(2)}) copy-start(bf16[128,2,32,128]{3,2,1,0:T(8,128)(2,1)} %param.7) | copy-start | bytes 6291460
  14.0 11.3 %collective-permute-start.2 = (bf16[2,64,2,4,128]{4,1,3,2,0:T(8,128)(2,1)}, bf16[2,64,2,4,128]{4,1,3,2,0:T(8,128)(2,1)}, u32[]{:S(2)}, u32[]{:S(2)}) collective-permute-start(bf16[2,64,2,4,128]{4,1,3,2,0:T(8,128)(2,1)} %pad_maximum_fusion.5), channel_id=1, source_target_pairs={{0,4},{4,0},{1,5},{5,1},{2,6},{6,2},{3,7},{7,3},{8,12},{12,8},{9,1... | collective-permute-start | bytes 786440 | tf_op jit(solution)/shard_map/ppermute | solution.py:148
  18.5 8.5 %collective-permute-start = (bf16[3,3,64,256]{3,2,1,0:T(8,128)(2,1)}, bf16[3,3,64,256]{3,2,1,0:T(8,128)(2,1)}, u32[]{:S(2)}, u32[]{:S(2)}) collective-permute-start(bf16[3,3,64,256]{3,2,1,0:T(8,128)(2,1)} %squeeze.6), channel_id=1, source_target_pairs={{0,8},{8,0},{16,24},{24,16},{1,9},{9,1},{17,25},{25,17},{2,10},{10... | collective-permute-start | bytes 884744 | tf_op jit(solution)/shard_map/ppermute | solution.py:84
  23.9 1.3 %copy-start.6 = (bf16[64,2,4,128]{3,0,2,1:T(8,128)(2,1)S(1)}, bf16[64,2,4,128]{3,0,2,1:T(8,128)(2,1)}, u32[]{:S(2)}) copy-start(bf16[64,2,4,128]{3,0,2,1:T(8,128)(2,1)} %copy.112) | copy-start | bytes 393220
  28.5 2.7 %copy-start.11 = (pred[4]{0:T(512)(128)(4,1)S(1)}, pred[4]{0:T(512)(128)(4,1)}, u32[]{:S(2)}) copy-start(pred[4]{0:T(512)(128)(4,1)} %compare_and_fusion) | copy-start | bytes 16
  30.0 23.6 %collective-permute-start.1 = (bf16[320,2,6,128]{3,0,2,1:T(8,128)(2,1)}, bf16[320,2,6,128]{3,0,2,1:T(8,128)(2,1)S(1)}, u32[]{:S(2)}, u32[]{:S(2)}) collective-permute-start(bf16[320,2,6,128]{3,0,2,1:T(8,128)(2,1)} %copy.58), channel_id=1, source_target_pairs={{0,4},{4,0},{1,5},{5,1},{2,6},{6,2},{3,7},{7,3},{8,12},{12,8},{9,1... | collective-permute-start | bytes 2949128 | tf_op jit(solution)/shard_map/ppermute | solution.py:112
  32.2 17.8 %all-to-all-start.1 = ((bf16[4,64,2,4,128]{4,1,3,2,0:T(8,128)(2,1)}), bf16[4,64,2,4,128]{4,1,3,2,0:T(8,128)(2,1)S(1)}, u32[]{:S(2)}, u32[]{:S(2)}) async-start(bf16[4,64,2,4,128]{4,1,3,2,0:T(8,128)(2,1)} %broadcast_select_fusion), calls=%async_computation.1 | async-start | bytes 1048576 | tf_op jit(solution)/shard_map/all_to_all | solution.py:157
  35.8 18.8 %copy-start.3 = (bf16[128,2,6,128]{3,2,1,0:T(8,128)(2,1)S(1)}, bf16[128,2,6,128]{3,2,1,0:T(8,128)(2,1)}, u32[]{:S(2)}) copy-start(bf16[128,2,6,128]{3,2,1,0:T(8,128)(2,1)} %get-tuple-element.10) | copy-start | bytes 1179652
  53.6 1.0 copy-start.1
  59.4 2.4 %slice-start = ((bf16[320,2,6,128]{3,0,2,1:T(8,128)(2,1)}), bf16[192,2,6,128]{3,0,2,1:T(8,128)(2,1)S(1)}, s32[]{:S(2)}) async-start(bf16[320,2,6,128]{3,0,2,1:T(8,128)(2,1)} %copy-done.1), calls=%async_computation.3 | async-start | bytes 1179648 | tf_op jit(solution)/shard_map/slice | solution.py:114
  62.5 1.2 %copy-start.4 = (bf16[256,6,2,8,19]{0,2,4,3,1:T(2,128)(2,1)S(1)}, bf16[256,6,2,8,19]{0,2,4,3,1:T(2,128)(2,1)}, u32[]{:S(2)}) copy-start(bf16[256,6,2,8,19]{0,2,4,3,1:T(2,128)(2,1)} %fusion.12) | copy-start | bytes 2801668
  62.5 1.2 %copy-start.14 = (pred[16,17]{0,1:T(8,128)(4,1)S(1)}, pred[16,17]{0,1:T(8,128)(4,1)}, u32[]{:S(2)}) copy-start(pred[16,17]{0,1:T(8,128)(4,1)} %constant.153) | copy-start | bytes 820
  63.6 1.5 %copy-start.9 = (bf16[3,3,512,256]{3,2,1,0:T(8,128)(2,1)}, bf16[3,3,512,256]{3,2,1,0:T(8,128)(2,1)S(1)}, u32[]{:S(2)}) copy-start(bf16[3,3,512,256]{3,2,1,0:T(8,128)(2,1)S(1)} %constant_dynamic-update-slice_fusion) | copy-start | bytes 7077892
  66.1 9.9 %collective-permute-start.3 = (bf16[512,1,4,128]{0,2,3,1:T(4,128)(2,1)S(1)}, bf16[512,1,4,128]{0,2,3,1:T(4,128)(2,1)S(1)}, u32[]{:S(2)}, u32[]{:S(2)}) collective-permute-start(bf16[512,1,4,128]{0,2,3,1:T(4,128)(2,1)S(1)} %get-tuple-element.12), channel_id=1, source_target_pairs={{0,8},{8,16},{16,24},{1,9},{9,17},{17,25},{2,10},{10,18},{18,26},{... | collective-permute-start | bytes 1572872 | tf_op jit(solution)/shard_map/ppermute | solution.py:46
  69.9 10.5 %collective-permute-start.4 = (bf16[512,1,4,128]{0,2,3,1:T(4,128)(2,1)S(1)}, bf16[512,1,4,128]{0,2,3,1:T(4,128)(2,1)S(1)}, u32[]{:S(2)}, u32[]{:S(2)}) collective-permute-start(bf16[512,1,4,128]{0,2,3,1:T(4,128)(2,1)S(1)} %get-tuple-element.13), channel_id=1, source_target_pairs={{8,0},{16,8},{24,16},{9,1},{17,9},{25,17},{10,2},{18,10},{26,18},{... | collective-permute-start | bytes 1572872 | tf_op jit(solution)/shard_map/ppermute | solution.py:47
  81.3 1.0 copy-start.8
  82.3 6.0 %copy-start.7 = (bf16[3,256,256]{2,1,0:T(8,128)(2,1)S(1)}, bf16[3,256,256]{2,1,0:T(8,128)(2,1)}, u32[]{:S(2)}) copy-start(bf16[3,256,256]{2,1,0:T(8,128)(2,1)} %param.9) | copy-start | bytes 1179652
  83.9 11.4 %collective-permute-start.5 = (bf16[256,2,1,128]{0,3,2,1:T(8,128)(2,1)S(1)}, bf16[256,2,1,128]{0,3,2,1:T(8,128)(2,1)S(1)}, u32[]{:S(2)}, u32[]{:S(2)}) collective-permute-start(bf16[256,2,1,128]{0,3,2,1:T(8,128)(2,1)S(1)} %get-tuple-element.18), channel_id=1, source_target_pairs={{0,4},{4,5},{5,1},{1,2},{2,6},{6,7},{7,3},{8,12},{12,13},{13,9},{9... | collective-permute-start | bytes 393224 | tf_op jit(solution)/shard_map/ppermute | solution.py:46
  87.0 8.2 %collective-permute-start.6 = (bf16[256,2,1,128]{0,3,2,1:T(8,128)(2,1)S(1)}, bf16[256,2,1,128]{0,3,2,1:T(8,128)(2,1)S(1)}, u32[]{:S(2)}, u32[]{:S(2)}) collective-permute-start(bf16[256,2,1,128]{0,3,2,1:T(8,128)(2,1)S(1)} %get-tuple-element.19), channel_id=1, source_target_pairs={{4,0},{5,4},{1,5},{2,1},{6,2},{7,6},{3,7},{12,8},{13,12},{9,13},{1... | collective-permute-start | bytes 393224 | tf_op jit(solution)/shard_map/ppermute | solution.py:47
  90.9 16.8 %all-to-all-start.2 = ((bf16[256,2,4,128]{3,2,1,0:T(4,128)(2,1)}), bf16[256,2,4,128]{3,2,1,0:T(4,128)(2,1)S(1)}, u32[]{:S(2)}, u32[]{:S(2)}) async-start(bf16[256,2,4,128]{3,2,1,0:T(4,128)(2,1)} %copy.74), calls=%async_computation.2 | async-start | bytes 1048576 | tf_op jit(solution)/shard_map/all_to_all | solution.py:129
  96.2 1.7 %copy-start.10 = (bf16[3,3,512,256]{3,2,1,0:T(8,128)(2,1)S(1)}, bf16[3,3,512,256]{3,2,1,0:T(8,128)(2,1)}, u32[]{:S(2)}) copy-start(bf16[3,3,512,256]{3,2,1,0:T(8,128)(2,1)} %copy-done.9) | copy-start | bytes 7077892
  100.1 5.3 %collective-permute-start.7 = (bf16[128,2,4,128]{0,2,3,1:T(4,128)(2,1)S(1)}, bf16[128,2,4,128]{0,2,3,1:T(4,128)(2,1)S(1)}, u32[]{:S(2)}, u32[]{:S(2)}) collective-permute-start(bf16[128,2,4,128]{0,2,3,1:T(4,128)(2,1)S(1)} %get-tuple-element.17), channel_id=1, source_target_pairs={{0,4},{1,5},{2,6},{3,7},{4,0},{5,1},{6,2},{7,3},{8,12},{9,13},{10,... | collective-permute-start | bytes 786440 | tf_op jit(solution)/shard_map/ppermute | solution.py:179

commit v22 on v18

--- a/solution.py
+++ b/solution.py
@@ -71,16 +71,14 @@
     return out[0]
 
 
-def gather_weight(weight):
+def finish_weight(weight):
     filts = lax.axis_size("filt")
     chans = lax.axis_size("chan")
     slabs = lax.axis_size("slab")
     core = lax.axis_index("slab") % 2
-    c_loc = weight.shape[2]
-    half = c_loc // 2
-    mine = lax.dynamic_slice_in_dim(weight, core * half, half, 2)
-    spread = jnp.broadcast_to(mine[None], (filts,) + mine.shape)
-    by_filt = gather_blocks(lax.all_to_all(spread, "filt", 0, 4, tiled=True)[0], "chan", 2)
+    half = weight.shape[2]
+    c_loc = 2 * half
+    by_filt = gather_blocks(weight, "chan", 2)
     other = lax.ppermute(by_filt, "slab", [(i, i ^ 1) for i in range(slabs)])
     first = jnp.where(core == 0, by_filt, other)
     second = jnp.where(core == 0, other, by_filt)
@@ -146,8 +144,22 @@
             for q, f in enumerate(need[t][r]):
                 slot[t][f] = k * per + q
     blocks = jnp.take(received, jnp.array(slot, jnp.int32)[chan], axis=0)
-    all_filters = lax.all_to_all(blocks, "filt", 0, 0, tiled=True)
-    return all_filters.reshape((-1,) + all_filters.shape[2:])
+    core = lax.axis_index("slab") % 2
+    half = weight.shape[2] // 2
+    mine = lax.dynamic_slice_in_dim(weight, core * half, half, 2)
+    tile = blocks[0, 0].size
+    if mine.size % tile == 0:
+        extra = mine.reshape((-1,) + blocks.shape[2:])
+        both = jnp.concatenate([blocks, jnp.broadcast_to(extra[None], (filts,) + extra.shape)], axis=1)
+        both = lax.all_to_all(both, "filt", 0, 0, tiled=True)
+        all_filters = both[:, : blocks.shape[1]]
+        got = both[:, blocks.shape[1] :].reshape((filts,) + mine.shape)
+        kernel = jnp.transpose(got, (1, 2, 3, 0, 4)).reshape(mine.shape[:3] + (-1,))
+    else:
+        all_filters = lax.all_to_all(blocks, "filt", 0, 0, tiled=True)
+        spread = jnp.broadcast_to(mine[None], (filts,) + mine.shape)
+        kernel = lax.all_to_all(spread, "filt", 0, 4, tiled=True)[0]
+    return all_filters.reshape((-1,) + all_filters.shape[2:]), kernel
 
 
 def backward_in(deep, weight, depth_weight):
@@ -173,9 +185,9 @@
 
 
 def local(volume, plane_weight, depth_weight, grad_out):
-    weight = gather_weight(plane_weight)
+    all_filters, kernel = backward(grad_out, plane_weight, depth_weight)
+    weight = finish_weight(kernel)
     mid = forward(volume, weight, depth_weight)
-    all_filters = backward(grad_out, weight, depth_weight)
     deep = halo(jnp.concatenate([mid, all_filters]), "slab", 1)
     output = forward_out(deep[: mid.shape[0]], depth_weight)
     grad_in = backward_in(deep[mid.shape[0] :], weight, depth_weight)

time: 94.2 us -> 117 us (1.24)
  blocking collectives: 0 us -> 24.1 us
  starting transfers between devices: 31.2 us -> 27.4 us
  waiting for transfers between devices: 20.9 us -> 24 us
  other arithmetic: 12.2 us -> 10.6 us
    all_to_all x0 -> x1, blocking collectives: none -> 24.1 us  [backward(): both = lax.all_to_all(both, 'filt', 0, 0, tiled=True)]
    all_to_all x2 -> x0, starting transfers between devices: 8.6 us -> none  [the longest x1 4.45 us: gather_weight(): lax.all_to_all(spread, 'filt', 0, 4, tiled=True)[0]]
    ppermute x1, waiting for transfers between devices: 0.01 us -> 5.31 us  [forward(): lax.ppermute(window((chan + k) % chans), 'chan', shift_pairs(chans, k))]
    all_to_all x2 -> x0, waiting for transfers between devices: 3.38 us -> none  [the longest x1 3.37 us: backward(): all_filters = lax.all_to_all(blocks, 'filt', 0, 0, tiled=True)]
    ppermute x1, starting transfers between devices: 2.58 us -> 5.52 us  [finish_weight(): other = lax.ppermute(by_filt, 'slab', [(i, i ^ 1) for i in range(slabs)])]
    ppermute x2, starting transfers between devices: 6.58 us -> 9.09 us  [halo(): lax.ppermute(lax.slice_in_dim(x, length - 1, length, axis=dim), axis, up)]
    ppermute x1, waiting for transfers between devices: 0.39 us -> 2.73 us  [gather_blocks(): lax.ppermute(x, axis, shift_pairs(n, k))]
    ppermute x1, starting transfers between devices: 0.26 us -> 2.13 us  [backward(): lax.ppermute(send, 'chan', shift_pairs(chans, k))]
  transfers between devices with their start and end apart: 12 -> 10, of which waited for: 6 -> 6; matrix products, arithmetic and copies ran while one was open for 27% -> 18% of each run, Pallas kernels for 0% -> 0%
where the time goes in v22:
time: 117 us; the launch traced here: 116 us
  starting transfers between devices  27.4 us (23%)
  blocking collectives  24.1 us (21%)
  waiting for transfers between devices  24 us (21%)
  local copies, waits for them, and re-layouts  20.4 us (17%)
  other arithmetic  10.6 us (9%)
  matrix products  5.77 us (5%)
  between operations  3.85 us (3%)
    all_to_all x1, blocking collectives, backward(): both = lax.all_to_all(both, 'filt', 0, 0, tiled=True)  24.1 us
    ppermute x2, starting transfers between devices, halo(): lax.ppermute(lax.slice_in_dim(x, length - 1, length, axis=dim), axis, up)  9.09 us
    ppermute x1, starting transfers between devices, finish_weight(): other = lax.ppermute(by_filt, 'slab', [(i, i ^ 1) for i in range(slabs)])  5.52 us
    ppermute x1, waiting for transfers between devices, backward(): lax.ppermute(send, 'chan', shift_pairs(chans, k))  5.49 us
    ppermute x1, waiting for transfers between devices, forward(): lax.ppermute(window((chan + k) % chans), 'chan', shift_pairs(chans, k))  5.31 us
    unnamed x15, local copies, waits for them, and re-layouts  5.01 us
    ppermute x2, waiting for transfers between devices, halo(): after = lax.ppermute(lax.slice_in_dim(x, 0, 1, axis=dim), axis, down)  4.5 us
    all_to_all x1, starting transfers between devices, forward_out(): return lax.all_to_all(out, 'filt', 0, 2, tiled=True)  3.96 us
  transfers between devices with their start and end apart: 10, of which 6 were waited for; matrix products, arithmetic and copies ran while one was open for 18% of the time, Pallas kernels for 0%

profile of v22, /device:TPU:1, one launch (start us, length us, event | category | flops | bytes accessed | tf_op | source)
XLA Modules:
  0.0 116.0 jit_solution(2569474744330107890)
XLA Ops:
  5.4 1.5 %constant_dynamic-slice_fusion.5 = (bf16[64,2,4,128]{3,2,1,0:T(4,128)(2,1)S(1)}, bf16[64,2,4,128]{3,2,1,0:T(4,128)(2,1)S(1)}, bf16[64,2,4,128]{3,2,1,0:T(4,128)(2,1)S(1)}, bf16[64,2,4,128]{3,2,1,0:T(4,128)(2,1)S(1)}) fusion(bf16[64,2,16,128]{3,2,1,0:T(8,128)(2,1)} %param.10, s32[]{:T(128)S(6)} %select_n.134, s32[]{:T(128)S(6)} %select_n.135, ...), kind=kLoop, calls=%fused_computation.69 | loop fusion | bytes 1048592 | tf_op jit(solution)/shard_map/dynamic_slice | solution.py:137
  7.0 2.1 %collective-permute-start.1 = (bf16[2,64,2,4,128]{4,1,3,2,0:T(8,128)(2,1)S(1)}, bf16[2,64,2,4,128]{4,1,3,2,0:T(8,128)(2,1)S(1)}, u32[]{:S(2)}, u32[]{:S(2)}) collective-permute-start(bf16[2,64,2,4,128]{4,1,3,2,0:T(8,128)(2,1)S(1)} %pad_maximum_fusion.5), channel_id=1, source_target_pairs={{0,4},{4,0},{1,5},{5,1},{2,6},{6,2},{3,7},{7,3},{8,12},{12,8},{9,1... | collective-permute-start | bytes 786440 | tf_op jit(solution)/shard_map/ppermute | solution.py:138
  9.6 5.5 %collective-permute-done.1 = bf16[2,64,2,4,128]{4,1,3,2,0:T(8,128)(2,1)S(1)} collective-permute-done((bf16[2,64,2,4,128]{4,1,3,2,0:T(8,128)(2,1)S(1)}, bf16[2,64,2,4,128]{4,1,3,2,0:T(8,128)(2,1)S(1)}, u32[]{:S(2)}, u32[]{:S(2)}) %collective-permute-start.1) | collective-permute-done | bytes 262176 | tf_op jit(solution)/shard_map/ppermute | solution.py:138
  16.4 24.1 %all_to_all.23 = bf16[4,100,2,4,128]{4,3,2,1,0:T(4,128)(2,1)S(1)} all-to-all(bf16[4,100,2,4,128]{4,3,2,1,0:T(4,128)(2,1)S(1)} %copy.94), channel_id=1, replica_groups=mesh['slab'=4,'chan'=2,'filt'=4] {'filt'}, dimensions={0} | all-to-all | bytes 1638400 | tf_op jit(solution)/shard_map/all_to_all | solution.py:154
  41.7 1.3 %collective-permute-start.2 = (bf16[3,3,64,256]{3,2,1,0:T(8,128)(2,1)S(1)}, bf16[3,3,64,256]{3,2,1,0:T(8,128)(2,1)S(1)}, u32[]{:S(2)}, u32[]{:S(2)}) collective-permute-start(bf16[3,3,64,256]{3,2,1,0:T(8,128)(2,1)S(1)} %reshape.76), channel_id=1, source_target_pairs={{0,4},{4,0},{1,5},{5,1},{2,6},{6,2},{3,7},{7,3},{8,12},{12,8},{9,1... | collective-permute-start | bytes 884744 | tf_op jit(solution)/shard_map/ppermute | solution.py:25
  43.0 2.2 %pad_dynamic-slice_fusion = (bf16[128,2,6,128]{3,2,1,0:T(8,128)(2,1)S(1)}, bf16[128,2,6,128]{3,2,1,0:T(8,128)(2,1)S(1)}) fusion(s32[]{:T(128)S(6)} %select_n.127, bf16[128,2,32,128]{3,2,1,0:T(8,128)(2,1)} %param.7, s32[]{:T(128)S(6)} %select_n.126), kind=kLoop, calls=%fused_computation.1 | loop fusion | bytes 2883592 | tf_op jit(solution)/shard_map/dynamic_slice | solution.py:105
  45.5 2.7 %collective-permute-done.2 = bf16[3,3,64,256]{3,2,1,0:T(8,128)(2,1)S(1)} collective-permute-done((bf16[3,3,64,256]{3,2,1,0:T(8,128)(2,1)S(1)}, bf16[3,3,64,256]{3,2,1,0:T(8,128)(2,1)S(1)}, u32[]{:S(2)}, u32[]{:S(2)}) %collective-permute-start.2) | collective-permute-done | bytes 294944 | tf_op jit(solution)/shard_map/ppermute | solution.py:25
  48.8 5.5 %collective-permute-start.3 = (bf16[3,3,128,256]{3,2,1,0:T(8,128)(2,1)S(1)}, bf16[3,3,128,256]{3,2,1,0:T(8,128)(2,1)}, u32[]{:S(2)}, u32[]{:S(2)}) collective-permute-start(bf16[3,3,128,256]{3,2,1,0:T(8,128)(2,1)S(1)} %fusion.18), channel_id=1, source_target_pairs={{0,8},{8,0},{16,24},{24,16},{1,9},{9,1},{17,25},{25,17},{2,10},{10... | collective-permute-start | bytes 1769480 | tf_op jit(solution)/shard_map/ppermute | solution.py:82
  54.3 5.3 %collective-permute-done = bf16[128,2,6,128]{3,2,1,0:T(8,128)(2,1)} collective-permute-done((bf16[128,2,6,128]{3,2,1,0:T(8,128)(2,1)S(1)}, bf16[128,2,6,128]{3,2,1,0:T(8,128)(2,1)}, u32[]{:S(2)}, u32[]{:S(2)}) %collective-permute-start) | collective-permute-done | bytes 393248 | tf_op jit(solution)/shard_map/ppermute | solution.py:108
  59.6 3.2 %fusion.7 = bf16[256,6,2,128]{3,1,2,0:T(8,128)(2,1)S(1)} fusion(s32[]{:T(128)S(6)} %select_n.129, bf16[128,2,6,128]{3,2,1,0:T(8,128)(2,1)} %collective-permute-done, bf16[128,2,6,128]{3,2,1,0:T(8,128)(2,1)S(1)} %get-tuple-element.12), kind=kLoop, calls=%fused_computation.25 | loop fusion | flops 1179648 | bytes 1572868 | tf_op jit(solution)/shard_map/jit(_roll_dynamic)/dynamic_slice | solution.py:19
  62.9 1.3 %copy.122 = bf16[256,6,2,128]{0,2,3,1:T(2,128)(2,1)S(1)} copy(bf16[256,6,2,128]{3,1,2,0:T(8,128)(2,1)S(1)} %fusion.7) | data formatting | bytes 1572864
  64.9 0.9 fusion.10
  66.4 1.1 broadcast_select_fusion.1
  67.7 1.5 %fusion.2 = bf16[4,16,17,256]{3,1,2,0:T(8,128)(2,1)S(1)} fusion(bf16[3,3,256,256]{3,2,1,0:T(8,128)(2,1)S(1)} %bitcast.96, bf16[256,6,2,8,19]{0,2,4,3,1:T(2,128)(2,1)S(1)} %fusion.10, pred[16,17]{0,1:T(8,128)(4,1)S(1)} %copy-done.4), kind=kOutput, calls=%fused_computation.13 | convolution fusion | flops 1284014080 | bytes 2670864 | tf_op jit(solution)/shard_map/conv_general_dilated | solution.py:52
  70.1 5.9 %collective-permute-start.4 = (bf16[512,1,4,128]{0,2,3,1:T(4,128)(2,1)S(1)}, bf16[512,1,4,128]{0,2,3,1:T(4,128)(2,1)}, u32[]{:S(2)}, u32[]{:S(2)}) collective-permute-start(bf16[512,1,4,128]{0,2,3,1:T(4,128)(2,1)S(1)} %get-tuple-element.16), channel_id=1, source_target_pairs={{0,8},{8,16},{16,24},{1,9},{9,17},{17,25},{2,10},{10,18},{18,26},{... | collective-permute-start | bytes 1572872 | tf_op jit(solution)/shard_map/ppermute | solution.py:46
  76.1 2.1 %collective-permute-start.5 = (bf16[512,1,4,128]{0,2,3,1:T(4,128)(2,1)S(1)}, bf16[512,1,4,128]{0,2,3,1:T(4,128)(2,1)}, u32[]{:S(2)}, u32[]{:S(2)}) collective-permute-start(bf16[512,1,4,128]{0,2,3,1:T(4,128)(2,1)S(1)} %get-tuple-element.17), channel_id=1, source_target_pairs={{8,0},{16,8},{24,16},{9,1},{17,9},{25,17},{10,2},{18,10},{26,18},{... | collective-permute-start | bytes 1572872 | tf_op jit(solution)/shard_map/ppermute | solution.py:47
  78.2 1.8 %rev.4 = bf16[3,256,256]{2,1,0:T(8,128)(2,1)} reverse(bf16[3,256,256]{2,1,0:T(8,128)(2,1)} %param.9), dimensions={0} | reverse | bytes 786432 | tf_op jit(solution)/shard_map/rev | solution.py:172
  80.0 2.2 %collective-permute-done.4 = bf16[512,1,4,128]{0,2,3,1:T(4,128)(2,1)} collective-permute-done((bf16[512,1,4,128]{0,2,3,1:T(4,128)(2,1)S(1)}, bf16[512,1,4,128]{0,2,3,1:T(4,128)(2,1)}, u32[]{:S(2)}, u32[]{:S(2)}) %collective-permute-start.4) | collective-permute-done | bytes 524320 | tf_op jit(solution)/shard_map/ppermute | solution.py:46
  82.2 4.5 %collective-permute-done.5 = bf16[512,1,4,128]{0,2,3,1:T(4,128)(2,1)} collective-permute-done((bf16[512,1,4,128]{0,2,3,1:T(4,128)(2,1)S(1)}, bf16[512,1,4,128]{0,2,3,1:T(4,128)(2,1)}, u32[]{:S(2)}, u32[]{:S(2)}) %collective-permute-start.5) | collective-permute-done | bytes 524320 | tf_op jit(solution)/shard_map/ppermute | solution.py:47
  86.7 2.0 %pad_maximum_fusion = bf16[512,4,4,128]{0,2,3,1:T(4,128)(2,1)S(1)} fusion(bf16[512,1,4,128]{0,2,3,1:T(4,128)(2,1)} %collective-permute-done.5, bf16[256,2,4,128]{0,2,3,1:T(4,128)(2,1)S(1)} %copy.100, bf16[256,2,4,128]{0,2,3,1:T(4,128)(2,1)S(1)} %slice_bitcast_fusion, bf16[512,1,4,128]{0,2,3,1:T(4,128)(2,1)} %collective-permute-done.4), kind=kLoop, calls=%fused_computation.7 | loop fusion | flops 8388608 | bytes 4194304 | tf_op jit(solution)/shard_map/concatenate | solution.py:48
  89.7 1.4 %convolution_convert_fusion = bf16[2,4,8,16,256]{4,2,3,1,0:T(8,128)(2,1)S(1)} fusion(bf16[256,4,4,8,16]{0,2,4,3,1:T(4,128)(2,1)S(1)} %bitcast.99, bf16[3,256,256]{2,1,0:T(8,128)(2,1)S(1)} %copy-done.2), kind=kOutput, calls=%fused_computation.15 | convolution fusion | flops 402915328 | bytes 1966080 | tf_op jit(solution)/shard_map/conv_general_dilated | solution.py:63
  91.2 3.1 %collective-permute-start.6 = (bf16[256,2,1,128]{0,3,2,1:T(8,128)(2,1)S(1)}, bf16[256,2,1,128]{0,3,2,1:T(8,128)(2,1)S(1)}, u32[]{:S(2)}, u32[]{:S(2)}) collective-permute-start(bf16[256,2,1,128]{0,3,2,1:T(8,128)(2,1)S(1)} %get-tuple-element.20), channel_id=1, source_target_pairs={{0,4},{4,5},{5,1},{1,2},{2,6},{6,7},{7,3},{8,12},{12,13},{13,9},{9... | collective-permute-start | bytes 393224 | tf_op jit(solution)/shard_map/ppermute | solution.py:46
  94.4 1.3 %collective-permute-start.7 = (bf16[256,2,1,128]{0,3,2,1:T(8,128)(2,1)S(1)}, bf16[256,2,1,128]{0,3,2,1:T(8,128)(2,1)S(1)}, u32[]{:S(2)}, u32[]{:S(2)}) collective-permute-start(bf16[256,2,1,128]{0,3,2,1:T(8,128)(2,1)S(1)} %get-tuple-element.21), channel_id=1, source_target_pairs={{4,0},{5,4},{1,5},{2,1},{6,2},{7,6},{3,7},{12,8},{13,12},{9,13},{1... | collective-permute-start | bytes 393224 | tf_op jit(solution)/shard_map/ppermute | solution.py:47
  95.7 1.4 %convolution_convert_fusion.1 = bf16[2,4,8,16,256]{4,2,3,1,0:T(8,128)(2,1)S(1)} fusion(bf16[256,4,4,8,16]{0,2,4,3,1:T(4,128)(2,1)S(1)} %bitcast.98, bf16[3,256,256]{2,1,0:T(8,128)(2,1)S(1)} %copy-done.1), kind=kOutput, calls=%fused_computation.16 | convolution fusion | flops 402915328 | bytes 1966080 | tf_op jit(solution)/shard_map/conv_general_dilated | solution.py:63
  97.2 1.1 copy.105
  98.3 4.0 %all-to-all-start.1 = ((bf16[256,2,4,128]{3,2,1,0:T(4,128)(2,1)}), bf16[256,2,4,128]{3,2,1,0:T(4,128)(2,1)S(1)}, u32[]{:S(2)}, u32[]{:S(2)}) async-start(bf16[256,2,4,128]{3,2,1,0:T(4,128)(2,1)} %copy.105), calls=%async_computation.1 | async-start | bytes 1048576 | tf_op jit(solution)/shard_map/all_to_all | solution.py:119
  104.7 1.5 %fusion.3 = bf16[4,16,17,256]{3,1,2,0:T(8,128)(2,1)S(1)} fusion(bf16[3,3,256,256]{3,2,1,0:T(8,128)(2,1)S(1)} %bitcast.97, bf16[256,6,2,8,19]{0,2,4,3,1:T(2,128)(2,1)S(1)} %fusion.11, pred[16,17]{0,1:T(8,128)(4,1)S(1)} %copy-done.4), kind=kOutput, calls=%fused_computation.14 | convolution fusion | flops 1284014080 | bytes 2670864 | tf_op jit(solution)/shard_map/conv_general_dilated | solution.py:52
  106.9 1.7 %collective-permute-start.8 = (bf16[128,2,4,128]{0,2,3,1:T(4,128)(2,1)S(1)}, bf16[128,2,4,128]{0,2,3,1:T(4,128)(2,1)S(1)}, u32[]{:S(2)}, u32[]{:S(2)}) collective-permute-start(bf16[128,2,4,128]{0,2,3,1:T(4,128)(2,1)S(1)} %get-tuple-element.19), channel_id=1, source_target_pairs={{0,4},{1,5},{2,6},{3,7},{4,0},{5,1},{6,2},{7,3},{8,12},{9,13},{10,... | collective-permute-start | bytes 786440 | tf_op jit(solution)/shard_map/ppermute | solution.py:183
  108.6 3.8 %collective-permute-done.8 = bf16[128,2,4,128]{0,2,3,1:T(4,128)(2,1)S(1)} collective-permute-done((bf16[128,2,4,128]{0,2,3,1:T(4,128)(2,1)S(1)}, bf16[128,2,4,128]{0,2,3,1:T(4,128)(2,1)S(1)}, u32[]{:S(2)}, u32[]{:S(2)}) %collective-permute-start.8) | collective-permute-done | bytes 262176 | tf_op jit(solution)/shard_map/ppermute | solution.py:183
  112.4 1.0 fusion.21
  113.4 1.3 %copy.116 = bf16[128,2,8,128]{3,2,1,0:T(8,128)(2,1)} copy(bf16[128,2,8,128]{0,2,3,1:T(8,128)(2,1)S(1)} %fusion.21) | data formatting | bytes 1048576
  114.9 1.1 copy.115
  (64 shorter events, 12.6 us)
Async XLA Ops:
  0.6 8.5 %copy-start = (bf16[3,3,128,64]{2,3,1,0:T(8,128)(2,1)S(1)}, bf16[3,3,128,64]{2,3,1,0:T(8,128)(2,1)}, u32[]{:S(2)}) copy-start(bf16[3,3,128,64]{2,3,1,0:T(8,128)(2,1)} %param.8) | copy-start | bytes 442372
  0.6 8.6 %copy-start.3 = (s32[2,4]{1,0:T(2,128)S(1)}, s32[2,4]{1,0:T(2,128)}, u32[]{:S(2)}) copy-start(s32[2,4]{1,0:T(2,128)} %constant.143.clone) | copy-start | bytes 100
  7.0 8.2 %collective-permute-start.1 = (bf16[2,64,2,4,128]{4,1,3,2,0:T(8,128)(2,1)S(1)}, bf16[2,64,2,4,128]{4,1,3,2,0:T(8,128)(2,1)S(1)}, u32[]{:S(2)}, u32[]{:S(2)}) collective-permute-start(bf16[2,64,2,4,128]{4,1,3,2,0:T(8,128)(2,1)S(1)} %pad_maximum_fusion.5), channel_id=1, source_target_pairs={{0,4},{4,0},{1,5},{5,1},{2,6},{6,2},{3,7},{7,3},{8,12},{12,8},{9,1... | collective-permute-start | bytes 786440 | tf_op jit(solution)/shard_map/ppermute | solution.py:138
  41.7 6.6 %collective-permute-start.2 = (bf16[3,3,64,256]{3,2,1,0:T(8,128)(2,1)S(1)}, bf16[3,3,64,256]{3,2,1,0:T(8,128)(2,1)S(1)}, u32[]{:S(2)}, u32[]{:S(2)}) collective-permute-start(bf16[3,3,64,256]{3,2,1,0:T(8,128)(2,1)S(1)} %reshape.76), channel_id=1, source_target_pairs={{0,4},{4,0},{1,5},{5,1},{2,6},{6,2},{3,7},{7,3},{8,12},{12,8},{9,1... | collective-permute-start | bytes 884744 | tf_op jit(solution)/shard_map/ppermute | solution.py:25
  45.2 14.4 %collective-permute-start = (bf16[128,2,6,128]{3,2,1,0:T(8,128)(2,1)S(1)}, bf16[128,2,6,128]{3,2,1,0:T(8,128)(2,1)}, u32[]{:S(2)}, u32[]{:S(2)}) collective-permute-start(bf16[128,2,6,128]{3,2,1,0:T(8,128)(2,1)S(1)} %get-tuple-element.13), channel_id=1, source_target_pairs={{0,4},{4,0},{1,5},{5,1},{2,6},{6,2},{3,7},{7,3},{8,12},{12,8},{9,1... | collective-permute-start | bytes 1179656 | tf_op jit(solution)/shard_map/ppermute | solution.py:108
  48.8 17.6 %collective-permute-start.3 = (bf16[3,3,128,256]{3,2,1,0:T(8,128)(2,1)S(1)}, bf16[3,3,128,256]{3,2,1,0:T(8,128)(2,1)}, u32[]{:S(2)}, u32[]{:S(2)}) collective-permute-start(bf16[3,3,128,256]{3,2,1,0:T(8,128)(2,1)S(1)} %fusion.18), channel_id=1, source_target_pairs={{0,8},{8,0},{16,24},{24,16},{1,9},{9,1},{17,25},{25,17},{2,10},{10... | collective-permute-start | bytes 1769480 | tf_op jit(solution)/shard_map/ppermute | solution.py:82
  66.4 1.3 %copy-start.4 = (pred[16,17]{0,1:T(8,128)(4,1)S(1)}, pred[16,17]{0,1:T(8,128)(4,1)}, u32[]{:S(2)}) copy-start(pred[16,17]{0,1:T(8,128)(4,1)} %constant.163) | copy-start | bytes 820
  70.1 12.1 %collective-permute-start.4 = (bf16[512,1,4,128]{0,2,3,1:T(4,128)(2,1)S(1)}, bf16[512,1,4,128]{0,2,3,1:T(4,128)(2,1)}, u32[]{:S(2)}, u32[]{:S(2)}) collective-permute-start(bf16[512,1,4,128]{0,2,3,1:T(4,128)(2,1)S(1)} %get-tuple-element.16), channel_id=1, source_target_pairs={{0,8},{8,16},{16,24},{1,9},{9,17},{17,25},{2,10},{10,18},{18,26},{... | collective-permute-start | bytes 1572872 | tf_op jit(solution)/shard_map/ppermute | solution.py:46
  76.1 10.6 %collective-permute-start.5 = (bf16[512,1,4,128]{0,2,3,1:T(4,128)(2,1)S(1)}, bf16[512,1,4,128]{0,2,3,1:T(4,128)(2,1)}, u32[]{:S(2)}, u32[]{:S(2)}) collective-permute-start(bf16[512,1,4,128]{0,2,3,1:T(4,128)(2,1)S(1)} %get-tuple-element.17), channel_id=1, source_target_pairs={{8,0},{16,8},{24,16},{9,1},{17,9},{25,17},{10,2},{18,10},{26,18},{... | collective-permute-start | bytes 1572872 | tf_op jit(solution)/shard_map/ppermute | solution.py:47
  88.7 1.0 copy-start.2
  89.7 6.0 %copy-start.1 = (bf16[3,256,256]{2,1,0:T(8,128)(2,1)S(1)}, bf16[3,256,256]{2,1,0:T(8,128)(2,1)}, u32[]{:S(2)}) copy-start(bf16[3,256,256]{2,1,0:T(8,128)(2,1)} %param.9) | copy-start | bytes 1179652
  91.2 11.0 %collective-permute-start.6 = (bf16[256,2,1,128]{0,3,2,1:T(8,128)(2,1)S(1)}, bf16[256,2,1,128]{0,3,2,1:T(8,128)(2,1)S(1)}, u32[]{:S(2)}, u32[]{:S(2)}) collective-permute-start(bf16[256,2,1,128]{0,3,2,1:T(8,128)(2,1)S(1)} %get-tuple-element.20), channel_id=1, source_target_pairs={{0,4},{4,5},{5,1},{1,2},{2,6},{6,7},{7,3},{8,12},{12,13},{13,9},{9... | collective-permute-start | bytes 393224 | tf_op jit(solution)/shard_map/ppermute | solution.py:46
  94.4 7.9 %collective-permute-start.7 = (bf16[256,2,1,128]{0,3,2,1:T(8,128)(2,1)S(1)}, bf16[256,2,1,128]{0,3,2,1:T(8,128)(2,1)S(1)}, u32[]{:S(2)}, u32[]{:S(2)}) collective-permute-start(bf16[256,2,1,128]{0,3,2,1:T(8,128)(2,1)S(1)} %get-tuple-element.21), channel_id=1, source_target_pairs={{4,0},{5,4},{1,5},{2,1},{6,2},{7,6},{3,7},{12,8},{13,12},{9,13},{1... | collective-permute-start | bytes 393224 | tf_op jit(solution)/shard_map/ppermute | solution.py:47
  98.3 16.5 %all-to-all-start.1 = ((bf16[256,2,4,128]{3,2,1,0:T(4,128)(2,1)}), bf16[256,2,4,128]{3,2,1,0:T(4,128)(2,1)S(1)}, u32[]{:S(2)}, u32[]{:S(2)}) async-start(bf16[256,2,4,128]{3,2,1,0:T(4,128)(2,1)} %copy.105), calls=%async_computation.1 | async-start | bytes 1048576 | tf_op jit(solution)/shard_map/all_to_all | solution.py:119
  106.9 5.4 %collective-permute-start.8 = (bf16[128,2,4,128]{0,2,3,1:T(4,128)(2,1)S(1)}, bf16[128,2,4,128]{0,2,3,1:T(4,128)(2,1)S(1)}, u32[]{:S(2)}, u32[]{:S(2)}) collective-permute-start(bf16[128,2,4,128]{0,2,3,1:T(4,128)(2,1)S(1)} %get-tuple-element.19), channel_id=1, source_target_pairs={{0,4},{1,5},{2,6},{3,7},{4,0},{5,1},{6,2},{7,3},{8,12},{9,13},{10,... | collective-permute-start | bytes 786440 | tf_op jit(solution)/shard_map/ppermute | solution.py:183

commit v23 on v18

--- a/solution.py
+++ b/solution.py
@@ -14,6 +14,8 @@
     n = len(pieces)
     if n == 1:
         return pieces[0]
+    if n == 2:
+        return jnp.where(me % 2 == 0, jnp.concatenate(pieces, axis=dim), jnp.concatenate(pieces[::-1], axis=dim))
     block = pieces[0].shape[dim]
     stacked = jnp.concatenate(pieces[::-1], axis=dim)
     return jnp.roll(stacked, (me + 1) * block, axis=dim)

time: 94.2 us -> 93.6 us (level)
  other arithmetic: 12.2 us -> 9.81 us
  waiting for transfers between devices: 20.9 us -> 22.7 us
    dynamic_slice x1 -> x0, other arithmetic: 3.24 us -> none  [order_blocks(): return jnp.roll(stacked, (me + 1) * block, axis=dim)]
    select_n x0 -> x3, other arithmetic: none -> 2.38 us  [order_blocks(): jnp.where(me % 2 == 0, jnp.concatenate(pieces, axis=dim), jnp.concatenate...]
    all_to_all x1, waiting for transfers between devices: 3.37 us -> 5.21 us  [backward(): all_filters = lax.all_to_all(blocks, 'filt', 0, 0, tiled=True)]
    concatenate x2 -> x0, other arithmetic: 1.53 us -> none  [order_blocks(): return jnp.roll(stacked, (me + 1) * block, axis=dim)]
  transfers between devices with their start and end apart: 12 -> 12, of which waited for: 6 -> 6; matrix products, arithmetic and copies ran while one was open for 27% -> 24% of each run, Pallas kernels for 0% -> 0%
where the time goes in v23:
time: 93.6 us; the launch traced here: 93 us
  starting transfers between devices  31.2 us (33%)
  waiting for transfers between devices  22.7 us (24%)
  local copies, waits for them, and re-layouts  19.8 us (21%)
  other arithmetic  9.81 us (10%)
  matrix products  5.75 us (6%)
  between operations  3.72 us (4%)
    ppermute x2, starting transfers between devices, halo(): lax.ppermute(lax.slice_in_dim(x, length - 1, length, axis=dim), axis, up)  6.58 us
    unnamed x26, local copies, waits for them, and re-layouts  6.47 us
    ppermute x1, waiting for transfers between devices, backward(): lax.ppermute(send, 'chan', shift_pairs(chans, k))  6.26 us
    all_to_all x1, waiting for transfers between devices, backward(): all_filters = lax.all_to_all(blocks, 'filt', 0, 0, tiled=True)  5.21 us
    all_to_all x1, starting transfers between devices, forward_out(): return lax.all_to_all(out, 'filt', 0, 2, tiled=True)  4.52 us
    ppermute x2, waiting for transfers between devices, halo(): after = lax.ppermute(lax.slice_in_dim(x, 0, 1, axis=dim), axis, down)  4.5 us
    all_to_all x1, starting transfers between devices, gather_weight(): lax.all_to_all(spread, 'filt', 0, 4, tiled=True)[0]  4.45 us
    ppermute x1, waiting for transfers between devices, backward_in(): lax.ppermute(lax.dynamic_slice_in_dim(grad_in, target * c_loc, c_loc, 0),...  4.17 us
  transfers between devices with their start and end apart: 12, of which 6 were waited for; matrix products, arithmetic and copies ran while one was open for 24% of the time, Pallas kernels for 0%

profile of v23, /device:TPU:1, one launch (start us, length us, event | category | flops | bytes accessed | tf_op | source)
XLA Modules:
  0.0 93.0 jit_solution(8633869312322841506)
XLA Ops:
  0.7 3.0 %pad_dynamic-slice_fusion.1 = (bf16[128,2,6,128]{3,2,1,0:T(8,128)(2,1)S(1)}, bf16[128,2,6,128]{3,2,1,0:T(8,128)(2,1)}) fusion(s32[]{:T(128)S(6)} %select_n.125, bf16[128,2,32,128]{3,2,1,0:T(8,128)(2,1)} %param.7, s32[]{:T(128)S(6)} %select_n.127), kind=kLoop, calls=%fused_computation.2 | loop fusion | bytes 2883592 | tf_op jit(solution)/shard_map/dynamic_slice | solution.py:109
  3.7 2.1 %collective-permute-start = (bf16[128,2,6,128]{3,2,1,0:T(8,128)(2,1)}, bf16[128,2,6,128]{3,2,1,0:T(8,128)(2,1)}, u32[]{:S(2)}, u32[]{:S(2)}) collective-permute-start(bf16[128,2,6,128]{3,2,1,0:T(8,128)(2,1)} %get-tuple-element.13), channel_id=1, source_target_pairs={{0,4},{4,0},{1,5},{5,1},{2,6},{6,2},{3,7},{7,3},{8,12},{12,8},{9,1... | collective-permute-start | bytes 1179656 | tf_op jit(solution)/shard_map/ppermute | solution.py:112
  6.2 1.2 %reshape.130 = bf16[4,2,18432]{2,1,0:T(2,128)(2,1)} reshape(bf16[4,3,3,64,64]{4,3,2,1,0:T(8,128)(2,1)S(1)} %broadcast_in_dim.28) | data formatting | bytes 589824
  7.4 4.5 %all-to-all-start = ((bf16[4,2,18432]{2,1,0:T(2,128)(2,1)}), bf16[4,2,18432]{2,1,0:T(2,128)(2,1)S(1)}, u32[]{:S(2)}, u32[]{:S(2)}) async-start(bf16[4,2,18432]{2,1,0:T(2,128)(2,1)} %reshape.130), calls=%async_computation | async-start | bytes 589824 | tf_op jit(solution)/shard_map/all_to_all | solution.py:85
  16.4 6.3 %collective-permute-done.3 = bf16[2,64,2,4,128]{4,1,3,2,0:T(8,128)(2,1)S(1)} collective-permute-done((bf16[2,64,2,4,128]{4,1,3,2,0:T(8,128)(2,1)S(1)}, bf16[2,64,2,4,128]{4,1,3,2,0:T(8,128)(2,1)S(1)}, u32[]{:S(2)}, u32[]{:S(2)}) %collective-permute-start.3) | collective-permute-done | bytes 262176 | tf_op jit(solution)/shard_map/ppermute | solution.py:142
  24.6 2.1 %collective-permute-start.1 = (bf16[3,3,64,256]{3,2,1,0:T(8,128)(2,1)S(1)}, bf16[3,3,64,256]{3,2,1,0:T(8,128)(2,1)S(1)}, u32[]{:S(2)}, u32[]{:S(2)}) collective-permute-start(bf16[3,3,64,256]{3,2,1,0:T(8,128)(2,1)S(1)} %squeeze.6), channel_id=1, source_target_pairs={{0,4},{4,0},{1,5},{5,1},{2,6},{6,2},{3,7},{7,3},{8,12},{12,8},{9,1... | collective-permute-start | bytes 884744 | tf_op jit(solution)/shard_map/ppermute | solution.py:27
  26.7 0.9 broadcast_select_fusion.2
  27.6 4.2 %all-to-all-start.1 = ((bf16[4,64,2,4,128]{4,1,3,2,0:T(8,128)(2,1)}), bf16[4,64,2,4,128]{4,1,3,2,0:T(8,128)(2,1)S(1)}, u32[]{:S(2)}, u32[]{:S(2)}) async-start(bf16[4,64,2,4,128]{4,1,3,2,0:T(8,128)(2,1)} %broadcast_select_fusion.2), calls=%async_computation.1 | async-start | bytes 1048576 | tf_op jit(solution)/shard_map/all_to_all | solution.py:151
  32.4 2.6 %collective-permute-start.2 = (bf16[3,3,128,256]{3,2,1,0:T(8,128)(2,1)S(1)}, bf16[3,3,128,256]{3,2,1,0:T(8,128)(2,1)}, u32[]{:S(2)}, u32[]{:S(2)}) collective-permute-start(bf16[3,3,128,256]{3,2,1,0:T(8,128)(2,1)S(1)} %maximum_select_fusion.1), channel_id=1, source_target_pairs={{0,8},{8,0},{16,24},{24,16},{1,9},{9,1},{17,25},{25,17},{2,10},{10... | collective-permute-start | bytes 1769480 | tf_op jit(solution)/shard_map/ppermute | solution.py:86
  35.0 1.6 %fusion.4 = bf16[256,6,2,128]{3,1,2,0:T(8,128)(2,1)S(1)} fusion(bf16[128,2,6,128]{3,2,1,0:T(8,128)(2,1)} %collective-permute-done, bf16[128,2,6,128]{3,2,1,0:T(8,128)(2,1)S(1)} %get-tuple-element.12, pred[]{:T(512)S(6)} %eq.23), kind=kLoop, calls=%fused_computation.15 | loop fusion | flops 1179648 | bytes 1572865 | tf_op jit(solution)/shard_map/jit(_where)/select_n | solution.py:18
  36.7 1.3 %copy.115 = bf16[256,6,2,128]{0,2,3,1:T(2,128)(2,1)S(1)} copy(bf16[256,6,2,128]{3,1,2,0:T(8,128)(2,1)S(1)} %fusion.4) | data formatting | bytes 1572864
  38.7 1.7 %fusion.7 = bf16[256,6,2,8,19]{0,2,4,3,1:T(2,128)(2,1)} fusion(bf16[256,6,2,7,2]{0,2,4,3,1:T(2,128)(2,1)S(1)} %slice.52, bf16[256,6,2,8,17]{0,2,4,3,1:T(2,128)(2,1)S(1)} %bitcast.84), kind=kLoop, calls=%fused_computation.20 | loop fusion | flops 2801664 | bytes 1855488 | tf_op jit(solution)/shard_map/conv_general_dilated | solution.py:54
  40.4 5.2 %all-to-all-done.1 = bf16[4,64,2,4,128]{4,1,3,2,0:T(8,128)(2,1)S(1)} async-done(((bf16[4,64,2,4,128]{4,1,3,2,0:T(8,128)(2,1)}), bf16[4,64,2,4,128]{4,1,3,2,0:T(8,128)(2,1)S(1)}, u32[]{:S(2)}, u32[]{:S(2)}) %all-to-all-start.1) | async-done | bytes 524320 | tf_op jit(solution)/shard_map/all_to_all | solution.py:151
  45.9 1.2 %broadcast_select_fusion.1 = (bf16[3,3,128,256]{3,2,1,0:T(8,128)(2,1)S(1)}, bf16[3,3,128,256]{3,2,1,0:T(8,128)(2,1)S(1)}) fusion(bf16[3,3,128,256]{3,2,1,0:T(8,128)(2,1)S(1)} %maximum_select_fusion.1, bf16[3,3,128,256]{3,2,1,0:T(8,128)(2,1)} %collective-permute-done.2, pred[]{:T(512)S(6)} %eq.24), kind=kLoop, calls=%fused_computation.29 | loop fusion | flops 589824 | bytes 2359297 | tf_op jit(solution)/shard_map/jit(_where)/select_n | solution.py:87
  47.3 1.5 %fusion.2 = bf16[4,16,17,256]{3,1,2,0:T(8,128)(2,1)S(1)} fusion(bf16[3,3,256,256]{3,2,1,0:T(8,128)(2,1)S(1)} %bitcast.96, bf16[256,6,2,8,19]{0,2,4,3,1:T(2,128)(2,1)S(1)} %copy-done.1, pred[16,17]{0,1:T(8,128)(4,1)S(1)} %copy-done.8), kind=kOutput, calls=%fused_computation.9 | convolution fusion | flops 1284014080 | bytes 2670864 | tf_op jit(solution)/shard_map/conv_general_dilated | solution.py:54
  49.7 4.7 %collective-permute-start.4 = (bf16[512,1,4,128]{0,2,3,1:T(4,128)(2,1)S(1)}, bf16[512,1,4,128]{0,2,3,1:T(4,128)(2,1)}, u32[]{:S(2)}, u32[]{:S(2)}) collective-permute-start(bf16[512,1,4,128]{0,2,3,1:T(4,128)(2,1)S(1)} %get-tuple-element.16), channel_id=1, source_target_pairs={{0,8},{8,16},{16,24},{1,9},{9,17},{17,25},{2,10},{10,18},{18,26},{... | collective-permute-start | bytes 1572872 | tf_op jit(solution)/shard_map/ppermute | solution.py:48
  54.4 2.1 %collective-permute-start.5 = (bf16[512,1,4,128]{0,2,3,1:T(4,128)(2,1)S(1)}, bf16[512,1,4,128]{0,2,3,1:T(4,128)(2,1)}, u32[]{:S(2)}, u32[]{:S(2)}) collective-permute-start(bf16[512,1,4,128]{0,2,3,1:T(4,128)(2,1)S(1)} %get-tuple-element.17), channel_id=1, source_target_pairs={{8,0},{16,8},{24,16},{9,1},{17,9},{25,17},{10,2},{18,10},{26,18},{... | collective-permute-start | bytes 1572872 | tf_op jit(solution)/shard_map/ppermute | solution.py:49
  56.5 1.8 %rev.4 = bf16[3,256,256]{2,1,0:T(8,128)(2,1)} reverse(bf16[3,256,256]{2,1,0:T(8,128)(2,1)} %param.9), dimensions={0} | reverse | bytes 786432 | tf_op jit(solution)/shard_map/rev | solution.py:162
  58.3 2.2 %collective-permute-done.4 = bf16[512,1,4,128]{0,2,3,1:T(4,128)(2,1)} collective-permute-done((bf16[512,1,4,128]{0,2,3,1:T(4,128)(2,1)S(1)}, bf16[512,1,4,128]{0,2,3,1:T(4,128)(2,1)}, u32[]{:S(2)}, u32[]{:S(2)}) %collective-permute-start.4) | collective-permute-done | bytes 524320 | tf_op jit(solution)/shard_map/ppermute | solution.py:48
  60.5 4.5 %collective-permute-done.5 = bf16[512,1,4,128]{0,2,3,1:T(4,128)(2,1)} collective-permute-done((bf16[512,1,4,128]{0,2,3,1:T(4,128)(2,1)S(1)}, bf16[512,1,4,128]{0,2,3,1:T(4,128)(2,1)}, u32[]{:S(2)}, u32[]{:S(2)}) %collective-permute-start.5) | collective-permute-done | bytes 524320 | tf_op jit(solution)/shard_map/ppermute | solution.py:49
  65.0 2.0 %pad_maximum_fusion = bf16[512,4,4,128]{0,2,3,1:T(4,128)(2,1)S(1)} fusion(bf16[512,1,4,128]{0,2,3,1:T(4,128)(2,1)} %collective-permute-done.5, bf16[256,2,4,128]{0,2,3,1:T(4,128)(2,1)S(1)} %copy.94, bf16[256,2,4,128]{0,2,3,1:T(4,128)(2,1)S(1)} %slice_bitcast_fusion, bf16[512,1,4,128]{0,2,3,1:T(4,128)(2,1)} %collective-permute-done.4), kind=kLoop, calls=%fused_computation.3 | loop fusion | flops 8388608 | bytes 4194304 | tf_op jit(solution)/shard_map/concatenate | solution.py:50
  68.0 1.4 %convolution_convert_fusion = bf16[2,4,8,16,256]{4,2,3,1,0:T(8,128)(2,1)S(1)} fusion(bf16[256,4,4,8,16]{0,2,4,3,1:T(4,128)(2,1)S(1)} %bitcast.99, bf16[3,256,256]{2,1,0:T(8,128)(2,1)S(1)} %copy-done.4), kind=kOutput, calls=%fused_computation.11 | convolution fusion | flops 402915328 | bytes 1966080 | tf_op jit(solution)/shard_map/conv_general_dilated | solution.py:65
  69.5 1.9 %collective-permute-start.6 = (bf16[256,2,1,128]{0,3,2,1:T(8,128)(2,1)S(1)}, bf16[256,2,1,128]{0,3,2,1:T(8,128)(2,1)S(1)}, u32[]{:S(2)}, u32[]{:S(2)}) collective-permute-start(bf16[256,2,1,128]{0,3,2,1:T(8,128)(2,1)S(1)} %get-tuple-element.20), channel_id=1, source_target_pairs={{0,4},{4,5},{5,1},{1,2},{2,6},{6,7},{7,3},{8,12},{12,13},{13,9},{9... | collective-permute-start | bytes 393224 | tf_op jit(solution)/shard_map/ppermute | solution.py:48
  71.5 1.3 %collective-permute-start.7 = (bf16[256,2,1,128]{0,3,2,1:T(8,128)(2,1)S(1)}, bf16[256,2,1,128]{0,3,2,1:T(8,128)(2,1)S(1)}, u32[]{:S(2)}, u32[]{:S(2)}) collective-permute-start(bf16[256,2,1,128]{0,3,2,1:T(8,128)(2,1)S(1)} %get-tuple-element.21), channel_id=1, source_target_pairs={{4,0},{5,4},{1,5},{2,1},{6,2},{7,6},{3,7},{12,8},{13,12},{9,13},{1... | collective-permute-start | bytes 393224 | tf_op jit(solution)/shard_map/ppermute | solution.py:49
  72.8 1.4 %convolution_convert_fusion.1 = bf16[2,4,8,16,256]{4,2,3,1,0:T(8,128)(2,1)S(1)} fusion(bf16[256,4,4,8,16]{0,2,4,3,1:T(4,128)(2,1)S(1)} %bitcast.98, bf16[3,256,256]{2,1,0:T(8,128)(2,1)S(1)} %copy-done.3), kind=kOutput, calls=%fused_computation.12 | convolution fusion | flops 402915328 | bytes 1966080 | tf_op jit(solution)/shard_map/conv_general_dilated | solution.py:65
  74.3 1.1 %copy.99 = bf16[256,2,4,128]{3,2,1,0:T(4,128)(2,1)} copy(bf16[256,2,4,128]{0,3,2,1:T(8,128)(2,1)S(1)} %bitcast.93) | data formatting | bytes 1048576 | tf_op jit(solution)/shard_map/convert_element_type | solution.py:122
  75.4 4.5 %all-to-all-start.2 = ((bf16[256,2,4,128]{3,2,1,0:T(4,128)(2,1)}), bf16[256,2,4,128]{3,2,1,0:T(4,128)(2,1)S(1)}, u32[]{:S(2)}, u32[]{:S(2)}) async-start(bf16[256,2,4,128]{3,2,1,0:T(4,128)(2,1)} %copy.99), calls=%async_computation.2 | async-start | bytes 1048576 | tf_op jit(solution)/shard_map/all_to_all | solution.py:123
  82.4 1.5 %fusion.3 = bf16[4,16,17,256]{3,1,2,0:T(8,128)(2,1)S(1)} fusion(bf16[3,3,256,256]{3,2,1,0:T(8,128)(2,1)S(1)} %bitcast.97, bf16[256,6,2,8,19]{0,2,4,3,1:T(2,128)(2,1)S(1)} %fusion.8, pred[16,17]{0,1:T(8,128)(4,1)S(1)} %copy-done.9), kind=kOutput, calls=%fused_computation.10 | convolution fusion | flops 1284014080 | bytes 2670864 | tf_op jit(solution)/shard_map/conv_general_dilated | solution.py:54
  84.6 1.1 %collective-permute-start.8 = (bf16[128,2,4,128]{0,2,3,1:T(4,128)(2,1)S(1)}, bf16[128,2,4,128]{0,2,3,1:T(4,128)(2,1)S(1)}, u32[]{:S(2)}, u32[]{:S(2)}) collective-permute-start(bf16[128,2,4,128]{0,2,3,1:T(4,128)(2,1)S(1)} %get-tuple-element.19), channel_id=1, source_target_pairs={{0,4},{1,5},{2,6},{3,7},{4,0},{5,1},{6,2},{7,3},{8,12},{9,13},{10,... | collective-permute-start | bytes 786440 | tf_op jit(solution)/shard_map/ppermute | solution.py:173
  85.7 4.2 %collective-permute-done.8 = bf16[128,2,4,128]{0,2,3,1:T(4,128)(2,1)S(1)} collective-permute-done((bf16[128,2,4,128]{0,2,3,1:T(4,128)(2,1)S(1)}, bf16[128,2,4,128]{0,2,3,1:T(4,128)(2,1)S(1)}, u32[]{:S(2)}, u32[]{:S(2)}) %collective-permute-start.8) | collective-permute-done | bytes 262176 | tf_op jit(solution)/shard_map/ppermute | solution.py:173
  90.4 1.3 %copy.110 = bf16[128,2,8,128]{3,2,1,0:T(8,128)(2,1)} copy(bf16[128,2,8,128]{0,2,3,1:T(8,128)(2,1)S(1)} %maximum_select_fusion.2) | data formatting | bytes 1048576
  91.9 1.1 %copy.109 = bf16[64,2,16,128]{3,2,1,0:T(8,128)(2,1)} copy(bf16[64,2,16,128]{3,0,2,1:T(8,128)(2,1)S(1)} %bitcast.95) | data formatting | bytes 1048576
  (72 shorter events, 12.0 us)
Async XLA Ops:
  0.6 5.2 %copy-start = (bf16[3,3,128,64]{2,3,1,0:T(8,128)(2,1)S(1)}, bf16[3,3,128,64]{2,3,1,0:T(8,128)(2,1)}, u32[]{:S(2)}) copy-start(bf16[3,3,128,64]{2,3,1,0:T(8,128)(2,1)} %param.8) | copy-start | bytes 442372
  3.7 8.1 %copy-start.5 = (s32[2,2]{1,0:T(2,128)S(1)}, s32[2,2]{1,0:T(2,128)}, u32[]{:S(2)}) copy-start(s32[2,2]{1,0:T(2,128)} %constant.92.clone) | copy-start | bytes 52
  3.7 8.1 %copy-start.6 = (s32[2,2]{1,0:T(2,128)S(1)}, s32[2,2]{1,0:T(2,128)}, u32[]{:S(2)}) copy-start(s32[2,2]{1,0:T(2,128)} %constant.93.clone) | copy-start | bytes 52
  3.7 11.9 %copy-start.2 = (bf16[64,2,16,128]{3,2,1,0:T(8,128)(2,1)S(1)}, bf16[64,2,16,128]{3,2,1,0:T(8,128)(2,1)}, u32[]{:S(2)}) copy-start(bf16[64,2,16,128]{3,2,1,0:T(8,128)(2,1)} %param.10) | copy-start | bytes 1572868
  3.7 31.3 %collective-permute-start = (bf16[128,2,6,128]{3,2,1,0:T(8,128)(2,1)}, bf16[128,2,6,128]{3,2,1,0:T(8,128)(2,1)}, u32[]{:S(2)}, u32[]{:S(2)}) collective-permute-start(bf16[128,2,6,128]{3,2,1,0:T(8,128)(2,1)} %get-tuple-element.13), channel_id=1, source_target_pairs={{0,4},{4,0},{1,5},{5,1},{2,6},{6,2},{3,7},{7,3},{8,12},{12,8},{9,1... | collective-permute-start | bytes 1179656 | tf_op jit(solution)/shard_map/ppermute | solution.py:112
  6.2 10.1 %copy-start.7 = (s32[2,4]{1,0:T(2,128)S(1)}, s32[2,4]{1,0:T(2,128)}, u32[]{:S(2)}) copy-start(s32[2,4]{1,0:T(2,128)} %constant.94.clone) | copy-start | bytes 100
  7.4 16.0 %all-to-all-start = ((bf16[4,2,18432]{2,1,0:T(2,128)(2,1)}), bf16[4,2,18432]{2,1,0:T(2,128)(2,1)S(1)}, u32[]{:S(2)}, u32[]{:S(2)}) async-start(bf16[4,2,18432]{2,1,0:T(2,128)(2,1)} %reshape.130), calls=%async_computation | async-start | bytes 589824 | tf_op jit(solution)/shard_map/all_to_all | solution.py:85
  16.0 6.6 %collective-permute-start.3 = (bf16[2,64,2,4,128]{4,1,3,2,0:T(8,128)(2,1)S(1)}, bf16[2,64,2,4,128]{4,1,3,2,0:T(8,128)(2,1)S(1)}, u32[]{:S(2)}, u32[]{:S(2)}) collective-permute-start(bf16[2,64,2,4,128]{4,1,3,2,0:T(8,128)(2,1)S(1)} %pad_maximum_fusion.4), channel_id=1, source_target_pairs={{0,4},{4,0},{1,5},{5,1},{2,6},{6,2},{3,7},{7,3},{8,12},{12,8},{9,1... | collective-permute-start | bytes 786440 | tf_op jit(solution)/shard_map/ppermute | solution.py:142
  24.6 7.5 %collective-permute-start.1 = (bf16[3,3,64,256]{3,2,1,0:T(8,128)(2,1)S(1)}, bf16[3,3,64,256]{3,2,1,0:T(8,128)(2,1)S(1)}, u32[]{:S(2)}, u32[]{:S(2)}) collective-permute-start(bf16[3,3,64,256]{3,2,1,0:T(8,128)(2,1)S(1)} %squeeze.6), channel_id=1, source_target_pairs={{0,4},{4,0},{1,5},{5,1},{2,6},{6,2},{3,7},{7,3},{8,12},{12,8},{9,1... | collective-permute-start | bytes 884744 | tf_op jit(solution)/shard_map/ppermute | solution.py:27
  27.6 17.9 %all-to-all-start.1 = ((bf16[4,64,2,4,128]{4,1,3,2,0:T(8,128)(2,1)}), bf16[4,64,2,4,128]{4,1,3,2,0:T(8,128)(2,1)S(1)}, u32[]{:S(2)}, u32[]{:S(2)}) async-start(bf16[4,64,2,4,128]{4,1,3,2,0:T(8,128)(2,1)} %broadcast_select_fusion.2), calls=%async_computation.1 | async-start | bytes 1048576 | tf_op jit(solution)/shard_map/all_to_all | solution.py:151
  32.4 13.5 %collective-permute-start.2 = (bf16[3,3,128,256]{3,2,1,0:T(8,128)(2,1)S(1)}, bf16[3,3,128,256]{3,2,1,0:T(8,128)(2,1)}, u32[]{:S(2)}, u32[]{:S(2)}) collective-permute-start(bf16[3,3,128,256]{3,2,1,0:T(8,128)(2,1)S(1)} %maximum_select_fusion.1), channel_id=1, source_target_pairs={{0,8},{8,0},{16,24},{24,16},{1,9},{9,1},{17,25},{25,17},{2,10},{10... | collective-permute-start | bytes 1769480 | tf_op jit(solution)/shard_map/ppermute | solution.py:86
  45.9 1.4 %copy-start.1 = (bf16[256,6,2,8,19]{0,2,4,3,1:T(2,128)(2,1)S(1)}, bf16[256,6,2,8,19]{0,2,4,3,1:T(2,128)(2,1)}, u32[]{:S(2)}) copy-start(bf16[256,6,2,8,19]{0,2,4,3,1:T(2,128)(2,1)} %fusion.7) | copy-start | bytes 2801668
  45.9 1.4 %copy-start.8 = (pred[16,17]{0,1:T(8,128)(4,1)S(1)}, pred[16,17]{0,1:T(8,128)(4,1)}, u32[]{:S(2)}) copy-start(pred[16,17]{0,1:T(8,128)(4,1)} %constant.114) | copy-start | bytes 820
  49.7 10.8 %collective-permute-start.4 = (bf16[512,1,4,128]{0,2,3,1:T(4,128)(2,1)S(1)}, bf16[512,1,4,128]{0,2,3,1:T(4,128)(2,1)}, u32[]{:S(2)}, u32[]{:S(2)}) collective-permute-start(bf16[512,1,4,128]{0,2,3,1:T(4,128)(2,1)S(1)} %get-tuple-element.16), channel_id=1, source_target_pairs={{0,8},{8,16},{16,24},{1,9},{9,17},{17,25},{2,10},{10,18},{18,26},{... | collective-permute-start | bytes 1572872 | tf_op jit(solution)/shard_map/ppermute | solution.py:48
  54.4 10.6 %collective-permute-start.5 = (bf16[512,1,4,128]{0,2,3,1:T(4,128)(2,1)S(1)}, bf16[512,1,4,128]{0,2,3,1:T(4,128)(2,1)}, u32[]{:S(2)}, u32[]{:S(2)}) collective-permute-start(bf16[512,1,4,128]{0,2,3,1:T(4,128)(2,1)S(1)} %get-tuple-element.17), channel_id=1, source_target_pairs={{8,0},{16,8},{24,16},{9,1},{17,9},{25,17},{10,2},{18,10},{26,18},{... | collective-permute-start | bytes 1572872 | tf_op jit(solution)/shard_map/ppermute | solution.py:49
  67.0 1.0 %copy-start.4 = (bf16[3,256,256]{2,1,0:T(8,128)(2,1)S(1)}, bf16[3,256,256]{2,1,0:T(8,128)(2,1)}, u32[]{:S(2)}) copy-start(bf16[3,256,256]{2,1,0:T(8,128)(2,1)} %rev.4) | copy-start | bytes 1179652
  68.0 4.8 %copy-start.3 = (bf16[3,256,256]{2,1,0:T(8,128)(2,1)S(1)}, bf16[3,256,256]{2,1,0:T(8,128)(2,1)}, u32[]{:S(2)}) copy-start(bf16[3,256,256]{2,1,0:T(8,128)(2,1)} %param.9) | copy-start | bytes 1179652
  69.5 10.3 %collective-permute-start.6 = (bf16[256,2,1,128]{0,3,2,1:T(8,128)(2,1)S(1)}, bf16[256,2,1,128]{0,3,2,1:T(8,128)(2,1)S(1)}, u32[]{:S(2)}, u32[]{:S(2)}) collective-permute-start(bf16[256,2,1,128]{0,3,2,1:T(8,128)(2,1)S(1)} %get-tuple-element.20), channel_id=1, source_target_pairs={{0,4},{4,5},{5,1},{1,2},{2,6},{6,7},{7,3},{8,12},{12,13},{13,9},{9... | collective-permute-start | bytes 393224 | tf_op jit(solution)/shard_map/ppermute | solution.py:48
  71.5 8.4 %collective-permute-start.7 = (bf16[256,2,1,128]{0,3,2,1:T(8,128)(2,1)S(1)}, bf16[256,2,1,128]{0,3,2,1:T(8,128)(2,1)S(1)}, u32[]{:S(2)}, u32[]{:S(2)}) collective-permute-start(bf16[256,2,1,128]{0,3,2,1:T(8,128)(2,1)S(1)} %get-tuple-element.21), channel_id=1, source_target_pairs={{4,0},{5,4},{1,5},{2,1},{6,2},{7,6},{3,7},{12,8},{13,12},{9,13},{1... | collective-permute-start | bytes 393224 | tf_op jit(solution)/shard_map/ppermute | solution.py:49
  75.4 16.4 %all-to-all-start.2 = ((bf16[256,2,4,128]{3,2,1,0:T(4,128)(2,1)}), bf16[256,2,4,128]{3,2,1,0:T(4,128)(2,1)S(1)}, u32[]{:S(2)}, u32[]{:S(2)}) async-start(bf16[256,2,4,128]{3,2,1,0:T(4,128)(2,1)} %copy.99), calls=%async_computation.2 | async-start | bytes 1048576 | tf_op jit(solution)/shard_map/all_to_all | solution.py:123
  80.8 1.6 %copy-start.9 = (pred[16,17]{0,1:T(8,128)(4,1)S(1)}, pred[16,17]{0,1:T(8,128)(4,1)}, u32[]{:S(2)}) copy-start(pred[16,17]{0,1:T(8,128)(4,1)} %constant.114) | copy-start | bytes 820
  84.6 5.3 %collective-permute-start.8 = (bf16[128,2,4,128]{0,2,3,1:T(4,128)(2,1)S(1)}, bf16[128,2,4,128]{0,2,3,1:T(4,128)(2,1)S(1)}, u32[]{:S(2)}, u32[]{:S(2)}) collective-permute-start(bf16[128,2,4,128]{0,2,3,1:T(4,128)(2,1)S(1)} %get-tuple-element.19), channel_id=1, source_target_pairs={{0,4},{1,5},{2,6},{3,7},{4,0},{5,1},{6,2},{7,3},{8,12},{9,13},{10,... | collective-permute-start | bytes 786440 | tf_op jit(solution)/shard_map/ppermute | solution.py:173

commit v24 on v23

--- a/solution.py
+++ b/solution.py
@@ -147,7 +147,11 @@
             r = (t - k) % chans
             for q, f in enumerate(need[t][r]):
                 slot[t][f] = k * per + q
-    blocks = jnp.take(received, jnp.array(slot, jnp.int32)[chan], axis=0)
+    if chans == 2:
+        order = lambda t: jnp.stack([received[slot[t][f]] for f in range(filts)])
+        blocks = jnp.where(chan == 0, order(0), order(1))
+    else:
+        blocks = jnp.take(received, jnp.array(slot, jnp.int32)[chan], axis=0)
     all_filters = lax.all_to_all(blocks, "filt", 0, 0, tiled=True)
     return all_filters.reshape((-1,) + all_filters.shape[2:])
 

time: 93.6 us -> 94.5 us (level)
  waiting for transfers between devices: 22.7 us -> 18.5 us
  starting transfers between devices: 31.2 us -> 34.6 us
  other arithmetic: 9.81 us -> 12.5 us
    ppermute x1, waiting for transfers between devices: 0.01 us -> 5.87 us  [forward(): lax.ppermute(window((chan + k) % chans), 'chan', shift_pairs(chans, k))]
    ppermute x1, waiting for transfers between devices: 6.26 us -> 0.48 us  [backward(): lax.ppermute(send, 'chan', shift_pairs(chans, k))]
    all_to_all x1, waiting for transfers between devices: 5.21 us -> 0.01 us  [backward(): all_filters = lax.all_to_all(blocks, 'filt', 0, 0, tiled=True)]
    ppermute x1, starting transfers between devices: 2.06 us -> 0.23 us  [forward(): lax.ppermute(window((chan + k) % chans), 'chan', shift_pairs(chans, k))]
    dynamic_slice x1, local copies, waits for them, and re-layouts: 3.04 us -> 1.34 us  [forward(): lax.dynamic_slice_in_dim(padded, (c * filts + filt) * rows, rows + 2, 2)]
    ppermute x1, starting transfers between devices: 2.58 us -> 4.11 us  [gather_weight(): other = lax.ppermute(by_filt, 'slab', [(i, i ^ 1) for i in range(slabs)])]
    ppermute x2, starting transfers between devices: 6.58 us -> 8.02 us  [halo(): lax.ppermute(lax.slice_in_dim(x, length - 1, length, axis=dim), axis, up)]
    all_to_all x1, waiting for transfers between devices: 0.01 us -> 1.27 us  [gather_weight(): lax.all_to_all(spread, 'filt', 0, 4, tiled=True)[0]]
  transfers between devices with their start and end apart: 12 -> 12, of which waited for: 6 -> 7; matrix products, arithmetic and copies ran while one was open for 24% -> 27% of each run, Pallas kernels for 0% -> 0%
where the time goes in v24:
time: 94.5 us; the launch traced here: 93.9 us
  starting transfers between devices  34.6 us (37%)
  local copies, waits for them, and re-layouts  18.9 us (20%)
  waiting for transfers between devices  18.5 us (20%)
  other arithmetic  12.5 us (13%)
  matrix products  5.75 us (6%)
  between operations  3.69 us (4%)
    ppermute x2, starting transfers between devices, halo(): lax.ppermute(lax.slice_in_dim(x, length - 1, length, axis=dim), axis, up)  8.02 us
    unnamed x34, local copies, waits for them, and re-layouts  7.42 us
    ppermute x1, waiting for transfers between devices, forward(): lax.ppermute(window((chan + k) % chans), 'chan', shift_pairs(chans, k))  5.87 us
    all_to_all x1, starting transfers between devices, gather_weight(): lax.all_to_all(spread, 'filt', 0, 4, tiled=True)[0]  5.42 us
    all_to_all x1, starting transfers between devices, forward_out(): return lax.all_to_all(out, 'filt', 0, 2, tiled=True)  5.37 us
    ppermute x2, waiting for transfers between devices, halo(): after = lax.ppermute(lax.slice_in_dim(x, 0, 1, axis=dim), axis, down)  4.5 us
    all_to_all x1, starting transfers between devices, backward(): all_filters = lax.all_to_all(blocks, 'filt', 0, 0, tiled=True)  4.23 us
    ppermute x1, starting transfers between devices, gather_weight(): other = lax.ppermute(by_filt, 'slab', [(i, i ^ 1) for i in range(slabs)])  4.11 us
  transfers between devices with their start and end apart: 12, of which 7 were waited for; matrix products, arithmetic and copies ran while one was open for 27% of the time, Pallas kernels for 0%

profile of v24, /device:TPU:1, one launch (start us, length us, event | category | flops | bytes accessed | tf_op | source)
XLA Modules:
  0.0 93.9 jit_solution(8383831548454776468)
XLA Ops:
  2.0 1.2 %reshape.88 = bf16[4,2,18432]{2,1,0:T(2,128)(2,1)} reshape(bf16[4,3,3,64,64]{4,3,2,1,0:T(8,128)(2,1)S(1)} %broadcast_in_dim.18) | data formatting | bytes 589824
  3.1 5.4 %all-to-all-start = ((bf16[4,2,18432]{2,1,0:T(2,128)(2,1)}), bf16[4,2,18432]{2,1,0:T(2,128)(2,1)S(1)}, u32[]{:S(2)}, u32[]{:S(2)}) async-start(bf16[4,2,18432]{2,1,0:T(2,128)(2,1)} %reshape.88), calls=%async_computation | async-start | bytes 589824 | tf_op jit(solution)/shard_map/all_to_all | solution.py:85
  14.1 1.2 %collective-permute-start.3 = (bf16[2,64,2,4,128]{4,1,3,2,0:T(8,128)(2,1)}, bf16[2,64,2,4,128]{4,1,3,2,0:T(8,128)(2,1)}, u32[]{:S(2)}, u32[]{:S(2)}) collective-permute-start(bf16[2,64,2,4,128]{4,1,3,2,0:T(8,128)(2,1)} %pad_maximum_fusion.3), channel_id=1, source_target_pairs={{0,4},{4,0},{1,5},{5,1},{2,6},{6,2},{3,7},{7,3},{8,12},{12,8},{9,1... | collective-permute-start | bytes 786440 | tf_op jit(solution)/shard_map/ppermute | solution.py:142
  15.3 1.3 %all-to-all-done = bf16[4,2,18432]{2,1,0:T(2,128)(2,1)S(1)} async-done(((bf16[4,2,18432]{2,1,0:T(2,128)(2,1)}), bf16[4,2,18432]{2,1,0:T(2,128)(2,1)S(1)}, u32[]{:S(2)}, u32[]{:S(2)}) %all-to-all-start) | async-done | bytes 294944 | tf_op jit(solution)/shard_map/all_to_all | solution.py:85
  17.8 1.3 %collective-permute-start.1 = (bf16[3,3,64,256]{3,2,1,0:T(8,128)(2,1)S(1)}, bf16[3,3,64,256]{3,2,1,0:T(8,128)(2,1)}, u32[]{:S(2)}, u32[]{:S(2)}) collective-permute-start(bf16[3,3,64,256]{3,2,1,0:T(8,128)(2,1)S(1)} %squeeze.2), channel_id=1, source_target_pairs={{0,4},{4,0},{1,5},{5,1},{2,6},{6,2},{3,7},{7,3},{8,12},{12,8},{9,1... | collective-permute-start | bytes 884744 | tf_op jit(solution)/shard_map/ppermute | solution.py:27
  19.1 1.3 %pad_dynamic-slice_fusion.1 = (bf16[128,2,6,128]{3,2,1,0:T(8,128)(2,1)}, bf16[128,2,6,128]{3,2,1,0:T(8,128)(2,1)S(1)}) fusion(s32[]{:T(128)S(6)} %select_n.112, bf16[128,2,32,128]{3,2,1,0:T(8,128)(2,1)S(1)} %copy-done.1, s32[]{:T(128)S(6)} %select_n.114), kind=kLoop, calls=%fused_computation.1 | loop fusion | bytes 2883592 | tf_op jit(solution)/shard_map/dynamic_slice | solution.py:109
  21.2 1.9 %maximum_select_fusion.2 = bf16[4,64,2,4,128]{4,1,3,2,0:T(8,128)(2,1)} fusion(bf16[2,64,2,4,128]{4,1,3,2,0:T(8,128)(2,1)} %collective-permute-done.3, bf16[1,64,2,4,128]{4,1,3,2,0:T(8,128)(2,1)S(1)} %bitcast.96, bf16[1,64,2,4,128]{4,1,3,2,0:T(8,128)(2,1)S(1)} %bitcast.97, pred[]{:T(512)S(6)} %eq.28), kind=kLoop, calls=%fused_computation.32 | loop fusion | flops 1310720 | bytes 1048577 | tf_op jit(solution)/shard_map/jit(_where)/select_n | solution.py:152
  23.2 4.2 %all-to-all-start.1 = ((bf16[4,64,2,4,128]{4,1,3,2,0:T(8,128)(2,1)}), bf16[4,64,2,4,128]{4,1,3,2,0:T(8,128)(2,1)S(1)}, u32[]{:S(2)}, u32[]{:S(2)}) async-start(bf16[4,64,2,4,128]{4,1,3,2,0:T(8,128)(2,1)} %maximum_select_fusion.2), calls=%async_computation.1 | async-start | bytes 1048576 | tf_op jit(solution)/shard_map/all_to_all | solution.py:155
  27.6 1.3 %maximum_select_fusion.1 = bf16[3,3,128,256]{3,2,1,0:T(8,128)(2,1)S(1)} fusion(bf16[3,3,64,256]{3,2,1,0:T(8,128)(2,1)} %collective-permute-done.1, bf16[3,3,64,256]{3,2,1,0:T(8,128)(2,1)S(1)} %squeeze.2, pred[]{:T(512)S(6)} %eq.26), kind=kLoop, calls=%fused_computation.26 | loop fusion | flops 2654208 | bytes 1179649 | tf_op jit(solution)/shard_map/jit(_where)/select_n | solution.py:18
  28.8 4.1 %collective-permute-start.2 = (bf16[3,3,128,256]{3,2,1,0:T(8,128)(2,1)S(1)}, bf16[3,3,128,256]{3,2,1,0:T(8,128)(2,1)}, u32[]{:S(2)}, u32[]{:S(2)}) collective-permute-start(bf16[3,3,128,256]{3,2,1,0:T(8,128)(2,1)S(1)} %maximum_select_fusion.1), channel_id=1, source_target_pairs={{0,8},{8,0},{16,24},{24,16},{1,9},{9,1},{17,25},{25,17},{2,10},{10... | collective-permute-start | bytes 1769480 | tf_op jit(solution)/shard_map/ppermute | solution.py:86
  32.9 5.9 %collective-permute-done = bf16[128,2,6,128]{3,2,1,0:T(8,128)(2,1)} collective-permute-done((bf16[128,2,6,128]{3,2,1,0:T(8,128)(2,1)S(1)}, bf16[128,2,6,128]{3,2,1,0:T(8,128)(2,1)}, u32[]{:S(2)}, u32[]{:S(2)}) %collective-permute-start) | collective-permute-done | bytes 393248 | tf_op jit(solution)/shard_map/ppermute | solution.py:112
  38.8 1.7 %fusion.4 = bf16[256,6,2,128]{3,1,2,0:T(8,128)(2,1)S(1)} fusion(bf16[128,2,6,128]{3,2,1,0:T(8,128)(2,1)} %collective-permute-done, bf16[128,2,6,128]{3,2,1,0:T(8,128)(2,1)S(1)} %copy-done.2, pred[]{:T(512)S(6)} %eq.26), kind=kLoop, calls=%fused_computation.14 | loop fusion | flops 1179648 | bytes 1572865 | tf_op jit(solution)/shard_map/jit(_where)/select_n | solution.py:18
  40.5 1.3 %copy.118 = bf16[256,6,2,128]{0,2,3,1:T(2,128)(2,1)S(1)} copy(bf16[256,6,2,128]{3,1,2,0:T(8,128)(2,1)S(1)} %fusion.4) | data formatting | bytes 1572864
  42.5 1.7 %fusion.7 = bf16[256,6,2,8,19]{0,2,4,3,1:T(2,128)(2,1)} fusion(bf16[256,6,2,7,2]{0,2,4,3,1:T(2,128)(2,1)S(1)} %slice.56, bf16[256,6,2,8,17]{0,2,4,3,1:T(2,128)(2,1)S(1)} %bitcast.78), kind=kLoop, calls=%fused_computation.19 | loop fusion | flops 2801664 | bytes 1855488 | tf_op jit(solution)/shard_map/conv_general_dilated | solution.py:54
  44.6 1.2 %broadcast_select_fusion.1 = (bf16[3,3,128,256]{3,2,1,0:T(8,128)(2,1)S(1)}, bf16[3,3,128,256]{3,2,1,0:T(8,128)(2,1)S(1)}) fusion(bf16[3,3,128,256]{3,2,1,0:T(8,128)(2,1)S(1)} %maximum_select_fusion.1, bf16[3,3,128,256]{3,2,1,0:T(8,128)(2,1)} %collective-permute-done.2, pred[]{:T(512)S(6)} %eq.27), kind=kLoop, calls=%fused_computation.28 | loop fusion | flops 589824 | bytes 2359297 | tf_op jit(solution)/shard_map/jit(_where)/select_n | solution.py:87
  46.0 1.5 %fusion.2 = bf16[4,16,17,256]{3,1,2,0:T(8,128)(2,1)S(1)} fusion(bf16[3,3,256,256]{3,2,1,0:T(8,128)(2,1)S(1)} %bitcast.90, bf16[256,6,2,8,19]{0,2,4,3,1:T(2,128)(2,1)S(1)} %copy-done.3, pred[16,17]{0,1:T(8,128)(4,1)S(1)} %copy-done.10), kind=kOutput, calls=%fused_computation.8 | convolution fusion | flops 1284014080 | bytes 2670864 | tf_op jit(solution)/shard_map/conv_general_dilated | solution.py:54
  48.4 4.9 %collective-permute-start.4 = (bf16[512,1,4,128]{0,2,3,1:T(4,128)(2,1)S(1)}, bf16[512,1,4,128]{0,2,3,1:T(4,128)(2,1)}, u32[]{:S(2)}, u32[]{:S(2)}) collective-permute-start(bf16[512,1,4,128]{0,2,3,1:T(4,128)(2,1)S(1)} %get-tuple-element.16), channel_id=1, source_target_pairs={{0,8},{8,16},{16,24},{1,9},{9,17},{17,25},{2,10},{10,18},{18,26},{... | collective-permute-start | bytes 1572872 | tf_op jit(solution)/shard_map/ppermute | solution.py:48
  53.3 2.1 %collective-permute-start.5 = (bf16[512,1,4,128]{0,2,3,1:T(4,128)(2,1)S(1)}, bf16[512,1,4,128]{0,2,3,1:T(4,128)(2,1)}, u32[]{:S(2)}, u32[]{:S(2)}) collective-permute-start(bf16[512,1,4,128]{0,2,3,1:T(4,128)(2,1)S(1)} %get-tuple-element.17), channel_id=1, source_target_pairs={{8,0},{16,8},{24,16},{9,1},{17,9},{25,17},{10,2},{18,10},{26,18},{... | collective-permute-start | bytes 1572872 | tf_op jit(solution)/shard_map/ppermute | solution.py:49
  55.4 1.8 %rev.4 = bf16[3,256,256]{2,1,0:T(8,128)(2,1)} reverse(bf16[3,256,256]{2,1,0:T(8,128)(2,1)} %param.8), dimensions={0} | reverse | bytes 786432 | tf_op jit(solution)/shard_map/rev | solution.py:166
  57.2 2.2 %collective-permute-done.4 = bf16[512,1,4,128]{0,2,3,1:T(4,128)(2,1)} collective-permute-done((bf16[512,1,4,128]{0,2,3,1:T(4,128)(2,1)S(1)}, bf16[512,1,4,128]{0,2,3,1:T(4,128)(2,1)}, u32[]{:S(2)}, u32[]{:S(2)}) %collective-permute-start.4) | collective-permute-done | bytes 524320 | tf_op jit(solution)/shard_map/ppermute | solution.py:48
  59.4 4.5 %collective-permute-done.5 = bf16[512,1,4,128]{0,2,3,1:T(4,128)(2,1)} collective-permute-done((bf16[512,1,4,128]{0,2,3,1:T(4,128)(2,1)S(1)}, bf16[512,1,4,128]{0,2,3,1:T(4,128)(2,1)}, u32[]{:S(2)}, u32[]{:S(2)}) %collective-permute-start.5) | collective-permute-done | bytes 524320 | tf_op jit(solution)/shard_map/ppermute | solution.py:49
  63.9 2.0 %pad_maximum_fusion = bf16[512,4,4,128]{0,2,3,1:T(4,128)(2,1)S(1)} fusion(bf16[512,1,4,128]{0,2,3,1:T(4,128)(2,1)} %collective-permute-done.5, bf16[256,2,4,128]{0,2,3,1:T(4,128)(2,1)S(1)} %copy.93, bf16[256,2,4,128]{0,2,3,1:T(4,128)(2,1)S(1)} %slice_bitcast_fusion, bf16[512,1,4,128]{0,2,3,1:T(4,128)(2,1)} %collective-permute-done.4), kind=kLoop, calls=%fused_computation.2 | loop fusion | flops 8388608 | bytes 4194304 | tf_op jit(solution)/shard_map/concatenate | solution.py:50
  66.9 1.4 %convolution_convert_fusion = bf16[2,4,8,16,256]{4,2,3,1,0:T(8,128)(2,1)S(1)} fusion(bf16[256,4,4,8,16]{0,2,4,3,1:T(4,128)(2,1)S(1)} %bitcast.93, bf16[3,256,256]{2,1,0:T(8,128)(2,1)S(1)} %copy-done.7), kind=kOutput, calls=%fused_computation.10 | convolution fusion | flops 402915328 | bytes 1966080 | tf_op jit(solution)/shard_map/conv_general_dilated | solution.py:65
  68.4 3.2 %collective-permute-start.6 = (bf16[256,2,1,128]{0,3,2,1:T(8,128)(2,1)S(1)}, bf16[256,2,1,128]{0,3,2,1:T(8,128)(2,1)S(1)}, u32[]{:S(2)}, u32[]{:S(2)}) collective-permute-start(bf16[256,2,1,128]{0,3,2,1:T(8,128)(2,1)S(1)} %get-tuple-element.20), channel_id=1, source_target_pairs={{0,4},{4,5},{5,1},{1,2},{2,6},{6,7},{7,3},{8,12},{12,13},{13,9},{9... | collective-permute-start | bytes 393224 | tf_op jit(solution)/shard_map/ppermute | solution.py:48
  71.6 1.3 %collective-permute-start.7 = (bf16[256,2,1,128]{0,3,2,1:T(8,128)(2,1)S(1)}, bf16[256,2,1,128]{0,3,2,1:T(8,128)(2,1)S(1)}, u32[]{:S(2)}, u32[]{:S(2)}) collective-permute-start(bf16[256,2,1,128]{0,3,2,1:T(8,128)(2,1)S(1)} %get-tuple-element.21), channel_id=1, source_target_pairs={{4,0},{5,4},{1,5},{2,1},{6,2},{7,6},{3,7},{12,8},{13,12},{9,13},{1... | collective-permute-start | bytes 393224 | tf_op jit(solution)/shard_map/ppermute | solution.py:49
  72.9 1.4 %convolution_convert_fusion.1 = bf16[2,4,8,16,256]{4,2,3,1,0:T(8,128)(2,1)S(1)} fusion(bf16[256,4,4,8,16]{0,2,4,3,1:T(4,128)(2,1)S(1)} %bitcast.92, bf16[3,256,256]{2,1,0:T(8,128)(2,1)S(1)} %copy-done.6), kind=kOutput, calls=%fused_computation.11 | convolution fusion | flops 402915328 | bytes 1966080 | tf_op jit(solution)/shard_map/conv_general_dilated | solution.py:65
  75.4 5.4 %all-to-all-start.2 = ((bf16[256,2,4,128]{3,2,1,0:T(4,128)(2,1)}), bf16[256,2,4,128]{3,2,1,0:T(4,128)(2,1)S(1)}, u32[]{:S(2)}, u32[]{:S(2)}) async-start(bf16[256,2,4,128]{3,2,1,0:T(4,128)(2,1)} %copy.98), calls=%async_computation.2 | async-start | bytes 1048576 | tf_op jit(solution)/shard_map/all_to_all | solution.py:123
  83.3 1.5 %fusion.3 = bf16[4,16,17,256]{3,1,2,0:T(8,128)(2,1)S(1)} fusion(bf16[3,3,256,256]{3,2,1,0:T(8,128)(2,1)S(1)} %bitcast.91, bf16[256,6,2,8,19]{0,2,4,3,1:T(2,128)(2,1)S(1)} %fusion.8, pred[16,17]{0,1:T(8,128)(4,1)S(1)} %copy-done.11), kind=kOutput, calls=%fused_computation.9 | convolution fusion | flops 1284014080 | bytes 2670864 | tf_op jit(solution)/shard_map/conv_general_dilated | solution.py:54
  85.5 1.3 %collective-permute-start.8 = (bf16[128,2,4,128]{0,2,3,1:T(4,128)(2,1)S(1)}, bf16[128,2,4,128]{0,2,3,1:T(4,128)(2,1)S(1)}, u32[]{:S(2)}, u32[]{:S(2)}) collective-permute-start(bf16[128,2,4,128]{0,2,3,1:T(4,128)(2,1)S(1)} %get-tuple-element.19), channel_id=1, source_target_pairs={{0,4},{1,5},{2,6},{3,7},{4,0},{5,1},{6,2},{7,3},{8,12},{9,13},{10,... | collective-permute-start | bytes 786440 | tf_op jit(solution)/shard_map/ppermute | solution.py:177
  86.8 4.0 %collective-permute-done.8 = bf16[128,2,4,128]{0,2,3,1:T(4,128)(2,1)S(1)} collective-permute-done((bf16[128,2,4,128]{0,2,3,1:T(4,128)(2,1)S(1)}, bf16[128,2,4,128]{0,2,3,1:T(4,128)(2,1)S(1)}, u32[]{:S(2)}, u32[]{:S(2)}) %collective-permute-start.8) | collective-permute-done | bytes 262176 | tf_op jit(solution)/shard_map/ppermute | solution.py:177
  91.3 1.3 %copy.109 = bf16[128,2,8,128]{3,2,1,0:T(8,128)(2,1)} copy(bf16[128,2,8,128]{0,2,3,1:T(8,128)(2,1)S(1)} %maximum_select_fusion.3) | data formatting | bytes 1048576
  92.8 1.1 %copy.108 = bf16[64,2,16,128]{3,2,1,0:T(8,128)(2,1)} copy(bf16[64,2,16,128]{3,0,2,1:T(8,128)(2,1)S(1)} %bitcast.89) | data formatting | bytes 1048576
  (71 shorter events, 14.4 us)
Async XLA Ops:
  0.6 0.9 copy-start
  0.6 7.9 %copy-start.8 = (s32[2,2]{1,0:T(2,128)S(1)}, s32[2,2]{1,0:T(2,128)}, u32[]{:S(2)}) copy-start(s32[2,2]{1,0:T(2,128)} %constant.76.clone) | copy-start | bytes 52
  0.7 7.9 %copy-start.9 = (s32[2,2]{1,0:T(2,128)S(1)}, s32[2,2]{1,0:T(2,128)}, u32[]{:S(2)}) copy-start(s32[2,2]{1,0:T(2,128)} %constant.77.clone) | copy-start | bytes 52
  0.7 11.7 %copy-start.4 = (bf16[64,2,16,128]{3,2,1,0:T(8,128)(2,1)S(1)}, bf16[64,2,16,128]{3,2,1,0:T(8,128)(2,1)}, u32[]{:S(2)}) copy-start(bf16[64,2,16,128]{3,2,1,0:T(8,128)(2,1)} %param.9) | copy-start | bytes 1572868
  3.1 13.5 %all-to-all-start = ((bf16[4,2,18432]{2,1,0:T(2,128)(2,1)}), bf16[4,2,18432]{2,1,0:T(2,128)(2,1)S(1)}, u32[]{:S(2)}, u32[]{:S(2)}) async-start(bf16[4,2,18432]{2,1,0:T(2,128)(2,1)} %reshape.88), calls=%async_computation | async-start | bytes 589824 | tf_op jit(solution)/shard_map/all_to_all | solution.py:85
  13.3 5.8 %copy-start.1 = (bf16[128,2,32,128]{3,2,1,0:T(8,128)(2,1)S(1)}, bf16[128,2,32,128]{3,2,1,0:T(8,128)(2,1)}, u32[]{:S(2)}) copy-start(bf16[128,2,32,128]{3,2,1,0:T(8,128)(2,1)} %param.6) | copy-start | bytes 6291460
  14.1 7.2 %collective-permute-start.3 = (bf16[2,64,2,4,128]{4,1,3,2,0:T(8,128)(2,1)}, bf16[2,64,2,4,128]{4,1,3,2,0:T(8,128)(2,1)}, u32[]{:S(2)}, u32[]{:S(2)}) collective-permute-start(bf16[2,64,2,4,128]{4,1,3,2,0:T(8,128)(2,1)} %pad_maximum_fusion.3), channel_id=1, source_target_pairs={{0,4},{4,0},{1,5},{5,1},{2,6},{6,2},{3,7},{7,3},{8,12},{12,8},{9,1... | collective-permute-start | bytes 786440 | tf_op jit(solution)/shard_map/ppermute | solution.py:142
  17.8 2.9 %copy-start.5 = (bf16[64,2,4,128]{3,2,1,0:T(4,128)(2,1)S(1)}, bf16[64,2,4,128]{3,2,1,0:T(4,128)(2,1)}, u32[]{:S(2)}) copy-start(bf16[64,2,4,128]{3,2,1,0:T(4,128)(2,1)} %get-tuple-element.24) | copy-start | bytes 393220
  17.8 9.7 %collective-permute-start.1 = (bf16[3,3,64,256]{3,2,1,0:T(8,128)(2,1)S(1)}, bf16[3,3,64,256]{3,2,1,0:T(8,128)(2,1)}, u32[]{:S(2)}, u32[]{:S(2)}) collective-permute-start(bf16[3,3,64,256]{3,2,1,0:T(8,128)(2,1)S(1)} %squeeze.2), channel_id=1, source_target_pairs={{0,4},{4,0},{1,5},{5,1},{2,6},{6,2},{3,7},{7,3},{8,12},{12,8},{9,1... | collective-permute-start | bytes 884744 | tf_op jit(solution)/shard_map/ppermute | solution.py:27
  20.5 18.3 %collective-permute-start = (bf16[128,2,6,128]{3,2,1,0:T(8,128)(2,1)S(1)}, bf16[128,2,6,128]{3,2,1,0:T(8,128)(2,1)}, u32[]{:S(2)}, u32[]{:S(2)}) collective-permute-start(bf16[128,2,6,128]{3,2,1,0:T(8,128)(2,1)S(1)} %get-tuple-element.13), channel_id=1, source_target_pairs={{0,4},{4,0},{1,5},{5,1},{2,6},{6,2},{3,7},{7,3},{8,12},{12,8},{9,1... | collective-permute-start | bytes 1179656 | tf_op jit(solution)/shard_map/ppermute | solution.py:112
  20.7 18.1 %copy-start.2 = (bf16[128,2,6,128]{3,2,1,0:T(8,128)(2,1)S(1)}, bf16[128,2,6,128]{3,2,1,0:T(8,128)(2,1)}, u32[]{:S(2)}) copy-start(bf16[128,2,6,128]{3,2,1,0:T(8,128)(2,1)} %get-tuple-element.12) | copy-start | bytes 1179652
  23.2 21.0 %all-to-all-start.1 = ((bf16[4,64,2,4,128]{4,1,3,2,0:T(8,128)(2,1)}), bf16[4,64,2,4,128]{4,1,3,2,0:T(8,128)(2,1)S(1)}, u32[]{:S(2)}, u32[]{:S(2)}) async-start(bf16[4,64,2,4,128]{4,1,3,2,0:T(8,128)(2,1)} %maximum_select_fusion.2), calls=%async_computation.1 | async-start | bytes 1048576 | tf_op jit(solution)/shard_map/all_to_all | solution.py:155
  28.8 15.8 %collective-permute-start.2 = (bf16[3,3,128,256]{3,2,1,0:T(8,128)(2,1)S(1)}, bf16[3,3,128,256]{3,2,1,0:T(8,128)(2,1)}, u32[]{:S(2)}, u32[]{:S(2)}) collective-permute-start(bf16[3,3,128,256]{3,2,1,0:T(8,128)(2,1)S(1)} %maximum_select_fusion.1), channel_id=1, source_target_pairs={{0,8},{8,0},{16,24},{24,16},{1,9},{9,1},{17,25},{25,17},{2,10},{10... | collective-permute-start | bytes 1769480 | tf_op jit(solution)/shard_map/ppermute | solution.py:86
  44.5 1.4 %copy-start.3 = (bf16[256,6,2,8,19]{0,2,4,3,1:T(2,128)(2,1)S(1)}, bf16[256,6,2,8,19]{0,2,4,3,1:T(2,128)(2,1)}, u32[]{:S(2)}) copy-start(bf16[256,6,2,8,19]{0,2,4,3,1:T(2,128)(2,1)} %fusion.7) | copy-start | bytes 2801668
  44.6 1.4 %copy-start.10 = (pred[16,17]{0,1:T(8,128)(4,1)S(1)}, pred[16,17]{0,1:T(8,128)(4,1)}, u32[]{:S(2)}) copy-start(pred[16,17]{0,1:T(8,128)(4,1)} %constant.97) | copy-start | bytes 820
  48.4 11.0 %collective-permute-start.4 = (bf16[512,1,4,128]{0,2,3,1:T(4,128)(2,1)S(1)}, bf16[512,1,4,128]{0,2,3,1:T(4,128)(2,1)}, u32[]{:S(2)}, u32[]{:S(2)}) collective-permute-start(bf16[512,1,4,128]{0,2,3,1:T(4,128)(2,1)S(1)} %get-tuple-element.16), channel_id=1, source_target_pairs={{0,8},{8,16},{16,24},{1,9},{9,17},{17,25},{2,10},{10,18},{18,26},{... | collective-permute-start | bytes 1572872 | tf_op jit(solution)/shard_map/ppermute | solution.py:48
  53.3 10.6 %collective-permute-start.5 = (bf16[512,1,4,128]{0,2,3,1:T(4,128)(2,1)S(1)}, bf16[512,1,4,128]{0,2,3,1:T(4,128)(2,1)}, u32[]{:S(2)}, u32[]{:S(2)}) collective-permute-start(bf16[512,1,4,128]{0,2,3,1:T(4,128)(2,1)S(1)} %get-tuple-element.17), channel_id=1, source_target_pairs={{8,0},{16,8},{24,16},{9,1},{17,9},{25,17},{10,2},{18,10},{26,18},{... | collective-permute-start | bytes 1572872 | tf_op jit(solution)/shard_map/ppermute | solution.py:49
  65.9 1.0 %copy-start.7 = (bf16[3,256,256]{2,1,0:T(8,128)(2,1)S(1)}, bf16[3,256,256]{2,1,0:T(8,128)(2,1)}, u32[]{:S(2)}) copy-start(bf16[3,256,256]{2,1,0:T(8,128)(2,1)} %rev.4) | copy-start | bytes 1179652
  66.9 6.0 %copy-start.6 = (bf16[3,256,256]{2,1,0:T(8,128)(2,1)S(1)}, bf16[3,256,256]{2,1,0:T(8,128)(2,1)}, u32[]{:S(2)}) copy-start(bf16[3,256,256]{2,1,0:T(8,128)(2,1)} %param.8) | copy-start | bytes 1179652
  68.4 12.4 %collective-permute-start.6 = (bf16[256,2,1,128]{0,3,2,1:T(8,128)(2,1)S(1)}, bf16[256,2,1,128]{0,3,2,1:T(8,128)(2,1)S(1)}, u32[]{:S(2)}, u32[]{:S(2)}) collective-permute-start(bf16[256,2,1,128]{0,3,2,1:T(8,128)(2,1)S(1)} %get-tuple-element.20), channel_id=1, source_target_pairs={{0,4},{4,5},{5,1},{1,2},{2,6},{6,7},{7,3},{8,12},{12,13},{13,9},{9... | collective-permute-start | bytes 393224 | tf_op jit(solution)/shard_map/ppermute | solution.py:48
  71.6 9.3 %collective-permute-start.7 = (bf16[256,2,1,128]{0,3,2,1:T(8,128)(2,1)S(1)}, bf16[256,2,1,128]{0,3,2,1:T(8,128)(2,1)S(1)}, u32[]{:S(2)}, u32[]{:S(2)}) collective-permute-start(bf16[256,2,1,128]{0,3,2,1:T(8,128)(2,1)S(1)} %get-tuple-element.21), channel_id=1, source_target_pairs={{4,0},{5,4},{1,5},{2,1},{6,2},{7,6},{3,7},{12,8},{13,12},{9,13},{1... | collective-permute-start | bytes 393224 | tf_op jit(solution)/shard_map/ppermute | solution.py:49
  75.4 17.2 %all-to-all-start.2 = ((bf16[256,2,4,128]{3,2,1,0:T(4,128)(2,1)}), bf16[256,2,4,128]{3,2,1,0:T(4,128)(2,1)S(1)}, u32[]{:S(2)}, u32[]{:S(2)}) async-start(bf16[256,2,4,128]{3,2,1,0:T(4,128)(2,1)} %copy.98), calls=%async_computation.2 | async-start | bytes 1048576 | tf_op jit(solution)/shard_map/all_to_all | solution.py:123
  81.7 1.6 %copy-start.11 = (pred[16,17]{0,1:T(8,128)(4,1)S(1)}, pred[16,17]{0,1:T(8,128)(4,1)}, u32[]{:S(2)}) copy-start(pred[16,17]{0,1:T(8,128)(4,1)} %constant.97) | copy-start | bytes 820
  85.5 5.3 %collective-permute-start.8 = (bf16[128,2,4,128]{0,2,3,1:T(4,128)(2,1)S(1)}, bf16[128,2,4,128]{0,2,3,1:T(4,128)(2,1)S(1)}, u32[]{:S(2)}, u32[]{:S(2)}) collective-permute-start(bf16[128,2,4,128]{0,2,3,1:T(4,128)(2,1)S(1)} %get-tuple-element.19), channel_id=1, source_target_pairs={{0,4},{1,5},{2,6},{3,7},{4,0},{5,1},{6,2},{7,3},{8,12},{9,13},{10,... | collective-permute-start | bytes 786440 | tf_op jit(solution)/shard_map/ppermute | solution.py:177

commit v25 on v23

--- a/solution.py
+++ b/solution.py
@@ -159,7 +159,9 @@
     rows = deep.shape[2]
     turn = lambda f, r: r if f % 2 == 0 else chans - 1 - r
     place = lambda g: turn(g // chans, g % chans) * filts + g // chans
-    grad_mid = depth_conv(deep, depth_weight[::-1], "DHWIO").astype(jnp.bfloat16)
+    taps = depth_weight.shape[0]
+    flipped = jnp.concatenate([depth_weight[t : t + 1] for t in reversed(range(taps))])
+    grad_mid = depth_conv(deep, flipped, "DHWIO").astype(jnp.bfloat16)
     rimmed = halo(grad_mid, ROWS, 2, place)
     grad_in = plane_conv(rimmed, weight[::-1, ::-1], "HWOI").astype(jnp.bfloat16)
     chan = lax.axis_index("chan")

time: 93.6 us -> 93.3 us (level)
  local copies, waits for them, and re-layouts: 19.8 us -> 18.8 us
    rev x1 -> x0, local copies, waits for them, and re-layouts: 1.77 us -> none  [backward_in(): depth_weight[::-1]]
    slice x0 -> x1, local copies, waits for them, and re-layouts: none -> 1.06 us  [backward_in(): depth_weight[t:t + 1]]
    unnamed x26 -> x24, local copies, waits for them, and re-layouts: 6.47 us -> 6.21 us
where the time goes in v25:
time: 93.3 us; the launch traced here: 92.7 us
  starting transfers between devices  31.2 us (33%)
  waiting for transfers between devices  23.4 us (25%)
  local copies, waits for them, and re-layouts  18.8 us (20%)
  other arithmetic  9.81 us (11%)
  matrix products  5.75 us (6%)
  between operations  3.72 us (4%)
    ppermute x2, starting transfers between devices, halo(): lax.ppermute(lax.slice_in_dim(x, length - 1, length, axis=dim), axis, up)  6.58 us
    ppermute x1, waiting for transfers between devices, backward(): lax.ppermute(send, 'chan', shift_pairs(chans, k))  6.26 us
    unnamed x24, local copies, waits for them, and re-layouts  6.21 us
    all_to_all x1, waiting for transfers between devices, backward(): all_filters = lax.all_to_all(blocks, 'filt', 0, 0, tiled=True)  5.21 us
    all_to_all x1, starting transfers between devices, forward_out(): return lax.all_to_all(out, 'filt', 0, 2, tiled=True)  4.52 us
    ppermute x2, waiting for transfers between devices, halo(): after = lax.ppermute(lax.slice_in_dim(x, 0, 1, axis=dim), axis, down)  4.5 us
    all_to_all x1, starting transfers between devices, gather_weight(): lax.all_to_all(spread, 'filt', 0, 4, tiled=True)[0]  4.45 us
    ppermute x1, waiting for transfers between devices, backward_in(): lax.ppermute(lax.dynamic_slice_in_dim(grad_in, target * c_loc, c_loc, 0),...  4.16 us
  transfers between devices with their start and end apart: 12, of which 6 were waited for; matrix products, arithmetic and copies ran while one was open for 24% of the time, Pallas kernels for 0%

profile of v25, /device:TPU:1, one launch (start us, length us, event | category | flops | bytes accessed | tf_op | source)
XLA Modules:
  0.0 92.7 jit_solution(15114728787408760168)
XLA Ops:
  0.7 3.0 %pad_dynamic-slice_fusion.1 = (bf16[128,2,6,128]{3,2,1,0:T(8,128)(2,1)S(1)}, bf16[128,2,6,128]{3,2,1,0:T(8,128)(2,1)}) fusion(s32[]{:T(128)S(6)} %select_n.125, bf16[128,2,32,128]{3,2,1,0:T(8,128)(2,1)} %param.7, s32[]{:T(128)S(6)} %select_n.127), kind=kLoop, calls=%fused_computation.2 | loop fusion | bytes 2883592 | tf_op jit(solution)/shard_map/dynamic_slice | solution.py:109
  3.7 2.1 %collective-permute-start = (bf16[128,2,6,128]{3,2,1,0:T(8,128)(2,1)}, bf16[128,2,6,128]{3,2,1,0:T(8,128)(2,1)}, u32[]{:S(2)}, u32[]{:S(2)}) collective-permute-start(bf16[128,2,6,128]{3,2,1,0:T(8,128)(2,1)} %get-tuple-element.13), channel_id=1, source_target_pairs={{0,4},{4,0},{1,5},{5,1},{2,6},{6,2},{3,7},{7,3},{8,12},{12,8},{9,1... | collective-permute-start | bytes 1179656 | tf_op jit(solution)/shard_map/ppermute | solution.py:112
  6.2 1.2 %reshape.130 = bf16[4,2,18432]{2,1,0:T(2,128)(2,1)} reshape(bf16[4,3,3,64,64]{4,3,2,1,0:T(8,128)(2,1)S(1)} %broadcast_in_dim.28) | data formatting | bytes 589824
  7.4 4.5 %all-to-all-start = ((bf16[4,2,18432]{2,1,0:T(2,128)(2,1)}), bf16[4,2,18432]{2,1,0:T(2,128)(2,1)S(1)}, u32[]{:S(2)}, u32[]{:S(2)}) async-start(bf16[4,2,18432]{2,1,0:T(2,128)(2,1)} %reshape.130), calls=%async_computation | async-start | bytes 589824 | tf_op jit(solution)/shard_map/all_to_all | solution.py:85
  16.4 6.3 %collective-permute-done.3 = bf16[2,64,2,4,128]{4,1,3,2,0:T(8,128)(2,1)S(1)} collective-permute-done((bf16[2,64,2,4,128]{4,1,3,2,0:T(8,128)(2,1)S(1)}, bf16[2,64,2,4,128]{4,1,3,2,0:T(8,128)(2,1)S(1)}, u32[]{:S(2)}, u32[]{:S(2)}) %collective-permute-start.3) | collective-permute-done | bytes 262176 | tf_op jit(solution)/shard_map/ppermute | solution.py:142
  24.6 2.1 %collective-permute-start.1 = (bf16[3,3,64,256]{3,2,1,0:T(8,128)(2,1)S(1)}, bf16[3,3,64,256]{3,2,1,0:T(8,128)(2,1)S(1)}, u32[]{:S(2)}, u32[]{:S(2)}) collective-permute-start(bf16[3,3,64,256]{3,2,1,0:T(8,128)(2,1)S(1)} %squeeze.6), channel_id=1, source_target_pairs={{0,4},{4,0},{1,5},{5,1},{2,6},{6,2},{3,7},{7,3},{8,12},{12,8},{9,1... | collective-permute-start | bytes 884744 | tf_op jit(solution)/shard_map/ppermute | solution.py:27
  26.7 0.9 broadcast_select_fusion.2
  27.6 4.2 %all-to-all-start.1 = ((bf16[4,64,2,4,128]{4,1,3,2,0:T(8,128)(2,1)}), bf16[4,64,2,4,128]{4,1,3,2,0:T(8,128)(2,1)S(1)}, u32[]{:S(2)}, u32[]{:S(2)}) async-start(bf16[4,64,2,4,128]{4,1,3,2,0:T(8,128)(2,1)} %broadcast_select_fusion.2), calls=%async_computation.1 | async-start | bytes 1048576 | tf_op jit(solution)/shard_map/all_to_all | solution.py:151
  32.4 2.6 %collective-permute-start.2 = (bf16[3,3,128,256]{3,2,1,0:T(8,128)(2,1)S(1)}, bf16[3,3,128,256]{3,2,1,0:T(8,128)(2,1)}, u32[]{:S(2)}, u32[]{:S(2)}) collective-permute-start(bf16[3,3,128,256]{3,2,1,0:T(8,128)(2,1)S(1)} %maximum_select_fusion.1), channel_id=1, source_target_pairs={{0,8},{8,0},{16,24},{24,16},{1,9},{9,1},{17,25},{25,17},{2,10},{10... | collective-permute-start | bytes 1769480 | tf_op jit(solution)/shard_map/ppermute | solution.py:86
  35.0 1.6 %fusion.4 = bf16[256,6,2,128]{3,1,2,0:T(8,128)(2,1)S(1)} fusion(bf16[128,2,6,128]{3,2,1,0:T(8,128)(2,1)} %collective-permute-done, bf16[128,2,6,128]{3,2,1,0:T(8,128)(2,1)S(1)} %get-tuple-element.12, pred[]{:T(512)S(6)} %eq.23), kind=kLoop, calls=%fused_computation.15 | loop fusion | flops 1179648 | bytes 1572865 | tf_op jit(solution)/shard_map/jit(_where)/select_n | solution.py:18
  36.7 1.3 %copy.110 = bf16[256,6,2,128]{0,2,3,1:T(2,128)(2,1)S(1)} copy(bf16[256,6,2,128]{3,1,2,0:T(8,128)(2,1)S(1)} %fusion.4) | data formatting | bytes 1572864
  38.7 1.7 %fusion.7 = bf16[256,6,2,8,19]{0,2,4,3,1:T(2,128)(2,1)} fusion(bf16[256,6,2,7,2]{0,2,4,3,1:T(2,128)(2,1)S(1)} %slice.64, bf16[256,6,2,8,17]{0,2,4,3,1:T(2,128)(2,1)S(1)} %bitcast.82), kind=kLoop, calls=%fused_computation.20 | loop fusion | flops 2801664 | bytes 1855488 | tf_op jit(solution)/shard_map/conv_general_dilated | solution.py:54
  40.4 5.2 %all-to-all-done.1 = bf16[4,64,2,4,128]{4,1,3,2,0:T(8,128)(2,1)S(1)} async-done(((bf16[4,64,2,4,128]{4,1,3,2,0:T(8,128)(2,1)}), bf16[4,64,2,4,128]{4,1,3,2,0:T(8,128)(2,1)S(1)}, u32[]{:S(2)}, u32[]{:S(2)}) %all-to-all-start.1) | async-done | bytes 524320 | tf_op jit(solution)/shard_map/all_to_all | solution.py:151
  45.9 1.2 %broadcast_select_fusion.1 = (bf16[3,3,128,256]{3,2,1,0:T(8,128)(2,1)S(1)}, bf16[3,3,128,256]{3,2,1,0:T(8,128)(2,1)S(1)}) fusion(bf16[3,3,128,256]{3,2,1,0:T(8,128)(2,1)S(1)} %maximum_select_fusion.1, bf16[3,3,128,256]{3,2,1,0:T(8,128)(2,1)} %collective-permute-done.2, pred[]{:T(512)S(6)} %eq.24), kind=kLoop, calls=%fused_computation.29 | loop fusion | flops 589824 | bytes 2359297 | tf_op jit(solution)/shard_map/jit(_where)/select_n | solution.py:87
  47.3 1.5 %fusion.2 = bf16[4,16,17,256]{3,1,2,0:T(8,128)(2,1)S(1)} fusion(bf16[3,3,256,256]{3,2,1,0:T(8,128)(2,1)S(1)} %bitcast.94, bf16[256,6,2,8,19]{0,2,4,3,1:T(2,128)(2,1)S(1)} %copy-done.1, pred[16,17]{0,1:T(8,128)(4,1)S(1)} %copy-done.7), kind=kOutput, calls=%fused_computation.9 | convolution fusion | flops 1284014080 | bytes 2670864 | tf_op jit(solution)/shard_map/conv_general_dilated | solution.py:54
  49.7 4.7 %collective-permute-start.4 = (bf16[512,1,4,128]{0,2,3,1:T(4,128)(2,1)S(1)}, bf16[512,1,4,128]{0,2,3,1:T(4,128)(2,1)}, u32[]{:S(2)}, u32[]{:S(2)}) collective-permute-start(bf16[512,1,4,128]{0,2,3,1:T(4,128)(2,1)S(1)} %get-tuple-element.16), channel_id=1, source_target_pairs={{0,8},{8,16},{16,24},{1,9},{9,17},{17,25},{2,10},{10,18},{18,26},{... | collective-permute-start | bytes 1572872 | tf_op jit(solution)/shard_map/ppermute | solution.py:48
  54.4 2.1 %collective-permute-start.5 = (bf16[512,1,4,128]{0,2,3,1:T(4,128)(2,1)S(1)}, bf16[512,1,4,128]{0,2,3,1:T(4,128)(2,1)}, u32[]{:S(2)}, u32[]{:S(2)}) collective-permute-start(bf16[512,1,4,128]{0,2,3,1:T(4,128)(2,1)S(1)} %get-tuple-element.17), channel_id=1, source_target_pairs={{8,0},{16,8},{24,16},{9,1},{17,9},{25,17},{10,2},{18,10},{26,18},{... | collective-permute-start | bytes 1572872 | tf_op jit(solution)/shard_map/ppermute | solution.py:49
  56.6 1.1 %fusion.23 = (bf16[1,256,256]{2,1,0:T(8,128)(2,1)S(1)}, bf16[1,256,256]{2,1,0:T(8,128)(2,1)S(1)}, bf16[1,256,256]{2,1,0:T(8,128)(2,1)S(1)}) fusion(bf16[3,256,256]{2,1,0:T(8,128)(2,1)} %param.9), kind=kLoop, calls=%fused_computation.65 | loop fusion | bytes 786432 | tf_op jit(solution)/shard_map/slice | solution.py:163
  57.6 2.9 %collective-permute-done.4 = bf16[512,1,4,128]{0,2,3,1:T(4,128)(2,1)} collective-permute-done((bf16[512,1,4,128]{0,2,3,1:T(4,128)(2,1)S(1)}, bf16[512,1,4,128]{0,2,3,1:T(4,128)(2,1)}, u32[]{:S(2)}, u32[]{:S(2)}) %collective-permute-start.4) | collective-permute-done | bytes 524320 | tf_op jit(solution)/shard_map/ppermute | solution.py:48
  60.5 4.5 %collective-permute-done.5 = bf16[512,1,4,128]{0,2,3,1:T(4,128)(2,1)} collective-permute-done((bf16[512,1,4,128]{0,2,3,1:T(4,128)(2,1)S(1)}, bf16[512,1,4,128]{0,2,3,1:T(4,128)(2,1)}, u32[]{:S(2)}, u32[]{:S(2)}) %collective-permute-start.5) | collective-permute-done | bytes 524320 | tf_op jit(solution)/shard_map/ppermute | solution.py:49
  65.0 2.0 %pad_maximum_fusion = bf16[512,4,4,128]{0,2,3,1:T(4,128)(2,1)S(1)} fusion(bf16[512,1,4,128]{0,2,3,1:T(4,128)(2,1)} %collective-permute-done.5, bf16[256,2,4,128]{0,2,3,1:T(4,128)(2,1)S(1)} %copy.90, bf16[256,2,4,128]{0,2,3,1:T(4,128)(2,1)S(1)} %slice_bitcast_fusion, bf16[512,1,4,128]{0,2,3,1:T(4,128)(2,1)} %collective-permute-done.4), kind=kLoop, calls=%fused_computation.3 | loop fusion | flops 8388608 | bytes 4194304 | tf_op jit(solution)/shard_map/concatenate | solution.py:50
  67.8 1.4 %convolution_convert_fusion = bf16[2,4,8,16,256]{4,2,3,1,0:T(8,128)(2,1)S(1)} fusion(bf16[256,4,4,8,16]{0,2,4,3,1:T(4,128)(2,1)S(1)} %bitcast.97, bf16[1,256,256]{2,1,0:T(8,128)(2,1)S(1)} %get-tuple-element.27, bf16[1,256,256]{2,1,0:T(8,128)(2,1)S(1)} %get-tuple-element.28, bf16[1,256,256]{2,1,0:T(8,128)(2,1)S(1)} %get-tuple-element.26), kind=kOutput, calls=%fused_computation.11 | convolution fusion | flops 403308544 | bytes 1966080 | tf_op jit(solution)/shard_map/conv_general_dilated | solution.py:65
  69.3 1.9 %collective-permute-start.6 = (bf16[256,2,1,128]{0,3,2,1:T(8,128)(2,1)S(1)}, bf16[256,2,1,128]{0,3,2,1:T(8,128)(2,1)S(1)}, u32[]{:S(2)}, u32[]{:S(2)}) collective-permute-start(bf16[256,2,1,128]{0,3,2,1:T(8,128)(2,1)S(1)} %get-tuple-element.20), channel_id=1, source_target_pairs={{0,4},{4,5},{5,1},{1,2},{2,6},{6,7},{7,3},{8,12},{12,13},{13,9},{9... | collective-permute-start | bytes 393224 | tf_op jit(solution)/shard_map/ppermute | solution.py:48
  71.2 1.3 %collective-permute-start.7 = (bf16[256,2,1,128]{0,3,2,1:T(8,128)(2,1)S(1)}, bf16[256,2,1,128]{0,3,2,1:T(8,128)(2,1)S(1)}, u32[]{:S(2)}, u32[]{:S(2)}) collective-permute-start(bf16[256,2,1,128]{0,3,2,1:T(8,128)(2,1)S(1)} %get-tuple-element.21), channel_id=1, source_target_pairs={{4,0},{5,4},{1,5},{2,1},{6,2},{7,6},{3,7},{12,8},{13,12},{9,13},{1... | collective-permute-start | bytes 393224 | tf_op jit(solution)/shard_map/ppermute | solution.py:49
  72.5 1.4 %convolution_convert_fusion.1 = bf16[2,4,8,16,256]{4,2,3,1,0:T(8,128)(2,1)S(1)} fusion(bf16[256,4,4,8,16]{0,2,4,3,1:T(4,128)(2,1)S(1)} %bitcast.96, bf16[3,256,256]{2,1,0:T(8,128)(2,1)S(1)} %copy-done.3), kind=kOutput, calls=%fused_computation.12 | convolution fusion | flops 402915328 | bytes 1966080 | tf_op jit(solution)/shard_map/conv_general_dilated | solution.py:65
  74.0 1.1 %copy.95 = bf16[256,2,4,128]{3,2,1,0:T(4,128)(2,1)} copy(bf16[256,2,4,128]{0,3,2,1:T(8,128)(2,1)S(1)} %bitcast.91) | data formatting | bytes 1048576 | tf_op jit(solution)/shard_map/convert_element_type | solution.py:122
  75.1 4.5 %all-to-all-start.2 = ((bf16[256,2,4,128]{3,2,1,0:T(4,128)(2,1)}), bf16[256,2,4,128]{3,2,1,0:T(4,128)(2,1)S(1)}, u32[]{:S(2)}, u32[]{:S(2)}) async-start(bf16[256,2,4,128]{3,2,1,0:T(4,128)(2,1)} %copy.95), calls=%async_computation.2 | async-start | bytes 1048576 | tf_op jit(solution)/shard_map/all_to_all | solution.py:123
  82.2 1.5 %fusion.3 = bf16[4,16,17,256]{3,1,2,0:T(8,128)(2,1)S(1)} fusion(bf16[3,3,256,256]{3,2,1,0:T(8,128)(2,1)S(1)} %bitcast.95, bf16[256,6,2,8,19]{0,2,4,3,1:T(2,128)(2,1)S(1)} %fusion.8, pred[16,17]{0,1:T(8,128)(4,1)S(1)} %copy-done.8), kind=kOutput, calls=%fused_computation.10 | convolution fusion | flops 1284014080 | bytes 2670864 | tf_op jit(solution)/shard_map/conv_general_dilated | solution.py:54
  84.4 1.1 %collective-permute-start.8 = (bf16[128,2,4,128]{0,2,3,1:T(4,128)(2,1)S(1)}, bf16[128,2,4,128]{0,2,3,1:T(4,128)(2,1)S(1)}, u32[]{:S(2)}, u32[]{:S(2)}) collective-permute-start(bf16[128,2,4,128]{0,2,3,1:T(4,128)(2,1)S(1)} %get-tuple-element.19), channel_id=1, source_target_pairs={{0,4},{1,5},{2,6},{3,7},{4,0},{5,1},{6,2},{7,3},{8,12},{9,13},{10,... | collective-permute-start | bytes 786440 | tf_op jit(solution)/shard_map/ppermute | solution.py:175
  85.5 4.2 %collective-permute-done.8 = bf16[128,2,4,128]{0,2,3,1:T(4,128)(2,1)S(1)} collective-permute-done((bf16[128,2,4,128]{0,2,3,1:T(4,128)(2,1)S(1)}, bf16[128,2,4,128]{0,2,3,1:T(4,128)(2,1)S(1)}, u32[]{:S(2)}, u32[]{:S(2)}) %collective-permute-start.8) | collective-permute-done | bytes 262176 | tf_op jit(solution)/shard_map/ppermute | solution.py:175
  90.1 1.3 %copy.105 = bf16[128,2,8,128]{3,2,1,0:T(8,128)(2,1)} copy(bf16[128,2,8,128]{0,2,3,1:T(8,128)(2,1)S(1)} %maximum_select_fusion.2) | data formatting | bytes 1048576
  91.6 1.1 %copy.104 = bf16[64,2,16,128]{3,2,1,0:T(8,128)(2,1)} copy(bf16[64,2,16,128]{3,0,2,1:T(8,128)(2,1)S(1)} %bitcast.93) | data formatting | bytes 1048576
  (70 shorter events, 11.7 us)
Async XLA Ops:
  0.6 5.2 %copy-start = (bf16[3,3,128,64]{2,3,1,0:T(8,128)(2,1)S(1)}, bf16[3,3,128,64]{2,3,1,0:T(8,128)(2,1)}, u32[]{:S(2)}) copy-start(bf16[3,3,128,64]{2,3,1,0:T(8,128)(2,1)} %param.8) | copy-start | bytes 442372
  3.7 8.1 %copy-start.4 = (s32[2,2]{1,0:T(2,128)S(1)}, s32[2,2]{1,0:T(2,128)}, u32[]{:S(2)}) copy-start(s32[2,2]{1,0:T(2,128)} %constant.92.clone) | copy-start | bytes 52
  3.7 8.1 %copy-start.5 = (s32[2,2]{1,0:T(2,128)S(1)}, s32[2,2]{1,0:T(2,128)}, u32[]{:S(2)}) copy-start(s32[2,2]{1,0:T(2,128)} %constant.93.clone) | copy-start | bytes 52
  3.7 11.9 %copy-start.2 = (bf16[64,2,16,128]{3,2,1,0:T(8,128)(2,1)S(1)}, bf16[64,2,16,128]{3,2,1,0:T(8,128)(2,1)}, u32[]{:S(2)}) copy-start(bf16[64,2,16,128]{3,2,1,0:T(8,128)(2,1)} %param.10) | copy-start | bytes 1572868
  3.7 31.3 %collective-permute-start = (bf16[128,2,6,128]{3,2,1,0:T(8,128)(2,1)}, bf16[128,2,6,128]{3,2,1,0:T(8,128)(2,1)}, u32[]{:S(2)}, u32[]{:S(2)}) collective-permute-start(bf16[128,2,6,128]{3,2,1,0:T(8,128)(2,1)} %get-tuple-element.13), channel_id=1, source_target_pairs={{0,4},{4,0},{1,5},{5,1},{2,6},{6,2},{3,7},{7,3},{8,12},{12,8},{9,1... | collective-permute-start | bytes 1179656 | tf_op jit(solution)/shard_map/ppermute | solution.py:112
  6.2 10.1 %copy-start.6 = (s32[2,4]{1,0:T(2,128)S(1)}, s32[2,4]{1,0:T(2,128)}, u32[]{:S(2)}) copy-start(s32[2,4]{1,0:T(2,128)} %constant.94.clone) | copy-start | bytes 100
  7.4 16.0 %all-to-all-start = ((bf16[4,2,18432]{2,1,0:T(2,128)(2,1)}), bf16[4,2,18432]{2,1,0:T(2,128)(2,1)S(1)}, u32[]{:S(2)}, u32[]{:S(2)}) async-start(bf16[4,2,18432]{2,1,0:T(2,128)(2,1)} %reshape.130), calls=%async_computation | async-start | bytes 589824 | tf_op jit(solution)/shard_map/all_to_all | solution.py:85
  16.0 6.6 %collective-permute-start.3 = (bf16[2,64,2,4,128]{4,1,3,2,0:T(8,128)(2,1)S(1)}, bf16[2,64,2,4,128]{4,1,3,2,0:T(8,128)(2,1)S(1)}, u32[]{:S(2)}, u32[]{:S(2)}) collective-permute-start(bf16[2,64,2,4,128]{4,1,3,2,0:T(8,128)(2,1)S(1)} %pad_maximum_fusion.4), channel_id=1, source_target_pairs={{0,4},{4,0},{1,5},{5,1},{2,6},{6,2},{3,7},{7,3},{8,12},{12,8},{9,1... | collective-permute-start | bytes 786440 | tf_op jit(solution)/shard_map/ppermute | solution.py:142
  24.6 7.5 %collective-permute-start.1 = (bf16[3,3,64,256]{3,2,1,0:T(8,128)(2,1)S(1)}, bf16[3,3,64,256]{3,2,1,0:T(8,128)(2,1)S(1)}, u32[]{:S(2)}, u32[]{:S(2)}) collective-permute-start(bf16[3,3,64,256]{3,2,1,0:T(8,128)(2,1)S(1)} %squeeze.6), channel_id=1, source_target_pairs={{0,4},{4,0},{1,5},{5,1},{2,6},{6,2},{3,7},{7,3},{8,12},{12,8},{9,1... | collective-permute-start | bytes 884744 | tf_op jit(solution)/shard_map/ppermute | solution.py:27
  27.6 17.9 %all-to-all-start.1 = ((bf16[4,64,2,4,128]{4,1,3,2,0:T(8,128)(2,1)}), bf16[4,64,2,4,128]{4,1,3,2,0:T(8,128)(2,1)S(1)}, u32[]{:S(2)}, u32[]{:S(2)}) async-start(bf16[4,64,2,4,128]{4,1,3,2,0:T(8,128)(2,1)} %broadcast_select_fusion.2), calls=%async_computation.1 | async-start | bytes 1048576 | tf_op jit(solution)/shard_map/all_to_all | solution.py:151
  32.4 13.5 %collective-permute-start.2 = (bf16[3,3,128,256]{3,2,1,0:T(8,128)(2,1)S(1)}, bf16[3,3,128,256]{3,2,1,0:T(8,128)(2,1)}, u32[]{:S(2)}, u32[]{:S(2)}) collective-permute-start(bf16[3,3,128,256]{3,2,1,0:T(8,128)(2,1)S(1)} %maximum_select_fusion.1), channel_id=1, source_target_pairs={{0,8},{8,0},{16,24},{24,16},{1,9},{9,1},{17,25},{25,17},{2,10},{10... | collective-permute-start | bytes 1769480 | tf_op jit(solution)/shard_map/ppermute | solution.py:86
  45.9 1.4 %copy-start.1 = (bf16[256,6,2,8,19]{0,2,4,3,1:T(2,128)(2,1)S(1)}, bf16[256,6,2,8,19]{0,2,4,3,1:T(2,128)(2,1)}, u32[]{:S(2)}) copy-start(bf16[256,6,2,8,19]{0,2,4,3,1:T(2,128)(2,1)} %fusion.7) | copy-start | bytes 2801668
  45.9 1.4 %copy-start.7 = (pred[16,17]{0,1:T(8,128)(4,1)S(1)}, pred[16,17]{0,1:T(8,128)(4,1)}, u32[]{:S(2)}) copy-start(pred[16,17]{0,1:T(8,128)(4,1)} %constant.114) | copy-start | bytes 820
  49.7 10.8 %collective-permute-start.4 = (bf16[512,1,4,128]{0,2,3,1:T(4,128)(2,1)S(1)}, bf16[512,1,4,128]{0,2,3,1:T(4,128)(2,1)}, u32[]{:S(2)}, u32[]{:S(2)}) collective-permute-start(bf16[512,1,4,128]{0,2,3,1:T(4,128)(2,1)S(1)} %get-tuple-element.16), channel_id=1, source_target_pairs={{0,8},{8,16},{16,24},{1,9},{9,17},{17,25},{2,10},{10,18},{18,26},{... | collective-permute-start | bytes 1572872 | tf_op jit(solution)/shard_map/ppermute | solution.py:48
  54.4 10.6 %collective-permute-start.5 = (bf16[512,1,4,128]{0,2,3,1:T(4,128)(2,1)S(1)}, bf16[512,1,4,128]{0,2,3,1:T(4,128)(2,1)}, u32[]{:S(2)}, u32[]{:S(2)}) collective-permute-start(bf16[512,1,4,128]{0,2,3,1:T(4,128)(2,1)S(1)} %get-tuple-element.17), channel_id=1, source_target_pairs={{8,0},{16,8},{24,16},{9,1},{17,9},{25,17},{10,2},{18,10},{26,18},{... | collective-permute-start | bytes 1572872 | tf_op jit(solution)/shard_map/ppermute | solution.py:49
  67.7 4.8 %copy-start.3 = (bf16[3,256,256]{2,1,0:T(8,128)(2,1)S(1)}, bf16[3,256,256]{2,1,0:T(8,128)(2,1)}, u32[]{:S(2)}) copy-start(bf16[3,256,256]{2,1,0:T(8,128)(2,1)} %param.9) | copy-start | bytes 1179652
  69.3 10.3 %collective-permute-start.6 = (bf16[256,2,1,128]{0,3,2,1:T(8,128)(2,1)S(1)}, bf16[256,2,1,128]{0,3,2,1:T(8,128)(2,1)S(1)}, u32[]{:S(2)}, u32[]{:S(2)}) collective-permute-start(bf16[256,2,1,128]{0,3,2,1:T(8,128)(2,1)S(1)} %get-tuple-element.20), channel_id=1, source_target_pairs={{0,4},{4,5},{5,1},{1,2},{2,6},{6,7},{7,3},{8,12},{12,13},{13,9},{9... | collective-permute-start | bytes 393224 | tf_op jit(solution)/shard_map/ppermute | solution.py:48
  71.2 8.4 %collective-permute-start.7 = (bf16[256,2,1,128]{0,3,2,1:T(8,128)(2,1)S(1)}, bf16[256,2,1,128]{0,3,2,1:T(8,128)(2,1)S(1)}, u32[]{:S(2)}, u32[]{:S(2)}) collective-permute-start(bf16[256,2,1,128]{0,3,2,1:T(8,128)(2,1)S(1)} %get-tuple-element.21), channel_id=1, source_target_pairs={{4,0},{5,4},{1,5},{2,1},{6,2},{7,6},{3,7},{12,8},{13,12},{9,13},{1... | collective-permute-start | bytes 393224 | tf_op jit(solution)/shard_map/ppermute | solution.py:49
  75.1 16.4 %all-to-all-start.2 = ((bf16[256,2,4,128]{3,2,1,0:T(4,128)(2,1)}), bf16[256,2,4,128]{3,2,1,0:T(4,128)(2,1)S(1)}, u32[]{:S(2)}, u32[]{:S(2)}) async-start(bf16[256,2,4,128]{3,2,1,0:T(4,128)(2,1)} %copy.95), calls=%async_computation.2 | async-start | bytes 1048576 | tf_op jit(solution)/shard_map/all_to_all | solution.py:123
  80.6 1.6 %copy-start.8 = (pred[16,17]{0,1:T(8,128)(4,1)S(1)}, pred[16,17]{0,1:T(8,128)(4,1)}, u32[]{:S(2)}) copy-start(pred[16,17]{0,1:T(8,128)(4,1)} %constant.114) | copy-start | bytes 820
  84.4 5.3 %collective-permute-start.8 = (bf16[128,2,4,128]{0,2,3,1:T(4,128)(2,1)S(1)}, bf16[128,2,4,128]{0,2,3,1:T(4,128)(2,1)S(1)}, u32[]{:S(2)}, u32[]{:S(2)}) collective-permute-start(bf16[128,2,4,128]{0,2,3,1:T(4,128)(2,1)S(1)} %get-tuple-element.19), channel_id=1, source_target_pairs={{0,4},{1,5},{2,6},{3,7},{4,0},{5,1},{6,2},{7,3},{8,12},{9,13},{10,... | collective-permute-start | bytes 786440 | tf_op jit(solution)/shard_map/ppermute | solution.py:175

commit v26 on v23

--- a/solution.py
+++ b/solution.py
@@ -82,7 +82,8 @@
     half = c_loc // 2
     mine = lax.dynamic_slice_in_dim(weight, core * half, half, 2)
     spread = jnp.broadcast_to(mine[None], (filts,) + mine.shape)
-    by_filt = gather_blocks(lax.all_to_all(spread, "filt", 0, 4, tiled=True)[0], "chan", 2)
+    got = lax.all_to_all(spread, "filt", 0, 4, tiled=True)[0]
+    by_filt = jnp.concatenate([got] + [lax.ppermute(got, "chan", shift_pairs(chans, k)) for k in range(1, chans)], axis=2)
     other = lax.ppermute(by_filt, "slab", [(i, i ^ 1) for i in range(slabs)])
     first = jnp.where(core == 0, by_filt, other)
     second = jnp.where(core == 0, other, by_filt)
@@ -110,7 +111,7 @@
     pieces = [window(chan)]
     for k in range(1, chans):
         pieces.append(lax.ppermute(window((chan + k) % chans), "chan", shift_pairs(chans, k)))
-    all_channels = order_blocks(pieces, chan, 0)
+    all_channels = jnp.concatenate(pieces, axis=0)
     return plane_conv(all_channels, weight, "HWIO").astype(jnp.bfloat16)
 
 
@@ -165,12 +166,13 @@
     chan = lax.axis_index("chan")
     c_loc = grad_in.shape[0] // chans
     even = filt % 2 == 0
-    pieces = [lax.dynamic_slice_in_dim(grad_in, chan * c_loc, c_loc, 0)]
+    pieces = [grad_in[:c_loc]]
     for k in range(1, chans):
         target = jnp.where(even, (chan + k) % chans, (chan - k) % chans)
         pairs = [(c * filts + f, (((c + k) if f % 2 == 0 else (c - k)) % chans) * filts + f)
                  for c in range(chans) for f in range(filts)]
-        pieces.append(lax.ppermute(lax.dynamic_slice_in_dim(grad_in, target * c_loc, c_loc, 0), ROWS, pairs))
+        at = (chan - target) % chans
+        pieces.append(lax.ppermute(lax.dynamic_slice_in_dim(grad_in, at * c_loc, c_loc, 0), ROWS, pairs))
     return order_blocks(pieces, jnp.where(even, chan, chans - 1 - chan), 2)
 
 

time: 93.6 us -> 92.8 us (level)
  waiting for transfers between devices: 22.7 us -> 21.6 us
    select_n x3 -> x1, other arithmetic: 2.38 us -> 0.48 us  [order_blocks(): jnp.where(me % 2 == 0, jnp.concatenate(pieces, axis=dim), jnp.concatenate...]
    concatenate x0 -> x2, local copies, waits for them, and re-layouts: none -> 1.35 us  [the longest x1 0.72 us: gather_weight(): jnp.concatenate([got] + [lax.ppermute(got, 'chan', shift_pairs(chans, k))...]
    concatenate x0 -> x1, other arithmetic: none -> 1.25 us  [forward(): all_channels = jnp.concatenate(pieces, axis=0)]
    unnamed x26 -> x25, local copies, waits for them, and re-layouts: 6.47 us -> 7.2 us
  transfers between devices with their start and end apart: 12 -> 12, of which waited for: 6 -> 5; matrix products, arithmetic and copies ran while one was open for 24% -> 26% of each run, Pallas kernels for 0% -> 0%
where the time goes in v26:
time: 92.8 us; the launch traced here: 92.2 us
  starting transfers between devices  31.1 us (34%)
  waiting for transfers between devices  21.6 us (23%)
  local copies, waits for them, and re-layouts  20.6 us (22%)
  other arithmetic  9.33 us (10%)
  matrix products  5.77 us (6%)
  between operations  3.72 us (4%)
    ppermute x2, starting transfers between devices, halo(): lax.ppermute(lax.slice_in_dim(x, length - 1, length, axis=dim), axis, up)  7.24 us
    unnamed x25, local copies, waits for them, and re-layouts  7.2 us
    ppermute x1, waiting for transfers between devices, backward(): lax.ppermute(send, 'chan', shift_pairs(chans, k))  6.26 us
    all_to_all x1, waiting for transfers between devices, backward(): all_filters = lax.all_to_all(blocks, 'filt', 0, 0, tiled=True)  4.59 us
    all_to_all x1, starting transfers between devices, forward_out(): return lax.all_to_all(out, 'filt', 0, 2, tiled=True)  4.52 us
    ppermute x2, waiting for transfers between devices, halo(): after = lax.ppermute(lax.slice_in_dim(x, 0, 1, axis=dim), axis, down)  4.5 us
    all_to_all x1, starting transfers between devices, gather_weight(): got = lax.all_to_all(spread, 'filt', 0, 4, tiled=True)[0]  4.45 us
    all_to_all x1, starting transfers between devices, backward(): all_filters = lax.all_to_all(blocks, 'filt', 0, 0, tiled=True)  4.1 us
  transfers between devices with their start and end apart: 12, of which 5 were waited for; matrix products, arithmetic and copies ran while one was open for 26% of the time, Pallas kernels for 0%

profile of v26, /device:TPU:1, one launch (start us, length us, event | category | flops | bytes accessed | tf_op | source)
XLA Modules:
  0.0 92.2 jit_solution(7104435493559935604)
XLA Ops:
  0.7 2.2 %pad_dynamic-slice_fusion.1 = (bf16[128,2,6,128]{3,2,1,0:T(8,128)(2,1)S(1)}, bf16[128,2,6,128]{3,2,1,0:T(8,128)(2,1)S(1)}) fusion(s32[]{:T(128)S(6)} %select_n.104, bf16[128,2,32,128]{3,2,1,0:T(8,128)(2,1)} %param.7, s32[]{:T(128)S(6)} %select_n.106), kind=kLoop, calls=%fused_computation.2 | loop fusion | bytes 2883592 | tf_op jit(solution)/shard_map/dynamic_slice | solution.py:110
  3.0 2.1 %collective-permute-start = (bf16[128,2,6,128]{3,2,1,0:T(8,128)(2,1)S(1)}, bf16[128,2,6,128]{3,2,1,0:T(8,128)(2,1)}, u32[]{:S(2)}, u32[]{:S(2)}) collective-permute-start(bf16[128,2,6,128]{3,2,1,0:T(8,128)(2,1)S(1)} %get-tuple-element.13), channel_id=1, source_target_pairs={{0,4},{4,0},{1,5},{5,1},{2,6},{6,2},{3,7},{7,3},{8,12},{12,8},{9,1... | collective-permute-start | bytes 1179656 | tf_op jit(solution)/shard_map/ppermute | solution.py:113
  5.5 1.2 %reshape.133 = bf16[4,2,18432]{2,1,0:T(2,128)(2,1)} reshape(bf16[4,3,3,64,64]{4,3,2,1,0:T(8,128)(2,1)S(1)} %broadcast_in_dim.28) | data formatting | bytes 589824
  6.7 4.5 %all-to-all-start = ((bf16[4,2,18432]{2,1,0:T(2,128)(2,1)}), bf16[4,2,18432]{2,1,0:T(2,128)(2,1)S(1)}, u32[]{:S(2)}, u32[]{:S(2)}) async-start(bf16[4,2,18432]{2,1,0:T(2,128)(2,1)} %reshape.133), calls=%async_computation | async-start | bytes 589824 | tf_op jit(solution)/shard_map/all_to_all | solution.py:85
  15.7 6.3 %collective-permute-done.3 = bf16[2,64,2,4,128]{4,1,3,2,0:T(8,128)(2,1)S(1)} collective-permute-done((bf16[2,64,2,4,128]{4,1,3,2,0:T(8,128)(2,1)S(1)}, bf16[2,64,2,4,128]{4,1,3,2,0:T(8,128)(2,1)S(1)}, u32[]{:S(2)}, u32[]{:S(2)}) %collective-permute-start.3) | collective-permute-done | bytes 262176 | tf_op jit(solution)/shard_map/ppermute | solution.py:143
  23.9 1.8 %collective-permute-start.1 = (bf16[3,3,64,256]{3,2,1,0:T(8,128)(2,1)S(1)}, bf16[3,3,64,256]{3,2,1,0:T(8,128)(2,1)S(1)}, u32[]{:S(2)}, u32[]{:S(2)}) collective-permute-start(bf16[3,3,64,256]{3,2,1,0:T(8,128)(2,1)S(1)} %squeeze.6), channel_id=1, source_target_pairs={{0,4},{4,0},{1,5},{5,1},{2,6},{6,2},{3,7},{7,3},{8,12},{12,8},{9,1... | collective-permute-start | bytes 884744 | tf_op jit(solution)/shard_map/ppermute | solution.py:86
  25.7 0.9 broadcast_select_fusion.2
  26.6 4.1 %all-to-all-start.1 = ((bf16[4,64,2,4,128]{4,1,3,2,0:T(8,128)(2,1)}), bf16[4,64,2,4,128]{4,1,3,2,0:T(8,128)(2,1)S(1)}, u32[]{:S(2)}, u32[]{:S(2)}) async-start(bf16[4,64,2,4,128]{4,1,3,2,0:T(8,128)(2,1)} %broadcast_select_fusion.2), calls=%async_computation.1 | async-start | bytes 1048576 | tf_op jit(solution)/shard_map/all_to_all | solution.py:152
  32.1 2.3 %collective-permute-start.2 = (bf16[3,3,128,256]{3,2,1,0:T(8,128)(2,1)}, bf16[3,3,128,256]{3,2,1,0:T(8,128)(2,1)}, u32[]{:S(2)}, u32[]{:S(2)}) collective-permute-start(bf16[3,3,128,256]{3,2,1,0:T(8,128)(2,1)} %constant_dynamic-update-slice_fusion), channel_id=1, source_target_pairs={{0,8},{8,0},{16,24},{24,16},{1,9},{9,1},{17,25},{25,17},{2,10},{10... | collective-permute-start | bytes 1769480 | tf_op jit(solution)/shard_map/ppermute | solution.py:87
  34.5 1.2 %maximum_bitcast_fusion = bf16[256,6,2,128]{3,1,2,0:T(8,128)(2,1)S(1)} fusion(bf16[128,2,6,128]{3,2,1,0:T(8,128)(2,1)} %collective-permute-done, bf16[128,2,6,128]{3,2,1,0:T(8,128)(2,1)S(1)} %get-tuple-element.12), kind=kLoop, calls=%fused_computation.14 | loop fusion | flops 393216 | bytes 1572864 | tf_op jit(solution)/shard_map/concatenate | solution.py:114
  35.7 1.3 %copy.119 = bf16[256,6,2,128]{0,2,3,1:T(2,128)(2,1)S(1)} copy(bf16[256,6,2,128]{3,1,2,0:T(8,128)(2,1)S(1)} %maximum_bitcast_fusion) | data formatting | bytes 1572864
  37.7 1.7 %fusion.6 = bf16[256,6,2,8,19]{0,2,4,3,1:T(2,128)(2,1)} fusion(bf16[256,6,2,7,2]{0,2,4,3,1:T(2,128)(2,1)S(1)} %slice.58, bf16[256,6,2,8,17]{0,2,4,3,1:T(2,128)(2,1)S(1)} %bitcast.85), kind=kLoop, calls=%fused_computation.19 | loop fusion | flops 2801664 | bytes 1855488 | tf_op jit(solution)/shard_map/conv_general_dilated | solution.py:54
  39.4 4.6 %all-to-all-done.1 = bf16[4,64,2,4,128]{4,1,3,2,0:T(8,128)(2,1)S(1)} async-done(((bf16[4,64,2,4,128]{4,1,3,2,0:T(8,128)(2,1)}), bf16[4,64,2,4,128]{4,1,3,2,0:T(8,128)(2,1)S(1)}, u32[]{:S(2)}, u32[]{:S(2)}) %all-to-all-start.1) | async-done | bytes 524320 | tf_op jit(solution)/shard_map/all_to_all | solution.py:152
  44.4 1.4 %broadcast_select_fusion.1 = (bf16[3,3,128,256]{3,2,1,0:T(8,128)(2,1)S(1)}, bf16[3,3,128,256]{3,2,1,0:T(8,128)(2,1)S(1)}) fusion(bf16[3,3,128,256]{3,2,1,0:T(8,128)(2,1)} %constant_dynamic-update-slice_fusion, bf16[3,3,128,256]{3,2,1,0:T(8,128)(2,1)} %collective-permute-done.2, pred[]{:T(512)S(6)} %eq.18), kind=kLoop, calls=%fused_computation.27 | loop fusion | flops 589824 | bytes 2359297 | tf_op jit(solution)/shard_map/jit(_where)/select_n | solution.py:88
  45.9 1.5 %fusion.2 = bf16[4,16,17,256]{3,1,2,0:T(8,128)(2,1)S(1)} fusion(bf16[3,3,256,256]{3,2,1,0:T(8,128)(2,1)S(1)} %bitcast.97, bf16[256,6,2,8,19]{0,2,4,3,1:T(2,128)(2,1)S(1)} %copy-done.1, pred[16,17]{0,1:T(8,128)(4,1)S(1)} %copy-done.8), kind=kOutput, calls=%fused_computation.9 | convolution fusion | flops 1284014080 | bytes 2670864 | tf_op jit(solution)/shard_map/conv_general_dilated | solution.py:54
  48.4 5.1 %collective-permute-start.4 = (bf16[512,1,4,128]{0,2,3,1:T(4,128)(2,1)S(1)}, bf16[512,1,4,128]{0,2,3,1:T(4,128)(2,1)}, u32[]{:S(2)}, u32[]{:S(2)}) collective-permute-start(bf16[512,1,4,128]{0,2,3,1:T(4,128)(2,1)S(1)} %get-tuple-element.16), channel_id=1, source_target_pairs={{0,8},{8,16},{16,24},{1,9},{9,17},{17,25},{2,10},{10,18},{18,26},{... | collective-permute-start | bytes 1572872 | tf_op jit(solution)/shard_map/ppermute | solution.py:48
  53.5 1.9 %collective-permute-start.5 = (bf16[512,1,4,128]{0,2,3,1:T(4,128)(2,1)S(1)}, bf16[512,1,4,128]{0,2,3,1:T(4,128)(2,1)}, u32[]{:S(2)}, u32[]{:S(2)}) collective-permute-start(bf16[512,1,4,128]{0,2,3,1:T(4,128)(2,1)S(1)} %get-tuple-element.17), channel_id=1, source_target_pairs={{8,0},{16,8},{24,16},{9,1},{17,9},{25,17},{10,2},{18,10},{26,18},{... | collective-permute-start | bytes 1572872 | tf_op jit(solution)/shard_map/ppermute | solution.py:49
  55.5 1.8 %rev.4 = bf16[3,256,256]{2,1,0:T(8,128)(2,1)} reverse(bf16[3,256,256]{2,1,0:T(8,128)(2,1)} %param.9), dimensions={0} | reverse | bytes 786432 | tf_op jit(solution)/shard_map/rev | solution.py:163
  57.2 2.4 %collective-permute-done.4 = bf16[512,1,4,128]{0,2,3,1:T(4,128)(2,1)} collective-permute-done((bf16[512,1,4,128]{0,2,3,1:T(4,128)(2,1)S(1)}, bf16[512,1,4,128]{0,2,3,1:T(4,128)(2,1)}, u32[]{:S(2)}, u32[]{:S(2)}) %collective-permute-start.4) | collective-permute-done | bytes 524320 | tf_op jit(solution)/shard_map/ppermute | solution.py:48
  59.6 4.5 %collective-permute-done.5 = bf16[512,1,4,128]{0,2,3,1:T(4,128)(2,1)} collective-permute-done((bf16[512,1,4,128]{0,2,3,1:T(4,128)(2,1)S(1)}, bf16[512,1,4,128]{0,2,3,1:T(4,128)(2,1)}, u32[]{:S(2)}, u32[]{:S(2)}) %collective-permute-start.5) | collective-permute-done | bytes 524320 | tf_op jit(solution)/shard_map/ppermute | solution.py:49
  64.1 2.0 %pad_maximum_fusion = bf16[512,4,4,128]{0,2,3,1:T(4,128)(2,1)S(1)} fusion(bf16[512,1,4,128]{0,2,3,1:T(4,128)(2,1)} %collective-permute-done.5, bf16[256,2,4,128]{0,2,3,1:T(4,128)(2,1)S(1)} %copy.97, bf16[256,2,4,128]{0,2,3,1:T(4,128)(2,1)S(1)} %slice_bitcast_fusion, bf16[512,1,4,128]{0,2,3,1:T(4,128)(2,1)} %collective-permute-done.4), kind=kLoop, calls=%fused_computation.3 | loop fusion | flops 8388608 | bytes 4194304 | tf_op jit(solution)/shard_map/concatenate | solution.py:50
  67.1 1.4 %convolution_convert_fusion = bf16[2,4,8,16,256]{4,2,3,1,0:T(8,128)(2,1)S(1)} fusion(bf16[256,4,4,8,16]{0,2,4,3,1:T(4,128)(2,1)S(1)} %bitcast.101, bf16[3,256,256]{2,1,0:T(8,128)(2,1)S(1)} %copy-done.4), kind=kOutput, calls=%fused_computation.11 | convolution fusion | flops 402915328 | bytes 1966080 | tf_op jit(solution)/shard_map/conv_general_dilated | solution.py:65
  68.6 2.1 %collective-permute-start.6 = (bf16[256,2,1,128]{0,3,2,1:T(8,128)(2,1)S(1)}, bf16[256,2,1,128]{0,3,2,1:T(8,128)(2,1)S(1)}, u32[]{:S(2)}, u32[]{:S(2)}) collective-permute-start(bf16[256,2,1,128]{0,3,2,1:T(8,128)(2,1)S(1)} %get-tuple-element.18), channel_id=1, source_target_pairs={{0,4},{4,5},{5,1},{1,2},{2,6},{6,7},{7,3},{8,12},{12,13},{13,9},{9... | collective-permute-start | bytes 393224 | tf_op jit(solution)/shard_map/ppermute | solution.py:48
  70.8 1.3 %collective-permute-start.7 = (bf16[256,2,1,128]{0,3,2,1:T(8,128)(2,1)S(1)}, bf16[256,2,1,128]{0,3,2,1:T(8,128)(2,1)S(1)}, u32[]{:S(2)}, u32[]{:S(2)}) collective-permute-start(bf16[256,2,1,128]{0,3,2,1:T(8,128)(2,1)S(1)} %get-tuple-element.19), channel_id=1, source_target_pairs={{4,0},{5,4},{1,5},{2,1},{6,2},{7,6},{3,7},{12,8},{13,12},{9,13},{1... | collective-permute-start | bytes 393224 | tf_op jit(solution)/shard_map/ppermute | solution.py:49
  72.1 1.4 %convolution_convert_fusion.1 = bf16[2,4,8,16,256]{4,2,3,1,0:T(8,128)(2,1)S(1)} fusion(bf16[256,4,4,8,16]{0,2,4,3,1:T(4,128)(2,1)S(1)} %bitcast.100, bf16[3,256,256]{2,1,0:T(8,128)(2,1)S(1)} %copy-done.3), kind=kOutput, calls=%fused_computation.12 | convolution fusion | flops 402915328 | bytes 1966080 | tf_op jit(solution)/shard_map/conv_general_dilated | solution.py:65
  73.6 1.1 %copy.102 = bf16[256,2,4,128]{3,2,1,0:T(4,128)(2,1)} copy(bf16[256,2,4,128]{0,3,2,1:T(8,128)(2,1)S(1)} %bitcast.94) | data formatting | bytes 1048576 | tf_op jit(solution)/shard_map/convert_element_type | solution.py:123
  74.7 4.5 %all-to-all-start.2 = ((bf16[256,2,4,128]{3,2,1,0:T(4,128)(2,1)}), bf16[256,2,4,128]{3,2,1,0:T(4,128)(2,1)S(1)}, u32[]{:S(2)}, u32[]{:S(2)}) async-start(bf16[256,2,4,128]{3,2,1,0:T(4,128)(2,1)} %copy.102), calls=%async_computation.2 | async-start | bytes 1048576 | tf_op jit(solution)/shard_map/all_to_all | solution.py:124
  81.7 1.5 %fusion.3 = bf16[4,16,17,256]{3,1,2,0:T(8,128)(2,1)S(1)} fusion(bf16[3,3,256,256]{3,2,1,0:T(8,128)(2,1)S(1)} %bitcast.98, bf16[256,6,2,8,19]{0,2,4,3,1:T(2,128)(2,1)S(1)} %fusion.7, pred[16,17]{0,1:T(8,128)(4,1)S(1)} %copy-done.8), kind=kOutput, calls=%fused_computation.10 | convolution fusion | flops 1284014080 | bytes 2670864 | tf_op jit(solution)/shard_map/conv_general_dilated | solution.py:54
  83.8 1.1 %collective-permute-start.8 = (bf16[128,2,4,128]{0,2,3,1:T(4,128)(2,1)S(1)}, bf16[128,2,4,128]{0,2,3,1:T(4,128)(2,1)S(1)}, u32[]{:S(2)}, u32[]{:S(2)}) collective-permute-start(bf16[128,2,4,128]{0,2,3,1:T(4,128)(2,1)S(1)} %dynamic-slice_bitcast_fusion), channel_id=1, source_target_pairs={{0,4},{1,5},{2,6},{3,7},{4,0},{5,1},{6,2},{7,3},{8,12},{9,13},{10,... | collective-permute-start | bytes 786440 | tf_op jit(solution)/shard_map/ppermute | solution.py:175
  85.2 3.9 %collective-permute-done.8 = bf16[128,2,4,128]{0,2,3,1:T(4,128)(2,1)S(1)} collective-permute-done((bf16[128,2,4,128]{0,2,3,1:T(4,128)(2,1)S(1)}, bf16[128,2,4,128]{0,2,3,1:T(4,128)(2,1)S(1)}, u32[]{:S(2)}, u32[]{:S(2)}) %collective-permute-start.8) | collective-permute-done | bytes 262176 | tf_op jit(solution)/shard_map/ppermute | solution.py:175
  89.6 1.3 %copy.114 = bf16[128,2,8,128]{3,2,1,0:T(8,128)(2,1)} copy(bf16[128,2,8,128]{0,2,3,1:T(8,128)(2,1)S(1)} %maximum_select_fusion) | data formatting | bytes 1048576
  91.0 1.1 %copy.113 = bf16[64,2,16,128]{3,2,1,0:T(8,128)(2,1)} copy(bf16[64,2,16,128]{3,0,2,1:T(8,128)(2,1)S(1)} %bitcast.96) | data formatting | bytes 1048576
  (74 shorter events, 12.9 us)
Async XLA Ops:
  0.6 4.5 %copy-start = (bf16[3,3,128,64]{2,3,1,0:T(8,128)(2,1)S(1)}, bf16[3,3,128,64]{2,3,1,0:T(8,128)(2,1)}, u32[]{:S(2)}) copy-start(bf16[3,3,128,64]{2,3,1,0:T(8,128)(2,1)} %param.8) | copy-start | bytes 442372
  2.9 8.2 %copy-start.5 = (s32[2,2]{1,0:T(2,128)S(1)}, s32[2,2]{1,0:T(2,128)}, u32[]{:S(2)}) copy-start(s32[2,2]{1,0:T(2,128)} %constant.90.clone) | copy-start | bytes 52
  2.9 8.2 %copy-start.6 = (s32[2,2]{1,0:T(2,128)S(1)}, s32[2,2]{1,0:T(2,128)}, u32[]{:S(2)}) copy-start(s32[2,2]{1,0:T(2,128)} %constant.91.clone) | copy-start | bytes 52
  2.9 12.0 %copy-start.2 = (bf16[64,2,16,128]{3,2,1,0:T(8,128)(2,1)S(1)}, bf16[64,2,16,128]{3,2,1,0:T(8,128)(2,1)}, u32[]{:S(2)}) copy-start(bf16[64,2,16,128]{3,2,1,0:T(8,128)(2,1)} %param.10) | copy-start | bytes 1572868
  3.0 31.5 %collective-permute-start = (bf16[128,2,6,128]{3,2,1,0:T(8,128)(2,1)S(1)}, bf16[128,2,6,128]{3,2,1,0:T(8,128)(2,1)}, u32[]{:S(2)}, u32[]{:S(2)}) collective-permute-start(bf16[128,2,6,128]{3,2,1,0:T(8,128)(2,1)S(1)} %get-tuple-element.13), channel_id=1, source_target_pairs={{0,4},{4,0},{1,5},{5,1},{2,6},{6,2},{3,7},{7,3},{8,12},{12,8},{9,1... | collective-permute-start | bytes 1179656 | tf_op jit(solution)/shard_map/ppermute | solution.py:113
  5.5 10.1 %copy-start.7 = (s32[2,4]{1,0:T(2,128)S(1)}, s32[2,4]{1,0:T(2,128)}, u32[]{:S(2)}) copy-start(s32[2,4]{1,0:T(2,128)} %constant.92.clone) | copy-start | bytes 100
  6.7 16.0 %all-to-all-start = ((bf16[4,2,18432]{2,1,0:T(2,128)(2,1)}), bf16[4,2,18432]{2,1,0:T(2,128)(2,1)S(1)}, u32[]{:S(2)}, u32[]{:S(2)}) async-start(bf16[4,2,18432]{2,1,0:T(2,128)(2,1)} %reshape.133), calls=%async_computation | async-start | bytes 589824 | tf_op jit(solution)/shard_map/all_to_all | solution.py:85
  15.3 6.6 %collective-permute-start.3 = (bf16[2,64,2,4,128]{4,1,3,2,0:T(8,128)(2,1)S(1)}, bf16[2,64,2,4,128]{4,1,3,2,0:T(8,128)(2,1)S(1)}, u32[]{:S(2)}, u32[]{:S(2)}) collective-permute-start(bf16[2,64,2,4,128]{4,1,3,2,0:T(8,128)(2,1)S(1)} %pad_maximum_fusion.4), channel_id=1, source_target_pairs={{0,4},{4,0},{1,5},{5,1},{2,6},{6,2},{3,7},{7,3},{8,12},{12,8},{9,1... | collective-permute-start | bytes 786440 | tf_op jit(solution)/shard_map/ppermute | solution.py:143
  23.9 7.5 %collective-permute-start.1 = (bf16[3,3,64,256]{3,2,1,0:T(8,128)(2,1)S(1)}, bf16[3,3,64,256]{3,2,1,0:T(8,128)(2,1)S(1)}, u32[]{:S(2)}, u32[]{:S(2)}) collective-permute-start(bf16[3,3,64,256]{3,2,1,0:T(8,128)(2,1)S(1)} %squeeze.6), channel_id=1, source_target_pairs={{0,4},{4,0},{1,5},{5,1},{2,6},{6,2},{3,7},{7,3},{8,12},{12,8},{9,1... | collective-permute-start | bytes 884744 | tf_op jit(solution)/shard_map/ppermute | solution.py:86
  26.6 17.4 %all-to-all-start.1 = ((bf16[4,64,2,4,128]{4,1,3,2,0:T(8,128)(2,1)}), bf16[4,64,2,4,128]{4,1,3,2,0:T(8,128)(2,1)S(1)}, u32[]{:S(2)}, u32[]{:S(2)}) async-start(bf16[4,64,2,4,128]{4,1,3,2,0:T(8,128)(2,1)} %broadcast_select_fusion.2), calls=%async_computation.1 | async-start | bytes 1048576 | tf_op jit(solution)/shard_map/all_to_all | solution.py:152
  32.1 12.2 %collective-permute-start.2 = (bf16[3,3,128,256]{3,2,1,0:T(8,128)(2,1)}, bf16[3,3,128,256]{3,2,1,0:T(8,128)(2,1)}, u32[]{:S(2)}, u32[]{:S(2)}) collective-permute-start(bf16[3,3,128,256]{3,2,1,0:T(8,128)(2,1)} %constant_dynamic-update-slice_fusion), channel_id=1, source_target_pairs={{0,8},{8,0},{16,24},{24,16},{1,9},{9,1},{17,25},{25,17},{2,10},{10... | collective-permute-start | bytes 1769480 | tf_op jit(solution)/shard_map/ppermute | solution.py:87
  44.4 1.6 %copy-start.1 = (bf16[256,6,2,8,19]{0,2,4,3,1:T(2,128)(2,1)S(1)}, bf16[256,6,2,8,19]{0,2,4,3,1:T(2,128)(2,1)}, u32[]{:S(2)}) copy-start(bf16[256,6,2,8,19]{0,2,4,3,1:T(2,128)(2,1)} %fusion.6) | copy-start | bytes 2801668
  44.4 1.6 %copy-start.8 = (pred[16,17]{0,1:T(8,128)(4,1)S(1)}, pred[16,17]{0,1:T(8,128)(4,1)}, u32[]{:S(2)}) copy-start(pred[16,17]{0,1:T(8,128)(4,1)} %constant.112) | copy-start | bytes 820
  48.4 11.2 %collective-permute-start.4 = (bf16[512,1,4,128]{0,2,3,1:T(4,128)(2,1)S(1)}, bf16[512,1,4,128]{0,2,3,1:T(4,128)(2,1)}, u32[]{:S(2)}, u32[]{:S(2)}) collective-permute-start(bf16[512,1,4,128]{0,2,3,1:T(4,128)(2,1)S(1)} %get-tuple-element.16), channel_id=1, source_target_pairs={{0,8},{8,16},{16,24},{1,9},{9,17},{17,25},{2,10},{10,18},{18,26},{... | collective-permute-start | bytes 1572872 | tf_op jit(solution)/shard_map/ppermute | solution.py:48
  53.5 10.6 %collective-permute-start.5 = (bf16[512,1,4,128]{0,2,3,1:T(4,128)(2,1)S(1)}, bf16[512,1,4,128]{0,2,3,1:T(4,128)(2,1)}, u32[]{:S(2)}, u32[]{:S(2)}) collective-permute-start(bf16[512,1,4,128]{0,2,3,1:T(4,128)(2,1)S(1)} %get-tuple-element.17), channel_id=1, source_target_pairs={{8,0},{16,8},{24,16},{9,1},{17,9},{25,17},{10,2},{18,10},{26,18},{... | collective-permute-start | bytes 1572872 | tf_op jit(solution)/shard_map/ppermute | solution.py:49
  66.1 1.0 %copy-start.4 = (bf16[3,256,256]{2,1,0:T(8,128)(2,1)S(1)}, bf16[3,256,256]{2,1,0:T(8,128)(2,1)}, u32[]{:S(2)}) copy-start(bf16[3,256,256]{2,1,0:T(8,128)(2,1)} %rev.4) | copy-start | bytes 1179652
  67.1 4.9 %copy-start.3 = (bf16[3,256,256]{2,1,0:T(8,128)(2,1)S(1)}, bf16[3,256,256]{2,1,0:T(8,128)(2,1)}, u32[]{:S(2)}) copy-start(bf16[3,256,256]{2,1,0:T(8,128)(2,1)} %param.9) | copy-start | bytes 1179652
  68.6 10.5 %collective-permute-start.6 = (bf16[256,2,1,128]{0,3,2,1:T(8,128)(2,1)S(1)}, bf16[256,2,1,128]{0,3,2,1:T(8,128)(2,1)S(1)}, u32[]{:S(2)}, u32[]{:S(2)}) collective-permute-start(bf16[256,2,1,128]{0,3,2,1:T(8,128)(2,1)S(1)} %get-tuple-element.18), channel_id=1, source_target_pairs={{0,4},{4,5},{5,1},{1,2},{2,6},{6,7},{7,3},{8,12},{12,13},{13,9},{9... | collective-permute-start | bytes 393224 | tf_op jit(solution)/shard_map/ppermute | solution.py:48
  70.8 8.4 %collective-permute-start.7 = (bf16[256,2,1,128]{0,3,2,1:T(8,128)(2,1)S(1)}, bf16[256,2,1,128]{0,3,2,1:T(8,128)(2,1)S(1)}, u32[]{:S(2)}, u32[]{:S(2)}) collective-permute-start(bf16[256,2,1,128]{0,3,2,1:T(8,128)(2,1)S(1)} %get-tuple-element.19), channel_id=1, source_target_pairs={{4,0},{5,4},{1,5},{2,1},{6,2},{7,6},{3,7},{12,8},{13,12},{9,13},{1... | collective-permute-start | bytes 393224 | tf_op jit(solution)/shard_map/ppermute | solution.py:49
  74.7 16.2 %all-to-all-start.2 = ((bf16[256,2,4,128]{3,2,1,0:T(4,128)(2,1)}), bf16[256,2,4,128]{3,2,1,0:T(4,128)(2,1)S(1)}, u32[]{:S(2)}, u32[]{:S(2)}) async-start(bf16[256,2,4,128]{3,2,1,0:T(4,128)(2,1)} %copy.102), calls=%async_computation.2 | async-start | bytes 1048576 | tf_op jit(solution)/shard_map/all_to_all | solution.py:124
  83.8 5.3 %collective-permute-start.8 = (bf16[128,2,4,128]{0,2,3,1:T(4,128)(2,1)S(1)}, bf16[128,2,4,128]{0,2,3,1:T(4,128)(2,1)S(1)}, u32[]{:S(2)}, u32[]{:S(2)}) collective-permute-start(bf16[128,2,4,128]{0,2,3,1:T(4,128)(2,1)S(1)} %dynamic-slice_bitcast_fusion), channel_id=1, source_target_pairs={{0,4},{1,5},{2,6},{3,7},{4,0},{5,1},{6,2},{7,3},{8,12},{9,13},{10,... | collective-permute-start | bytes 786440 | tf_op jit(solution)/shard_map/ppermute | solution.py:175

commit v27 on v16

--- a/solution.py
+++ b/solution.py
@@ -14,6 +14,8 @@
     n = len(pieces)
     if n == 1:
         return pieces[0]
+    if n == 2:
+        return jnp.where(me % 2 == 0, jnp.concatenate(pieces, axis=dim), jnp.concatenate(pieces[::-1], axis=dim))
     block = pieces[0].shape[dim]
     stacked = jnp.concatenate(pieces[::-1], axis=dim)
     return jnp.roll(stacked, (me + 1) * block, axis=dim)
@@ -73,11 +75,10 @@
 
 def gather_weight(weight):
     filts = lax.axis_size("filt")
+    chans = lax.axis_size("chan")
     spread = jnp.broadcast_to(weight[None], (filts,) + weight.shape)
-    by_filt = lax.all_to_all(spread, "filt", 0, 4, tiled=True)[0]
-    chans = lax.axis_size("chan")
-    pieces = [by_filt] + [lax.ppermute(by_filt, "chan", shift_pairs(chans, k)) for k in range(1, chans)]
-    return jnp.concatenate(pieces, axis=2)
+    got = lax.all_to_all(spread, "filt", 0, 4, tiled=True)[0]
+    return jnp.concatenate([got] + [lax.ppermute(got, "chan", shift_pairs(chans, k)) for k in range(1, chans)], axis=2)
 
 
 def sub_block(chan, filt, filts):

time: 95.6 us -> 95 us (level)
    concatenate x1 -> x0, other arithmetic: 1.03 us -> none  [order_blocks(): return jnp.roll(stacked, (me + 1) * block, axis=dim)]
  transfers between devices with their start and end apart: 11 -> 11, of which waited for: 7 -> 7; matrix products, arithmetic and copies ran while one was open for 23% -> 22% of each run, Pallas kernels for 0% -> 0%
where the time goes in v27:
time: 95 us; the launch traced here: 94.1 us
  waiting for transfers between devices  30.7 us (32%)
  starting transfers between devices  28.1 us (30%)
  local copies, waits for them, and re-layouts  17.4 us (18%)
  matrix products  8.26 us (9%)
  other arithmetic  5.97 us (6%)
  between operations  3.68 us (4%)
    all_to_all x1, waiting for transfers between devices, backward(): all_filters = lax.all_to_all(blocks, 'filt', 0, 0, tiled=True)  8.45 us
    ppermute x2, starting transfers between devices, halo(): lax.ppermute(lax.slice_in_dim(x, length - 1, length, axis=dim), axis, up)  7.49 us
    ppermute x1, waiting for transfers between devices, backward(): lax.ppermute(send, 'chan', shift_pairs(chans, k))  6.54 us
    all_to_all x1, starting transfers between devices, forward_out(): return lax.all_to_all(out, 'filt', 0, 2, tiled=True)  6.38 us
    conv_general_dilated x2, matrix products, plane_conv(): lax.conv_general_dilated(rows, weight, window_strides=(1, 1), padding=((0...  5.47 us
    unnamed x20, local copies, waits for them, and re-layouts  4.91 us
    ppermute x1, waiting for transfers between devices, backward_in(): lax.ppermute(lax.dynamic_slice_in_dim(grad_in, at * c_loc, c_loc, 0), ROW...  4.72 us
    all_to_all x1, starting transfers between devices, gather_weight(): got = lax.all_to_all(spread, 'filt', 0, 4, tiled=True)[0]  4.48 us
  transfers between devices with their start and end apart: 11, of which 7 were waited for; matrix products, arithmetic and copies ran while one was open for 22% of the time, Pallas kernels for 0%

profile of v27, /device:TPU:1, one launch (start us, length us, event | category | flops | bytes accessed | tf_op | source)
XLA Modules:
  0.0 94.1 jit_solution(4393529171370646420)
XLA Ops:
  0.7 2.3 %pad_dynamic-slice_fusion.1 = (bf16[128,2,6,128]{3,2,1,0:T(8,128)(2,1)S(1)}, bf16[128,2,6,128]{3,2,1,0:T(8,128)(2,1)S(1)}) fusion(s32[]{:T(128)S(6)} %select_n.85, bf16[128,2,32,128]{3,2,1,0:T(8,128)(2,1)} %param.7, s32[]{:T(128)S(6)} %select_n.87), kind=kLoop, calls=%fused_computation.2 | loop fusion | bytes 2883592 | tf_op jit(solution)/shard_map/dynamic_slice | solution.py:99
  3.0 2.1 %collective-permute-start = (bf16[128,2,6,128]{3,2,1,0:T(8,128)(2,1)S(1)}, bf16[128,2,6,128]{3,2,1,0:T(8,128)(2,1)}, u32[]{:S(2)}, u32[]{:S(2)}) collective-permute-start(bf16[128,2,6,128]{3,2,1,0:T(8,128)(2,1)S(1)} %get-tuple-element.11), channel_id=1, source_target_pairs={{0,4},{4,0},{1,5},{5,1},{2,6},{6,2},{3,7},{7,3},{8,12},{12,8},{9,1... | collective-permute-start | bytes 1179656 | tf_op jit(solution)/shard_map/ppermute | solution.py:102
  5.1 1.0 %broadcast_in_dim.28 = bf16[4,3,3,128,64]{3,4,2,1,0:T(8,128)(2,1)} broadcast(bf16[3,3,128,64]{2,3,1,0:T(8,128)(2,1)S(1)} %copy-done.3), dimensions={1,2,3,4} | broadcast | bytes 737280 | tf_op jit(solution)/shard_map/broadcast_in_dim | solution.py:79
  6.1 4.5 %all-to-all-start = ((bf16[4,3,3,128,64]{3,4,2,1,0:T(8,128)(2,1)}), bf16[4,3,3,128,64]{3,4,2,1,0:T(8,128)(2,1)S(1)}, u32[]{:S(2)}, u32[]{:S(2)}) async-start(bf16[4,3,3,128,64]{3,4,2,1,0:T(8,128)(2,1)} %broadcast_in_dim.28), calls=%async_computation | async-start | bytes 1179648 | tf_op jit(solution)/shard_map/all_to_all | solution.py:80
  15.0 6.5 %collective-permute-done.2 = bf16[2,64,2,4,128]{4,1,3,2,0:T(8,128)(2,1)S(1)} collective-permute-done((bf16[2,64,2,4,128]{4,1,3,2,0:T(8,128)(2,1)S(1)}, bf16[2,64,2,4,128]{4,1,3,2,0:T(8,128)(2,1)S(1)}, u32[]{:S(2)}, u32[]{:S(2)}) %collective-permute-start.2) | collective-permute-done | bytes 262176 | tf_op jit(solution)/shard_map/ppermute | solution.py:132
  22.3 0.9 broadcast_select_fusion
  23.2 2.7 %all-to-all-done = bf16[4,3,3,128,64]{3,4,2,1,0:T(8,128)(2,1)S(1)} async-done(((bf16[4,3,3,128,64]{3,4,2,1,0:T(8,128)(2,1)}), bf16[4,3,3,128,64]{3,4,2,1,0:T(8,128)(2,1)S(1)}, u32[]{:S(2)}, u32[]{:S(2)}) %all-to-all-start) | async-done | bytes 589856 | tf_op jit(solution)/shard_map/all_to_all | solution.py:80
  25.9 3.5 %all-to-all-start.1 = ((bf16[4,64,2,4,128]{4,1,3,2,0:T(8,128)(2,1)}), bf16[4,64,2,4,128]{4,1,3,2,0:T(8,128)(2,1)S(1)}, u32[]{:S(2)}, u32[]{:S(2)}) async-start(bf16[4,64,2,4,128]{4,1,3,2,0:T(8,128)(2,1)} %broadcast_select_fusion), calls=%async_computation.1 | async-start | bytes 1048576 | tf_op jit(solution)/shard_map/all_to_all | solution.py:141
  29.5 1.1 %copy.64 = bf16[3,3,128,256]{3,2,1,0:T(8,128)(2,1)} copy(bf16[3,3,128,256]{2,3,1,0:T(8,128)(2,1)S(1)} %bitcast.81) | data formatting | bytes 1179648 | tf_op jit(solution)/shard_map/squeeze | solution.py:80
  30.7 1.2 %maximum_bitcast_fusion = bf16[256,6,2,128]{3,1,2,0:T(8,128)(2,1)S(1)} fusion(bf16[128,2,6,128]{3,2,1,0:T(8,128)(2,1)} %collective-permute-done, bf16[128,2,6,128]{3,2,1,0:T(8,128)(2,1)S(1)} %get-tuple-element.10), kind=kLoop, calls=%fused_computation.14 | loop fusion | flops 393216 | bytes 1572864 | tf_op jit(solution)/shard_map/concatenate | solution.py:103
  32.0 1.3 %copy.93 = bf16[256,6,2,128]{0,2,3,1:T(2,128)(2,1)S(1)} copy(bf16[256,6,2,128]{3,1,2,0:T(8,128)(2,1)S(1)} %maximum_bitcast_fusion) | data formatting | bytes 1572864
  34.0 0.9 fusion.6
  34.9 8.5 %all-to-all-done.1 = bf16[4,64,2,4,128]{4,1,3,2,0:T(8,128)(2,1)S(1)} async-done(((bf16[4,64,2,4,128]{4,1,3,2,0:T(8,128)(2,1)}), bf16[4,64,2,4,128]{4,1,3,2,0:T(8,128)(2,1)S(1)}, u32[]{:S(2)}, u32[]{:S(2)}) %all-to-all-start.1) | async-done | bytes 524320 | tf_op jit(solution)/shard_map/all_to_all | solution.py:141
  44.2 2.7 %fusion.2 = bf16[4,16,17,256]{3,1,2,0:T(8,128)(2,1)S(1)} fusion(bf16[256,6,2,8,19]{0,2,4,3,1:T(2,128)(2,1)S(1)} %fusion.6, bf16[3,3,128,256]{3,2,1,0:T(8,128)(2,1)} %collective-permute-done.1, bf16[3,3,128,256]{3,2,1,0:T(8,128)(2,1)} %copy.64, pred[16,17]{0,1:T(8,128)(4,1)S(1)} %copy-done.7), kind=kOutput, calls=%fused_computation.9 | convolution fusion | flops 1286373376 | bytes 2670864 | tf_op jit(solution)/shard_map/conv_general_dilated | solution.py:54
  47.9 5.4 %collective-permute-start.3 = (bf16[512,1,4,128]{0,2,3,1:T(4,128)(2,1)S(1)}, bf16[512,1,4,128]{0,2,3,1:T(4,128)(2,1)S(1)}, u32[]{:S(2)}, u32[]{:S(2)}) collective-permute-start(bf16[512,1,4,128]{0,2,3,1:T(4,128)(2,1)S(1)} %get-tuple-element.12), channel_id=1, source_target_pairs={{0,8},{8,16},{16,24},{1,9},{9,17},{17,25},{2,10},{10,18},{18,26},{... | collective-permute-start | bytes 1572872 | tf_op jit(solution)/shard_map/ppermute | solution.py:48
  53.3 1.9 %collective-permute-start.4 = (bf16[512,1,4,128]{0,2,3,1:T(4,128)(2,1)S(1)}, bf16[512,1,4,128]{0,2,3,1:T(4,128)(2,1)S(1)}, u32[]{:S(2)}, u32[]{:S(2)}) collective-permute-start(bf16[512,1,4,128]{0,2,3,1:T(4,128)(2,1)S(1)} %get-tuple-element.13), channel_id=1, source_target_pairs={{8,0},{16,8},{24,16},{9,1},{17,9},{25,17},{10,2},{18,10},{26,18},{... | collective-permute-start | bytes 1572872 | tf_op jit(solution)/shard_map/ppermute | solution.py:49
  55.3 0.8 rev.4
  56.0 3.3 %collective-permute-done.3 = bf16[512,1,4,128]{0,2,3,1:T(4,128)(2,1)S(1)} collective-permute-done((bf16[512,1,4,128]{0,2,3,1:T(4,128)(2,1)S(1)}, bf16[512,1,4,128]{0,2,3,1:T(4,128)(2,1)S(1)}, u32[]{:S(2)}, u32[]{:S(2)}) %collective-permute-start.3) | collective-permute-done | bytes 524320 | tf_op jit(solution)/shard_map/ppermute | solution.py:48
  59.4 4.4 %collective-permute-done.4 = bf16[512,1,4,128]{0,2,3,1:T(4,128)(2,1)S(1)} collective-permute-done((bf16[512,1,4,128]{0,2,3,1:T(4,128)(2,1)S(1)}, bf16[512,1,4,128]{0,2,3,1:T(4,128)(2,1)S(1)}, u32[]{:S(2)}, u32[]{:S(2)}) %collective-permute-start.4) | collective-permute-done | bytes 524320 | tf_op jit(solution)/shard_map/ppermute | solution.py:49
  63.8 1.0 %pad_maximum_fusion = bf16[512,4,4,128]{0,2,3,1:T(4,128)(2,1)S(1)} fusion(bf16[512,1,4,128]{0,2,3,1:T(4,128)(2,1)S(1)} %collective-permute-done.4, bf16[256,2,4,128]{0,2,3,1:T(4,128)(2,1)S(1)} %copy.71, bf16[256,2,4,128]{0,2,3,1:T(4,128)(2,1)S(1)} %slice_bitcast_fusion, bf16[512,1,4,128]{0,2,3,1:T(4,128)(2,1)S(1)} %collective-permute-done.3), kind=kLoop, calls=%fused_computation.3 | loop fusion | flops 8388608 | bytes 4194304 | tf_op jit(solution)/shard_map/concatenate | solution.py:50
  65.8 1.4 %convolution_convert_fusion = bf16[2,4,8,16,256]{4,2,3,1,0:T(8,128)(2,1)S(1)} fusion(bf16[256,4,4,8,16]{0,2,4,3,1:T(4,128)(2,1)S(1)} %bitcast.90, bf16[3,256,256]{2,1,0:T(8,128)(2,1)S(1)} %copy-done.2), kind=kOutput, calls=%fused_computation.11 | convolution fusion | flops 402915328 | bytes 1966080 | tf_op jit(solution)/shard_map/conv_general_dilated | solution.py:65
  67.3 2.1 %collective-permute-start.5 = (bf16[256,2,1,128]{0,3,2,1:T(8,128)(2,1)S(1)}, bf16[256,2,1,128]{0,3,2,1:T(8,128)(2,1)S(1)}, u32[]{:S(2)}, u32[]{:S(2)}) collective-permute-start(bf16[256,2,1,128]{0,3,2,1:T(8,128)(2,1)S(1)} %get-tuple-element.14), channel_id=1, source_target_pairs={{0,4},{4,5},{5,1},{1,2},{2,6},{6,7},{7,3},{8,12},{12,13},{13,9},{9... | collective-permute-start | bytes 393224 | tf_op jit(solution)/shard_map/ppermute | solution.py:48
  69.4 1.5 %collective-permute-start.6 = (bf16[256,2,1,128]{0,3,2,1:T(8,128)(2,1)S(1)}, bf16[256,2,1,128]{0,3,2,1:T(8,128)(2,1)S(1)}, u32[]{:S(2)}, u32[]{:S(2)}) collective-permute-start(bf16[256,2,1,128]{0,3,2,1:T(8,128)(2,1)S(1)} %get-tuple-element.15), channel_id=1, source_target_pairs={{4,0},{5,4},{1,5},{2,1},{6,2},{7,6},{3,7},{12,8},{13,12},{9,13},{1... | collective-permute-start | bytes 393224 | tf_op jit(solution)/shard_map/ppermute | solution.py:49
  70.9 1.4 %convolution_convert_fusion.1 = bf16[2,4,8,16,256]{4,2,3,1,0:T(8,128)(2,1)S(1)} fusion(bf16[256,4,4,8,16]{0,2,4,3,1:T(4,128)(2,1)S(1)} %bitcast.89, bf16[3,256,256]{2,1,0:T(8,128)(2,1)S(1)} %copy-done.1), kind=kOutput, calls=%fused_computation.12 | convolution fusion | flops 402915328 | bytes 1966080 | tf_op jit(solution)/shard_map/conv_general_dilated | solution.py:65
  72.4 1.1 %copy.76 = bf16[256,2,4,128]{3,2,1,0:T(4,128)(2,1)} copy(bf16[256,2,4,128]{0,3,2,1:T(8,128)(2,1)S(1)} %bitcast.85) | data formatting | bytes 1048576 | tf_op jit(solution)/shard_map/convert_element_type | solution.py:112
  73.5 6.4 %all-to-all-start.2 = ((bf16[256,2,4,128]{3,2,1,0:T(4,128)(2,1)}), bf16[256,2,4,128]{3,2,1,0:T(4,128)(2,1)S(1)}, u32[]{:S(2)}, u32[]{:S(2)}) async-start(bf16[256,2,4,128]{3,2,1,0:T(4,128)(2,1)} %copy.76), calls=%async_computation.2 | async-start | bytes 1048576 | tf_op jit(solution)/shard_map/all_to_all | solution.py:113
  80.0 0.8 copy.94
  81.5 0.9 fusion.7
  82.4 2.8 %fusion.3 = bf16[4,16,17,256]{3,1,2,0:T(8,128)(2,1)S(1)} fusion(bf16[256,6,2,8,19]{0,2,4,3,1:T(2,128)(2,1)S(1)} %fusion.7, bf16[3,3,128,256]{3,2,1,0:T(8,128)(2,1)} %collective-permute-done.1, bf16[3,3,128,256]{3,2,1,0:T(8,128)(2,1)} %copy.64, pred[16,17]{0,1:T(8,128)(4,1)S(1)} %copy-done.7), kind=kOutput, calls=%fused_computation.10 | convolution fusion | flops 1286373376 | bytes 2670864 | tf_op jit(solution)/shard_map/conv_general_dilated | solution.py:54
  86.3 4.7 %collective-permute-done.7 = bf16[128,2,4,128]{0,2,3,1:T(4,128)(2,1)S(1)} collective-permute-done((bf16[128,2,4,128]{0,2,3,1:T(4,128)(2,1)S(1)}, bf16[128,2,4,128]{0,2,3,1:T(4,128)(2,1)S(1)}, u32[]{:S(2)}, u32[]{:S(2)}) %collective-permute-start.7) | collective-permute-done | bytes 262176 | tf_op jit(solution)/shard_map/ppermute | solution.py:164
  91.5 1.3 %copy.88 = bf16[128,2,8,128]{3,2,1,0:T(8,128)(2,1)} copy(bf16[128,2,8,128]{0,2,3,1:T(8,128)(2,1)S(1)} %maximum_select_fusion) | data formatting | bytes 1048576
  93.0 1.1 %copy.87 = bf16[64,2,16,128]{3,2,1,0:T(8,128)(2,1)} copy(bf16[64,2,16,128]{3,0,2,1:T(8,128)(2,1)S(1)} %bitcast.87) | data formatting | bytes 1048576
  (62 shorter events, 9.0 us)
Async XLA Ops:
  0.6 4.5 %copy-start.3 = (bf16[3,3,128,64]{2,3,1,0:T(8,128)(2,1)S(1)}, bf16[3,3,128,64]{2,3,1,0:T(8,128)(2,1)}, u32[]{:S(2)}) copy-start(bf16[3,3,128,64]{2,3,1,0:T(8,128)(2,1)} %param.8) | copy-start | bytes 442372
  0.7 9.9 %copy-start.4 = (s32[2,2]{1,0:T(2,128)S(1)}, s32[2,2]{1,0:T(2,128)}, u32[]{:S(2)}) copy-start(s32[2,2]{1,0:T(2,128)} %constant.81.clone) | copy-start | bytes 52
  0.7 9.9 %copy-start.5 = (s32[2,2]{1,0:T(2,128)S(1)}, s32[2,2]{1,0:T(2,128)}, u32[]{:S(2)}) copy-start(s32[2,2]{1,0:T(2,128)} %constant.82.clone) | copy-start | bytes 52
  0.7 13.6 %copy-start = (bf16[64,2,16,128]{3,2,1,0:T(8,128)(2,1)S(1)}, bf16[64,2,16,128]{3,2,1,0:T(8,128)(2,1)}, u32[]{:S(2)}) copy-start(bf16[64,2,16,128]{3,2,1,0:T(8,128)(2,1)} %param.10) | copy-start | bytes 1572868
  3.0 12.0 %copy-start.6 = (s32[2,4]{1,0:T(2,128)S(1)}, s32[2,4]{1,0:T(2,128)}, u32[]{:S(2)}) copy-start(s32[2,4]{1,0:T(2,128)} %constant.83.clone) | copy-start | bytes 100
  3.0 27.7 %collective-permute-start = (bf16[128,2,6,128]{3,2,1,0:T(8,128)(2,1)S(1)}, bf16[128,2,6,128]{3,2,1,0:T(8,128)(2,1)}, u32[]{:S(2)}, u32[]{:S(2)}) collective-permute-start(bf16[128,2,6,128]{3,2,1,0:T(8,128)(2,1)S(1)} %get-tuple-element.11), channel_id=1, source_target_pairs={{0,4},{4,0},{1,5},{5,1},{2,6},{6,2},{3,7},{7,3},{8,12},{12,8},{9,1... | collective-permute-start | bytes 1179656 | tf_op jit(solution)/shard_map/ppermute | solution.py:102
  6.1 19.9 %all-to-all-start = ((bf16[4,3,3,128,64]{3,4,2,1,0:T(8,128)(2,1)}), bf16[4,3,3,128,64]{3,4,2,1,0:T(8,128)(2,1)S(1)}, u32[]{:S(2)}, u32[]{:S(2)}) async-start(bf16[4,3,3,128,64]{3,4,2,1,0:T(8,128)(2,1)} %broadcast_in_dim.28), calls=%async_computation | async-start | bytes 1179648 | tf_op jit(solution)/shard_map/all_to_all | solution.py:80
  14.7 6.9 %collective-permute-start.2 = (bf16[2,64,2,4,128]{4,1,3,2,0:T(8,128)(2,1)S(1)}, bf16[2,64,2,4,128]{4,1,3,2,0:T(8,128)(2,1)S(1)}, u32[]{:S(2)}, u32[]{:S(2)}) collective-permute-start(bf16[2,64,2,4,128]{4,1,3,2,0:T(8,128)(2,1)S(1)} %pad_maximum_fusion.6), channel_id=1, source_target_pairs={{0,4},{4,0},{1,5},{5,1},{2,6},{6,2},{3,7},{7,3},{8,12},{12,8},{9,1... | collective-permute-start | bytes 786440 | tf_op jit(solution)/shard_map/ppermute | solution.py:132
  25.9 17.4 %all-to-all-start.1 = ((bf16[4,64,2,4,128]{4,1,3,2,0:T(8,128)(2,1)}), bf16[4,64,2,4,128]{4,1,3,2,0:T(8,128)(2,1)S(1)}, u32[]{:S(2)}, u32[]{:S(2)}) async-start(bf16[4,64,2,4,128]{4,1,3,2,0:T(8,128)(2,1)} %broadcast_select_fusion), calls=%async_computation.1 | async-start | bytes 1048576 | tf_op jit(solution)/shard_map/all_to_all | solution.py:141
  30.5 13.7 %collective-permute-start.1 = (bf16[3,3,128,256]{3,2,1,0:T(8,128)(2,1)}, bf16[3,3,128,256]{3,2,1,0:T(8,128)(2,1)}, u32[]{:S(2)}, u32[]{:S(2)}) collective-permute-start(bf16[3,3,128,256]{3,2,1,0:T(8,128)(2,1)} %copy.64), channel_id=1, source_target_pairs={{0,4},{4,0},{1,5},{5,1},{2,6},{6,2},{3,7},{7,3},{8,12},{12,8},{9,1... | collective-permute-start | bytes 1769480 | tf_op jit(solution)/shard_map/ppermute | solution.py:81
  34.0 10.3 %copy-start.7 = (pred[16,17]{0,1:T(8,128)(4,1)S(1)}, pred[16,17]{0,1:T(8,128)(4,1)}, u32[]{:S(2)}) copy-start(pred[16,17]{0,1:T(8,128)(4,1)} %constant.103) | copy-start | bytes 820
  46.9 8.3 %copy-start.1 = (bf16[3,256,256]{2,1,0:T(8,128)(2,1)S(1)}, bf16[3,256,256]{2,1,0:T(8,128)(2,1)}, u32[]{:S(2)}) copy-start(bf16[3,256,256]{2,1,0:T(8,128)(2,1)} %param.9) | copy-start | bytes 1179652
  47.9 11.5 %collective-permute-start.3 = (bf16[512,1,4,128]{0,2,3,1:T(4,128)(2,1)S(1)}, bf16[512,1,4,128]{0,2,3,1:T(4,128)(2,1)S(1)}, u32[]{:S(2)}, u32[]{:S(2)}) collective-permute-start(bf16[512,1,4,128]{0,2,3,1:T(4,128)(2,1)S(1)} %get-tuple-element.12), channel_id=1, source_target_pairs={{0,8},{8,16},{16,24},{1,9},{9,17},{17,25},{2,10},{10,18},{18,26},{... | collective-permute-start | bytes 1572872 | tf_op jit(solution)/shard_map/ppermute | solution.py:48
  53.3 10.5 %collective-permute-start.4 = (bf16[512,1,4,128]{0,2,3,1:T(4,128)(2,1)S(1)}, bf16[512,1,4,128]{0,2,3,1:T(4,128)(2,1)S(1)}, u32[]{:S(2)}, u32[]{:S(2)}) collective-permute-start(bf16[512,1,4,128]{0,2,3,1:T(4,128)(2,1)S(1)} %get-tuple-element.13), channel_id=1, source_target_pairs={{8,0},{16,8},{24,16},{9,1},{17,9},{25,17},{10,2},{18,10},{26,18},{... | collective-permute-start | bytes 1572872 | tf_op jit(solution)/shard_map/ppermute | solution.py:49
  64.8 1.0 %copy-start.2 = (bf16[3,256,256]{2,1,0:T(8,128)(2,1)S(1)}, bf16[3,256,256]{2,1,0:T(8,128)(2,1)}, u32[]{:S(2)}) copy-start(bf16[3,256,256]{2,1,0:T(8,128)(2,1)} %rev.4) | copy-start | bytes 1179652
  67.3 12.6 %collective-permute-start.5 = (bf16[256,2,1,128]{0,3,2,1:T(8,128)(2,1)S(1)}, bf16[256,2,1,128]{0,3,2,1:T(8,128)(2,1)S(1)}, u32[]{:S(2)}, u32[]{:S(2)}) collective-permute-start(bf16[256,2,1,128]{0,3,2,1:T(8,128)(2,1)S(1)} %get-tuple-element.14), channel_id=1, source_target_pairs={{0,4},{4,5},{5,1},{1,2},{2,6},{6,7},{7,3},{8,12},{12,13},{13,9},{9... | collective-permute-start | bytes 393224 | tf_op jit(solution)/shard_map/ppermute | solution.py:48
  69.4 10.5 %collective-permute-start.6 = (bf16[256,2,1,128]{0,3,2,1:T(8,128)(2,1)S(1)}, bf16[256,2,1,128]{0,3,2,1:T(8,128)(2,1)S(1)}, u32[]{:S(2)}, u32[]{:S(2)}) collective-permute-start(bf16[256,2,1,128]{0,3,2,1:T(8,128)(2,1)S(1)} %get-tuple-element.15), channel_id=1, source_target_pairs={{4,0},{5,4},{1,5},{2,1},{6,2},{7,6},{3,7},{12,8},{13,12},{9,13},{1... | collective-permute-start | bytes 393224 | tf_op jit(solution)/shard_map/ppermute | solution.py:49
  73.5 19.4 %all-to-all-start.2 = ((bf16[256,2,4,128]{3,2,1,0:T(4,128)(2,1)}), bf16[256,2,4,128]{3,2,1,0:T(4,128)(2,1)S(1)}, u32[]{:S(2)}, u32[]{:S(2)}) async-start(bf16[256,2,4,128]{3,2,1,0:T(4,128)(2,1)} %copy.76), calls=%async_computation.2 | async-start | bytes 1048576 | tf_op jit(solution)/shard_map/all_to_all | solution.py:113
  85.7 5.3 %collective-permute-start.7 = (bf16[128,2,4,128]{0,2,3,1:T(4,128)(2,1)S(1)}, bf16[128,2,4,128]{0,2,3,1:T(4,128)(2,1)S(1)}, u32[]{:S(2)}, u32[]{:S(2)}) collective-permute-start(bf16[128,2,4,128]{0,2,3,1:T(4,128)(2,1)S(1)} %dynamic-slice_bitcast_fusion), channel_id=1, source_target_pairs={{0,4},{1,5},{2,6},{3,7},{4,0},{5,1},{6,2},{7,3},{8,12},{9,13},{10,... | collective-permute-start | bytes 786440 | tf_op jit(solution)/shard_map/ppermute | solution.py:164

commit v28 on v26

--- a/solution.py
+++ b/solution.py
@@ -160,7 +160,9 @@
     rows = deep.shape[2]
     turn = lambda f, r: r if f % 2 == 0 else chans - 1 - r
     place = lambda g: turn(g // chans, g % chans) * filts + g // chans
-    grad_mid = depth_conv(deep, depth_weight[::-1], "DHWIO").astype(jnp.bfloat16)
+    taps = depth_weight.shape[0]
+    flipped = jnp.concatenate([depth_weight[t : t + 1] for t in reversed(range(taps))])
+    grad_mid = depth_conv(deep, flipped, "DHWIO").astype(jnp.bfloat16)
     rimmed = halo(grad_mid, ROWS, 2, place)
     grad_in = plane_conv(rimmed, weight[::-1, ::-1], "HWOI").astype(jnp.bfloat16)
     chan = lax.axis_index("chan")

time: 92.8 us -> 92.5 us (level)
  local copies, waits for them, and re-layouts: 20.6 us -> 19.6 us
    rev x1 -> x0, local copies, waits for them, and re-layouts: 1.77 us -> none  [backward_in(): depth_weight[::-1]]
    slice x0 -> x1, local copies, waits for them, and re-layouts: none -> 1.06 us  [backward_in(): depth_weight[t:t + 1]]
    unnamed x25 -> x23, local copies, waits for them, and re-layouts: 7.2 us -> 6.95 us
  transfers between devices with their start and end apart: 12 -> 12, of which waited for: 5 -> 5; matrix products, arithmetic and copies ran while one was open for 26% -> 25% of each run, Pallas kernels for 0% -> 0%
where the time goes in v28:
time: 92.5 us; the launch traced here: 91.9 us
  starting transfers between devices  31.1 us (34%)
  waiting for transfers between devices  22.3 us (24%)
  local copies, waits for them, and re-layouts  19.6 us (21%)
  other arithmetic  9.33 us (10%)
  matrix products  5.78 us (6%)
  between operations  3.73 us (4%)
    ppermute x2, starting transfers between devices, halo(): lax.ppermute(lax.slice_in_dim(x, length - 1, length, axis=dim), axis, up)  7.06 us
    unnamed x23, local copies, waits for them, and re-layouts  6.95 us
    ppermute x1, waiting for transfers between devices, backward(): lax.ppermute(send, 'chan', shift_pairs(chans, k))  6.26 us
    all_to_all x1, waiting for transfers between devices, backward(): all_filters = lax.all_to_all(blocks, 'filt', 0, 0, tiled=True)  4.59 us
    all_to_all x1, starting transfers between devices, forward_out(): return lax.all_to_all(out, 'filt', 0, 2, tiled=True)  4.52 us
    ppermute x2, waiting for transfers between devices, halo(): after = lax.ppermute(lax.slice_in_dim(x, 0, 1, axis=dim), axis, down)  4.5 us
    all_to_all x1, starting transfers between devices, gather_weight(): got = lax.all_to_all(spread, 'filt', 0, 4, tiled=True)[0]  4.45 us
    all_to_all x1, starting transfers between devices, backward(): all_filters = lax.all_to_all(blocks, 'filt', 0, 0, tiled=True)  4.1 us
  transfers between devices with their start and end apart: 12, of which 5 were waited for; matrix products, arithmetic and copies ran while one was open for 25% of the time, Pallas kernels for 0%

profile of v28, /device:TPU:1, one launch (start us, length us, event | category | flops | bytes accessed | tf_op | source)
XLA Modules:
  0.0 91.9 jit_solution(1368419589793073451)
XLA Ops:
  0.7 2.2 %pad_dynamic-slice_fusion.1 = (bf16[128,2,6,128]{3,2,1,0:T(8,128)(2,1)S(1)}, bf16[128,2,6,128]{3,2,1,0:T(8,128)(2,1)S(1)}) fusion(s32[]{:T(128)S(6)} %select_n.104, bf16[128,2,32,128]{3,2,1,0:T(8,128)(2,1)} %param.7, s32[]{:T(128)S(6)} %select_n.106), kind=kLoop, calls=%fused_computation.2 | loop fusion | bytes 2883592 | tf_op jit(solution)/shard_map/dynamic_slice | solution.py:110
  3.0 2.1 %collective-permute-start = (bf16[128,2,6,128]{3,2,1,0:T(8,128)(2,1)S(1)}, bf16[128,2,6,128]{3,2,1,0:T(8,128)(2,1)}, u32[]{:S(2)}, u32[]{:S(2)}) collective-permute-start(bf16[128,2,6,128]{3,2,1,0:T(8,128)(2,1)S(1)} %get-tuple-element.13), channel_id=1, source_target_pairs={{0,4},{4,0},{1,5},{5,1},{2,6},{6,2},{3,7},{7,3},{8,12},{12,8},{9,1... | collective-permute-start | bytes 1179656 | tf_op jit(solution)/shard_map/ppermute | solution.py:113
  5.5 1.2 %reshape.133 = bf16[4,2,18432]{2,1,0:T(2,128)(2,1)} reshape(bf16[4,3,3,64,64]{4,3,2,1,0:T(8,128)(2,1)S(1)} %broadcast_in_dim.28) | data formatting | bytes 589824
  6.7 4.5 %all-to-all-start = ((bf16[4,2,18432]{2,1,0:T(2,128)(2,1)}), bf16[4,2,18432]{2,1,0:T(2,128)(2,1)S(1)}, u32[]{:S(2)}, u32[]{:S(2)}) async-start(bf16[4,2,18432]{2,1,0:T(2,128)(2,1)} %reshape.133), calls=%async_computation | async-start | bytes 589824 | tf_op jit(solution)/shard_map/all_to_all | solution.py:85
  15.7 6.3 %collective-permute-done.3 = bf16[2,64,2,4,128]{4,1,3,2,0:T(8,128)(2,1)S(1)} collective-permute-done((bf16[2,64,2,4,128]{4,1,3,2,0:T(8,128)(2,1)S(1)}, bf16[2,64,2,4,128]{4,1,3,2,0:T(8,128)(2,1)S(1)}, u32[]{:S(2)}, u32[]{:S(2)}) %collective-permute-start.3) | collective-permute-done | bytes 262176 | tf_op jit(solution)/shard_map/ppermute | solution.py:143
  23.9 1.8 %collective-permute-start.1 = (bf16[3,3,64,256]{3,2,1,0:T(8,128)(2,1)S(1)}, bf16[3,3,64,256]{3,2,1,0:T(8,128)(2,1)S(1)}, u32[]{:S(2)}, u32[]{:S(2)}) collective-permute-start(bf16[3,3,64,256]{3,2,1,0:T(8,128)(2,1)S(1)} %squeeze.6), channel_id=1, source_target_pairs={{0,4},{4,0},{1,5},{5,1},{2,6},{6,2},{3,7},{7,3},{8,12},{12,8},{9,1... | collective-permute-start | bytes 884744 | tf_op jit(solution)/shard_map/ppermute | solution.py:86
  25.7 0.9 broadcast_select_fusion.2
  26.6 4.1 %all-to-all-start.1 = ((bf16[4,64,2,4,128]{4,1,3,2,0:T(8,128)(2,1)}), bf16[4,64,2,4,128]{4,1,3,2,0:T(8,128)(2,1)S(1)}, u32[]{:S(2)}, u32[]{:S(2)}) async-start(bf16[4,64,2,4,128]{4,1,3,2,0:T(8,128)(2,1)} %broadcast_select_fusion.2), calls=%async_computation.1 | async-start | bytes 1048576 | tf_op jit(solution)/shard_map/all_to_all | solution.py:152
  32.1 2.3 %collective-permute-start.2 = (bf16[3,3,128,256]{3,2,1,0:T(8,128)(2,1)}, bf16[3,3,128,256]{3,2,1,0:T(8,128)(2,1)}, u32[]{:S(2)}, u32[]{:S(2)}) collective-permute-start(bf16[3,3,128,256]{3,2,1,0:T(8,128)(2,1)} %constant_dynamic-update-slice_fusion), channel_id=1, source_target_pairs={{0,8},{8,0},{16,24},{24,16},{1,9},{9,1},{17,25},{25,17},{2,10},{10... | collective-permute-start | bytes 1769480 | tf_op jit(solution)/shard_map/ppermute | solution.py:87
  34.5 1.2 %maximum_bitcast_fusion = bf16[256,6,2,128]{3,1,2,0:T(8,128)(2,1)S(1)} fusion(bf16[128,2,6,128]{3,2,1,0:T(8,128)(2,1)} %collective-permute-done, bf16[128,2,6,128]{3,2,1,0:T(8,128)(2,1)S(1)} %get-tuple-element.12), kind=kLoop, calls=%fused_computation.14 | loop fusion | flops 393216 | bytes 1572864 | tf_op jit(solution)/shard_map/concatenate | solution.py:114
  35.7 1.3 %copy.114 = bf16[256,6,2,128]{0,2,3,1:T(2,128)(2,1)S(1)} copy(bf16[256,6,2,128]{3,1,2,0:T(8,128)(2,1)S(1)} %maximum_bitcast_fusion) | data formatting | bytes 1572864
  37.7 1.7 %fusion.6 = bf16[256,6,2,8,19]{0,2,4,3,1:T(2,128)(2,1)} fusion(bf16[256,6,2,7,2]{0,2,4,3,1:T(2,128)(2,1)S(1)} %slice.70, bf16[256,6,2,8,17]{0,2,4,3,1:T(2,128)(2,1)S(1)} %bitcast.83), kind=kLoop, calls=%fused_computation.19 | loop fusion | flops 2801664 | bytes 1855488 | tf_op jit(solution)/shard_map/conv_general_dilated | solution.py:54
  39.4 4.6 %all-to-all-done.1 = bf16[4,64,2,4,128]{4,1,3,2,0:T(8,128)(2,1)S(1)} async-done(((bf16[4,64,2,4,128]{4,1,3,2,0:T(8,128)(2,1)}), bf16[4,64,2,4,128]{4,1,3,2,0:T(8,128)(2,1)S(1)}, u32[]{:S(2)}, u32[]{:S(2)}) %all-to-all-start.1) | async-done | bytes 524320 | tf_op jit(solution)/shard_map/all_to_all | solution.py:152
  44.4 1.4 %broadcast_select_fusion.1 = (bf16[3,3,128,256]{3,2,1,0:T(8,128)(2,1)S(1)}, bf16[3,3,128,256]{3,2,1,0:T(8,128)(2,1)S(1)}) fusion(bf16[3,3,128,256]{3,2,1,0:T(8,128)(2,1)} %constant_dynamic-update-slice_fusion, bf16[3,3,128,256]{3,2,1,0:T(8,128)(2,1)} %collective-permute-done.2, pred[]{:T(512)S(6)} %eq.18), kind=kLoop, calls=%fused_computation.27 | loop fusion | flops 589824 | bytes 2359297 | tf_op jit(solution)/shard_map/jit(_where)/select_n | solution.py:88
  45.9 1.5 %fusion.2 = bf16[4,16,17,256]{3,1,2,0:T(8,128)(2,1)S(1)} fusion(bf16[3,3,256,256]{3,2,1,0:T(8,128)(2,1)S(1)} %bitcast.95, bf16[256,6,2,8,19]{0,2,4,3,1:T(2,128)(2,1)S(1)} %copy-done.1, pred[16,17]{0,1:T(8,128)(4,1)S(1)} %copy-done.7), kind=kOutput, calls=%fused_computation.9 | convolution fusion | flops 1284014080 | bytes 2670864 | tf_op jit(solution)/shard_map/conv_general_dilated | solution.py:54
  48.4 5.1 %collective-permute-start.4 = (bf16[512,1,4,128]{0,2,3,1:T(4,128)(2,1)S(1)}, bf16[512,1,4,128]{0,2,3,1:T(4,128)(2,1)}, u32[]{:S(2)}, u32[]{:S(2)}) collective-permute-start(bf16[512,1,4,128]{0,2,3,1:T(4,128)(2,1)S(1)} %get-tuple-element.16), channel_id=1, source_target_pairs={{0,8},{8,16},{16,24},{1,9},{9,17},{17,25},{2,10},{10,18},{18,26},{... | collective-permute-start | bytes 1572872 | tf_op jit(solution)/shard_map/ppermute | solution.py:48
  53.5 1.9 %collective-permute-start.5 = (bf16[512,1,4,128]{0,2,3,1:T(4,128)(2,1)S(1)}, bf16[512,1,4,128]{0,2,3,1:T(4,128)(2,1)}, u32[]{:S(2)}, u32[]{:S(2)}) collective-permute-start(bf16[512,1,4,128]{0,2,3,1:T(4,128)(2,1)S(1)} %get-tuple-element.17), channel_id=1, source_target_pairs={{8,0},{16,8},{24,16},{9,1},{17,9},{25,17},{10,2},{18,10},{26,18},{... | collective-permute-start | bytes 1572872 | tf_op jit(solution)/shard_map/ppermute | solution.py:49
  55.5 1.1 %fusion.22 = (bf16[1,256,256]{2,1,0:T(8,128)(2,1)S(1)}, bf16[1,256,256]{2,1,0:T(8,128)(2,1)S(1)}, bf16[1,256,256]{2,1,0:T(8,128)(2,1)S(1)}) fusion(bf16[3,256,256]{2,1,0:T(8,128)(2,1)} %param.9), kind=kLoop, calls=%fused_computation.65 | loop fusion | bytes 786432 | tf_op jit(solution)/shard_map/slice | solution.py:164
  56.5 3.1 %collective-permute-done.4 = bf16[512,1,4,128]{0,2,3,1:T(4,128)(2,1)} collective-permute-done((bf16[512,1,4,128]{0,2,3,1:T(4,128)(2,1)S(1)}, bf16[512,1,4,128]{0,2,3,1:T(4,128)(2,1)}, u32[]{:S(2)}, u32[]{:S(2)}) %collective-permute-start.4) | collective-permute-done | bytes 524320 | tf_op jit(solution)/shard_map/ppermute | solution.py:48
  59.6 4.5 %collective-permute-done.5 = bf16[512,1,4,128]{0,2,3,1:T(4,128)(2,1)} collective-permute-done((bf16[512,1,4,128]{0,2,3,1:T(4,128)(2,1)S(1)}, bf16[512,1,4,128]{0,2,3,1:T(4,128)(2,1)}, u32[]{:S(2)}, u32[]{:S(2)}) %collective-permute-start.5) | collective-permute-done | bytes 524320 | tf_op jit(solution)/shard_map/ppermute | solution.py:49
  64.1 2.0 %pad_maximum_fusion = bf16[512,4,4,128]{0,2,3,1:T(4,128)(2,1)S(1)} fusion(bf16[512,1,4,128]{0,2,3,1:T(4,128)(2,1)} %collective-permute-done.5, bf16[256,2,4,128]{0,2,3,1:T(4,128)(2,1)S(1)} %copy.93, bf16[256,2,4,128]{0,2,3,1:T(4,128)(2,1)S(1)} %slice_bitcast_fusion, bf16[512,1,4,128]{0,2,3,1:T(4,128)(2,1)} %collective-permute-done.4), kind=kLoop, calls=%fused_computation.3 | loop fusion | flops 8388608 | bytes 4194304 | tf_op jit(solution)/shard_map/concatenate | solution.py:50
  66.9 1.4 %convolution_convert_fusion = bf16[2,4,8,16,256]{4,2,3,1,0:T(8,128)(2,1)S(1)} fusion(bf16[256,4,4,8,16]{0,2,4,3,1:T(4,128)(2,1)S(1)} %bitcast.99, bf16[1,256,256]{2,1,0:T(8,128)(2,1)S(1)} %get-tuple-element.25, bf16[1,256,256]{2,1,0:T(8,128)(2,1)S(1)} %get-tuple-element.26, bf16[1,256,256]{2,1,0:T(8,128)(2,1)S(1)} %get-tuple-element.24), kind=kOutput, calls=%fused_computation.11 | convolution fusion | flops 403308544 | bytes 1966080 | tf_op jit(solution)/shard_map/conv_general_dilated | solution.py:65
  68.4 1.9 %collective-permute-start.6 = (bf16[256,2,1,128]{0,3,2,1:T(8,128)(2,1)S(1)}, bf16[256,2,1,128]{0,3,2,1:T(8,128)(2,1)S(1)}, u32[]{:S(2)}, u32[]{:S(2)}) collective-permute-start(bf16[256,2,1,128]{0,3,2,1:T(8,128)(2,1)S(1)} %get-tuple-element.18), channel_id=1, source_target_pairs={{0,4},{4,5},{5,1},{1,2},{2,6},{6,7},{7,3},{8,12},{12,13},{13,9},{9... | collective-permute-start | bytes 393224 | tf_op jit(solution)/shard_map/ppermute | solution.py:48
  70.3 1.5 %collective-permute-start.7 = (bf16[256,2,1,128]{0,3,2,1:T(8,128)(2,1)S(1)}, bf16[256,2,1,128]{0,3,2,1:T(8,128)(2,1)S(1)}, u32[]{:S(2)}, u32[]{:S(2)}) collective-permute-start(bf16[256,2,1,128]{0,3,2,1:T(8,128)(2,1)S(1)} %get-tuple-element.19), channel_id=1, source_target_pairs={{4,0},{5,4},{1,5},{2,1},{6,2},{7,6},{3,7},{12,8},{13,12},{9,13},{1... | collective-permute-start | bytes 393224 | tf_op jit(solution)/shard_map/ppermute | solution.py:49
  71.8 1.4 %convolution_convert_fusion.1 = bf16[2,4,8,16,256]{4,2,3,1,0:T(8,128)(2,1)S(1)} fusion(bf16[256,4,4,8,16]{0,2,4,3,1:T(4,128)(2,1)S(1)} %bitcast.98, bf16[3,256,256]{2,1,0:T(8,128)(2,1)S(1)} %copy-done.3), kind=kOutput, calls=%fused_computation.12 | convolution fusion | flops 402915328 | bytes 1966080 | tf_op jit(solution)/shard_map/conv_general_dilated | solution.py:65
  73.3 1.1 %copy.98 = bf16[256,2,4,128]{3,2,1,0:T(4,128)(2,1)} copy(bf16[256,2,4,128]{0,3,2,1:T(8,128)(2,1)S(1)} %bitcast.92) | data formatting | bytes 1048576 | tf_op jit(solution)/shard_map/convert_element_type | solution.py:123
  74.4 4.5 %all-to-all-start.2 = ((bf16[256,2,4,128]{3,2,1,0:T(4,128)(2,1)}), bf16[256,2,4,128]{3,2,1,0:T(4,128)(2,1)S(1)}, u32[]{:S(2)}, u32[]{:S(2)}) async-start(bf16[256,2,4,128]{3,2,1,0:T(4,128)(2,1)} %copy.98), calls=%async_computation.2 | async-start | bytes 1048576 | tf_op jit(solution)/shard_map/all_to_all | solution.py:124
  81.4 1.5 %fusion.3 = bf16[4,16,17,256]{3,1,2,0:T(8,128)(2,1)S(1)} fusion(bf16[3,3,256,256]{3,2,1,0:T(8,128)(2,1)S(1)} %bitcast.96, bf16[256,6,2,8,19]{0,2,4,3,1:T(2,128)(2,1)S(1)} %fusion.7, pred[16,17]{0,1:T(8,128)(4,1)S(1)} %copy-done.7), kind=kOutput, calls=%fused_computation.10 | convolution fusion | flops 1284014080 | bytes 2670864 | tf_op jit(solution)/shard_map/conv_general_dilated | solution.py:54
  83.5 1.1 %collective-permute-start.8 = (bf16[128,2,4,128]{0,2,3,1:T(4,128)(2,1)S(1)}, bf16[128,2,4,128]{0,2,3,1:T(4,128)(2,1)S(1)}, u32[]{:S(2)}, u32[]{:S(2)}) collective-permute-start(bf16[128,2,4,128]{0,2,3,1:T(4,128)(2,1)S(1)} %dynamic-slice_bitcast_fusion), channel_id=1, source_target_pairs={{0,4},{1,5},{2,6},{3,7},{4,0},{5,1},{6,2},{7,3},{8,12},{9,13},{10,... | collective-permute-start | bytes 786440 | tf_op jit(solution)/shard_map/ppermute | solution.py:177
  84.9 3.9 %collective-permute-done.8 = bf16[128,2,4,128]{0,2,3,1:T(4,128)(2,1)S(1)} collective-permute-done((bf16[128,2,4,128]{0,2,3,1:T(4,128)(2,1)S(1)}, bf16[128,2,4,128]{0,2,3,1:T(4,128)(2,1)S(1)}, u32[]{:S(2)}, u32[]{:S(2)}) %collective-permute-start.8) | collective-permute-done | bytes 262176 | tf_op jit(solution)/shard_map/ppermute | solution.py:177
  89.3 1.3 %copy.109 = bf16[128,2,8,128]{3,2,1,0:T(8,128)(2,1)} copy(bf16[128,2,8,128]{0,2,3,1:T(8,128)(2,1)S(1)} %maximum_select_fusion) | data formatting | bytes 1048576
  90.8 1.1 %copy.108 = bf16[64,2,16,128]{3,2,1,0:T(8,128)(2,1)} copy(bf16[64,2,16,128]{3,0,2,1:T(8,128)(2,1)S(1)} %bitcast.94) | data formatting | bytes 1048576
  (72 shorter events, 12.7 us)
Async XLA Ops:
  0.6 4.5 %copy-start = (bf16[3,3,128,64]{2,3,1,0:T(8,128)(2,1)S(1)}, bf16[3,3,128,64]{2,3,1,0:T(8,128)(2,1)}, u32[]{:S(2)}) copy-start(bf16[3,3,128,64]{2,3,1,0:T(8,128)(2,1)} %param.8) | copy-start | bytes 442372
  2.9 8.2 %copy-start.4 = (s32[2,2]{1,0:T(2,128)S(1)}, s32[2,2]{1,0:T(2,128)}, u32[]{:S(2)}) copy-start(s32[2,2]{1,0:T(2,128)} %constant.90.clone) | copy-start | bytes 52
  2.9 8.2 %copy-start.5 = (s32[2,2]{1,0:T(2,128)S(1)}, s32[2,2]{1,0:T(2,128)}, u32[]{:S(2)}) copy-start(s32[2,2]{1,0:T(2,128)} %constant.91.clone) | copy-start | bytes 52
  2.9 12.0 %copy-start.2 = (bf16[64,2,16,128]{3,2,1,0:T(8,128)(2,1)S(1)}, bf16[64,2,16,128]{3,2,1,0:T(8,128)(2,1)}, u32[]{:S(2)}) copy-start(bf16[64,2,16,128]{3,2,1,0:T(8,128)(2,1)} %param.10) | copy-start | bytes 1572868
  3.0 31.5 %collective-permute-start = (bf16[128,2,6,128]{3,2,1,0:T(8,128)(2,1)S(1)}, bf16[128,2,6,128]{3,2,1,0:T(8,128)(2,1)}, u32[]{:S(2)}, u32[]{:S(2)}) collective-permute-start(bf16[128,2,6,128]{3,2,1,0:T(8,128)(2,1)S(1)} %get-tuple-element.13), channel_id=1, source_target_pairs={{0,4},{4,0},{1,5},{5,1},{2,6},{6,2},{3,7},{7,3},{8,12},{12,8},{9,1... | collective-permute-start | bytes 1179656 | tf_op jit(solution)/shard_map/ppermute | solution.py:113
  5.5 10.1 %copy-start.6 = (s32[2,4]{1,0:T(2,128)S(1)}, s32[2,4]{1,0:T(2,128)}, u32[]{:S(2)}) copy-start(s32[2,4]{1,0:T(2,128)} %constant.92.clone) | copy-start | bytes 100
  6.7 16.0 %all-to-all-start = ((bf16[4,2,18432]{2,1,0:T(2,128)(2,1)}), bf16[4,2,18432]{2,1,0:T(2,128)(2,1)S(1)}, u32[]{:S(2)}, u32[]{:S(2)}) async-start(bf16[4,2,18432]{2,1,0:T(2,128)(2,1)} %reshape.133), calls=%async_computation | async-start | bytes 589824 | tf_op jit(solution)/shard_map/all_to_all | solution.py:85
  15.3 6.6 %collective-permute-start.3 = (bf16[2,64,2,4,128]{4,1,3,2,0:T(8,128)(2,1)S(1)}, bf16[2,64,2,4,128]{4,1,3,2,0:T(8,128)(2,1)S(1)}, u32[]{:S(2)}, u32[]{:S(2)}) collective-permute-start(bf16[2,64,2,4,128]{4,1,3,2,0:T(8,128)(2,1)S(1)} %pad_maximum_fusion.4), channel_id=1, source_target_pairs={{0,4},{4,0},{1,5},{5,1},{2,6},{6,2},{3,7},{7,3},{8,12},{12,8},{9,1... | collective-permute-start | bytes 786440 | tf_op jit(solution)/shard_map/ppermute | solution.py:143
  23.9 7.5 %collective-permute-start.1 = (bf16[3,3,64,256]{3,2,1,0:T(8,128)(2,1)S(1)}, bf16[3,3,64,256]{3,2,1,0:T(8,128)(2,1)S(1)}, u32[]{:S(2)}, u32[]{:S(2)}) collective-permute-start(bf16[3,3,64,256]{3,2,1,0:T(8,128)(2,1)S(1)} %squeeze.6), channel_id=1, source_target_pairs={{0,4},{4,0},{1,5},{5,1},{2,6},{6,2},{3,7},{7,3},{8,12},{12,8},{9,1... | collective-permute-start | bytes 884744 | tf_op jit(solution)/shard_map/ppermute | solution.py:86
  26.6 17.4 %all-to-all-start.1 = ((bf16[4,64,2,4,128]{4,1,3,2,0:T(8,128)(2,1)}), bf16[4,64,2,4,128]{4,1,3,2,0:T(8,128)(2,1)S(1)}, u32[]{:S(2)}, u32[]{:S(2)}) async-start(bf16[4,64,2,4,128]{4,1,3,2,0:T(8,128)(2,1)} %broadcast_select_fusion.2), calls=%async_computation.1 | async-start | bytes 1048576 | tf_op jit(solution)/shard_map/all_to_all | solution.py:152
  32.1 12.2 %collective-permute-start.2 = (bf16[3,3,128,256]{3,2,1,0:T(8,128)(2,1)}, bf16[3,3,128,256]{3,2,1,0:T(8,128)(2,1)}, u32[]{:S(2)}, u32[]{:S(2)}) collective-permute-start(bf16[3,3,128,256]{3,2,1,0:T(8,128)(2,1)} %constant_dynamic-update-slice_fusion), channel_id=1, source_target_pairs={{0,8},{8,0},{16,24},{24,16},{1,9},{9,1},{17,25},{25,17},{2,10},{10... | collective-permute-start | bytes 1769480 | tf_op jit(solution)/shard_map/ppermute | solution.py:87
  44.4 1.6 %copy-start.1 = (bf16[256,6,2,8,19]{0,2,4,3,1:T(2,128)(2,1)S(1)}, bf16[256,6,2,8,19]{0,2,4,3,1:T(2,128)(2,1)}, u32[]{:S(2)}) copy-start(bf16[256,6,2,8,19]{0,2,4,3,1:T(2,128)(2,1)} %fusion.6) | copy-start | bytes 2801668
  44.4 1.6 %copy-start.7 = (pred[16,17]{0,1:T(8,128)(4,1)S(1)}, pred[16,17]{0,1:T(8,128)(4,1)}, u32[]{:S(2)}) copy-start(pred[16,17]{0,1:T(8,128)(4,1)} %constant.112) | copy-start | bytes 820
  48.4 11.2 %collective-permute-start.4 = (bf16[512,1,4,128]{0,2,3,1:T(4,128)(2,1)S(1)}, bf16[512,1,4,128]{0,2,3,1:T(4,128)(2,1)}, u32[]{:S(2)}, u32[]{:S(2)}) collective-permute-start(bf16[512,1,4,128]{0,2,3,1:T(4,128)(2,1)S(1)} %get-tuple-element.16), channel_id=1, source_target_pairs={{0,8},{8,16},{16,24},{1,9},{9,17},{17,25},{2,10},{10,18},{18,26},{... | collective-permute-start | bytes 1572872 | tf_op jit(solution)/shard_map/ppermute | solution.py:48
  53.5 10.6 %collective-permute-start.5 = (bf16[512,1,4,128]{0,2,3,1:T(4,128)(2,1)S(1)}, bf16[512,1,4,128]{0,2,3,1:T(4,128)(2,1)}, u32[]{:S(2)}, u32[]{:S(2)}) collective-permute-start(bf16[512,1,4,128]{0,2,3,1:T(4,128)(2,1)S(1)} %get-tuple-element.17), channel_id=1, source_target_pairs={{8,0},{16,8},{24,16},{9,1},{17,9},{25,17},{10,2},{18,10},{26,18},{... | collective-permute-start | bytes 1572872 | tf_op jit(solution)/shard_map/ppermute | solution.py:49
  66.8 5.0 %copy-start.3 = (bf16[3,256,256]{2,1,0:T(8,128)(2,1)S(1)}, bf16[3,256,256]{2,1,0:T(8,128)(2,1)}, u32[]{:S(2)}) copy-start(bf16[3,256,256]{2,1,0:T(8,128)(2,1)} %param.9) | copy-start | bytes 1179652
  68.4 10.5 %collective-permute-start.6 = (bf16[256,2,1,128]{0,3,2,1:T(8,128)(2,1)S(1)}, bf16[256,2,1,128]{0,3,2,1:T(8,128)(2,1)S(1)}, u32[]{:S(2)}, u32[]{:S(2)}) collective-permute-start(bf16[256,2,1,128]{0,3,2,1:T(8,128)(2,1)S(1)} %get-tuple-element.18), channel_id=1, source_target_pairs={{0,4},{4,5},{5,1},{1,2},{2,6},{6,7},{7,3},{8,12},{12,13},{13,9},{9... | collective-permute-start | bytes 393224 | tf_op jit(solution)/shard_map/ppermute | solution.py:48
  70.3 8.6 %collective-permute-start.7 = (bf16[256,2,1,128]{0,3,2,1:T(8,128)(2,1)S(1)}, bf16[256,2,1,128]{0,3,2,1:T(8,128)(2,1)S(1)}, u32[]{:S(2)}, u32[]{:S(2)}) collective-permute-start(bf16[256,2,1,128]{0,3,2,1:T(8,128)(2,1)S(1)} %get-tuple-element.19), channel_id=1, source_target_pairs={{4,0},{5,4},{1,5},{2,1},{6,2},{7,6},{3,7},{12,8},{13,12},{9,13},{1... | collective-permute-start | bytes 393224 | tf_op jit(solution)/shard_map/ppermute | solution.py:49
  74.4 16.2 %all-to-all-start.2 = ((bf16[256,2,4,128]{3,2,1,0:T(4,128)(2,1)}), bf16[256,2,4,128]{3,2,1,0:T(4,128)(2,1)S(1)}, u32[]{:S(2)}, u32[]{:S(2)}) async-start(bf16[256,2,4,128]{3,2,1,0:T(4,128)(2,1)} %copy.98), calls=%async_computation.2 | async-start | bytes 1048576 | tf_op jit(solution)/shard_map/all_to_all | solution.py:124
  83.5 5.3 %collective-permute-start.8 = (bf16[128,2,4,128]{0,2,3,1:T(4,128)(2,1)S(1)}, bf16[128,2,4,128]{0,2,3,1:T(4,128)(2,1)S(1)}, u32[]{:S(2)}, u32[]{:S(2)}) collective-permute-start(bf16[128,2,4,128]{0,2,3,1:T(4,128)(2,1)S(1)} %dynamic-slice_bitcast_fusion), channel_id=1, source_target_pairs={{0,4},{1,5},{2,6},{3,7},{4,0},{5,1},{6,2},{7,3},{8,12},{9,13},{10,... | collective-permute-start | bytes 786440 | tf_op jit(solution)/shard_map/ppermute | solution.py:177
